TPU v7x, 32 devices: a whole 2x2x4 slice. The times are simulated.
32 devices in a mesh: atoms: 8 (over y, x, core), bands: 4 (over z).
Axes of the slice: x: 2, y: 2, z: 4, core: 2. Of those that a mesh axis runs over, the one named last changes fastest.
Arguments:
- subspace: bfloat16 [512, 6144], P('bands', 'atoms'), may hold values from -120 to 120
- diag_block: bfloat16 [6144, 768], P('atoms'), may hold values from -0.0625 to 0.0625
- pair_block: bfloat16 [2, 6144, 768], P(None, 'atoms'), may hold values from -0.0625 to 0.0625
- pair_pattern: int32 [2, 32, 4], P(None, 'atoms'), may hold values 0 or 1
- atom_sizes: int32 [8, 4], replicated, may hold values from 1 to 256, 768 in all within a row
- rotations: bfloat16 [4, 512, 512], P(None, None, 'bands'), may hold values from -0.25 to 0.25
Outputs:
- rotated: float32 [512, 6144], P('bands', 'atoms')
Inputs may be any that keep to these rules, and one draw needn't show every extreme that they name: `atom_sizes`: each row holds the orbital counts of the 4 atoms of one partition in order and sums to 768.
All inputs are finite; a program needn't handle non-finite values. No bound on the sum of `pair_pattern` on one device may be relied on, other than what follows from the above.
Results may differ from a plain program's by a relative error of at most 0.028.
Values may be sent and summed in bfloat16 or wider, within the bound.
No kernel may reach another device: no remote copies, remote signals or barrier semaphores. Data moves between devices by JAX's collectives and lax.ppermute only.
A program may use at most 64 MiB of HBM per device.

v0:
```python
import jax
import jax.numpy as jnp
from jax import lax
from jax.sharding import PartitionSpec as P

ROUNDS = 2
DEGREE = 8
ROTS = 4


filter_center = 0.1
filter_half = 1.25
norm_eps = 1e-06


def swapped(value, axis, stride):
    mask = 2**stride
    pairs = [(source, source ^ mask) for source in range(lax.axis_size(axis))]
    return lax.ppermute(value, axis, pairs)


def atom_onehot(atom_counts, length_total):
    atom_ends = jnp.cumsum(atom_counts, axis=-1)
    atom_starts = atom_ends - atom_counts
    positions = jnp.arange(length_total, dtype=jnp.int32)
    inside = (positions >= atom_starts[..., None]) & (positions < atom_ends[..., None])
    return inside.astype(jnp.float32)


def diagonal_weights(onehot_rows):
    levels = jnp.arange(onehot_rows.shape[0], dtype=jnp.float32)
    atom_index = jnp.sum(onehot_rows * levels[:, None], axis=0)
    upper_flag = (atom_index[:, None] < atom_index[None, :]).astype(jnp.float32)
    same_atom = (atom_index[:, None] == atom_index[None, :]).astype(jnp.float32)
    return upper_flag + 0.5 * same_atom


def apply_operator(values, diag_sym, coupling):
    result = jnp.dot(values, diag_sym, preferred_element_type=jnp.float32)
    for round_index in range(ROUNDS):
        pair_mat = coupling[round_index]
        other_rows = swapped(values, "atoms", round_index)
        own_term = lax.dot_general(
            other_rows, pair_mat, (((1,), (1,)), ((), ())), preferred_element_type=jnp.float32
        )
        sent_term = jnp.dot(values, pair_mat, preferred_element_type=jnp.float32)
        returned = swapped(sent_term.astype(jnp.bfloat16), "atoms", round_index).astype(
            sent_term.dtype
        )
        result = result + own_term + returned
    return result


def body(subspace, diag_block, pair_block, pair_pattern, atom_sizes, rotations):
    orb_dev = diag_block.shape[1]
    atoms_here = lax.axis_index("atoms")
    onehot_own = atom_onehot(
        lax.dynamic_index_in_dim(atom_sizes, atoms_here, 0, keepdims=False), orb_dev
    )
    upper_part = diag_block.astype(jnp.float32) * diagonal_weights(onehot_own)
    diag_sym = (upper_part + upper_part.T).astype(jnp.bfloat16)
    coupling = []
    for round_index in range(ROUNDS):
        partner = jnp.bitwise_xor(atoms_here, 1 << round_index)
        onehot_other = atom_onehot(
            lax.dynamic_index_in_dim(atom_sizes, partner, 0, keepdims=False), orb_dev
        )
        pattern = pair_pattern[round_index].astype(jnp.float32)
        right_side = jnp.dot(pattern, onehot_other, precision=lax.Precision.HIGHEST)
        pair_mask = lax.dot_general(
            onehot_own, right_side, (((0,), (0,)), ((), ())), precision=lax.Precision.HIGHEST
        )
        pair_mat = (pair_block[round_index].astype(jnp.float32) * pair_mask).astype(jnp.bfloat16)
        coupling.append(pair_mat)
    previous = subspace.astype(jnp.float32)
    current = (
        apply_operator(subspace, diag_sym, coupling) - filter_center * previous
    ) / filter_half
    for degree_index in range(1, DEGREE):
        applied = apply_operator(current.astype(jnp.bfloat16), diag_sym, coupling)
        following = 2.0 * (applied - filter_center * current) / filter_half - previous
        previous, current = (current, following)
    total_orbitals = orb_dev * lax.axis_size("atoms")
    basis_rows = current
    for rotation_index in range(ROTS):
        rounded = basis_rows.astype(jnp.bfloat16)
        local_cols = rotations[rotation_index]
        mixed_rows = lax.dot_general(
            local_cols,
            lax.all_gather(rounded, "bands", axis=0, tiled=True),
            (((0,), (0,)), ((), ())),
            preferred_element_type=jnp.float32,
        )
        squares = lax.psum(jnp.sum(mixed_rows * mixed_rows, axis=1), "atoms")
        col_norm = jnp.sqrt(squares / total_orbitals + norm_eps)
        basis_rows = mixed_rows / col_norm[:, None]
    return basis_rows


def solution(mesh):
    placed = (
        P("bands", "atoms"),
        P("atoms", None),
        P(None, "atoms", None),
        P(None, "atoms", None),
        P(),
        P(None, None, "bands"),
    )
    return jax.shard_map(
        body, mesh=mesh, in_specs=placed, out_specs=P("bands", "atoms"), check_vma=False
    )
```

profile of v0, /device:TPU:0, one launch (start us, length us, event | category | flops | bytes accessed | tf_op | source)
XLA Modules:
  0.0 228.8 jit_solution(13515440379078869902)
XLA Ops:
  0.0 2.9 %collective-permute-start.2 = (bf16[128,768]{1,0:T(8,128)(2,1)}, bf16[128,768]{1,0:T(8,128)(2,1)}, u32[]{:S(2)}, u32[]{:S(2)}) collective-permute-start(bf16[128,768]{1,0:T(8,128)(2,1)} %param.6), channel_id=1, source_target_pairs={{0,8},{4,12},{8,0},{12,4},{16,24},{20,28},{24,16},{28,20},{1,9},{5... | collective-permute-start | bytes 589832 | tf_op jit(solution)/shard_map/ppermute | solution.py:19
  5.7 2.7 %fusion.1 = bf16[768,768]{1,0:T(8,128)(2,1)S(1)} fusion(f32[768,4]{1,0:T(8,128)S(1)} %fusion.77, bf16[2,768,768]{2,1,0:T(8,128)(2,1)} %param.8, s32[4]{0:T(128)S(1)} %bitcast.155, s32[4]{0:T(128)S(1)} %bitcast_subtract_fusion.2), kind=kOutput, calls=%fused_computation.3 | convolution fusion | flops 30093312 | bytes 2371616 | tf_op jit(solution)/shard_map/dot_general | solution.py:70
  13.1 1.7 copy.41
  14.9 2.0 add_multiply_fusion
  16.9 3.1 %copy.40 = f32[768,768]{0,1:T(8,128)} copy(f32[768,768]{1,0:T(8,128)} %add_multiply_fusion) | data formatting | bytes 4718592 | tf_op jit(solution)/shard_map/mul | solution.py:60
  19.9 2.7 %fusion.2 = bf16[768,768]{1,0:T(8,128)(2,1)S(1)} fusion(f32[768,768]{0,1:T(8,128)} %copy.40, f32[768]{0:T(1024)S(1)} %select_reduce_fusion, bf16[768,768]{1,0:T(8,128)(2,1)} %param.7), kind=kLoop, calls=%fused_computation.5 | loop fusion | flops 5308416 | bytes 4721664 | tf_op jit(solution)/shard_map/convert_element_type | solution.py:61
  24.7 1.6 multiply_convert_fusion
  26.9 2.1 collective-permute-start.6
  30.7 3.9 %collective-permute-done.6 = bf16[128,768]{0,1:T(8,128)(2,1)S(1)} collective-permute-done((bf16[128,768]{0,1:T(8,128)(2,1)S(1)}, bf16[128,768]{0,1:T(8,128)(2,1)S(1)}, u32[]{:S(2)}, u32[]{:S(2)}) %collective-permute-start.6) | collective-permute-done | bytes 196640 | tf_op jit(solution)/shard_map/ppermute | solution.py:19
  35.1 2.9 %collective-permute-done.7 = bf16[128,768]{0,1:T(8,128)(2,1)S(1)} collective-permute-done((bf16[128,768]{0,1:T(8,128)(2,1)S(1)}, bf16[128,768]{0,1:T(8,128)(2,1)S(1)}, u32[]{:S(2)}, u32[]{:S(2)}) %collective-permute-start.7) | collective-permute-done | bytes 196640 | tf_op jit(solution)/shard_map/ppermute | solution.py:19
  39.0 1.8 collective-permute-start.10
  42.9 2.7 %collective-permute-done.10 = bf16[128,768]{0,1:T(8,128)(2,1)S(1)} collective-permute-done((bf16[128,768]{0,1:T(8,128)(2,1)S(1)}, bf16[128,768]{0,1:T(8,128)(2,1)S(1)}, u32[]{:S(2)}, u32[]{:S(2)}) %collective-permute-start.10) | collective-permute-done | bytes 196640 | tf_op jit(solution)/shard_map/ppermute | solution.py:19
  46.1 3.2 %collective-permute-done.11 = bf16[128,768]{0,1:T(8,128)(2,1)S(1)} collective-permute-done((bf16[128,768]{0,1:T(8,128)(2,1)S(1)}, bf16[128,768]{0,1:T(8,128)(2,1)S(1)}, u32[]{:S(2)}, u32[]{:S(2)}) %collective-permute-start.11) | collective-permute-done | bytes 196640 | tf_op jit(solution)/shard_map/ppermute | solution.py:19
  54.3 4.0 %collective-permute-done.14 = bf16[128,768]{0,1:T(8,128)(2,1)S(1)} collective-permute-done((bf16[128,768]{0,1:T(8,128)(2,1)S(1)}, bf16[128,768]{0,1:T(8,128)(2,1)S(1)}, u32[]{:S(2)}, u32[]{:S(2)}) %collective-permute-start.14) | collective-permute-done | bytes 196640 | tf_op jit(solution)/shard_map/ppermute | solution.py:19
  58.8 2.4 %collective-permute-done.15 = bf16[128,768]{0,1:T(8,128)(2,1)S(1)} collective-permute-done((bf16[128,768]{0,1:T(8,128)(2,1)S(1)}, bf16[128,768]{0,1:T(8,128)(2,1)S(1)}, u32[]{:S(2)}, u32[]{:S(2)}) %collective-permute-start.15) | collective-permute-done | bytes 196640 | tf_op jit(solution)/shard_map/ppermute | solution.py:19
  66.4 3.0 %collective-permute-done.18 = bf16[128,768]{0,1:T(8,128)(2,1)S(1)} collective-permute-done((bf16[128,768]{0,1:T(8,128)(2,1)S(1)}, bf16[128,768]{0,1:T(8,128)(2,1)S(1)}, u32[]{:S(2)}, u32[]{:S(2)}) %collective-permute-start.18) | collective-permute-done | bytes 196640 | tf_op jit(solution)/shard_map/ppermute | solution.py:19
  69.9 2.4 %collective-permute-done.19 = bf16[128,768]{0,1:T(8,128)(2,1)S(1)} collective-permute-done((bf16[128,768]{0,1:T(8,128)(2,1)S(1)}, bf16[128,768]{0,1:T(8,128)(2,1)S(1)}, u32[]{:S(2)}, u32[]{:S(2)}) %collective-permute-start.19) | collective-permute-done | bytes 196640 | tf_op jit(solution)/shard_map/ppermute | solution.py:19
  77.2 3.1 %collective-permute-done.22 = bf16[128,768]{0,1:T(8,128)(2,1)S(1)} collective-permute-done((bf16[128,768]{0,1:T(8,128)(2,1)S(1)}, bf16[128,768]{0,1:T(8,128)(2,1)S(1)}, u32[]{:S(2)}, u32[]{:S(2)}) %collective-permute-start.22) | collective-permute-done | bytes 196640 | tf_op jit(solution)/shard_map/ppermute | solution.py:19
  80.8 2.5 %collective-permute-done.23 = bf16[128,768]{0,1:T(8,128)(2,1)S(1)} collective-permute-done((bf16[128,768]{0,1:T(8,128)(2,1)S(1)}, bf16[128,768]{0,1:T(8,128)(2,1)S(1)}, u32[]{:S(2)}, u32[]{:S(2)}) %collective-permute-start.23) | collective-permute-done | bytes 196640 | tf_op jit(solution)/shard_map/ppermute | solution.py:19
  88.3 2.3 collective-permute-done.26
  91.0 3.3 %collective-permute-done.27 = bf16[128,768]{0,1:T(8,128)(2,1)S(1)} collective-permute-done((bf16[128,768]{0,1:T(8,128)(2,1)S(1)}, bf16[128,768]{0,1:T(8,128)(2,1)S(1)}, u32[]{:S(2)}, u32[]{:S(2)}) %collective-permute-start.27) | collective-permute-done | bytes 196640 | tf_op jit(solution)/shard_map/ppermute | solution.py:19
  96.0 1.6 collective-permute-start.30
  99.2 4.7 %collective-permute-done.30 = bf16[128,768]{0,1:T(8,128)(2,1)S(1)} collective-permute-done((bf16[128,768]{0,1:T(8,128)(2,1)S(1)}, bf16[128,768]{0,1:T(8,128)(2,1)S(1)}, u32[]{:S(2)}, u32[]{:S(2)}) %collective-permute-start.30) | collective-permute-done | bytes 196640 | tf_op jit(solution)/shard_map/ppermute | solution.py:19
  104.4 2.4 %collective-permute-done.31 = bf16[128,768]{0,1:T(8,128)(2,1)S(1)} collective-permute-done((bf16[128,768]{0,1:T(8,128)(2,1)S(1)}, bf16[128,768]{0,1:T(8,128)(2,1)S(1)}, u32[]{:S(2)}, u32[]{:S(2)}) %collective-permute-start.31) | collective-permute-done | bytes 196640 | tf_op jit(solution)/shard_map/ppermute | solution.py:19
  107.3 18.9 %all_gather.12 = bf16[512,768]{0,1:T(8,128)(2,1)S(1)} all-gather(bf16[128,768]{0,1:T(8,128)(2,1)S(1)} %fusion.50), channel_id=1, replica_groups=mesh['atoms'=8,'bands'=4] {'bands'}, dimensions={0}, use_global_device_ids=true | all-gather | bytes 983040 | tf_op jit(solution)/shard_map/all_gather | solution.py:90
  126.6 11.8 %psum.28 = f32[128]{0:T(128)S(1)} all-reduce(f32[128]{0:T(128)S(1)} %get-tuple-element.22), channel_id=1, replica_groups=mesh['atoms'=8,'bands'=4] {'atoms'}, use_global_device_ids=true, to_apply=%region_5.6 | all-reduce | flops 128 | bytes 1024 | tf_op jit(solution)/shard_map/psum | solution.py:94
  138.5 17.6 %all_gather.13 = bf16[512,768]{0,1:T(8,128)(2,1)S(1)} all-gather(bf16[128,768]{0,1:T(8,128)(2,1)S(1)} %fusion.53), channel_id=1, replica_groups=mesh['atoms'=8,'bands'=4] {'bands'}, dimensions={0}, use_global_device_ids=true | all-gather | bytes 983040 | tf_op jit(solution)/shard_map/all_gather | solution.py:90
  156.4 11.8 %psum.29 = f32[128]{0:T(128)S(1)} all-reduce(f32[128]{0:T(128)S(1)} %get-tuple-element.24), channel_id=1, replica_groups=mesh['atoms'=8,'bands'=4] {'atoms'}, use_global_device_ids=true, to_apply=%region_7.8 | all-reduce | flops 128 | bytes 1024 | tf_op jit(solution)/shard_map/psum | solution.py:94
  168.3 17.6 %all_gather.14 = bf16[512,768]{0,1:T(8,128)(2,1)S(1)} all-gather(bf16[128,768]{0,1:T(8,128)(2,1)S(1)} %fusion.54), channel_id=1, replica_groups=mesh['atoms'=8,'bands'=4] {'bands'}, dimensions={0}, use_global_device_ids=true | all-gather | bytes 983040 | tf_op jit(solution)/shard_map/all_gather | solution.py:90
  186.2 11.8 %psum.30 = f32[128]{0:T(128)S(1)} all-reduce(f32[128]{0:T(128)S(1)} %get-tuple-element.26), channel_id=1, replica_groups=mesh['atoms'=8,'bands'=4] {'atoms'}, use_global_device_ids=true, to_apply=%region_9.10 | all-reduce | flops 128 | bytes 1024 | tf_op jit(solution)/shard_map/psum | solution.py:94
  198.1 17.6 %all_gather.15 = bf16[512,768]{0,1:T(8,128)(2,1)S(1)} all-gather(bf16[128,768]{0,1:T(8,128)(2,1)S(1)} %fusion.55), channel_id=1, replica_groups=mesh['atoms'=8,'bands'=4] {'bands'}, dimensions={0}, use_global_device_ids=true | all-gather | bytes 983040 | tf_op jit(solution)/shard_map/all_gather | solution.py:90
  216.0 11.8 %psum.31 = f32[128]{0:T(128)S(1)} all-reduce(f32[128]{0:T(128)S(1)} %get-tuple-element.28), channel_id=1, replica_groups=mesh['atoms'=8,'bands'=4] {'atoms'}, use_global_device_ids=true, to_apply=%region_11.12 | all-reduce | flops 128 | bytes 1024 | tf_op jit(solution)/shard_map/psum | solution.py:94
  (122 shorter events, 44.4 us)
Async XLA Ops:
  0.0 23.2 %collective-permute-start.2 = (bf16[128,768]{1,0:T(8,128)(2,1)}, bf16[128,768]{1,0:T(8,128)(2,1)}, u32[]{:S(2)}, u32[]{:S(2)}) collective-permute-start(bf16[128,768]{1,0:T(8,128)(2,1)} %param.6), channel_id=1, source_target_pairs={{0,8},{4,12},{8,0},{12,4},{16,24},{20,28},{24,16},{28,20},{1,9},{5... | collective-permute-start | bytes 589832 | tf_op jit(solution)/shard_map/ppermute | solution.py:19
  2.9 21.7 %collective-permute-start = (bf16[128,768]{1,0:T(8,128)(2,1)}, bf16[128,768]{1,0:T(8,128)(2,1)}, u32[]{:S(2)}, u32[]{:S(2)}) collective-permute-start(bf16[128,768]{1,0:T(8,128)(2,1)} %param.6), channel_id=1, source_target_pairs={{0,4},{4,0},{8,12},{12,8},{16,20},{20,16},{24,28},{28,24},{1,5},{5... | collective-permute-start | bytes 589832 | tf_op jit(solution)/shard_map/ppermute | solution.py:19
  9.6 15.1 %collective-permute-start.1 = (bf16[128,768]{0,1:T(8,128)(2,1)}, bf16[128,768]{0,1:T(8,128)(2,1)}, u32[]{:S(2)}, u32[]{:S(2)}) collective-permute-start(bf16[128,768]{0,1:T(8,128)(2,1)} %fusion.51), channel_id=1, source_target_pairs={{0,4},{4,0},{8,12},{12,8},{16,20},{20,16},{24,28},{28,24},{1,5},{5... | collective-permute-start | bytes 589832 | tf_op jit(solution)/shard_map/ppermute | solution.py:19
  13.0 11.6 %collective-permute-start.3 = (bf16[128,768]{0,1:T(8,128)(2,1)}, bf16[128,768]{0,1:T(8,128)(2,1)}, u32[]{:S(2)}, u32[]{:S(2)}) collective-permute-start(bf16[128,768]{0,1:T(8,128)(2,1)} %fusion.52), channel_id=1, source_target_pairs={{0,8},{4,12},{8,0},{12,4},{16,24},{20,28},{24,16},{28,20},{1,9},{5... | collective-permute-start | bytes 589832 | tf_op jit(solution)/shard_map/ppermute | solution.py:19
  26.9 7.7 %collective-permute-start.6 = (bf16[128,768]{0,1:T(8,128)(2,1)S(1)}, bf16[128,768]{0,1:T(8,128)(2,1)S(1)}, u32[]{:S(2)}, u32[]{:S(2)}) collective-permute-start(bf16[128,768]{0,1:T(8,128)(2,1)S(1)} %get-tuple-element.8), channel_id=1, source_target_pairs={{0,8},{4,12},{8,0},{12,4},{16,24},{20,28},{24,16},{28,20},{1,9},{5... | collective-permute-start | bytes 589832 | tf_op jit(solution)/shard_map/ppermute | solution.py:19
  29.6 8.4 %collective-permute-start.4 = (bf16[128,768]{0,1:T(8,128)(2,1)S(1)}, bf16[128,768]{0,1:T(8,128)(2,1)S(1)}, u32[]{:S(2)}, u32[]{:S(2)}) collective-permute-start(bf16[128,768]{0,1:T(8,128)(2,1)S(1)} %get-tuple-element.8), channel_id=1, source_target_pairs={{0,4},{4,0},{8,12},{12,8},{16,20},{20,16},{24,28},{28,24},{1,5},{5... | collective-permute-start | bytes 589832 | tf_op jit(solution)/shard_map/ppermute | solution.py:19
  29.6 5.5 %collective-permute-start.5 = (bf16[128,768]{0,1:T(8,128)(2,1)S(1)}, bf16[128,768]{0,1:T(8,128)(2,1)S(1)}, u32[]{:S(2)}, u32[]{:S(2)}) collective-permute-start(bf16[128,768]{0,1:T(8,128)(2,1)S(1)} %convolution_convert_fusion.13), channel_id=1, source_target_pairs={{0,4},{4,0},{8,12},{12,8},{16,20},{20,16},{24,28},{28,24},{1,5},{5... | collective-permute-start | bytes 589832 | tf_op jit(solution)/shard_map/ppermute | solution.py:19
  30.1 7.8 %collective-permute-start.7 = (bf16[128,768]{0,1:T(8,128)(2,1)S(1)}, bf16[128,768]{0,1:T(8,128)(2,1)S(1)}, u32[]{:S(2)}, u32[]{:S(2)}) collective-permute-start(bf16[128,768]{0,1:T(8,128)(2,1)S(1)} %convolution_convert_fusion.12), channel_id=1, source_target_pairs={{0,8},{4,12},{8,0},{12,4},{16,24},{20,28},{24,16},{28,20},{1,9},{5... | collective-permute-start | bytes 589832 | tf_op jit(solution)/shard_map/ppermute | solution.py:19
  39.0 6.6 %collective-permute-start.10 = (bf16[128,768]{0,1:T(8,128)(2,1)S(1)}, bf16[128,768]{0,1:T(8,128)(2,1)S(1)}, u32[]{:S(2)}, u32[]{:S(2)}) collective-permute-start(bf16[128,768]{0,1:T(8,128)(2,1)S(1)} %get-tuple-element.10), channel_id=1, source_target_pairs={{0,8},{4,12},{8,0},{12,4},{16,24},{20,28},{24,16},{28,20},{1,9},{5... | collective-permute-start | bytes 589832 | tf_op jit(solution)/shard_map/ppermute | solution.py:19
  41.4 7.9 %collective-permute-start.8 = (bf16[128,768]{0,1:T(8,128)(2,1)S(1)}, bf16[128,768]{0,1:T(8,128)(2,1)S(1)}, u32[]{:S(2)}, u32[]{:S(2)}) collective-permute-start(bf16[128,768]{0,1:T(8,128)(2,1)S(1)} %get-tuple-element.10), channel_id=1, source_target_pairs={{0,4},{4,0},{8,12},{12,8},{16,20},{20,16},{24,28},{28,24},{1,5},{5... | collective-permute-start | bytes 589832 | tf_op jit(solution)/shard_map/ppermute | solution.py:19
  41.5 4.6 %collective-permute-start.9 = (bf16[128,768]{0,1:T(8,128)(2,1)S(1)}, bf16[128,768]{0,1:T(8,128)(2,1)S(1)}, u32[]{:S(2)}, u32[]{:S(2)}) collective-permute-start(bf16[128,768]{0,1:T(8,128)(2,1)S(1)} %convolution_convert_fusion.11), channel_id=1, source_target_pairs={{0,4},{4,0},{8,12},{12,8},{16,20},{20,16},{24,28},{28,24},{1,5},{5... | collective-permute-start | bytes 589832 | tf_op jit(solution)/shard_map/ppermute | solution.py:19
  42.0 7.4 %collective-permute-start.11 = (bf16[128,768]{0,1:T(8,128)(2,1)S(1)}, bf16[128,768]{0,1:T(8,128)(2,1)S(1)}, u32[]{:S(2)}, u32[]{:S(2)}) collective-permute-start(bf16[128,768]{0,1:T(8,128)(2,1)S(1)} %convolution_convert_fusion.10), channel_id=1, source_target_pairs={{0,8},{4,12},{8,0},{12,4},{16,24},{20,28},{24,16},{28,20},{1,9},{5... | collective-permute-start | bytes 589832 | tf_op jit(solution)/shard_map/ppermute | solution.py:19
  50.5 7.9 %collective-permute-start.14 = (bf16[128,768]{0,1:T(8,128)(2,1)S(1)}, bf16[128,768]{0,1:T(8,128)(2,1)S(1)}, u32[]{:S(2)}, u32[]{:S(2)}) collective-permute-start(bf16[128,768]{0,1:T(8,128)(2,1)S(1)} %get-tuple-element.12), channel_id=1, source_target_pairs={{0,8},{4,12},{8,0},{12,4},{16,24},{20,28},{24,16},{28,20},{1,9},{5... | collective-permute-start | bytes 589832 | tf_op jit(solution)/shard_map/ppermute | solution.py:19
  52.5 8.8 %collective-permute-start.12 = (bf16[128,768]{0,1:T(8,128)(2,1)S(1)}, bf16[128,768]{0,1:T(8,128)(2,1)S(1)}, u32[]{:S(2)}, u32[]{:S(2)}) collective-permute-start(bf16[128,768]{0,1:T(8,128)(2,1)S(1)} %get-tuple-element.12), channel_id=1, source_target_pairs={{0,4},{4,0},{8,12},{12,8},{16,20},{20,16},{24,28},{28,24},{1,5},{5... | collective-permute-start | bytes 589832 | tf_op jit(solution)/shard_map/ppermute | solution.py:19
  52.6 6.3 %collective-permute-start.13 = (bf16[128,768]{0,1:T(8,128)(2,1)S(1)}, bf16[128,768]{0,1:T(8,128)(2,1)S(1)}, u32[]{:S(2)}, u32[]{:S(2)}) collective-permute-start(bf16[128,768]{0,1:T(8,128)(2,1)S(1)} %convolution_convert_fusion.9), channel_id=1, source_target_pairs={{0,4},{4,0},{8,12},{12,8},{16,20},{20,16},{24,28},{28,24},{1,5},{5... | collective-permute-start | bytes 589832 | tf_op jit(solution)/shard_map/ppermute | solution.py:19
  53.1 8.2 %collective-permute-start.15 = (bf16[128,768]{0,1:T(8,128)(2,1)S(1)}, bf16[128,768]{0,1:T(8,128)(2,1)S(1)}, u32[]{:S(2)}, u32[]{:S(2)}) collective-permute-start(bf16[128,768]{0,1:T(8,128)(2,1)S(1)} %convolution_convert_fusion.8), channel_id=1, source_target_pairs={{0,8},{4,12},{8,0},{12,4},{16,24},{20,28},{24,16},{28,20},{1,9},{5... | collective-permute-start | bytes 589832 | tf_op jit(solution)/shard_map/ppermute | solution.py:19
  62.3 7.1 %collective-permute-start.18 = (bf16[128,768]{0,1:T(8,128)(2,1)S(1)}, bf16[128,768]{0,1:T(8,128)(2,1)S(1)}, u32[]{:S(2)}, u32[]{:S(2)}) collective-permute-start(bf16[128,768]{0,1:T(8,128)(2,1)S(1)} %get-tuple-element.14), channel_id=1, source_target_pairs={{0,8},{4,12},{8,0},{12,4},{16,24},{20,28},{24,16},{28,20},{1,9},{5... | collective-permute-start | bytes 589832 | tf_op jit(solution)/shard_map/ppermute | solution.py:19
  63.5 8.8 %collective-permute-start.16 = (bf16[128,768]{0,1:T(8,128)(2,1)S(1)}, bf16[128,768]{0,1:T(8,128)(2,1)S(1)}, u32[]{:S(2)}, u32[]{:S(2)}) collective-permute-start(bf16[128,768]{0,1:T(8,128)(2,1)S(1)} %get-tuple-element.14), channel_id=1, source_target_pairs={{0,4},{4,0},{8,12},{12,8},{16,20},{20,16},{24,28},{28,24},{1,5},{5... | collective-permute-start | bytes 589832 | tf_op jit(solution)/shard_map/ppermute | solution.py:19
  63.6 6.3 %collective-permute-start.17 = (bf16[128,768]{0,1:T(8,128)(2,1)S(1)}, bf16[128,768]{0,1:T(8,128)(2,1)S(1)}, u32[]{:S(2)}, u32[]{:S(2)}) collective-permute-start(bf16[128,768]{0,1:T(8,128)(2,1)S(1)} %convolution_convert_fusion.7), channel_id=1, source_target_pairs={{0,4},{4,0},{8,12},{12,8},{16,20},{20,16},{24,28},{28,24},{1,5},{5... | collective-permute-start | bytes 589832 | tf_op jit(solution)/shard_map/ppermute | solution.py:19
  64.1 8.2 %collective-permute-start.19 = (bf16[128,768]{0,1:T(8,128)(2,1)S(1)}, bf16[128,768]{0,1:T(8,128)(2,1)S(1)}, u32[]{:S(2)}, u32[]{:S(2)}) collective-permute-start(bf16[128,768]{0,1:T(8,128)(2,1)S(1)} %convolution_convert_fusion.6), channel_id=1, source_target_pairs={{0,8},{4,12},{8,0},{12,4},{16,24},{20,28},{24,16},{28,20},{1,9},{5... | collective-permute-start | bytes 589832 | tf_op jit(solution)/shard_map/ppermute | solution.py:19
  73.4 7.0 %collective-permute-start.22 = (bf16[128,768]{0,1:T(8,128)(2,1)S(1)}, bf16[128,768]{0,1:T(8,128)(2,1)S(1)}, u32[]{:S(2)}, u32[]{:S(2)}) collective-permute-start(bf16[128,768]{0,1:T(8,128)(2,1)S(1)} %get-tuple-element.16), channel_id=1, source_target_pairs={{0,8},{4,12},{8,0},{12,4},{16,24},{20,28},{24,16},{28,20},{1,9},{5... | collective-permute-start | bytes 589832 | tf_op jit(solution)/shard_map/ppermute | solution.py:19
  74.6 8.7 %collective-permute-start.20 = (bf16[128,768]{0,1:T(8,128)(2,1)S(1)}, bf16[128,768]{0,1:T(8,128)(2,1)S(1)}, u32[]{:S(2)}, u32[]{:S(2)}) collective-permute-start(bf16[128,768]{0,1:T(8,128)(2,1)S(1)} %get-tuple-element.16), channel_id=1, source_target_pairs={{0,4},{4,0},{8,12},{12,8},{16,20},{20,16},{24,28},{28,24},{1,5},{5... | collective-permute-start | bytes 589832 | tf_op jit(solution)/shard_map/ppermute | solution.py:19
  74.7 6.1 %collective-permute-start.21 = (bf16[128,768]{0,1:T(8,128)(2,1)S(1)}, bf16[128,768]{0,1:T(8,128)(2,1)S(1)}, u32[]{:S(2)}, u32[]{:S(2)}) collective-permute-start(bf16[128,768]{0,1:T(8,128)(2,1)S(1)} %convolution_convert_fusion.5), channel_id=1, source_target_pairs={{0,4},{4,0},{8,12},{12,8},{16,20},{20,16},{24,28},{28,24},{1,5},{5... | collective-permute-start | bytes 589832 | tf_op jit(solution)/shard_map/ppermute | solution.py:19
  75.2 8.1 %collective-permute-start.23 = (bf16[128,768]{0,1:T(8,128)(2,1)S(1)}, bf16[128,768]{0,1:T(8,128)(2,1)S(1)}, u32[]{:S(2)}, u32[]{:S(2)}) collective-permute-start(bf16[128,768]{0,1:T(8,128)(2,1)S(1)} %convolution_convert_fusion.4), channel_id=1, source_target_pairs={{0,8},{4,12},{8,0},{12,4},{16,24},{20,28},{24,16},{28,20},{1,9},{5... | collective-permute-start | bytes 589832 | tf_op jit(solution)/shard_map/ppermute | solution.py:19
  84.4 6.1 %collective-permute-start.26 = (bf16[128,768]{0,1:T(8,128)(2,1)S(1)}, bf16[128,768]{0,1:T(8,128)(2,1)S(1)}, u32[]{:S(2)}, u32[]{:S(2)}) collective-permute-start(bf16[128,768]{0,1:T(8,128)(2,1)S(1)} %get-tuple-element.18), channel_id=1, source_target_pairs={{0,8},{4,12},{8,0},{12,4},{16,24},{20,28},{24,16},{28,20},{1,9},{5... | collective-permute-start | bytes 589832 | tf_op jit(solution)/shard_map/ppermute | solution.py:19
  86.4 7.9 %collective-permute-start.24 = (bf16[128,768]{0,1:T(8,128)(2,1)S(1)}, bf16[128,768]{0,1:T(8,128)(2,1)S(1)}, u32[]{:S(2)}, u32[]{:S(2)}) collective-permute-start(bf16[128,768]{0,1:T(8,128)(2,1)S(1)} %get-tuple-element.18), channel_id=1, source_target_pairs={{0,4},{4,0},{8,12},{12,8},{16,20},{20,16},{24,28},{28,24},{1,5},{5... | collective-permute-start | bytes 589832 | tf_op jit(solution)/shard_map/ppermute | solution.py:19
  86.5 4.5 %collective-permute-start.25 = (bf16[128,768]{0,1:T(8,128)(2,1)S(1)}, bf16[128,768]{0,1:T(8,128)(2,1)S(1)}, u32[]{:S(2)}, u32[]{:S(2)}) collective-permute-start(bf16[128,768]{0,1:T(8,128)(2,1)S(1)} %convolution_convert_fusion.3), channel_id=1, source_target_pairs={{0,4},{4,0},{8,12},{12,8},{16,20},{20,16},{24,28},{28,24},{1,5},{5... | collective-permute-start | bytes 589832 | tf_op jit(solution)/shard_map/ppermute | solution.py:19
  87.0 7.3 %collective-permute-start.27 = (bf16[128,768]{0,1:T(8,128)(2,1)S(1)}, bf16[128,768]{0,1:T(8,128)(2,1)S(1)}, u32[]{:S(2)}, u32[]{:S(2)}) collective-permute-start(bf16[128,768]{0,1:T(8,128)(2,1)S(1)} %convolution_convert_fusion.2), channel_id=1, source_target_pairs={{0,8},{4,12},{8,0},{12,4},{16,24},{20,28},{24,16},{28,20},{1,9},{5... | collective-permute-start | bytes 589832 | tf_op jit(solution)/shard_map/ppermute | solution.py:19
  96.0 7.9 %collective-permute-start.30 = (bf16[128,768]{0,1:T(8,128)(2,1)S(1)}, bf16[128,768]{0,1:T(8,128)(2,1)S(1)}, u32[]{:S(2)}, u32[]{:S(2)}) collective-permute-start(bf16[128,768]{0,1:T(8,128)(2,1)S(1)} %get-tuple-element.20), channel_id=1, source_target_pairs={{0,8},{4,12},{8,0},{12,4},{16,24},{20,28},{24,16},{28,20},{1,9},{5... | collective-permute-start | bytes 589832 | tf_op jit(solution)/shard_map/ppermute | solution.py:19
  97.6 9.2 %collective-permute-start.28 = (bf16[128,768]{0,1:T(8,128)(2,1)S(1)}, bf16[128,768]{0,1:T(8,128)(2,1)S(1)}, u32[]{:S(2)}, u32[]{:S(2)}) collective-permute-start(bf16[128,768]{0,1:T(8,128)(2,1)S(1)} %get-tuple-element.20), channel_id=1, source_target_pairs={{0,4},{4,0},{8,12},{12,8},{16,20},{20,16},{24,28},{28,24},{1,5},{5... | collective-permute-start | bytes 589832 | tf_op jit(solution)/shard_map/ppermute | solution.py:19
  97.6 6.8 %collective-permute-start.29 = (bf16[128,768]{0,1:T(8,128)(2,1)S(1)}, bf16[128,768]{0,1:T(8,128)(2,1)S(1)}, u32[]{:S(2)}, u32[]{:S(2)}) collective-permute-start(bf16[128,768]{0,1:T(8,128)(2,1)S(1)} %convolution_convert_fusion.1), channel_id=1, source_target_pairs={{0,4},{4,0},{8,12},{12,8},{16,20},{20,16},{24,28},{28,24},{1,5},{5... | collective-permute-start | bytes 589832 | tf_op jit(solution)/shard_map/ppermute | solution.py:19
  98.1 8.7 %collective-permute-start.31 = (bf16[128,768]{0,1:T(8,128)(2,1)S(1)}, bf16[128,768]{0,1:T(8,128)(2,1)S(1)}, u32[]{:S(2)}, u32[]{:S(2)}) collective-permute-start(bf16[128,768]{0,1:T(8,128)(2,1)S(1)} %convolution_convert_fusion), channel_id=1, source_target_pairs={{0,8},{4,12},{8,0},{12,4},{16,24},{20,28},{24,16},{28,20},{1,9},{5... | collective-permute-start | bytes 589832 | tf_op jit(solution)/shard_map/ppermute | solution.py:19
  (7 other events, 36.0 us)
where the time goes:
time: 229 us
  blocking collectives  119 us (52%)
  waiting for transfers between devices  42.9 us (19%)
  matrix products  32.2 us (14%)
  starting transfers between devices  22 us (10%)
  local copies, waits for them, and re-layouts  6.76 us (3%)
  other arithmetic  5.57 us (2%)
    all_gather x4, blocking collectives, body(): lax.all_gather(rounded, 'bands', axis=0, tiled=True)  71.6 us
    psum x4, blocking collectives, body(): squares = lax.psum(jnp.sum(mixed_rows * mixed_rows, axis=1), 'atoms')  47.2 us
    ppermute x32, waiting for transfers between devices, swapped(): return lax.ppermute(value, axis, pairs)  42.9 us
    ppermute x32, starting transfers between devices, swapped(): return lax.ppermute(value, axis, pairs)  22 us
    dot_general x16, matrix products, apply_operator(): sent_term = jnp.dot(values, pair_mat, preferred_element_type=jnp.float32)  10.7 us
    dot_general x16, matrix products, apply_operator(): lax.dot_general(other_rows, pair_mat, (((1,), (1,)), ((), ())), preferred...  9.66 us
    dot_general x8, matrix products, apply_operator(): result = jnp.dot(values, diag_sym, preferred_element_type=jnp.float32)  4.85 us
  transfers between devices with their start and end apart: 32, of which 14 were waited for; matrix products, arithmetic and copies ran while one was open for 14% of the time, Pallas kernels for 0%

commit v1 on v0

--- a/solution.py
+++ b/solution.py
@@ -17,6 +17,26 @@
     mask = 2**stride
     pairs = [(source, source ^ mask) for source in range(lax.axis_size(axis))]
     return lax.ppermute(value, axis, pairs)
+
+
+def gather_bands(value):
+    count = lax.axis_size("bands")
+    here = lax.axis_index("bands")
+    pieces = [value]
+    for shift in range(1, count):
+        pairs = [(source, (source + shift) % count) for source in range(count)]
+        pieces.append(lax.ppermute(value, "bands", pairs))
+    order = (here - jnp.arange(count, dtype=jnp.int32)) % count
+    return jnp.take(jnp.stack(pieces), order, axis=0)
+
+
+def atoms_sum(value):
+    count = lax.axis_size("atoms")
+    stride = 0
+    while (1 << stride) < count:
+        value = value + swapped(value, "atoms", stride)
+        stride += 1
+    return value
 
 
 def atom_onehot(atom_counts, length_total):
@@ -81,20 +101,31 @@
         following = 2.0 * (applied - filter_center * current) / filter_half - previous
         previous, current = (current, following)
     total_orbitals = orb_dev * lax.axis_size("atoms")
-    basis_rows = current
-    for rotation_index in range(ROTS):
-        rounded = basis_rows.astype(jnp.bfloat16)
-        local_cols = rotations[rotation_index]
+    band_count = lax.axis_size("bands")
+    local_bands = current.shape[0]
+    rot_steps, all_bands, _ = rotations.shape
+    full_rot = gather_bands(rotations)
+    full_rot = jnp.transpose(full_rot, (1, 2, 0, 3)).reshape(rot_steps, all_bands, all_bands)
+    basis_all = gather_bands(current.astype(jnp.bfloat16)).reshape(all_bands, orb_dev)
+    for rotation_index in range(ROTS - 1):
         mixed_rows = lax.dot_general(
-            local_cols,
-            lax.all_gather(rounded, "bands", axis=0, tiled=True),
+            full_rot[rotation_index],
+            basis_all,
             (((0,), (0,)), ((), ())),
             preferred_element_type=jnp.float32,
         )
-        squares = lax.psum(jnp.sum(mixed_rows * mixed_rows, axis=1), "atoms")
+        squares = atoms_sum(jnp.sum(mixed_rows * mixed_rows, axis=1))
         col_norm = jnp.sqrt(squares / total_orbitals + norm_eps)
-        basis_rows = mixed_rows / col_norm[:, None]
-    return basis_rows
+        basis_all = (mixed_rows / col_norm[:, None]).astype(jnp.bfloat16)
+    mixed_rows = lax.dot_general(
+        rotations[ROTS - 1],
+        basis_all,
+        (((0,), (0,)), ((), ())),
+        preferred_element_type=jnp.float32,
+    )
+    squares = atoms_sum(jnp.sum(mixed_rows * mixed_rows, axis=1))
+    col_norm = jnp.sqrt(squares / total_orbitals + norm_eps)
+    return mixed_rows / col_norm[:, None]
 
 
 def solution(mesh):

time: 229 us -> 190 us (0.83)
  blocking collectives: 119 us -> 0 us
  waiting for transfers between devices: 42.9 us -> 76.3 us
  starting transfers between devices: 22 us -> 41.4 us
  matrix products: 32.2 us -> 45.8 us
  other arithmetic: 5.57 us -> 12.4 us
  local copies, waits for them, and re-layouts: 6.76 us -> 11.1 us
    all_gather x4 -> x0, blocking collectives: 71.6 us -> none  [body(): lax.all_gather(rounded, 'bands', axis=0, tiled=True)]
    psum x4 -> x0, blocking collectives: 47.2 us -> none  [body(): squares = lax.psum(jnp.sum(mixed_rows * mixed_rows, axis=1), 'atoms')]
    ppermute x32 -> x44, waiting for transfers between devices: 42.9 us -> 64.2 us  [swapped(): return lax.ppermute(value, axis, pairs)]
    ppermute x0 -> x6, waiting for transfers between devices: none -> 12.1 us  [gather_bands(): pieces.append(lax.ppermute(value, 'bands', pairs))]
    ppermute x32 -> x44, starting transfers between devices: 22 us -> 32.1 us  [swapped(): return lax.ppermute(value, axis, pairs)]
    ppermute x0 -> x6, starting transfers between devices: none -> 9.39 us  [gather_bands(): pieces.append(lax.ppermute(value, 'bands', pairs))]
    dot_general x4, matrix products: 1.5 us -> 8.64 us  [the longest x3 7.22 us: body(): lax.dot_general(full_rot[rotation_index], basis_all, (((0,), (0,)), ((),...]
    gather x0 -> x2, local copies, waits for them, and re-layouts: none -> 4.43 us  [gather_bands(): return jnp.take(jnp.stack(pieces), order, axis=0)]
  transfers between devices with their start and end apart: 32 -> 50, of which waited for: 14 -> 28; matrix products, arithmetic and copies ran while one was open for 14% -> 26% of each run, Pallas kernels for 0% -> 0%
where the time goes in v1:
time: 190 us; the launch traced here: 188 us
  waiting for transfers between devices  76.3 us (40%)
  matrix products  45.8 us (24%)
  starting transfers between devices  41.4 us (22%)
  other arithmetic  12.4 us (7%)
  local copies, waits for them, and re-layouts  11.1 us (6%)
    ppermute x44, waiting for transfers between devices, swapped(): return lax.ppermute(value, axis, pairs)  64.2 us
    ppermute x44, starting transfers between devices, swapped(): return lax.ppermute(value, axis, pairs)  32.1 us
    dot_general x16, matrix products, apply_operator(): sent_term = jnp.dot(values, pair_mat, preferred_element_type=jnp.float32)  13.2 us
    dot_general x16, matrix products, apply_operator(): lax.dot_general(other_rows, pair_mat, (((1,), (1,)), ((), ())), preferred...  12.7 us
    ppermute x6, waiting for transfers between devices, gather_bands(): pieces.append(lax.ppermute(value, 'bands', pairs))  12.1 us
    ppermute x6, starting transfers between devices, gather_bands(): pieces.append(lax.ppermute(value, 'bands', pairs))  9.39 us
    dot_general x3, matrix products, body(): lax.dot_general(full_rot[rotation_index], basis_all, (((0,), (0,)), ((),...  7.22 us
    dot_general x8, matrix products, apply_operator(): result = jnp.dot(values, diag_sym, preferred_element_type=jnp.float32)  6.33 us
  transfers between devices with their start and end apart: 50, of which 28 were waited for; matrix products, arithmetic and copies ran while one was open for 26% of the time, Pallas kernels for 0%

profile of v1, /device:TPU:0, one launch (start us, length us, event | category | flops | bytes accessed | tf_op | source)
XLA Modules:
  0.0 187.7 jit_solution(8509550070755075304)
XLA Ops:
  0.0 2.9 %collective-permute-start.5 = (bf16[128,768]{1,0:T(8,128)(2,1)}, bf16[128,768]{1,0:T(8,128)(2,1)}, u32[]{:S(2)}, u32[]{:S(2)}) collective-permute-start(bf16[128,768]{1,0:T(8,128)(2,1)} %param.6), channel_id=1, source_target_pairs={{0,8},{4,12},{8,0},{12,4},{16,24},{20,28},{24,16},{28,20},{1,9},{5... | collective-permute-start | bytes 589832 | tf_op jit(solution)/shard_map/ppermute | solution.py:19
  4.5 2.6 %collective-permute-start.1 = (bf16[4,512,128]{2,1,0:T(8,128)(2,1)}, bf16[4,512,128]{2,1,0:T(8,128)(2,1)}, u32[]{:S(2)}, u32[]{:S(2)}) collective-permute-start(bf16[4,512,128]{2,1,0:T(8,128)(2,1)} %param.11), channel_id=1, source_target_pairs={{0,2},{1,3},{2,0},{3,1},{4,6},{5,7},{6,4},{7,5},{8,10},{9,11},{10,... | collective-permute-start | bytes 1572872 | tf_op jit(solution)/shard_map/ppermute | solution.py:28
  10.1 2.5 %fusion.1 = bf16[768,768]{1,0:T(8,128)(2,1)S(1)} fusion(f32[768,4]{0,1:T(4,128)S(1)} %fusion.62, bf16[2,768,768]{2,1,0:T(8,128)(2,1)} %param.8, s32[4]{0:T(128)S(1)} %bitcast.160, s32[4]{0:T(128)S(1)} %bitcast_subtract_fusion.2), kind=kOutput, calls=%fused_computation.5 | convolution fusion | flops 30090240 | bytes 2371616 | tf_op jit(solution)/shard_map/dot_general | solution.py:90
  19.2 2.8 %fusion.2 = bf16[768,768]{1,0:T(8,128)(2,1)S(1)} fusion(f32[768,768]{0,1:T(8,128)} %copy.129, f32[768]{0:T(1024)S(1)} %select_reduce_fusion, bf16[768,768]{1,0:T(8,128)(2,1)} %param.7), kind=kLoop, calls=%fused_computation.7 | loop fusion | flops 5308416 | bytes 4721664 | tf_op jit(solution)/shard_map/convert_element_type | solution.py:81
  26.9 5.4 %collective-permute-done.6 = bf16[128,768]{0,1:T(8,128)(2,1)S(1)} collective-permute-done((bf16[128,768]{0,1:T(8,128)(2,1)S(1)}, bf16[128,768]{0,1:T(8,128)(2,1)S(1)}, u32[]{:S(2)}, u32[]{:S(2)}) %collective-permute-start.6) | collective-permute-done | bytes 196640 | tf_op jit(solution)/shard_map/ppermute | solution.py:19
  37.8 4.4 %collective-permute-done.9 = bf16[128,768]{0,1:T(8,128)(2,1)S(1)} collective-permute-done((bf16[128,768]{0,1:T(8,128)(2,1)S(1)}, bf16[128,768]{0,1:T(8,128)(2,1)S(1)}, u32[]{:S(2)}, u32[]{:S(2)}) %collective-permute-start.9) | collective-permute-done | bytes 196640 | tf_op jit(solution)/shard_map/ppermute | solution.py:19
  42.7 2.6 %collective-permute-done.10 = bf16[128,768]{0,1:T(8,128)(2,1)S(1)} collective-permute-done((bf16[128,768]{0,1:T(8,128)(2,1)S(1)}, bf16[128,768]{0,1:T(8,128)(2,1)S(1)}, u32[]{:S(2)}, u32[]{:S(2)}) %collective-permute-start.10) | collective-permute-done | bytes 196640 | tf_op jit(solution)/shard_map/ppermute | solution.py:19
  47.9 2.2 %convolution_convert_fusion.11 = bf16[128,768]{0,1:T(8,128)(2,1)} fusion(bf16[128,768]{0,1:T(8,128)(2,1)} %get-tuple-element.13, bf16[768,768]{1,0:T(8,128)(2,1)S(1)} %fusion.1), kind=kOutput, calls=%fused_computation.85 | convolution fusion | flops 151093248 | bytes 1572864 | tf_op jit(solution)/shard_map/dot_general | solution.py:66
  50.6 2.2 %convolution_convert_fusion.10 = bf16[128,768]{0,1:T(8,128)(2,1)} fusion(bf16[128,768]{0,1:T(8,128)(2,1)} %get-tuple-element.13, bf16[768,768]{1,0:T(8,128)(2,1)S(1)} %fusion), kind=kOutput, calls=%fused_computation.84 | convolution fusion | flops 151093248 | bytes 1572864 | tf_op jit(solution)/shard_map/dot_general | solution.py:66
  52.9 2.3 %fusion.91 = f32[128,768]{0,1:T(8,128)} fusion(bf16[128,768]{0,1:T(8,128)(2,1)} %get-tuple-element.13, bf16[768,768]{1,0:T(8,128)(2,1)S(1)} %fusion.2), kind=kOutput, calls=%fused_computation.159 | convolution fusion | flops 150994944 | bytes 1769472 | tf_op jit(solution)/shard_map/dot_general | solution.py:59
  58.0 2.8 %pad_maximum_fusion = bf16[4,4,512,128]{3,2,1,0:T(8,128)(2,1)} fusion(bf16[1,4,512,128]{3,2,1,0:T(8,128)(2,1)S(1)} %bitcast.156, bf16[1,4,512,128]{3,2,1,0:T(8,128)(2,1)} %bitcast.2, bf16[1,4,512,128]{3,2,1,0:T(8,128)(2,1)} %bitcast.1, bf16[1,4,512,128]{3,2,1,0:T(8,128)(2,1)S(1)} %bitcast.155), kind=kLoop, calls=%fused_computation.9 | loop fusion | flops 3145728 | bytes 4194304 | tf_op jit(solution)/shard_map/stack | solution.py:30
  60.8 3.7 %gather_fusion = bf16[4,4,512,128]{3,2,1,0:T(8,128)(2,1)} fusion(bf16[4,4,512,128]{3,2,1,0:T(8,128)(2,1)} %pad_maximum_fusion, s32[1024]{0:T(1024)S(1)} %pad_clamp_fusion), kind=kCustom, calls=%fused_computation | custom fusion | bytes 4194320 | tf_op jit(solution)/shard_map/jit(_take)/gather | solution.py:30
  74.1 3.3 %collective-permute-done.17 = bf16[128,768]{0,1:T(8,128)(2,1)S(1)} collective-permute-done((bf16[128,768]{0,1:T(8,128)(2,1)S(1)}, bf16[128,768]{0,1:T(8,128)(2,1)S(1)}, u32[]{:S(2)}, u32[]{:S(2)}) %collective-permute-start.17) | collective-permute-done | bytes 196640 | tf_op jit(solution)/shard_map/ppermute | solution.py:19
  77.9 2.4 %collective-permute-done.18 = bf16[128,768]{0,1:T(8,128)(2,1)S(1)} collective-permute-done((bf16[128,768]{0,1:T(8,128)(2,1)S(1)}, bf16[128,768]{0,1:T(8,128)(2,1)S(1)}, u32[]{:S(2)}, u32[]{:S(2)}) %collective-permute-start.18) | collective-permute-done | bytes 196640 | tf_op jit(solution)/shard_map/ppermute | solution.py:19
  85.2 3.2 %collective-permute-done.21 = bf16[128,768]{0,1:T(8,128)(2,1)S(1)} collective-permute-done((bf16[128,768]{0,1:T(8,128)(2,1)S(1)}, bf16[128,768]{0,1:T(8,128)(2,1)S(1)}, u32[]{:S(2)}, u32[]{:S(2)}) %collective-permute-start.21) | collective-permute-done | bytes 196640 | tf_op jit(solution)/shard_map/ppermute | solution.py:19
  88.8 2.4 %collective-permute-done.22 = bf16[128,768]{0,1:T(8,128)(2,1)S(1)} collective-permute-done((bf16[128,768]{0,1:T(8,128)(2,1)S(1)}, bf16[128,768]{0,1:T(8,128)(2,1)S(1)}, u32[]{:S(2)}, u32[]{:S(2)}) %collective-permute-start.22) | collective-permute-done | bytes 196640 | tf_op jit(solution)/shard_map/ppermute | solution.py:19
  96.2 2.4 %collective-permute-done.25 = bf16[128,768]{0,1:T(8,128)(2,1)S(1)} collective-permute-done((bf16[128,768]{0,1:T(8,128)(2,1)S(1)}, bf16[128,768]{0,1:T(8,128)(2,1)S(1)}, u32[]{:S(2)}, u32[]{:S(2)}) %collective-permute-start.25) | collective-permute-done | bytes 196640 | tf_op jit(solution)/shard_map/ppermute | solution.py:19
  99.3 3.0 %collective-permute-done.26 = bf16[128,768]{0,1:T(8,128)(2,1)S(1)} collective-permute-done((bf16[128,768]{0,1:T(8,128)(2,1)S(1)}, bf16[128,768]{0,1:T(8,128)(2,1)S(1)}, u32[]{:S(2)}, u32[]{:S(2)}) %collective-permute-start.26) | collective-permute-done | bytes 196640 | tf_op jit(solution)/shard_map/ppermute | solution.py:19
  107.2 3.7 %collective-permute-done.29 = bf16[128,768]{0,1:T(8,128)(2,1)S(1)} collective-permute-done((bf16[128,768]{0,1:T(8,128)(2,1)S(1)}, bf16[128,768]{0,1:T(8,128)(2,1)S(1)}, u32[]{:S(2)}, u32[]{:S(2)}) %collective-permute-start.29) | collective-permute-done | bytes 196640 | tf_op jit(solution)/shard_map/ppermute | solution.py:19
  111.4 2.7 %collective-permute-done.30 = bf16[128,768]{0,1:T(8,128)(2,1)S(1)} collective-permute-done((bf16[128,768]{0,1:T(8,128)(2,1)S(1)}, bf16[128,768]{0,1:T(8,128)(2,1)S(1)}, u32[]{:S(2)}, u32[]{:S(2)}) %collective-permute-start.30) | collective-permute-done | bytes 196640 | tf_op jit(solution)/shard_map/ppermute | solution.py:19
  119.0 4.7 %collective-permute-done.33 = bf16[128,768]{0,1:T(8,128)(2,1)S(1)} collective-permute-done((bf16[128,768]{0,1:T(8,128)(2,1)S(1)}, bf16[128,768]{0,1:T(8,128)(2,1)S(1)}, u32[]{:S(2)}, u32[]{:S(2)}) %collective-permute-start.33) | collective-permute-done | bytes 196640 | tf_op jit(solution)/shard_map/ppermute | solution.py:19
  127.2 3.0 %collective-permute-start.36 = (bf16[128,768]{0,1:T(8,128)(2,1)S(1)}, bf16[128,768]{0,1:T(8,128)(2,1)S(1)}, u32[]{:S(2)}, u32[]{:S(2)}) collective-permute-start(bf16[128,768]{0,1:T(8,128)(2,1)S(1)} %fusion.50), channel_id=1, source_target_pairs={{0,2},{1,3},{2,0},{3,1},{4,6},{5,7},{6,4},{7,5},{8,10},{9,11},{10,... | collective-permute-start | bytes 589832 | tf_op jit(solution)/shard_map/ppermute | solution.py:28
  130.7 5.5 %collective-permute-done.35 = bf16[128,768]{0,1:T(8,128)(2,1)S(1)} collective-permute-done((bf16[128,768]{0,1:T(8,128)(2,1)S(1)}, bf16[128,768]{0,1:T(8,128)(2,1)S(1)}, u32[]{:S(2)}, u32[]{:S(2)}) %collective-permute-start.35) | collective-permute-done | bytes 196640 | tf_op jit(solution)/shard_map/ppermute | solution.py:28
  136.2 5.7 %collective-permute-done.36 = bf16[128,768]{0,1:T(8,128)(2,1)S(1)} collective-permute-done((bf16[128,768]{0,1:T(8,128)(2,1)S(1)}, bf16[128,768]{0,1:T(8,128)(2,1)S(1)}, u32[]{:S(2)}, u32[]{:S(2)}) %collective-permute-start.36) | collective-permute-done | bytes 196640 | tf_op jit(solution)/shard_map/ppermute | solution.py:28
  148.7 2.5 %collective-permute-done.39 = f32[512]{0:T(512)S(1)} collective-permute-done((f32[512]{0:T(512)S(1)}, f32[512]{0:T(512)S(1)}, u32[]{:S(2)}, u32[]{:S(2)}) %collective-permute-start.39) | collective-permute-done | bytes 2080 | tf_op jit(solution)/shard_map/ppermute | solution.py:19
  154.8 3.3 %multiply_reduce_fusion.1 = (f32[512]{0:T(512)S(1)}, f32[512,768]{1,0:T(8,128)}) fusion(bf16[512,512]{0,1:T(8,128)(2,1)S(1)} %bitcast.153, f32[512,768]{1,0:T(8,128)} %get-tuple-element.26, f32[512]{0:T(512)S(1)} %add_sqrt_fusion.2), kind=kOutput, calls=%fused_computation.14 | convolution fusion | flops 404225536 | bytes 3674112 | tf_op jit(solution)/shard_map/dot_general | solution.py:111
  160.3 2.5 %collective-permute-done.42 = f32[512]{0:T(512)S(1)} collective-permute-done((f32[512]{0:T(512)S(1)}, f32[512]{0:T(512)S(1)}, u32[]{:S(2)}, u32[]{:S(2)}) %collective-permute-start.42) | collective-permute-done | bytes 2080 | tf_op jit(solution)/shard_map/ppermute | solution.py:19
  166.4 2.2 %multiply_reduce_fusion = (f32[512]{0:T(512)S(1)}, f32[512,768]{1,0:T(8,128)S(1)}) fusion(bf16[512,512]{0,1:T(8,128)(2,1)S(1)} %bitcast.154, f32[512,768]{1,0:T(8,128)} %get-tuple-element.28, f32[512]{0:T(512)S(1)} %add_sqrt_fusion.1), kind=kOutput, calls=%fused_computation.12 | convolution fusion | flops 404225536 | bytes 3674112 | tf_op jit(solution)/shard_map/dot_general | solution.py:111
  170.9 2.5 %collective-permute-done.45 = f32[512]{0:T(512)S(1)} collective-permute-done((f32[512]{0:T(512)S(1)}, f32[512]{0:T(512)S(1)}, u32[]{:S(2)}, u32[]{:S(2)}) %collective-permute-start.45) | collective-permute-done | bytes 2080 | tf_op jit(solution)/shard_map/ppermute | solution.py:19
  174.9 2.1 %collective-permute-done.46 = f32[512]{0:T(512)S(1)} collective-permute-done((f32[512]{0:T(512)S(1)}, f32[512]{0:T(512)S(1)}, u32[]{:S(2)}, u32[]{:S(2)}) %collective-permute-start.46) | collective-permute-done | bytes 2080 | tf_op jit(solution)/shard_map/ppermute | solution.py:19
  180.7 2.5 %collective-permute-done.48 = f32[128]{0:T(128)S(1)} collective-permute-done((f32[128]{0:T(128)S(1)}, f32[128]{0:T(128)S(1)}, u32[]{:S(2)}, u32[]{:S(2)}) %collective-permute-start.48) | collective-permute-done | bytes 544 | tf_op jit(solution)/shard_map/ppermute | solution.py:19
  184.7 2.0 %collective-permute-done.49 = f32[128]{0:T(128)S(1)} collective-permute-done((f32[128]{0:T(128)S(1)}, f32[128]{0:T(128)S(1)}, u32[]{:S(2)}, u32[]{:S(2)}) %collective-permute-start.49) | collective-permute-done | bytes 544 | tf_op jit(solution)/shard_map/ppermute | solution.py:19
  (185 shorter events, 89.1 us)
Async XLA Ops:
  0.0 24.8 %collective-permute-start.5 = (bf16[128,768]{1,0:T(8,128)(2,1)}, bf16[128,768]{1,0:T(8,128)(2,1)}, u32[]{:S(2)}, u32[]{:S(2)}) collective-permute-start(bf16[128,768]{1,0:T(8,128)(2,1)} %param.6), channel_id=1, source_target_pairs={{0,8},{4,12},{8,0},{12,4},{16,24},{20,28},{24,16},{28,20},{1,9},{5... | collective-permute-start | bytes 589832 | tf_op jit(solution)/shard_map/ppermute | solution.py:19
  2.9 29.3 %collective-permute-start.3 = (bf16[128,768]{1,0:T(8,128)(2,1)}, bf16[128,768]{1,0:T(8,128)(2,1)}, u32[]{:S(2)}, u32[]{:S(2)}) collective-permute-start(bf16[128,768]{1,0:T(8,128)(2,1)} %param.6), channel_id=1, source_target_pairs={{0,4},{4,0},{8,12},{12,8},{16,20},{20,16},{24,28},{28,24},{1,5},{5... | collective-permute-start | bytes 589832 | tf_op jit(solution)/shard_map/ppermute | solution.py:19
  2.9 52.2 %collective-permute-start = (bf16[4,512,128]{2,1,0:T(8,128)(2,1)}, bf16[4,512,128]{2,1,0:T(8,128)(2,1)}, u32[]{:S(2)}, u32[]{:S(2)}) collective-permute-start(bf16[4,512,128]{2,1,0:T(8,128)(2,1)} %param.11), channel_id=1, source_target_pairs={{0,1},{1,2},{2,3},{3,0},{4,5},{5,6},{6,7},{7,4},{8,9},{9,10},{10,1... | collective-permute-start | bytes 1572872 | tf_op jit(solution)/shard_map/ppermute | solution.py:28
  4.5 51.1 %collective-permute-start.1 = (bf16[4,512,128]{2,1,0:T(8,128)(2,1)}, bf16[4,512,128]{2,1,0:T(8,128)(2,1)}, u32[]{:S(2)}, u32[]{:S(2)}) collective-permute-start(bf16[4,512,128]{2,1,0:T(8,128)(2,1)} %param.11), channel_id=1, source_target_pairs={{0,2},{1,3},{2,0},{3,1},{4,6},{5,7},{6,4},{7,5},{8,10},{9,11},{10,... | collective-permute-start | bytes 1572872 | tf_op jit(solution)/shard_map/ppermute | solution.py:28
  13.8 13.0 %collective-permute-start.4 = (bf16[128,768]{0,1:T(8,128)(2,1)}, bf16[128,768]{0,1:T(8,128)(2,1)}, u32[]{:S(2)}, u32[]{:S(2)}) collective-permute-start(bf16[128,768]{0,1:T(8,128)(2,1)} %fusion.51), channel_id=1, source_target_pairs={{0,4},{4,0},{8,12},{12,8},{16,20},{20,16},{24,28},{28,24},{1,5},{5... | collective-permute-start | bytes 589832 | tf_op jit(solution)/shard_map/ppermute | solution.py:19
  24.8 7.4 %collective-permute-start.6 = (bf16[128,768]{0,1:T(8,128)(2,1)S(1)}, bf16[128,768]{0,1:T(8,128)(2,1)S(1)}, u32[]{:S(2)}, u32[]{:S(2)}) collective-permute-start(bf16[128,768]{0,1:T(8,128)(2,1)S(1)} %fusion.52), channel_id=1, source_target_pairs={{0,8},{4,12},{8,0},{12,4},{16,24},{20,28},{24,16},{28,20},{1,9},{5... | collective-permute-start | bytes 589832 | tf_op jit(solution)/shard_map/ppermute | solution.py:19
  34.3 7.9 %collective-permute-start.9 = (bf16[128,768]{0,1:T(8,128)(2,1)S(1)}, bf16[128,768]{0,1:T(8,128)(2,1)S(1)}, u32[]{:S(2)}, u32[]{:S(2)}) collective-permute-start(bf16[128,768]{0,1:T(8,128)(2,1)S(1)} %get-tuple-element.11), channel_id=1, source_target_pairs={{0,8},{4,12},{8,0},{12,4},{16,24},{20,28},{24,16},{28,20},{1,9},{5... | collective-permute-start | bytes 589832 | tf_op jit(solution)/shard_map/ppermute | solution.py:19
  35.5 11.1 %collective-permute-start.7 = (bf16[128,768]{0,1:T(8,128)(2,1)S(1)}, bf16[128,768]{0,1:T(8,128)(2,1)S(1)}, u32[]{:S(2)}, u32[]{:S(2)}) collective-permute-start(bf16[128,768]{0,1:T(8,128)(2,1)S(1)} %get-tuple-element.11), channel_id=1, source_target_pairs={{0,4},{4,0},{8,12},{12,8},{16,20},{20,16},{24,28},{28,24},{1,5},{5... | collective-permute-start | bytes 589832 | tf_op jit(solution)/shard_map/ppermute | solution.py:19
  35.6 9.6 %collective-permute-start.10 = (bf16[128,768]{0,1:T(8,128)(2,1)S(1)}, bf16[128,768]{0,1:T(8,128)(2,1)S(1)}, u32[]{:S(2)}, u32[]{:S(2)}) collective-permute-start(bf16[128,768]{0,1:T(8,128)(2,1)S(1)} %convolution_convert_fusion.12), channel_id=1, source_target_pairs={{0,8},{4,12},{8,0},{12,4},{16,24},{20,28},{24,16},{28,20},{1,9},{5... | collective-permute-start | bytes 589832 | tf_op jit(solution)/shard_map/ppermute | solution.py:19
  45.3 12.8 %collective-permute-start.2 = (bf16[4,512,128]{2,1,0:T(8,128)(2,1)S(1)}, bf16[4,512,128]{2,1,0:T(8,128)(2,1)S(1)}, u32[]{:S(2)}, u32[]{:S(2)}) collective-permute-start(bf16[4,512,128]{2,1,0:T(8,128)(2,1)S(1)} %copy-done.8), channel_id=1, source_target_pairs={{0,3},{1,0},{2,1},{3,2},{4,7},{5,4},{6,5},{7,6},{8,11},{9,8},{10,9... | collective-permute-start | bytes 1572872 | tf_op jit(solution)/shard_map/ppermute | solution.py:28
  50.1 16.4 %collective-permute-start.13 = (bf16[128,768]{0,1:T(8,128)(2,1)}, bf16[128,768]{0,1:T(8,128)(2,1)}, u32[]{:S(2)}, u32[]{:S(2)}) collective-permute-start(bf16[128,768]{0,1:T(8,128)(2,1)} %get-tuple-element.13), channel_id=1, source_target_pairs={{0,8},{4,12},{8,0},{12,4},{16,24},{20,28},{24,16},{28,20},{1,9},{5... | collective-permute-start | bytes 589832 | tf_op jit(solution)/shard_map/ppermute | solution.py:19
  50.6 17.4 %collective-permute-start.11 = (bf16[128,768]{0,1:T(8,128)(2,1)}, bf16[128,768]{0,1:T(8,128)(2,1)}, u32[]{:S(2)}, u32[]{:S(2)}) collective-permute-start(bf16[128,768]{0,1:T(8,128)(2,1)} %get-tuple-element.13), channel_id=1, source_target_pairs={{0,4},{4,0},{8,12},{12,8},{16,20},{20,16},{24,28},{28,24},{1,5},{5... | collective-permute-start | bytes 589832 | tf_op jit(solution)/shard_map/ppermute | solution.py:19
  55.2 12.8 %collective-permute-start.12 = (bf16[128,768]{0,1:T(8,128)(2,1)}, bf16[128,768]{0,1:T(8,128)(2,1)}, u32[]{:S(2)}, u32[]{:S(2)}) collective-permute-start(bf16[128,768]{0,1:T(8,128)(2,1)} %convolution_convert_fusion.11), channel_id=1, source_target_pairs={{0,4},{4,0},{8,12},{12,8},{16,20},{20,16},{24,28},{28,24},{1,5},{5... | collective-permute-start | bytes 589832 | tf_op jit(solution)/shard_map/ppermute | solution.py:19
  55.7 12.3 %collective-permute-start.14 = (bf16[128,768]{0,1:T(8,128)(2,1)}, bf16[128,768]{0,1:T(8,128)(2,1)}, u32[]{:S(2)}, u32[]{:S(2)}) collective-permute-start(bf16[128,768]{0,1:T(8,128)(2,1)} %convolution_convert_fusion.10), channel_id=1, source_target_pairs={{0,8},{4,12},{8,0},{12,4},{16,24},{20,28},{24,16},{28,20},{1,9},{5... | collective-permute-start | bytes 589832 | tf_op jit(solution)/shard_map/ppermute | solution.py:19
  70.2 7.2 %collective-permute-start.17 = (bf16[128,768]{0,1:T(8,128)(2,1)S(1)}, bf16[128,768]{0,1:T(8,128)(2,1)S(1)}, u32[]{:S(2)}, u32[]{:S(2)}) collective-permute-start(bf16[128,768]{0,1:T(8,128)(2,1)S(1)} %get-tuple-element.15), channel_id=1, source_target_pairs={{0,8},{4,12},{8,0},{12,4},{16,24},{20,28},{24,16},{28,20},{1,9},{5... | collective-permute-start | bytes 589832 | tf_op jit(solution)/shard_map/ppermute | solution.py:19
  71.4 8.8 %collective-permute-start.15 = (bf16[128,768]{0,1:T(8,128)(2,1)S(1)}, bf16[128,768]{0,1:T(8,128)(2,1)S(1)}, u32[]{:S(2)}, u32[]{:S(2)}) collective-permute-start(bf16[128,768]{0,1:T(8,128)(2,1)S(1)} %get-tuple-element.15), channel_id=1, source_target_pairs={{0,4},{4,0},{8,12},{12,8},{16,20},{20,16},{24,28},{28,24},{1,5},{5... | collective-permute-start | bytes 589832 | tf_op jit(solution)/shard_map/ppermute | solution.py:19
  72.0 8.2 %collective-permute-start.18 = (bf16[128,768]{0,1:T(8,128)(2,1)S(1)}, bf16[128,768]{0,1:T(8,128)(2,1)S(1)}, u32[]{:S(2)}, u32[]{:S(2)}) collective-permute-start(bf16[128,768]{0,1:T(8,128)(2,1)S(1)} %convolution_convert_fusion.8), channel_id=1, source_target_pairs={{0,8},{4,12},{8,0},{12,4},{16,24},{20,28},{24,16},{28,20},{1,9},{5... | collective-permute-start | bytes 589832 | tf_op jit(solution)/shard_map/ppermute | solution.py:19
  81.3 7.1 %collective-permute-start.21 = (bf16[128,768]{0,1:T(8,128)(2,1)S(1)}, bf16[128,768]{0,1:T(8,128)(2,1)S(1)}, u32[]{:S(2)}, u32[]{:S(2)}) collective-permute-start(bf16[128,768]{0,1:T(8,128)(2,1)S(1)} %get-tuple-element.17), channel_id=1, source_target_pairs={{0,8},{4,12},{8,0},{12,4},{16,24},{20,28},{24,16},{28,20},{1,9},{5... | collective-permute-start | bytes 589832 | tf_op jit(solution)/shard_map/ppermute | solution.py:19
  82.5 8.8 %collective-permute-start.19 = (bf16[128,768]{0,1:T(8,128)(2,1)S(1)}, bf16[128,768]{0,1:T(8,128)(2,1)S(1)}, u32[]{:S(2)}, u32[]{:S(2)}) collective-permute-start(bf16[128,768]{0,1:T(8,128)(2,1)S(1)} %get-tuple-element.17), channel_id=1, source_target_pairs={{0,4},{4,0},{8,12},{12,8},{16,20},{20,16},{24,28},{28,24},{1,5},{5... | collective-permute-start | bytes 589832 | tf_op jit(solution)/shard_map/ppermute | solution.py:19
  83.1 8.2 %collective-permute-start.22 = (bf16[128,768]{0,1:T(8,128)(2,1)S(1)}, bf16[128,768]{0,1:T(8,128)(2,1)S(1)}, u32[]{:S(2)}, u32[]{:S(2)}) collective-permute-start(bf16[128,768]{0,1:T(8,128)(2,1)S(1)} %convolution_convert_fusion.6), channel_id=1, source_target_pairs={{0,8},{4,12},{8,0},{12,4},{16,24},{20,28},{24,16},{28,20},{1,9},{5... | collective-permute-start | bytes 589832 | tf_op jit(solution)/shard_map/ppermute | solution.py:19
  94.3 8.0 %collective-permute-start.23 = (bf16[128,768]{0,1:T(8,128)(2,1)S(1)}, bf16[128,768]{0,1:T(8,128)(2,1)S(1)}, u32[]{:S(2)}, u32[]{:S(2)}) collective-permute-start(bf16[128,768]{0,1:T(8,128)(2,1)S(1)} %get-tuple-element.19), channel_id=1, source_target_pairs={{0,4},{4,0},{8,12},{12,8},{16,20},{20,16},{24,28},{28,24},{1,5},{5... | collective-permute-start | bytes 589832 | tf_op jit(solution)/shard_map/ppermute | solution.py:19
  94.8 7.4 %collective-permute-start.26 = (bf16[128,768]{0,1:T(8,128)(2,1)S(1)}, bf16[128,768]{0,1:T(8,128)(2,1)S(1)}, u32[]{:S(2)}, u32[]{:S(2)}) collective-permute-start(bf16[128,768]{0,1:T(8,128)(2,1)S(1)} %convolution_convert_fusion.4), channel_id=1, source_target_pairs={{0,8},{4,12},{8,0},{12,4},{16,24},{20,28},{24,16},{28,20},{1,9},{5... | collective-permute-start | bytes 589832 | tf_op jit(solution)/shard_map/ppermute | solution.py:19
  103.4 7.5 %collective-permute-start.29 = (bf16[128,768]{0,1:T(8,128)(2,1)S(1)}, bf16[128,768]{0,1:T(8,128)(2,1)S(1)}, u32[]{:S(2)}, u32[]{:S(2)}) collective-permute-start(bf16[128,768]{0,1:T(8,128)(2,1)S(1)} %get-tuple-element.21), channel_id=1, source_target_pairs={{0,8},{4,12},{8,0},{12,4},{16,24},{20,28},{24,16},{28,20},{1,9},{5... | collective-permute-start | bytes 589832 | tf_op jit(solution)/shard_map/ppermute | solution.py:19
  105.5 8.5 %collective-permute-start.27 = (bf16[128,768]{0,1:T(8,128)(2,1)S(1)}, bf16[128,768]{0,1:T(8,128)(2,1)S(1)}, u32[]{:S(2)}, u32[]{:S(2)}) collective-permute-start(bf16[128,768]{0,1:T(8,128)(2,1)S(1)} %get-tuple-element.21), channel_id=1, source_target_pairs={{0,4},{4,0},{8,12},{12,8},{16,20},{20,16},{24,28},{28,24},{1,5},{5... | collective-permute-start | bytes 589832 | tf_op jit(solution)/shard_map/ppermute | solution.py:19
  106.1 8.0 %collective-permute-start.30 = (bf16[128,768]{0,1:T(8,128)(2,1)S(1)}, bf16[128,768]{0,1:T(8,128)(2,1)S(1)}, u32[]{:S(2)}, u32[]{:S(2)}) collective-permute-start(bf16[128,768]{0,1:T(8,128)(2,1)S(1)} %convolution_convert_fusion.2), channel_id=1, source_target_pairs={{0,8},{4,12},{8,0},{12,4},{16,24},{20,28},{24,16},{28,20},{1,9},{5... | collective-permute-start | bytes 589832 | tf_op jit(solution)/shard_map/ppermute | solution.py:19
  115.8 7.9 %collective-permute-start.33 = (bf16[128,768]{0,1:T(8,128)(2,1)S(1)}, bf16[128,768]{0,1:T(8,128)(2,1)S(1)}, u32[]{:S(2)}, u32[]{:S(2)}) collective-permute-start(bf16[128,768]{0,1:T(8,128)(2,1)S(1)} %get-tuple-element.23), channel_id=1, source_target_pairs={{0,8},{4,12},{8,0},{12,4},{16,24},{20,28},{24,16},{28,20},{1,9},{5... | collective-permute-start | bytes 589832 | tf_op jit(solution)/shard_map/ppermute | solution.py:19
  116.6 9.4 %collective-permute-start.31 = (bf16[128,768]{0,1:T(8,128)(2,1)S(1)}, bf16[128,768]{0,1:T(8,128)(2,1)S(1)}, u32[]{:S(2)}, u32[]{:S(2)}) collective-permute-start(bf16[128,768]{0,1:T(8,128)(2,1)S(1)} %get-tuple-element.23), channel_id=1, source_target_pairs={{0,4},{4,0},{8,12},{12,8},{16,20},{20,16},{24,28},{28,24},{1,5},{5... | collective-permute-start | bytes 589832 | tf_op jit(solution)/shard_map/ppermute | solution.py:19
  116.6 7.6 %collective-permute-start.32 = (bf16[128,768]{0,1:T(8,128)(2,1)S(1)}, bf16[128,768]{0,1:T(8,128)(2,1)S(1)}, u32[]{:S(2)}, u32[]{:S(2)}) collective-permute-start(bf16[128,768]{0,1:T(8,128)(2,1)S(1)} %convolution_convert_fusion.1), channel_id=1, source_target_pairs={{0,4},{4,0},{8,12},{12,8},{16,20},{20,16},{24,28},{28,24},{1,5},{5... | collective-permute-start | bytes 589832 | tf_op jit(solution)/shard_map/ppermute | solution.py:19
  117.1 8.9 %collective-permute-start.34 = (bf16[128,768]{0,1:T(8,128)(2,1)S(1)}, bf16[128,768]{0,1:T(8,128)(2,1)S(1)}, u32[]{:S(2)}, u32[]{:S(2)}) collective-permute-start(bf16[128,768]{0,1:T(8,128)(2,1)S(1)} %convolution_convert_fusion), channel_id=1, source_target_pairs={{0,8},{4,12},{8,0},{12,4},{16,24},{20,28},{24,16},{28,20},{1,9},{5... | collective-permute-start | bytes 589832 | tf_op jit(solution)/shard_map/ppermute | solution.py:19
  126.4 9.7 %collective-permute-start.35 = (bf16[128,768]{0,1:T(8,128)(2,1)S(1)}, bf16[128,768]{0,1:T(8,128)(2,1)S(1)}, u32[]{:S(2)}, u32[]{:S(2)}) collective-permute-start(bf16[128,768]{0,1:T(8,128)(2,1)S(1)} %fusion.50), channel_id=1, source_target_pairs={{0,1},{1,2},{2,3},{3,0},{4,5},{5,6},{6,7},{7,4},{8,9},{9,10},{10,1... | collective-permute-start | bytes 589832 | tf_op jit(solution)/shard_map/ppermute | solution.py:28
  127.2 14.7 %collective-permute-start.36 = (bf16[128,768]{0,1:T(8,128)(2,1)S(1)}, bf16[128,768]{0,1:T(8,128)(2,1)S(1)}, u32[]{:S(2)}, u32[]{:S(2)}) collective-permute-start(bf16[128,768]{0,1:T(8,128)(2,1)S(1)} %fusion.50), channel_id=1, source_target_pairs={{0,2},{1,3},{2,0},{3,1},{4,6},{5,7},{6,4},{7,5},{8,10},{9,11},{10,... | collective-permute-start | bytes 589832 | tf_op jit(solution)/shard_map/ppermute | solution.py:28
  130.2 11.7 %collective-permute-start.37 = (bf16[128,768]{0,1:T(8,128)(2,1)S(1)}, bf16[128,768]{0,1:T(8,128)(2,1)S(1)}, u32[]{:S(2)}, u32[]{:S(2)}) collective-permute-start(bf16[128,768]{0,1:T(8,128)(2,1)S(1)} %fusion.50), channel_id=1, source_target_pairs={{0,3},{1,0},{2,1},{3,2},{4,7},{5,4},{6,5},{7,6},{8,11},{9,8},{10,9... | collective-permute-start | bytes 589832 | tf_op jit(solution)/shard_map/ppermute | solution.py:28
  (33 other events, 114.3 us)

commit v2 on v1

v2 whole, which is shorter than its diff:
```python
import jax
import jax.numpy as jnp
from jax import lax
from jax.sharding import PartitionSpec as P

ROUNDS = 2
DEGREE = 8
ROTS = 4
PAD_ROWS = 16


filter_center = 0.1
filter_half = 1.25
norm_eps = 1e-06


def swapped(value, axis, stride):
    mask = 2**stride
    pairs = [(source, source ^ mask) for source in range(lax.axis_size(axis))]
    return lax.ppermute(value, axis, pairs)


def gather_bands(value):
    count = lax.axis_size("bands")
    here = lax.axis_index("bands")
    pieces = [value]
    for shift in range(1, count):
        pairs = [(source, (source + shift) % count) for source in range(count)]
        pieces.append(lax.ppermute(value, "bands", pairs))
    order = (here - jnp.arange(count, dtype=jnp.int32)) % count
    return jnp.take(jnp.stack(pieces), order, axis=0)


def atoms_sum(value):
    count = lax.axis_size("atoms")
    stride = 0
    while (1 << stride) < count:
        value = value + swapped(value, "atoms", stride)
        stride += 1
    return value


def atom_index(atom_counts, length_total):
    atom_ends = jnp.cumsum(atom_counts)
    positions = jnp.arange(length_total, dtype=jnp.int32)
    return jnp.sum((positions[:, None] >= atom_ends[None, :]).astype(jnp.int32), axis=1)


def pattern_mask(pattern, row_atoms, col_atoms):
    atoms_dev = pattern.shape[0]
    col_onehot = (col_atoms[None, :] == jnp.arange(atoms_dev, dtype=jnp.int32)[:, None])
    per_row = jnp.dot(
        pattern.astype(jnp.float32), col_onehot.astype(jnp.float32), precision=lax.Precision.HIGHEST
    )
    mask = jnp.broadcast_to(per_row[0][None, :], (row_atoms.shape[0], col_atoms.shape[0]))
    for atom in range(1, atoms_dev):
        mask = jnp.where((row_atoms == atom)[:, None], per_row[atom][None, :], mask)
    return mask > 0.5


def body(subspace, diag_block, pair_block, pair_pattern, atom_sizes, rotations):
    orb_dev = diag_block.shape[1]
    atoms_dev = pair_pattern.shape[2]
    atoms_here = lax.axis_index("atoms")
    shipped = []
    for round_index in range(ROUNDS):
        pattern_rows = jnp.zeros((PAD_ROWS, orb_dev), jnp.bfloat16)
        pattern_rows = lax.dynamic_update_slice(
            pattern_rows, pair_pattern[round_index].astype(jnp.bfloat16), (0, 0)
        )
        packed = jnp.concatenate([pair_block[round_index], pattern_rows], axis=0)
        shipped.append(swapped(packed, "atoms", round_index))
    full_rot = gather_bands(rotations)
    own_atoms = atom_index(
        lax.dynamic_index_in_dim(atom_sizes, atoms_here, 0, keepdims=False), orb_dev
    )
    upper_flag = (own_atoms[:, None] < own_atoms[None, :]).astype(jnp.float32)
    same_atom = (own_atoms[:, None] == own_atoms[None, :]).astype(jnp.float32)
    upper_part = diag_block.astype(jnp.float32) * (upper_flag + 0.5 * same_atom)
    diag_sym = (upper_part + upper_part.T).astype(jnp.bfloat16)
    own_pair_t = []
    other_pair = []
    for round_index in range(ROUNDS):
        partner = jnp.bitwise_xor(atoms_here, 1 << round_index)
        other_atoms = atom_index(
            lax.dynamic_index_in_dim(atom_sizes, partner, 0, keepdims=False), orb_dev
        )
        own_mask = pattern_mask(pair_pattern[round_index], own_atoms, other_atoms)
        own_pair = jnp.where(own_mask, pair_block[round_index], jnp.zeros((), jnp.bfloat16))
        own_pair_t.append(own_pair.T)
        received = shipped[round_index]
        other_pattern = received[orb_dev : orb_dev + atoms_dev, :atoms_dev]
        other_mask = pattern_mask(other_pattern, other_atoms, own_atoms)
        other_pair.append(
            jnp.where(other_mask, received[:orb_dev], jnp.zeros((), jnp.bfloat16))
        )

    def apply_operator(values):
        result = jnp.dot(values, diag_sym, preferred_element_type=jnp.float32)
        for round_index in range(ROUNDS):
            other_rows = swapped(values, "atoms", round_index)
            result = result + jnp.dot(
                other_rows, own_pair_t[round_index], preferred_element_type=jnp.float32
            )
            result = result + jnp.dot(
                other_rows, other_pair[round_index], preferred_element_type=jnp.float32
            )
        return result

    previous = subspace.astype(jnp.float32)
    current = (apply_operator(subspace) - filter_center * previous) / filter_half
    for degree_index in range(1, DEGREE):
        applied = apply_operator(current.astype(jnp.bfloat16))
        following = 2.0 * (applied - filter_center * current) / filter_half - previous
        previous, current = (current, following)
    total_orbitals = orb_dev * lax.axis_size("atoms")
    rot_steps, all_bands, _ = rotations.shape
    full_rot = jnp.transpose(full_rot, (1, 2, 0, 3)).reshape(rot_steps, all_bands, all_bands)
    basis_all = gather_bands(current.astype(jnp.bfloat16)).reshape(all_bands, orb_dev)
    for rotation_index in range(ROTS - 1):
        mixed_rows = lax.dot_general(
            full_rot[rotation_index],
            basis_all,
            (((0,), (0,)), ((), ())),
            preferred_element_type=jnp.float32,
        )
        squares = atoms_sum(jnp.sum(mixed_rows * mixed_rows, axis=1))
        col_norm = jnp.sqrt(squares / total_orbitals + norm_eps)
        basis_all = (mixed_rows / col_norm[:, None]).astype(jnp.bfloat16)
    mixed_rows = lax.dot_general(
        rotations[ROTS - 1],
        basis_all,
        (((0,), (0,)), ((), ())),
        preferred_element_type=jnp.float32,
    )
    squares = atoms_sum(jnp.sum(mixed_rows * mixed_rows, axis=1))
    col_norm = jnp.sqrt(squares / total_orbitals + norm_eps)
    return mixed_rows / col_norm[:, None]


def solution(mesh):
    placed = (
        P("bands", "atoms"),
        P("atoms", None),
        P(None, "atoms", None),
        P(None, "atoms", None),
        P(),
        P(None, None, "bands"),
    )
    return jax.shard_map(
        body, mesh=mesh, in_specs=placed, out_specs=P("bands", "atoms"), check_vma=False
    )
```

time: 190 us -> 201 us (1.058)
  waiting for transfers between devices: 76.3 us -> 95.1 us
  starting transfers between devices: 41.4 us -> 26.1 us
  other arithmetic: 12.4 us -> 25.4 us
  matrix products: 45.8 us -> 38.8 us
  local copies, waits for them, and re-layouts: 11.1 us -> 13.6 us
    ppermute x6, waiting for transfers between devices: 12.1 us -> 27.8 us  [gather_bands(): pieces.append(lax.ppermute(value, 'bands', pairs))]
    ppermute x44 -> x30, starting transfers between devices: 32.1 us -> 16.6 us  [swapped(): return lax.ppermute(value, axis, pairs)]
    select_n x0 -> x3, other arithmetic: none -> 8.94 us  [the longest x2 4.96 us: body(): jnp.where(other_mask, received[:orb_dev], jnp.zeros((), jnp.bfloat16))]
    dot_general x36, matrix products: 30.8 us -> 24.8 us  [the longest x16 11.2 us: apply_operator(): jnp.dot(other_rows, own_pair_t[round_index], preferred_element_type=jnp.f...]
    concatenate x0 -> x2, other arithmetic: none -> 3.68 us  [body(): packed = jnp.concatenate([pair_block[round_index], pattern_rows], axis=0)]
    ppermute x44 -> x30, waiting for transfers between devices: 64.2 us -> 67.3 us  [swapped(): return lax.ppermute(value, axis, pairs)]
    squeeze x0 -> x1, local copies, waits for them, and re-layouts: none -> 2.79 us  [body(): pair_block[round_index]]
  transfers between devices with their start and end apart: 50 -> 36, of which waited for: 28 -> 23; matrix products, arithmetic and copies ran while one was open for 26% -> 25% of each run, Pallas kernels for 0% -> 0%
where the time goes in v2:
time: 201 us; the launch traced here: 200 us
  waiting for transfers between devices  95.1 us (47%)
  matrix products  38.8 us (19%)
  starting transfers between devices  26.1 us (13%)
  other arithmetic  25.4 us (13%)
  local copies, waits for them, and re-layouts  13.6 us (7%)
    ppermute x30, waiting for transfers between devices, swapped(): return lax.ppermute(value, axis, pairs)  67.3 us
    ppermute x6, waiting for transfers between devices, gather_bands(): pieces.append(lax.ppermute(value, 'bands', pairs))  27.8 us
    ppermute x30, starting transfers between devices, swapped(): return lax.ppermute(value, axis, pairs)  16.6 us
    dot_general x16, matrix products, apply_operator(): jnp.dot(other_rows, own_pair_t[round_index], preferred_element_type=jnp.f...  11.2 us
    dot_general x16, matrix products, apply_operator(): jnp.dot(other_rows, other_pair[round_index], preferred_element_type=jnp.f...  11.1 us
    ppermute x6, starting transfers between devices, gather_bands(): pieces.append(lax.ppermute(value, 'bands', pairs))  9.44 us
    dot_general x3, matrix products, body(): lax.dot_general(full_rot[rotation_index], basis_all, (((0,), (0,)), ((),...  7.16 us
    dot_general x8, matrix products, apply_operator(): result = jnp.dot(values, diag_sym, preferred_element_type=jnp.float32)  5.38 us
  transfers between devices with their start and end apart: 36, of which 23 were waited for; matrix products, arithmetic and copies ran while one was open for 25% of the time, Pallas kernels for 0%

profile of v2, /device:TPU:0, one launch (start us, length us, event | category | flops | bytes accessed | tf_op | source)
XLA Modules:
  0.0 199.7 jit_solution(2901549293263197805)
XLA Ops:
  0.0 2.9 %collective-permute-start.5 = (bf16[128,768]{1,0:T(8,128)(2,1)}, bf16[128,768]{1,0:T(8,128)(2,1)}, u32[]{:S(2)}, u32[]{:S(2)}) collective-permute-start(bf16[128,768]{1,0:T(8,128)(2,1)} %param.6), channel_id=1, source_target_pairs={{0,8},{4,12},{8,0},{12,4},{16,24},{20,28},{24,16},{28,20},{1,9},{5... | collective-permute-start | bytes 589832 | tf_op jit(solution)/shard_map/ppermute | solution.py:20
  4.5 2.6 %collective-permute-start.1 = (bf16[4,512,128]{2,1,0:T(8,128)(2,1)}, bf16[4,512,128]{2,1,0:T(8,128)(2,1)}, u32[]{:S(2)}, u32[]{:S(2)}) collective-permute-start(bf16[4,512,128]{2,1,0:T(8,128)(2,1)} %param.11), channel_id=1, source_target_pairs={{0,2},{1,3},{2,0},{3,1},{4,6},{5,7},{6,4},{7,5},{8,10},{9,11},{10,... | collective-permute-start | bytes 1572872 | tf_op jit(solution)/shard_map/ppermute | solution.py:29
  7.1 2.8 %slice_bitcast_fusion.1 = (bf16[768,768]{1,0:T(8,128)(2,1)S(1)}, bf16[768,768]{1,0:T(8,128)(2,1)}) fusion(bf16[2,768,768]{2,1,0:T(8,128)(2,1)} %param.8), kind=kLoop, calls=%fused_computation.82 | loop fusion | bytes 4718592 | tf_op jit(solution)/shard_map/squeeze | solution.py:89
  17.4 2.0 %copy.129 = f32[768,768]{0,1:T(8,128)S(1)} copy(f32[768,768]{1,0:T(8,128)} %add_multiply_fusion) | data formatting | bytes 4718592 | tf_op jit(solution)/shard_map/mul | solution.py:79
  19.4 2.0 %fusion.2 = bf16[768,768]{1,0:T(8,128)(2,1)S(1)} fusion(f32[768,768]{0,1:T(8,128)S(1)} %copy.129, s32[768]{0:T(1024)S(1)} %convert_reduce_fusion.2, bf16[768,768]{1,0:T(8,128)(2,1)} %param.7), kind=kLoop, calls=%fused_computation.6 | loop fusion | flops 5308416 | bytes 4721664 | tf_op jit(solution)/shard_map/convert_element_type | solution.py:80
  23.4 4.0 %fusion.3 = (bf16[768,768]{1,0:T(8,128)(2,1)S(1)}, bf16[768,768]{1,0:T(8,128)(2,1)S(1)}) fusion(f32[768]{0:T(1024)S(1)} %get-tuple-element.66, f32[768]{0:T(1024)S(1)} %get-tuple-element.65, f32[768]{0:T(1024)S(1)} %get-tuple-element.64, f32[768]{0:T(1024)S(1)} %get-tuple-element.67, pred[768]{0:T(1024)(128)(4,1)} %get-tuple-element.37, ...), kind=kLoop, calls=%fused_computation.12 | loop fusion | flops 5898240 | bytes 4745472 | tf_op jit(solution)/shard_map/jit(_where)/select_n | solution.py:89
  29.2 2.5 %fusion.8 = bf16[784,768]{1,0:T(8,128)(2,1)} fusion(bf16[4,4]{1,0:T(4,128)(2,1)S(1)} %copy-done.16, bf16[768,768]{1,0:T(8,128)(2,1)} %get-tuple-element.27), kind=kLoop, calls=%fused_computation.25 | loop fusion | flops 3612672 | bytes 2383904 | tf_op jit(solution)/shard_map/concatenate | solution.py:71
  33.7 2.1 %fusion.90 = f32[768,128]{1,0:T(8,128)} fusion(bf16[768,768]{1,0:T(8,128)(2,1)S(1)} %get-tuple-element.25, bf16[128,768]{1,0:T(8,128)(2,1)} %collective-permute-done.5), kind=kOutput, calls=%fused_computation.179 | convolution fusion | flops 150994944 | bytes 1769472 | tf_op jit(solution)/shard_map/dot_general | solution.py:102
  35.8 2.2 %convolution_add_fusion.8 = f32[768,128]{1,0:T(8,128)} fusion(f32[768,128]{1,0:T(8,128)S(1)} %copy-done.4, bf16[768,768]{1,0:T(8,128)(2,1)S(1)} %get-tuple-element.24, bf16[128,768]{1,0:T(8,128)(2,1)} %collective-permute-done.3), kind=kOutput, calls=%fused_computation.34 | convolution fusion | flops 151093248 | bytes 2162688 | tf_op jit(solution)/shard_map/dot_general | solution.py:102
  38.0 4.0 %collective-permute-done.1 = bf16[4,512,128]{2,1,0:T(8,128)(2,1)} collective-permute-done((bf16[4,512,128]{2,1,0:T(8,128)(2,1)}, bf16[4,512,128]{2,1,0:T(8,128)(2,1)}, u32[]{:S(2)}, u32[]{:S(2)}) %collective-permute-start.1) | collective-permute-done | bytes 524320 | tf_op jit(solution)/shard_map/ppermute | solution.py:29
  42.0 11.0 %collective-permute-done.2 = bf16[4,512,128]{2,1,0:T(8,128)(2,1)S(1)} collective-permute-done((bf16[4,512,128]{2,1,0:T(8,128)(2,1)S(1)}, bf16[4,512,128]{2,1,0:T(8,128)(2,1)S(1)}, u32[]{:S(2)}, u32[]{:S(2)}) %collective-permute-start.2) | collective-permute-done | bytes 524320 | tf_op jit(solution)/shard_map/ppermute | solution.py:29
  53.1 2.8 %pad_maximum_fusion = bf16[4,4,512,128]{3,2,1,0:T(8,128)(2,1)} fusion(bf16[1,4,512,128]{3,2,1,0:T(8,128)(2,1)S(1)} %bitcast.149, bf16[1,4,512,128]{3,2,1,0:T(8,128)(2,1)} %bitcast.2, bf16[1,4,512,128]{3,2,1,0:T(8,128)(2,1)} %bitcast.1, bf16[1,4,512,128]{3,2,1,0:T(8,128)(2,1)S(1)} %bitcast.148), kind=kLoop, calls=%fused_computation.16 | loop fusion | flops 3145728 | bytes 4194304 | tf_op jit(solution)/shard_map/stack | solution.py:31
  55.9 3.8 %gather_fusion = bf16[4,4,512,128]{3,2,1,0:T(8,128)(2,1)} fusion(bf16[4,4,512,128]{3,2,1,0:T(8,128)(2,1)} %pad_maximum_fusion, s32[1024]{0:T(1024)} %pad_clamp_fusion), kind=kCustom, calls=%fused_computation | custom fusion | bytes 4194320 | tf_op jit(solution)/shard_map/jit(_take)/gather | solution.py:31
  63.3 2.3 %fusion.6 = bf16[768,768]{1,0:T(8,128)(2,1)S(1)} fusion(bf16[784,768]{1,0:T(8,128)(2,1)} %collective-permute-done.6, f32[768]{0:T(1024)S(1)} %get-tuple-element.18, f32[768]{0:T(1024)S(1)} %get-tuple-element.19, f32[768]{0:T(1024)S(1)} %get-tuple-element.20, f32[768]{0:T(1024)S(1)} %get-tuple-element.17, pred[768]{0:T(1024)(128)(4,1)S(1)} %copy-done.14, ...), kind=kLoop, calls=%fused_computation.15 | loop fusion | flops 2949120 | bytes 2373888 | tf_op jit(solution)/shard_map/jit(_where)/select_n | solution.py:95
  67.2 2.6 %fusion.4 = bf16[768,768]{1,0:T(8,128)(2,1)S(1)} fusion(bf16[784,768]{1,0:T(8,128)(2,1)} %collective-permute-done.4, f32[768]{0:T(1024)S(1)} %get-tuple-element.6, f32[768]{0:T(1024)S(1)} %get-tuple-element.7, f32[768]{0:T(1024)S(1)} %get-tuple-element.8, f32[768]{0:T(1024)S(1)} %get-tuple-element.5, pred[768]{0:T(1024)(128)(4,1)S(1)} %copy-done.11, ...), kind=kLoop, calls=%fused_computation.13 | loop fusion | flops 2949120 | bytes 2373888 | tf_op jit(solution)/shard_map/jit(_where)/select_n | solution.py:95
  72.6 6.0 %collective-permute-done.8 = bf16[128,768]{0,1:T(8,128)(2,1)S(1)} collective-permute-done((bf16[128,768]{0,1:T(8,128)(2,1)S(1)}, bf16[128,768]{0,1:T(8,128)(2,1)S(1)}, u32[]{:S(2)}, u32[]{:S(2)}) %collective-permute-start.8) | collective-permute-done | bytes 196640 | tf_op jit(solution)/shard_map/ppermute | solution.py:20
  82.1 6.1 %collective-permute-done.10 = bf16[128,768]{0,1:T(8,128)(2,1)S(1)} collective-permute-done((bf16[128,768]{0,1:T(8,128)(2,1)S(1)}, bf16[128,768]{0,1:T(8,128)(2,1)S(1)}, u32[]{:S(2)}, u32[]{:S(2)}) %collective-permute-start.10) | collective-permute-done | bytes 196640 | tf_op jit(solution)/shard_map/ppermute | solution.py:20
  91.6 6.1 %collective-permute-done.12 = bf16[128,768]{0,1:T(8,128)(2,1)S(1)} collective-permute-done((bf16[128,768]{0,1:T(8,128)(2,1)S(1)}, bf16[128,768]{0,1:T(8,128)(2,1)S(1)}, u32[]{:S(2)}, u32[]{:S(2)}) %collective-permute-start.12) | collective-permute-done | bytes 196640 | tf_op jit(solution)/shard_map/ppermute | solution.py:20
  101.2 6.1 %collective-permute-done.14 = bf16[128,768]{0,1:T(8,128)(2,1)S(1)} collective-permute-done((bf16[128,768]{0,1:T(8,128)(2,1)S(1)}, bf16[128,768]{0,1:T(8,128)(2,1)S(1)}, u32[]{:S(2)}, u32[]{:S(2)}) %collective-permute-start.14) | collective-permute-done | bytes 196640 | tf_op jit(solution)/shard_map/ppermute | solution.py:20
  110.8 6.1 %collective-permute-done.16 = bf16[128,768]{0,1:T(8,128)(2,1)S(1)} collective-permute-done((bf16[128,768]{0,1:T(8,128)(2,1)S(1)}, bf16[128,768]{0,1:T(8,128)(2,1)S(1)}, u32[]{:S(2)}, u32[]{:S(2)}) %collective-permute-start.16) | collective-permute-done | bytes 196640 | tf_op jit(solution)/shard_map/ppermute | solution.py:20
  120.5 6.1 %collective-permute-done.18 = bf16[128,768]{0,1:T(8,128)(2,1)S(1)} collective-permute-done((bf16[128,768]{0,1:T(8,128)(2,1)S(1)}, bf16[128,768]{0,1:T(8,128)(2,1)S(1)}, u32[]{:S(2)}, u32[]{:S(2)}) %collective-permute-start.18) | collective-permute-done | bytes 196640 | tf_op jit(solution)/shard_map/ppermute | solution.py:20
  130.1 6.1 %collective-permute-done.20 = bf16[128,768]{0,1:T(8,128)(2,1)S(1)} collective-permute-done((bf16[128,768]{0,1:T(8,128)(2,1)S(1)}, bf16[128,768]{0,1:T(8,128)(2,1)S(1)}, u32[]{:S(2)}, u32[]{:S(2)}) %collective-permute-start.20) | collective-permute-done | bytes 196640 | tf_op jit(solution)/shard_map/ppermute | solution.py:20
  142.6 5.5 %collective-permute-done.21 = bf16[128,768]{0,1:T(8,128)(2,1)S(1)} collective-permute-done((bf16[128,768]{0,1:T(8,128)(2,1)S(1)}, bf16[128,768]{0,1:T(8,128)(2,1)S(1)}, u32[]{:S(2)}, u32[]{:S(2)}) %collective-permute-start.21) | collective-permute-done | bytes 196640 | tf_op jit(solution)/shard_map/ppermute | solution.py:29
  148.2 7.2 %collective-permute-done.22 = bf16[128,768]{0,1:T(8,128)(2,1)S(1)} collective-permute-done((bf16[128,768]{0,1:T(8,128)(2,1)S(1)}, bf16[128,768]{0,1:T(8,128)(2,1)S(1)}, u32[]{:S(2)}, u32[]{:S(2)}) %collective-permute-start.22) | collective-permute-done | bytes 196640 | tf_op jit(solution)/shard_map/ppermute | solution.py:29
  160.1 3.1 %collective-permute-done.25 = f32[512]{0:T(512)S(1)} collective-permute-done((f32[512]{0:T(512)S(1)}, f32[512]{0:T(512)S(1)}, u32[]{:S(2)}, u32[]{:S(2)}) %collective-permute-start.25) | collective-permute-done | bytes 2080 | tf_op jit(solution)/shard_map/ppermute | solution.py:20
  166.8 3.2 %multiply_reduce_fusion.1 = (f32[512]{0:T(512)S(1)}, f32[512,768]{1,0:T(8,128)}) fusion(bf16[512,512]{0,1:T(8,128)(2,1)S(1)} %bitcast.146, f32[512,768]{1,0:T(8,128)} %get-tuple-element.57, f32[512]{0:T(512)S(1)} %add_sqrt_fusion.2), kind=kOutput, calls=%fused_computation.21 | convolution fusion | flops 404225536 | bytes 3674112 | tf_op jit(solution)/shard_map/dot_general | solution.py:121
  171.7 3.0 %collective-permute-done.28 = f32[512]{0:T(512)S(1)} collective-permute-done((f32[512]{0:T(512)S(1)}, f32[512]{0:T(512)S(1)}, u32[]{:S(2)}, u32[]{:S(2)}) %collective-permute-start.28) | collective-permute-done | bytes 2080 | tf_op jit(solution)/shard_map/ppermute | solution.py:20
  178.4 2.2 %multiply_reduce_fusion = (f32[512]{0:T(512)S(1)}, f32[512,768]{1,0:T(8,128)S(1)}) fusion(bf16[512,512]{0,1:T(8,128)(2,1)S(1)} %bitcast.147, f32[512,768]{1,0:T(8,128)} %get-tuple-element.59, f32[512]{0:T(512)S(1)} %add_sqrt_fusion.1), kind=kOutput, calls=%fused_computation.19 | convolution fusion | flops 404225536 | bytes 3674112 | tf_op jit(solution)/shard_map/dot_general | solution.py:121
  182.3 3.1 %collective-permute-done.31 = f32[512]{0:T(512)S(1)} collective-permute-done((f32[512]{0:T(512)S(1)}, f32[512]{0:T(512)S(1)}, u32[]{:S(2)}, u32[]{:S(2)}) %collective-permute-start.31) | collective-permute-done | bytes 2080 | tf_op jit(solution)/shard_map/ppermute | solution.py:20
  186.9 2.1 %collective-permute-done.32 = f32[512]{0:T(512)S(1)} collective-permute-done((f32[512]{0:T(512)S(1)}, f32[512]{0:T(512)S(1)}, u32[]{:S(2)}, u32[]{:S(2)}) %collective-permute-start.32) | collective-permute-done | bytes 2080 | tf_op jit(solution)/shard_map/ppermute | solution.py:20
  192.1 3.0 %collective-permute-done.34 = f32[128]{0:T(128)S(1)} collective-permute-done((f32[128]{0:T(128)S(1)}, f32[128]{0:T(128)S(1)}, u32[]{:S(2)}, u32[]{:S(2)}) %collective-permute-start.34) | collective-permute-done | bytes 544 | tf_op jit(solution)/shard_map/ppermute | solution.py:20
  196.7 2.0 %collective-permute-done.35 = f32[128]{0:T(128)S(1)} collective-permute-done((f32[128]{0:T(128)S(1)}, f32[128]{0:T(128)S(1)}, u32[]{:S(2)}, u32[]{:S(2)}) %collective-permute-start.35) | collective-permute-done | bytes 544 | tf_op jit(solution)/shard_map/ppermute | solution.py:20
  (174 shorter events, 71.9 us)
Async XLA Ops:
  0.0 31.7 %collective-permute-start.5 = (bf16[128,768]{1,0:T(8,128)(2,1)}, bf16[128,768]{1,0:T(8,128)(2,1)}, u32[]{:S(2)}, u32[]{:S(2)}) collective-permute-start(bf16[128,768]{1,0:T(8,128)(2,1)} %param.6), channel_id=1, source_target_pairs={{0,8},{4,12},{8,0},{12,4},{16,24},{20,28},{24,16},{28,20},{1,9},{5... | collective-permute-start | bytes 589832 | tf_op jit(solution)/shard_map/ppermute | solution.py:20
  2.9 30.2 %collective-permute-start.3 = (bf16[128,768]{1,0:T(8,128)(2,1)}, bf16[128,768]{1,0:T(8,128)(2,1)}, u32[]{:S(2)}, u32[]{:S(2)}) collective-permute-start(bf16[128,768]{1,0:T(8,128)(2,1)} %param.6), channel_id=1, source_target_pairs={{0,4},{4,0},{8,12},{12,8},{16,20},{20,16},{24,28},{28,24},{1,5},{5... | collective-permute-start | bytes 589832 | tf_op jit(solution)/shard_map/ppermute | solution.py:20
  2.9 35.1 %collective-permute-start = (bf16[4,512,128]{2,1,0:T(8,128)(2,1)}, bf16[4,512,128]{2,1,0:T(8,128)(2,1)}, u32[]{:S(2)}, u32[]{:S(2)}) collective-permute-start(bf16[4,512,128]{2,1,0:T(8,128)(2,1)} %param.11), channel_id=1, source_target_pairs={{0,1},{1,2},{2,3},{3,0},{4,5},{5,6},{6,7},{7,4},{8,9},{9,10},{10,1... | collective-permute-start | bytes 1572872 | tf_op jit(solution)/shard_map/ppermute | solution.py:29
  4.5 37.5 %collective-permute-start.1 = (bf16[4,512,128]{2,1,0:T(8,128)(2,1)}, bf16[4,512,128]{2,1,0:T(8,128)(2,1)}, u32[]{:S(2)}, u32[]{:S(2)}) collective-permute-start(bf16[4,512,128]{2,1,0:T(8,128)(2,1)} %param.11), channel_id=1, source_target_pairs={{0,2},{1,3},{2,0},{3,1},{4,6},{5,7},{6,4},{7,5},{8,10},{9,11},{10,... | collective-permute-start | bytes 1572872 | tf_op jit(solution)/shard_map/ppermute | solution.py:29
  11.6 49.9 %collective-permute-start.4 = (bf16[784,768]{1,0:T(8,128)(2,1)}, bf16[784,768]{1,0:T(8,128)(2,1)}, u32[]{:S(2)}, u32[]{:S(2)}) collective-permute-start(bf16[784,768]{1,0:T(8,128)(2,1)} %fusion.7), channel_id=1, source_target_pairs={{0,4},{4,0},{8,12},{12,8},{16,20},{20,16},{24,28},{28,24},{1,5},{5... | collective-permute-start | bytes 3612680 | tf_op jit(solution)/shard_map/ppermute | solution.py:20
  31.7 21.3 %collective-permute-start.2 = (bf16[4,512,128]{2,1,0:T(8,128)(2,1)S(1)}, bf16[4,512,128]{2,1,0:T(8,128)(2,1)S(1)}, u32[]{:S(2)}, u32[]{:S(2)}) collective-permute-start(bf16[4,512,128]{2,1,0:T(8,128)(2,1)S(1)} %copy-done.6), channel_id=1, source_target_pairs={{0,3},{1,0},{2,1},{3,2},{4,7},{5,4},{6,5},{7,6},{8,11},{9,8},{10,9... | collective-permute-start | bytes 1572872 | tf_op jit(solution)/shard_map/ppermute | solution.py:29
  33.1 29.3 %collective-permute-start.6 = (bf16[784,768]{1,0:T(8,128)(2,1)}, bf16[784,768]{1,0:T(8,128)(2,1)}, u32[]{:S(2)}, u32[]{:S(2)}) collective-permute-start(bf16[784,768]{1,0:T(8,128)(2,1)} %fusion.8), channel_id=1, source_target_pairs={{0,8},{4,12},{8,0},{12,4},{16,24},{20,28},{24,16},{28,20},{1,9},{5... | collective-permute-start | bytes 3612680 | tf_op jit(solution)/shard_map/ppermute | solution.py:20
  71.3 8.5 %collective-permute-start.7 = (bf16[128,768]{0,1:T(8,128)(2,1)S(1)}, bf16[128,768]{0,1:T(8,128)(2,1)S(1)}, u32[]{:S(2)}, u32[]{:S(2)}) collective-permute-start(bf16[128,768]{0,1:T(8,128)(2,1)S(1)} %get-tuple-element.42), channel_id=1, source_target_pairs={{0,4},{4,0},{8,12},{12,8},{16,20},{20,16},{24,28},{28,24},{1,5},{5... | collective-permute-start | bytes 589832 | tf_op jit(solution)/shard_map/ppermute | solution.py:20
  71.5 7.1 %collective-permute-start.8 = (bf16[128,768]{0,1:T(8,128)(2,1)S(1)}, bf16[128,768]{0,1:T(8,128)(2,1)S(1)}, u32[]{:S(2)}, u32[]{:S(2)}) collective-permute-start(bf16[128,768]{0,1:T(8,128)(2,1)S(1)} %get-tuple-element.42), channel_id=1, source_target_pairs={{0,8},{4,12},{8,0},{12,4},{16,24},{20,28},{24,16},{28,20},{1,9},{5... | collective-permute-start | bytes 589832 | tf_op jit(solution)/shard_map/ppermute | solution.py:20
  80.8 8.5 %collective-permute-start.9 = (bf16[128,768]{0,1:T(8,128)(2,1)S(1)}, bf16[128,768]{0,1:T(8,128)(2,1)S(1)}, u32[]{:S(2)}, u32[]{:S(2)}) collective-permute-start(bf16[128,768]{0,1:T(8,128)(2,1)S(1)} %get-tuple-element.44), channel_id=1, source_target_pairs={{0,4},{4,0},{8,12},{12,8},{16,20},{20,16},{24,28},{28,24},{1,5},{5... | collective-permute-start | bytes 589832 | tf_op jit(solution)/shard_map/ppermute | solution.py:20
  80.9 7.3 %collective-permute-start.10 = (bf16[128,768]{0,1:T(8,128)(2,1)S(1)}, bf16[128,768]{0,1:T(8,128)(2,1)S(1)}, u32[]{:S(2)}, u32[]{:S(2)}) collective-permute-start(bf16[128,768]{0,1:T(8,128)(2,1)S(1)} %get-tuple-element.44), channel_id=1, source_target_pairs={{0,8},{4,12},{8,0},{12,4},{16,24},{20,28},{24,16},{28,20},{1,9},{5... | collective-permute-start | bytes 589832 | tf_op jit(solution)/shard_map/ppermute | solution.py:20
  90.4 8.5 %collective-permute-start.11 = (bf16[128,768]{0,1:T(8,128)(2,1)S(1)}, bf16[128,768]{0,1:T(8,128)(2,1)S(1)}, u32[]{:S(2)}, u32[]{:S(2)}) collective-permute-start(bf16[128,768]{0,1:T(8,128)(2,1)S(1)} %get-tuple-element.46), channel_id=1, source_target_pairs={{0,4},{4,0},{8,12},{12,8},{16,20},{20,16},{24,28},{28,24},{1,5},{5... | collective-permute-start | bytes 589832 | tf_op jit(solution)/shard_map/ppermute | solution.py:20
  90.4 7.3 %collective-permute-start.12 = (bf16[128,768]{0,1:T(8,128)(2,1)S(1)}, bf16[128,768]{0,1:T(8,128)(2,1)S(1)}, u32[]{:S(2)}, u32[]{:S(2)}) collective-permute-start(bf16[128,768]{0,1:T(8,128)(2,1)S(1)} %get-tuple-element.46), channel_id=1, source_target_pairs={{0,8},{4,12},{8,0},{12,4},{16,24},{20,28},{24,16},{28,20},{1,9},{5... | collective-permute-start | bytes 589832 | tf_op jit(solution)/shard_map/ppermute | solution.py:20
  99.9 8.5 %collective-permute-start.13 = (bf16[128,768]{0,1:T(8,128)(2,1)S(1)}, bf16[128,768]{0,1:T(8,128)(2,1)S(1)}, u32[]{:S(2)}, u32[]{:S(2)}) collective-permute-start(bf16[128,768]{0,1:T(8,128)(2,1)S(1)} %get-tuple-element.48), channel_id=1, source_target_pairs={{0,4},{4,0},{8,12},{12,8},{16,20},{20,16},{24,28},{28,24},{1,5},{5... | collective-permute-start | bytes 589832 | tf_op jit(solution)/shard_map/ppermute | solution.py:20
  100.0 7.3 %collective-permute-start.14 = (bf16[128,768]{0,1:T(8,128)(2,1)S(1)}, bf16[128,768]{0,1:T(8,128)(2,1)S(1)}, u32[]{:S(2)}, u32[]{:S(2)}) collective-permute-start(bf16[128,768]{0,1:T(8,128)(2,1)S(1)} %get-tuple-element.48), channel_id=1, source_target_pairs={{0,8},{4,12},{8,0},{12,4},{16,24},{20,28},{24,16},{28,20},{1,9},{5... | collective-permute-start | bytes 589832 | tf_op jit(solution)/shard_map/ppermute | solution.py:20
  109.5 8.7 %collective-permute-start.15 = (bf16[128,768]{0,1:T(8,128)(2,1)S(1)}, bf16[128,768]{0,1:T(8,128)(2,1)S(1)}, u32[]{:S(2)}, u32[]{:S(2)}) collective-permute-start(bf16[128,768]{0,1:T(8,128)(2,1)S(1)} %get-tuple-element.50), channel_id=1, source_target_pairs={{0,4},{4,0},{8,12},{12,8},{16,20},{20,16},{24,28},{28,24},{1,5},{5... | collective-permute-start | bytes 589832 | tf_op jit(solution)/shard_map/ppermute | solution.py:20
  109.6 7.3 %collective-permute-start.16 = (bf16[128,768]{0,1:T(8,128)(2,1)S(1)}, bf16[128,768]{0,1:T(8,128)(2,1)S(1)}, u32[]{:S(2)}, u32[]{:S(2)}) collective-permute-start(bf16[128,768]{0,1:T(8,128)(2,1)S(1)} %get-tuple-element.50), channel_id=1, source_target_pairs={{0,8},{4,12},{8,0},{12,4},{16,24},{20,28},{24,16},{28,20},{1,9},{5... | collective-permute-start | bytes 589832 | tf_op jit(solution)/shard_map/ppermute | solution.py:20
  119.3 8.5 %collective-permute-start.17 = (bf16[128,768]{0,1:T(8,128)(2,1)S(1)}, bf16[128,768]{0,1:T(8,128)(2,1)S(1)}, u32[]{:S(2)}, u32[]{:S(2)}) collective-permute-start(bf16[128,768]{0,1:T(8,128)(2,1)S(1)} %get-tuple-element.52), channel_id=1, source_target_pairs={{0,4},{4,0},{8,12},{12,8},{16,20},{20,16},{24,28},{28,24},{1,5},{5... | collective-permute-start | bytes 589832 | tf_op jit(solution)/shard_map/ppermute | solution.py:20
  119.3 7.3 %collective-permute-start.18 = (bf16[128,768]{0,1:T(8,128)(2,1)S(1)}, bf16[128,768]{0,1:T(8,128)(2,1)S(1)}, u32[]{:S(2)}, u32[]{:S(2)}) collective-permute-start(bf16[128,768]{0,1:T(8,128)(2,1)S(1)} %get-tuple-element.52), channel_id=1, source_target_pairs={{0,8},{4,12},{8,0},{12,4},{16,24},{20,28},{24,16},{28,20},{1,9},{5... | collective-permute-start | bytes 589832 | tf_op jit(solution)/shard_map/ppermute | solution.py:20
  128.8 8.5 %collective-permute-start.19 = (bf16[128,768]{0,1:T(8,128)(2,1)S(1)}, bf16[128,768]{0,1:T(8,128)(2,1)S(1)}, u32[]{:S(2)}, u32[]{:S(2)}) collective-permute-start(bf16[128,768]{0,1:T(8,128)(2,1)S(1)} %get-tuple-element.54), channel_id=1, source_target_pairs={{0,4},{4,0},{8,12},{12,8},{16,20},{20,16},{24,28},{28,24},{1,5},{5... | collective-permute-start | bytes 589832 | tf_op jit(solution)/shard_map/ppermute | solution.py:20
  128.9 7.3 %collective-permute-start.20 = (bf16[128,768]{0,1:T(8,128)(2,1)S(1)}, bf16[128,768]{0,1:T(8,128)(2,1)S(1)}, u32[]{:S(2)}, u32[]{:S(2)}) collective-permute-start(bf16[128,768]{0,1:T(8,128)(2,1)S(1)} %get-tuple-element.54), channel_id=1, source_target_pairs={{0,8},{4,12},{8,0},{12,4},{16,24},{20,28},{24,16},{28,20},{1,9},{5... | collective-permute-start | bytes 589832 | tf_op jit(solution)/shard_map/ppermute | solution.py:20
  138.4 9.8 %collective-permute-start.21 = (bf16[128,768]{0,1:T(8,128)(2,1)S(1)}, bf16[128,768]{0,1:T(8,128)(2,1)S(1)}, u32[]{:S(2)}, u32[]{:S(2)}) collective-permute-start(bf16[128,768]{0,1:T(8,128)(2,1)S(1)} %fusion.55), channel_id=1, source_target_pairs={{0,1},{1,2},{2,3},{3,0},{4,5},{5,6},{6,7},{7,4},{8,9},{9,10},{10,1... | collective-permute-start | bytes 589832 | tf_op jit(solution)/shard_map/ppermute | solution.py:29
  139.1 16.3 %collective-permute-start.22 = (bf16[128,768]{0,1:T(8,128)(2,1)S(1)}, bf16[128,768]{0,1:T(8,128)(2,1)S(1)}, u32[]{:S(2)}, u32[]{:S(2)}) collective-permute-start(bf16[128,768]{0,1:T(8,128)(2,1)S(1)} %fusion.55), channel_id=1, source_target_pairs={{0,2},{1,3},{2,0},{3,1},{4,6},{5,7},{6,4},{7,5},{8,10},{9,11},{10,... | collective-permute-start | bytes 589832 | tf_op jit(solution)/shard_map/ppermute | solution.py:29
  140.8 14.6 %collective-permute-start.23 = (bf16[128,768]{0,1:T(8,128)(2,1)S(1)}, bf16[128,768]{0,1:T(8,128)(2,1)S(1)}, u32[]{:S(2)}, u32[]{:S(2)}) collective-permute-start(bf16[128,768]{0,1:T(8,128)(2,1)S(1)} %fusion.55), channel_id=1, source_target_pairs={{0,3},{1,0},{2,1},{3,2},{4,7},{5,4},{6,5},{7,6},{8,11},{9,8},{10,9... | collective-permute-start | bytes 589832 | tf_op jit(solution)/shard_map/ppermute | solution.py:29
  159.6 3.6 %collective-permute-start.25 = (f32[512]{0:T(512)S(1)}, f32[512]{0:T(512)S(1)}, u32[]{:S(2)}, u32[]{:S(2)}) collective-permute-start(f32[512]{0:T(512)S(1)} %add.251), channel_id=1, source_target_pairs={{0,8},{4,12},{8,0},{12,4},{16,24},{20,28},{24,16},{28,20},{1,9},{5... | collective-permute-start | bytes 6152 | tf_op jit(solution)/shard_map/ppermute | solution.py:20
  163.2 3.6 %collective-permute-start.26 = (f32[512]{0:T(512)S(1)}, f32[512]{0:T(512)S(1)}, u32[]{:S(2)}, u32[]{:S(2)}) collective-permute-start(f32[512]{0:T(512)S(1)} %add.252), channel_id=1, source_target_pairs={{0,16},{4,20},{8,24},{12,28},{16,0},{20,4},{24,8},{28,12},{1,17},{... | collective-permute-start | bytes 6152 | tf_op jit(solution)/shard_map/ppermute | solution.py:20
  171.2 3.6 %collective-permute-start.28 = (f32[512]{0:T(512)S(1)}, f32[512]{0:T(512)S(1)}, u32[]{:S(2)}, u32[]{:S(2)}) collective-permute-start(f32[512]{0:T(512)S(1)} %add.255), channel_id=1, source_target_pairs={{0,8},{4,12},{8,0},{12,4},{16,24},{20,28},{24,16},{28,20},{1,9},{5... | collective-permute-start | bytes 6152 | tf_op jit(solution)/shard_map/ppermute | solution.py:20
  174.8 3.6 %collective-permute-start.29 = (f32[512]{0:T(512)S(1)}, f32[512]{0:T(512)S(1)}, u32[]{:S(2)}, u32[]{:S(2)}) collective-permute-start(f32[512]{0:T(512)S(1)} %add.256), channel_id=1, source_target_pairs={{0,16},{4,20},{8,24},{12,28},{16,0},{20,4},{24,8},{28,12},{1,17},{... | collective-permute-start | bytes 6152 | tf_op jit(solution)/shard_map/ppermute | solution.py:20
  181.8 3.6 %collective-permute-start.31 = (f32[512]{0:T(512)S(1)}, f32[512]{0:T(512)S(1)}, u32[]{:S(2)}, u32[]{:S(2)}) collective-permute-start(f32[512]{0:T(512)S(1)} %add.259), channel_id=1, source_target_pairs={{0,8},{4,12},{8,0},{12,4},{16,24},{20,28},{24,16},{28,20},{1,9},{5... | collective-permute-start | bytes 6152 | tf_op jit(solution)/shard_map/ppermute | solution.py:20
  185.4 3.6 %collective-permute-start.32 = (f32[512]{0:T(512)S(1)}, f32[512]{0:T(512)S(1)}, u32[]{:S(2)}, u32[]{:S(2)}) collective-permute-start(f32[512]{0:T(512)S(1)} %add.260), channel_id=1, source_target_pairs={{0,16},{4,20},{8,24},{12,28},{16,0},{20,4},{24,8},{28,12},{1,17},{... | collective-permute-start | bytes 6152 | tf_op jit(solution)/shard_map/ppermute | solution.py:20
  191.6 3.5 %collective-permute-start.34 = (f32[128]{0:T(128)S(1)}, f32[128]{0:T(128)S(1)}, u32[]{:S(2)}, u32[]{:S(2)}) collective-permute-start(f32[128]{0:T(128)S(1)} %add.263), channel_id=1, source_target_pairs={{0,8},{4,12},{8,0},{12,4},{16,24},{20,28},{24,16},{28,20},{1,9},{5... | collective-permute-start | bytes 1544 | tf_op jit(solution)/shard_map/ppermute | solution.py:20
  195.1 3.5 %collective-permute-start.35 = (f32[128]{0:T(128)S(1)}, f32[128]{0:T(128)S(1)}, u32[]{:S(2)}, u32[]{:S(2)}) collective-permute-start(f32[128]{0:T(128)S(1)} %add.264), channel_id=1, source_target_pairs={{0,16},{4,20},{8,24},{12,28},{16,0},{20,4},{24,8},{28,12},{1,17},{... | collective-permute-start | bytes 1544 | tf_op jit(solution)/shard_map/ppermute | solution.py:20
  (21 other events, 60.0 us)

commit v3 on v2

--- a/solution.py
+++ b/solution.py
@@ -47,14 +47,14 @@
 
 
 def pattern_mask(pattern, row_atoms, col_atoms):
-    atoms_dev = pattern.shape[0]
-    col_onehot = (col_atoms[None, :] == jnp.arange(atoms_dev, dtype=jnp.int32)[:, None])
-    per_row = jnp.dot(
-        pattern.astype(jnp.float32), col_onehot.astype(jnp.float32), precision=lax.Precision.HIGHEST
+    levels = jnp.arange(pattern.shape[0], dtype=jnp.int32)
+    row_onehot = (row_atoms[:, None] == levels[None, :]).astype(jnp.bfloat16)
+    col_onehot = (col_atoms[:, None] == levels[None, :]).astype(jnp.bfloat16)
+    per_row = jnp.dot(row_onehot, pattern.astype(jnp.bfloat16), preferred_element_type=jnp.float32)
+    mask = lax.dot_general(
+        per_row.astype(jnp.bfloat16), col_onehot, (((1,), (1,)), ((), ())),
+        preferred_element_type=jnp.float32,
     )
-    mask = jnp.broadcast_to(per_row[0][None, :], (row_atoms.shape[0], col_atoms.shape[0]))
-    for atom in range(1, atoms_dev):
-        mask = jnp.where((row_atoms == atom)[:, None], per_row[atom][None, :], mask)
     return mask > 0.5
 
 
@@ -87,7 +87,7 @@
         )
         own_mask = pattern_mask(pair_pattern[round_index], own_atoms, other_atoms)
         own_pair = jnp.where(own_mask, pair_block[round_index], jnp.zeros((), jnp.bfloat16))
-        own_pair_t.append(own_pair.T)
+        own_pair_t.append(own_pair)
         received = shipped[round_index]
         other_pattern = received[orb_dev : orb_dev + atoms_dev, :atoms_dev]
         other_mask = pattern_mask(other_pattern, other_atoms, own_atoms)
@@ -99,20 +99,28 @@
         result = jnp.dot(values, diag_sym, preferred_element_type=jnp.float32)
         for round_index in range(ROUNDS):
             other_rows = swapped(values, "atoms", round_index)
-            result = result + jnp.dot(
-                other_rows, own_pair_t[round_index], preferred_element_type=jnp.float32
+            result = result + lax.dot_general(
+                other_rows, own_pair_t[round_index], (((1,), (1,)), ((), ())),
+                preferred_element_type=jnp.float32,
             )
             result = result + jnp.dot(
                 other_rows, other_pair[round_index], preferred_element_type=jnp.float32
             )
         return result
 
-    previous = subspace.astype(jnp.float32)
-    current = (apply_operator(subspace) - filter_center * previous) / filter_half
-    for degree_index in range(1, DEGREE):
-        applied = apply_operator(current.astype(jnp.bfloat16))
-        following = 2.0 * (applied - filter_center * current) / filter_half - previous
-        previous, current = (current, following)
+    def chebyshev(start_rows):
+        previous = start_rows.astype(jnp.float32)
+        current = (apply_operator(start_rows) - filter_center * previous) / filter_half
+        for degree_index in range(1, DEGREE):
+            applied = apply_operator(current.astype(jnp.bfloat16))
+            following = 2.0 * (applied - filter_center * current) / filter_half - previous
+            previous, current = (current, following)
+        return current
+
+    half_bands = subspace.shape[0] // 2
+    current = jnp.concatenate(
+        [chebyshev(subspace[:half_bands]), chebyshev(subspace[half_bands:])], axis=0
+    )
     total_orbitals = orb_dev * lax.axis_size("atoms")
     rot_steps, all_bands, _ = rotations.shape
     full_rot = jnp.transpose(full_rot, (1, 2, 0, 3)).reshape(rot_steps, all_bands, all_bands)

time: 201 us -> 200 us (level)
  waiting for transfers between devices: 95.1 us -> 68.1 us
  starting transfers between devices: 26.1 us -> 43.5 us
  matrix products: 38.8 us -> 55.6 us
  other arithmetic: 25.4 us -> 17.7 us
    ppermute x30 -> x46, starting transfers between devices: 16.6 us -> 34.1 us  [swapped(): return lax.ppermute(value, axis, pairs)]
    dot_general x20 -> x36, matrix products: 13.7 us -> 28.9 us  [the longest x32 20.4 us: apply_operator(): lax.dot_general(other_rows, own_pair_t[round_index], (((1,), (1,)), ((),...]
    ppermute x6, waiting for transfers between devices: 27.8 us -> 12.7 us  [gather_bands(): pieces.append(lax.ppermute(value, 'bands', pairs))]
    ppermute x30 -> x46, waiting for transfers between devices: 67.3 us -> 55.4 us  [swapped(): return lax.ppermute(value, axis, pairs)]
    select_n x3 -> x0, other arithmetic: 8.94 us -> none  [the longest x2 4.96 us: body(): jnp.where(other_mask, received[:orb_dev], jnp.zeros((), jnp.bfloat16))]
    dot_general x16 -> x32, matrix products: 11.1 us -> 13.9 us  [apply_operator(): jnp.dot(other_rows, other_pair[round_index], preferred_element_type=jnp.f...]
    dot_general x3, matrix products: 7.16 us -> 4.72 us  [body(): lax.dot_general(full_rot[rotation_index], basis_all, (((0,), (0,)), ((),...]
    dot_general x8 -> x16, matrix products: 5.38 us -> 6.62 us  [apply_operator(): result = jnp.dot(values, diag_sym, preferred_element_type=jnp.float32)]
  transfers between devices with their start and end apart: 36 -> 52, of which waited for: 23 -> 27; matrix products, arithmetic and copies ran while one was open for 25% -> 36% of each run, Pallas kernels for 0% -> 0%
where the time goes in v3:
time: 200 us; the launch traced here: 198 us
  waiting for transfers between devices  68.1 us (34%)
  matrix products  55.6 us (28%)
  starting transfers between devices  43.5 us (22%)
  other arithmetic  17.7 us (9%)
  local copies, waits for them, and re-layouts  12.4 us (6%)
    ppermute x46, waiting for transfers between devices, swapped(): return lax.ppermute(value, axis, pairs)  55.4 us
    ppermute x46, starting transfers between devices, swapped(): return lax.ppermute(value, axis, pairs)  34.1 us
    dot_general x32, matrix products, apply_operator(): lax.dot_general(other_rows, own_pair_t[round_index], (((1,), (1,)), ((),...  20.4 us
    dot_general x32, matrix products, apply_operator(): jnp.dot(other_rows, other_pair[round_index], preferred_element_type=jnp.f...  13.9 us
    ppermute x6, waiting for transfers between devices, gather_bands(): pieces.append(lax.ppermute(value, 'bands', pairs))  12.7 us
    ppermute x6, starting transfers between devices, gather_bands(): pieces.append(lax.ppermute(value, 'bands', pairs))  9.39 us
    dot_general x4, matrix products, pattern_mask(): lax.dot_general(per_row.astype(jnp.bfloat16), col_onehot, (((1,), (1,)),...  8.51 us
    dot_general x16, matrix products, apply_operator(): result = jnp.dot(values, diag_sym, preferred_element_type=jnp.float32)  6.62 us
  transfers between devices with their start and end apart: 52, of which 27 were waited for; matrix products, arithmetic and copies ran while one was open for 36% of the time, Pallas kernels for 0%

profile of v3, /device:TPU:0, one launch (start us, length us, event | category | flops | bytes accessed | tf_op | source)
XLA Modules:
  0.0 198.1 jit_solution(3048104390205325613)
XLA Ops:
  2.1 2.5 %collective-permute-start.5 = (bf16[64,768]{1,0:T(8,128)(2,1)}, bf16[64,768]{1,0:T(8,128)(2,1)}, u32[]{:S(2)}, u32[]{:S(2)}) collective-permute-start(bf16[64,768]{1,0:T(8,128)(2,1)} %get-tuple-element.13), channel_id=1, source_target_pairs={{0,8},{4,12},{8,0},{12,4},{16,24},{20,28},{24,16},{28,20},{1,9},{5... | collective-permute-start | bytes 294920 | tf_op jit(solution)/shard_map/ppermute | solution.py:20
  6.1 2.6 %collective-permute-start.1 = (bf16[4,512,128]{2,1,0:T(8,128)(2,1)}, bf16[4,512,128]{2,1,0:T(8,128)(2,1)}, u32[]{:S(2)}, u32[]{:S(2)}) collective-permute-start(bf16[4,512,128]{2,1,0:T(8,128)(2,1)} %param.11), channel_id=1, source_target_pairs={{0,2},{1,3},{2,0},{3,1},{4,6},{5,7},{6,4},{7,5},{8,10},{9,11},{10,... | collective-permute-start | bytes 1572872 | tf_op jit(solution)/shard_map/ppermute | solution.py:29
  12.1 3.3 %add_multiply_fusion = f32[768,768]{1,0:T(8,128)} fusion(bf16[768,768]{1,0:T(8,128)(2,1)} %param.7, s32[768]{0:T(1024)S(1)} %get-tuple-element.54), kind=kLoop, calls=%fused_computation.7 | loop fusion | flops 4128768 | bytes 3542016 | tf_op jit(solution)/shard_map/mul | solution.py:79
  15.4 2.0 %copy.19 = f32[768,768]{0,1:T(8,128)S(1)} copy(f32[768,768]{1,0:T(8,128)} %add_multiply_fusion) | data formatting | bytes 4718592 | tf_op jit(solution)/shard_map/mul | solution.py:79
  17.4 2.0 %fusion.2 = bf16[768,768]{1,0:T(8,128)(2,1)S(1)} fusion(f32[768,768]{0,1:T(8,128)S(1)} %copy.19, s32[768]{0:T(1024)S(1)} %get-tuple-element.54, bf16[768,768]{1,0:T(8,128)(2,1)} %param.7), kind=kLoop, calls=%fused_computation.6 | loop fusion | flops 5308416 | bytes 4721664 | tf_op jit(solution)/shard_map/convert_element_type | solution.py:80
  24.0 2.1 %compare_select_fusion.3 = bf16[768,768]{1,0:T(8,128)(2,1)S(1)} fusion(s32[768]{0:T(1024)} %convert_reduce_fusion.1, s32[768]{0:T(1024)S(1)} %get-tuple-element.54, bf16[2,4,4]{2,1,0:T(4,128)(2,1)S(1)} %convert.14, bf16[2,768,768]{2,1,0:T(8,128)(2,1)} %param.8), kind=kOutput, calls=%fused_computation.11 | convolution fusion | flops 5932032 | bytes 2367488 | tf_op jit(solution)/shard_map/dot_general | solution.py:54
  26.2 2.1 %compare_select_fusion.1 = bf16[768,768]{1,0:T(8,128)(2,1)S(1)} fusion(s32[768]{0:T(1024)} %get-tuple-element.53, s32[768]{0:T(1024)S(1)} %get-tuple-element.54, bf16[2,4,4]{2,1,0:T(4,128)(2,1)S(1)} %convert.14, bf16[2,768,768]{2,1,0:T(8,128)(2,1)} %param.8), kind=kOutput, calls=%fused_computation.9 | convolution fusion | flops 5932032 | bytes 2367488 | tf_op jit(solution)/shard_map/dot_general | solution.py:54
  28.4 2.8 %fusion.4 = bf16[784,768]{1,0:T(8,128)(2,1)} fusion(bf16[4,4]{1,0:T(4,128)(2,1)S(1)} %get-tuple-element.16, bf16[768,768]{1,0:T(8,128)(2,1)} %get-tuple-element.9), kind=kLoop, calls=%fused_computation.21 | loop fusion | flops 3612672 | bytes 2383904 | tf_op jit(solution)/shard_map/concatenate | solution.py:71
  32.5 2.1 %convolution_add_fusion.31 = f32[768,64]{0,1:T(8,128)} fusion(f32[768,64]{0,1:T(8,128)S(1)} %copy-done.12, bf16[768,768]{1,0:T(8,128)(2,1)S(1)} %compare_select_fusion.3, bf16[64,768]{1,0:T(8,128)(2,1)} %collective-permute-done.3), kind=kOutput, calls=%fused_computation.133 | convolution fusion | flops 75546624 | bytes 1671168 | tf_op jit(solution)/shard_map/dot_general | solution.py:102
  37.8 2.1 %fusion.131 = f32[768,64]{0,1:T(8,128)} fusion(bf16[768,768]{1,0:T(8,128)(2,1)S(1)} %compare_select_fusion.1, bf16[64,768]{1,0:T(8,128)(2,1)} %collective-permute-done.5), kind=kOutput, calls=%fused_computation.217 | convolution fusion | flops 75497472 | bytes 1474560 | tf_op jit(solution)/shard_map/dot_general | solution.py:102
  39.8 25.9 %collective-permute-done.22 = bf16[64,768]{1,0:T(8,128)(2,1)S(1)} collective-permute-done((bf16[64,768]{1,0:T(8,128)(2,1)S(1)}, bf16[64,768]{1,0:T(8,128)(2,1)S(1)}, u32[]{:S(2)}, u32[]{:S(2)}) %collective-permute-start.22) | collective-permute-done | bytes 98336 | tf_op jit(solution)/shard_map/ppermute | solution.py:20
  67.0 3.0 %pad_maximum_fusion = bf16[4,4,512,128]{3,2,1,0:T(8,128)(2,1)} fusion(bf16[1,4,512,128]{3,2,1,0:T(8,128)(2,1)} %bitcast.3, bf16[1,4,512,128]{3,2,1,0:T(8,128)(2,1)} %bitcast.2, bf16[1,4,512,128]{3,2,1,0:T(8,128)(2,1)} %bitcast.1, bf16[1,4,512,128]{3,2,1,0:T(8,128)(2,1)S(1)} %bitcast.226), kind=kLoop, calls=%fused_computation.12 | loop fusion | flops 3145728 | bytes 4194304 | tf_op jit(solution)/shard_map/stack | solution.py:31
  69.9 3.8 %gather_fusion = bf16[4,4,512,128]{3,2,1,0:T(8,128)(2,1)} fusion(bf16[4,4,512,128]{3,2,1,0:T(8,128)(2,1)} %pad_maximum_fusion, s32[1024]{0:T(1024)S(1)} %pad_clamp_fusion), kind=kCustom, calls=%fused_computation | custom fusion | bytes 4194320 | tf_op jit(solution)/shard_map/jit(_take)/gather | solution.py:31
  73.7 3.2 %select_bitcast_fusion = bf16[4,512,4,128]{3,1,0,2:T(8,128)(2,1)} fusion(bf16[4,4,512,128]{3,2,1,0:T(8,128)(2,1)} %gather_fusion, pred[4]{0:T(512)(128)(4,1)S(1)} %compare_and_fusion), kind=kLoop, calls=%fused_computation.13 | loop fusion | flops 1048576 | bytes 4194308 | tf_op jit(solution)/shard_map/jit(_take)/select_n | solution.py:31
  76.9 2.1 %compare_select_fusion = bf16[768,768]{1,0:T(8,128)(2,1)S(1)} fusion(bf16[784,768]{1,0:T(8,128)(2,1)} %collective-permute-done.6, s32[768]{0:T(1024)S(1)} %copy-done.21, s32[768]{0:T(1024)S(1)} %get-tuple-element.54), kind=kOutput, calls=%fused_computation.8 | convolution fusion | flops 5932032 | bytes 2366464 | tf_op jit(solution)/shard_map/dot_general | solution.py:54
  79.1 2.0 %fusion.175 = f32[768,64]{0,1:T(8,128)} fusion(bf16[64,768]{1,0:T(8,128)(2,1)} %collective-permute-done.5, bf16[768,768]{1,0:T(8,128)(2,1)S(1)} %compare_select_fusion), kind=kOutput, calls=%fused_computation.261 | convolution fusion | flops 75497472 | bytes 1474560 | tf_op jit(solution)/shard_map/dot_general | solution.py:106
  81.1 2.1 %compare_select_fusion.2 = bf16[768,768]{1,0:T(8,128)(2,1)S(1)} fusion(bf16[784,768]{1,0:T(8,128)(2,1)} %collective-permute-done.4, s32[768]{0:T(1024)S(1)} %copy-done.20, s32[768]{0:T(1024)S(1)} %get-tuple-element.54), kind=kOutput, calls=%fused_computation.10 | convolution fusion | flops 5932032 | bytes 2366464 | tf_op jit(solution)/shard_map/dot_general | solution.py:54
  110.1 1.6 collective-permute-start.30
  135.2 1.9 collective-permute-done.36
  140.9 2.8 %collective-permute-start.39 = (bf16[128,768]{1,0:T(8,128)(2,1)S(1)}, bf16[128,768]{1,0:T(8,128)(2,1)S(1)}, u32[]{:S(2)}, u32[]{:S(2)}) collective-permute-start(bf16[128,768]{1,0:T(8,128)(2,1)S(1)} %pad_maximum_fusion.2), channel_id=1, source_target_pairs={{0,3},{1,0},{2,1},{3,2},{4,7},{5,4},{6,5},{7,6},{8,11},{9,8},{10,9... | collective-permute-start | bytes 589832 | tf_op jit(solution)/shard_map/ppermute | solution.py:29
  144.0 5.5 %collective-permute-done.37 = bf16[128,768]{1,0:T(8,128)(2,1)S(1)} collective-permute-done((bf16[128,768]{1,0:T(8,128)(2,1)S(1)}, bf16[128,768]{1,0:T(8,128)(2,1)S(1)}, u32[]{:S(2)}, u32[]{:S(2)}) %collective-permute-start.37) | collective-permute-done | bytes 196640 | tf_op jit(solution)/shard_map/ppermute | solution.py:29
  149.5 7.2 %collective-permute-done.38 = bf16[128,768]{1,0:T(8,128)(2,1)S(1)} collective-permute-done((bf16[128,768]{1,0:T(8,128)(2,1)S(1)}, bf16[128,768]{1,0:T(8,128)(2,1)S(1)}, u32[]{:S(2)}, u32[]{:S(2)}) %collective-permute-start.38) | collective-permute-done | bytes 196640 | tf_op jit(solution)/shard_map/ppermute | solution.py:29
  161.0 2.0 %collective-permute-done.41 = f32[512]{0:T(512)S(1)} collective-permute-done((f32[512]{0:T(512)S(1)}, f32[512]{0:T(512)S(1)}, u32[]{:S(2)}, u32[]{:S(2)}) %collective-permute-start.41) | collective-permute-done | bytes 2080 | tf_op jit(solution)/shard_map/ppermute | solution.py:20
  164.7 1.8 collective-permute-done.42
  166.6 1.9 multiply_reduce_fusion.1
  171.2 2.0 %collective-permute-done.44 = f32[512]{0:T(512)S(1)} collective-permute-done((f32[512]{0:T(512)S(1)}, f32[512]{0:T(512)S(1)}, u32[]{:S(2)}, u32[]{:S(2)}) %collective-permute-start.44) | collective-permute-done | bytes 2080 | tf_op jit(solution)/shard_map/ppermute | solution.py:20
  174.9 1.8 collective-permute-done.45
  176.8 2.2 %multiply_reduce_fusion = (f32[512]{0:T(512)S(1)}, f32[512,768]{1,0:T(8,128)S(1)}) fusion(bf16[512,512]{0,1:T(8,128)(2,1)S(1)} %bitcast.225, f32[512,768]{1,0:T(8,128)} %get-tuple-element.48, f32[512]{0:T(512)S(1)} %add_sqrt_fusion.1), kind=kOutput, calls=%fused_computation.15 | convolution fusion | flops 404225536 | bytes 3674112 | tf_op jit(solution)/shard_map/dot_general | solution.py:129
  181.8 2.0 %collective-permute-done.47 = f32[512]{0:T(512)S(1)} collective-permute-done((f32[512]{0:T(512)S(1)}, f32[512]{0:T(512)S(1)}, u32[]{:S(2)}, u32[]{:S(2)}) %collective-permute-start.47) | collective-permute-done | bytes 2080 | tf_op jit(solution)/shard_map/ppermute | solution.py:20
  185.3 2.1 %collective-permute-done.48 = f32[512]{0:T(512)S(1)} collective-permute-done((f32[512]{0:T(512)S(1)}, f32[512]{0:T(512)S(1)}, u32[]{:S(2)}, u32[]{:S(2)}) %collective-permute-start.48) | collective-permute-done | bytes 2080 | tf_op jit(solution)/shard_map/ppermute | solution.py:20
  191.6 2.0 collective-permute-done.50
  195.1 2.0 %collective-permute-done.51 = f32[128]{0:T(128)S(1)} collective-permute-done((f32[128]{0:T(128)S(1)}, f32[128]{0:T(128)S(1)}, u32[]{:S(2)}, u32[]{:S(2)}) %collective-permute-start.51) | collective-permute-done | bytes 544 | tf_op jit(solution)/shard_map/ppermute | solution.py:20
  (247 shorter events, 92.6 us)
Async XLA Ops:
  1.6 30.7 %collective-permute-start.3 = (bf16[64,768]{1,0:T(8,128)(2,1)}, bf16[64,768]{1,0:T(8,128)(2,1)}, u32[]{:S(2)}, u32[]{:S(2)}) collective-permute-start(bf16[64,768]{1,0:T(8,128)(2,1)} %get-tuple-element.13), channel_id=1, source_target_pairs={{0,4},{4,0},{8,12},{12,8},{16,20},{20,16},{24,28},{28,24},{1,5},{5... | collective-permute-start | bytes 294920 | tf_op jit(solution)/shard_map/ppermute | solution.py:20
  2.1 34.2 %collective-permute-start.5 = (bf16[64,768]{1,0:T(8,128)(2,1)}, bf16[64,768]{1,0:T(8,128)(2,1)}, u32[]{:S(2)}, u32[]{:S(2)}) collective-permute-start(bf16[64,768]{1,0:T(8,128)(2,1)} %get-tuple-element.13), channel_id=1, source_target_pairs={{0,8},{4,12},{8,0},{12,4},{16,24},{20,28},{24,16},{28,20},{1,9},{5... | collective-permute-start | bytes 294920 | tf_op jit(solution)/shard_map/ppermute | solution.py:20
  4.6 62.4 %collective-permute-start = (bf16[4,512,128]{2,1,0:T(8,128)(2,1)}, bf16[4,512,128]{2,1,0:T(8,128)(2,1)}, u32[]{:S(2)}, u32[]{:S(2)}) collective-permute-start(bf16[4,512,128]{2,1,0:T(8,128)(2,1)} %param.11), channel_id=1, source_target_pairs={{0,1},{1,2},{2,3},{3,0},{4,5},{5,6},{6,7},{7,4},{8,9},{9,10},{10,1... | collective-permute-start | bytes 1572872 | tf_op jit(solution)/shard_map/ppermute | solution.py:29
  6.1 60.8 %collective-permute-start.1 = (bf16[4,512,128]{2,1,0:T(8,128)(2,1)}, bf16[4,512,128]{2,1,0:T(8,128)(2,1)}, u32[]{:S(2)}, u32[]{:S(2)}) collective-permute-start(bf16[4,512,128]{2,1,0:T(8,128)(2,1)} %param.11), channel_id=1, source_target_pairs={{0,2},{1,3},{2,0},{3,1},{4,6},{5,7},{6,4},{7,5},{8,10},{9,11},{10,... | collective-permute-start | bytes 1572872 | tf_op jit(solution)/shard_map/ppermute | solution.py:29
  8.7 58.2 %collective-permute-start.2 = (bf16[4,512,128]{2,1,0:T(8,128)(2,1)}, bf16[4,512,128]{2,1,0:T(8,128)(2,1)}, u32[]{:S(2)}, u32[]{:S(2)}) collective-permute-start(bf16[4,512,128]{2,1,0:T(8,128)(2,1)} %param.11), channel_id=1, source_target_pairs={{0,3},{1,0},{2,1},{3,2},{4,7},{5,4},{6,5},{7,6},{8,11},{9,8},{10,9... | collective-permute-start | bytes 1572872 | tf_op jit(solution)/shard_map/ppermute | solution.py:29
  34.5 42.4 %collective-permute-start.6 = (bf16[784,768]{1,0:T(8,128)(2,1)}, bf16[784,768]{1,0:T(8,128)(2,1)}, u32[]{:S(2)}, u32[]{:S(2)}) collective-permute-start(bf16[784,768]{1,0:T(8,128)(2,1)} %fusion.4), channel_id=1, source_target_pairs={{0,8},{4,12},{8,0},{12,4},{16,24},{20,28},{24,16},{28,20},{1,9},{5... | collective-permute-start | bytes 3612680 | tf_op jit(solution)/shard_map/ppermute | solution.py:20
  36.2 29.5 %collective-permute-start.22 = (bf16[64,768]{1,0:T(8,128)(2,1)S(1)}, bf16[64,768]{1,0:T(8,128)(2,1)S(1)}, u32[]{:S(2)}, u32[]{:S(2)}) collective-permute-start(bf16[64,768]{1,0:T(8,128)(2,1)S(1)} %copy-done.18), channel_id=1, source_target_pairs={{0,8},{4,12},{8,0},{12,4},{16,24},{20,28},{24,16},{28,20},{1,9},{5... | collective-permute-start | bytes 294920 | tf_op jit(solution)/shard_map/ppermute | solution.py:20
  65.8 15.3 %collective-permute-start.4 = (bf16[784,768]{1,0:T(8,128)(2,1)}, bf16[784,768]{1,0:T(8,128)(2,1)}, u32[]{:S(2)}, u32[]{:S(2)}) collective-permute-start(bf16[784,768]{1,0:T(8,128)(2,1)} %fusion.3), channel_id=1, source_target_pairs={{0,4},{4,0},{8,12},{12,8},{16,20},{20,16},{24,28},{28,24},{1,5},{5... | collective-permute-start | bytes 3612680 | tf_op jit(solution)/shard_map/ppermute | solution.py:20
  85.2 6.2 %collective-permute-start.7 = (bf16[64,768]{1,0:T(8,128)(2,1)S(1)}, bf16[64,768]{1,0:T(8,128)(2,1)S(1)}, u32[]{:S(2)}, u32[]{:S(2)}) collective-permute-start(bf16[64,768]{1,0:T(8,128)(2,1)S(1)} %get-tuple-element.31), channel_id=1, source_target_pairs={{0,4},{4,0},{8,12},{12,8},{16,20},{20,16},{24,28},{28,24},{1,5},{5... | collective-permute-start | bytes 294920 | tf_op jit(solution)/shard_map/ppermute | solution.py:20
  87.3 6.7 %collective-permute-start.23 = (bf16[64,768]{1,0:T(8,128)(2,1)S(1)}, bf16[64,768]{1,0:T(8,128)(2,1)S(1)}, u32[]{:S(2)}, u32[]{:S(2)}) collective-permute-start(bf16[64,768]{1,0:T(8,128)(2,1)S(1)} %get-tuple-element.17), channel_id=1, source_target_pairs={{0,4},{4,0},{8,12},{12,8},{16,20},{20,16},{24,28},{28,24},{1,5},{5... | collective-permute-start | bytes 294920 | tf_op jit(solution)/shard_map/ppermute | solution.py:20
  87.7 5.5 %collective-permute-start.24 = (bf16[64,768]{1,0:T(8,128)(2,1)S(1)}, bf16[64,768]{1,0:T(8,128)(2,1)S(1)}, u32[]{:S(2)}, u32[]{:S(2)}) collective-permute-start(bf16[64,768]{1,0:T(8,128)(2,1)S(1)} %get-tuple-element.17), channel_id=1, source_target_pairs={{0,8},{4,12},{8,0},{12,4},{16,24},{20,28},{24,16},{28,20},{1,9},{5... | collective-permute-start | bytes 294920 | tf_op jit(solution)/shard_map/ppermute | solution.py:20
  92.6 6.1 %collective-permute-start.9 = (bf16[64,768]{1,0:T(8,128)(2,1)S(1)}, bf16[64,768]{1,0:T(8,128)(2,1)S(1)}, u32[]{:S(2)}, u32[]{:S(2)}) collective-permute-start(bf16[64,768]{1,0:T(8,128)(2,1)S(1)} %get-tuple-element.33), channel_id=1, source_target_pairs={{0,4},{4,0},{8,12},{12,8},{16,20},{20,16},{24,28},{28,24},{1,5},{5... | collective-permute-start | bytes 294920 | tf_op jit(solution)/shard_map/ppermute | solution.py:20
  95.2 6.1 %collective-permute-start.25 = (bf16[64,768]{1,0:T(8,128)(2,1)S(1)}, bf16[64,768]{1,0:T(8,128)(2,1)S(1)}, u32[]{:S(2)}, u32[]{:S(2)}) collective-permute-start(bf16[64,768]{1,0:T(8,128)(2,1)S(1)} %get-tuple-element.19), channel_id=1, source_target_pairs={{0,4},{4,0},{8,12},{12,8},{16,20},{20,16},{24,28},{28,24},{1,5},{5... | collective-permute-start | bytes 294920 | tf_op jit(solution)/shard_map/ppermute | solution.py:20
  99.9 6.1 %collective-permute-start.11 = (bf16[64,768]{1,0:T(8,128)(2,1)S(1)}, bf16[64,768]{1,0:T(8,128)(2,1)S(1)}, u32[]{:S(2)}, u32[]{:S(2)}) collective-permute-start(bf16[64,768]{1,0:T(8,128)(2,1)S(1)} %get-tuple-element.35), channel_id=1, source_target_pairs={{0,4},{4,0},{8,12},{12,8},{16,20},{20,16},{24,28},{28,24},{1,5},{5... | collective-permute-start | bytes 294920 | tf_op jit(solution)/shard_map/ppermute | solution.py:20
  102.7 6.1 %collective-permute-start.27 = (bf16[64,768]{1,0:T(8,128)(2,1)S(1)}, bf16[64,768]{1,0:T(8,128)(2,1)S(1)}, u32[]{:S(2)}, u32[]{:S(2)}) collective-permute-start(bf16[64,768]{1,0:T(8,128)(2,1)S(1)} %get-tuple-element.21), channel_id=1, source_target_pairs={{0,4},{4,0},{8,12},{12,8},{16,20},{20,16},{24,28},{28,24},{1,5},{5... | collective-permute-start | bytes 294920 | tf_op jit(solution)/shard_map/ppermute | solution.py:20
  107.2 6.1 %collective-permute-start.13 = (bf16[64,768]{1,0:T(8,128)(2,1)S(1)}, bf16[64,768]{1,0:T(8,128)(2,1)S(1)}, u32[]{:S(2)}, u32[]{:S(2)}) collective-permute-start(bf16[64,768]{1,0:T(8,128)(2,1)S(1)} %get-tuple-element.37), channel_id=1, source_target_pairs={{0,4},{4,0},{8,12},{12,8},{16,20},{20,16},{24,28},{28,24},{1,5},{5... | collective-permute-start | bytes 294920 | tf_op jit(solution)/shard_map/ppermute | solution.py:20
  107.3 5.2 %collective-permute-start.14 = (bf16[64,768]{1,0:T(8,128)(2,1)S(1)}, bf16[64,768]{1,0:T(8,128)(2,1)S(1)}, u32[]{:S(2)}, u32[]{:S(2)}) collective-permute-start(bf16[64,768]{1,0:T(8,128)(2,1)S(1)} %get-tuple-element.37), channel_id=1, source_target_pairs={{0,8},{4,12},{8,0},{12,4},{16,24},{20,28},{24,16},{28,20},{1,9},{5... | collective-permute-start | bytes 294920 | tf_op jit(solution)/shard_map/ppermute | solution.py:20
  110.0 6.1 %collective-permute-start.29 = (bf16[64,768]{1,0:T(8,128)(2,1)S(1)}, bf16[64,768]{1,0:T(8,128)(2,1)S(1)}, u32[]{:S(2)}, u32[]{:S(2)}) collective-permute-start(bf16[64,768]{1,0:T(8,128)(2,1)S(1)} %get-tuple-element.23), channel_id=1, source_target_pairs={{0,4},{4,0},{8,12},{12,8},{16,20},{20,16},{24,28},{28,24},{1,5},{5... | collective-permute-start | bytes 294920 | tf_op jit(solution)/shard_map/ppermute | solution.py:20
  110.1 5.2 %collective-permute-start.30 = (bf16[64,768]{1,0:T(8,128)(2,1)S(1)}, bf16[64,768]{1,0:T(8,128)(2,1)S(1)}, u32[]{:S(2)}, u32[]{:S(2)}) collective-permute-start(bf16[64,768]{1,0:T(8,128)(2,1)S(1)} %get-tuple-element.23), channel_id=1, source_target_pairs={{0,8},{4,12},{8,0},{12,4},{16,24},{20,28},{24,16},{28,20},{1,9},{5... | collective-permute-start | bytes 294920 | tf_op jit(solution)/shard_map/ppermute | solution.py:20
  114.5 6.1 %collective-permute-start.15 = (bf16[64,768]{1,0:T(8,128)(2,1)S(1)}, bf16[64,768]{1,0:T(8,128)(2,1)S(1)}, u32[]{:S(2)}, u32[]{:S(2)}) collective-permute-start(bf16[64,768]{1,0:T(8,128)(2,1)S(1)} %get-tuple-element.39), channel_id=1, source_target_pairs={{0,4},{4,0},{8,12},{12,8},{16,20},{20,16},{24,28},{28,24},{1,5},{5... | collective-permute-start | bytes 294920 | tf_op jit(solution)/shard_map/ppermute | solution.py:20
  114.6 5.2 %collective-permute-start.16 = (bf16[64,768]{1,0:T(8,128)(2,1)S(1)}, bf16[64,768]{1,0:T(8,128)(2,1)S(1)}, u32[]{:S(2)}, u32[]{:S(2)}) collective-permute-start(bf16[64,768]{1,0:T(8,128)(2,1)S(1)} %get-tuple-element.39), channel_id=1, source_target_pairs={{0,8},{4,12},{8,0},{12,4},{16,24},{20,28},{24,16},{28,20},{1,9},{5... | collective-permute-start | bytes 294920 | tf_op jit(solution)/shard_map/ppermute | solution.py:20
  117.3 6.1 %collective-permute-start.31 = (bf16[64,768]{1,0:T(8,128)(2,1)S(1)}, bf16[64,768]{1,0:T(8,128)(2,1)S(1)}, u32[]{:S(2)}, u32[]{:S(2)}) collective-permute-start(bf16[64,768]{1,0:T(8,128)(2,1)S(1)} %get-tuple-element.25), channel_id=1, source_target_pairs={{0,4},{4,0},{8,12},{12,8},{16,20},{20,16},{24,28},{28,24},{1,5},{5... | collective-permute-start | bytes 294920 | tf_op jit(solution)/shard_map/ppermute | solution.py:20
  121.8 6.1 %collective-permute-start.17 = (bf16[64,768]{1,0:T(8,128)(2,1)S(1)}, bf16[64,768]{1,0:T(8,128)(2,1)S(1)}, u32[]{:S(2)}, u32[]{:S(2)}) collective-permute-start(bf16[64,768]{1,0:T(8,128)(2,1)S(1)} %get-tuple-element.41), channel_id=1, source_target_pairs={{0,4},{4,0},{8,12},{12,8},{16,20},{20,16},{24,28},{28,24},{1,5},{5... | collective-permute-start | bytes 294920 | tf_op jit(solution)/shard_map/ppermute | solution.py:20
  121.9 5.2 %collective-permute-start.18 = (bf16[64,768]{1,0:T(8,128)(2,1)S(1)}, bf16[64,768]{1,0:T(8,128)(2,1)S(1)}, u32[]{:S(2)}, u32[]{:S(2)}) collective-permute-start(bf16[64,768]{1,0:T(8,128)(2,1)S(1)} %get-tuple-element.41), channel_id=1, source_target_pairs={{0,8},{4,12},{8,0},{12,4},{16,24},{20,28},{24,16},{28,20},{1,9},{5... | collective-permute-start | bytes 294920 | tf_op jit(solution)/shard_map/ppermute | solution.py:20
  124.6 6.1 %collective-permute-start.33 = (bf16[64,768]{1,0:T(8,128)(2,1)S(1)}, bf16[64,768]{1,0:T(8,128)(2,1)S(1)}, u32[]{:S(2)}, u32[]{:S(2)}) collective-permute-start(bf16[64,768]{1,0:T(8,128)(2,1)S(1)} %get-tuple-element.27), channel_id=1, source_target_pairs={{0,4},{4,0},{8,12},{12,8},{16,20},{20,16},{24,28},{28,24},{1,5},{5... | collective-permute-start | bytes 294920 | tf_op jit(solution)/shard_map/ppermute | solution.py:20
  129.1 8.6 %collective-permute-start.19 = (bf16[64,768]{1,0:T(8,128)(2,1)S(1)}, bf16[64,768]{1,0:T(8,128)(2,1)S(1)}, u32[]{:S(2)}, u32[]{:S(2)}) collective-permute-start(bf16[64,768]{1,0:T(8,128)(2,1)S(1)} %get-tuple-element.43), channel_id=1, source_target_pairs={{0,4},{4,0},{8,12},{12,8},{16,20},{20,16},{24,28},{28,24},{1,5},{5... | collective-permute-start | bytes 294920 | tf_op jit(solution)/shard_map/ppermute | solution.py:20
  129.2 5.2 %collective-permute-start.20 = (bf16[64,768]{1,0:T(8,128)(2,1)S(1)}, bf16[64,768]{1,0:T(8,128)(2,1)S(1)}, u32[]{:S(2)}, u32[]{:S(2)}) collective-permute-start(bf16[64,768]{1,0:T(8,128)(2,1)S(1)} %get-tuple-element.43), channel_id=1, source_target_pairs={{0,8},{4,12},{8,0},{12,4},{16,24},{20,28},{24,16},{28,20},{1,9},{5... | collective-permute-start | bytes 294920 | tf_op jit(solution)/shard_map/ppermute | solution.py:20
  131.9 6.6 %collective-permute-start.35 = (bf16[64,768]{1,0:T(8,128)(2,1)S(1)}, bf16[64,768]{1,0:T(8,128)(2,1)S(1)}, u32[]{:S(2)}, u32[]{:S(2)}) collective-permute-start(bf16[64,768]{1,0:T(8,128)(2,1)S(1)} %get-tuple-element.29), channel_id=1, source_target_pairs={{0,4},{4,0},{8,12},{12,8},{16,20},{20,16},{24,28},{28,24},{1,5},{5... | collective-permute-start | bytes 294920 | tf_op jit(solution)/shard_map/ppermute | solution.py:20
  132.0 5.2 %collective-permute-start.36 = (bf16[64,768]{1,0:T(8,128)(2,1)S(1)}, bf16[64,768]{1,0:T(8,128)(2,1)S(1)}, u32[]{:S(2)}, u32[]{:S(2)}) collective-permute-start(bf16[64,768]{1,0:T(8,128)(2,1)S(1)} %get-tuple-element.29), channel_id=1, source_target_pairs={{0,8},{4,12},{8,0},{12,4},{16,24},{20,28},{24,16},{28,20},{1,9},{5... | collective-permute-start | bytes 294920 | tf_op jit(solution)/shard_map/ppermute | solution.py:20
  139.8 9.8 %collective-permute-start.37 = (bf16[128,768]{1,0:T(8,128)(2,1)S(1)}, bf16[128,768]{1,0:T(8,128)(2,1)S(1)}, u32[]{:S(2)}, u32[]{:S(2)}) collective-permute-start(bf16[128,768]{1,0:T(8,128)(2,1)S(1)} %pad_maximum_fusion.2), channel_id=1, source_target_pairs={{0,1},{1,2},{2,3},{3,0},{4,5},{5,6},{6,7},{7,4},{8,9},{9,10},{10,1... | collective-permute-start | bytes 589832 | tf_op jit(solution)/shard_map/ppermute | solution.py:29
  140.5 16.2 %collective-permute-start.38 = (bf16[128,768]{1,0:T(8,128)(2,1)S(1)}, bf16[128,768]{1,0:T(8,128)(2,1)S(1)}, u32[]{:S(2)}, u32[]{:S(2)}) collective-permute-start(bf16[128,768]{1,0:T(8,128)(2,1)S(1)} %pad_maximum_fusion.2), channel_id=1, source_target_pairs={{0,2},{1,3},{2,0},{3,1},{4,6},{5,7},{6,4},{7,5},{8,10},{9,11},{10,... | collective-permute-start | bytes 589832 | tf_op jit(solution)/shard_map/ppermute | solution.py:29
  140.9 15.8 %collective-permute-start.39 = (bf16[128,768]{1,0:T(8,128)(2,1)S(1)}, bf16[128,768]{1,0:T(8,128)(2,1)S(1)}, u32[]{:S(2)}, u32[]{:S(2)}) collective-permute-start(bf16[128,768]{1,0:T(8,128)(2,1)S(1)} %pad_maximum_fusion.2), channel_id=1, source_target_pairs={{0,3},{1,0},{2,1},{3,2},{4,7},{5,4},{6,5},{7,6},{8,11},{9,8},{10,9... | collective-permute-start | bytes 589832 | tf_op jit(solution)/shard_map/ppermute | solution.py:29
  (42 other events, 187.3 us)

commit v4 on v3

--- a/solution.py
+++ b/solution.py
@@ -6,7 +6,7 @@
 ROUNDS = 2
 DEGREE = 8
 ROTS = 4
-PAD_ROWS = 16
+GATHER_AT = 2
 
 
 filter_center = 0.1
@@ -29,6 +29,15 @@
         pieces.append(lax.ppermute(value, "bands", pairs))
     order = (here - jnp.arange(count, dtype=jnp.int32)) % count
     return jnp.take(jnp.stack(pieces), order, axis=0)
+
+
+def gather_pieces(value):
+    count = lax.axis_size("bands")
+    pieces = [value]
+    for shift in range(1, count):
+        pairs = [(source, (source + shift) % count) for source in range(count)]
+        pieces.append(lax.ppermute(value, "bands", pairs))
+    return jnp.stack(pieces)
 
 
 def atoms_sum(value):
@@ -62,15 +71,8 @@
     orb_dev = diag_block.shape[1]
     atoms_dev = pair_pattern.shape[2]
     atoms_here = lax.axis_index("atoms")
-    shipped = []
-    for round_index in range(ROUNDS):
-        pattern_rows = jnp.zeros((PAD_ROWS, orb_dev), jnp.bfloat16)
-        pattern_rows = lax.dynamic_update_slice(
-            pattern_rows, pair_pattern[round_index].astype(jnp.bfloat16), (0, 0)
-        )
-        packed = jnp.concatenate([pair_block[round_index], pattern_rows], axis=0)
-        shipped.append(swapped(packed, "atoms", round_index))
-    full_rot = gather_bands(rotations)
+    shipped = [swapped(pair_block[r], "atoms", r) for r in range(ROUNDS)]
+    shipped_pattern = [swapped(pair_pattern[r], "atoms", r) for r in range(ROUNDS)]
     own_atoms = atom_index(
         lax.dynamic_index_in_dim(atom_sizes, atoms_here, 0, keepdims=False), orb_dev
     )
@@ -88,11 +90,9 @@
         own_mask = pattern_mask(pair_pattern[round_index], own_atoms, other_atoms)
         own_pair = jnp.where(own_mask, pair_block[round_index], jnp.zeros((), jnp.bfloat16))
         own_pair_t.append(own_pair)
-        received = shipped[round_index]
-        other_pattern = received[orb_dev : orb_dev + atoms_dev, :atoms_dev]
-        other_mask = pattern_mask(other_pattern, other_atoms, own_atoms)
+        other_mask = pattern_mask(shipped_pattern[round_index], other_atoms, own_atoms)
         other_pair.append(
-            jnp.where(other_mask, received[:orb_dev], jnp.zeros((), jnp.bfloat16))
+            jnp.where(other_mask, shipped[round_index], jnp.zeros((), jnp.bfloat16))
         )
 
     def apply_operator(values):
@@ -108,30 +108,53 @@
             )
         return result
 
-    def chebyshev(start_rows):
+    def chebyshev(start_rows, hook):
         previous = start_rows.astype(jnp.float32)
         current = (apply_operator(start_rows) - filter_center * previous) / filter_half
         for degree_index in range(1, DEGREE):
+            if degree_index == GATHER_AT:
+                current = hook(current)
             applied = apply_operator(current.astype(jnp.bfloat16))
             following = 2.0 * (applied - filter_center * current) / filter_half - previous
             previous, current = (current, following)
         return current
 
+    gathered = []
+
+    def start_rotation_gather(current):
+        held, current = lax.optimization_barrier((rotations[: ROTS - 1], current))
+        gathered.append(gather_pieces(held))
+        return current
+
     half_bands = subspace.shape[0] // 2
     current = jnp.concatenate(
-        [chebyshev(subspace[:half_bands]), chebyshev(subspace[half_bands:])], axis=0
+        [
+            chebyshev(subspace[:half_bands], start_rotation_gather),
+            chebyshev(subspace[half_bands:], lambda rows: rows),
+        ],
+        axis=0,
     )
+    rot_pieces = gathered[0]
     total_orbitals = orb_dev * lax.axis_size("atoms")
-    rot_steps, all_bands, _ = rotations.shape
-    full_rot = jnp.transpose(full_rot, (1, 2, 0, 3)).reshape(rot_steps, all_bands, all_bands)
+    band_count = lax.axis_size("bands")
+    band_here = lax.axis_index("bands")
+    all_bands = rotations.shape[1]
     basis_all = gather_bands(current.astype(jnp.bfloat16)).reshape(all_bands, orb_dev)
     for rotation_index in range(ROTS - 1):
-        mixed_rows = lax.dot_general(
-            full_rot[rotation_index],
-            basis_all,
-            (((0,), (0,)), ((), ())),
-            preferred_element_type=jnp.float32,
-        )
+        groups = []
+        for group in range(band_count):
+            piece = lax.dynamic_index_in_dim(
+                rot_pieces, (band_here - group) % band_count, 0, keepdims=False
+            )
+            groups.append(
+                lax.dot_general(
+                    piece[rotation_index],
+                    basis_all,
+                    (((0,), (0,)), ((), ())),
+                    preferred_element_type=jnp.float32,
+                )
+            )
+        mixed_rows = jnp.concatenate(groups, axis=0)
         squares = atoms_sum(jnp.sum(mixed_rows * mixed_rows, axis=1))
         col_norm = jnp.sqrt(squares / total_orbitals + norm_eps)
         basis_all = (mixed_rows / col_norm[:, None]).astype(jnp.bfloat16)

time: 200 us -> 179 us (0.90)
  waiting for transfers between devices: 68.1 us -> 50.5 us
  other arithmetic: 17.7 us -> 8.44 us
  starting transfers between devices: 43.5 us -> 47.8 us
  matrix products: 55.6 us -> 57.9 us
    ppermute x46 -> x48, waiting for transfers between devices: 55.4 us -> 34.3 us  [swapped(): return lax.ppermute(value, axis, pairs)]
    ppermute x6 -> x3, starting transfers between devices: 9.39 us -> 4 us  [gather_bands(): pieces.append(lax.ppermute(value, 'bands', pairs))]
    ppermute x0 -> x3, starting transfers between devices: none -> 5.05 us  [gather_pieces(): pieces.append(lax.ppermute(value, 'bands', pairs))]
    ppermute x46 -> x48, starting transfers between devices: 34.1 us -> 38.7 us  [swapped(): return lax.ppermute(value, axis, pairs)]
    concatenate x3 -> x1, other arithmetic: 3.98 us -> 0.01 us  [body(): jnp.concatenate([chebyshev(subspace[:half_bands], start_rotation_gather),...]
    gather x2 -> x1, local copies, waits for them, and re-layouts: 4.36 us -> 0.6 us  [gather_bands(): return jnp.take(jnp.stack(pieces), order, axis=0)]
    ppermute x6 -> x3, waiting for transfers between devices: 12.7 us -> 16.2 us  [gather_bands(): pieces.append(lax.ppermute(value, 'bands', pairs))]
    select_n x3 -> x2, other arithmetic: 3.36 us -> 0.15 us  [gather_bands(): return jnp.take(jnp.stack(pieces), order, axis=0)]
  transfers between devices with their start and end apart: 52 -> 54, of which waited for: 27 -> 25; matrix products, arithmetic and copies ran while one was open for 36% -> 36% of each run, Pallas kernels for 0% -> 0%
where the time goes in v4:
time: 179 us; the launch traced here: 178 us
  matrix products  57.9 us (32%)
  waiting for transfers between devices  50.5 us (28%)
  starting transfers between devices  47.8 us (27%)
  local copies, waits for them, and re-layouts  12.5 us (7%)
  other arithmetic  8.44 us (5%)
    ppermute x48, starting transfers between devices, swapped(): return lax.ppermute(value, axis, pairs)  38.7 us
    ppermute x48, waiting for transfers between devices, swapped(): return lax.ppermute(value, axis, pairs)  34.3 us
    dot_general x32, matrix products, apply_operator(): lax.dot_general(other_rows, own_pair_t[round_index], (((1,), (1,)), ((),...  22.4 us
    ppermute x3, waiting for transfers between devices, gather_bands(): pieces.append(lax.ppermute(value, 'bands', pairs))  16.2 us
    dot_general x32, matrix products, apply_operator(): jnp.dot(other_rows, other_pair[round_index], preferred_element_type=jnp.f...  15.6 us
    dot_general x4, matrix products, pattern_mask(): lax.dot_general(per_row.astype(jnp.bfloat16), col_onehot, (((1,), (1,)),...  8.21 us
    dot_general x16, matrix products, apply_operator(): result = jnp.dot(values, diag_sym, preferred_element_type=jnp.float32)  6.61 us
    ppermute x3, starting transfers between devices, gather_pieces(): pieces.append(lax.ppermute(value, 'bands', pairs))  5.05 us
  transfers between devices with their start and end apart: 54, of which 25 were waited for; matrix products, arithmetic and copies ran while one was open for 36% of the time, Pallas kernels for 0%

profile of v4, /device:TPU:0, one launch (start us, length us, event | category | flops | bytes accessed | tf_op | source)
XLA Modules:
  0.0 178.0 jit_solution(15178791356393673944)
XLA Ops:
  2.1 2.5 %collective-permute-start.3 = (bf16[64,768]{1,0:T(8,128)(2,1)}, bf16[64,768]{1,0:T(8,128)(2,1)}, u32[]{:S(2)}, u32[]{:S(2)}) collective-permute-start(bf16[64,768]{1,0:T(8,128)(2,1)} %get-tuple-element.14), channel_id=1, source_target_pairs={{0,8},{4,12},{8,0},{12,4},{16,24},{20,28},{24,16},{28,20},{1,9},{5... | collective-permute-start | bytes 294920 | tf_op jit(solution)/shard_map/ppermute | solution.py:20
  5.1 3.2 %slice_bitcast_fusion.1 = (bf16[768,768]{1,0:T(8,128)(2,1)}, bf16[768,768]{1,0:T(8,128)(2,1)}) fusion(bf16[2,768,768]{2,1,0:T(8,128)(2,1)} %param.8), kind=kLoop, calls=%fused_computation.19 | loop fusion | bytes 4718592 | tf_op jit(solution)/shard_map/squeeze | solution.py:91
  8.3 1.7 collective-permute-start.5
  10.7 2.0 %add_multiply_fusion = f32[768,768]{1,0:T(8,128)} fusion(bf16[768,768]{1,0:T(8,128)(2,1)S(1)} %copy-done.4, s32[768]{0:T(1024)S(1)} %get-tuple-element.47), kind=kLoop, calls=%fused_computation.3 | loop fusion | flops 4128768 | bytes 3542016 | tf_op jit(solution)/shard_map/mul | solution.py:81
  12.8 2.0 %copy.9 = f32[768,768]{0,1:T(8,128)S(1)} copy(f32[768,768]{1,0:T(8,128)} %add_multiply_fusion) | data formatting | bytes 4718592 | tf_op jit(solution)/shard_map/mul | solution.py:81
  14.8 2.0 %fusion = bf16[768,768]{1,0:T(8,128)(2,1)S(1)} fusion(f32[768,768]{0,1:T(8,128)S(1)} %copy.9, s32[768]{0:T(1024)S(1)} %get-tuple-element.47, bf16[768,768]{1,0:T(8,128)(2,1)} %param.7), kind=kLoop, calls=%fused_computation.2 | loop fusion | flops 5308416 | bytes 4721664 | tf_op jit(solution)/shard_map/convert_element_type | solution.py:82
  19.8 1.9 %compare_select_fusion.1 = bf16[768,768]{1,0:T(8,128)(2,1)S(1)} fusion(s32[768]{0:T(1024)S(1)} %get-tuple-element.46, s32[768]{0:T(1024)S(1)} %get-tuple-element.47, s32[2,4,4]{2,1,0:T(4,128)S(1)} %copy-done.14, bf16[2,768,768]{2,1,0:T(8,128)(2,1)} %param.8), kind=kOutput, calls=%fused_computation.5 | convolution fusion | flops 5932048 | bytes 2369536 | tf_op jit(solution)/shard_map/dot_general | solution.py:63
  21.7 2.4 %compare_select_fusion.3 = bf16[768,768]{1,0:T(8,128)(2,1)S(1)} fusion(s32[768]{0:T(1024)S(1)} %convert_reduce_fusion.1, s32[768]{0:T(1024)S(1)} %get-tuple-element.47, s32[2,4,4]{2,1,0:T(4,128)S(1)} %copy-done.14, bf16[2,768,768]{2,1,0:T(8,128)(2,1)} %param.8), kind=kOutput, calls=%fused_computation.7 | convolution fusion | flops 5932048 | bytes 2369536 | tf_op jit(solution)/shard_map/dot_general | solution.py:63
  24.1 1.8 %slice.76 = bf16[3,512,128]{2,1,0:T(8,128)(2,1)} slice(bf16[4,512,128]{2,1,0:T(8,128)(2,1)} %param.11), slice={[0:3], [0:512], [0:128]} | slice | bytes 786432 | tf_op jit(solution)/shard_map/slice | solution.py:125
  26.0 2.2 %convolution_add_fusion.31 = f32[768,64]{0,1:T(8,128)} fusion(f32[768,64]{0,1:T(8,128)} %fusion.137, bf16[768,768]{1,0:T(8,128)(2,1)S(1)} %compare_select_fusion.3, bf16[64,768]{1,0:T(8,128)(2,1)} %collective-permute-done), kind=kOutput, calls=%fused_computation.133 | convolution fusion | flops 75546624 | bytes 1671168 | tf_op jit(solution)/shard_map/dot_general | solution.py:102
  28.7 2.1 %convolution_add_fusion.16 = f32[768,64]{0,1:T(8,128)} fusion(f32[768,64]{0,1:T(8,128)S(1)} %copy-done.12, bf16[768,768]{1,0:T(8,128)(2,1)S(1)} %compare_select_fusion.3, bf16[64,768]{1,0:T(8,128)(2,1)} %collective-permute-done.23), kind=kOutput, calls=%fused_computation.83 | convolution fusion | flops 75546624 | bytes 1671168 | tf_op jit(solution)/shard_map/dot_general | solution.py:102
  31.0 2.1 %fusion.173 = f32[768,64]{0,1:T(8,128)} fusion(bf16[768,768]{1,0:T(8,128)(2,1)S(1)} %compare_select_fusion.1, bf16[64,768]{1,0:T(8,128)(2,1)} %collective-permute-done.24), kind=kOutput, calls=%fused_computation.269 | convolution fusion | flops 75497472 | bytes 1474560 | tf_op jit(solution)/shard_map/dot_general | solution.py:102
  33.1 2.1 %fusion.151 = f32[768,64]{0,1:T(8,128)} fusion(bf16[768,768]{1,0:T(8,128)(2,1)S(1)} %compare_select_fusion.1, bf16[64,768]{1,0:T(8,128)(2,1)} %collective-permute-done.3), kind=kOutput, calls=%fused_computation.247 | convolution fusion | flops 75497472 | bytes 1474560 | tf_op jit(solution)/shard_map/dot_general | solution.py:102
  37.2 1.9 %compare_select_fusion = bf16[768,768]{1,0:T(8,128)(2,1)S(1)} fusion(bf16[768,768]{1,0:T(8,128)(2,1)} %collective-permute-done.5, s32[768]{0:T(1024)S(1)} %get-tuple-element.46, s32[768]{0:T(1024)S(1)} %get-tuple-element.47, s32[4,4]{1,0:T(4,128)} %copy-done.16), kind=kOutput, calls=%fused_computation.4 | convolution fusion | flops 5932048 | bytes 2365504 | tf_op jit(solution)/shard_map/dot_general | solution.py:63
  39.2 2.0 %fusion.196 = f32[768,64]{0,1:T(8,128)} fusion(bf16[64,768]{1,0:T(8,128)(2,1)} %collective-permute-done.24, bf16[768,768]{1,0:T(8,128)(2,1)S(1)} %compare_select_fusion), kind=kOutput, calls=%fused_computation.292 | convolution fusion | flops 75497472 | bytes 1474560 | tf_op jit(solution)/shard_map/dot_general | solution.py:106
  41.2 1.9 %compare_select_fusion.2 = bf16[768,768]{1,0:T(8,128)(2,1)S(1)} fusion(bf16[768,768]{1,0:T(8,128)(2,1)} %collective-permute-done.2, s32[768]{0:T(1024)S(1)} %convert_reduce_fusion.1, s32[768]{0:T(1024)S(1)} %get-tuple-element.47, s32[4,4]{1,0:T(4,128)} %collective-permute-done.1), kind=kOutput, calls=%fused_computation.6 | convolution fusion | flops 5932048 | bytes 2365504 | tf_op jit(solution)/shard_map/dot_general | solution.py:63
  43.2 1.7 multiply_convert_fusion
  44.8 1.7 collective-permute-start.26
  52.7 1.7 collective-permute-start.28
  57.5 3.8 %collective-permute-start.10 = (bf16[3,512,128]{2,1,0:T(8,128)(2,1)}, bf16[3,512,128]{2,1,0:T(8,128)(2,1)}, u32[]{:S(2)}, u32[]{:S(2)}) collective-permute-start(bf16[3,512,128]{2,1,0:T(8,128)(2,1)} %slice.76), channel_id=1, source_target_pairs={{0,3},{1,0},{2,1},{3,2},{4,7},{5,4},{6,5},{7,6},{8,11},{9,8},{10,9... | collective-permute-start | bytes 1179656 | tf_op jit(solution)/shard_map/ppermute | solution.py:39
  108.5 2.3 %collective-permute-done.22 = bf16[64,768]{1,0:T(8,128)(2,1)S(1)} collective-permute-done((bf16[64,768]{1,0:T(8,128)(2,1)S(1)}, bf16[64,768]{1,0:T(8,128)(2,1)S(1)}, u32[]{:S(2)}, u32[]{:S(2)}) %collective-permute-start.22) | collective-permute-done | bytes 98336 | tf_op jit(solution)/shard_map/ppermute | solution.py:20
  113.9 2.9 %collective-permute-start.41 = (bf16[128,768]{1,0:T(8,128)(2,1)S(1)}, bf16[128,768]{1,0:T(8,128)(2,1)S(1)}, u32[]{:S(2)}, u32[]{:S(2)}) collective-permute-start(bf16[128,768]{1,0:T(8,128)(2,1)S(1)} %pad_maximum_fusion.5), channel_id=1, source_target_pairs={{0,3},{1,0},{2,1},{3,2},{4,7},{5,4},{6,5},{7,6},{8,11},{9,8},{10,9... | collective-permute-start | bytes 589832 | tf_op jit(solution)/shard_map/ppermute | solution.py:29
  119.6 2.4 %collective-permute-done.41 = bf16[128,768]{1,0:T(8,128)(2,1)S(1)} collective-permute-done((bf16[128,768]{1,0:T(8,128)(2,1)S(1)}, bf16[128,768]{1,0:T(8,128)(2,1)S(1)}, u32[]{:S(2)}, u32[]{:S(2)}) %collective-permute-start.41) | collective-permute-done | bytes 196640 | tf_op jit(solution)/shard_map/ppermute | solution.py:29
  122.1 13.7 %collective-permute-done.40 = bf16[128,768]{1,0:T(8,128)(2,1)S(1)} collective-permute-done((bf16[128,768]{1,0:T(8,128)(2,1)S(1)}, bf16[128,768]{1,0:T(8,128)(2,1)S(1)}, u32[]{:S(2)}, u32[]{:S(2)}) %collective-permute-start.40) | collective-permute-done | bytes 196640 | tf_op jit(solution)/shard_map/ppermute | solution.py:29
  141.6 2.1 %collective-permute-done.43 = f32[512]{0:T(512)S(1)} collective-permute-done((f32[512]{0:T(512)S(1)}, f32[512]{0:T(512)S(1)}, u32[]{:S(2)}, u32[]{:S(2)}) %collective-permute-start.43) | collective-permute-done | bytes 2080 | tf_op jit(solution)/shard_map/ppermute | solution.py:20
  145.2 2.1 %collective-permute-done.44 = f32[512]{0:T(512)S(1)} collective-permute-done((f32[512]{0:T(512)S(1)}, f32[512]{0:T(512)S(1)}, u32[]{:S(2)}, u32[]{:S(2)}) %collective-permute-start.44) | collective-permute-done | bytes 2080 | tf_op jit(solution)/shard_map/ppermute | solution.py:20
  151.6 2.1 %collective-permute-done.46 = f32[512]{0:T(512)S(1)} collective-permute-done((f32[512]{0:T(512)S(1)}, f32[512]{0:T(512)S(1)}, u32[]{:S(2)}, u32[]{:S(2)}) %collective-permute-start.46) | collective-permute-done | bytes 2080 | tf_op jit(solution)/shard_map/ppermute | solution.py:20
  155.2 2.1 %collective-permute-done.47 = f32[512]{0:T(512)S(1)} collective-permute-done((f32[512]{0:T(512)S(1)}, f32[512]{0:T(512)S(1)}, u32[]{:S(2)}, u32[]{:S(2)}) %collective-permute-start.47) | collective-permute-done | bytes 2080 | tf_op jit(solution)/shard_map/ppermute | solution.py:20
  161.6 2.1 %collective-permute-done.49 = f32[512]{0:T(512)S(1)} collective-permute-done((f32[512]{0:T(512)S(1)}, f32[512]{0:T(512)S(1)}, u32[]{:S(2)}, u32[]{:S(2)}) %collective-permute-start.49) | collective-permute-done | bytes 2080 | tf_op jit(solution)/shard_map/ppermute | solution.py:20
  165.2 2.1 %collective-permute-done.50 = f32[512]{0:T(512)S(1)} collective-permute-done((f32[512]{0:T(512)S(1)}, f32[512]{0:T(512)S(1)}, u32[]{:S(2)}, u32[]{:S(2)}) %collective-permute-start.50) | collective-permute-done | bytes 2080 | tf_op jit(solution)/shard_map/ppermute | solution.py:20
  171.4 2.1 %collective-permute-done.52 = f32[128]{0:T(128)S(1)} collective-permute-done((f32[128]{0:T(128)S(1)}, f32[128]{0:T(128)S(1)}, u32[]{:S(2)}, u32[]{:S(2)}) %collective-permute-start.52) | collective-permute-done | bytes 544 | tf_op jit(solution)/shard_map/ppermute | solution.py:20
  175.0 2.0 %collective-permute-done.53 = f32[128]{0:T(128)S(1)} collective-permute-done((f32[128]{0:T(128)S(1)}, f32[128]{0:T(128)S(1)}, u32[]{:S(2)}, u32[]{:S(2)}) %collective-permute-start.53) | collective-permute-done | bytes 544 | tf_op jit(solution)/shard_map/ppermute | solution.py:20
  (248 shorter events, 96.3 us)
Async XLA Ops:
  1.6 24.3 %collective-permute-start = (bf16[64,768]{1,0:T(8,128)(2,1)}, bf16[64,768]{1,0:T(8,128)(2,1)}, u32[]{:S(2)}, u32[]{:S(2)}) collective-permute-start(bf16[64,768]{1,0:T(8,128)(2,1)} %get-tuple-element.14), channel_id=1, source_target_pairs={{0,4},{4,0},{8,12},{12,8},{16,20},{20,16},{24,28},{28,24},{1,5},{5... | collective-permute-start | bytes 294920 | tf_op jit(solution)/shard_map/ppermute | solution.py:20
  2.1 31.0 %collective-permute-start.3 = (bf16[64,768]{1,0:T(8,128)(2,1)}, bf16[64,768]{1,0:T(8,128)(2,1)}, u32[]{:S(2)}, u32[]{:S(2)}) collective-permute-start(bf16[64,768]{1,0:T(8,128)(2,1)} %get-tuple-element.14), channel_id=1, source_target_pairs={{0,8},{4,12},{8,0},{12,4},{16,24},{20,28},{24,16},{28,20},{1,9},{5... | collective-permute-start | bytes 294920 | tf_op jit(solution)/shard_map/ppermute | solution.py:20
  4.6 23.6 %collective-permute-start.23 = (bf16[64,768]{1,0:T(8,128)(2,1)}, bf16[64,768]{1,0:T(8,128)(2,1)}, u32[]{:S(2)}, u32[]{:S(2)}) collective-permute-start(bf16[64,768]{1,0:T(8,128)(2,1)} %get-tuple-element.15), channel_id=1, source_target_pairs={{0,4},{4,0},{8,12},{12,8},{16,20},{20,16},{24,28},{28,24},{1,5},{5... | collective-permute-start | bytes 294920 | tf_op jit(solution)/shard_map/ppermute | solution.py:20
  4.8 25.9 %collective-permute-start.24 = (bf16[64,768]{1,0:T(8,128)(2,1)}, bf16[64,768]{1,0:T(8,128)(2,1)}, u32[]{:S(2)}, u32[]{:S(2)}) collective-permute-start(bf16[64,768]{1,0:T(8,128)(2,1)} %get-tuple-element.15), channel_id=1, source_target_pairs={{0,8},{4,12},{8,0},{12,4},{16,24},{20,28},{24,16},{28,20},{1,9},{5... | collective-permute-start | bytes 294920 | tf_op jit(solution)/shard_map/ppermute | solution.py:20
  8.3 28.9 %collective-permute-start.5 = (bf16[768,768]{1,0:T(8,128)(2,1)}, bf16[768,768]{1,0:T(8,128)(2,1)}, u32[]{:S(2)}, u32[]{:S(2)}) collective-permute-start(bf16[768,768]{1,0:T(8,128)(2,1)} %get-tuple-element.13), channel_id=1, source_target_pairs={{0,8},{4,12},{8,0},{12,4},{16,24},{20,28},{24,16},{28,20},{1,9},{5... | collective-permute-start | bytes 3538952 | tf_op jit(solution)/shard_map/ppermute | solution.py:20
  25.9 15.2 %collective-permute-start.1 = (s32[4,4]{1,0:T(4,128)}, s32[4,4]{1,0:T(4,128)}, u32[]{:S(2)}, u32[]{:S(2)}) collective-permute-start(s32[4,4]{1,0:T(4,128)} %get-tuple-element.16), channel_id=1, source_target_pairs={{0,4},{4,0},{8,12},{12,8},{16,20},{20,16},{24,28},{28,24},{1,5},{5... | collective-permute-start | bytes 200 | tf_op jit(solution)/shard_map/ppermute | solution.py:20
  28.2 13.0 %collective-permute-start.2 = (bf16[768,768]{1,0:T(8,128)(2,1)}, bf16[768,768]{1,0:T(8,128)(2,1)}, u32[]{:S(2)}, u32[]{:S(2)}) collective-permute-start(bf16[768,768]{1,0:T(8,128)(2,1)} %get-tuple-element.12), channel_id=1, source_target_pairs={{0,4},{4,0},{8,12},{12,8},{16,20},{20,16},{24,28},{28,24},{1,5},{5... | collective-permute-start | bytes 3538952 | tf_op jit(solution)/shard_map/ppermute | solution.py:20
  30.8 5.9 %collective-permute-start.4 = (s32[4,4]{1,0:T(4,128)S(1)}, s32[4,4]{1,0:T(4,128)S(1)}, u32[]{:S(2)}, u32[]{:S(2)}) collective-permute-start(s32[4,4]{1,0:T(4,128)S(1)} %copy-done.15), channel_id=1, source_target_pairs={{0,8},{4,12},{8,0},{12,4},{16,24},{20,28},{24,16},{28,20},{1,9},{5... | collective-permute-start | bytes 200 | tf_op jit(solution)/shard_map/ppermute | solution.py:20
  44.8 5.6 %collective-permute-start.26 = (bf16[64,768]{1,0:T(8,128)(2,1)S(1)}, bf16[64,768]{1,0:T(8,128)(2,1)S(1)}, u32[]{:S(2)}, u32[]{:S(2)}) collective-permute-start(bf16[64,768]{1,0:T(8,128)(2,1)S(1)} %get-tuple-element.18), channel_id=1, source_target_pairs={{0,8},{4,12},{8,0},{12,4},{16,24},{20,28},{24,16},{28,20},{1,9},{5... | collective-permute-start | bytes 294920 | tf_op jit(solution)/shard_map/ppermute | solution.py:20
  46.6 5.3 %collective-permute-start.25 = (bf16[64,768]{1,0:T(8,128)(2,1)S(1)}, bf16[64,768]{1,0:T(8,128)(2,1)S(1)}, u32[]{:S(2)}, u32[]{:S(2)}) collective-permute-start(bf16[64,768]{1,0:T(8,128)(2,1)S(1)} %get-tuple-element.18), channel_id=1, source_target_pairs={{0,4},{4,0},{8,12},{12,8},{16,20},{20,16},{24,28},{28,24},{1,5},{5... | collective-permute-start | bytes 294920 | tf_op jit(solution)/shard_map/ppermute | solution.py:20
  49.1 5.7 %collective-permute-start.7 = (bf16[64,768]{1,0:T(8,128)(2,1)S(1)}, bf16[64,768]{1,0:T(8,128)(2,1)S(1)}, u32[]{:S(2)}, u32[]{:S(2)}) collective-permute-start(bf16[64,768]{1,0:T(8,128)(2,1)S(1)} %get-tuple-element.32), channel_id=1, source_target_pairs={{0,8},{4,12},{8,0},{12,4},{16,24},{20,28},{24,16},{28,20},{1,9},{5... | collective-permute-start | bytes 294920 | tf_op jit(solution)/shard_map/ppermute | solution.py:20
  49.5 6.1 %collective-permute-start.6 = (bf16[64,768]{1,0:T(8,128)(2,1)S(1)}, bf16[64,768]{1,0:T(8,128)(2,1)S(1)}, u32[]{:S(2)}, u32[]{:S(2)}) collective-permute-start(bf16[64,768]{1,0:T(8,128)(2,1)S(1)} %get-tuple-element.32), channel_id=1, source_target_pairs={{0,4},{4,0},{8,12},{12,8},{16,20},{20,16},{24,28},{28,24},{1,5},{5... | collective-permute-start | bytes 294920 | tf_op jit(solution)/shard_map/ppermute | solution.py:20
  52.7 8.6 %collective-permute-start.28 = (bf16[64,768]{1,0:T(8,128)(2,1)S(1)}, bf16[64,768]{1,0:T(8,128)(2,1)S(1)}, u32[]{:S(2)}, u32[]{:S(2)}) collective-permute-start(bf16[64,768]{1,0:T(8,128)(2,1)S(1)} %get-tuple-element.20), channel_id=1, source_target_pairs={{0,8},{4,12},{8,0},{12,4},{16,24},{20,28},{24,16},{28,20},{1,9},{5... | collective-permute-start | bytes 294920 | tf_op jit(solution)/shard_map/ppermute | solution.py:20
  54.4 7.7 %collective-permute-start.27 = (bf16[64,768]{1,0:T(8,128)(2,1)S(1)}, bf16[64,768]{1,0:T(8,128)(2,1)S(1)}, u32[]{:S(2)}, u32[]{:S(2)}) collective-permute-start(bf16[64,768]{1,0:T(8,128)(2,1)S(1)} %get-tuple-element.20), channel_id=1, source_target_pairs={{0,4},{4,0},{8,12},{12,8},{16,20},{20,16},{24,28},{28,24},{1,5},{5... | collective-permute-start | bytes 294920 | tf_op jit(solution)/shard_map/ppermute | solution.py:20
  56.5 8.1 %collective-permute-start.12 = (bf16[64,768]{1,0:T(8,128)(2,1)S(1)}, bf16[64,768]{1,0:T(8,128)(2,1)S(1)}, u32[]{:S(2)}, u32[]{:S(2)}) collective-permute-start(bf16[64,768]{1,0:T(8,128)(2,1)S(1)} %convert_element_type.132), channel_id=1, source_target_pairs={{0,8},{4,12},{8,0},{12,4},{16,24},{20,28},{24,16},{28,20},{1,9},{5... | collective-permute-start | bytes 294920 | tf_op jit(solution)/shard_map/ppermute | solution.py:20
  56.9 10.0 %collective-permute-start.11 = (bf16[64,768]{1,0:T(8,128)(2,1)S(1)}, bf16[64,768]{1,0:T(8,128)(2,1)S(1)}, u32[]{:S(2)}, u32[]{:S(2)}) collective-permute-start(bf16[64,768]{1,0:T(8,128)(2,1)S(1)} %convert_element_type.132), channel_id=1, source_target_pairs={{0,4},{4,0},{8,12},{12,8},{16,20},{20,16},{24,28},{28,24},{1,5},{5... | collective-permute-start | bytes 294920 | tf_op jit(solution)/shard_map/ppermute | solution.py:20
  57.5 60.4 %collective-permute-start.10 = (bf16[3,512,128]{2,1,0:T(8,128)(2,1)}, bf16[3,512,128]{2,1,0:T(8,128)(2,1)}, u32[]{:S(2)}, u32[]{:S(2)}) collective-permute-start(bf16[3,512,128]{2,1,0:T(8,128)(2,1)} %slice.76), channel_id=1, source_target_pairs={{0,3},{1,0},{2,1},{3,2},{4,7},{5,4},{6,5},{7,6},{8,11},{9,8},{10,9... | collective-permute-start | bytes 1179656 | tf_op jit(solution)/shard_map/ppermute | solution.py:39
  61.3 56.7 %collective-permute-start.9 = (bf16[3,512,128]{2,1,0:T(8,128)(2,1)}, bf16[3,512,128]{2,1,0:T(8,128)(2,1)}, u32[]{:S(2)}, u32[]{:S(2)}) collective-permute-start(bf16[3,512,128]{2,1,0:T(8,128)(2,1)} %slice.76), channel_id=1, source_target_pairs={{0,2},{1,3},{2,0},{3,1},{4,6},{5,7},{6,4},{7,5},{8,10},{9,11},{10,... | collective-permute-start | bytes 1179656 | tf_op jit(solution)/shard_map/ppermute | solution.py:39
  62.1 55.9 %collective-permute-start.8 = (bf16[3,512,128]{2,1,0:T(8,128)(2,1)}, bf16[3,512,128]{2,1,0:T(8,128)(2,1)}, u32[]{:S(2)}, u32[]{:S(2)}) collective-permute-start(bf16[3,512,128]{2,1,0:T(8,128)(2,1)} %slice.76), channel_id=1, source_target_pairs={{0,1},{1,2},{2,3},{3,0},{4,5},{5,6},{6,7},{7,4},{8,9},{9,10},{10,1... | collective-permute-start | bytes 1179656 | tf_op jit(solution)/shard_map/ppermute | solution.py:39
  64.6 4.7 %collective-permute-start.30 = (bf16[64,768]{1,0:T(8,128)(2,1)S(1)}, bf16[64,768]{1,0:T(8,128)(2,1)S(1)}, u32[]{:S(2)}, u32[]{:S(2)}) collective-permute-start(bf16[64,768]{1,0:T(8,128)(2,1)S(1)} %get-tuple-element.22), channel_id=1, source_target_pairs={{0,8},{4,12},{8,0},{12,4},{16,24},{20,28},{24,16},{28,20},{1,9},{5... | collective-permute-start | bytes 294920 | tf_op jit(solution)/shard_map/ppermute | solution.py:20
  69.3 4.6 %collective-permute-start.14 = (bf16[64,768]{1,0:T(8,128)(2,1)S(1)}, bf16[64,768]{1,0:T(8,128)(2,1)S(1)}, u32[]{:S(2)}, u32[]{:S(2)}) collective-permute-start(bf16[64,768]{1,0:T(8,128)(2,1)S(1)} %get-tuple-element.34), channel_id=1, source_target_pairs={{0,8},{4,12},{8,0},{12,4},{16,24},{20,28},{24,16},{28,20},{1,9},{5... | collective-permute-start | bytes 294920 | tf_op jit(solution)/shard_map/ppermute | solution.py:20
  73.9 4.6 %collective-permute-start.32 = (bf16[64,768]{1,0:T(8,128)(2,1)S(1)}, bf16[64,768]{1,0:T(8,128)(2,1)S(1)}, u32[]{:S(2)}, u32[]{:S(2)}) collective-permute-start(bf16[64,768]{1,0:T(8,128)(2,1)S(1)} %get-tuple-element.24), channel_id=1, source_target_pairs={{0,8},{4,12},{8,0},{12,4},{16,24},{20,28},{24,16},{28,20},{1,9},{5... | collective-permute-start | bytes 294920 | tf_op jit(solution)/shard_map/ppermute | solution.py:20
  78.5 4.6 %collective-permute-start.16 = (bf16[64,768]{1,0:T(8,128)(2,1)S(1)}, bf16[64,768]{1,0:T(8,128)(2,1)S(1)}, u32[]{:S(2)}, u32[]{:S(2)}) collective-permute-start(bf16[64,768]{1,0:T(8,128)(2,1)S(1)} %get-tuple-element.36), channel_id=1, source_target_pairs={{0,8},{4,12},{8,0},{12,4},{16,24},{20,28},{24,16},{28,20},{1,9},{5... | collective-permute-start | bytes 294920 | tf_op jit(solution)/shard_map/ppermute | solution.py:20
  83.1 4.6 %collective-permute-start.34 = (bf16[64,768]{1,0:T(8,128)(2,1)S(1)}, bf16[64,768]{1,0:T(8,128)(2,1)S(1)}, u32[]{:S(2)}, u32[]{:S(2)}) collective-permute-start(bf16[64,768]{1,0:T(8,128)(2,1)S(1)} %get-tuple-element.26), channel_id=1, source_target_pairs={{0,8},{4,12},{8,0},{12,4},{16,24},{20,28},{24,16},{28,20},{1,9},{5... | collective-permute-start | bytes 294920 | tf_op jit(solution)/shard_map/ppermute | solution.py:20
  87.7 4.6 %collective-permute-start.18 = (bf16[64,768]{1,0:T(8,128)(2,1)S(1)}, bf16[64,768]{1,0:T(8,128)(2,1)S(1)}, u32[]{:S(2)}, u32[]{:S(2)}) collective-permute-start(bf16[64,768]{1,0:T(8,128)(2,1)S(1)} %get-tuple-element.38), channel_id=1, source_target_pairs={{0,8},{4,12},{8,0},{12,4},{16,24},{20,28},{24,16},{28,20},{1,9},{5... | collective-permute-start | bytes 294920 | tf_op jit(solution)/shard_map/ppermute | solution.py:20
  92.4 4.6 %collective-permute-start.36 = (bf16[64,768]{1,0:T(8,128)(2,1)S(1)}, bf16[64,768]{1,0:T(8,128)(2,1)S(1)}, u32[]{:S(2)}, u32[]{:S(2)}) collective-permute-start(bf16[64,768]{1,0:T(8,128)(2,1)S(1)} %get-tuple-element.28), channel_id=1, source_target_pairs={{0,8},{4,12},{8,0},{12,4},{16,24},{20,28},{24,16},{28,20},{1,9},{5... | collective-permute-start | bytes 294920 | tf_op jit(solution)/shard_map/ppermute | solution.py:20
  97.0 4.6 %collective-permute-start.20 = (bf16[64,768]{1,0:T(8,128)(2,1)S(1)}, bf16[64,768]{1,0:T(8,128)(2,1)S(1)}, u32[]{:S(2)}, u32[]{:S(2)}) collective-permute-start(bf16[64,768]{1,0:T(8,128)(2,1)S(1)} %get-tuple-element.40), channel_id=1, source_target_pairs={{0,8},{4,12},{8,0},{12,4},{16,24},{20,28},{24,16},{28,20},{1,9},{5... | collective-permute-start | bytes 294920 | tf_op jit(solution)/shard_map/ppermute | solution.py:20
  101.6 4.6 %collective-permute-start.38 = (bf16[64,768]{1,0:T(8,128)(2,1)S(1)}, bf16[64,768]{1,0:T(8,128)(2,1)S(1)}, u32[]{:S(2)}, u32[]{:S(2)}) collective-permute-start(bf16[64,768]{1,0:T(8,128)(2,1)S(1)} %get-tuple-element.30), channel_id=1, source_target_pairs={{0,8},{4,12},{8,0},{12,4},{16,24},{20,28},{24,16},{28,20},{1,9},{5... | collective-permute-start | bytes 294920 | tf_op jit(solution)/shard_map/ppermute | solution.py:20
  103.9 7.2 %collective-permute-start.37 = (bf16[64,768]{1,0:T(8,128)(2,1)S(1)}, bf16[64,768]{1,0:T(8,128)(2,1)S(1)}, u32[]{:S(2)}, u32[]{:S(2)}) collective-permute-start(bf16[64,768]{1,0:T(8,128)(2,1)S(1)} %get-tuple-element.30), channel_id=1, source_target_pairs={{0,4},{4,0},{8,12},{12,8},{16,20},{20,16},{24,28},{28,24},{1,5},{5... | collective-permute-start | bytes 294920 | tf_op jit(solution)/shard_map/ppermute | solution.py:20
  113.9 8.2 %collective-permute-start.41 = (bf16[128,768]{1,0:T(8,128)(2,1)S(1)}, bf16[128,768]{1,0:T(8,128)(2,1)S(1)}, u32[]{:S(2)}, u32[]{:S(2)}) collective-permute-start(bf16[128,768]{1,0:T(8,128)(2,1)S(1)} %pad_maximum_fusion.5), channel_id=1, source_target_pairs={{0,3},{1,0},{2,1},{3,2},{4,7},{5,4},{6,5},{7,6},{8,11},{9,8},{10,9... | collective-permute-start | bytes 589832 | tf_op jit(solution)/shard_map/ppermute | solution.py:29
  116.8 19.0 %collective-permute-start.40 = (bf16[128,768]{1,0:T(8,128)(2,1)S(1)}, bf16[128,768]{1,0:T(8,128)(2,1)S(1)}, u32[]{:S(2)}, u32[]{:S(2)}) collective-permute-start(bf16[128,768]{1,0:T(8,128)(2,1)S(1)} %pad_maximum_fusion.5), channel_id=1, source_target_pairs={{0,2},{1,3},{2,0},{3,1},{4,6},{5,7},{6,4},{7,5},{8,10},{9,11},{10,... | collective-permute-start | bytes 589832 | tf_op jit(solution)/shard_map/ppermute | solution.py:29
  117.9 17.9 %collective-permute-start.39 = (bf16[128,768]{1,0:T(8,128)(2,1)S(1)}, bf16[128,768]{1,0:T(8,128)(2,1)S(1)}, u32[]{:S(2)}, u32[]{:S(2)}) collective-permute-start(bf16[128,768]{1,0:T(8,128)(2,1)S(1)} %pad_maximum_fusion.5), channel_id=1, source_target_pairs={{0,1},{1,2},{2,3},{3,0},{4,5},{5,6},{6,7},{7,4},{8,9},{9,10},{10,1... | collective-permute-start | bytes 589832 | tf_op jit(solution)/shard_map/ppermute | solution.py:29
  (39 other events, 151.5 us)

commit v5 on v4

--- a/solution.py
+++ b/solution.py
@@ -6,7 +6,7 @@
 ROUNDS = 2
 DEGREE = 8
 ROTS = 4
-GATHER_AT = 2
+GATHER_AT = 1
 
 
 filter_center = 0.1
@@ -58,12 +58,10 @@
 def pattern_mask(pattern, row_atoms, col_atoms):
     levels = jnp.arange(pattern.shape[0], dtype=jnp.int32)
     row_onehot = (row_atoms[:, None] == levels[None, :]).astype(jnp.bfloat16)
-    col_onehot = (col_atoms[:, None] == levels[None, :]).astype(jnp.bfloat16)
     per_row = jnp.dot(row_onehot, pattern.astype(jnp.bfloat16), preferred_element_type=jnp.float32)
-    mask = lax.dot_general(
-        per_row.astype(jnp.bfloat16), col_onehot, (((1,), (1,)), ((), ())),
-        preferred_element_type=jnp.float32,
-    )
+    mask = jnp.broadcast_to(per_row[:, :1], (row_atoms.shape[0], col_atoms.shape[0]))
+    for atom in range(1, pattern.shape[1]):
+        mask = jnp.where((col_atoms == atom)[None, :], per_row[:, atom : atom + 1], mask)
     return mask > 0.5
 
 
@@ -76,10 +74,13 @@
     own_atoms = atom_index(
         lax.dynamic_index_in_dim(atom_sizes, atoms_here, 0, keepdims=False), orb_dev
     )
-    upper_flag = (own_atoms[:, None] < own_atoms[None, :]).astype(jnp.float32)
-    same_atom = (own_atoms[:, None] == own_atoms[None, :]).astype(jnp.float32)
-    upper_part = diag_block.astype(jnp.float32) * (upper_flag + 0.5 * same_atom)
-    diag_sym = (upper_part + upper_part.T).astype(jnp.bfloat16)
+    row_atom = own_atoms[:, None]
+    col_atom = own_atoms[None, :]
+    weight = (row_atom < col_atom).astype(jnp.float32) + 0.5 * (row_atom == col_atom).astype(jnp.float32)
+    weight_t = (col_atom < row_atom).astype(jnp.float32) + 0.5 * (row_atom == col_atom).astype(jnp.float32)
+    diag_sym = (
+        diag_block.astype(jnp.float32) * weight + diag_block.T.astype(jnp.float32) * weight_t
+    ).astype(jnp.bfloat16)
     own_pair_t = []
     other_pair = []
     for round_index in range(ROUNDS):

time: 179 us -> 218 us (1.22)
  waiting for transfers between devices: 50.5 us -> 92.1 us
  matrix products: 57.9 us -> 46.1 us
  other arithmetic: 8.44 us -> 16.2 us
    ppermute x48, waiting for transfers between devices: 34.3 us -> 79.5 us  [swapped(): return lax.ppermute(value, axis, pairs)]
    select_n x0 -> x2, other arithmetic: none -> 6.45 us  [the longest x1 3.81 us: body(): jnp.where(other_mask, shipped[round_index], jnp.zeros((), jnp.bfloat16))]
    dot_general x32, matrix products: 22.4 us -> 17.8 us  [apply_operator(): lax.dot_general(other_rows, own_pair_t[round_index], (((1,), (1,)), ((),...]
    dot_general x4, matrix products: 8.21 us -> 3.75 us  [pattern_mask(): jnp.dot(row_onehot, pattern.astype(jnp.bfloat16), preferred_element_type=...]
    ppermute x3, waiting for transfers between devices: 16.2 us -> 12.6 us  [gather_bands(): pieces.append(lax.ppermute(value, 'bands', pairs))]
    dot_general x32, matrix products: 15.6 us -> 12.9 us  [apply_operator(): jnp.dot(other_rows, other_pair[round_index], preferred_element_type=jnp.f...]
  transfers between devices with their start and end apart: 54 -> 54, of which waited for: 25 -> 29; matrix products, arithmetic and copies ran while one was open for 36% -> 26% of each run, Pallas kernels for 0% -> 0%
where the time goes in v5:
time: 218 us; the launch traced here: 216 us
  waiting for transfers between devices  92.1 us (42%)
  starting transfers between devices  49.6 us (23%)
  matrix products  46.1 us (21%)
  other arithmetic  16.2 us (7%)
  local copies, waits for them, and re-layouts  11.2 us (5%)
    ppermute x48, waiting for transfers between devices, swapped(): return lax.ppermute(value, axis, pairs)  79.5 us
    ppermute x48, starting transfers between devices, swapped(): return lax.ppermute(value, axis, pairs)  40 us
    dot_general x32, matrix products, apply_operator(): lax.dot_general(other_rows, own_pair_t[round_index], (((1,), (1,)), ((),...  17.8 us
    dot_general x32, matrix products, apply_operator(): jnp.dot(other_rows, other_pair[round_index], preferred_element_type=jnp.f...  12.9 us
    ppermute x3, waiting for transfers between devices, gather_bands(): pieces.append(lax.ppermute(value, 'bands', pairs))  12.6 us
    dot_general x16, matrix products, apply_operator(): result = jnp.dot(values, diag_sym, preferred_element_type=jnp.float32)  6.6 us
    ppermute x3, starting transfers between devices, gather_pieces(): pieces.append(lax.ppermute(value, 'bands', pairs))  5.72 us
  transfers between devices with their start and end apart: 54, of which 29 were waited for; matrix products, arithmetic and copies ran while one was open for 26% of the time, Pallas kernels for 0%

profile of v5, /device:TPU:0, one launch (start us, length us, event | category | flops | bytes accessed | tf_op | source)
XLA Modules:
  0.0 216.1 jit_solution(1659199908061244907)
XLA Ops:
  2.1 2.5 %collective-permute-start.3 = (bf16[64,768]{1,0:T(8,128)(2,1)}, bf16[64,768]{1,0:T(8,128)(2,1)}, u32[]{:S(2)}, u32[]{:S(2)}) collective-permute-start(bf16[64,768]{1,0:T(8,128)(2,1)} %get-tuple-element.32), channel_id=1, source_target_pairs={{0,8},{4,12},{8,0},{12,4},{16,24},{20,28},{24,16},{28,20},{1,9},{5... | collective-permute-start | bytes 294920 | tf_op jit(solution)/shard_map/ppermute | solution.py:20
  6.4 3.3 %slice_bitcast_fusion.1 = (bf16[768,768]{1,0:T(8,128)(2,1)}, bf16[768,768]{1,0:T(8,128)(2,1)}) fusion(bf16[2,768,768]{2,1,0:T(8,128)(2,1)} %param.8), kind=kLoop, calls=%fused_computation.27 | loop fusion | bytes 4718592 | tf_op jit(solution)/shard_map/squeeze | solution.py:92
  14.1 2.0 copy.9
  16.2 2.3 %fusion.1 = bf16[768,768]{1,0:T(8,128)(2,1)S(1)} fusion(bf16[768,768]{1,0:T(8,128)(2,1)} %param.7, f32[768,768]{1,0:T(8,128)S(1)} %copy.9, s32[768]{0:T(1024)S(1)} %convert_reduce_fusion.2), kind=kLoop, calls=%fused_computation.6 | loop fusion | flops 7667712 | bytes 4721664 | tf_op jit(solution)/shard_map/convert_element_type | solution.py:83
  23.2 2.6 %fusion.3 = (bf16[768,768]{1,0:T(8,128)(2,1)S(1)}, bf16[768,768]{1,0:T(8,128)(2,1)S(1)}) fusion(f32[768]{0:T(1024)S(1)} %get-tuple-element.77, f32[768]{0:T(1024)S(1)} %get-tuple-element.76, f32[768]{0:T(1024)S(1)} %get-tuple-element.75, f32[768]{0:T(1024)S(1)} %get-tuple-element.78, pred[768]{0:T(1024)(128)(4,1)S(1)} %get-tuple-element.80, ...), kind=kLoop, calls=%fused_computation.12 | loop fusion | flops 5898240 | bytes 4747776 | tf_op jit(solution)/shard_map/jit(_where)/select_n | solution.py:92
  33.2 23.2 %collective-permute-done.24 = bf16[64,768]{1,0:T(8,128)(2,1)S(1)} collective-permute-done((bf16[64,768]{1,0:T(8,128)(2,1)S(1)}, bf16[64,768]{1,0:T(8,128)(2,1)S(1)}, u32[]{:S(2)}, u32[]{:S(2)}) %collective-permute-start.24) | collective-permute-done | bytes 98336 | tf_op jit(solution)/shard_map/ppermute | solution.py:20
  57.6 3.8 %fusion.4 = (bf16[768,768]{1,0:T(8,128)(2,1)S(1)}, bf16[768,768]{1,0:T(8,128)(2,1)S(1)}) fusion(bf16[768,768]{1,0:T(8,128)(2,1)} %collective-permute-done.2, f32[768]{0:T(1024)S(1)} %get-tuple-element.10, f32[768]{0:T(1024)S(1)} %get-tuple-element.11, f32[768]{0:T(1024)S(1)} %get-tuple-element.12, f32[768]{0:T(1024)S(1)} %get-tuple-element.9, ...), kind=kLoop, calls=%fused_computation.13 | loop fusion | flops 5898240 | bytes 4745472 | tf_op jit(solution)/shard_map/jit(_where)/select_n | solution.py:96
  65.8 2.6 %collective-permute-start.7 = (bf16[3,512,128]{2,1,0:T(8,128)(2,1)S(1)}, bf16[3,512,128]{2,1,0:T(8,128)(2,1)S(1)}, u32[]{:S(2)}, u32[]{:S(2)}) collective-permute-start(bf16[3,512,128]{2,1,0:T(8,128)(2,1)S(1)} %slice.124), channel_id=1, source_target_pairs={{0,2},{1,3},{2,0},{3,1},{4,6},{5,7},{6,4},{7,5},{8,10},{9,11},{10,... | collective-permute-start | bytes 1179656 | tf_op jit(solution)/shard_map/ppermute | solution.py:39
  72.7 2.6 %collective-permute-done.10 = bf16[64,768]{1,0:T(8,128)(2,1)S(1)} collective-permute-done((bf16[64,768]{1,0:T(8,128)(2,1)S(1)}, bf16[64,768]{1,0:T(8,128)(2,1)S(1)}, u32[]{:S(2)}, u32[]{:S(2)}) %collective-permute-start.10) | collective-permute-done | bytes 98336 | tf_op jit(solution)/shard_map/ppermute | solution.py:20
  78.9 2.5 %collective-permute-done.26 = bf16[64,768]{1,0:T(8,128)(2,1)S(1)} collective-permute-done((bf16[64,768]{1,0:T(8,128)(2,1)S(1)}, bf16[64,768]{1,0:T(8,128)(2,1)S(1)}, u32[]{:S(2)}, u32[]{:S(2)}) %collective-permute-start.26) | collective-permute-done | bytes 98336 | tf_op jit(solution)/shard_map/ppermute | solution.py:20
  85.0 2.5 %collective-permute-done.12 = bf16[64,768]{1,0:T(8,128)(2,1)S(1)} collective-permute-done((bf16[64,768]{1,0:T(8,128)(2,1)S(1)}, bf16[64,768]{1,0:T(8,128)(2,1)S(1)}, u32[]{:S(2)}, u32[]{:S(2)}) %collective-permute-start.12) | collective-permute-done | bytes 98336 | tf_op jit(solution)/shard_map/ppermute | solution.py:20
  91.1 2.5 %collective-permute-done.28 = bf16[64,768]{1,0:T(8,128)(2,1)S(1)} collective-permute-done((bf16[64,768]{1,0:T(8,128)(2,1)S(1)}, bf16[64,768]{1,0:T(8,128)(2,1)S(1)}, u32[]{:S(2)}, u32[]{:S(2)}) %collective-permute-start.28) | collective-permute-done | bytes 98336 | tf_op jit(solution)/shard_map/ppermute | solution.py:20
  97.3 2.5 %collective-permute-done.14 = bf16[64,768]{1,0:T(8,128)(2,1)S(1)} collective-permute-done((bf16[64,768]{1,0:T(8,128)(2,1)S(1)}, bf16[64,768]{1,0:T(8,128)(2,1)S(1)}, u32[]{:S(2)}, u32[]{:S(2)}) %collective-permute-start.14) | collective-permute-done | bytes 98336 | tf_op jit(solution)/shard_map/ppermute | solution.py:20
  103.4 2.5 %collective-permute-done.30 = bf16[64,768]{1,0:T(8,128)(2,1)S(1)} collective-permute-done((bf16[64,768]{1,0:T(8,128)(2,1)S(1)}, bf16[64,768]{1,0:T(8,128)(2,1)S(1)}, u32[]{:S(2)}, u32[]{:S(2)}) %collective-permute-start.30) | collective-permute-done | bytes 98336 | tf_op jit(solution)/shard_map/ppermute | solution.py:20
  109.5 2.5 %collective-permute-done.16 = bf16[64,768]{1,0:T(8,128)(2,1)S(1)} collective-permute-done((bf16[64,768]{1,0:T(8,128)(2,1)S(1)}, bf16[64,768]{1,0:T(8,128)(2,1)S(1)}, u32[]{:S(2)}, u32[]{:S(2)}) %collective-permute-start.16) | collective-permute-done | bytes 98336 | tf_op jit(solution)/shard_map/ppermute | solution.py:20
  115.6 2.5 %collective-permute-done.32 = bf16[64,768]{1,0:T(8,128)(2,1)S(1)} collective-permute-done((bf16[64,768]{1,0:T(8,128)(2,1)S(1)}, bf16[64,768]{1,0:T(8,128)(2,1)S(1)}, u32[]{:S(2)}, u32[]{:S(2)}) %collective-permute-start.32) | collective-permute-done | bytes 98336 | tf_op jit(solution)/shard_map/ppermute | solution.py:20
  121.8 2.5 %collective-permute-done.18 = bf16[64,768]{1,0:T(8,128)(2,1)S(1)} collective-permute-done((bf16[64,768]{1,0:T(8,128)(2,1)S(1)}, bf16[64,768]{1,0:T(8,128)(2,1)S(1)}, u32[]{:S(2)}, u32[]{:S(2)}) %collective-permute-start.18) | collective-permute-done | bytes 98336 | tf_op jit(solution)/shard_map/ppermute | solution.py:20
  127.9 2.5 %collective-permute-done.34 = bf16[64,768]{1,0:T(8,128)(2,1)S(1)} collective-permute-done((bf16[64,768]{1,0:T(8,128)(2,1)S(1)}, bf16[64,768]{1,0:T(8,128)(2,1)S(1)}, u32[]{:S(2)}, u32[]{:S(2)}) %collective-permute-start.34) | collective-permute-done | bytes 98336 | tf_op jit(solution)/shard_map/ppermute | solution.py:20
  134.2 2.3 %collective-permute-done.20 = bf16[64,768]{1,0:T(8,128)(2,1)S(1)} collective-permute-done((bf16[64,768]{1,0:T(8,128)(2,1)S(1)}, bf16[64,768]{1,0:T(8,128)(2,1)S(1)}, u32[]{:S(2)}, u32[]{:S(2)}) %collective-permute-start.20) | collective-permute-done | bytes 98336 | tf_op jit(solution)/shard_map/ppermute | solution.py:20
  140.1 2.5 %collective-permute-done.36 = bf16[64,768]{1,0:T(8,128)(2,1)S(1)} collective-permute-done((bf16[64,768]{1,0:T(8,128)(2,1)S(1)}, bf16[64,768]{1,0:T(8,128)(2,1)S(1)}, u32[]{:S(2)}, u32[]{:S(2)}) %collective-permute-start.36) | collective-permute-done | bytes 98336 | tf_op jit(solution)/shard_map/ppermute | solution.py:20
  146.2 2.5 %collective-permute-done.22 = bf16[64,768]{1,0:T(8,128)(2,1)S(1)} collective-permute-done((bf16[64,768]{1,0:T(8,128)(2,1)S(1)}, bf16[64,768]{1,0:T(8,128)(2,1)S(1)}, u32[]{:S(2)}, u32[]{:S(2)}) %collective-permute-start.22) | collective-permute-done | bytes 98336 | tf_op jit(solution)/shard_map/ppermute | solution.py:20
  151.1 2.3 %collective-permute-done.38 = bf16[64,768]{1,0:T(8,128)(2,1)S(1)} collective-permute-done((bf16[64,768]{1,0:T(8,128)(2,1)S(1)}, bf16[64,768]{1,0:T(8,128)(2,1)S(1)}, u32[]{:S(2)}, u32[]{:S(2)}) %collective-permute-start.38) | collective-permute-done | bytes 98336 | tf_op jit(solution)/shard_map/ppermute | solution.py:20
  157.1 2.8 %collective-permute-start.41 = (bf16[128,768]{1,0:T(8,128)(2,1)S(1)}, bf16[128,768]{1,0:T(8,128)(2,1)}, u32[]{:S(2)}, u32[]{:S(2)}) collective-permute-start(bf16[128,768]{1,0:T(8,128)(2,1)S(1)} %pad_maximum_fusion.5), channel_id=1, source_target_pairs={{0,3},{1,0},{2,1},{3,2},{4,7},{5,4},{6,5},{7,6},{8,11},{9,8},{10,9... | collective-permute-start | bytes 589832 | tf_op jit(solution)/shard_map/ppermute | solution.py:29
  161.2 4.5 %collective-permute-done.39 = bf16[128,768]{1,0:T(8,128)(2,1)S(1)} collective-permute-done((bf16[128,768]{1,0:T(8,128)(2,1)S(1)}, bf16[128,768]{1,0:T(8,128)(2,1)S(1)}, u32[]{:S(2)}, u32[]{:S(2)}) %collective-permute-start.39) | collective-permute-done | bytes 196640 | tf_op jit(solution)/shard_map/ppermute | solution.py:29
  165.7 8.1 %collective-permute-done.40 = bf16[128,768]{1,0:T(8,128)(2,1)} collective-permute-done((bf16[128,768]{1,0:T(8,128)(2,1)S(1)}, bf16[128,768]{1,0:T(8,128)(2,1)}, u32[]{:S(2)}, u32[]{:S(2)}) %collective-permute-start.40) | collective-permute-done | bytes 196640 | tf_op jit(solution)/shard_map/ppermute | solution.py:29
  179.7 2.1 collective-permute-done.43
  183.3 2.1 collective-permute-done.44
  189.7 2.1 collective-permute-done.46
  193.3 2.1 collective-permute-done.47
  199.7 2.1 collective-permute-done.49
  203.3 2.1 collective-permute-done.50
  209.5 2.1 collective-permute-done.52
  (248 shorter events, 107.8 us)
Async XLA Ops:
  1.6 28.3 %collective-permute-start = (bf16[64,768]{1,0:T(8,128)(2,1)}, bf16[64,768]{1,0:T(8,128)(2,1)}, u32[]{:S(2)}, u32[]{:S(2)}) collective-permute-start(bf16[64,768]{1,0:T(8,128)(2,1)} %get-tuple-element.32), channel_id=1, source_target_pairs={{0,4},{4,0},{8,12},{12,8},{16,20},{20,16},{24,28},{28,24},{1,5},{5... | collective-permute-start | bytes 294920 | tf_op jit(solution)/shard_map/ppermute | solution.py:20
  2.1 29.7 %collective-permute-start.3 = (bf16[64,768]{1,0:T(8,128)(2,1)}, bf16[64,768]{1,0:T(8,128)(2,1)}, u32[]{:S(2)}, u32[]{:S(2)}) collective-permute-start(bf16[64,768]{1,0:T(8,128)(2,1)} %get-tuple-element.32), channel_id=1, source_target_pairs={{0,8},{4,12},{8,0},{12,4},{16,24},{20,28},{24,16},{28,20},{1,9},{5... | collective-permute-start | bytes 294920 | tf_op jit(solution)/shard_map/ppermute | solution.py:20
  5.8 20.0 %collective-permute-start.1 = (s32[4,4]{1,0:T(4,128)}, s32[4,4]{1,0:T(4,128)}, u32[]{:S(2)}, u32[]{:S(2)}) collective-permute-start(s32[4,4]{1,0:T(4,128)} %get-tuple-element.34), channel_id=1, source_target_pairs={{0,4},{4,0},{8,12},{12,8},{16,20},{20,16},{24,28},{28,24},{1,5},{5... | collective-permute-start | bytes 200 | tf_op jit(solution)/shard_map/ppermute | solution.py:20
  6.1 22.5 %collective-permute-start.4 = (s32[4,4]{1,0:T(4,128)}, s32[4,4]{1,0:T(4,128)}, u32[]{:S(2)}, u32[]{:S(2)}) collective-permute-start(s32[4,4]{1,0:T(4,128)} %get-tuple-element.35), channel_id=1, source_target_pairs={{0,8},{4,12},{8,0},{12,4},{16,24},{20,28},{24,16},{28,20},{1,9},{5... | collective-permute-start | bytes 200 | tf_op jit(solution)/shard_map/ppermute | solution.py:20
  9.6 47.8 %collective-permute-start.2 = (bf16[768,768]{1,0:T(8,128)(2,1)}, bf16[768,768]{1,0:T(8,128)(2,1)}, u32[]{:S(2)}, u32[]{:S(2)}) collective-permute-start(bf16[768,768]{1,0:T(8,128)(2,1)} %get-tuple-element.28), channel_id=1, source_target_pairs={{0,4},{4,0},{8,12},{12,8},{16,20},{20,16},{24,28},{28,24},{1,5},{5... | collective-permute-start | bytes 3538952 | tf_op jit(solution)/shard_map/ppermute | solution.py:20
  25.9 31.6 %collective-permute-start.5 = (bf16[768,768]{1,0:T(8,128)(2,1)S(1)}, bf16[768,768]{1,0:T(8,128)(2,1)S(1)}, u32[]{:S(2)}, u32[]{:S(2)}) collective-permute-start(bf16[768,768]{1,0:T(8,128)(2,1)S(1)} %copy-done.4), channel_id=1, source_target_pairs={{0,8},{4,12},{8,0},{12,4},{16,24},{20,28},{24,16},{28,20},{1,9},{5... | collective-permute-start | bytes 3538952 | tf_op jit(solution)/shard_map/ppermute | solution.py:20
  28.6 28.4 %collective-permute-start.23 = (bf16[64,768]{1,0:T(8,128)(2,1)S(1)}, bf16[64,768]{1,0:T(8,128)(2,1)S(1)}, u32[]{:S(2)}, u32[]{:S(2)}) collective-permute-start(bf16[64,768]{1,0:T(8,128)(2,1)S(1)} %copy-done.8), channel_id=1, source_target_pairs={{0,4},{4,0},{8,12},{12,8},{16,20},{20,16},{24,28},{28,24},{1,5},{5... | collective-permute-start | bytes 294920 | tf_op jit(solution)/shard_map/ppermute | solution.py:20
  29.9 26.5 %collective-permute-start.24 = (bf16[64,768]{1,0:T(8,128)(2,1)S(1)}, bf16[64,768]{1,0:T(8,128)(2,1)S(1)}, u32[]{:S(2)}, u32[]{:S(2)}) collective-permute-start(bf16[64,768]{1,0:T(8,128)(2,1)S(1)} %copy-done.8), channel_id=1, source_target_pairs={{0,8},{4,12},{8,0},{12,4},{16,24},{20,28},{24,16},{28,20},{1,9},{5... | collective-permute-start | bytes 294920 | tf_op jit(solution)/shard_map/ppermute | solution.py:20
  64.0 93.1 %collective-permute-start.6 = (bf16[3,512,128]{2,1,0:T(8,128)(2,1)S(1)}, bf16[3,512,128]{2,1,0:T(8,128)(2,1)S(1)}, u32[]{:S(2)}, u32[]{:S(2)}) collective-permute-start(bf16[3,512,128]{2,1,0:T(8,128)(2,1)S(1)} %slice.124), channel_id=1, source_target_pairs={{0,1},{1,2},{2,3},{3,0},{4,5},{5,6},{6,7},{7,4},{8,9},{9,10},{10,1... | collective-permute-start | bytes 1179656 | tf_op jit(solution)/shard_map/ppermute | solution.py:39
  65.8 94.2 %collective-permute-start.7 = (bf16[3,512,128]{2,1,0:T(8,128)(2,1)S(1)}, bf16[3,512,128]{2,1,0:T(8,128)(2,1)S(1)}, u32[]{:S(2)}, u32[]{:S(2)}) collective-permute-start(bf16[3,512,128]{2,1,0:T(8,128)(2,1)S(1)} %slice.124), channel_id=1, source_target_pairs={{0,2},{1,3},{2,0},{3,1},{4,6},{5,7},{6,4},{7,5},{8,10},{9,11},{10,... | collective-permute-start | bytes 1179656 | tf_op jit(solution)/shard_map/ppermute | solution.py:39
  68.3 91.6 %collective-permute-start.8 = (bf16[3,512,128]{2,1,0:T(8,128)(2,1)S(1)}, bf16[3,512,128]{2,1,0:T(8,128)(2,1)}, u32[]{:S(2)}, u32[]{:S(2)}) collective-permute-start(bf16[3,512,128]{2,1,0:T(8,128)(2,1)S(1)} %slice.124), channel_id=1, source_target_pairs={{0,3},{1,0},{2,1},{3,2},{4,7},{5,4},{6,5},{7,6},{8,11},{9,8},{10,9... | collective-permute-start | bytes 1179656 | tf_op jit(solution)/shard_map/ppermute | solution.py:39
  70.0 6.1 %collective-permute-start.9 = (bf16[64,768]{1,0:T(8,128)(2,1)S(1)}, bf16[64,768]{1,0:T(8,128)(2,1)S(1)}, u32[]{:S(2)}, u32[]{:S(2)}) collective-permute-start(bf16[64,768]{1,0:T(8,128)(2,1)S(1)} %convert_element_type.124), channel_id=1, source_target_pairs={{0,4},{4,0},{8,12},{12,8},{16,20},{20,16},{24,28},{28,24},{1,5},{5... | collective-permute-start | bytes 294920 | tf_op jit(solution)/shard_map/ppermute | solution.py:20
  75.3 7.0 %collective-permute-start.25 = (bf16[64,768]{1,0:T(8,128)(2,1)S(1)}, bf16[64,768]{1,0:T(8,128)(2,1)S(1)}, u32[]{:S(2)}, u32[]{:S(2)}) collective-permute-start(bf16[64,768]{1,0:T(8,128)(2,1)S(1)} %get-tuple-element.47), channel_id=1, source_target_pairs={{0,4},{4,0},{8,12},{12,8},{16,20},{20,16},{24,28},{28,24},{1,5},{5... | collective-permute-start | bytes 294920 | tf_op jit(solution)/shard_map/ppermute | solution.py:20
  81.4 7.0 %collective-permute-start.11 = (bf16[64,768]{1,0:T(8,128)(2,1)S(1)}, bf16[64,768]{1,0:T(8,128)(2,1)S(1)}, u32[]{:S(2)}, u32[]{:S(2)}) collective-permute-start(bf16[64,768]{1,0:T(8,128)(2,1)S(1)} %get-tuple-element.61), channel_id=1, source_target_pairs={{0,4},{4,0},{8,12},{12,8},{16,20},{20,16},{24,28},{28,24},{1,5},{5... | collective-permute-start | bytes 294920 | tf_op jit(solution)/shard_map/ppermute | solution.py:20
  82.3 5.3 %collective-permute-start.12 = (bf16[64,768]{1,0:T(8,128)(2,1)S(1)}, bf16[64,768]{1,0:T(8,128)(2,1)S(1)}, u32[]{:S(2)}, u32[]{:S(2)}) collective-permute-start(bf16[64,768]{1,0:T(8,128)(2,1)S(1)} %get-tuple-element.61), channel_id=1, source_target_pairs={{0,8},{4,12},{8,0},{12,4},{16,24},{20,28},{24,16},{28,20},{1,9},{5... | collective-permute-start | bytes 294920 | tf_op jit(solution)/shard_map/ppermute | solution.py:20
  87.6 7.0 %collective-permute-start.27 = (bf16[64,768]{1,0:T(8,128)(2,1)S(1)}, bf16[64,768]{1,0:T(8,128)(2,1)S(1)}, u32[]{:S(2)}, u32[]{:S(2)}) collective-permute-start(bf16[64,768]{1,0:T(8,128)(2,1)S(1)} %get-tuple-element.49), channel_id=1, source_target_pairs={{0,4},{4,0},{8,12},{12,8},{16,20},{20,16},{24,28},{28,24},{1,5},{5... | collective-permute-start | bytes 294920 | tf_op jit(solution)/shard_map/ppermute | solution.py:20
  88.4 5.3 %collective-permute-start.28 = (bf16[64,768]{1,0:T(8,128)(2,1)S(1)}, bf16[64,768]{1,0:T(8,128)(2,1)S(1)}, u32[]{:S(2)}, u32[]{:S(2)}) collective-permute-start(bf16[64,768]{1,0:T(8,128)(2,1)S(1)} %get-tuple-element.49), channel_id=1, source_target_pairs={{0,8},{4,12},{8,0},{12,4},{16,24},{20,28},{24,16},{28,20},{1,9},{5... | collective-permute-start | bytes 294920 | tf_op jit(solution)/shard_map/ppermute | solution.py:20
  93.7 7.0 %collective-permute-start.13 = (bf16[64,768]{1,0:T(8,128)(2,1)S(1)}, bf16[64,768]{1,0:T(8,128)(2,1)S(1)}, u32[]{:S(2)}, u32[]{:S(2)}) collective-permute-start(bf16[64,768]{1,0:T(8,128)(2,1)S(1)} %get-tuple-element.63), channel_id=1, source_target_pairs={{0,4},{4,0},{8,12},{12,8},{16,20},{20,16},{24,28},{28,24},{1,5},{5... | collective-permute-start | bytes 294920 | tf_op jit(solution)/shard_map/ppermute | solution.py:20
  99.8 7.0 %collective-permute-start.29 = (bf16[64,768]{1,0:T(8,128)(2,1)S(1)}, bf16[64,768]{1,0:T(8,128)(2,1)S(1)}, u32[]{:S(2)}, u32[]{:S(2)}) collective-permute-start(bf16[64,768]{1,0:T(8,128)(2,1)S(1)} %get-tuple-element.51), channel_id=1, source_target_pairs={{0,4},{4,0},{8,12},{12,8},{16,20},{20,16},{24,28},{28,24},{1,5},{5... | collective-permute-start | bytes 294920 | tf_op jit(solution)/shard_map/ppermute | solution.py:20
  105.9 7.0 %collective-permute-start.15 = (bf16[64,768]{1,0:T(8,128)(2,1)S(1)}, bf16[64,768]{1,0:T(8,128)(2,1)S(1)}, u32[]{:S(2)}, u32[]{:S(2)}) collective-permute-start(bf16[64,768]{1,0:T(8,128)(2,1)S(1)} %get-tuple-element.65), channel_id=1, source_target_pairs={{0,4},{4,0},{8,12},{12,8},{16,20},{20,16},{24,28},{28,24},{1,5},{5... | collective-permute-start | bytes 294920 | tf_op jit(solution)/shard_map/ppermute | solution.py:20
  106.8 5.3 %collective-permute-start.16 = (bf16[64,768]{1,0:T(8,128)(2,1)S(1)}, bf16[64,768]{1,0:T(8,128)(2,1)S(1)}, u32[]{:S(2)}, u32[]{:S(2)}) collective-permute-start(bf16[64,768]{1,0:T(8,128)(2,1)S(1)} %get-tuple-element.65), channel_id=1, source_target_pairs={{0,8},{4,12},{8,0},{12,4},{16,24},{20,28},{24,16},{28,20},{1,9},{5... | collective-permute-start | bytes 294920 | tf_op jit(solution)/shard_map/ppermute | solution.py:20
  112.0 7.0 %collective-permute-start.31 = (bf16[64,768]{1,0:T(8,128)(2,1)S(1)}, bf16[64,768]{1,0:T(8,128)(2,1)S(1)}, u32[]{:S(2)}, u32[]{:S(2)}) collective-permute-start(bf16[64,768]{1,0:T(8,128)(2,1)S(1)} %get-tuple-element.53), channel_id=1, source_target_pairs={{0,4},{4,0},{8,12},{12,8},{16,20},{20,16},{24,28},{28,24},{1,5},{5... | collective-permute-start | bytes 294920 | tf_op jit(solution)/shard_map/ppermute | solution.py:20
  112.9 5.3 %collective-permute-start.32 = (bf16[64,768]{1,0:T(8,128)(2,1)S(1)}, bf16[64,768]{1,0:T(8,128)(2,1)S(1)}, u32[]{:S(2)}, u32[]{:S(2)}) collective-permute-start(bf16[64,768]{1,0:T(8,128)(2,1)S(1)} %get-tuple-element.53), channel_id=1, source_target_pairs={{0,8},{4,12},{8,0},{12,4},{16,24},{20,28},{24,16},{28,20},{1,9},{5... | collective-permute-start | bytes 294920 | tf_op jit(solution)/shard_map/ppermute | solution.py:20
  118.2 7.0 %collective-permute-start.17 = (bf16[64,768]{1,0:T(8,128)(2,1)S(1)}, bf16[64,768]{1,0:T(8,128)(2,1)S(1)}, u32[]{:S(2)}, u32[]{:S(2)}) collective-permute-start(bf16[64,768]{1,0:T(8,128)(2,1)S(1)} %get-tuple-element.67), channel_id=1, source_target_pairs={{0,4},{4,0},{8,12},{12,8},{16,20},{20,16},{24,28},{28,24},{1,5},{5... | collective-permute-start | bytes 294920 | tf_op jit(solution)/shard_map/ppermute | solution.py:20
  124.3 7.0 %collective-permute-start.33 = (bf16[64,768]{1,0:T(8,128)(2,1)S(1)}, bf16[64,768]{1,0:T(8,128)(2,1)S(1)}, u32[]{:S(2)}, u32[]{:S(2)}) collective-permute-start(bf16[64,768]{1,0:T(8,128)(2,1)S(1)} %get-tuple-element.55), channel_id=1, source_target_pairs={{0,4},{4,0},{8,12},{12,8},{16,20},{20,16},{24,28},{28,24},{1,5},{5... | collective-permute-start | bytes 294920 | tf_op jit(solution)/shard_map/ppermute | solution.py:20
  125.1 5.3 %collective-permute-start.34 = (bf16[64,768]{1,0:T(8,128)(2,1)S(1)}, bf16[64,768]{1,0:T(8,128)(2,1)S(1)}, u32[]{:S(2)}, u32[]{:S(2)}) collective-permute-start(bf16[64,768]{1,0:T(8,128)(2,1)S(1)} %get-tuple-element.55), channel_id=1, source_target_pairs={{0,8},{4,12},{8,0},{12,4},{16,24},{20,28},{24,16},{28,20},{1,9},{5... | collective-permute-start | bytes 294920 | tf_op jit(solution)/shard_map/ppermute | solution.py:20
  130.4 7.0 %collective-permute-start.19 = (bf16[64,768]{1,0:T(8,128)(2,1)S(1)}, bf16[64,768]{1,0:T(8,128)(2,1)S(1)}, u32[]{:S(2)}, u32[]{:S(2)}) collective-permute-start(bf16[64,768]{1,0:T(8,128)(2,1)S(1)} %get-tuple-element.69), channel_id=1, source_target_pairs={{0,4},{4,0},{8,12},{12,8},{16,20},{20,16},{24,28},{28,24},{1,5},{5... | collective-permute-start | bytes 294920 | tf_op jit(solution)/shard_map/ppermute | solution.py:20
  136.5 7.0 %collective-permute-start.35 = (bf16[64,768]{1,0:T(8,128)(2,1)S(1)}, bf16[64,768]{1,0:T(8,128)(2,1)S(1)}, u32[]{:S(2)}, u32[]{:S(2)}) collective-permute-start(bf16[64,768]{1,0:T(8,128)(2,1)S(1)} %get-tuple-element.57), channel_id=1, source_target_pairs={{0,4},{4,0},{8,12},{12,8},{16,20},{20,16},{24,28},{28,24},{1,5},{5... | collective-permute-start | bytes 294920 | tf_op jit(solution)/shard_map/ppermute | solution.py:20
  142.7 11.2 %collective-permute-start.21 = (bf16[64,768]{1,0:T(8,128)(2,1)S(1)}, bf16[64,768]{1,0:T(8,128)(2,1)S(1)}, u32[]{:S(2)}, u32[]{:S(2)}) collective-permute-start(bf16[64,768]{1,0:T(8,128)(2,1)S(1)} %get-tuple-element.71), channel_id=1, source_target_pairs={{0,4},{4,0},{8,12},{12,8},{16,20},{20,16},{24,28},{28,24},{1,5},{5... | collective-permute-start | bytes 294920 | tf_op jit(solution)/shard_map/ppermute | solution.py:20
  156.0 9.7 %collective-permute-start.39 = (bf16[128,768]{1,0:T(8,128)(2,1)S(1)}, bf16[128,768]{1,0:T(8,128)(2,1)S(1)}, u32[]{:S(2)}, u32[]{:S(2)}) collective-permute-start(bf16[128,768]{1,0:T(8,128)(2,1)S(1)} %pad_maximum_fusion.5), channel_id=1, source_target_pairs={{0,1},{1,2},{2,3},{3,0},{4,5},{5,6},{6,7},{7,4},{8,9},{9,10},{10,1... | collective-permute-start | bytes 589832 | tf_op jit(solution)/shard_map/ppermute | solution.py:29
  156.7 17.1 %collective-permute-start.40 = (bf16[128,768]{1,0:T(8,128)(2,1)S(1)}, bf16[128,768]{1,0:T(8,128)(2,1)}, u32[]{:S(2)}, u32[]{:S(2)}) collective-permute-start(bf16[128,768]{1,0:T(8,128)(2,1)S(1)} %pad_maximum_fusion.5), channel_id=1, source_target_pairs={{0,2},{1,3},{2,0},{3,1},{4,6},{5,7},{6,4},{7,5},{8,10},{9,11},{10,... | collective-permute-start | bytes 589832 | tf_op jit(solution)/shard_map/ppermute | solution.py:29
  157.1 16.7 %collective-permute-start.41 = (bf16[128,768]{1,0:T(8,128)(2,1)S(1)}, bf16[128,768]{1,0:T(8,128)(2,1)}, u32[]{:S(2)}, u32[]{:S(2)}) collective-permute-start(bf16[128,768]{1,0:T(8,128)(2,1)S(1)} %pad_maximum_fusion.5), channel_id=1, source_target_pairs={{0,3},{1,0},{2,1},{3,2},{4,7},{5,4},{6,5},{7,6},{8,11},{9,8},{10,9... | collective-permute-start | bytes 589832 | tf_op jit(solution)/shard_map/ppermute | solution.py:29
  (35 other events, 145.8 us)

commit v6 on v4

--- a/solution.py
+++ b/solution.py
@@ -58,12 +58,10 @@
 def pattern_mask(pattern, row_atoms, col_atoms):
     levels = jnp.arange(pattern.shape[0], dtype=jnp.int32)
     row_onehot = (row_atoms[:, None] == levels[None, :]).astype(jnp.bfloat16)
-    col_onehot = (col_atoms[:, None] == levels[None, :]).astype(jnp.bfloat16)
     per_row = jnp.dot(row_onehot, pattern.astype(jnp.bfloat16), preferred_element_type=jnp.float32)
-    mask = lax.dot_general(
-        per_row.astype(jnp.bfloat16), col_onehot, (((1,), (1,)), ((), ())),
-        preferred_element_type=jnp.float32,
-    )
+    mask = jnp.broadcast_to(per_row[:, :1], (row_atoms.shape[0], col_atoms.shape[0]))
+    for atom in range(1, pattern.shape[1]):
+        mask = jnp.where((col_atoms == atom)[None, :], per_row[:, atom : atom + 1], mask)
     return mask > 0.5
 
 
@@ -71,7 +69,13 @@
     orb_dev = diag_block.shape[1]
     atoms_dev = pair_pattern.shape[2]
     atoms_here = lax.axis_index("atoms")
-    shipped = [swapped(pair_block[r], "atoms", r) for r in range(ROUNDS)]
+    half_bands = subspace.shape[0] // 2
+    packed = [
+        swapped(jnp.concatenate([subspace[:half_bands], pair_block[r]], axis=0), "atoms", r)
+        for r in range(ROUNDS)
+    ]
+    first_rows = [piece[:half_bands] for piece in packed]
+    shipped = [piece[half_bands:] for piece in packed]
     shipped_pattern = [swapped(pair_pattern[r], "atoms", r) for r in range(ROUNDS)]
     own_atoms = atom_index(
         lax.dynamic_index_in_dim(atom_sizes, atoms_here, 0, keepdims=False), orb_dev
@@ -95,10 +99,13 @@
             jnp.where(other_mask, shipped[round_index], jnp.zeros((), jnp.bfloat16))
         )
 
-    def apply_operator(values):
+    def apply_operator(values, received=None):
         result = jnp.dot(values, diag_sym, preferred_element_type=jnp.float32)
         for round_index in range(ROUNDS):
-            other_rows = swapped(values, "atoms", round_index)
+            if received is None:
+                other_rows = swapped(values, "atoms", round_index)
+            else:
+                other_rows = received[round_index]
             result = result + lax.dot_general(
                 other_rows, own_pair_t[round_index], (((1,), (1,)), ((), ())),
                 preferred_element_type=jnp.float32,
@@ -108,9 +115,9 @@
             )
         return result
 
-    def chebyshev(start_rows, hook):
+    def chebyshev(start_rows, hook, received=None):
         previous = start_rows.astype(jnp.float32)
-        current = (apply_operator(start_rows) - filter_center * previous) / filter_half
+        current = (apply_operator(start_rows, received) - filter_center * previous) / filter_half
         for degree_index in range(1, DEGREE):
             if degree_index == GATHER_AT:
                 current = hook(current)
@@ -126,10 +133,9 @@
         gathered.append(gather_pieces(held))
         return current
 
-    half_bands = subspace.shape[0] // 2
     current = jnp.concatenate(
         [
-            chebyshev(subspace[:half_bands], start_rotation_gather),
+            chebyshev(subspace[:half_bands], start_rotation_gather, first_rows),
             chebyshev(subspace[half_bands:], lambda rows: rows),
         ],
         axis=0,

time: 179 us -> 186 us (1.039)
  waiting for transfers between devices: 50.5 us -> 72.5 us
  starting transfers between devices: 47.8 us -> 33.7 us
  other arithmetic: 8.44 us -> 20.2 us
  matrix products: 57.9 us -> 48.3 us
  local copies, waits for them, and re-layouts: 12.5 us -> 10.1 us
    ppermute x48 -> x46, waiting for transfers between devices: 34.3 us -> 55.8 us  [swapped(): return lax.ppermute(value, axis, pairs)]
    ppermute x48 -> x46, starting transfers between devices: 38.7 us -> 24.7 us  [swapped(): return lax.ppermute(value, axis, pairs)]
    select_n x0 -> x2, other arithmetic: none -> 6.71 us  [the longest x1 4.07 us: body(): jnp.where(other_mask, shipped[round_index], jnp.zeros((), jnp.bfloat16))]
    dot_general x4, matrix products: 8.21 us -> 2.48 us  [pattern_mask(): jnp.dot(row_onehot, pattern.astype(jnp.bfloat16), preferred_element_type=...]
    dot_general x32, matrix products: 22.4 us -> 19.7 us  [apply_operator(): lax.dot_general(other_rows, own_pair_t[round_index], (((1,), (1,)), ((),...]
  transfers between devices with their start and end apart: 54 -> 52, of which waited for: 25 -> 26; matrix products, arithmetic and copies ran while one was open for 36% -> 33% of each run, Pallas kernels for 0% -> 0%
where the time goes in v6:
time: 186 us
  waiting for transfers between devices  72.5 us (39%)
  matrix products  48.3 us (26%)
  starting transfers between devices  33.7 us (18%)
  other arithmetic  20.2 us (11%)
  local copies, waits for them, and re-layouts  10.1 us (5%)
    ppermute x46, waiting for transfers between devices, swapped(): return lax.ppermute(value, axis, pairs)  55.8 us
    ppermute x46, starting transfers between devices, swapped(): return lax.ppermute(value, axis, pairs)  24.7 us
    dot_general x32, matrix products, apply_operator(): lax.dot_general(other_rows, own_pair_t[round_index], (((1,), (1,)), ((),...  19.7 us
    ppermute x3, waiting for transfers between devices, gather_bands(): pieces.append(lax.ppermute(value, 'bands', pairs))  16.7 us
    dot_general x32, matrix products, apply_operator(): jnp.dot(other_rows, other_pair[round_index], preferred_element_type=jnp.f...  14.5 us
    dot_general x16, matrix products, apply_operator(): result = jnp.dot(values, diag_sym, preferred_element_type=jnp.float32)  6.6 us
    ppermute x3, starting transfers between devices, gather_pieces(): pieces.append(lax.ppermute(value, 'bands', pairs))  4.88 us
    select_n x1, other arithmetic, body(): jnp.where(other_mask, shipped[round_index], jnp.zeros((), jnp.bfloat16))  4.07 us
  transfers between devices with their start and end apart: 52, of which 26 were waited for; matrix products, arithmetic and copies ran while one was open for 33% of the time, Pallas kernels for 0%

profile of v6, /device:TPU:0, one launch (start us, length us, event | category | flops | bytes accessed | tf_op | source)
XLA Modules:
  0.0 185.6 jit_solution(5207312228986653269)
XLA Ops:
  2.0 2.5 %collective-permute-start.22 = (bf16[64,768]{1,0:T(8,128)(2,1)}, bf16[64,768]{1,0:T(8,128)(2,1)}, u32[]{:S(2)}, u32[]{:S(2)}) collective-permute-start(bf16[64,768]{1,0:T(8,128)(2,1)} %get-tuple-element.33), channel_id=1, source_target_pairs={{0,8},{4,12},{8,0},{12,4},{16,24},{20,28},{24,16},{28,20},{1,9},{5... | collective-permute-start | bytes 294920 | tf_op jit(solution)/shard_map/ppermute | solution.py:20
  12.7 2.0 %add_multiply_fusion = f32[768,768]{1,0:T(8,128)} fusion(bf16[768,768]{1,0:T(8,128)(2,1)S(1)} %copy-done.1, s32[768]{0:T(1024)S(1)} %convert_reduce_fusion.2), kind=kLoop, calls=%fused_computation.7 | loop fusion | flops 4128768 | bytes 3542016 | tf_op jit(solution)/shard_map/mul | solution.py:85
  14.7 2.0 %copy.9 = f32[768,768]{0,1:T(8,128)S(1)} copy(f32[768,768]{1,0:T(8,128)} %add_multiply_fusion) | data formatting | bytes 4718592 | tf_op jit(solution)/shard_map/mul | solution.py:85
  16.7 2.0 %fusion = bf16[768,768]{1,0:T(8,128)(2,1)S(1)} fusion(f32[768,768]{0,1:T(8,128)S(1)} %copy.9, s32[768]{0:T(1024)S(1)} %convert_reduce_fusion.2, bf16[768,768]{1,0:T(8,128)(2,1)} %param.7), kind=kLoop, calls=%fused_computation.2 | loop fusion | flops 5308416 | bytes 4721664 | tf_op jit(solution)/shard_map/convert_element_type | solution.py:86
  25.3 2.6 %fusion.1 = (bf16[768,768]{1,0:T(8,128)(2,1)S(1)}, bf16[768,768]{1,0:T(8,128)(2,1)S(1)}) fusion(f32[768]{0:T(1024)S(1)} %get-tuple-element.79, f32[768]{0:T(1024)S(1)} %get-tuple-element.78, f32[768]{0:T(1024)S(1)} %get-tuple-element.77, f32[768]{0:T(1024)S(1)} %get-tuple-element.80, pred[768]{0:T(1024)(128)(4,1)S(1)} %get-tuple-element.82, ...), kind=kLoop, calls=%fused_computation.8 | loop fusion | flops 5898240 | bytes 4747776 | tf_op jit(solution)/shard_map/jit(_where)/select_n | solution.py:95
  28.0 2.1 %collective-permute-start.3 = (s32[4,4]{1,0:T(4,128)S(1)}, s32[4,4]{1,0:T(4,128)S(1)}, u32[]{:S(2)}, u32[]{:S(2)}) collective-permute-start(s32[4,4]{1,0:T(4,128)S(1)} %copy-done.12), channel_id=1, source_target_pairs={{0,8},{4,12},{8,0},{12,4},{16,24},{20,28},{24,16},{28,20},{1,9},{5... | collective-permute-start | bytes 200 | tf_op jit(solution)/shard_map/ppermute | solution.py:20
  31.1 9.2 %collective-permute-done.3 = s32[4,4]{1,0:T(4,128)S(1)} collective-permute-done((s32[4,4]{1,0:T(4,128)S(1)}, s32[4,4]{1,0:T(4,128)S(1)}, u32[]{:S(2)}, u32[]{:S(2)}) %collective-permute-start.3) | collective-permute-done | bytes 96 | tf_op jit(solution)/shard_map/ppermute | solution.py:20
  43.6 4.1 %fusion.2 = (bf16[768,768]{1,0:T(8,128)(2,1)S(1)}, bf16[768,768]{1,0:T(8,128)(2,1)S(1)}) fusion(bf16[832,768]{1,0:T(8,128)(2,1)} %collective-permute-done, f32[768]{0:T(1024)S(1)} %get-tuple-element.10, f32[768]{0:T(1024)S(1)} %get-tuple-element.11, f32[768]{0:T(1024)S(1)} %get-tuple-element.12, f32[768]{0:T(1024)S(1)} %get-tuple-element.9, ...), kind=kLoop, calls=%fused_computation.9 | loop fusion | flops 5898240 | bytes 4745472 | tf_op jit(solution)/shard_map/jit(_where)/select_n | solution.py:99
  56.2 1.8 collective-permute-start.5
  63.2 1.8 collective-permute-start.10
  65.4 3.6 %collective-permute-start.8 = (bf16[3,512,128]{2,1,0:T(8,128)(2,1)S(1)}, bf16[3,512,128]{2,1,0:T(8,128)(2,1)S(1)}, u32[]{:S(2)}, u32[]{:S(2)}) collective-permute-start(bf16[3,512,128]{2,1,0:T(8,128)(2,1)S(1)} %slice.138), channel_id=1, source_target_pairs={{0,3},{1,0},{2,1},{3,2},{4,7},{5,4},{6,5},{7,6},{8,11},{9,8},{10,9... | collective-permute-start | bytes 1179656 | tf_op jit(solution)/shard_map/ppermute | solution.py:39
  75.0 2.0 %collective-permute-done.28 = bf16[64,768]{1,0:T(8,128)(2,1)S(1)} collective-permute-done((bf16[64,768]{1,0:T(8,128)(2,1)S(1)}, bf16[64,768]{1,0:T(8,128)(2,1)S(1)}, u32[]{:S(2)}, u32[]{:S(2)}) %collective-permute-start.28) | collective-permute-done | bytes 98336 | tf_op jit(solution)/shard_map/ppermute | solution.py:20
  79.6 2.0 %collective-permute-done.12 = bf16[64,768]{1,0:T(8,128)(2,1)S(1)} collective-permute-done((bf16[64,768]{1,0:T(8,128)(2,1)S(1)}, bf16[64,768]{1,0:T(8,128)(2,1)S(1)}, u32[]{:S(2)}, u32[]{:S(2)}) %collective-permute-start.12) | collective-permute-done | bytes 98336 | tf_op jit(solution)/shard_map/ppermute | solution.py:20
  84.3 2.0 %collective-permute-done.30 = bf16[64,768]{1,0:T(8,128)(2,1)S(1)} collective-permute-done((bf16[64,768]{1,0:T(8,128)(2,1)S(1)}, bf16[64,768]{1,0:T(8,128)(2,1)S(1)}, u32[]{:S(2)}, u32[]{:S(2)}) %collective-permute-start.30) | collective-permute-done | bytes 98336 | tf_op jit(solution)/shard_map/ppermute | solution.py:20
  88.9 2.0 %collective-permute-done.14 = bf16[64,768]{1,0:T(8,128)(2,1)S(1)} collective-permute-done((bf16[64,768]{1,0:T(8,128)(2,1)S(1)}, bf16[64,768]{1,0:T(8,128)(2,1)S(1)}, u32[]{:S(2)}, u32[]{:S(2)}) %collective-permute-start.14) | collective-permute-done | bytes 98336 | tf_op jit(solution)/shard_map/ppermute | solution.py:20
  93.5 2.0 %collective-permute-done.32 = bf16[64,768]{1,0:T(8,128)(2,1)S(1)} collective-permute-done((bf16[64,768]{1,0:T(8,128)(2,1)S(1)}, bf16[64,768]{1,0:T(8,128)(2,1)S(1)}, u32[]{:S(2)}, u32[]{:S(2)}) %collective-permute-start.32) | collective-permute-done | bytes 98336 | tf_op jit(solution)/shard_map/ppermute | solution.py:20
  98.1 2.0 %collective-permute-done.16 = bf16[64,768]{1,0:T(8,128)(2,1)S(1)} collective-permute-done((bf16[64,768]{1,0:T(8,128)(2,1)S(1)}, bf16[64,768]{1,0:T(8,128)(2,1)S(1)}, u32[]{:S(2)}, u32[]{:S(2)}) %collective-permute-start.16) | collective-permute-done | bytes 98336 | tf_op jit(solution)/shard_map/ppermute | solution.py:20
  102.7 2.0 %collective-permute-done.34 = bf16[64,768]{1,0:T(8,128)(2,1)S(1)} collective-permute-done((bf16[64,768]{1,0:T(8,128)(2,1)S(1)}, bf16[64,768]{1,0:T(8,128)(2,1)S(1)}, u32[]{:S(2)}, u32[]{:S(2)}) %collective-permute-start.34) | collective-permute-done | bytes 98336 | tf_op jit(solution)/shard_map/ppermute | solution.py:20
  107.3 2.0 %collective-permute-done.18 = bf16[64,768]{1,0:T(8,128)(2,1)S(1)} collective-permute-done((bf16[64,768]{1,0:T(8,128)(2,1)S(1)}, bf16[64,768]{1,0:T(8,128)(2,1)S(1)}, u32[]{:S(2)}, u32[]{:S(2)}) %collective-permute-start.18) | collective-permute-done | bytes 98336 | tf_op jit(solution)/shard_map/ppermute | solution.py:20
  112.0 2.0 %collective-permute-done.36 = bf16[64,768]{1,0:T(8,128)(2,1)S(1)} collective-permute-done((bf16[64,768]{1,0:T(8,128)(2,1)S(1)}, bf16[64,768]{1,0:T(8,128)(2,1)S(1)}, u32[]{:S(2)}, u32[]{:S(2)}) %collective-permute-start.36) | collective-permute-done | bytes 98336 | tf_op jit(solution)/shard_map/ppermute | solution.py:20
  115.3 3.3 %collective-permute-done.20 = bf16[64,768]{1,0:T(8,128)(2,1)S(1)} collective-permute-done((bf16[64,768]{1,0:T(8,128)(2,1)S(1)}, bf16[64,768]{1,0:T(8,128)(2,1)S(1)}, u32[]{:S(2)}, u32[]{:S(2)}) %collective-permute-start.20) | collective-permute-done | bytes 98336 | tf_op jit(solution)/shard_map/ppermute | solution.py:20
  121.3 2.9 %collective-permute-start.39 = (bf16[128,768]{1,0:T(8,128)(2,1)S(1)}, bf16[128,768]{1,0:T(8,128)(2,1)S(1)}, u32[]{:S(2)}, u32[]{:S(2)}) collective-permute-start(bf16[128,768]{1,0:T(8,128)(2,1)S(1)} %pad_maximum_fusion.7), channel_id=1, source_target_pairs={{0,3},{1,0},{2,1},{3,2},{4,7},{5,4},{6,5},{7,6},{8,11},{9,8},{10,9... | collective-permute-start | bytes 589832 | tf_op jit(solution)/shard_map/ppermute | solution.py:29
  126.7 2.9 %collective-permute-done.39 = bf16[128,768]{1,0:T(8,128)(2,1)S(1)} collective-permute-done((bf16[128,768]{1,0:T(8,128)(2,1)S(1)}, bf16[128,768]{1,0:T(8,128)(2,1)S(1)}, u32[]{:S(2)}, u32[]{:S(2)}) %collective-permute-start.39) | collective-permute-done | bytes 196640 | tf_op jit(solution)/shard_map/ppermute | solution.py:29
  129.6 13.8 %collective-permute-done.38 = bf16[128,768]{1,0:T(8,128)(2,1)} collective-permute-done((bf16[128,768]{1,0:T(8,128)(2,1)S(1)}, bf16[128,768]{1,0:T(8,128)(2,1)}, u32[]{:S(2)}, u32[]{:S(2)}) %collective-permute-start.38) | collective-permute-done | bytes 196640 | tf_op jit(solution)/shard_map/ppermute | solution.py:29
  148.3 3.0 %collective-permute-done.41 = f32[512]{0:T(512)S(1)} collective-permute-done((f32[512]{0:T(512)S(1)}, f32[512]{0:T(512)S(1)}, u32[]{:S(2)}, u32[]{:S(2)}) %collective-permute-start.41) | collective-permute-done | bytes 2080 | tf_op jit(solution)/shard_map/ppermute | solution.py:20
  152.9 2.1 %collective-permute-done.42 = f32[512]{0:T(512)S(1)} collective-permute-done((f32[512]{0:T(512)S(1)}, f32[512]{0:T(512)S(1)}, u32[]{:S(2)}, u32[]{:S(2)}) %collective-permute-start.42) | collective-permute-done | bytes 2080 | tf_op jit(solution)/shard_map/ppermute | solution.py:20
  158.3 3.0 %collective-permute-done.44 = f32[512]{0:T(512)S(1)} collective-permute-done((f32[512]{0:T(512)S(1)}, f32[512]{0:T(512)S(1)}, u32[]{:S(2)}, u32[]{:S(2)}) %collective-permute-start.44) | collective-permute-done | bytes 2080 | tf_op jit(solution)/shard_map/ppermute | solution.py:20
  162.9 2.1 %collective-permute-done.45 = f32[512]{0:T(512)S(1)} collective-permute-done((f32[512]{0:T(512)S(1)}, f32[512]{0:T(512)S(1)}, u32[]{:S(2)}, u32[]{:S(2)}) %collective-permute-start.45) | collective-permute-done | bytes 2080 | tf_op jit(solution)/shard_map/ppermute | solution.py:20
  168.3 3.0 %collective-permute-done.47 = f32[512]{0:T(512)S(1)} collective-permute-done((f32[512]{0:T(512)S(1)}, f32[512]{0:T(512)S(1)}, u32[]{:S(2)}, u32[]{:S(2)}) %collective-permute-start.47) | collective-permute-done | bytes 2080 | tf_op jit(solution)/shard_map/ppermute | solution.py:20
  172.9 2.1 %collective-permute-done.48 = f32[512]{0:T(512)S(1)} collective-permute-done((f32[512]{0:T(512)S(1)}, f32[512]{0:T(512)S(1)}, u32[]{:S(2)}, u32[]{:S(2)}) %collective-permute-start.48) | collective-permute-done | bytes 2080 | tf_op jit(solution)/shard_map/ppermute | solution.py:20
  178.1 3.0 %collective-permute-done.50 = f32[128]{0:T(128)S(1)} collective-permute-done((f32[128]{0:T(128)S(1)}, f32[128]{0:T(128)S(1)}, u32[]{:S(2)}, u32[]{:S(2)}) %collective-permute-start.50) | collective-permute-done | bytes 544 | tf_op jit(solution)/shard_map/ppermute | solution.py:20
  182.7 2.0 %collective-permute-done.51 = f32[128]{0:T(128)S(1)} collective-permute-done((f32[128]{0:T(128)S(1)}, f32[128]{0:T(128)S(1)}, u32[]{:S(2)}, u32[]{:S(2)}) %collective-permute-start.51) | collective-permute-done | bytes 544 | tf_op jit(solution)/shard_map/ppermute | solution.py:20
  (247 shorter events, 90.0 us)
Async XLA Ops:
  1.6 40.6 %collective-permute-start.21 = (bf16[64,768]{1,0:T(8,128)(2,1)}, bf16[64,768]{1,0:T(8,128)(2,1)}, u32[]{:S(2)}, u32[]{:S(2)}) collective-permute-start(bf16[64,768]{1,0:T(8,128)(2,1)} %get-tuple-element.33), channel_id=1, source_target_pairs={{0,4},{4,0},{8,12},{12,8},{16,20},{20,16},{24,28},{28,24},{1,5},{5... | collective-permute-start | bytes 294920 | tf_op jit(solution)/shard_map/ppermute | solution.py:20
  2.0 38.7 %collective-permute-start.22 = (bf16[64,768]{1,0:T(8,128)(2,1)}, bf16[64,768]{1,0:T(8,128)(2,1)}, u32[]{:S(2)}, u32[]{:S(2)}) collective-permute-start(bf16[64,768]{1,0:T(8,128)(2,1)} %get-tuple-element.33), channel_id=1, source_target_pairs={{0,8},{4,12},{8,0},{12,4},{16,24},{20,28},{24,16},{28,20},{1,9},{5... | collective-permute-start | bytes 294920 | tf_op jit(solution)/shard_map/ppermute | solution.py:20
  5.8 22.2 %collective-permute-start.1 = (s32[4,4]{1,0:T(4,128)}, s32[4,4]{1,0:T(4,128)}, u32[]{:S(2)}, u32[]{:S(2)}) collective-permute-start(s32[4,4]{1,0:T(4,128)} %get-tuple-element.36), channel_id=1, source_target_pairs={{0,4},{4,0},{8,12},{12,8},{16,20},{20,16},{24,28},{28,24},{1,5},{5... | collective-permute-start | bytes 200 | tf_op jit(solution)/shard_map/ppermute | solution.py:20
  9.5 34.0 %collective-permute-start = (bf16[832,768]{1,0:T(8,128)(2,1)}, bf16[832,768]{1,0:T(8,128)(2,1)}, u32[]{:S(2)}, u32[]{:S(2)}) collective-permute-start(bf16[832,768]{1,0:T(8,128)(2,1)} %get-tuple-element.34), channel_id=1, source_target_pairs={{0,4},{4,0},{8,12},{12,8},{16,20},{20,16},{24,28},{28,24},{1,5},{5... | collective-permute-start | bytes 3833864 | tf_op jit(solution)/shard_map/ppermute | solution.py:20
  9.8 33.8 %collective-permute-start.2 = (bf16[832,768]{1,0:T(8,128)(2,1)}, bf16[832,768]{1,0:T(8,128)(2,1)}, u32[]{:S(2)}, u32[]{:S(2)}) collective-permute-start(bf16[832,768]{1,0:T(8,128)(2,1)} %get-tuple-element.35), channel_id=1, source_target_pairs={{0,8},{4,12},{8,0},{12,4},{16,24},{20,28},{24,16},{28,20},{1,9},{5... | collective-permute-start | bytes 3833864 | tf_op jit(solution)/shard_map/ppermute | solution.py:20
  28.0 12.3 %collective-permute-start.3 = (s32[4,4]{1,0:T(4,128)S(1)}, s32[4,4]{1,0:T(4,128)S(1)}, u32[]{:S(2)}, u32[]{:S(2)}) collective-permute-start(s32[4,4]{1,0:T(4,128)S(1)} %copy-done.12), channel_id=1, source_target_pairs={{0,8},{4,12},{8,0},{12,4},{16,24},{20,28},{24,16},{28,20},{1,9},{5... | collective-permute-start | bytes 200 | tf_op jit(solution)/shard_map/ppermute | solution.py:20
  50.2 8.4 %collective-permute-start.24 = (bf16[64,768]{1,0:T(8,128)(2,1)S(1)}, bf16[64,768]{1,0:T(8,128)(2,1)S(1)}, u32[]{:S(2)}, u32[]{:S(2)}) collective-permute-start(bf16[64,768]{1,0:T(8,128)(2,1)S(1)} %get-tuple-element.49), channel_id=1, source_target_pairs={{0,8},{4,12},{8,0},{12,4},{16,24},{20,28},{24,16},{28,20},{1,9},{5... | collective-permute-start | bytes 294920 | tf_op jit(solution)/shard_map/ppermute | solution.py:20
  50.6 8.9 %collective-permute-start.23 = (bf16[64,768]{1,0:T(8,128)(2,1)S(1)}, bf16[64,768]{1,0:T(8,128)(2,1)S(1)}, u32[]{:S(2)}, u32[]{:S(2)}) collective-permute-start(bf16[64,768]{1,0:T(8,128)(2,1)S(1)} %get-tuple-element.49), channel_id=1, source_target_pairs={{0,4},{4,0},{8,12},{12,8},{16,20},{20,16},{24,28},{28,24},{1,5},{5... | collective-permute-start | bytes 294920 | tf_op jit(solution)/shard_map/ppermute | solution.py:20
  56.2 5.3 %collective-permute-start.5 = (bf16[64,768]{1,0:T(8,128)(2,1)S(1)}, bf16[64,768]{1,0:T(8,128)(2,1)S(1)}, u32[]{:S(2)}, u32[]{:S(2)}) collective-permute-start(bf16[64,768]{1,0:T(8,128)(2,1)S(1)} %get-tuple-element.63), channel_id=1, source_target_pairs={{0,8},{4,12},{8,0},{12,4},{16,24},{20,28},{24,16},{28,20},{1,9},{5... | collective-permute-start | bytes 294920 | tf_op jit(solution)/shard_map/ppermute | solution.py:20
  60.3 8.7 %collective-permute-start.26 = (bf16[64,768]{1,0:T(8,128)(2,1)S(1)}, bf16[64,768]{1,0:T(8,128)(2,1)S(1)}, u32[]{:S(2)}, u32[]{:S(2)}) collective-permute-start(bf16[64,768]{1,0:T(8,128)(2,1)S(1)} %get-tuple-element.51), channel_id=1, source_target_pairs={{0,8},{4,12},{8,0},{12,4},{16,24},{20,28},{24,16},{28,20},{1,9},{5... | collective-permute-start | bytes 294920 | tf_op jit(solution)/shard_map/ppermute | solution.py:20
  60.7 9.1 %collective-permute-start.25 = (bf16[64,768]{1,0:T(8,128)(2,1)S(1)}, bf16[64,768]{1,0:T(8,128)(2,1)S(1)}, u32[]{:S(2)}, u32[]{:S(2)}) collective-permute-start(bf16[64,768]{1,0:T(8,128)(2,1)S(1)} %get-tuple-element.51), channel_id=1, source_target_pairs={{0,4},{4,0},{8,12},{12,8},{16,20},{20,16},{24,28},{28,24},{1,5},{5... | collective-permute-start | bytes 294920 | tf_op jit(solution)/shard_map/ppermute | solution.py:20
  63.2 9.1 %collective-permute-start.10 = (bf16[64,768]{1,0:T(8,128)(2,1)S(1)}, bf16[64,768]{1,0:T(8,128)(2,1)S(1)}, u32[]{:S(2)}, u32[]{:S(2)}) collective-permute-start(bf16[64,768]{1,0:T(8,128)(2,1)S(1)} %convert_element_type.112), channel_id=1, source_target_pairs={{0,8},{4,12},{8,0},{12,4},{16,24},{20,28},{24,16},{28,20},{1,9},{5... | collective-permute-start | bytes 294920 | tf_op jit(solution)/shard_map/ppermute | solution.py:20
  65.0 8.7 %collective-permute-start.9 = (bf16[64,768]{1,0:T(8,128)(2,1)S(1)}, bf16[64,768]{1,0:T(8,128)(2,1)S(1)}, u32[]{:S(2)}, u32[]{:S(2)}) collective-permute-start(bf16[64,768]{1,0:T(8,128)(2,1)S(1)} %convert_element_type.112), channel_id=1, source_target_pairs={{0,4},{4,0},{8,12},{12,8},{16,20},{20,16},{24,28},{28,24},{1,5},{5... | collective-permute-start | bytes 294920 | tf_op jit(solution)/shard_map/ppermute | solution.py:20
  65.4 60.0 %collective-permute-start.8 = (bf16[3,512,128]{2,1,0:T(8,128)(2,1)S(1)}, bf16[3,512,128]{2,1,0:T(8,128)(2,1)S(1)}, u32[]{:S(2)}, u32[]{:S(2)}) collective-permute-start(bf16[3,512,128]{2,1,0:T(8,128)(2,1)S(1)} %slice.138), channel_id=1, source_target_pairs={{0,3},{1,0},{2,1},{3,2},{4,7},{5,4},{6,5},{7,6},{8,11},{9,8},{10,9... | collective-permute-start | bytes 1179656 | tf_op jit(solution)/shard_map/ppermute | solution.py:39
  69.0 56.5 %collective-permute-start.7 = (bf16[3,512,128]{2,1,0:T(8,128)(2,1)S(1)}, bf16[3,512,128]{2,1,0:T(8,128)(2,1)S(1)}, u32[]{:S(2)}, u32[]{:S(2)}) collective-permute-start(bf16[3,512,128]{2,1,0:T(8,128)(2,1)S(1)} %slice.138), channel_id=1, source_target_pairs={{0,2},{1,3},{2,0},{3,1},{4,6},{5,7},{6,4},{7,5},{8,10},{9,11},{10,... | collective-permute-start | bytes 1179656 | tf_op jit(solution)/shard_map/ppermute | solution.py:39
  69.9 55.6 %collective-permute-start.6 = (bf16[3,512,128]{2,1,0:T(8,128)(2,1)S(1)}, bf16[3,512,128]{2,1,0:T(8,128)(2,1)}, u32[]{:S(2)}, u32[]{:S(2)}) collective-permute-start(bf16[3,512,128]{2,1,0:T(8,128)(2,1)S(1)} %slice.138), channel_id=1, source_target_pairs={{0,1},{1,2},{2,3},{3,0},{4,5},{5,6},{6,7},{7,4},{8,9},{9,10},{10,1... | collective-permute-start | bytes 1179656 | tf_op jit(solution)/shard_map/ppermute | solution.py:39
  72.3 4.7 %collective-permute-start.28 = (bf16[64,768]{1,0:T(8,128)(2,1)S(1)}, bf16[64,768]{1,0:T(8,128)(2,1)S(1)}, u32[]{:S(2)}, u32[]{:S(2)}) collective-permute-start(bf16[64,768]{1,0:T(8,128)(2,1)S(1)} %get-tuple-element.53), channel_id=1, source_target_pairs={{0,8},{4,12},{8,0},{12,4},{16,24},{20,28},{24,16},{28,20},{1,9},{5... | collective-permute-start | bytes 294920 | tf_op jit(solution)/shard_map/ppermute | solution.py:20
  73.8 4.6 %collective-permute-start.27 = (bf16[64,768]{1,0:T(8,128)(2,1)S(1)}, bf16[64,768]{1,0:T(8,128)(2,1)S(1)}, u32[]{:S(2)}, u32[]{:S(2)}) collective-permute-start(bf16[64,768]{1,0:T(8,128)(2,1)S(1)} %get-tuple-element.53), channel_id=1, source_target_pairs={{0,4},{4,0},{8,12},{12,8},{16,20},{20,16},{24,28},{28,24},{1,5},{5... | collective-permute-start | bytes 294920 | tf_op jit(solution)/shard_map/ppermute | solution.py:20
  77.0 4.6 %collective-permute-start.12 = (bf16[64,768]{1,0:T(8,128)(2,1)S(1)}, bf16[64,768]{1,0:T(8,128)(2,1)S(1)}, u32[]{:S(2)}, u32[]{:S(2)}) collective-permute-start(bf16[64,768]{1,0:T(8,128)(2,1)S(1)} %get-tuple-element.65), channel_id=1, source_target_pairs={{0,8},{4,12},{8,0},{12,4},{16,24},{20,28},{24,16},{28,20},{1,9},{5... | collective-permute-start | bytes 294920 | tf_op jit(solution)/shard_map/ppermute | solution.py:20
  81.6 4.6 %collective-permute-start.30 = (bf16[64,768]{1,0:T(8,128)(2,1)S(1)}, bf16[64,768]{1,0:T(8,128)(2,1)S(1)}, u32[]{:S(2)}, u32[]{:S(2)}) collective-permute-start(bf16[64,768]{1,0:T(8,128)(2,1)S(1)} %get-tuple-element.55), channel_id=1, source_target_pairs={{0,8},{4,12},{8,0},{12,4},{16,24},{20,28},{24,16},{28,20},{1,9},{5... | collective-permute-start | bytes 294920 | tf_op jit(solution)/shard_map/ppermute | solution.py:20
  86.2 4.6 %collective-permute-start.14 = (bf16[64,768]{1,0:T(8,128)(2,1)S(1)}, bf16[64,768]{1,0:T(8,128)(2,1)S(1)}, u32[]{:S(2)}, u32[]{:S(2)}) collective-permute-start(bf16[64,768]{1,0:T(8,128)(2,1)S(1)} %get-tuple-element.67), channel_id=1, source_target_pairs={{0,8},{4,12},{8,0},{12,4},{16,24},{20,28},{24,16},{28,20},{1,9},{5... | collective-permute-start | bytes 294920 | tf_op jit(solution)/shard_map/ppermute | solution.py:20
  90.8 4.6 %collective-permute-start.32 = (bf16[64,768]{1,0:T(8,128)(2,1)S(1)}, bf16[64,768]{1,0:T(8,128)(2,1)S(1)}, u32[]{:S(2)}, u32[]{:S(2)}) collective-permute-start(bf16[64,768]{1,0:T(8,128)(2,1)S(1)} %get-tuple-element.57), channel_id=1, source_target_pairs={{0,8},{4,12},{8,0},{12,4},{16,24},{20,28},{24,16},{28,20},{1,9},{5... | collective-permute-start | bytes 294920 | tf_op jit(solution)/shard_map/ppermute | solution.py:20
  92.2 4.6 %collective-permute-start.31 = (bf16[64,768]{1,0:T(8,128)(2,1)S(1)}, bf16[64,768]{1,0:T(8,128)(2,1)S(1)}, u32[]{:S(2)}, u32[]{:S(2)}) collective-permute-start(bf16[64,768]{1,0:T(8,128)(2,1)S(1)} %get-tuple-element.57), channel_id=1, source_target_pairs={{0,4},{4,0},{8,12},{12,8},{16,20},{20,16},{24,28},{28,24},{1,5},{5... | collective-permute-start | bytes 294920 | tf_op jit(solution)/shard_map/ppermute | solution.py:20
  95.5 4.6 %collective-permute-start.16 = (bf16[64,768]{1,0:T(8,128)(2,1)S(1)}, bf16[64,768]{1,0:T(8,128)(2,1)S(1)}, u32[]{:S(2)}, u32[]{:S(2)}) collective-permute-start(bf16[64,768]{1,0:T(8,128)(2,1)S(1)} %get-tuple-element.69), channel_id=1, source_target_pairs={{0,8},{4,12},{8,0},{12,4},{16,24},{20,28},{24,16},{28,20},{1,9},{5... | collective-permute-start | bytes 294920 | tf_op jit(solution)/shard_map/ppermute | solution.py:20
  100.1 4.6 %collective-permute-start.34 = (bf16[64,768]{1,0:T(8,128)(2,1)S(1)}, bf16[64,768]{1,0:T(8,128)(2,1)S(1)}, u32[]{:S(2)}, u32[]{:S(2)}) collective-permute-start(bf16[64,768]{1,0:T(8,128)(2,1)S(1)} %get-tuple-element.59), channel_id=1, source_target_pairs={{0,8},{4,12},{8,0},{12,4},{16,24},{20,28},{24,16},{28,20},{1,9},{5... | collective-permute-start | bytes 294920 | tf_op jit(solution)/shard_map/ppermute | solution.py:20
  104.7 4.6 %collective-permute-start.18 = (bf16[64,768]{1,0:T(8,128)(2,1)S(1)}, bf16[64,768]{1,0:T(8,128)(2,1)S(1)}, u32[]{:S(2)}, u32[]{:S(2)}) collective-permute-start(bf16[64,768]{1,0:T(8,128)(2,1)S(1)} %get-tuple-element.71), channel_id=1, source_target_pairs={{0,8},{4,12},{8,0},{12,4},{16,24},{20,28},{24,16},{28,20},{1,9},{5... | collective-permute-start | bytes 294920 | tf_op jit(solution)/shard_map/ppermute | solution.py:20
  109.3 4.6 %collective-permute-start.36 = (bf16[64,768]{1,0:T(8,128)(2,1)S(1)}, bf16[64,768]{1,0:T(8,128)(2,1)S(1)}, u32[]{:S(2)}, u32[]{:S(2)}) collective-permute-start(bf16[64,768]{1,0:T(8,128)(2,1)S(1)} %get-tuple-element.61), channel_id=1, source_target_pairs={{0,8},{4,12},{8,0},{12,4},{16,24},{20,28},{24,16},{28,20},{1,9},{5... | collective-permute-start | bytes 294920 | tf_op jit(solution)/shard_map/ppermute | solution.py:20
  110.7 8.2 %collective-permute-start.35 = (bf16[64,768]{1,0:T(8,128)(2,1)S(1)}, bf16[64,768]{1,0:T(8,128)(2,1)S(1)}, u32[]{:S(2)}, u32[]{:S(2)}) collective-permute-start(bf16[64,768]{1,0:T(8,128)(2,1)S(1)} %get-tuple-element.61), channel_id=1, source_target_pairs={{0,4},{4,0},{8,12},{12,8},{16,20},{20,16},{24,28},{28,24},{1,5},{5... | collective-permute-start | bytes 294920 | tf_op jit(solution)/shard_map/ppermute | solution.py:20
  113.9 4.6 %collective-permute-start.20 = (bf16[64,768]{1,0:T(8,128)(2,1)S(1)}, bf16[64,768]{1,0:T(8,128)(2,1)S(1)}, u32[]{:S(2)}, u32[]{:S(2)}) collective-permute-start(bf16[64,768]{1,0:T(8,128)(2,1)S(1)} %get-tuple-element.73), channel_id=1, source_target_pairs={{0,8},{4,12},{8,0},{12,4},{16,24},{20,28},{24,16},{28,20},{1,9},{5... | collective-permute-start | bytes 294920 | tf_op jit(solution)/shard_map/ppermute | solution.py:20
  121.3 8.2 %collective-permute-start.39 = (bf16[128,768]{1,0:T(8,128)(2,1)S(1)}, bf16[128,768]{1,0:T(8,128)(2,1)S(1)}, u32[]{:S(2)}, u32[]{:S(2)}) collective-permute-start(bf16[128,768]{1,0:T(8,128)(2,1)S(1)} %pad_maximum_fusion.7), channel_id=1, source_target_pairs={{0,3},{1,0},{2,1},{3,2},{4,7},{5,4},{6,5},{7,6},{8,11},{9,8},{10,9... | collective-permute-start | bytes 589832 | tf_op jit(solution)/shard_map/ppermute | solution.py:29
  124.2 19.1 %collective-permute-start.38 = (bf16[128,768]{1,0:T(8,128)(2,1)S(1)}, bf16[128,768]{1,0:T(8,128)(2,1)}, u32[]{:S(2)}, u32[]{:S(2)}) collective-permute-start(bf16[128,768]{1,0:T(8,128)(2,1)S(1)} %pad_maximum_fusion.7), channel_id=1, source_target_pairs={{0,2},{1,3},{2,0},{3,1},{4,6},{5,7},{6,4},{7,5},{8,10},{9,11},{10,... | collective-permute-start | bytes 589832 | tf_op jit(solution)/shard_map/ppermute | solution.py:29
  125.3 18.0 %collective-permute-start.37 = (bf16[128,768]{1,0:T(8,128)(2,1)S(1)}, bf16[128,768]{1,0:T(8,128)(2,1)}, u32[]{:S(2)}, u32[]{:S(2)}) collective-permute-start(bf16[128,768]{1,0:T(8,128)(2,1)S(1)} %pad_maximum_fusion.7), channel_id=1, source_target_pairs={{0,1},{1,2},{2,3},{3,0},{4,5},{5,6},{6,7},{7,4},{8,9},{9,10},{10,1... | collective-permute-start | bytes 589832 | tf_op jit(solution)/shard_map/ppermute | solution.py:29
  (34 other events, 117.1 us)

commit v7 on v4

--- a/solution.py
+++ b/solution.py
@@ -58,12 +58,10 @@
 def pattern_mask(pattern, row_atoms, col_atoms):
     levels = jnp.arange(pattern.shape[0], dtype=jnp.int32)
     row_onehot = (row_atoms[:, None] == levels[None, :]).astype(jnp.bfloat16)
-    col_onehot = (col_atoms[:, None] == levels[None, :]).astype(jnp.bfloat16)
     per_row = jnp.dot(row_onehot, pattern.astype(jnp.bfloat16), preferred_element_type=jnp.float32)
-    mask = lax.dot_general(
-        per_row.astype(jnp.bfloat16), col_onehot, (((1,), (1,)), ((), ())),
-        preferred_element_type=jnp.float32,
-    )
+    mask = jnp.broadcast_to(per_row[:, :1], (row_atoms.shape[0], col_atoms.shape[0]))
+    for atom in range(1, pattern.shape[1]):
+        mask = jnp.where((col_atoms == atom)[None, :], per_row[:, atom : atom + 1], mask)
     return mask > 0.5
 
 
@@ -71,8 +69,6 @@
     orb_dev = diag_block.shape[1]
     atoms_dev = pair_pattern.shape[2]
     atoms_here = lax.axis_index("atoms")
-    shipped = [swapped(pair_block[r], "atoms", r) for r in range(ROUNDS)]
-    shipped_pattern = [swapped(pair_pattern[r], "atoms", r) for r in range(ROUNDS)]
     own_atoms = atom_index(
         lax.dynamic_index_in_dim(atom_sizes, atoms_here, 0, keepdims=False), orb_dev
     )
@@ -90,10 +86,7 @@
         own_mask = pattern_mask(pair_pattern[round_index], own_atoms, other_atoms)
         own_pair = jnp.where(own_mask, pair_block[round_index], jnp.zeros((), jnp.bfloat16))
         own_pair_t.append(own_pair)
-        other_mask = pattern_mask(shipped_pattern[round_index], other_atoms, own_atoms)
-        other_pair.append(
-            jnp.where(other_mask, shipped[round_index], jnp.zeros((), jnp.bfloat16))
-        )
+        other_pair.append(swapped(own_pair, "atoms", round_index))
 
     def apply_operator(values):
         result = jnp.dot(values, diag_sym, preferred_element_type=jnp.float32)

time: 179 us -> 184 us (1.028)
  starting transfers between devices: 47.8 us -> 40 us
  matrix products: 57.9 us -> 65 us
  waiting for transfers between devices: 50.5 us -> 55.4 us
  other arithmetic: 8.44 us -> 13.2 us
  local copies, waits for them, and re-layouts: 12.5 us -> 9.06 us
    dot_general x32, matrix products: 15.6 us -> 33 us  [apply_operator(): jnp.dot(other_rows, other_pair[round_index], preferred_element_type=jnp.f...]
    ppermute x48 -> x46, starting transfers between devices: 38.7 us -> 30.9 us  [swapped(): return lax.ppermute(value, axis, pairs)]
    dot_general x4 -> x2, matrix products: 8.21 us -> 0.61 us  [pattern_mask(): jnp.dot(row_onehot, pattern.astype(jnp.bfloat16), preferred_element_type=...]
    ppermute x48 -> x46, waiting for transfers between devices: 34.3 us -> 39.1 us  [swapped(): return lax.ppermute(value, axis, pairs)]
    select_n x0 -> x1, other arithmetic: none -> 4.14 us  [body(): jnp.where(own_mask, pair_block[round_index], jnp.zeros((), jnp.bfloat16))]
    squeeze x2 -> x0, local copies, waits for them, and re-layouts: 3.81 us -> none  [the longest x1 3.22 us: body(): pair_block[round_index]]
    dot_general x32, matrix products: 22.4 us -> 19.7 us  [apply_operator(): lax.dot_general(other_rows, own_pair_t[round_index], (((1,), (1,)), ((),...]
  transfers between devices with their start and end apart: 54 -> 52, of which waited for: 25 -> 24; matrix products, arithmetic and copies ran while one was open for 36% -> 42% of each run, Pallas kernels for 0% -> 0%
where the time goes in v7:
time: 184 us; the launch traced here: 183 us
  matrix products  65 us (35%)
  waiting for transfers between devices  55.4 us (30%)
  starting transfers between devices  40 us (22%)
  other arithmetic  13.2 us (7%)
  local copies, waits for them, and re-layouts  9.06 us (5%)
    ppermute x46, waiting for transfers between devices, swapped(): return lax.ppermute(value, axis, pairs)  39.1 us
    dot_general x32, matrix products, apply_operator(): jnp.dot(other_rows, other_pair[round_index], preferred_element_type=jnp.f...  33 us
    ppermute x46, starting transfers between devices, swapped(): return lax.ppermute(value, axis, pairs)  30.9 us
    dot_general x32, matrix products, apply_operator(): lax.dot_general(other_rows, own_pair_t[round_index], (((1,), (1,)), ((),...  19.7 us
    ppermute x3, waiting for transfers between devices, gather_bands(): pieces.append(lax.ppermute(value, 'bands', pairs))  16.2 us
    dot_general x16, matrix products, apply_operator(): result = jnp.dot(values, diag_sym, preferred_element_type=jnp.float32)  6.61 us
    ppermute x3, starting transfers between devices, gather_pieces(): pieces.append(lax.ppermute(value, 'bands', pairs))  5.08 us
    select_n x1, other arithmetic, body(): jnp.where(own_mask, pair_block[round_index], jnp.zeros((), jnp.bfloat16))  4.14 us
  transfers between devices with their start and end apart: 52, of which 24 were waited for; matrix products, arithmetic and copies ran while one was open for 42% of the time, Pallas kernels for 0%

profile of v7, /device:TPU:0, one launch (start us, length us, event | category | flops | bytes accessed | tf_op | source)
XLA Modules:
  0.0 183.4 jit_solution(4518085245650794867)
XLA Ops:
  0.0 1.6 fusion.125
  1.6 2.9 %collective-permute-start.22 = (bf16[64,768]{1,0:T(8,128)(2,1)}, bf16[64,768]{1,0:T(8,128)(2,1)}, u32[]{:S(2)}, u32[]{:S(2)}) collective-permute-start(bf16[64,768]{1,0:T(8,128)(2,1)} %get-tuple-element.23), channel_id=1, source_target_pairs={{0,8},{4,12},{8,0},{12,4},{16,24},{20,28},{24,16},{28,20},{1,9},{5... | collective-permute-start | bytes 294920 | tf_op jit(solution)/shard_map/ppermute | solution.py:20
  8.3 4.1 %fusion.1 = (bf16[768,768]{1,0:T(8,128)(2,1)S(1)}, bf16[768,768]{1,0:T(8,128)(2,1)S(1)}) fusion(bf16[2,768,768]{2,1,0:T(8,128)(2,1)} %param.8, f32[768]{0:T(1024)S(1)} %get-tuple-element.60, f32[768]{0:T(1024)S(1)} %get-tuple-element.59, f32[768]{0:T(1024)S(1)} %get-tuple-element.58, f32[768]{0:T(1024)S(1)} %get-tuple-element.61, ...), kind=kLoop, calls=%fused_computation.6 | loop fusion | flops 5898240 | bytes 4747776 | tf_op jit(solution)/shard_map/jit(_where)/select_n | solution.py:87
  12.5 1.8 collective-permute-start.3
  14.3 2.0 %add_multiply_fusion = f32[768,768]{1,0:T(8,128)} fusion(bf16[768,768]{1,0:T(8,128)(2,1)S(1)} %copy-done, s32[768]{0:T(1024)S(1)} %convert_reduce_fusion.2), kind=kLoop, calls=%fused_computation.5 | loop fusion | flops 4128768 | bytes 3542016 | tf_op jit(solution)/shard_map/mul | solution.py:77
  16.3 3.1 %copy.9 = f32[768,768]{0,1:T(8,128)} copy(f32[768,768]{1,0:T(8,128)} %add_multiply_fusion) | data formatting | bytes 4718592 | tf_op jit(solution)/shard_map/mul | solution.py:77
  19.3 2.7 %fusion = bf16[768,768]{1,0:T(8,128)(2,1)S(1)} fusion(f32[768,768]{0,1:T(8,128)} %copy.9, s32[768]{0:T(1024)S(1)} %convert_reduce_fusion.2, bf16[768,768]{1,0:T(8,128)(2,1)} %param.7), kind=kLoop, calls=%fused_computation.2 | loop fusion | flops 5308416 | bytes 4721664 | tf_op jit(solution)/shard_map/convert_element_type | solution.py:78
  24.1 1.8 slice.98
  31.8 9.0 %collective-permute-done.3 = bf16[768,768]{1,0:T(8,128)(2,1)} collective-permute-done((bf16[768,768]{1,0:T(8,128)(2,1)S(1)}, bf16[768,768]{1,0:T(8,128)(2,1)}, u32[]{:S(2)}, u32[]{:S(2)}) %collective-permute-start.3) | collective-permute-done | bytes 1179680 | tf_op jit(solution)/shard_map/ppermute | solution.py:20
  40.8 1.7 fusion.182
  43.7 1.8 collective-permute-start.24
  45.9 1.7 fusion.181
  52.7 1.8 collective-permute-start.26
  54.9 1.6 fusion.140
  58.9 3.8 %collective-permute-start.8 = (bf16[3,512,128]{2,1,0:T(8,128)(2,1)}, bf16[3,512,128]{2,1,0:T(8,128)(2,1)}, u32[]{:S(2)}, u32[]{:S(2)}) collective-permute-start(bf16[3,512,128]{2,1,0:T(8,128)(2,1)} %slice.98), channel_id=1, source_target_pairs={{0,3},{1,0},{2,1},{3,2},{4,7},{5,4},{6,5},{7,6},{8,11},{9,8},{10,9... | collective-permute-start | bytes 1179656 | tf_op jit(solution)/shard_map/ppermute | solution.py:39
  62.7 1.6 fusion.165
  68.8 1.6 fusion.143
  78.1 1.6 fusion.146
  83.0 1.6 fusion.171
  88.2 1.6 fusion.149
  114.2 1.9 %collective-permute-done.20 = bf16[64,768]{1,0:T(8,128)(2,1)S(1)} collective-permute-done((bf16[64,768]{1,0:T(8,128)(2,1)S(1)}, bf16[64,768]{1,0:T(8,128)(2,1)S(1)}, u32[]{:S(2)}, u32[]{:S(2)}) %collective-permute-start.20) | collective-permute-done | bytes 98336 | tf_op jit(solution)/shard_map/ppermute | solution.py:20
  120.2 2.9 %collective-permute-start.39 = (bf16[128,768]{1,0:T(8,128)(2,1)S(1)}, bf16[128,768]{1,0:T(8,128)(2,1)S(1)}, u32[]{:S(2)}, u32[]{:S(2)}) collective-permute-start(bf16[128,768]{1,0:T(8,128)(2,1)S(1)} %pad_maximum_fusion.5), channel_id=1, source_target_pairs={{0,3},{1,0},{2,1},{3,2},{4,7},{5,4},{6,5},{7,6},{8,11},{9,8},{10,9... | collective-permute-start | bytes 589832 | tf_op jit(solution)/shard_map/ppermute | solution.py:29
  125.9 2.5 %collective-permute-done.39 = bf16[128,768]{1,0:T(8,128)(2,1)S(1)} collective-permute-done((bf16[128,768]{1,0:T(8,128)(2,1)S(1)}, bf16[128,768]{1,0:T(8,128)(2,1)S(1)}, u32[]{:S(2)}, u32[]{:S(2)}) %collective-permute-start.39) | collective-permute-done | bytes 196640 | tf_op jit(solution)/shard_map/ppermute | solution.py:29
  128.4 13.7 %collective-permute-done.38 = bf16[128,768]{1,0:T(8,128)(2,1)S(1)} collective-permute-done((bf16[128,768]{1,0:T(8,128)(2,1)S(1)}, bf16[128,768]{1,0:T(8,128)(2,1)S(1)}, u32[]{:S(2)}, u32[]{:S(2)}) %collective-permute-start.38) | collective-permute-done | bytes 196640 | tf_op jit(solution)/shard_map/ppermute | solution.py:29
  146.1 3.0 %collective-permute-done.41 = f32[512]{0:T(512)S(1)} collective-permute-done((f32[512]{0:T(512)S(1)}, f32[512]{0:T(512)S(1)}, u32[]{:S(2)}, u32[]{:S(2)}) %collective-permute-start.41) | collective-permute-done | bytes 2080 | tf_op jit(solution)/shard_map/ppermute | solution.py:20
  150.6 2.1 %collective-permute-done.42 = f32[512]{0:T(512)S(1)} collective-permute-done((f32[512]{0:T(512)S(1)}, f32[512]{0:T(512)S(1)}, u32[]{:S(2)}, u32[]{:S(2)}) %collective-permute-start.42) | collective-permute-done | bytes 2080 | tf_op jit(solution)/shard_map/ppermute | solution.py:20
  156.1 3.0 %collective-permute-done.44 = f32[512]{0:T(512)S(1)} collective-permute-done((f32[512]{0:T(512)S(1)}, f32[512]{0:T(512)S(1)}, u32[]{:S(2)}, u32[]{:S(2)}) %collective-permute-start.44) | collective-permute-done | bytes 2080 | tf_op jit(solution)/shard_map/ppermute | solution.py:20
  160.6 2.1 %collective-permute-done.45 = f32[512]{0:T(512)S(1)} collective-permute-done((f32[512]{0:T(512)S(1)}, f32[512]{0:T(512)S(1)}, u32[]{:S(2)}, u32[]{:S(2)}) %collective-permute-start.45) | collective-permute-done | bytes 2080 | tf_op jit(solution)/shard_map/ppermute | solution.py:20
  166.1 3.0 %collective-permute-done.47 = f32[512]{0:T(512)S(1)} collective-permute-done((f32[512]{0:T(512)S(1)}, f32[512]{0:T(512)S(1)}, u32[]{:S(2)}, u32[]{:S(2)}) %collective-permute-start.47) | collective-permute-done | bytes 2080 | tf_op jit(solution)/shard_map/ppermute | solution.py:20
  170.6 2.1 %collective-permute-done.48 = f32[512]{0:T(512)S(1)} collective-permute-done((f32[512]{0:T(512)S(1)}, f32[512]{0:T(512)S(1)}, u32[]{:S(2)}, u32[]{:S(2)}) %collective-permute-start.48) | collective-permute-done | bytes 2080 | tf_op jit(solution)/shard_map/ppermute | solution.py:20
  175.9 3.0 %collective-permute-done.50 = f32[128]{0:T(128)S(1)} collective-permute-done((f32[128]{0:T(128)S(1)}, f32[128]{0:T(128)S(1)}, u32[]{:S(2)}, u32[]{:S(2)}) %collective-permute-start.50) | collective-permute-done | bytes 544 | tf_op jit(solution)/shard_map/ppermute | solution.py:20
  180.4 2.0 %collective-permute-done.51 = f32[128]{0:T(128)S(1)} collective-permute-done((f32[128]{0:T(128)S(1)}, f32[128]{0:T(128)S(1)}, u32[]{:S(2)}, u32[]{:S(2)}) %collective-permute-start.51) | collective-permute-done | bytes 544 | tf_op jit(solution)/shard_map/ppermute | solution.py:20
  (219 shorter events, 91.9 us)
Async XLA Ops:
  1.6 25.9 %collective-permute-start.22 = (bf16[64,768]{1,0:T(8,128)(2,1)}, bf16[64,768]{1,0:T(8,128)(2,1)}, u32[]{:S(2)}, u32[]{:S(2)}) collective-permute-start(bf16[64,768]{1,0:T(8,128)(2,1)} %get-tuple-element.23), channel_id=1, source_target_pairs={{0,8},{4,12},{8,0},{12,4},{16,24},{20,28},{24,16},{28,20},{1,9},{5... | collective-permute-start | bytes 294920 | tf_op jit(solution)/shard_map/ppermute | solution.py:20
  4.6 21.3 %collective-permute-start.21 = (bf16[64,768]{1,0:T(8,128)(2,1)}, bf16[64,768]{1,0:T(8,128)(2,1)}, u32[]{:S(2)}, u32[]{:S(2)}) collective-permute-start(bf16[64,768]{1,0:T(8,128)(2,1)} %get-tuple-element.23), channel_id=1, source_target_pairs={{0,4},{4,0},{8,12},{12,8},{16,20},{20,16},{24,28},{28,24},{1,5},{5... | collective-permute-start | bytes 294920 | tf_op jit(solution)/shard_map/ppermute | solution.py:20
  4.6 24.4 %collective-permute-start.2 = (bf16[64,768]{1,0:T(8,128)(2,1)}, bf16[64,768]{1,0:T(8,128)(2,1)}, u32[]{:S(2)}, u32[]{:S(2)}) collective-permute-start(bf16[64,768]{1,0:T(8,128)(2,1)} %get-tuple-element.22), channel_id=1, source_target_pairs={{0,8},{4,12},{8,0},{12,4},{16,24},{20,28},{24,16},{28,20},{1,9},{5... | collective-permute-start | bytes 294920 | tf_op jit(solution)/shard_map/ppermute | solution.py:20
  4.6 25.7 %collective-permute-start = (bf16[64,768]{1,0:T(8,128)(2,1)}, bf16[64,768]{1,0:T(8,128)(2,1)}, u32[]{:S(2)}, u32[]{:S(2)}) collective-permute-start(bf16[64,768]{1,0:T(8,128)(2,1)} %get-tuple-element.22), channel_id=1, source_target_pairs={{0,4},{4,0},{8,12},{12,8},{16,20},{20,16},{24,28},{28,24},{1,5},{5... | collective-permute-start | bytes 294920 | tf_op jit(solution)/shard_map/ppermute | solution.py:20
  12.5 28.3 %collective-permute-start.3 = (bf16[768,768]{1,0:T(8,128)(2,1)S(1)}, bf16[768,768]{1,0:T(8,128)(2,1)}, u32[]{:S(2)}, u32[]{:S(2)}) collective-permute-start(bf16[768,768]{1,0:T(8,128)(2,1)S(1)} %get-tuple-element.21), channel_id=1, source_target_pairs={{0,8},{4,12},{8,0},{12,4},{16,24},{20,28},{24,16},{28,20},{1,9},{5... | collective-permute-start | bytes 3538952 | tf_op jit(solution)/shard_map/ppermute | solution.py:20
  25.9 16.5 %collective-permute-start.1 = (bf16[768,768]{1,0:T(8,128)(2,1)S(1)}, bf16[768,768]{1,0:T(8,128)(2,1)S(1)}, u32[]{:S(2)}, u32[]{:S(2)}) collective-permute-start(bf16[768,768]{1,0:T(8,128)(2,1)S(1)} %get-tuple-element.20), channel_id=1, source_target_pairs={{0,4},{4,0},{8,12},{12,8},{16,20},{20,16},{24,28},{28,24},{1,5},{5... | collective-permute-start | bytes 3538952 | tf_op jit(solution)/shard_map/ppermute | solution.py:20
  43.7 6.1 %collective-permute-start.24 = (bf16[64,768]{1,0:T(8,128)(2,1)S(1)}, bf16[64,768]{1,0:T(8,128)(2,1)S(1)}, u32[]{:S(2)}, u32[]{:S(2)}) collective-permute-start(bf16[64,768]{1,0:T(8,128)(2,1)S(1)} %get-tuple-element.30), channel_id=1, source_target_pairs={{0,8},{4,12},{8,0},{12,4},{16,24},{20,28},{24,16},{28,20},{1,9},{5... | collective-permute-start | bytes 294920 | tf_op jit(solution)/shard_map/ppermute | solution.py:20
  45.8 6.0 %collective-permute-start.23 = (bf16[64,768]{1,0:T(8,128)(2,1)S(1)}, bf16[64,768]{1,0:T(8,128)(2,1)S(1)}, u32[]{:S(2)}, u32[]{:S(2)}) collective-permute-start(bf16[64,768]{1,0:T(8,128)(2,1)S(1)} %get-tuple-element.30), channel_id=1, source_target_pairs={{0,4},{4,0},{8,12},{12,8},{16,20},{20,16},{24,28},{28,24},{1,5},{5... | collective-permute-start | bytes 294920 | tf_op jit(solution)/shard_map/ppermute | solution.py:20
  48.8 6.1 %collective-permute-start.5 = (bf16[64,768]{1,0:T(8,128)(2,1)S(1)}, bf16[64,768]{1,0:T(8,128)(2,1)S(1)}, u32[]{:S(2)}, u32[]{:S(2)}) collective-permute-start(bf16[64,768]{1,0:T(8,128)(2,1)S(1)} %get-tuple-element.44), channel_id=1, source_target_pairs={{0,8},{4,12},{8,0},{12,4},{16,24},{20,28},{24,16},{28,20},{1,9},{5... | collective-permute-start | bytes 294920 | tf_op jit(solution)/shard_map/ppermute | solution.py:20
  49.5 7.5 %collective-permute-start.4 = (bf16[64,768]{1,0:T(8,128)(2,1)S(1)}, bf16[64,768]{1,0:T(8,128)(2,1)S(1)}, u32[]{:S(2)}, u32[]{:S(2)}) collective-permute-start(bf16[64,768]{1,0:T(8,128)(2,1)S(1)} %get-tuple-element.44), channel_id=1, source_target_pairs={{0,4},{4,0},{8,12},{12,8},{16,20},{20,16},{24,28},{28,24},{1,5},{5... | collective-permute-start | bytes 294920 | tf_op jit(solution)/shard_map/ppermute | solution.py:20
  52.7 10.0 %collective-permute-start.26 = (bf16[64,768]{1,0:T(8,128)(2,1)S(1)}, bf16[64,768]{1,0:T(8,128)(2,1)S(1)}, u32[]{:S(2)}, u32[]{:S(2)}) collective-permute-start(bf16[64,768]{1,0:T(8,128)(2,1)S(1)} %get-tuple-element.32), channel_id=1, source_target_pairs={{0,8},{4,12},{8,0},{12,4},{16,24},{20,28},{24,16},{28,20},{1,9},{5... | collective-permute-start | bytes 294920 | tf_op jit(solution)/shard_map/ppermute | solution.py:20
  54.9 10.0 %collective-permute-start.25 = (bf16[64,768]{1,0:T(8,128)(2,1)S(1)}, bf16[64,768]{1,0:T(8,128)(2,1)S(1)}, u32[]{:S(2)}, u32[]{:S(2)}) collective-permute-start(bf16[64,768]{1,0:T(8,128)(2,1)S(1)} %get-tuple-element.32), channel_id=1, source_target_pairs={{0,4},{4,0},{8,12},{12,8},{16,20},{20,16},{24,28},{28,24},{1,5},{5... | collective-permute-start | bytes 294920 | tf_op jit(solution)/shard_map/ppermute | solution.py:20
  57.9 9.3 %collective-permute-start.10 = (bf16[64,768]{1,0:T(8,128)(2,1)S(1)}, bf16[64,768]{1,0:T(8,128)(2,1)S(1)}, u32[]{:S(2)}, u32[]{:S(2)}) collective-permute-start(bf16[64,768]{1,0:T(8,128)(2,1)S(1)} %convert_element_type.104), channel_id=1, source_target_pairs={{0,8},{4,12},{8,0},{12,4},{16,24},{20,28},{24,16},{28,20},{1,9},{5... | collective-permute-start | bytes 294920 | tf_op jit(solution)/shard_map/ppermute | solution.py:20
  58.6 12.3 %collective-permute-start.9 = (bf16[64,768]{1,0:T(8,128)(2,1)S(1)}, bf16[64,768]{1,0:T(8,128)(2,1)S(1)}, u32[]{:S(2)}, u32[]{:S(2)}) collective-permute-start(bf16[64,768]{1,0:T(8,128)(2,1)S(1)} %convert_element_type.104), channel_id=1, source_target_pairs={{0,4},{4,0},{8,12},{12,8},{16,20},{20,16},{24,28},{28,24},{1,5},{5... | collective-permute-start | bytes 294920 | tf_op jit(solution)/shard_map/ppermute | solution.py:20
  58.9 65.3 %collective-permute-start.8 = (bf16[3,512,128]{2,1,0:T(8,128)(2,1)}, bf16[3,512,128]{2,1,0:T(8,128)(2,1)}, u32[]{:S(2)}, u32[]{:S(2)}) collective-permute-start(bf16[3,512,128]{2,1,0:T(8,128)(2,1)} %slice.98), channel_id=1, source_target_pairs={{0,3},{1,0},{2,1},{3,2},{4,7},{5,4},{6,5},{7,6},{8,11},{9,8},{10,9... | collective-permute-start | bytes 1179656 | tf_op jit(solution)/shard_map/ppermute | solution.py:39
  62.7 61.6 %collective-permute-start.7 = (bf16[3,512,128]{2,1,0:T(8,128)(2,1)}, bf16[3,512,128]{2,1,0:T(8,128)(2,1)}, u32[]{:S(2)}, u32[]{:S(2)}) collective-permute-start(bf16[3,512,128]{2,1,0:T(8,128)(2,1)} %slice.98), channel_id=1, source_target_pairs={{0,2},{1,3},{2,0},{3,1},{4,6},{5,7},{6,4},{7,5},{8,10},{9,11},{10,... | collective-permute-start | bytes 1179656 | tf_op jit(solution)/shard_map/ppermute | solution.py:39
  64.8 59.5 %collective-permute-start.6 = (bf16[3,512,128]{2,1,0:T(8,128)(2,1)}, bf16[3,512,128]{2,1,0:T(8,128)(2,1)}, u32[]{:S(2)}, u32[]{:S(2)}) collective-permute-start(bf16[3,512,128]{2,1,0:T(8,128)(2,1)} %slice.98), channel_id=1, source_target_pairs={{0,1},{1,2},{2,3},{3,0},{4,5},{5,6},{6,7},{7,4},{8,9},{9,10},{10,1... | collective-permute-start | bytes 1179656 | tf_op jit(solution)/shard_map/ppermute | solution.py:39
  67.3 4.9 %collective-permute-start.28 = (bf16[64,768]{1,0:T(8,128)(2,1)S(1)}, bf16[64,768]{1,0:T(8,128)(2,1)S(1)}, u32[]{:S(2)}, u32[]{:S(2)}) collective-permute-start(bf16[64,768]{1,0:T(8,128)(2,1)S(1)} %get-tuple-element.34), channel_id=1, source_target_pairs={{0,8},{4,12},{8,0},{12,4},{16,24},{20,28},{24,16},{28,20},{1,9},{5... | collective-permute-start | bytes 294920 | tf_op jit(solution)/shard_map/ppermute | solution.py:20
  72.2 5.3 %collective-permute-start.12 = (bf16[64,768]{1,0:T(8,128)(2,1)S(1)}, bf16[64,768]{1,0:T(8,128)(2,1)S(1)}, u32[]{:S(2)}, u32[]{:S(2)}) collective-permute-start(bf16[64,768]{1,0:T(8,128)(2,1)S(1)} %get-tuple-element.46), channel_id=1, source_target_pairs={{0,8},{4,12},{8,0},{12,4},{16,24},{20,28},{24,16},{28,20},{1,9},{5... | collective-permute-start | bytes 294920 | tf_op jit(solution)/shard_map/ppermute | solution.py:20
  80.2 4.9 %collective-permute-start.29 = (bf16[64,768]{1,0:T(8,128)(2,1)S(1)}, bf16[64,768]{1,0:T(8,128)(2,1)S(1)}, u32[]{:S(2)}, u32[]{:S(2)}) collective-permute-start(bf16[64,768]{1,0:T(8,128)(2,1)S(1)} %get-tuple-element.36), channel_id=1, source_target_pairs={{0,4},{4,0},{8,12},{12,8},{16,20},{20,16},{24,28},{28,24},{1,5},{5... | collective-permute-start | bytes 294920 | tf_op jit(solution)/shard_map/ppermute | solution.py:20
  85.1 5.2 %collective-permute-start.13 = (bf16[64,768]{1,0:T(8,128)(2,1)S(1)}, bf16[64,768]{1,0:T(8,128)(2,1)S(1)}, u32[]{:S(2)}, u32[]{:S(2)}) collective-permute-start(bf16[64,768]{1,0:T(8,128)(2,1)S(1)} %get-tuple-element.48), channel_id=1, source_target_pairs={{0,4},{4,0},{8,12},{12,8},{16,20},{20,16},{24,28},{28,24},{1,5},{5... | collective-permute-start | bytes 294920 | tf_op jit(solution)/shard_map/ppermute | solution.py:20
  86.7 4.9 %collective-permute-start.32 = (bf16[64,768]{1,0:T(8,128)(2,1)S(1)}, bf16[64,768]{1,0:T(8,128)(2,1)S(1)}, u32[]{:S(2)}, u32[]{:S(2)}) collective-permute-start(bf16[64,768]{1,0:T(8,128)(2,1)S(1)} %get-tuple-element.38), channel_id=1, source_target_pairs={{0,8},{4,12},{8,0},{12,4},{16,24},{20,28},{24,16},{28,20},{1,9},{5... | collective-permute-start | bytes 294920 | tf_op jit(solution)/shard_map/ppermute | solution.py:20
  91.6 5.2 %collective-permute-start.16 = (bf16[64,768]{1,0:T(8,128)(2,1)S(1)}, bf16[64,768]{1,0:T(8,128)(2,1)S(1)}, u32[]{:S(2)}, u32[]{:S(2)}) collective-permute-start(bf16[64,768]{1,0:T(8,128)(2,1)S(1)} %get-tuple-element.50), channel_id=1, source_target_pairs={{0,8},{4,12},{8,0},{12,4},{16,24},{20,28},{24,16},{28,20},{1,9},{5... | collective-permute-start | bytes 294920 | tf_op jit(solution)/shard_map/ppermute | solution.py:20
  96.8 4.6 %collective-permute-start.34 = (bf16[64,768]{1,0:T(8,128)(2,1)S(1)}, bf16[64,768]{1,0:T(8,128)(2,1)S(1)}, u32[]{:S(2)}, u32[]{:S(2)}) collective-permute-start(bf16[64,768]{1,0:T(8,128)(2,1)S(1)} %get-tuple-element.40), channel_id=1, source_target_pairs={{0,8},{4,12},{8,0},{12,4},{16,24},{20,28},{24,16},{28,20},{1,9},{5... | collective-permute-start | bytes 294920 | tf_op jit(solution)/shard_map/ppermute | solution.py:20
  99.5 4.9 %collective-permute-start.33 = (bf16[64,768]{1,0:T(8,128)(2,1)S(1)}, bf16[64,768]{1,0:T(8,128)(2,1)S(1)}, u32[]{:S(2)}, u32[]{:S(2)}) collective-permute-start(bf16[64,768]{1,0:T(8,128)(2,1)S(1)} %get-tuple-element.40), channel_id=1, source_target_pairs={{0,4},{4,0},{8,12},{12,8},{16,20},{20,16},{24,28},{28,24},{1,5},{5... | collective-permute-start | bytes 294920 | tf_op jit(solution)/shard_map/ppermute | solution.py:20
  104.4 5.2 %collective-permute-start.17 = (bf16[64,768]{1,0:T(8,128)(2,1)S(1)}, bf16[64,768]{1,0:T(8,128)(2,1)S(1)}, u32[]{:S(2)}, u32[]{:S(2)}) collective-permute-start(bf16[64,768]{1,0:T(8,128)(2,1)S(1)} %get-tuple-element.52), channel_id=1, source_target_pairs={{0,4},{4,0},{8,12},{12,8},{16,20},{20,16},{24,28},{28,24},{1,5},{5... | collective-permute-start | bytes 294920 | tf_op jit(solution)/shard_map/ppermute | solution.py:20
  106.0 4.9 %collective-permute-start.36 = (bf16[64,768]{1,0:T(8,128)(2,1)S(1)}, bf16[64,768]{1,0:T(8,128)(2,1)S(1)}, u32[]{:S(2)}, u32[]{:S(2)}) collective-permute-start(bf16[64,768]{1,0:T(8,128)(2,1)S(1)} %get-tuple-element.42), channel_id=1, source_target_pairs={{0,8},{4,12},{8,0},{12,4},{16,24},{20,28},{24,16},{28,20},{1,9},{5... | collective-permute-start | bytes 294920 | tf_op jit(solution)/shard_map/ppermute | solution.py:20
  109.6 8.1 %collective-permute-start.35 = (bf16[64,768]{1,0:T(8,128)(2,1)S(1)}, bf16[64,768]{1,0:T(8,128)(2,1)S(1)}, u32[]{:S(2)}, u32[]{:S(2)}) collective-permute-start(bf16[64,768]{1,0:T(8,128)(2,1)S(1)} %get-tuple-element.42), channel_id=1, source_target_pairs={{0,4},{4,0},{8,12},{12,8},{16,20},{20,16},{24,28},{28,24},{1,5},{5... | collective-permute-start | bytes 294920 | tf_op jit(solution)/shard_map/ppermute | solution.py:20
  110.9 5.2 %collective-permute-start.20 = (bf16[64,768]{1,0:T(8,128)(2,1)S(1)}, bf16[64,768]{1,0:T(8,128)(2,1)S(1)}, u32[]{:S(2)}, u32[]{:S(2)}) collective-permute-start(bf16[64,768]{1,0:T(8,128)(2,1)S(1)} %get-tuple-element.54), channel_id=1, source_target_pairs={{0,8},{4,12},{8,0},{12,4},{16,24},{20,28},{24,16},{28,20},{1,9},{5... | collective-permute-start | bytes 294920 | tf_op jit(solution)/shard_map/ppermute | solution.py:20
  120.2 8.2 %collective-permute-start.39 = (bf16[128,768]{1,0:T(8,128)(2,1)S(1)}, bf16[128,768]{1,0:T(8,128)(2,1)S(1)}, u32[]{:S(2)}, u32[]{:S(2)}) collective-permute-start(bf16[128,768]{1,0:T(8,128)(2,1)S(1)} %pad_maximum_fusion.5), channel_id=1, source_target_pairs={{0,3},{1,0},{2,1},{3,2},{4,7},{5,4},{6,5},{7,6},{8,11},{9,8},{10,9... | collective-permute-start | bytes 589832 | tf_op jit(solution)/shard_map/ppermute | solution.py:29
  123.1 19.1 %collective-permute-start.38 = (bf16[128,768]{1,0:T(8,128)(2,1)S(1)}, bf16[128,768]{1,0:T(8,128)(2,1)S(1)}, u32[]{:S(2)}, u32[]{:S(2)}) collective-permute-start(bf16[128,768]{1,0:T(8,128)(2,1)S(1)} %pad_maximum_fusion.5), channel_id=1, source_target_pairs={{0,2},{1,3},{2,0},{3,1},{4,6},{5,7},{6,4},{7,5},{8,10},{9,11},{10,... | collective-permute-start | bytes 589832 | tf_op jit(solution)/shard_map/ppermute | solution.py:29
  124.2 17.9 %collective-permute-start.37 = (bf16[128,768]{1,0:T(8,128)(2,1)S(1)}, bf16[128,768]{1,0:T(8,128)(2,1)S(1)}, u32[]{:S(2)}, u32[]{:S(2)}) collective-permute-start(bf16[128,768]{1,0:T(8,128)(2,1)S(1)} %pad_maximum_fusion.5), channel_id=1, source_target_pairs={{0,1},{1,2},{2,3},{3,0},{4,5},{5,6},{6,7},{7,4},{8,9},{9,10},{10,1... | collective-permute-start | bytes 589832 | tf_op jit(solution)/shard_map/ppermute | solution.py:29
  (24 other events, 92.3 us)

commit v8 on v4

--- a/solution.py
+++ b/solution.py
@@ -123,7 +123,18 @@
 
     def start_rotation_gather(current):
         held, current = lax.optimization_barrier((rotations[: ROTS - 1], current))
-        gathered.append(gather_pieces(held))
+        half_rows = held.shape[1] // 2
+        first_of_pair = (atoms_here % 2) == 0
+        mine = jnp.where(first_of_pair, held[:, :half_rows], held[:, half_rows:])
+        mine = gather_pieces(mine)
+        theirs = swapped(mine, "atoms", 0)
+        gathered.append(
+            jnp.where(
+                first_of_pair,
+                jnp.concatenate([mine, theirs], axis=2),
+                jnp.concatenate([theirs, mine], axis=2),
+            )
+        )
         return current
 
     half_bands = subspace.shape[0] // 2

time: 179 us -> 181 us (1.011)
  other arithmetic: 8.44 us -> 11.3 us
  starting transfers between devices: 47.8 us -> 45.5 us
    ppermute x48 -> x49, starting transfers between devices: 38.7 us -> 31.8 us  [swapped(): return lax.ppermute(value, axis, pairs)]
    ppermute x3, waiting for transfers between devices: 0.01 us -> 5.05 us  [gather_pieces(): pieces.append(lax.ppermute(value, 'bands', pairs))]
    select_n x0 -> x2, other arithmetic: none -> 3.84 us  [the longest x1 3.81 us: start_rotation_gather(): jnp.where(first_of_pair, jnp.concatenate([mine, theirs], axis=2), jnp.con...]
    ppermute x48 -> x49, waiting for transfers between devices: 34.3 us -> 30.9 us  [swapped(): return lax.ppermute(value, axis, pairs)]
    ppermute x3, starting transfers between devices: 4 us -> 6.72 us  [gather_bands(): pieces.append(lax.ppermute(value, 'bands', pairs))]
    ppermute x3, starting transfers between devices: 5.05 us -> 6.89 us  [gather_pieces(): pieces.append(lax.ppermute(value, 'bands', pairs))]
  transfers between devices with their start and end apart: 54 -> 55, of which waited for: 25 -> 21; matrix products, arithmetic and copies ran while one was open for 36% -> 36% of each run, Pallas kernels for 0% -> 0%
where the time goes in v8:
time: 181 us; the launch traced here: 180 us
  matrix products  57.9 us (32%)
  waiting for transfers between devices  51.4 us (28%)
  starting transfers between devices  45.5 us (25%)
  local copies, waits for them, and re-layouts  13.3 us (7%)
  other arithmetic  11.3 us (6%)
    ppermute x49, starting transfers between devices, swapped(): return lax.ppermute(value, axis, pairs)  31.8 us
    ppermute x49, waiting for transfers between devices, swapped(): return lax.ppermute(value, axis, pairs)  30.9 us
    dot_general x32, matrix products, apply_operator(): lax.dot_general(other_rows, own_pair_t[round_index], (((1,), (1,)), ((),...  22.4 us
    dot_general x32, matrix products, apply_operator(): jnp.dot(other_rows, other_pair[round_index], preferred_element_type=jnp.f...  15.6 us
    ppermute x3, waiting for transfers between devices, gather_bands(): pieces.append(lax.ppermute(value, 'bands', pairs))  15.4 us
    dot_general x4, matrix products, pattern_mask(): lax.dot_general(per_row.astype(jnp.bfloat16), col_onehot, (((1,), (1,)),...  8.21 us
    ppermute x3, starting transfers between devices, gather_pieces(): pieces.append(lax.ppermute(value, 'bands', pairs))  6.89 us
    ppermute x3, starting transfers between devices, gather_bands(): pieces.append(lax.ppermute(value, 'bands', pairs))  6.72 us
  transfers between devices with their start and end apart: 55, of which 21 were waited for; matrix products, arithmetic and copies ran while one was open for 36% of the time, Pallas kernels for 0%

profile of v8, /device:TPU:0, one launch (start us, length us, event | category | flops | bytes accessed | tf_op | source)
XLA Modules:
  0.0 180.1 jit_solution(2109349050587981646)
XLA Ops:
  2.1 2.5 %collective-permute-start.3 = (bf16[64,768]{1,0:T(8,128)(2,1)}, bf16[64,768]{1,0:T(8,128)(2,1)}, u32[]{:S(2)}, u32[]{:S(2)}) collective-permute-start(bf16[64,768]{1,0:T(8,128)(2,1)} %get-tuple-element.14), channel_id=1, source_target_pairs={{0,8},{4,12},{8,0},{12,4},{16,24},{20,28},{24,16},{28,20},{1,9},{5... | collective-permute-start | bytes 294920 | tf_op jit(solution)/shard_map/ppermute | solution.py:20
  5.1 3.3 %slice_bitcast_fusion.1 = (bf16[768,768]{1,0:T(8,128)(2,1)}, bf16[768,768]{1,0:T(8,128)(2,1)}) fusion(bf16[2,768,768]{2,1,0:T(8,128)(2,1)} %param.8), kind=kLoop, calls=%fused_computation.19 | loop fusion | bytes 4718592 | tf_op jit(solution)/shard_map/squeeze | solution.py:91
  8.3 1.7 collective-permute-start.5
  10.8 2.0 %add_multiply_fusion = f32[768,768]{1,0:T(8,128)} fusion(bf16[768,768]{1,0:T(8,128)(2,1)S(1)} %copy-done.4, s32[768]{0:T(1024)S(1)} %get-tuple-element.47), kind=kLoop, calls=%fused_computation.3 | loop fusion | flops 4128768 | bytes 3542016 | tf_op jit(solution)/shard_map/mul | solution.py:81
  12.8 2.0 %copy.9 = f32[768,768]{0,1:T(8,128)S(1)} copy(f32[768,768]{1,0:T(8,128)} %add_multiply_fusion) | data formatting | bytes 4718592 | tf_op jit(solution)/shard_map/mul | solution.py:81
  14.8 2.0 %fusion = bf16[768,768]{1,0:T(8,128)(2,1)S(1)} fusion(f32[768,768]{0,1:T(8,128)S(1)} %copy.9, s32[768]{0:T(1024)S(1)} %get-tuple-element.47, bf16[768,768]{1,0:T(8,128)(2,1)} %param.7), kind=kLoop, calls=%fused_computation.2 | loop fusion | flops 5308416 | bytes 4721664 | tf_op jit(solution)/shard_map/convert_element_type | solution.py:82
  19.2 1.9 %compare_select_fusion.1 = bf16[768,768]{1,0:T(8,128)(2,1)S(1)} fusion(s32[768]{0:T(1024)S(1)} %get-tuple-element.46, s32[768]{0:T(1024)S(1)} %get-tuple-element.47, s32[2,4,4]{2,1,0:T(4,128)S(1)} %copy-done.20, bf16[2,768,768]{2,1,0:T(8,128)(2,1)} %param.8), kind=kOutput, calls=%fused_computation.5 | convolution fusion | flops 5932048 | bytes 2369536 | tf_op jit(solution)/shard_map/dot_general | solution.py:63
  21.1 2.4 %compare_select_fusion.3 = bf16[768,768]{1,0:T(8,128)(2,1)S(1)} fusion(s32[768]{0:T(1024)S(1)} %convert_reduce_fusion.1, s32[768]{0:T(1024)S(1)} %get-tuple-element.47, s32[2,4,4]{2,1,0:T(4,128)S(1)} %copy-done.20, bf16[2,768,768]{2,1,0:T(8,128)(2,1)} %param.8), kind=kOutput, calls=%fused_computation.7 | convolution fusion | flops 5932048 | bytes 2369536 | tf_op jit(solution)/shard_map/dot_general | solution.py:63
  24.1 1.8 slice.82
  26.4 2.1 %convolution_add_fusion.31 = f32[768,64]{0,1:T(8,128)} fusion(f32[768,64]{0,1:T(8,128)} %fusion.137, bf16[768,768]{1,0:T(8,128)(2,1)S(1)} %compare_select_fusion.3, bf16[64,768]{1,0:T(8,128)(2,1)} %collective-permute-done), kind=kOutput, calls=%fused_computation.133 | convolution fusion | flops 75546624 | bytes 1671168 | tf_op jit(solution)/shard_map/dot_general | solution.py:102
  29.1 2.1 %convolution_add_fusion.16 = f32[768,64]{0,1:T(8,128)} fusion(f32[768,64]{0,1:T(8,128)S(1)} %copy-done.11, bf16[768,768]{1,0:T(8,128)(2,1)S(1)} %compare_select_fusion.3, bf16[64,768]{1,0:T(8,128)(2,1)} %collective-permute-done.24), kind=kOutput, calls=%fused_computation.83 | convolution fusion | flops 75546624 | bytes 1671168 | tf_op jit(solution)/shard_map/dot_general | solution.py:102
  31.4 2.1 %fusion.173 = f32[768,64]{0,1:T(8,128)} fusion(bf16[768,768]{1,0:T(8,128)(2,1)S(1)} %compare_select_fusion.1, bf16[64,768]{1,0:T(8,128)(2,1)} %collective-permute-done.25), kind=kOutput, calls=%fused_computation.271 | convolution fusion | flops 75497472 | bytes 1474560 | tf_op jit(solution)/shard_map/dot_general | solution.py:102
  33.5 2.1 %fusion.151 = f32[768,64]{0,1:T(8,128)} fusion(bf16[768,768]{1,0:T(8,128)(2,1)S(1)} %compare_select_fusion.1, bf16[64,768]{1,0:T(8,128)(2,1)} %collective-permute-done.3), kind=kOutput, calls=%fused_computation.249 | convolution fusion | flops 75497472 | bytes 1474560 | tf_op jit(solution)/shard_map/dot_general | solution.py:102
  37.2 1.9 %compare_select_fusion = bf16[768,768]{1,0:T(8,128)(2,1)S(1)} fusion(bf16[768,768]{1,0:T(8,128)(2,1)} %collective-permute-done.5, s32[768]{0:T(1024)S(1)} %get-tuple-element.46, s32[768]{0:T(1024)S(1)} %get-tuple-element.47, s32[4,4]{1,0:T(4,128)} %copy-done.23), kind=kOutput, calls=%fused_computation.4 | convolution fusion | flops 5932048 | bytes 2365504 | tf_op jit(solution)/shard_map/dot_general | solution.py:63
  39.2 2.0 %fusion.196 = f32[768,64]{0,1:T(8,128)} fusion(bf16[64,768]{1,0:T(8,128)(2,1)} %collective-permute-done.25, bf16[768,768]{1,0:T(8,128)(2,1)S(1)} %compare_select_fusion), kind=kOutput, calls=%fused_computation.294 | convolution fusion | flops 75497472 | bytes 1474560 | tf_op jit(solution)/shard_map/dot_general | solution.py:106
  41.2 1.9 %compare_select_fusion.2 = bf16[768,768]{1,0:T(8,128)(2,1)S(1)} fusion(bf16[768,768]{1,0:T(8,128)(2,1)} %collective-permute-done.2, s32[768]{0:T(1024)S(1)} %convert_reduce_fusion.1, s32[768]{0:T(1024)S(1)} %get-tuple-element.47, s32[4,4]{1,0:T(4,128)} %collective-permute-done.1), kind=kOutput, calls=%fused_computation.6 | convolution fusion | flops 5932048 | bytes 2365504 | tf_op jit(solution)/shard_map/dot_general | solution.py:63
  57.6 2.8 %collective-permute-start.9 = (bf16[3,256,128]{2,1,0:T(8,128)(2,1)S(1)}, bf16[3,256,128]{2,1,0:T(8,128)(2,1)S(1)}, u32[]{:S(2)}, u32[]{:S(2)}) collective-permute-start(bf16[3,256,128]{2,1,0:T(8,128)(2,1)S(1)} %slice_select_fusion), channel_id=1, source_target_pairs={{0,2},{1,3},{2,0},{3,1},{4,6},{5,7},{6,4},{7,5},{8,10},{9,11},{10,... | collective-permute-start | bytes 589832 | tf_op jit(solution)/shard_map/ppermute | solution.py:39
  62.8 2.5 %collective-permute-start.10 = (bf16[3,256,128]{2,1,0:T(8,128)(2,1)S(1)}, bf16[3,256,128]{2,1,0:T(8,128)(2,1)S(1)}, u32[]{:S(2)}, u32[]{:S(2)}) collective-permute-start(bf16[3,256,128]{2,1,0:T(8,128)(2,1)S(1)} %slice_select_fusion), channel_id=1, source_target_pairs={{0,3},{1,0},{2,1},{3,2},{4,7},{5,4},{6,5},{7,6},{8,11},{9,8},{10,9... | collective-permute-start | bytes 589832 | tf_op jit(solution)/shard_map/ppermute | solution.py:39
  70.2 4.5 %collective-permute-done.9 = bf16[3,256,128]{2,1,0:T(8,128)(2,1)S(1)} collective-permute-done((bf16[3,256,128]{2,1,0:T(8,128)(2,1)S(1)}, bf16[3,256,128]{2,1,0:T(8,128)(2,1)S(1)}, u32[]{:S(2)}, u32[]{:S(2)}) %collective-permute-start.9) | collective-permute-done | bytes 196640 | tf_op jit(solution)/shard_map/ppermute | solution.py:39
  105.9 3.1 %collective-permute-done.23 = bf16[64,768]{1,0:T(8,128)(2,1)S(1)} collective-permute-done((bf16[64,768]{1,0:T(8,128)(2,1)S(1)}, bf16[64,768]{1,0:T(8,128)(2,1)S(1)}, u32[]{:S(2)}, u32[]{:S(2)}) %collective-permute-start.23) | collective-permute-done | bytes 98336 | tf_op jit(solution)/shard_map/ppermute | solution.py:20
  112.8 3.8 %collective-permute-start.41 = (bf16[128,768]{1,0:T(8,128)(2,1)S(1)}, bf16[128,768]{1,0:T(8,128)(2,1)S(1)}, u32[]{:S(2)}, u32[]{:S(2)}) collective-permute-start(bf16[128,768]{1,0:T(8,128)(2,1)S(1)} %pad_maximum_fusion.5), channel_id=1, source_target_pairs={{0,2},{1,3},{2,0},{3,1},{4,6},{5,7},{6,4},{7,5},{8,10},{9,11},{10,... | collective-permute-start | bytes 589832 | tf_op jit(solution)/shard_map/ppermute | solution.py:29
  116.6 1.9 %collective-permute-start.40 = (bf16[128,768]{1,0:T(8,128)(2,1)S(1)}, bf16[128,768]{1,0:T(8,128)(2,1)S(1)}, u32[]{:S(2)}, u32[]{:S(2)}) collective-permute-start(bf16[128,768]{1,0:T(8,128)(2,1)S(1)} %pad_maximum_fusion.5), channel_id=1, source_target_pairs={{0,1},{1,2},{2,3},{3,0},{4,5},{5,6},{6,7},{7,4},{8,9},{9,10},{10,1... | collective-permute-start | bytes 589832 | tf_op jit(solution)/shard_map/ppermute | solution.py:29
  119.4 14.5 %collective-permute-done.41 = bf16[128,768]{1,0:T(8,128)(2,1)S(1)} collective-permute-done((bf16[128,768]{1,0:T(8,128)(2,1)S(1)}, bf16[128,768]{1,0:T(8,128)(2,1)S(1)}, u32[]{:S(2)}, u32[]{:S(2)}) %collective-permute-start.41) | collective-permute-done | bytes 196640 | tf_op jit(solution)/shard_map/ppermute | solution.py:29
  135.8 3.8 %maximum_select_fusion = bf16[4,3,512,128]{3,2,1,0:T(8,128)(2,1)S(1)} fusion(bf16[4,3,256,128]{3,2,1,0:T(8,128)(2,1)} %collective-permute-done.11, bf16[1,3,256,128]{3,2,1,0:T(8,128)(2,1)S(1)} %bitcast.275, bf16[1,3,256,128]{3,2,1,0:T(8,128)(2,1)S(1)} %bitcast.271, bf16[1,3,256,128]{3,2,1,0:T(8,128)(2,1)S(1)} %bitcast.273, ...), kind=kLoop, calls=%fused_computation.8 | loop fusion | flops 16515072 | bytes 3145729 | tf_op jit(solution)/shard_map/jit(_where)/select_n | solution.py:132
  142.8 3.0 %collective-permute-done.44 = f32[512]{0:T(512)S(1)} collective-permute-done((f32[512]{0:T(512)S(1)}, f32[512]{0:T(512)S(1)}, u32[]{:S(2)}, u32[]{:S(2)}) %collective-permute-start.44) | collective-permute-done | bytes 2080 | tf_op jit(solution)/shard_map/ppermute | solution.py:20
  147.3 2.1 %collective-permute-done.45 = f32[512]{0:T(512)S(1)} collective-permute-done((f32[512]{0:T(512)S(1)}, f32[512]{0:T(512)S(1)}, u32[]{:S(2)}, u32[]{:S(2)}) %collective-permute-start.45) | collective-permute-done | bytes 2080 | tf_op jit(solution)/shard_map/ppermute | solution.py:20
  152.8 3.0 %collective-permute-done.47 = f32[512]{0:T(512)S(1)} collective-permute-done((f32[512]{0:T(512)S(1)}, f32[512]{0:T(512)S(1)}, u32[]{:S(2)}, u32[]{:S(2)}) %collective-permute-start.47) | collective-permute-done | bytes 2080 | tf_op jit(solution)/shard_map/ppermute | solution.py:20
  157.3 2.1 %collective-permute-done.48 = f32[512]{0:T(512)S(1)} collective-permute-done((f32[512]{0:T(512)S(1)}, f32[512]{0:T(512)S(1)}, u32[]{:S(2)}, u32[]{:S(2)}) %collective-permute-start.48) | collective-permute-done | bytes 2080 | tf_op jit(solution)/shard_map/ppermute | solution.py:20
  162.8 3.0 %collective-permute-done.50 = f32[512]{0:T(512)S(1)} collective-permute-done((f32[512]{0:T(512)S(1)}, f32[512]{0:T(512)S(1)}, u32[]{:S(2)}, u32[]{:S(2)}) %collective-permute-start.50) | collective-permute-done | bytes 2080 | tf_op jit(solution)/shard_map/ppermute | solution.py:20
  167.3 2.1 %collective-permute-done.51 = f32[512]{0:T(512)S(1)} collective-permute-done((f32[512]{0:T(512)S(1)}, f32[512]{0:T(512)S(1)}, u32[]{:S(2)}, u32[]{:S(2)}) %collective-permute-start.51) | collective-permute-done | bytes 2080 | tf_op jit(solution)/shard_map/ppermute | solution.py:20
  172.6 3.0 %collective-permute-done.53 = f32[128]{0:T(128)S(1)} collective-permute-done((f32[128]{0:T(128)S(1)}, f32[128]{0:T(128)S(1)}, u32[]{:S(2)}, u32[]{:S(2)}) %collective-permute-start.53) | collective-permute-done | bytes 544 | tf_op jit(solution)/shard_map/ppermute | solution.py:20
  177.1 2.0 %collective-permute-done.54 = f32[128]{0:T(128)S(1)} collective-permute-done((f32[128]{0:T(128)S(1)}, f32[128]{0:T(128)S(1)}, u32[]{:S(2)}, u32[]{:S(2)}) %collective-permute-start.54) | collective-permute-done | bytes 544 | tf_op jit(solution)/shard_map/ppermute | solution.py:20
  (267 shorter events, 88.0 us)
Async XLA Ops:
  1.6 24.8 %collective-permute-start = (bf16[64,768]{1,0:T(8,128)(2,1)}, bf16[64,768]{1,0:T(8,128)(2,1)}, u32[]{:S(2)}, u32[]{:S(2)}) collective-permute-start(bf16[64,768]{1,0:T(8,128)(2,1)} %get-tuple-element.14), channel_id=1, source_target_pairs={{0,4},{4,0},{8,12},{12,8},{16,20},{20,16},{24,28},{28,24},{1,5},{5... | collective-permute-start | bytes 294920 | tf_op jit(solution)/shard_map/ppermute | solution.py:20
  2.1 31.4 %collective-permute-start.3 = (bf16[64,768]{1,0:T(8,128)(2,1)}, bf16[64,768]{1,0:T(8,128)(2,1)}, u32[]{:S(2)}, u32[]{:S(2)}) collective-permute-start(bf16[64,768]{1,0:T(8,128)(2,1)} %get-tuple-element.14), channel_id=1, source_target_pairs={{0,8},{4,12},{8,0},{12,4},{16,24},{20,28},{24,16},{28,20},{1,9},{5... | collective-permute-start | bytes 294920 | tf_op jit(solution)/shard_map/ppermute | solution.py:20
  4.6 24.0 %collective-permute-start.24 = (bf16[64,768]{1,0:T(8,128)(2,1)}, bf16[64,768]{1,0:T(8,128)(2,1)}, u32[]{:S(2)}, u32[]{:S(2)}) collective-permute-start(bf16[64,768]{1,0:T(8,128)(2,1)} %get-tuple-element.15), channel_id=1, source_target_pairs={{0,4},{4,0},{8,12},{12,8},{16,20},{20,16},{24,28},{28,24},{1,5},{5... | collective-permute-start | bytes 294920 | tf_op jit(solution)/shard_map/ppermute | solution.py:20
  4.8 26.4 %collective-permute-start.25 = (bf16[64,768]{1,0:T(8,128)(2,1)}, bf16[64,768]{1,0:T(8,128)(2,1)}, u32[]{:S(2)}, u32[]{:S(2)}) collective-permute-start(bf16[64,768]{1,0:T(8,128)(2,1)} %get-tuple-element.15), channel_id=1, source_target_pairs={{0,8},{4,12},{8,0},{12,4},{16,24},{20,28},{24,16},{28,20},{1,9},{5... | collective-permute-start | bytes 294920 | tf_op jit(solution)/shard_map/ppermute | solution.py:20
  8.3 28.9 %collective-permute-start.5 = (bf16[768,768]{1,0:T(8,128)(2,1)}, bf16[768,768]{1,0:T(8,128)(2,1)}, u32[]{:S(2)}, u32[]{:S(2)}) collective-permute-start(bf16[768,768]{1,0:T(8,128)(2,1)} %get-tuple-element.13), channel_id=1, source_target_pairs={{0,8},{4,12},{8,0},{12,4},{16,24},{20,28},{24,16},{28,20},{1,9},{5... | collective-permute-start | bytes 3538952 | tf_op jit(solution)/shard_map/ppermute | solution.py:20
  26.4 14.8 %collective-permute-start.1 = (s32[4,4]{1,0:T(4,128)}, s32[4,4]{1,0:T(4,128)}, u32[]{:S(2)}, u32[]{:S(2)}) collective-permute-start(s32[4,4]{1,0:T(4,128)} %get-tuple-element.16), channel_id=1, source_target_pairs={{0,4},{4,0},{8,12},{12,8},{16,20},{20,16},{24,28},{28,24},{1,5},{5... | collective-permute-start | bytes 200 | tf_op jit(solution)/shard_map/ppermute | solution.py:20
  28.6 12.6 %collective-permute-start.2 = (bf16[768,768]{1,0:T(8,128)(2,1)}, bf16[768,768]{1,0:T(8,128)(2,1)}, u32[]{:S(2)}, u32[]{:S(2)}) collective-permute-start(bf16[768,768]{1,0:T(8,128)(2,1)} %get-tuple-element.12), channel_id=1, source_target_pairs={{0,4},{4,0},{8,12},{12,8},{16,20},{20,16},{24,28},{28,24},{1,5},{5... | collective-permute-start | bytes 3538952 | tf_op jit(solution)/shard_map/ppermute | solution.py:20
  31.2 5.5 %collective-permute-start.4 = (s32[4,4]{1,0:T(4,128)S(1)}, s32[4,4]{1,0:T(4,128)S(1)}, u32[]{:S(2)}, u32[]{:S(2)}) collective-permute-start(s32[4,4]{1,0:T(4,128)S(1)} %copy-done.21), channel_id=1, source_target_pairs={{0,8},{4,12},{8,0},{12,4},{16,24},{20,28},{24,16},{28,20},{1,9},{5... | collective-permute-start | bytes 200 | tf_op jit(solution)/shard_map/ppermute | solution.py:20
  44.9 5.6 %collective-permute-start.27 = (bf16[64,768]{1,0:T(8,128)(2,1)S(1)}, bf16[64,768]{1,0:T(8,128)(2,1)S(1)}, u32[]{:S(2)}, u32[]{:S(2)}) collective-permute-start(bf16[64,768]{1,0:T(8,128)(2,1)S(1)} %get-tuple-element.18), channel_id=1, source_target_pairs={{0,8},{4,12},{8,0},{12,4},{16,24},{20,28},{24,16},{28,20},{1,9},{5... | collective-permute-start | bytes 294920 | tf_op jit(solution)/shard_map/ppermute | solution.py:20
  49.1 5.7 %collective-permute-start.7 = (bf16[64,768]{1,0:T(8,128)(2,1)S(1)}, bf16[64,768]{1,0:T(8,128)(2,1)S(1)}, u32[]{:S(2)}, u32[]{:S(2)}) collective-permute-start(bf16[64,768]{1,0:T(8,128)(2,1)S(1)} %get-tuple-element.32), channel_id=1, source_target_pairs={{0,8},{4,12},{8,0},{12,4},{16,24},{20,28},{24,16},{28,20},{1,9},{5... | collective-permute-start | bytes 294920 | tf_op jit(solution)/shard_map/ppermute | solution.py:20
  49.5 6.1 %collective-permute-start.6 = (bf16[64,768]{1,0:T(8,128)(2,1)S(1)}, bf16[64,768]{1,0:T(8,128)(2,1)S(1)}, u32[]{:S(2)}, u32[]{:S(2)}) collective-permute-start(bf16[64,768]{1,0:T(8,128)(2,1)S(1)} %get-tuple-element.32), channel_id=1, source_target_pairs={{0,4},{4,0},{8,12},{12,8},{16,20},{20,16},{24,28},{28,24},{1,5},{5... | collective-permute-start | bytes 294920 | tf_op jit(solution)/shard_map/ppermute | solution.py:20
  52.7 7.7 %collective-permute-start.29 = (bf16[64,768]{1,0:T(8,128)(2,1)S(1)}, bf16[64,768]{1,0:T(8,128)(2,1)S(1)}, u32[]{:S(2)}, u32[]{:S(2)}) collective-permute-start(bf16[64,768]{1,0:T(8,128)(2,1)S(1)} %get-tuple-element.20), channel_id=1, source_target_pairs={{0,8},{4,12},{8,0},{12,4},{16,24},{20,28},{24,16},{28,20},{1,9},{5... | collective-permute-start | bytes 294920 | tf_op jit(solution)/shard_map/ppermute | solution.py:20
  54.4 8.4 %collective-permute-start.28 = (bf16[64,768]{1,0:T(8,128)(2,1)S(1)}, bf16[64,768]{1,0:T(8,128)(2,1)S(1)}, u32[]{:S(2)}, u32[]{:S(2)}) collective-permute-start(bf16[64,768]{1,0:T(8,128)(2,1)S(1)} %get-tuple-element.20), channel_id=1, source_target_pairs={{0,4},{4,0},{8,12},{12,8},{16,20},{20,16},{24,28},{28,24},{1,5},{5... | collective-permute-start | bytes 294920 | tf_op jit(solution)/shard_map/ppermute | solution.py:20
  56.5 10.0 %collective-permute-start.13 = (bf16[64,768]{1,0:T(8,128)(2,1)S(1)}, bf16[64,768]{1,0:T(8,128)(2,1)S(1)}, u32[]{:S(2)}, u32[]{:S(2)}) collective-permute-start(bf16[64,768]{1,0:T(8,128)(2,1)S(1)} %convert_element_type.132), channel_id=1, source_target_pairs={{0,8},{4,12},{8,0},{12,4},{16,24},{20,28},{24,16},{28,20},{1,9},{5... | collective-permute-start | bytes 294920 | tf_op jit(solution)/shard_map/ppermute | solution.py:20
  57.0 12.0 %collective-permute-start.12 = (bf16[64,768]{1,0:T(8,128)(2,1)S(1)}, bf16[64,768]{1,0:T(8,128)(2,1)S(1)}, u32[]{:S(2)}, u32[]{:S(2)}) collective-permute-start(bf16[64,768]{1,0:T(8,128)(2,1)S(1)} %convert_element_type.132), channel_id=1, source_target_pairs={{0,4},{4,0},{8,12},{12,8},{16,20},{20,16},{24,28},{28,24},{1,5},{5... | collective-permute-start | bytes 294920 | tf_op jit(solution)/shard_map/ppermute | solution.py:20
  57.6 17.1 %collective-permute-start.9 = (bf16[3,256,128]{2,1,0:T(8,128)(2,1)S(1)}, bf16[3,256,128]{2,1,0:T(8,128)(2,1)S(1)}, u32[]{:S(2)}, u32[]{:S(2)}) collective-permute-start(bf16[3,256,128]{2,1,0:T(8,128)(2,1)S(1)} %slice_select_fusion), channel_id=1, source_target_pairs={{0,2},{1,3},{2,0},{3,1},{4,6},{5,7},{6,4},{7,5},{8,10},{9,11},{10,... | collective-permute-start | bytes 589832 | tf_op jit(solution)/shard_map/ppermute | solution.py:39
  60.4 16.0 %collective-permute-start.8 = (bf16[3,256,128]{2,1,0:T(8,128)(2,1)S(1)}, bf16[3,256,128]{2,1,0:T(8,128)(2,1)S(1)}, u32[]{:S(2)}, u32[]{:S(2)}) collective-permute-start(bf16[3,256,128]{2,1,0:T(8,128)(2,1)S(1)} %slice_select_fusion), channel_id=1, source_target_pairs={{0,1},{1,2},{2,3},{3,0},{4,5},{5,6},{6,7},{7,4},{8,9},{9,10},{10,1... | collective-permute-start | bytes 589832 | tf_op jit(solution)/shard_map/ppermute | solution.py:39
  62.8 14.1 %collective-permute-start.10 = (bf16[3,256,128]{2,1,0:T(8,128)(2,1)S(1)}, bf16[3,256,128]{2,1,0:T(8,128)(2,1)S(1)}, u32[]{:S(2)}, u32[]{:S(2)}) collective-permute-start(bf16[3,256,128]{2,1,0:T(8,128)(2,1)S(1)} %slice_select_fusion), channel_id=1, source_target_pairs={{0,3},{1,0},{2,1},{3,2},{4,7},{5,4},{6,5},{7,6},{8,11},{9,8},{10,9... | collective-permute-start | bytes 589832 | tf_op jit(solution)/shard_map/ppermute | solution.py:39
  66.5 11.4 %collective-permute-start.31 = (bf16[64,768]{1,0:T(8,128)(2,1)S(1)}, bf16[64,768]{1,0:T(8,128)(2,1)S(1)}, u32[]{:S(2)}, u32[]{:S(2)}) collective-permute-start(bf16[64,768]{1,0:T(8,128)(2,1)S(1)} %get-tuple-element.22), channel_id=1, source_target_pairs={{0,8},{4,12},{8,0},{12,4},{16,24},{20,28},{24,16},{28,20},{1,9},{5... | collective-permute-start | bytes 294920 | tf_op jit(solution)/shard_map/ppermute | solution.py:20
  68.9 9.9 %collective-permute-start.30 = (bf16[64,768]{1,0:T(8,128)(2,1)S(1)}, bf16[64,768]{1,0:T(8,128)(2,1)S(1)}, u32[]{:S(2)}, u32[]{:S(2)}) collective-permute-start(bf16[64,768]{1,0:T(8,128)(2,1)S(1)} %get-tuple-element.22), channel_id=1, source_target_pairs={{0,4},{4,0},{8,12},{12,8},{16,20},{20,16},{24,28},{28,24},{1,5},{5... | collective-permute-start | bytes 294920 | tf_op jit(solution)/shard_map/ppermute | solution.py:20
  74.7 7.0 %collective-permute-start.15 = (bf16[64,768]{1,0:T(8,128)(2,1)S(1)}, bf16[64,768]{1,0:T(8,128)(2,1)S(1)}, u32[]{:S(2)}, u32[]{:S(2)}) collective-permute-start(bf16[64,768]{1,0:T(8,128)(2,1)S(1)} %get-tuple-element.34), channel_id=1, source_target_pairs={{0,8},{4,12},{8,0},{12,4},{16,24},{20,28},{24,16},{28,20},{1,9},{5... | collective-permute-start | bytes 294920 | tf_op jit(solution)/shard_map/ppermute | solution.py:20
  76.4 6.2 %collective-permute-start.14 = (bf16[64,768]{1,0:T(8,128)(2,1)S(1)}, bf16[64,768]{1,0:T(8,128)(2,1)S(1)}, u32[]{:S(2)}, u32[]{:S(2)}) collective-permute-start(bf16[64,768]{1,0:T(8,128)(2,1)S(1)} %get-tuple-element.34), channel_id=1, source_target_pairs={{0,4},{4,0},{8,12},{12,8},{16,20},{20,16},{24,28},{28,24},{1,5},{5... | collective-permute-start | bytes 294920 | tf_op jit(solution)/shard_map/ppermute | solution.py:20
  77.9 56.9 %collective-permute-start.11 = (bf16[4,3,256,128]{3,2,1,0:T(8,128)(2,1)}, bf16[4,3,256,128]{3,2,1,0:T(8,128)(2,1)}, u32[]{:S(2)}, u32[]{:S(2)}) collective-permute-start(bf16[4,3,256,128]{3,2,1,0:T(8,128)(2,1)} %pad_maximum_fusion.3), channel_id=1, source_target_pairs={{0,4},{4,0},{8,12},{12,8},{16,20},{20,16},{24,28},{28,24},{1,5},{5... | collective-permute-start | bytes 2359304 | tf_op jit(solution)/shard_map/ppermute | solution.py:20
  79.6 5.3 %collective-permute-start.33 = (bf16[64,768]{1,0:T(8,128)(2,1)S(1)}, bf16[64,768]{1,0:T(8,128)(2,1)S(1)}, u32[]{:S(2)}, u32[]{:S(2)}) collective-permute-start(bf16[64,768]{1,0:T(8,128)(2,1)S(1)} %get-tuple-element.24), channel_id=1, source_target_pairs={{0,8},{4,12},{8,0},{12,4},{16,24},{20,28},{24,16},{28,20},{1,9},{5... | collective-permute-start | bytes 294920 | tf_op jit(solution)/shard_map/ppermute | solution.py:20
  84.1 5.3 %collective-permute-start.16 = (bf16[64,768]{1,0:T(8,128)(2,1)S(1)}, bf16[64,768]{1,0:T(8,128)(2,1)S(1)}, u32[]{:S(2)}, u32[]{:S(2)}) collective-permute-start(bf16[64,768]{1,0:T(8,128)(2,1)S(1)} %get-tuple-element.36), channel_id=1, source_target_pairs={{0,4},{4,0},{8,12},{12,8},{16,20},{20,16},{24,28},{28,24},{1,5},{5... | collective-permute-start | bytes 294920 | tf_op jit(solution)/shard_map/ppermute | solution.py:20
  90.2 5.3 %collective-permute-start.19 = (bf16[64,768]{1,0:T(8,128)(2,1)S(1)}, bf16[64,768]{1,0:T(8,128)(2,1)S(1)}, u32[]{:S(2)}, u32[]{:S(2)}) collective-permute-start(bf16[64,768]{1,0:T(8,128)(2,1)S(1)} %get-tuple-element.38), channel_id=1, source_target_pairs={{0,8},{4,12},{8,0},{12,4},{16,24},{20,28},{24,16},{28,20},{1,9},{5... | collective-permute-start | bytes 294920 | tf_op jit(solution)/shard_map/ppermute | solution.py:20
  90.8 5.5 %collective-permute-start.18 = (bf16[64,768]{1,0:T(8,128)(2,1)S(1)}, bf16[64,768]{1,0:T(8,128)(2,1)S(1)}, u32[]{:S(2)}, u32[]{:S(2)}) collective-permute-start(bf16[64,768]{1,0:T(8,128)(2,1)S(1)} %get-tuple-element.38), channel_id=1, source_target_pairs={{0,4},{4,0},{8,12},{12,8},{16,20},{20,16},{24,28},{28,24},{1,5},{5... | collective-permute-start | bytes 294920 | tf_op jit(solution)/shard_map/ppermute | solution.py:20
  101.4 8.0 %collective-permute-start.38 = (bf16[64,768]{1,0:T(8,128)(2,1)S(1)}, bf16[64,768]{1,0:T(8,128)(2,1)S(1)}, u32[]{:S(2)}, u32[]{:S(2)}) collective-permute-start(bf16[64,768]{1,0:T(8,128)(2,1)S(1)} %get-tuple-element.30), channel_id=1, source_target_pairs={{0,4},{4,0},{8,12},{12,8},{16,20},{20,16},{24,28},{28,24},{1,5},{5... | collective-permute-start | bytes 294920 | tf_op jit(solution)/shard_map/ppermute | solution.py:20
  104.6 6.0 %collective-permute-start.22 = (bf16[64,768]{1,0:T(8,128)(2,1)S(1)}, bf16[64,768]{1,0:T(8,128)(2,1)S(1)}, u32[]{:S(2)}, u32[]{:S(2)}) collective-permute-start(bf16[64,768]{1,0:T(8,128)(2,1)S(1)} %get-tuple-element.42), channel_id=1, source_target_pairs={{0,4},{4,0},{8,12},{12,8},{16,20},{20,16},{24,28},{28,24},{1,5},{5... | collective-permute-start | bytes 294920 | tf_op jit(solution)/shard_map/ppermute | solution.py:20
  111.8 7.6 %collective-permute-start.42 = (bf16[128,768]{1,0:T(8,128)(2,1)S(1)}, bf16[128,768]{1,0:T(8,128)(2,1)S(1)}, u32[]{:S(2)}, u32[]{:S(2)}) collective-permute-start(bf16[128,768]{1,0:T(8,128)(2,1)S(1)} %pad_maximum_fusion.5), channel_id=1, source_target_pairs={{0,3},{1,0},{2,1},{3,2},{4,7},{5,4},{6,5},{7,6},{8,11},{9,8},{10,9... | collective-permute-start | bytes 589832 | tf_op jit(solution)/shard_map/ppermute | solution.py:29
  112.8 21.1 %collective-permute-start.41 = (bf16[128,768]{1,0:T(8,128)(2,1)S(1)}, bf16[128,768]{1,0:T(8,128)(2,1)S(1)}, u32[]{:S(2)}, u32[]{:S(2)}) collective-permute-start(bf16[128,768]{1,0:T(8,128)(2,1)S(1)} %pad_maximum_fusion.5), channel_id=1, source_target_pairs={{0,2},{1,3},{2,0},{3,1},{4,6},{5,7},{6,4},{7,5},{8,10},{9,11},{10,... | collective-permute-start | bytes 589832 | tf_op jit(solution)/shard_map/ppermute | solution.py:29
  116.6 17.4 %collective-permute-start.40 = (bf16[128,768]{1,0:T(8,128)(2,1)S(1)}, bf16[128,768]{1,0:T(8,128)(2,1)S(1)}, u32[]{:S(2)}, u32[]{:S(2)}) collective-permute-start(bf16[128,768]{1,0:T(8,128)(2,1)S(1)} %pad_maximum_fusion.5), channel_id=1, source_target_pairs={{0,1},{1,2},{2,3},{3,0},{4,5},{5,6},{6,7},{7,4},{8,9},{9,10},{10,1... | collective-permute-start | bytes 589832 | tf_op jit(solution)/shard_map/ppermute | solution.py:29
  (47 other events, 175.6 us)

commit v9 on v8

--- a/solution.py
+++ b/solution.py
@@ -91,18 +91,15 @@
         own_pair = jnp.where(own_mask, pair_block[round_index], jnp.zeros((), jnp.bfloat16))
         own_pair_t.append(own_pair)
         other_mask = pattern_mask(shipped_pattern[round_index], other_atoms, own_atoms)
+        other_block = jnp.where(other_mask, shipped[round_index], jnp.zeros((), jnp.bfloat16))
         other_pair.append(
-            jnp.where(other_mask, shipped[round_index], jnp.zeros((), jnp.bfloat16))
+            (other_block.astype(jnp.float32) + own_pair.T.astype(jnp.float32)).astype(jnp.bfloat16)
         )
 
     def apply_operator(values):
         result = jnp.dot(values, diag_sym, preferred_element_type=jnp.float32)
         for round_index in range(ROUNDS):
             other_rows = swapped(values, "atoms", round_index)
-            result = result + lax.dot_general(
-                other_rows, own_pair_t[round_index], (((1,), (1,)), ((), ())),
-                preferred_element_type=jnp.float32,
-            )
             result = result + jnp.dot(
                 other_rows, other_pair[round_index], preferred_element_type=jnp.float32
             )

time: 181 us -> 169 us (0.934)
  matrix products: 57.9 us -> 34.7 us
  local copies, waits for them, and re-layouts: 13.3 us -> 23.5 us
  waiting for transfers between devices: 51.4 us -> 45.1 us
  other arithmetic: 11.3 us -> 14.3 us
  starting transfers between devices: 45.5 us -> 48.5 us
    dot_general x32 -> x0, matrix products: 22.4 us -> none  [apply_operator(): lax.dot_general(other_rows, own_pair_t[round_index], (((1,), (1,)), ((),...]
    ppermute x49, starting transfers between devices: 31.8 us -> 37.7 us  [swapped(): return lax.ppermute(value, axis, pairs)]
    gt x0 -> x2, local copies, waits for them, and re-layouts: none -> 5.17 us  [pattern_mask(): return mask > 0.5]
    ppermute x3, waiting for transfers between devices: 5.05 us -> 0.01 us  [gather_pieces(): pieces.append(lax.ppermute(value, 'bands', pairs))]
    ppermute x3, waiting for transfers between devices: 15.4 us -> 12.4 us  [gather_bands(): pieces.append(lax.ppermute(value, 'bands', pairs))]
    convert_element_type x0 -> x1, other arithmetic: none -> 2.78 us  [body(): (other_block.astype(jnp.float32) + own_pair.T.astype(jnp.float32)).astype...]
    squeeze x2 -> x3, local copies, waits for them, and re-layouts: 3.84 us -> 6.48 us  [the longest x2 5.2 us: body(): shipped = [swapped(pair_block[r], 'atoms', r) for r in range(ROUNDS)]]
    ppermute x0 -> x1, local copies, waits for them, and re-layouts: none -> 2.43 us  [swapped(): return lax.ppermute(value, axis, pairs)]
  transfers between devices with their start and end apart: 55 -> 55, of which waited for: 21 -> 22; matrix products, arithmetic and copies ran while one was open for 36% -> 35% of each run, Pallas kernels for 0% -> 0%
where the time goes in v9:
time: 169 us; the launch traced here: 167 us
  starting transfers between devices  48.5 us (29%)
  waiting for transfers between devices  45.1 us (27%)
  matrix products  34.7 us (21%)
  local copies, waits for them, and re-layouts  23.5 us (14%)
  other arithmetic  14.3 us (8%)
    ppermute x49, starting transfers between devices, swapped(): return lax.ppermute(value, axis, pairs)  37.7 us
    ppermute x49, waiting for transfers between devices, swapped(): return lax.ppermute(value, axis, pairs)  32.6 us
    dot_general x32, matrix products, apply_operator(): jnp.dot(other_rows, other_pair[round_index], preferred_element_type=jnp.f...  14.5 us
    ppermute x3, waiting for transfers between devices, gather_bands(): pieces.append(lax.ppermute(value, 'bands', pairs))  12.4 us
    dot_general x4, matrix products, pattern_mask(): lax.dot_general(per_row.astype(jnp.bfloat16), col_onehot, (((1,), (1,)),...  8.51 us
    dot_general x16, matrix products, apply_operator(): result = jnp.dot(values, diag_sym, preferred_element_type=jnp.float32)  6.65 us
    ppermute x3, starting transfers between devices, gather_pieces(): pieces.append(lax.ppermute(value, 'bands', pairs))  5.65 us
    squeeze x2, local copies, waits for them, and re-layouts, body(): shipped = [swapped(pair_block[r], 'atoms', r) for r in range(ROUNDS)]  5.2 us
  transfers between devices with their start and end apart: 55, of which 22 were waited for; matrix products, arithmetic and copies ran while one was open for 35% of the time, Pallas kernels for 0%

profile of v9, /device:TPU:0, one launch (start us, length us, event | category | flops | bytes accessed | tf_op | source)
XLA Modules:
  0.0 166.8 jit_solution(776917666151871910)
XLA Ops:
  2.1 2.5 %collective-permute-start.5 = (bf16[64,768]{1,0:T(8,128)(2,1)}, bf16[64,768]{1,0:T(8,128)(2,1)}, u32[]{:S(2)}, u32[]{:S(2)}) collective-permute-start(bf16[64,768]{1,0:T(8,128)(2,1)} %get-tuple-element.14), channel_id=1, source_target_pairs={{0,8},{4,12},{8,0},{12,4},{16,24},{20,28},{24,16},{28,20},{1,9},{5... | collective-permute-start | bytes 294920 | tf_op jit(solution)/shard_map/ppermute | solution.py:20
  6.1 2.8 %slice_bitcast_fusion = (bf16[768,768]{1,0:T(8,128)(2,1)}, bf16[1,768,768]{2,1,0:T(8,128)(2,1)S(1)}) fusion(bf16[2,768,768]{2,1,0:T(8,128)(2,1)} %param.8), kind=kLoop, calls=%fused_computation.22 | loop fusion | bytes 4718592 | tf_op jit(solution)/shard_map/squeeze | solution.py:74
  12.4 1.9 %add_multiply_fusion = f32[768,768]{1,0:T(8,128)S(1)} fusion(bf16[768,768]{1,0:T(8,128)(2,1)} %param.7, s32[768]{0:T(1024)S(1)} %get-tuple-element.47), kind=kLoop, calls=%fused_computation.7 | loop fusion | flops 4128768 | bytes 3542016 | tf_op jit(solution)/shard_map/mul | solution.py:81
  16.4 2.4 %copy.23 = bf16[768,768]{0,1:T(8,128)(2,1)} copy(bf16[768,768]{1,0:T(8,128)(2,1)} %get-tuple-element.12) | data formatting | bytes 2359296 | tf_op jit(solution)/shard_map/squeeze | solution.py:74
  18.8 2.4 %copy.20 = pred[768,768]{0,1:T(8,128)(4,1)} copy(pred[768,768]{1,0:T(8,128)(4,1)} %convolution_compare_fusion.1) | data formatting | bytes 1179648 | tf_op jit(solution)/shard_map/gt | solution.py:67
  21.2 2.0 %copy.16 = f32[768,768]{0,1:T(8,128)} copy(f32[768,768]{1,0:T(8,128)S(1)} %add_multiply_fusion) | data formatting | bytes 4718592 | tf_op jit(solution)/shard_map/mul | solution.py:81
  23.2 2.7 %copy.22 = pred[768,768]{0,1:T(32,128)(4,1)} copy(pred[768,768]{1,0:T(32,128)(4,1)} %convolution_compare_fusion) | data formatting | bytes 1179648 | tf_op jit(solution)/shard_map/gt | solution.py:67
  27.7 2.4 %fusion.2 = bf16[768,768]{1,0:T(8,128)(2,1)S(1)} fusion(f32[768,768]{0,1:T(8,128)} %copy.16, s32[768]{0:T(1024)S(1)} %get-tuple-element.47, bf16[768,768]{1,0:T(8,128)(2,1)S(1)} %copy-done), kind=kLoop, calls=%fused_computation.6 | loop fusion | flops 5308416 | bytes 4721664 | tf_op jit(solution)/shard_map/convert_element_type | solution.py:82
  32.2 1.9 %collective-permute-start.3 = (s32[4,4]{1,0:T(4,128)S(1)}, s32[4,4]{1,0:T(4,128)}, u32[]{:S(2)}, u32[]{:S(2)}) collective-permute-start(s32[4,4]{1,0:T(4,128)S(1)} %copy-done.15), channel_id=1, source_target_pairs={{0,8},{4,12},{8,0},{12,4},{16,24},{20,28},{24,16},{28,20},{1,9},{5... | collective-permute-start | bytes 200 | tf_op jit(solution)/shard_map/ppermute | solution.py:20
  34.1 2.7 %fusion.3 = f32[768,768]{1,0:T(8,128)} fusion(s32[768]{0:T(1024)S(1)} %get-tuple-element.47, s32[768]{0:T(1024)S(1)} %convert_reduce_fusion.1, s32[4,4]{1,0:T(4,128)} %collective-permute-done), kind=kOutput, calls=%fused_computation.27 | convolution fusion | flops 4752400 | bytes 2365504 | tf_op jit(solution)/shard_map/dot_general | solution.py:63
  36.8 2.4 %copy.18 = bf16[768,768]{1,0:T(8,128)(2,1)} copy(bf16[768,768]{0,1:T(8,128)(2,1)} %collective-permute-done.1) | data formatting | bytes 2359296 | tf_op jit(solution)/shard_map/ppermute | solution.py:20
  39.3 2.8 %fusion.1 = bf16[768,768]{1,0:T(8,128)(2,1)S(1)} fusion(bf16[768,768]{1,0:T(8,128)(2,1)} %copy.18, f32[768,768]{1,0:T(8,128)} %fusion.3, pred[768,768]{0,1:T(8,128)(4,1)} %copy.20, bf16[1,768,768]{1,2,0:T(8,128)(2,1)S(1)} %copy.25), kind=kLoop, calls=%fused_computation.4 | loop fusion | flops 4128768 | bytes 6488064 | tf_op jit(solution)/shard_map/convert_element_type | solution.py:96
  42.2 2.7 %fusion = bf16[768,768]{1,0:T(8,128)(2,1)S(1)} fusion(bf16[768,768]{1,0:T(8,128)(2,1)} %collective-permute-done.4, pred[768,768]{0,1:T(32,128)(4,1)} %copy.22, bf16[768,768]{0,1:T(8,128)(2,1)} %copy.23, s32[768]{0:T(1024)S(1)} %get-tuple-element.46, s32[768]{0:T(1024)S(1)} %get-tuple-element.47, s32[4,4]{1,0:T(4,128)} %collective-permute-done.3), kind=kOutput, calls=%fused_computation.2 | convolution fusion | flops 8881168 | bytes 4134976 | tf_op jit(solution)/shard_map/dot_general | solution.py:63
  56.6 2.6 %collective-permute-start.9 = (bf16[3,256,128]{2,1,0:T(8,128)(2,1)S(1)}, bf16[3,256,128]{2,1,0:T(8,128)(2,1)S(1)}, u32[]{:S(2)}, u32[]{:S(2)}) collective-permute-start(bf16[3,256,128]{2,1,0:T(8,128)(2,1)S(1)} %slice_select_fusion), channel_id=1, source_target_pairs={{0,2},{1,3},{2,0},{3,1},{4,6},{5,7},{6,4},{7,5},{8,10},{9,11},{10,... | collective-permute-start | bytes 589832 | tf_op jit(solution)/shard_map/ppermute | solution.py:39
  64.2 2.4 %collective-permute-done.13 = bf16[64,768]{1,0:T(8,128)(2,1)S(1)} collective-permute-done((bf16[64,768]{1,0:T(8,128)(2,1)S(1)}, bf16[64,768]{1,0:T(8,128)(2,1)S(1)}, u32[]{:S(2)}, u32[]{:S(2)}) %collective-permute-start.13) | collective-permute-done | bytes 98336 | tf_op jit(solution)/shard_map/ppermute | solution.py:20
  69.2 2.0 %collective-permute-done.29 = bf16[64,768]{1,0:T(8,128)(2,1)S(1)} collective-permute-done((bf16[64,768]{1,0:T(8,128)(2,1)S(1)}, bf16[64,768]{1,0:T(8,128)(2,1)S(1)}, u32[]{:S(2)}, u32[]{:S(2)}) %collective-permute-start.29) | collective-permute-done | bytes 98336 | tf_op jit(solution)/shard_map/ppermute | solution.py:20
  82.5 1.9 %collective-permute-start.19 = (bf16[64,768]{1,0:T(8,128)(2,1)S(1)}, bf16[64,768]{1,0:T(8,128)(2,1)S(1)}, u32[]{:S(2)}, u32[]{:S(2)}) collective-permute-start(bf16[64,768]{1,0:T(8,128)(2,1)S(1)} %get-tuple-element.38), channel_id=1, source_target_pairs={{0,8},{4,12},{8,0},{12,4},{16,24},{20,28},{24,16},{28,20},{1,9},{5... | collective-permute-start | bytes 294920 | tf_op jit(solution)/shard_map/ppermute | solution.py:20
  88.5 1.9 %collective-permute-start.21 = (bf16[64,768]{1,0:T(8,128)(2,1)S(1)}, bf16[64,768]{1,0:T(8,128)(2,1)S(1)}, u32[]{:S(2)}, u32[]{:S(2)}) collective-permute-start(bf16[64,768]{1,0:T(8,128)(2,1)S(1)} %get-tuple-element.40), channel_id=1, source_target_pairs={{0,8},{4,12},{8,0},{12,4},{16,24},{20,28},{24,16},{28,20},{1,9},{5... | collective-permute-start | bytes 294920 | tf_op jit(solution)/shard_map/ppermute | solution.py:20
  100.5 2.2 %collective-permute-done.39 = bf16[64,768]{1,0:T(8,128)(2,1)S(1)} collective-permute-done((bf16[64,768]{1,0:T(8,128)(2,1)S(1)}, bf16[64,768]{1,0:T(8,128)(2,1)S(1)}, u32[]{:S(2)}, u32[]{:S(2)}) %collective-permute-start.39) | collective-permute-done | bytes 98336 | tf_op jit(solution)/shard_map/ppermute | solution.py:20
  103.1 2.7 %collective-permute-start.40 = (bf16[128,768]{1,0:T(8,128)(2,1)S(1)}, bf16[128,768]{1,0:T(8,128)(2,1)S(1)}, u32[]{:S(2)}, u32[]{:S(2)}) collective-permute-start(bf16[128,768]{1,0:T(8,128)(2,1)S(1)} %pad_maximum_fusion.5), channel_id=1, source_target_pairs={{0,1},{1,2},{2,3},{3,0},{4,5},{5,6},{6,7},{7,4},{8,9},{9,10},{10,1... | collective-permute-start | bytes 589832 | tf_op jit(solution)/shard_map/ppermute | solution.py:29
  105.8 2.2 %collective-permute-start.41 = (bf16[128,768]{1,0:T(8,128)(2,1)S(1)}, bf16[128,768]{1,0:T(8,128)(2,1)S(1)}, u32[]{:S(2)}, u32[]{:S(2)}) collective-permute-start(bf16[128,768]{1,0:T(8,128)(2,1)S(1)} %pad_maximum_fusion.5), channel_id=1, source_target_pairs={{0,2},{1,3},{2,0},{3,1},{4,6},{5,7},{6,4},{7,5},{8,10},{9,11},{10,... | collective-permute-start | bytes 589832 | tf_op jit(solution)/shard_map/ppermute | solution.py:29
  108.3 5.0 %collective-permute-done.40 = bf16[128,768]{1,0:T(8,128)(2,1)S(1)} collective-permute-done((bf16[128,768]{1,0:T(8,128)(2,1)S(1)}, bf16[128,768]{1,0:T(8,128)(2,1)S(1)}, u32[]{:S(2)}, u32[]{:S(2)}) %collective-permute-start.40) | collective-permute-done | bytes 196640 | tf_op jit(solution)/shard_map/ppermute | solution.py:29
  113.3 7.4 %collective-permute-done.41 = bf16[128,768]{1,0:T(8,128)(2,1)S(1)} collective-permute-done((bf16[128,768]{1,0:T(8,128)(2,1)S(1)}, bf16[128,768]{1,0:T(8,128)(2,1)S(1)}, u32[]{:S(2)}, u32[]{:S(2)}) %collective-permute-start.41) | collective-permute-done | bytes 196640 | tf_op jit(solution)/shard_map/ppermute | solution.py:29
  122.6 3.8 %maximum_select_fusion = bf16[4,3,512,128]{3,2,1,0:T(8,128)(2,1)S(1)} fusion(bf16[4,3,256,128]{3,2,1,0:T(8,128)(2,1)} %collective-permute-done.11, bf16[1,3,256,128]{3,2,1,0:T(8,128)(2,1)S(1)} %bitcast.216, bf16[1,3,256,128]{3,2,1,0:T(8,128)(2,1)S(1)} %bitcast.214, bf16[1,3,256,128]{3,2,1,0:T(8,128)(2,1)S(1)} %bitcast.212, ...), kind=kLoop, calls=%fused_computation.10 | loop fusion | flops 16515072 | bytes 3145729 | tf_op jit(solution)/shard_map/jit(_where)/select_n | solution.py:129
  130.4 2.2 %collective-permute-done.44 = f32[512]{0:T(512)S(1)} collective-permute-done((f32[512]{0:T(512)S(1)}, f32[512]{0:T(512)S(1)}, u32[]{:S(2)}, u32[]{:S(2)}) %collective-permute-start.44) | collective-permute-done | bytes 2080 | tf_op jit(solution)/shard_map/ppermute | solution.py:20
  134.1 2.1 %collective-permute-done.45 = f32[512]{0:T(512)S(1)} collective-permute-done((f32[512]{0:T(512)S(1)}, f32[512]{0:T(512)S(1)}, u32[]{:S(2)}, u32[]{:S(2)}) %collective-permute-start.45) | collective-permute-done | bytes 2080 | tf_op jit(solution)/shard_map/ppermute | solution.py:20
  140.4 2.2 %collective-permute-done.47 = f32[512]{0:T(512)S(1)} collective-permute-done((f32[512]{0:T(512)S(1)}, f32[512]{0:T(512)S(1)}, u32[]{:S(2)}, u32[]{:S(2)}) %collective-permute-start.47) | collective-permute-done | bytes 2080 | tf_op jit(solution)/shard_map/ppermute | solution.py:20
  144.1 2.1 %collective-permute-done.48 = f32[512]{0:T(512)S(1)} collective-permute-done((f32[512]{0:T(512)S(1)}, f32[512]{0:T(512)S(1)}, u32[]{:S(2)}, u32[]{:S(2)}) %collective-permute-start.48) | collective-permute-done | bytes 2080 | tf_op jit(solution)/shard_map/ppermute | solution.py:20
  150.4 2.2 %collective-permute-done.50 = f32[512]{0:T(512)S(1)} collective-permute-done((f32[512]{0:T(512)S(1)}, f32[512]{0:T(512)S(1)}, u32[]{:S(2)}, u32[]{:S(2)}) %collective-permute-start.50) | collective-permute-done | bytes 2080 | tf_op jit(solution)/shard_map/ppermute | solution.py:20
  154.1 2.1 %collective-permute-done.51 = f32[512]{0:T(512)S(1)} collective-permute-done((f32[512]{0:T(512)S(1)}, f32[512]{0:T(512)S(1)}, u32[]{:S(2)}, u32[]{:S(2)}) %collective-permute-start.51) | collective-permute-done | bytes 2080 | tf_op jit(solution)/shard_map/ppermute | solution.py:20
  160.2 2.1 %collective-permute-done.53 = f32[128]{0:T(128)S(1)} collective-permute-done((f32[128]{0:T(128)S(1)}, f32[128]{0:T(128)S(1)}, u32[]{:S(2)}, u32[]{:S(2)}) %collective-permute-start.53) | collective-permute-done | bytes 544 | tf_op jit(solution)/shard_map/ppermute | solution.py:20
  163.8 2.0 %collective-permute-done.54 = f32[128]{0:T(128)S(1)} collective-permute-done((f32[128]{0:T(128)S(1)}, f32[128]{0:T(128)S(1)}, u32[]{:S(2)}, u32[]{:S(2)}) %collective-permute-start.54) | collective-permute-done | bytes 544 | tf_op jit(solution)/shard_map/ppermute | solution.py:20
  (227 shorter events, 83.4 us)
Async XLA Ops:
  1.6 43.3 %collective-permute-start.2 = (bf16[64,768]{1,0:T(8,128)(2,1)}, bf16[64,768]{1,0:T(8,128)(2,1)}, u32[]{:S(2)}, u32[]{:S(2)}) collective-permute-start(bf16[64,768]{1,0:T(8,128)(2,1)} %get-tuple-element.14), channel_id=1, source_target_pairs={{0,4},{4,0},{8,12},{12,8},{16,20},{20,16},{24,28},{28,24},{1,5},{5... | collective-permute-start | bytes 294920 | tf_op jit(solution)/shard_map/ppermute | solution.py:20
  2.1 44.2 %collective-permute-start.5 = (bf16[64,768]{1,0:T(8,128)(2,1)}, bf16[64,768]{1,0:T(8,128)(2,1)}, u32[]{:S(2)}, u32[]{:S(2)}) collective-permute-start(bf16[64,768]{1,0:T(8,128)(2,1)} %get-tuple-element.14), channel_id=1, source_target_pairs={{0,8},{4,12},{8,0},{12,4},{16,24},{20,28},{24,16},{28,20},{1,9},{5... | collective-permute-start | bytes 294920 | tf_op jit(solution)/shard_map/ppermute | solution.py:20
  5.8 26.3 %collective-permute-start = (s32[4,4]{1,0:T(4,128)}, s32[4,4]{1,0:T(4,128)}, u32[]{:S(2)}, u32[]{:S(2)}) collective-permute-start(s32[4,4]{1,0:T(4,128)} %get-tuple-element.17), channel_id=1, source_target_pairs={{0,4},{4,0},{8,12},{12,8},{16,20},{20,16},{24,28},{28,24},{1,5},{5... | collective-permute-start | bytes 200 | tf_op jit(solution)/shard_map/ppermute | solution.py:20
  9.5 27.3 %collective-permute-start.1 = (bf16[768,768]{0,1:T(8,128)(2,1)S(1)}, bf16[768,768]{0,1:T(8,128)(2,1)}, u32[]{:S(2)}, u32[]{:S(2)}) collective-permute-start(bf16[768,768]{0,1:T(8,128)(2,1)S(1)} %bitcast.208), channel_id=1, source_target_pairs={{0,4},{4,0},{8,12},{12,8},{16,20},{20,16},{24,28},{28,24},{1,5},{5... | collective-permute-start | bytes 3538952 | tf_op jit(solution)/shard_map/ppermute | solution.py:20
  9.9 32.3 %collective-permute-start.4 = (bf16[768,768]{1,0:T(8,128)(2,1)}, bf16[768,768]{1,0:T(8,128)(2,1)}, u32[]{:S(2)}, u32[]{:S(2)}) collective-permute-start(bf16[768,768]{1,0:T(8,128)(2,1)} %get-tuple-element.12), channel_id=1, source_target_pairs={{0,8},{4,12},{8,0},{12,4},{16,24},{20,28},{24,16},{28,20},{1,9},{5... | collective-permute-start | bytes 3538952 | tf_op jit(solution)/shard_map/ppermute | solution.py:20
  32.2 9.9 %collective-permute-start.3 = (s32[4,4]{1,0:T(4,128)S(1)}, s32[4,4]{1,0:T(4,128)}, u32[]{:S(2)}, u32[]{:S(2)}) collective-permute-start(s32[4,4]{1,0:T(4,128)S(1)} %copy-done.15), channel_id=1, source_target_pairs={{0,8},{4,12},{8,0},{12,4},{16,24},{20,28},{24,16},{28,20},{1,9},{5... | collective-permute-start | bytes 200 | tf_op jit(solution)/shard_map/ppermute | solution.py:20
  36.8 13.3 %collective-permute-start.24 = (bf16[64,768]{1,0:T(8,128)(2,1)}, bf16[64,768]{1,0:T(8,128)(2,1)}, u32[]{:S(2)}, u32[]{:S(2)}) collective-permute-start(bf16[64,768]{1,0:T(8,128)(2,1)} %get-tuple-element.15), channel_id=1, source_target_pairs={{0,4},{4,0},{8,12},{12,8},{16,20},{20,16},{24,28},{28,24},{1,5},{5... | collective-permute-start | bytes 294920 | tf_op jit(solution)/shard_map/ppermute | solution.py:20
  42.0 9.3 %collective-permute-start.25 = (bf16[64,768]{1,0:T(8,128)(2,1)}, bf16[64,768]{1,0:T(8,128)(2,1)}, u32[]{:S(2)}, u32[]{:S(2)}) collective-permute-start(bf16[64,768]{1,0:T(8,128)(2,1)} %get-tuple-element.15), channel_id=1, source_target_pairs={{0,8},{4,12},{8,0},{12,4},{16,24},{20,28},{24,16},{28,20},{1,9},{5... | collective-permute-start | bytes 294920 | tf_op jit(solution)/shard_map/ppermute | solution.py:20
  47.9 5.6 %collective-permute-start.6 = (bf16[64,768]{1,0:T(8,128)(2,1)S(1)}, bf16[64,768]{1,0:T(8,128)(2,1)S(1)}, u32[]{:S(2)}, u32[]{:S(2)}) collective-permute-start(bf16[64,768]{1,0:T(8,128)(2,1)S(1)} %get-tuple-element.32), channel_id=1, source_target_pairs={{0,4},{4,0},{8,12},{12,8},{16,20},{20,16},{24,28},{28,24},{1,5},{5... | collective-permute-start | bytes 294920 | tf_op jit(solution)/shard_map/ppermute | solution.py:20
  48.4 5.5 %collective-permute-start.7 = (bf16[64,768]{1,0:T(8,128)(2,1)S(1)}, bf16[64,768]{1,0:T(8,128)(2,1)S(1)}, u32[]{:S(2)}, u32[]{:S(2)}) collective-permute-start(bf16[64,768]{1,0:T(8,128)(2,1)S(1)} %get-tuple-element.32), channel_id=1, source_target_pairs={{0,8},{4,12},{8,0},{12,4},{16,24},{20,28},{24,16},{28,20},{1,9},{5... | collective-permute-start | bytes 294920 | tf_op jit(solution)/shard_map/ppermute | solution.py:20
  52.9 7.9 %collective-permute-start.26 = (bf16[64,768]{1,0:T(8,128)(2,1)S(1)}, bf16[64,768]{1,0:T(8,128)(2,1)S(1)}, u32[]{:S(2)}, u32[]{:S(2)}) collective-permute-start(bf16[64,768]{1,0:T(8,128)(2,1)S(1)} %get-tuple-element.18), channel_id=1, source_target_pairs={{0,4},{4,0},{8,12},{12,8},{16,20},{20,16},{24,28},{28,24},{1,5},{5... | collective-permute-start | bytes 294920 | tf_op jit(solution)/shard_map/ppermute | solution.py:20
  53.0 8.3 %collective-permute-start.27 = (bf16[64,768]{1,0:T(8,128)(2,1)S(1)}, bf16[64,768]{1,0:T(8,128)(2,1)S(1)}, u32[]{:S(2)}, u32[]{:S(2)}) collective-permute-start(bf16[64,768]{1,0:T(8,128)(2,1)S(1)} %get-tuple-element.18), channel_id=1, source_target_pairs={{0,8},{4,12},{8,0},{12,4},{16,24},{20,28},{24,16},{28,20},{1,9},{5... | collective-permute-start | bytes 294920 | tf_op jit(solution)/shard_map/ppermute | solution.py:20
  54.9 18.5 %collective-permute-start.8 = (bf16[3,256,128]{2,1,0:T(8,128)(2,1)S(1)}, bf16[3,256,128]{2,1,0:T(8,128)(2,1)S(1)}, u32[]{:S(2)}, u32[]{:S(2)}) collective-permute-start(bf16[3,256,128]{2,1,0:T(8,128)(2,1)S(1)} %slice_select_fusion), channel_id=1, source_target_pairs={{0,1},{1,2},{2,3},{3,0},{4,5},{5,6},{6,7},{7,4},{8,9},{9,10},{10,1... | collective-permute-start | bytes 589832 | tf_op jit(solution)/shard_map/ppermute | solution.py:39
  56.6 16.9 %collective-permute-start.9 = (bf16[3,256,128]{2,1,0:T(8,128)(2,1)S(1)}, bf16[3,256,128]{2,1,0:T(8,128)(2,1)S(1)}, u32[]{:S(2)}, u32[]{:S(2)}) collective-permute-start(bf16[3,256,128]{2,1,0:T(8,128)(2,1)S(1)} %slice_select_fusion), channel_id=1, source_target_pairs={{0,2},{1,3},{2,0},{3,1},{4,6},{5,7},{6,4},{7,5},{8,10},{9,11},{10,... | collective-permute-start | bytes 589832 | tf_op jit(solution)/shard_map/ppermute | solution.py:39
  59.2 14.9 %collective-permute-start.10 = (bf16[3,256,128]{2,1,0:T(8,128)(2,1)S(1)}, bf16[3,256,128]{2,1,0:T(8,128)(2,1)S(1)}, u32[]{:S(2)}, u32[]{:S(2)}) collective-permute-start(bf16[3,256,128]{2,1,0:T(8,128)(2,1)S(1)} %slice_select_fusion), channel_id=1, source_target_pairs={{0,3},{1,0},{2,1},{3,2},{4,7},{5,4},{6,5},{7,6},{8,11},{9,8},{10,9... | collective-permute-start | bytes 589832 | tf_op jit(solution)/shard_map/ppermute | solution.py:39
  61.4 5.2 %collective-permute-start.13 = (bf16[64,768]{1,0:T(8,128)(2,1)S(1)}, bf16[64,768]{1,0:T(8,128)(2,1)S(1)}, u32[]{:S(2)}, u32[]{:S(2)}) collective-permute-start(bf16[64,768]{1,0:T(8,128)(2,1)S(1)} %convert_element_type.164), channel_id=1, source_target_pairs={{0,8},{4,12},{8,0},{12,4},{16,24},{20,28},{24,16},{28,20},{1,9},{5... | collective-permute-start | bytes 294920 | tf_op jit(solution)/shard_map/ppermute | solution.py:20
  68.4 6.8 %collective-permute-start.14 = (bf16[64,768]{1,0:T(8,128)(2,1)S(1)}, bf16[64,768]{1,0:T(8,128)(2,1)S(1)}, u32[]{:S(2)}, u32[]{:S(2)}) collective-permute-start(bf16[64,768]{1,0:T(8,128)(2,1)S(1)} %get-tuple-element.34), channel_id=1, source_target_pairs={{0,4},{4,0},{8,12},{12,8},{16,20},{20,16},{24,28},{28,24},{1,5},{5... | collective-permute-start | bytes 294920 | tf_op jit(solution)/shard_map/ppermute | solution.py:20
  73.5 5.2 %collective-permute-start.31 = (bf16[64,768]{1,0:T(8,128)(2,1)S(1)}, bf16[64,768]{1,0:T(8,128)(2,1)S(1)}, u32[]{:S(2)}, u32[]{:S(2)}) collective-permute-start(bf16[64,768]{1,0:T(8,128)(2,1)S(1)} %get-tuple-element.22), channel_id=1, source_target_pairs={{0,8},{4,12},{8,0},{12,4},{16,24},{20,28},{24,16},{28,20},{1,9},{5... | collective-permute-start | bytes 294920 | tf_op jit(solution)/shard_map/ppermute | solution.py:20
  75.1 46.4 %collective-permute-start.11 = (bf16[4,3,256,128]{3,2,1,0:T(8,128)(2,1)}, bf16[4,3,256,128]{3,2,1,0:T(8,128)(2,1)}, u32[]{:S(2)}, u32[]{:S(2)}) collective-permute-start(bf16[4,3,256,128]{3,2,1,0:T(8,128)(2,1)} %pad_maximum_fusion.3), channel_id=1, source_target_pairs={{0,4},{4,0},{8,12},{12,8},{16,20},{20,16},{24,28},{28,24},{1,5},{5... | collective-permute-start | bytes 2359304 | tf_op jit(solution)/shard_map/ppermute | solution.py:20
  76.7 5.0 %collective-permute-start.17 = (bf16[64,768]{1,0:T(8,128)(2,1)S(1)}, bf16[64,768]{1,0:T(8,128)(2,1)S(1)}, u32[]{:S(2)}, u32[]{:S(2)}) collective-permute-start(bf16[64,768]{1,0:T(8,128)(2,1)S(1)} %get-tuple-element.36), channel_id=1, source_target_pairs={{0,8},{4,12},{8,0},{12,4},{16,24},{20,28},{24,16},{28,20},{1,9},{5... | collective-permute-start | bytes 294920 | tf_op jit(solution)/shard_map/ppermute | solution.py:20
  79.3 5.1 %collective-permute-start.32 = (bf16[64,768]{1,0:T(8,128)(2,1)S(1)}, bf16[64,768]{1,0:T(8,128)(2,1)S(1)}, u32[]{:S(2)}, u32[]{:S(2)}) collective-permute-start(bf16[64,768]{1,0:T(8,128)(2,1)S(1)} %get-tuple-element.24), channel_id=1, source_target_pairs={{0,4},{4,0},{8,12},{12,8},{16,20},{20,16},{24,28},{28,24},{1,5},{5... | collective-permute-start | bytes 294920 | tf_op jit(solution)/shard_map/ppermute | solution.py:20
  79.5 5.2 %collective-permute-start.33 = (bf16[64,768]{1,0:T(8,128)(2,1)S(1)}, bf16[64,768]{1,0:T(8,128)(2,1)S(1)}, u32[]{:S(2)}, u32[]{:S(2)}) collective-permute-start(bf16[64,768]{1,0:T(8,128)(2,1)S(1)} %get-tuple-element.24), channel_id=1, source_target_pairs={{0,8},{4,12},{8,0},{12,4},{16,24},{20,28},{24,16},{28,20},{1,9},{5... | collective-permute-start | bytes 294920 | tf_op jit(solution)/shard_map/ppermute | solution.py:20
  82.5 5.3 %collective-permute-start.19 = (bf16[64,768]{1,0:T(8,128)(2,1)S(1)}, bf16[64,768]{1,0:T(8,128)(2,1)S(1)}, u32[]{:S(2)}, u32[]{:S(2)}) collective-permute-start(bf16[64,768]{1,0:T(8,128)(2,1)S(1)} %get-tuple-element.38), channel_id=1, source_target_pairs={{0,8},{4,12},{8,0},{12,4},{16,24},{20,28},{24,16},{28,20},{1,9},{5... | collective-permute-start | bytes 294920 | tf_op jit(solution)/shard_map/ppermute | solution.py:20
  85.4 5.0 %collective-permute-start.34 = (bf16[64,768]{1,0:T(8,128)(2,1)S(1)}, bf16[64,768]{1,0:T(8,128)(2,1)S(1)}, u32[]{:S(2)}, u32[]{:S(2)}) collective-permute-start(bf16[64,768]{1,0:T(8,128)(2,1)S(1)} %get-tuple-element.26), channel_id=1, source_target_pairs={{0,4},{4,0},{8,12},{12,8},{16,20},{20,16},{24,28},{28,24},{1,5},{5... | collective-permute-start | bytes 294920 | tf_op jit(solution)/shard_map/ppermute | solution.py:20
  85.6 5.1 %collective-permute-start.35 = (bf16[64,768]{1,0:T(8,128)(2,1)S(1)}, bf16[64,768]{1,0:T(8,128)(2,1)S(1)}, u32[]{:S(2)}, u32[]{:S(2)}) collective-permute-start(bf16[64,768]{1,0:T(8,128)(2,1)S(1)} %get-tuple-element.26), channel_id=1, source_target_pairs={{0,8},{4,12},{8,0},{12,4},{16,24},{20,28},{24,16},{28,20},{1,9},{5... | collective-permute-start | bytes 294920 | tf_op jit(solution)/shard_map/ppermute | solution.py:20
  88.5 5.3 %collective-permute-start.21 = (bf16[64,768]{1,0:T(8,128)(2,1)S(1)}, bf16[64,768]{1,0:T(8,128)(2,1)S(1)}, u32[]{:S(2)}, u32[]{:S(2)}) collective-permute-start(bf16[64,768]{1,0:T(8,128)(2,1)S(1)} %get-tuple-element.40), channel_id=1, source_target_pairs={{0,8},{4,12},{8,0},{12,4},{16,24},{20,28},{24,16},{28,20},{1,9},{5... | collective-permute-start | bytes 294920 | tf_op jit(solution)/shard_map/ppermute | solution.py:20
  91.7 5.1 %collective-permute-start.37 = (bf16[64,768]{1,0:T(8,128)(2,1)S(1)}, bf16[64,768]{1,0:T(8,128)(2,1)S(1)}, u32[]{:S(2)}, u32[]{:S(2)}) collective-permute-start(bf16[64,768]{1,0:T(8,128)(2,1)S(1)} %get-tuple-element.28), channel_id=1, source_target_pairs={{0,8},{4,12},{8,0},{12,4},{16,24},{20,28},{24,16},{28,20},{1,9},{5... | collective-permute-start | bytes 294920 | tf_op jit(solution)/shard_map/ppermute | solution.py:20
  94.6 5.2 %collective-permute-start.23 = (bf16[64,768]{1,0:T(8,128)(2,1)S(1)}, bf16[64,768]{1,0:T(8,128)(2,1)S(1)}, u32[]{:S(2)}, u32[]{:S(2)}) collective-permute-start(bf16[64,768]{1,0:T(8,128)(2,1)S(1)} %get-tuple-element.42), channel_id=1, source_target_pairs={{0,8},{4,12},{8,0},{12,4},{16,24},{20,28},{24,16},{28,20},{1,9},{5... | collective-permute-start | bytes 294920 | tf_op jit(solution)/shard_map/ppermute | solution.py:20
  97.7 5.0 %collective-permute-start.39 = (bf16[64,768]{1,0:T(8,128)(2,1)S(1)}, bf16[64,768]{1,0:T(8,128)(2,1)S(1)}, u32[]{:S(2)}, u32[]{:S(2)}) collective-permute-start(bf16[64,768]{1,0:T(8,128)(2,1)S(1)} %get-tuple-element.30), channel_id=1, source_target_pairs={{0,8},{4,12},{8,0},{12,4},{16,24},{20,28},{24,16},{28,20},{1,9},{5... | collective-permute-start | bytes 294920 | tf_op jit(solution)/shard_map/ppermute | solution.py:20
  103.1 10.2 %collective-permute-start.40 = (bf16[128,768]{1,0:T(8,128)(2,1)S(1)}, bf16[128,768]{1,0:T(8,128)(2,1)S(1)}, u32[]{:S(2)}, u32[]{:S(2)}) collective-permute-start(bf16[128,768]{1,0:T(8,128)(2,1)S(1)} %pad_maximum_fusion.5), channel_id=1, source_target_pairs={{0,1},{1,2},{2,3},{3,0},{4,5},{5,6},{6,7},{7,4},{8,9},{9,10},{10,1... | collective-permute-start | bytes 589832 | tf_op jit(solution)/shard_map/ppermute | solution.py:29
  105.8 14.9 %collective-permute-start.41 = (bf16[128,768]{1,0:T(8,128)(2,1)S(1)}, bf16[128,768]{1,0:T(8,128)(2,1)S(1)}, u32[]{:S(2)}, u32[]{:S(2)}) collective-permute-start(bf16[128,768]{1,0:T(8,128)(2,1)S(1)} %pad_maximum_fusion.5), channel_id=1, source_target_pairs={{0,2},{1,3},{2,0},{3,1},{4,6},{5,7},{6,4},{7,5},{8,10},{9,11},{10,... | collective-permute-start | bytes 589832 | tf_op jit(solution)/shard_map/ppermute | solution.py:29
  108.0 12.7 %collective-permute-start.42 = (bf16[128,768]{1,0:T(8,128)(2,1)S(1)}, bf16[128,768]{1,0:T(8,128)(2,1)S(1)}, u32[]{:S(2)}, u32[]{:S(2)}) collective-permute-start(bf16[128,768]{1,0:T(8,128)(2,1)S(1)} %pad_maximum_fusion.5), channel_id=1, source_target_pairs={{0,3},{1,0},{2,1},{3,2},{4,7},{5,4},{6,5},{7,6},{8,11},{9,8},{10,9... | collective-permute-start | bytes 589832 | tf_op jit(solution)/shard_map/ppermute | solution.py:29
  (40 other events, 123.5 us)

commit v10 on v4

--- a/solution.py
+++ b/solution.py
@@ -76,33 +76,32 @@
     own_atoms = atom_index(
         lax.dynamic_index_in_dim(atom_sizes, atoms_here, 0, keepdims=False), orb_dev
     )
-    upper_flag = (own_atoms[:, None] < own_atoms[None, :]).astype(jnp.float32)
-    same_atom = (own_atoms[:, None] == own_atoms[None, :]).astype(jnp.float32)
-    upper_part = diag_block.astype(jnp.float32) * (upper_flag + 0.5 * same_atom)
-    diag_sym = (upper_part + upper_part.T).astype(jnp.bfloat16)
-    own_pair_t = []
+    row_atom = own_atoms[:, None]
+    col_atom = own_atoms[None, :]
+    same_atom = 0.5 * (row_atom == col_atom).astype(jnp.float32)
+    weight = (row_atom < col_atom).astype(jnp.float32) + same_atom
+    weight_t = (col_atom < row_atom).astype(jnp.float32) + same_atom
+    diag_sym = (
+        diag_block.astype(jnp.float32) * weight + diag_block.T.astype(jnp.float32) * weight_t
+    ).astype(jnp.bfloat16)
     other_pair = []
     for round_index in range(ROUNDS):
         partner = jnp.bitwise_xor(atoms_here, 1 << round_index)
         other_atoms = atom_index(
             lax.dynamic_index_in_dim(atom_sizes, partner, 0, keepdims=False), orb_dev
         )
-        own_mask = pattern_mask(pair_pattern[round_index], own_atoms, other_atoms)
-        own_pair = jnp.where(own_mask, pair_block[round_index], jnp.zeros((), jnp.bfloat16))
-        own_pair_t.append(own_pair)
+        own_mask_t = pattern_mask(pair_pattern[round_index].T, other_atoms, own_atoms)
+        own_block_t = jnp.where(own_mask_t, pair_block[round_index].T, jnp.zeros((), jnp.bfloat16))
         other_mask = pattern_mask(shipped_pattern[round_index], other_atoms, own_atoms)
+        other_block = jnp.where(other_mask, shipped[round_index], jnp.zeros((), jnp.bfloat16))
         other_pair.append(
-            jnp.where(other_mask, shipped[round_index], jnp.zeros((), jnp.bfloat16))
+            (other_block.astype(jnp.float32) + own_block_t.astype(jnp.float32)).astype(jnp.bfloat16)
         )
 
     def apply_operator(values):
         result = jnp.dot(values, diag_sym, preferred_element_type=jnp.float32)
         for round_index in range(ROUNDS):
             other_rows = swapped(values, "atoms", round_index)
-            result = result + lax.dot_general(
-                other_rows, own_pair_t[round_index], (((1,), (1,)), ((), ())),
-                preferred_element_type=jnp.float32,
-            )
             result = result + jnp.dot(
                 other_rows, other_pair[round_index], preferred_element_type=jnp.float32
             )

time: 179 us -> 170 us (0.950)
  matrix products: 57.9 us -> 36.1 us
  waiting for transfers between devices: 50.5 us -> 61.7 us
  starting transfers between devices: 47.8 us -> 43.7 us
  other arithmetic: 8.44 us -> 11.4 us
  local copies, waits for them, and re-layouts: 12.5 us -> 14.7 us
    dot_general x32 -> x0, matrix products: 22.4 us -> none  [apply_operator(): lax.dot_general(other_rows, own_pair_t[round_index], (((1,), (1,)), ((),...]
    ppermute x48, waiting for transfers between devices: 34.3 us -> 52.5 us  [swapped(): return lax.ppermute(value, axis, pairs)]
    ppermute x3, waiting for transfers between devices: 16.2 us -> 9.14 us  [gather_bands(): pieces.append(lax.ppermute(value, 'bands', pairs))]
    ppermute x48, starting transfers between devices: 38.7 us -> 34.1 us  [swapped(): return lax.ppermute(value, axis, pairs)]
    convert_element_type x1 -> x3, other arithmetic: 2.02 us -> 6.37 us  [the longest x1 2.45 us: body(): (other_block.astype(jnp.float32) + own_block_t.astype(jnp.float32)).astyp...]
    convert_element_type x0 -> x1, local copies, waits for them, and re-layouts: none -> 2.03 us  [body(): diag_block.T.astype(jnp.float32) * weight_t]
    mul x1 -> x0, local copies, waits for them, and re-layouts: 2.03 us -> none  [body(): upper_part = diag_block.astype(jnp.float32) * (upper_flag + 0.5 * same_atom)]
    mul x1 -> x0, other arithmetic: 2.01 us -> none  [body(): upper_part = diag_block.astype(jnp.float32) * (upper_flag + 0.5 * same_atom)]
  transfers between devices with their start and end apart: 54 -> 54, of which waited for: 25 -> 29; matrix products, arithmetic and copies ran while one was open for 36% -> 31% of each run, Pallas kernels for 0% -> 0%
where the time goes in v10:
time: 170 us; the launch traced here: 168 us
  waiting for transfers between devices  61.7 us (36%)
  starting transfers between devices  43.7 us (26%)
  matrix products  36.1 us (21%)
  local copies, waits for them, and re-layouts  14.7 us (9%)
  other arithmetic  11.4 us (7%)
    ppermute x48, waiting for transfers between devices, swapped(): return lax.ppermute(value, axis, pairs)  52.5 us
    ppermute x48, starting transfers between devices, swapped(): return lax.ppermute(value, axis, pairs)  34.1 us
    dot_general x32, matrix products, apply_operator(): jnp.dot(other_rows, other_pair[round_index], preferred_element_type=jnp.f...  14.5 us
    dot_general x4, matrix products, pattern_mask(): lax.dot_general(per_row.astype(jnp.bfloat16), col_onehot, (((1,), (1,)),...  9.9 us
    ppermute x3, waiting for transfers between devices, gather_bands(): pieces.append(lax.ppermute(value, 'bands', pairs))  9.14 us
    dot_general x16, matrix products, apply_operator(): result = jnp.dot(values, diag_sym, preferred_element_type=jnp.float32)  6.65 us
    ppermute x3, starting transfers between devices, gather_pieces(): pieces.append(lax.ppermute(value, 'bands', pairs))  5.73 us
    ppermute x3, starting transfers between devices, gather_bands(): pieces.append(lax.ppermute(value, 'bands', pairs))  3.88 us
  transfers between devices with their start and end apart: 54, of which 29 were waited for; matrix products, arithmetic and copies ran while one was open for 31% of the time, Pallas kernels for 0%

profile of v10, /device:TPU:0, one launch (start us, length us, event | category | flops | bytes accessed | tf_op | source)
XLA Modules:
  0.0 168.4 jit_solution(3216368868716380429)
XLA Ops:
  2.1 2.5 %collective-permute-start.5 = (bf16[64,768]{1,0:T(8,128)(2,1)}, bf16[64,768]{1,0:T(8,128)(2,1)}, u32[]{:S(2)}, u32[]{:S(2)}) collective-permute-start(bf16[64,768]{1,0:T(8,128)(2,1)} %get-tuple-element.15), channel_id=1, source_target_pairs={{0,8},{4,12},{8,0},{12,4},{16,24},{20,28},{24,16},{28,20},{1,9},{5... | collective-permute-start | bytes 294920 | tf_op jit(solution)/shard_map/ppermute | solution.py:20
  6.1 3.3 %slice_bitcast_fusion.1 = (bf16[768,768]{1,0:T(8,128)(2,1)}, bf16[768,768]{0,1:T(8,128)(2,1)}, bf16[1,768,768]{2,1,0:T(8,128)(2,1)S(1)}) fusion(bf16[2,768,768]{2,1,0:T(8,128)(2,1)} %param.8), kind=kLoop, calls=%fused_computation.110 | loop fusion | bytes 5898240 | tf_op jit(solution)/shard_map/squeeze | solution.py:74
  13.6 2.0 %copy.12 = f32[768,768]{1,0:T(8,128)S(1)} copy(f32[768,768]{0,1:T(8,128)} %convert_bitcast_fusion) | data formatting | bytes 4718592 | tf_op jit(solution)/shard_map/convert_element_type | solution.py:85
  16.3 2.3 %fusion.1 = bf16[768,768]{1,0:T(8,128)(2,1)S(1)} fusion(bf16[768,768]{1,0:T(8,128)(2,1)} %param.7, f32[768,768]{1,0:T(8,128)S(1)} %copy.12, s32[768]{0:T(1024)S(1)} %get-tuple-element.48), kind=kLoop, calls=%fused_computation.6 | loop fusion | flops 7667712 | bytes 4721664 | tf_op jit(solution)/shard_map/convert_element_type | solution.py:86
  20.7 3.0 %compare_select_fusion.2 = bf16[768,768]{1,0:T(8,128)(2,1)} fusion(bf16[1,768,768]{1,2,0:T(8,128)(2,1)} %copy.17, s32[768]{0:T(1024)S(1)} %get-tuple-element.48, s32[768]{0:T(1024)S(1)} %convert_reduce_fusion.1, s32[2,4,4]{2,1,0:T(4,128)S(1)} %copy-done.11), kind=kOutput, calls=%fused_computation.12 | convolution fusion | flops 5932048 | bytes 2369536 | tf_op jit(solution)/shard_map/dot_general | solution.py:63
  27.3 2.0 %collective-permute-start.3 = (s32[4,4]{1,0:T(4,128)}, s32[4,4]{1,0:T(4,128)S(1)}, u32[]{:S(2)}, u32[]{:S(2)}) collective-permute-start(s32[4,4]{1,0:T(4,128)} %get-tuple-element.17), channel_id=1, source_target_pairs={{0,8},{4,12},{8,0},{12,4},{16,24},{20,28},{24,16},{28,20},{1,9},{5... | collective-permute-start | bytes 200 | tf_op jit(solution)/shard_map/ppermute | solution.py:20
  29.3 2.7 %fusion.3 = f32[768,768]{1,0:T(8,128)} fusion(s32[768]{0:T(1024)S(1)} %get-tuple-element.48, s32[768]{0:T(1024)S(1)} %convert_reduce_fusion.1, s32[4,4]{1,0:T(4,128)} %collective-permute-done), kind=kOutput, calls=%fused_computation.28 | convolution fusion | flops 4752400 | bytes 2365504 | tf_op jit(solution)/shard_map/dot_general | solution.py:63
  33.6 2.5 %add_convert_fusion.1 = bf16[768,768]{1,0:T(8,128)(2,1)S(1)} fusion(bf16[768,768]{1,0:T(8,128)(2,1)} %compare_select_fusion.2, bf16[768,768]{1,0:T(8,128)(2,1)S(1)} %copy.14, f32[768,768]{1,0:T(8,128)} %fusion.3), kind=kLoop, calls=%fused_computation.9 | loop fusion | flops 3538944 | bytes 5898240 | tf_op jit(solution)/shard_map/convert_element_type | solution.py:98
  36.1 3.5 %collective-permute-done.3 = s32[4,4]{1,0:T(4,128)S(1)} collective-permute-done((s32[4,4]{1,0:T(4,128)}, s32[4,4]{1,0:T(4,128)S(1)}, u32[]{:S(2)}, u32[]{:S(2)}) %collective-permute-start.3) | collective-permute-done | bytes 96 | tf_op jit(solution)/shard_map/ppermute | solution.py:20
  39.9 2.4 %add_convert_fusion = bf16[768,768]{1,0:T(8,128)(2,1)S(1)} fusion(bf16[768,768]{1,0:T(8,128)(2,1)} %compare_select_fusion, bf16[768,768]{1,0:T(8,128)(2,1)} %collective-permute-done.4, s32[768]{0:T(1024)S(1)} %copy-done.13, s32[768]{0:T(1024)S(1)} %get-tuple-element.48, s32[4,4]{1,0:T(4,128)S(1)} %collective-permute-done.3), kind=kOutput, calls=%fused_computation.8 | convolution fusion | flops 8291344 | bytes 3545152 | tf_op jit(solution)/shard_map/dot_general | solution.py:63
  53.0 2.6 %collective-permute-start.9 = (bf16[3,512,128]{2,1,0:T(8,128)(2,1)}, bf16[3,512,128]{2,1,0:T(8,128)(2,1)}, u32[]{:S(2)}, u32[]{:S(2)}) collective-permute-start(bf16[3,512,128]{2,1,0:T(8,128)(2,1)} %slice.76), channel_id=1, source_target_pairs={{0,2},{1,3},{2,0},{3,1},{4,6},{5,7},{6,4},{7,5},{8,10},{9,11},{10,... | collective-permute-start | bytes 1179656 | tf_op jit(solution)/shard_map/ppermute | solution.py:39
  60.5 2.4 %collective-permute-done.12 = bf16[64,768]{1,0:T(8,128)(2,1)S(1)} collective-permute-done((bf16[64,768]{1,0:T(8,128)(2,1)S(1)}, bf16[64,768]{1,0:T(8,128)(2,1)S(1)}, u32[]{:S(2)}, u32[]{:S(2)}) %collective-permute-start.12) | collective-permute-done | bytes 98336 | tf_op jit(solution)/shard_map/ppermute | solution.py:20
  65.5 2.0 %collective-permute-done.28 = bf16[64,768]{1,0:T(8,128)(2,1)S(1)} collective-permute-done((bf16[64,768]{1,0:T(8,128)(2,1)S(1)}, bf16[64,768]{1,0:T(8,128)(2,1)S(1)}, u32[]{:S(2)}, u32[]{:S(2)}) %collective-permute-start.28) | collective-permute-done | bytes 98336 | tf_op jit(solution)/shard_map/ppermute | solution.py:20
  70.1 2.0 %collective-permute-done.14 = bf16[64,768]{1,0:T(8,128)(2,1)S(1)} collective-permute-done((bf16[64,768]{1,0:T(8,128)(2,1)S(1)}, bf16[64,768]{1,0:T(8,128)(2,1)S(1)}, u32[]{:S(2)}, u32[]{:S(2)}) %collective-permute-start.14) | collective-permute-done | bytes 98336 | tf_op jit(solution)/shard_map/ppermute | solution.py:20
  74.7 2.0 %collective-permute-done.30 = bf16[64,768]{1,0:T(8,128)(2,1)S(1)} collective-permute-done((bf16[64,768]{1,0:T(8,128)(2,1)S(1)}, bf16[64,768]{1,0:T(8,128)(2,1)S(1)}, u32[]{:S(2)}, u32[]{:S(2)}) %collective-permute-start.30) | collective-permute-done | bytes 98336 | tf_op jit(solution)/shard_map/ppermute | solution.py:20
  82.1 3.0 %collective-permute-done.32 = bf16[64,768]{1,0:T(8,128)(2,1)S(1)} collective-permute-done((bf16[64,768]{1,0:T(8,128)(2,1)S(1)}, bf16[64,768]{1,0:T(8,128)(2,1)S(1)}, u32[]{:S(2)}, u32[]{:S(2)}) %collective-permute-start.32) | collective-permute-done | bytes 98336 | tf_op jit(solution)/shard_map/ppermute | solution.py:20
  86.8 3.0 %collective-permute-done.18 = bf16[64,768]{1,0:T(8,128)(2,1)S(1)} collective-permute-done((bf16[64,768]{1,0:T(8,128)(2,1)S(1)}, bf16[64,768]{1,0:T(8,128)(2,1)S(1)}, u32[]{:S(2)}, u32[]{:S(2)}) %collective-permute-start.18) | collective-permute-done | bytes 98336 | tf_op jit(solution)/shard_map/ppermute | solution.py:20
  91.4 3.0 %collective-permute-done.34 = bf16[64,768]{1,0:T(8,128)(2,1)S(1)} collective-permute-done((bf16[64,768]{1,0:T(8,128)(2,1)S(1)}, bf16[64,768]{1,0:T(8,128)(2,1)S(1)}, u32[]{:S(2)}, u32[]{:S(2)}) %collective-permute-start.34) | collective-permute-done | bytes 98336 | tf_op jit(solution)/shard_map/ppermute | solution.py:20
  99.8 2.1 %collective-permute-done.36 = bf16[64,768]{1,0:T(8,128)(2,1)S(1)} collective-permute-done((bf16[64,768]{1,0:T(8,128)(2,1)S(1)}, bf16[64,768]{1,0:T(8,128)(2,1)S(1)}, u32[]{:S(2)}, u32[]{:S(2)}) %collective-permute-start.36) | collective-permute-done | bytes 98336 | tf_op jit(solution)/shard_map/ppermute | solution.py:20
  104.4 2.0 %collective-permute-done.22 = bf16[64,768]{1,0:T(8,128)(2,1)S(1)} collective-permute-done((bf16[64,768]{1,0:T(8,128)(2,1)S(1)}, bf16[64,768]{1,0:T(8,128)(2,1)S(1)}, u32[]{:S(2)}, u32[]{:S(2)}) %collective-permute-start.22) | collective-permute-done | bytes 98336 | tf_op jit(solution)/shard_map/ppermute | solution.py:20
  108.7 2.4 %collective-permute-done.38 = bf16[64,768]{1,0:T(8,128)(2,1)S(1)} collective-permute-done((bf16[64,768]{1,0:T(8,128)(2,1)S(1)}, bf16[64,768]{1,0:T(8,128)(2,1)S(1)}, u32[]{:S(2)}, u32[]{:S(2)}) %collective-permute-start.38) | collective-permute-done | bytes 98336 | tf_op jit(solution)/shard_map/ppermute | solution.py:20
  112.6 2.8 %collective-permute-start.41 = (bf16[128,768]{1,0:T(8,128)(2,1)S(1)}, bf16[128,768]{1,0:T(8,128)(2,1)S(1)}, u32[]{:S(2)}, u32[]{:S(2)}) collective-permute-start(bf16[128,768]{1,0:T(8,128)(2,1)S(1)} %pad_maximum_fusion.5), channel_id=1, source_target_pairs={{0,3},{1,0},{2,1},{3,2},{4,7},{5,4},{6,5},{7,6},{8,11},{9,8},{10,9... | collective-permute-start | bytes 589832 | tf_op jit(solution)/shard_map/ppermute | solution.py:29
  117.1 4.1 %collective-permute-done.39 = bf16[128,768]{1,0:T(8,128)(2,1)S(1)} collective-permute-done((bf16[128,768]{1,0:T(8,128)(2,1)S(1)}, bf16[128,768]{1,0:T(8,128)(2,1)S(1)}, u32[]{:S(2)}, u32[]{:S(2)}) %collective-permute-start.39) | collective-permute-done | bytes 196640 | tf_op jit(solution)/shard_map/ppermute | solution.py:29
  121.2 5.0 %collective-permute-done.40 = bf16[128,768]{1,0:T(8,128)(2,1)S(1)} collective-permute-done((bf16[128,768]{1,0:T(8,128)(2,1)S(1)}, bf16[128,768]{1,0:T(8,128)(2,1)S(1)}, u32[]{:S(2)}, u32[]{:S(2)}) %collective-permute-start.40) | collective-permute-done | bytes 196640 | tf_op jit(solution)/shard_map/ppermute | solution.py:29
  131.6 2.5 %collective-permute-done.43 = f32[512]{0:T(512)S(1)} collective-permute-done((f32[512]{0:T(512)S(1)}, f32[512]{0:T(512)S(1)}, u32[]{:S(2)}, u32[]{:S(2)}) %collective-permute-start.43) | collective-permute-done | bytes 2080 | tf_op jit(solution)/shard_map/ppermute | solution.py:20
  135.6 2.1 %collective-permute-done.44 = f32[512]{0:T(512)S(1)} collective-permute-done((f32[512]{0:T(512)S(1)}, f32[512]{0:T(512)S(1)}, u32[]{:S(2)}, u32[]{:S(2)}) %collective-permute-start.44) | collective-permute-done | bytes 2080 | tf_op jit(solution)/shard_map/ppermute | solution.py:20
  141.6 2.5 %collective-permute-done.46 = f32[512]{0:T(512)S(1)} collective-permute-done((f32[512]{0:T(512)S(1)}, f32[512]{0:T(512)S(1)}, u32[]{:S(2)}, u32[]{:S(2)}) %collective-permute-start.46) | collective-permute-done | bytes 2080 | tf_op jit(solution)/shard_map/ppermute | solution.py:20
  145.6 2.1 %collective-permute-done.47 = f32[512]{0:T(512)S(1)} collective-permute-done((f32[512]{0:T(512)S(1)}, f32[512]{0:T(512)S(1)}, u32[]{:S(2)}, u32[]{:S(2)}) %collective-permute-start.47) | collective-permute-done | bytes 2080 | tf_op jit(solution)/shard_map/ppermute | solution.py:20
  151.6 2.5 %collective-permute-done.49 = f32[512]{0:T(512)S(1)} collective-permute-done((f32[512]{0:T(512)S(1)}, f32[512]{0:T(512)S(1)}, u32[]{:S(2)}, u32[]{:S(2)}) %collective-permute-start.49) | collective-permute-done | bytes 2080 | tf_op jit(solution)/shard_map/ppermute | solution.py:20
  155.6 2.1 %collective-permute-done.50 = f32[512]{0:T(512)S(1)} collective-permute-done((f32[512]{0:T(512)S(1)}, f32[512]{0:T(512)S(1)}, u32[]{:S(2)}, u32[]{:S(2)}) %collective-permute-start.50) | collective-permute-done | bytes 2080 | tf_op jit(solution)/shard_map/ppermute | solution.py:20
  161.4 2.4 %collective-permute-done.52 = f32[128]{0:T(128)S(1)} collective-permute-done((f32[128]{0:T(128)S(1)}, f32[128]{0:T(128)S(1)}, u32[]{:S(2)}, u32[]{:S(2)}) %collective-permute-start.52) | collective-permute-done | bytes 544 | tf_op jit(solution)/shard_map/ppermute | solution.py:20
  165.4 2.0 %collective-permute-done.53 = f32[128]{0:T(128)S(1)} collective-permute-done((f32[128]{0:T(128)S(1)}, f32[128]{0:T(128)S(1)}, u32[]{:S(2)}, u32[]{:S(2)}) %collective-permute-start.53) | collective-permute-done | bytes 544 | tf_op jit(solution)/shard_map/ppermute | solution.py:20
  (214 shorter events, 84.7 us)
Async XLA Ops:
  1.6 40.7 %collective-permute-start.2 = (bf16[64,768]{1,0:T(8,128)(2,1)}, bf16[64,768]{1,0:T(8,128)(2,1)}, u32[]{:S(2)}, u32[]{:S(2)}) collective-permute-start(bf16[64,768]{1,0:T(8,128)(2,1)} %get-tuple-element.15), channel_id=1, source_target_pairs={{0,4},{4,0},{8,12},{12,8},{16,20},{20,16},{24,28},{28,24},{1,5},{5... | collective-permute-start | bytes 294920 | tf_op jit(solution)/shard_map/ppermute | solution.py:20
  2.1 41.6 %collective-permute-start.5 = (bf16[64,768]{1,0:T(8,128)(2,1)}, bf16[64,768]{1,0:T(8,128)(2,1)}, u32[]{:S(2)}, u32[]{:S(2)}) collective-permute-start(bf16[64,768]{1,0:T(8,128)(2,1)} %get-tuple-element.15), channel_id=1, source_target_pairs={{0,8},{4,12},{8,0},{12,4},{16,24},{20,28},{24,16},{28,20},{1,9},{5... | collective-permute-start | bytes 294920 | tf_op jit(solution)/shard_map/ppermute | solution.py:20
  5.9 21.4 %collective-permute-start = (s32[4,4]{1,0:T(4,128)}, s32[4,4]{1,0:T(4,128)}, u32[]{:S(2)}, u32[]{:S(2)}) collective-permute-start(s32[4,4]{1,0:T(4,128)} %get-tuple-element.18), channel_id=1, source_target_pairs={{0,4},{4,0},{8,12},{12,8},{16,20},{20,16},{24,28},{28,24},{1,5},{5... | collective-permute-start | bytes 200 | tf_op jit(solution)/shard_map/ppermute | solution.py:20
  10.9 21.1 %collective-permute-start.1 = (bf16[768,768]{0,1:T(8,128)(2,1)}, bf16[768,768]{0,1:T(8,128)(2,1)}, u32[]{:S(2)}, u32[]{:S(2)}) collective-permute-start(bf16[768,768]{0,1:T(8,128)(2,1)} %bitcast.4), channel_id=1, source_target_pairs={{0,4},{4,0},{8,12},{12,8},{16,20},{20,16},{24,28},{28,24},{1,5},{5... | collective-permute-start | bytes 3538952 | tf_op jit(solution)/shard_map/ppermute | solution.py:20
  11.2 28.7 %collective-permute-start.4 = (bf16[768,768]{1,0:T(8,128)(2,1)}, bf16[768,768]{1,0:T(8,128)(2,1)}, u32[]{:S(2)}, u32[]{:S(2)}) collective-permute-start(bf16[768,768]{1,0:T(8,128)(2,1)} %get-tuple-element.12), channel_id=1, source_target_pairs={{0,8},{4,12},{8,0},{12,4},{16,24},{20,28},{24,16},{28,20},{1,9},{5... | collective-permute-start | bytes 3538952 | tf_op jit(solution)/shard_map/ppermute | solution.py:20
  27.3 12.3 %collective-permute-start.3 = (s32[4,4]{1,0:T(4,128)}, s32[4,4]{1,0:T(4,128)S(1)}, u32[]{:S(2)}, u32[]{:S(2)}) collective-permute-start(s32[4,4]{1,0:T(4,128)} %get-tuple-element.17), channel_id=1, source_target_pairs={{0,8},{4,12},{8,0},{12,4},{16,24},{20,28},{24,16},{28,20},{1,9},{5... | collective-permute-start | bytes 200 | tf_op jit(solution)/shard_map/ppermute | solution.py:20
  32.0 15.1 %collective-permute-start.23 = (bf16[64,768]{1,0:T(8,128)(2,1)}, bf16[64,768]{1,0:T(8,128)(2,1)}, u32[]{:S(2)}, u32[]{:S(2)}) collective-permute-start(bf16[64,768]{1,0:T(8,128)(2,1)} %get-tuple-element.16), channel_id=1, source_target_pairs={{0,4},{4,0},{8,12},{12,8},{16,20},{20,16},{24,28},{28,24},{1,5},{5... | collective-permute-start | bytes 294920 | tf_op jit(solution)/shard_map/ppermute | solution.py:20
  39.6 8.7 %collective-permute-start.24 = (bf16[64,768]{1,0:T(8,128)(2,1)}, bf16[64,768]{1,0:T(8,128)(2,1)}, u32[]{:S(2)}, u32[]{:S(2)}) collective-permute-start(bf16[64,768]{1,0:T(8,128)(2,1)} %get-tuple-element.16), channel_id=1, source_target_pairs={{0,8},{4,12},{8,0},{12,4},{16,24},{20,28},{24,16},{28,20},{1,9},{5... | collective-permute-start | bytes 294920 | tf_op jit(solution)/shard_map/ppermute | solution.py:20
  45.2 5.3 %collective-permute-start.6 = (bf16[64,768]{1,0:T(8,128)(2,1)S(1)}, bf16[64,768]{1,0:T(8,128)(2,1)S(1)}, u32[]{:S(2)}, u32[]{:S(2)}) collective-permute-start(bf16[64,768]{1,0:T(8,128)(2,1)S(1)} %get-tuple-element.33), channel_id=1, source_target_pairs={{0,4},{4,0},{8,12},{12,8},{16,20},{20,16},{24,28},{28,24},{1,5},{5... | collective-permute-start | bytes 294920 | tf_op jit(solution)/shard_map/ppermute | solution.py:20
  45.3 5.5 %collective-permute-start.7 = (bf16[64,768]{1,0:T(8,128)(2,1)S(1)}, bf16[64,768]{1,0:T(8,128)(2,1)S(1)}, u32[]{:S(2)}, u32[]{:S(2)}) collective-permute-start(bf16[64,768]{1,0:T(8,128)(2,1)S(1)} %get-tuple-element.33), channel_id=1, source_target_pairs={{0,8},{4,12},{8,0},{12,4},{16,24},{20,28},{24,16},{28,20},{1,9},{5... | collective-permute-start | bytes 294920 | tf_op jit(solution)/shard_map/ppermute | solution.py:20
  49.9 7.0 %collective-permute-start.25 = (bf16[64,768]{1,0:T(8,128)(2,1)S(1)}, bf16[64,768]{1,0:T(8,128)(2,1)S(1)}, u32[]{:S(2)}, u32[]{:S(2)}) collective-permute-start(bf16[64,768]{1,0:T(8,128)(2,1)S(1)} %get-tuple-element.19), channel_id=1, source_target_pairs={{0,4},{4,0},{8,12},{12,8},{16,20},{20,16},{24,28},{28,24},{1,5},{5... | collective-permute-start | bytes 294920 | tf_op jit(solution)/shard_map/ppermute | solution.py:20
  50.1 7.6 %collective-permute-start.26 = (bf16[64,768]{1,0:T(8,128)(2,1)S(1)}, bf16[64,768]{1,0:T(8,128)(2,1)S(1)}, u32[]{:S(2)}, u32[]{:S(2)}) collective-permute-start(bf16[64,768]{1,0:T(8,128)(2,1)S(1)} %get-tuple-element.19), channel_id=1, source_target_pairs={{0,8},{4,12},{8,0},{12,4},{16,24},{20,28},{24,16},{28,20},{1,9},{5... | collective-permute-start | bytes 294920 | tf_op jit(solution)/shard_map/ppermute | solution.py:20
  51.2 61.4 %collective-permute-start.8 = (bf16[3,512,128]{2,1,0:T(8,128)(2,1)}, bf16[3,512,128]{2,1,0:T(8,128)(2,1)}, u32[]{:S(2)}, u32[]{:S(2)}) collective-permute-start(bf16[3,512,128]{2,1,0:T(8,128)(2,1)} %slice.76), channel_id=1, source_target_pairs={{0,1},{1,2},{2,3},{3,0},{4,5},{5,6},{6,7},{7,4},{8,9},{9,10},{10,1... | collective-permute-start | bytes 1179656 | tf_op jit(solution)/shard_map/ppermute | solution.py:39
  53.0 62.4 %collective-permute-start.9 = (bf16[3,512,128]{2,1,0:T(8,128)(2,1)}, bf16[3,512,128]{2,1,0:T(8,128)(2,1)}, u32[]{:S(2)}, u32[]{:S(2)}) collective-permute-start(bf16[3,512,128]{2,1,0:T(8,128)(2,1)} %slice.76), channel_id=1, source_target_pairs={{0,2},{1,3},{2,0},{3,1},{4,6},{5,7},{6,4},{7,5},{8,10},{9,11},{10,... | collective-permute-start | bytes 1179656 | tf_op jit(solution)/shard_map/ppermute | solution.py:39
  55.6 59.9 %collective-permute-start.10 = (bf16[3,512,128]{2,1,0:T(8,128)(2,1)}, bf16[3,512,128]{2,1,0:T(8,128)(2,1)}, u32[]{:S(2)}, u32[]{:S(2)}) collective-permute-start(bf16[3,512,128]{2,1,0:T(8,128)(2,1)} %slice.76), channel_id=1, source_target_pairs={{0,3},{1,0},{2,1},{3,2},{4,7},{5,4},{6,5},{7,6},{8,11},{9,8},{10,9... | collective-permute-start | bytes 1179656 | tf_op jit(solution)/shard_map/ppermute | solution.py:39
  57.7 5.2 %collective-permute-start.12 = (bf16[64,768]{1,0:T(8,128)(2,1)S(1)}, bf16[64,768]{1,0:T(8,128)(2,1)S(1)}, u32[]{:S(2)}, u32[]{:S(2)}) collective-permute-start(bf16[64,768]{1,0:T(8,128)(2,1)S(1)} %convert_element_type.170), channel_id=1, source_target_pairs={{0,8},{4,12},{8,0},{12,4},{16,24},{20,28},{24,16},{28,20},{1,9},{5... | collective-permute-start | bytes 294920 | tf_op jit(solution)/shard_map/ppermute | solution.py:20
  60.0 4.8 %collective-permute-start.27 = (bf16[64,768]{1,0:T(8,128)(2,1)S(1)}, bf16[64,768]{1,0:T(8,128)(2,1)S(1)}, u32[]{:S(2)}, u32[]{:S(2)}) collective-permute-start(bf16[64,768]{1,0:T(8,128)(2,1)S(1)} %get-tuple-element.21), channel_id=1, source_target_pairs={{0,4},{4,0},{8,12},{12,8},{16,20},{20,16},{24,28},{28,24},{1,5},{5... | collective-permute-start | bytes 294920 | tf_op jit(solution)/shard_map/ppermute | solution.py:20
  62.9 4.6 %collective-permute-start.28 = (bf16[64,768]{1,0:T(8,128)(2,1)S(1)}, bf16[64,768]{1,0:T(8,128)(2,1)S(1)}, u32[]{:S(2)}, u32[]{:S(2)}) collective-permute-start(bf16[64,768]{1,0:T(8,128)(2,1)S(1)} %get-tuple-element.21), channel_id=1, source_target_pairs={{0,8},{4,12},{8,0},{12,4},{16,24},{20,28},{24,16},{28,20},{1,9},{5... | collective-permute-start | bytes 294920 | tf_op jit(solution)/shard_map/ppermute | solution.py:20
  67.5 4.6 %collective-permute-start.14 = (bf16[64,768]{1,0:T(8,128)(2,1)S(1)}, bf16[64,768]{1,0:T(8,128)(2,1)S(1)}, u32[]{:S(2)}, u32[]{:S(2)}) collective-permute-start(bf16[64,768]{1,0:T(8,128)(2,1)S(1)} %get-tuple-element.35), channel_id=1, source_target_pairs={{0,8},{4,12},{8,0},{12,4},{16,24},{20,28},{24,16},{28,20},{1,9},{5... | collective-permute-start | bytes 294920 | tf_op jit(solution)/shard_map/ppermute | solution.py:20
  72.1 4.6 %collective-permute-start.30 = (bf16[64,768]{1,0:T(8,128)(2,1)S(1)}, bf16[64,768]{1,0:T(8,128)(2,1)S(1)}, u32[]{:S(2)}, u32[]{:S(2)}) collective-permute-start(bf16[64,768]{1,0:T(8,128)(2,1)S(1)} %get-tuple-element.23), channel_id=1, source_target_pairs={{0,8},{4,12},{8,0},{12,4},{16,24},{20,28},{24,16},{28,20},{1,9},{5... | collective-permute-start | bytes 294920 | tf_op jit(solution)/shard_map/ppermute | solution.py:20
  74.0 4.9 %collective-permute-start.15 = (bf16[64,768]{1,0:T(8,128)(2,1)S(1)}, bf16[64,768]{1,0:T(8,128)(2,1)S(1)}, u32[]{:S(2)}, u32[]{:S(2)}) collective-permute-start(bf16[64,768]{1,0:T(8,128)(2,1)S(1)} %get-tuple-element.37), channel_id=1, source_target_pairs={{0,4},{4,0},{8,12},{12,8},{16,20},{20,16},{24,28},{28,24},{1,5},{5... | collective-permute-start | bytes 294920 | tf_op jit(solution)/shard_map/ppermute | solution.py:20
  76.8 4.6 %collective-permute-start.16 = (bf16[64,768]{1,0:T(8,128)(2,1)S(1)}, bf16[64,768]{1,0:T(8,128)(2,1)S(1)}, u32[]{:S(2)}, u32[]{:S(2)}) collective-permute-start(bf16[64,768]{1,0:T(8,128)(2,1)S(1)} %get-tuple-element.37), channel_id=1, source_target_pairs={{0,8},{4,12},{8,0},{12,4},{16,24},{20,28},{24,16},{28,20},{1,9},{5... | collective-permute-start | bytes 294920 | tf_op jit(solution)/shard_map/ppermute | solution.py:20
  80.3 4.9 %collective-permute-start.32 = (bf16[64,768]{1,0:T(8,128)(2,1)S(1)}, bf16[64,768]{1,0:T(8,128)(2,1)S(1)}, u32[]{:S(2)}, u32[]{:S(2)}) collective-permute-start(bf16[64,768]{1,0:T(8,128)(2,1)S(1)} %get-tuple-element.25), channel_id=1, source_target_pairs={{0,8},{4,12},{8,0},{12,4},{16,24},{20,28},{24,16},{28,20},{1,9},{5... | collective-permute-start | bytes 294920 | tf_op jit(solution)/shard_map/ppermute | solution.py:20
  85.2 4.6 %collective-permute-start.18 = (bf16[64,768]{1,0:T(8,128)(2,1)S(1)}, bf16[64,768]{1,0:T(8,128)(2,1)S(1)}, u32[]{:S(2)}, u32[]{:S(2)}) collective-permute-start(bf16[64,768]{1,0:T(8,128)(2,1)S(1)} %get-tuple-element.39), channel_id=1, source_target_pairs={{0,8},{4,12},{8,0},{12,4},{16,24},{20,28},{24,16},{28,20},{1,9},{5... | collective-permute-start | bytes 294920 | tf_op jit(solution)/shard_map/ppermute | solution.py:20
  89.8 4.6 %collective-permute-start.34 = (bf16[64,768]{1,0:T(8,128)(2,1)S(1)}, bf16[64,768]{1,0:T(8,128)(2,1)S(1)}, u32[]{:S(2)}, u32[]{:S(2)}) collective-permute-start(bf16[64,768]{1,0:T(8,128)(2,1)S(1)} %get-tuple-element.27), channel_id=1, source_target_pairs={{0,8},{4,12},{8,0},{12,4},{16,24},{20,28},{24,16},{28,20},{1,9},{5... | collective-permute-start | bytes 294920 | tf_op jit(solution)/shard_map/ppermute | solution.py:20
  90.7 4.9 %collective-permute-start.19 = (bf16[64,768]{1,0:T(8,128)(2,1)S(1)}, bf16[64,768]{1,0:T(8,128)(2,1)S(1)}, u32[]{:S(2)}, u32[]{:S(2)}) collective-permute-start(bf16[64,768]{1,0:T(8,128)(2,1)S(1)} %get-tuple-element.41), channel_id=1, source_target_pairs={{0,4},{4,0},{8,12},{12,8},{16,20},{20,16},{24,28},{28,24},{1,5},{5... | collective-permute-start | bytes 294920 | tf_op jit(solution)/shard_map/ppermute | solution.py:20
  94.4 4.6 %collective-permute-start.20 = (bf16[64,768]{1,0:T(8,128)(2,1)S(1)}, bf16[64,768]{1,0:T(8,128)(2,1)S(1)}, u32[]{:S(2)}, u32[]{:S(2)}) collective-permute-start(bf16[64,768]{1,0:T(8,128)(2,1)S(1)} %get-tuple-element.41), channel_id=1, source_target_pairs={{0,8},{4,12},{8,0},{12,4},{16,24},{20,28},{24,16},{28,20},{1,9},{5... | collective-permute-start | bytes 294920 | tf_op jit(solution)/shard_map/ppermute | solution.py:20
  97.0 4.9 %collective-permute-start.36 = (bf16[64,768]{1,0:T(8,128)(2,1)S(1)}, bf16[64,768]{1,0:T(8,128)(2,1)S(1)}, u32[]{:S(2)}, u32[]{:S(2)}) collective-permute-start(bf16[64,768]{1,0:T(8,128)(2,1)S(1)} %get-tuple-element.29), channel_id=1, source_target_pairs={{0,8},{4,12},{8,0},{12,4},{16,24},{20,28},{24,16},{28,20},{1,9},{5... | collective-permute-start | bytes 294920 | tf_op jit(solution)/shard_map/ppermute | solution.py:20
  101.8 4.6 %collective-permute-start.22 = (bf16[64,768]{1,0:T(8,128)(2,1)S(1)}, bf16[64,768]{1,0:T(8,128)(2,1)S(1)}, u32[]{:S(2)}, u32[]{:S(2)}) collective-permute-start(bf16[64,768]{1,0:T(8,128)(2,1)S(1)} %get-tuple-element.43), channel_id=1, source_target_pairs={{0,8},{4,12},{8,0},{12,4},{16,24},{20,28},{24,16},{28,20},{1,9},{5... | collective-permute-start | bytes 294920 | tf_op jit(solution)/shard_map/ppermute | solution.py:20
  111.5 9.7 %collective-permute-start.39 = (bf16[128,768]{1,0:T(8,128)(2,1)S(1)}, bf16[128,768]{1,0:T(8,128)(2,1)S(1)}, u32[]{:S(2)}, u32[]{:S(2)}) collective-permute-start(bf16[128,768]{1,0:T(8,128)(2,1)S(1)} %pad_maximum_fusion.5), channel_id=1, source_target_pairs={{0,1},{1,2},{2,3},{3,0},{4,5},{5,6},{6,7},{7,4},{8,9},{9,10},{10,1... | collective-permute-start | bytes 589832 | tf_op jit(solution)/shard_map/ppermute | solution.py:29
  112.2 14.0 %collective-permute-start.40 = (bf16[128,768]{1,0:T(8,128)(2,1)S(1)}, bf16[128,768]{1,0:T(8,128)(2,1)S(1)}, u32[]{:S(2)}, u32[]{:S(2)}) collective-permute-start(bf16[128,768]{1,0:T(8,128)(2,1)S(1)} %pad_maximum_fusion.5), channel_id=1, source_target_pairs={{0,2},{1,3},{2,0},{3,1},{4,6},{5,7},{6,4},{7,5},{8,10},{9,11},{10,... | collective-permute-start | bytes 589832 | tf_op jit(solution)/shard_map/ppermute | solution.py:29
  112.6 13.6 %collective-permute-start.41 = (bf16[128,768]{1,0:T(8,128)(2,1)S(1)}, bf16[128,768]{1,0:T(8,128)(2,1)S(1)}, u32[]{:S(2)}, u32[]{:S(2)}) collective-permute-start(bf16[128,768]{1,0:T(8,128)(2,1)S(1)} %pad_maximum_fusion.5), channel_id=1, source_target_pairs={{0,3},{1,0},{2,1},{3,2},{4,7},{5,4},{6,5},{7,6},{8,11},{9,8},{10,9... | collective-permute-start | bytes 589832 | tf_op jit(solution)/shard_map/ppermute | solution.py:29
  (36 other events, 112.7 us)

commit v11 on v10

--- a/solution.py
+++ b/solution.py
@@ -122,7 +122,11 @@
 
     def start_rotation_gather(current):
         held, current = lax.optimization_barrier((rotations[: ROTS - 1], current))
-        gathered.append(gather_pieces(held))
+        half_rows = held.shape[1] // 2
+        first_of_pair = (atoms_here % 2) == 0
+        mine = jnp.where(first_of_pair, held[:, :half_rows], held[:, half_rows:])
+        mine = gather_pieces(mine)
+        gathered.append((mine, swapped(mine, "atoms", 0)))
         return current
 
     half_bands = subspace.shape[0] // 2
@@ -133,23 +137,31 @@
         ],
         axis=0,
     )
-    rot_pieces = gathered[0]
+    rot_mine, rot_theirs = gathered[0]
     total_orbitals = orb_dev * lax.axis_size("atoms")
     band_count = lax.axis_size("bands")
     band_here = lax.axis_index("bands")
     all_bands = rotations.shape[1]
+    half_rows = all_bands // 2
+    mine_start = (atoms_here % 2) * half_rows
     basis_all = gather_bands(current.astype(jnp.bfloat16)).reshape(all_bands, orb_dev)
     for rotation_index in range(ROTS - 1):
+        basis_mine = lax.dynamic_slice_in_dim(basis_all, mine_start, half_rows, axis=0)
+        basis_theirs = lax.dynamic_slice_in_dim(
+            basis_all, half_rows - mine_start, half_rows, axis=0
+        )
         groups = []
         for group in range(band_count):
-            piece = lax.dynamic_index_in_dim(
-                rot_pieces, (band_here - group) % band_count, 0, keepdims=False
-            )
+            shift = (band_here - group) % band_count
+            piece_mine = lax.dynamic_index_in_dim(rot_mine, shift, 0, keepdims=False)
+            piece_theirs = lax.dynamic_index_in_dim(rot_theirs, shift, 0, keepdims=False)
             groups.append(
                 lax.dot_general(
-                    piece[rotation_index],
-                    basis_all,
-                    (((0,), (0,)), ((), ())),
+                    piece_mine[rotation_index], basis_mine, (((0,), (0,)), ((), ())),
+                    preferred_element_type=jnp.float32,
+                )
+                + lax.dot_general(
+                    piece_theirs[rotation_index], basis_theirs, (((0,), (0,)), ((), ())),
                     preferred_element_type=jnp.float32,
                 )
             )

time: 170 us -> 183 us (1.076)
  matrix products: 36.1 us -> 49 us
  local copies, waits for them, and re-layouts: 14.7 us -> 17.4 us
  waiting for transfers between devices: 61.7 us -> 59.6 us
    dot_general x12 -> x24, matrix products: 3.61 us -> 15.8 us  [the longest x12 13 us: body(): lax.dot_general(piece_theirs[rotation_index], basis_theirs, (((0,), (0,))...]
    ppermute x48 -> x49, waiting for transfers between devices: 52.5 us -> 49 us  [swapped(): return lax.ppermute(value, axis, pairs)]
    ppermute x48 -> x49, starting transfers between devices: 34.1 us -> 34.3 us  [swapped(): return lax.ppermute(value, axis, pairs)]
  transfers between devices with their start and end apart: 54 -> 55, of which waited for: 29 -> 28; matrix products, arithmetic and copies ran while one was open for 31% -> 31% of each run, Pallas kernels for 0% -> 0%
where the time goes in v11:
time: 183 us; the launch traced here: 181 us
  waiting for transfers between devices  59.6 us (33%)
  matrix products  49 us (27%)
  starting transfers between devices  43.9 us (24%)
  local copies, waits for them, and re-layouts  17.4 us (10%)
  other arithmetic  10.1 us (6%)
    ppermute x49, waiting for transfers between devices, swapped(): return lax.ppermute(value, axis, pairs)  49 us
    ppermute x49, starting transfers between devices, swapped(): return lax.ppermute(value, axis, pairs)  34.3 us
    dot_general x32, matrix products, apply_operator(): jnp.dot(other_rows, other_pair[round_index], preferred_element_type=jnp.f...  14.5 us
    dot_general x12, matrix products, body(): lax.dot_general(piece_theirs[rotation_index], basis_theirs, (((0,), (0,))...  13 us
    ppermute x3, waiting for transfers between devices, gather_bands(): pieces.append(lax.ppermute(value, 'bands', pairs))  10.6 us
    dot_general x4, matrix products, pattern_mask(): lax.dot_general(per_row.astype(jnp.bfloat16), col_onehot, (((1,), (1,)),...  10.6 us
    dot_general x16, matrix products, apply_operator(): result = jnp.dot(values, diag_sym, preferred_element_type=jnp.float32)  6.64 us
    ppermute x3, starting transfers between devices, gather_pieces(): pieces.append(lax.ppermute(value, 'bands', pairs))  5.64 us
  transfers between devices with their start and end apart: 55, of which 28 were waited for; matrix products, arithmetic and copies ran while one was open for 31% of the time, Pallas kernels for 0%

profile of v11, /device:TPU:0, one launch (start us, length us, event | category | flops | bytes accessed | tf_op | source)
XLA Modules:
  0.0 180.9 jit_solution(4072367330940495352)
XLA Ops:
  2.1 2.5 %collective-permute-start.5 = (bf16[64,768]{1,0:T(8,128)(2,1)}, bf16[64,768]{1,0:T(8,128)(2,1)}, u32[]{:S(2)}, u32[]{:S(2)}) collective-permute-start(bf16[64,768]{1,0:T(8,128)(2,1)} %get-tuple-element.15), channel_id=1, source_target_pairs={{0,8},{4,12},{8,0},{12,4},{16,24},{20,28},{24,16},{28,20},{1,9},{5... | collective-permute-start | bytes 294920 | tf_op jit(solution)/shard_map/ppermute | solution.py:20
  6.1 3.3 %slice_bitcast_fusion.1 = (bf16[768,768]{1,0:T(8,128)(2,1)}, bf16[768,768]{0,1:T(8,128)(2,1)}, bf16[1,768,768]{2,1,0:T(8,128)(2,1)S(1)}) fusion(bf16[2,768,768]{2,1,0:T(8,128)(2,1)} %param.8), kind=kLoop, calls=%fused_computation.121 | loop fusion | bytes 5898240 | tf_op jit(solution)/shard_map/squeeze | solution.py:74
  14.1 2.1 %copy.12 = f32[768,768]{1,0:T(8,128)S(1)} copy(f32[768,768]{0,1:T(8,128)} %convert_bitcast_fusion) | data formatting | bytes 4718592 | tf_op jit(solution)/shard_map/convert_element_type | solution.py:85
  16.9 3.1 %compare_select_fusion.2 = bf16[768,768]{1,0:T(8,128)(2,1)} fusion(bf16[1,768,768]{1,2,0:T(8,128)(2,1)} %copy.17, s32[768]{0:T(1024)S(1)} %get-tuple-element.48, s32[768]{0:T(1024)S(1)} %convert_reduce_fusion.1, s32[2,4,4]{2,1,0:T(4,128)S(1)} %copy-done.8), kind=kOutput, calls=%fused_computation.12 | convolution fusion | flops 5932048 | bytes 2369536 | tf_op jit(solution)/shard_map/dot_general | solution.py:63
  20.0 2.3 %fusion.1 = bf16[768,768]{1,0:T(8,128)(2,1)S(1)} fusion(bf16[768,768]{1,0:T(8,128)(2,1)} %param.7, f32[768,768]{1,0:T(8,128)S(1)} %copy.12, s32[768]{0:T(1024)S(1)} %get-tuple-element.48), kind=kLoop, calls=%fused_computation.6 | loop fusion | flops 7667712 | bytes 4721664 | tf_op jit(solution)/shard_map/convert_element_type | solution.py:86
  28.7 2.4 %compare_select_fusion = bf16[768,768]{1,0:T(8,128)(2,1)} fusion(bf16[768,768]{1,0:T(8,128)(2,1)S(1)} %copy.15, s32[768]{0:T(1024)} %get-tuple-element.47, s32[768]{0:T(1024)S(1)} %get-tuple-element.48, s32[2,4,4]{2,1,0:T(4,128)S(1)} %copy-done.8), kind=kOutput, calls=%fused_computation.10 | convolution fusion | flops 5932048 | bytes 2368512 | tf_op jit(solution)/shard_map/dot_general | solution.py:63
  31.0 2.0 %collective-permute-start.3 = (s32[4,4]{1,0:T(4,128)}, s32[4,4]{1,0:T(4,128)S(1)}, u32[]{:S(2)}, u32[]{:S(2)}) collective-permute-start(s32[4,4]{1,0:T(4,128)} %get-tuple-element.17), channel_id=1, source_target_pairs={{0,8},{4,12},{8,0},{12,4},{16,24},{20,28},{24,16},{28,20},{1,9},{5... | collective-permute-start | bytes 200 | tf_op jit(solution)/shard_map/ppermute | solution.py:20
  33.1 2.8 %fusion.3 = f32[768,768]{1,0:T(8,128)} fusion(s32[768]{0:T(1024)S(1)} %get-tuple-element.48, s32[768]{0:T(1024)S(1)} %convert_reduce_fusion.1, s32[4,4]{1,0:T(4,128)} %collective-permute-done), kind=kOutput, calls=%fused_computation.39 | convolution fusion | flops 4752400 | bytes 2365504 | tf_op jit(solution)/shard_map/dot_general | solution.py:63
  37.4 2.5 %add_convert_fusion.1 = bf16[768,768]{1,0:T(8,128)(2,1)S(1)} fusion(bf16[768,768]{1,0:T(8,128)(2,1)} %compare_select_fusion.2, bf16[768,768]{1,0:T(8,128)(2,1)S(1)} %copy.14, f32[768,768]{1,0:T(8,128)} %fusion.3), kind=kLoop, calls=%fused_computation.9 | loop fusion | flops 3538944 | bytes 5898240 | tf_op jit(solution)/shard_map/convert_element_type | solution.py:98
  40.0 2.4 %add_convert_fusion = bf16[768,768]{1,0:T(8,128)(2,1)S(1)} fusion(bf16[768,768]{1,0:T(8,128)(2,1)} %compare_select_fusion, bf16[768,768]{1,0:T(8,128)(2,1)} %collective-permute-done.4, s32[768]{0:T(1024)S(1)} %copy-done.9, s32[768]{0:T(1024)S(1)} %get-tuple-element.48, s32[4,4]{1,0:T(4,128)S(1)} %collective-permute-done.3), kind=kOutput, calls=%fused_computation.8 | convolution fusion | flops 8291344 | bytes 3545152 | tf_op jit(solution)/shard_map/dot_general | solution.py:63
  54.1 2.6 %collective-permute-start.9 = (bf16[3,256,128]{2,1,0:T(8,128)(2,1)S(1)}, bf16[3,256,128]{2,1,0:T(8,128)(2,1)S(1)}, u32[]{:S(2)}, u32[]{:S(2)}) collective-permute-start(bf16[3,256,128]{2,1,0:T(8,128)(2,1)S(1)} %slice_select_fusion), channel_id=1, source_target_pairs={{0,2},{1,3},{2,0},{3,1},{4,6},{5,7},{6,4},{7,5},{8,10},{9,11},{10,... | collective-permute-start | bytes 589832 | tf_op jit(solution)/shard_map/ppermute | solution.py:39
  61.6 2.4 %collective-permute-done.12 = bf16[64,768]{1,0:T(8,128)(2,1)S(1)} collective-permute-done((bf16[64,768]{1,0:T(8,128)(2,1)S(1)}, bf16[64,768]{1,0:T(8,128)(2,1)S(1)}, u32[]{:S(2)}, u32[]{:S(2)}) %collective-permute-start.12) | collective-permute-done | bytes 98336 | tf_op jit(solution)/shard_map/ppermute | solution.py:20
  66.6 2.0 %collective-permute-done.28 = bf16[64,768]{1,0:T(8,128)(2,1)S(1)} collective-permute-done((bf16[64,768]{1,0:T(8,128)(2,1)S(1)}, bf16[64,768]{1,0:T(8,128)(2,1)S(1)}, u32[]{:S(2)}, u32[]{:S(2)}) %collective-permute-start.28) | collective-permute-done | bytes 98336 | tf_op jit(solution)/shard_map/ppermute | solution.py:20
  71.2 2.0 %collective-permute-done.14 = bf16[64,768]{1,0:T(8,128)(2,1)S(1)} collective-permute-done((bf16[64,768]{1,0:T(8,128)(2,1)S(1)}, bf16[64,768]{1,0:T(8,128)(2,1)S(1)}, u32[]{:S(2)}, u32[]{:S(2)}) %collective-permute-start.14) | collective-permute-done | bytes 98336 | tf_op jit(solution)/shard_map/ppermute | solution.py:20
  75.8 2.0 %collective-permute-done.30 = bf16[64,768]{1,0:T(8,128)(2,1)S(1)} collective-permute-done((bf16[64,768]{1,0:T(8,128)(2,1)S(1)}, bf16[64,768]{1,0:T(8,128)(2,1)S(1)}, u32[]{:S(2)}, u32[]{:S(2)}) %collective-permute-start.30) | collective-permute-done | bytes 98336 | tf_op jit(solution)/shard_map/ppermute | solution.py:20
  83.2 3.1 %collective-permute-done.32 = bf16[64,768]{1,0:T(8,128)(2,1)S(1)} collective-permute-done((bf16[64,768]{1,0:T(8,128)(2,1)S(1)}, bf16[64,768]{1,0:T(8,128)(2,1)S(1)}, u32[]{:S(2)}, u32[]{:S(2)}) %collective-permute-start.32) | collective-permute-done | bytes 98336 | tf_op jit(solution)/shard_map/ppermute | solution.py:20
  87.9 3.0 %collective-permute-done.18 = bf16[64,768]{1,0:T(8,128)(2,1)S(1)} collective-permute-done((bf16[64,768]{1,0:T(8,128)(2,1)S(1)}, bf16[64,768]{1,0:T(8,128)(2,1)S(1)}, u32[]{:S(2)}, u32[]{:S(2)}) %collective-permute-start.18) | collective-permute-done | bytes 98336 | tf_op jit(solution)/shard_map/ppermute | solution.py:20
  92.5 3.0 %collective-permute-done.34 = bf16[64,768]{1,0:T(8,128)(2,1)S(1)} collective-permute-done((bf16[64,768]{1,0:T(8,128)(2,1)S(1)}, bf16[64,768]{1,0:T(8,128)(2,1)S(1)}, u32[]{:S(2)}, u32[]{:S(2)}) %collective-permute-start.34) | collective-permute-done | bytes 98336 | tf_op jit(solution)/shard_map/ppermute | solution.py:20
  100.8 2.1 %collective-permute-done.36 = bf16[64,768]{1,0:T(8,128)(2,1)S(1)} collective-permute-done((bf16[64,768]{1,0:T(8,128)(2,1)S(1)}, bf16[64,768]{1,0:T(8,128)(2,1)S(1)}, u32[]{:S(2)}, u32[]{:S(2)}) %collective-permute-start.36) | collective-permute-done | bytes 98336 | tf_op jit(solution)/shard_map/ppermute | solution.py:20
  105.5 2.0 %collective-permute-done.22 = bf16[64,768]{1,0:T(8,128)(2,1)S(1)} collective-permute-done((bf16[64,768]{1,0:T(8,128)(2,1)S(1)}, bf16[64,768]{1,0:T(8,128)(2,1)S(1)}, u32[]{:S(2)}, u32[]{:S(2)}) %collective-permute-start.22) | collective-permute-done | bytes 98336 | tf_op jit(solution)/shard_map/ppermute | solution.py:20
  109.7 2.4 %collective-permute-done.38 = bf16[64,768]{1,0:T(8,128)(2,1)S(1)} collective-permute-done((bf16[64,768]{1,0:T(8,128)(2,1)S(1)}, bf16[64,768]{1,0:T(8,128)(2,1)S(1)}, u32[]{:S(2)}, u32[]{:S(2)}) %collective-permute-start.38) | collective-permute-done | bytes 98336 | tf_op jit(solution)/shard_map/ppermute | solution.py:20
  113.6 2.8 %collective-permute-start.41 = (bf16[128,768]{1,0:T(8,128)(2,1)S(1)}, bf16[128,768]{1,0:T(8,128)(2,1)S(1)}, u32[]{:S(2)}, u32[]{:S(2)}) collective-permute-start(bf16[128,768]{1,0:T(8,128)(2,1)S(1)} %pad_maximum_fusion.5), channel_id=1, source_target_pairs={{0,3},{1,0},{2,1},{3,2},{4,7},{5,4},{6,5},{7,6},{8,11},{9,8},{10,9... | collective-permute-start | bytes 589832 | tf_op jit(solution)/shard_map/ppermute | solution.py:29
  116.7 5.6 %collective-permute-done.39 = bf16[128,768]{1,0:T(8,128)(2,1)S(1)} collective-permute-done((bf16[128,768]{1,0:T(8,128)(2,1)S(1)}, bf16[128,768]{1,0:T(8,128)(2,1)S(1)}, u32[]{:S(2)}, u32[]{:S(2)}) %collective-permute-start.39) | collective-permute-done | bytes 196640 | tf_op jit(solution)/shard_map/ppermute | solution.py:29
  122.3 5.0 %collective-permute-done.40 = bf16[128,768]{1,0:T(8,128)(2,1)S(1)} collective-permute-done((bf16[128,768]{1,0:T(8,128)(2,1)S(1)}, bf16[128,768]{1,0:T(8,128)(2,1)S(1)}, u32[]{:S(2)}, u32[]{:S(2)}) %collective-permute-start.40) | collective-permute-done | bytes 196640 | tf_op jit(solution)/shard_map/ppermute | solution.py:29
  136.0 2.5 %collective-permute-done.44 = f32[512]{0:T(512)S(1)} collective-permute-done((f32[512]{0:T(512)S(1)}, f32[512]{0:T(512)S(1)}, u32[]{:S(2)}, u32[]{:S(2)}) %collective-permute-start.44) | collective-permute-done | bytes 2080 | tf_op jit(solution)/shard_map/ppermute | solution.py:20
  140.0 2.1 %collective-permute-done.45 = f32[512]{0:T(512)S(1)} collective-permute-done((f32[512]{0:T(512)S(1)}, f32[512]{0:T(512)S(1)}, u32[]{:S(2)}, u32[]{:S(2)}) %collective-permute-start.45) | collective-permute-done | bytes 2080 | tf_op jit(solution)/shard_map/ppermute | solution.py:20
  150.1 2.5 %collective-permute-done.47 = f32[512]{0:T(512)S(1)} collective-permute-done((f32[512]{0:T(512)S(1)}, f32[512]{0:T(512)S(1)}, u32[]{:S(2)}, u32[]{:S(2)}) %collective-permute-start.47) | collective-permute-done | bytes 2080 | tf_op jit(solution)/shard_map/ppermute | solution.py:20
  154.1 2.1 %collective-permute-done.48 = f32[512]{0:T(512)S(1)} collective-permute-done((f32[512]{0:T(512)S(1)}, f32[512]{0:T(512)S(1)}, u32[]{:S(2)}, u32[]{:S(2)}) %collective-permute-start.48) | collective-permute-done | bytes 2080 | tf_op jit(solution)/shard_map/ppermute | solution.py:20
  164.2 2.5 %collective-permute-done.50 = f32[512]{0:T(512)S(1)} collective-permute-done((f32[512]{0:T(512)S(1)}, f32[512]{0:T(512)S(1)}, u32[]{:S(2)}, u32[]{:S(2)}) %collective-permute-start.50) | collective-permute-done | bytes 2080 | tf_op jit(solution)/shard_map/ppermute | solution.py:20
  168.2 2.1 %collective-permute-done.51 = f32[512]{0:T(512)S(1)} collective-permute-done((f32[512]{0:T(512)S(1)}, f32[512]{0:T(512)S(1)}, u32[]{:S(2)}, u32[]{:S(2)}) %collective-permute-start.51) | collective-permute-done | bytes 2080 | tf_op jit(solution)/shard_map/ppermute | solution.py:20
  174.0 2.4 %collective-permute-done.53 = f32[128]{0:T(128)S(1)} collective-permute-done((f32[128]{0:T(128)S(1)}, f32[128]{0:T(128)S(1)}, u32[]{:S(2)}, u32[]{:S(2)}) %collective-permute-start.53) | collective-permute-done | bytes 544 | tf_op jit(solution)/shard_map/ppermute | solution.py:20
  177.9 2.0 %collective-permute-done.54 = f32[128]{0:T(128)S(1)} collective-permute-done((f32[128]{0:T(128)S(1)}, f32[128]{0:T(128)S(1)}, u32[]{:S(2)}, u32[]{:S(2)}) %collective-permute-start.54) | collective-permute-done | bytes 544 | tf_op jit(solution)/shard_map/ppermute | solution.py:20
  (227 shorter events, 96.6 us)
Async XLA Ops:
  1.6 40.7 %collective-permute-start.2 = (bf16[64,768]{1,0:T(8,128)(2,1)}, bf16[64,768]{1,0:T(8,128)(2,1)}, u32[]{:S(2)}, u32[]{:S(2)}) collective-permute-start(bf16[64,768]{1,0:T(8,128)(2,1)} %get-tuple-element.15), channel_id=1, source_target_pairs={{0,4},{4,0},{8,12},{12,8},{16,20},{20,16},{24,28},{28,24},{1,5},{5... | collective-permute-start | bytes 294920 | tf_op jit(solution)/shard_map/ppermute | solution.py:20
  2.1 41.6 %collective-permute-start.5 = (bf16[64,768]{1,0:T(8,128)(2,1)}, bf16[64,768]{1,0:T(8,128)(2,1)}, u32[]{:S(2)}, u32[]{:S(2)}) collective-permute-start(bf16[64,768]{1,0:T(8,128)(2,1)} %get-tuple-element.15), channel_id=1, source_target_pairs={{0,8},{4,12},{8,0},{12,4},{16,24},{20,28},{24,16},{28,20},{1,9},{5... | collective-permute-start | bytes 294920 | tf_op jit(solution)/shard_map/ppermute | solution.py:20
  5.9 25.1 %collective-permute-start = (s32[4,4]{1,0:T(4,128)}, s32[4,4]{1,0:T(4,128)}, u32[]{:S(2)}, u32[]{:S(2)}) collective-permute-start(s32[4,4]{1,0:T(4,128)} %get-tuple-element.18), channel_id=1, source_target_pairs={{0,4},{4,0},{8,12},{12,8},{16,20},{20,16},{24,28},{28,24},{1,5},{5... | collective-permute-start | bytes 200 | tf_op jit(solution)/shard_map/ppermute | solution.py:20
  10.9 24.9 %collective-permute-start.1 = (bf16[768,768]{0,1:T(8,128)(2,1)}, bf16[768,768]{0,1:T(8,128)(2,1)}, u32[]{:S(2)}, u32[]{:S(2)}) collective-permute-start(bf16[768,768]{0,1:T(8,128)(2,1)} %bitcast.4), channel_id=1, source_target_pairs={{0,4},{4,0},{8,12},{12,8},{16,20},{20,16},{24,28},{28,24},{1,5},{5... | collective-permute-start | bytes 3538952 | tf_op jit(solution)/shard_map/ppermute | solution.py:20
  11.2 28.8 %collective-permute-start.4 = (bf16[768,768]{1,0:T(8,128)(2,1)}, bf16[768,768]{1,0:T(8,128)(2,1)}, u32[]{:S(2)}, u32[]{:S(2)}) collective-permute-start(bf16[768,768]{1,0:T(8,128)(2,1)} %get-tuple-element.12), channel_id=1, source_target_pairs={{0,8},{4,12},{8,0},{12,4},{16,24},{20,28},{24,16},{28,20},{1,9},{5... | collective-permute-start | bytes 3538952 | tf_op jit(solution)/shard_map/ppermute | solution.py:20
  31.0 8.8 %collective-permute-start.3 = (s32[4,4]{1,0:T(4,128)}, s32[4,4]{1,0:T(4,128)S(1)}, u32[]{:S(2)}, u32[]{:S(2)}) collective-permute-start(s32[4,4]{1,0:T(4,128)} %get-tuple-element.17), channel_id=1, source_target_pairs={{0,8},{4,12},{8,0},{12,4},{16,24},{20,28},{24,16},{28,20},{1,9},{5... | collective-permute-start | bytes 200 | tf_op jit(solution)/shard_map/ppermute | solution.py:20
  35.8 11.8 %collective-permute-start.23 = (bf16[64,768]{1,0:T(8,128)(2,1)}, bf16[64,768]{1,0:T(8,128)(2,1)}, u32[]{:S(2)}, u32[]{:S(2)}) collective-permute-start(bf16[64,768]{1,0:T(8,128)(2,1)} %get-tuple-element.16), channel_id=1, source_target_pairs={{0,4},{4,0},{8,12},{12,8},{16,20},{20,16},{24,28},{28,24},{1,5},{5... | collective-permute-start | bytes 294920 | tf_op jit(solution)/shard_map/ppermute | solution.py:20
  39.9 9.0 %collective-permute-start.24 = (bf16[64,768]{1,0:T(8,128)(2,1)}, bf16[64,768]{1,0:T(8,128)(2,1)}, u32[]{:S(2)}, u32[]{:S(2)}) collective-permute-start(bf16[64,768]{1,0:T(8,128)(2,1)} %get-tuple-element.16), channel_id=1, source_target_pairs={{0,8},{4,12},{8,0},{12,4},{16,24},{20,28},{24,16},{28,20},{1,9},{5... | collective-permute-start | bytes 294920 | tf_op jit(solution)/shard_map/ppermute | solution.py:20
  45.3 5.7 %collective-permute-start.6 = (bf16[64,768]{1,0:T(8,128)(2,1)S(1)}, bf16[64,768]{1,0:T(8,128)(2,1)S(1)}, u32[]{:S(2)}, u32[]{:S(2)}) collective-permute-start(bf16[64,768]{1,0:T(8,128)(2,1)S(1)} %get-tuple-element.33), channel_id=1, source_target_pairs={{0,4},{4,0},{8,12},{12,8},{16,20},{20,16},{24,28},{28,24},{1,5},{5... | collective-permute-start | bytes 294920 | tf_op jit(solution)/shard_map/ppermute | solution.py:20
  45.9 5.5 %collective-permute-start.7 = (bf16[64,768]{1,0:T(8,128)(2,1)S(1)}, bf16[64,768]{1,0:T(8,128)(2,1)S(1)}, u32[]{:S(2)}, u32[]{:S(2)}) collective-permute-start(bf16[64,768]{1,0:T(8,128)(2,1)S(1)} %get-tuple-element.33), channel_id=1, source_target_pairs={{0,8},{4,12},{8,0},{12,4},{16,24},{20,28},{24,16},{28,20},{1,9},{5... | collective-permute-start | bytes 294920 | tf_op jit(solution)/shard_map/ppermute | solution.py:20
  50.4 7.6 %collective-permute-start.25 = (bf16[64,768]{1,0:T(8,128)(2,1)S(1)}, bf16[64,768]{1,0:T(8,128)(2,1)S(1)}, u32[]{:S(2)}, u32[]{:S(2)}) collective-permute-start(bf16[64,768]{1,0:T(8,128)(2,1)S(1)} %get-tuple-element.19), channel_id=1, source_target_pairs={{0,4},{4,0},{8,12},{12,8},{16,20},{20,16},{24,28},{28,24},{1,5},{5... | collective-permute-start | bytes 294920 | tf_op jit(solution)/shard_map/ppermute | solution.py:20
  50.5 8.3 %collective-permute-start.26 = (bf16[64,768]{1,0:T(8,128)(2,1)S(1)}, bf16[64,768]{1,0:T(8,128)(2,1)S(1)}, u32[]{:S(2)}, u32[]{:S(2)}) collective-permute-start(bf16[64,768]{1,0:T(8,128)(2,1)S(1)} %get-tuple-element.19), channel_id=1, source_target_pairs={{0,8},{4,12},{8,0},{12,4},{16,24},{20,28},{24,16},{28,20},{1,9},{5... | collective-permute-start | bytes 294920 | tf_op jit(solution)/shard_map/ppermute | solution.py:20
  52.4 61.2 %collective-permute-start.8 = (bf16[3,256,128]{2,1,0:T(8,128)(2,1)S(1)}, bf16[3,256,128]{2,1,0:T(8,128)(2,1)S(1)}, u32[]{:S(2)}, u32[]{:S(2)}) collective-permute-start(bf16[3,256,128]{2,1,0:T(8,128)(2,1)S(1)} %slice_select_fusion), channel_id=1, source_target_pairs={{0,1},{1,2},{2,3},{3,0},{4,5},{5,6},{6,7},{7,4},{8,9},{9,10},{10,1... | collective-permute-start | bytes 589832 | tf_op jit(solution)/shard_map/ppermute | solution.py:39
  54.1 62.4 %collective-permute-start.9 = (bf16[3,256,128]{2,1,0:T(8,128)(2,1)S(1)}, bf16[3,256,128]{2,1,0:T(8,128)(2,1)S(1)}, u32[]{:S(2)}, u32[]{:S(2)}) collective-permute-start(bf16[3,256,128]{2,1,0:T(8,128)(2,1)S(1)} %slice_select_fusion), channel_id=1, source_target_pairs={{0,2},{1,3},{2,0},{3,1},{4,6},{5,7},{6,4},{7,5},{8,10},{9,11},{10,... | collective-permute-start | bytes 589832 | tf_op jit(solution)/shard_map/ppermute | solution.py:39
  56.7 59.8 %collective-permute-start.10 = (bf16[3,256,128]{2,1,0:T(8,128)(2,1)S(1)}, bf16[3,256,128]{2,1,0:T(8,128)(2,1)S(1)}, u32[]{:S(2)}, u32[]{:S(2)}) collective-permute-start(bf16[3,256,128]{2,1,0:T(8,128)(2,1)S(1)} %slice_select_fusion), channel_id=1, source_target_pairs={{0,3},{1,0},{2,1},{3,2},{4,7},{5,4},{6,5},{7,6},{8,11},{9,8},{10,9... | collective-permute-start | bytes 589832 | tf_op jit(solution)/shard_map/ppermute | solution.py:39
  58.8 5.2 %collective-permute-start.12 = (bf16[64,768]{1,0:T(8,128)(2,1)S(1)}, bf16[64,768]{1,0:T(8,128)(2,1)S(1)}, u32[]{:S(2)}, u32[]{:S(2)}) collective-permute-start(bf16[64,768]{1,0:T(8,128)(2,1)S(1)} %convert_element_type.170), channel_id=1, source_target_pairs={{0,8},{4,12},{8,0},{12,4},{16,24},{20,28},{24,16},{28,20},{1,9},{5... | collective-permute-start | bytes 294920 | tf_op jit(solution)/shard_map/ppermute | solution.py:20
  61.0 4.8 %collective-permute-start.27 = (bf16[64,768]{1,0:T(8,128)(2,1)S(1)}, bf16[64,768]{1,0:T(8,128)(2,1)S(1)}, u32[]{:S(2)}, u32[]{:S(2)}) collective-permute-start(bf16[64,768]{1,0:T(8,128)(2,1)S(1)} %get-tuple-element.21), channel_id=1, source_target_pairs={{0,4},{4,0},{8,12},{12,8},{16,20},{20,16},{24,28},{28,24},{1,5},{5... | collective-permute-start | bytes 294920 | tf_op jit(solution)/shard_map/ppermute | solution.py:20
  64.0 4.6 %collective-permute-start.28 = (bf16[64,768]{1,0:T(8,128)(2,1)S(1)}, bf16[64,768]{1,0:T(8,128)(2,1)S(1)}, u32[]{:S(2)}, u32[]{:S(2)}) collective-permute-start(bf16[64,768]{1,0:T(8,128)(2,1)S(1)} %get-tuple-element.21), channel_id=1, source_target_pairs={{0,8},{4,12},{8,0},{12,4},{16,24},{20,28},{24,16},{28,20},{1,9},{5... | collective-permute-start | bytes 294920 | tf_op jit(solution)/shard_map/ppermute | solution.py:20
  68.6 4.6 %collective-permute-start.14 = (bf16[64,768]{1,0:T(8,128)(2,1)S(1)}, bf16[64,768]{1,0:T(8,128)(2,1)S(1)}, u32[]{:S(2)}, u32[]{:S(2)}) collective-permute-start(bf16[64,768]{1,0:T(8,128)(2,1)S(1)} %get-tuple-element.35), channel_id=1, source_target_pairs={{0,8},{4,12},{8,0},{12,4},{16,24},{20,28},{24,16},{28,20},{1,9},{5... | collective-permute-start | bytes 294920 | tf_op jit(solution)/shard_map/ppermute | solution.py:20
  73.2 4.6 %collective-permute-start.30 = (bf16[64,768]{1,0:T(8,128)(2,1)S(1)}, bf16[64,768]{1,0:T(8,128)(2,1)S(1)}, u32[]{:S(2)}, u32[]{:S(2)}) collective-permute-start(bf16[64,768]{1,0:T(8,128)(2,1)S(1)} %get-tuple-element.23), channel_id=1, source_target_pairs={{0,8},{4,12},{8,0},{12,4},{16,24},{20,28},{24,16},{28,20},{1,9},{5... | collective-permute-start | bytes 294920 | tf_op jit(solution)/shard_map/ppermute | solution.py:20
  75.1 4.9 %collective-permute-start.15 = (bf16[64,768]{1,0:T(8,128)(2,1)S(1)}, bf16[64,768]{1,0:T(8,128)(2,1)S(1)}, u32[]{:S(2)}, u32[]{:S(2)}) collective-permute-start(bf16[64,768]{1,0:T(8,128)(2,1)S(1)} %get-tuple-element.37), channel_id=1, source_target_pairs={{0,4},{4,0},{8,12},{12,8},{16,20},{20,16},{24,28},{28,24},{1,5},{5... | collective-permute-start | bytes 294920 | tf_op jit(solution)/shard_map/ppermute | solution.py:20
  77.8 4.6 %collective-permute-start.16 = (bf16[64,768]{1,0:T(8,128)(2,1)S(1)}, bf16[64,768]{1,0:T(8,128)(2,1)S(1)}, u32[]{:S(2)}, u32[]{:S(2)}) collective-permute-start(bf16[64,768]{1,0:T(8,128)(2,1)S(1)} %get-tuple-element.37), channel_id=1, source_target_pairs={{0,8},{4,12},{8,0},{12,4},{16,24},{20,28},{24,16},{28,20},{1,9},{5... | collective-permute-start | bytes 294920 | tf_op jit(solution)/shard_map/ppermute | solution.py:20
  81.4 4.9 %collective-permute-start.32 = (bf16[64,768]{1,0:T(8,128)(2,1)S(1)}, bf16[64,768]{1,0:T(8,128)(2,1)S(1)}, u32[]{:S(2)}, u32[]{:S(2)}) collective-permute-start(bf16[64,768]{1,0:T(8,128)(2,1)S(1)} %get-tuple-element.25), channel_id=1, source_target_pairs={{0,8},{4,12},{8,0},{12,4},{16,24},{20,28},{24,16},{28,20},{1,9},{5... | collective-permute-start | bytes 294920 | tf_op jit(solution)/shard_map/ppermute | solution.py:20
  86.2 4.6 %collective-permute-start.18 = (bf16[64,768]{1,0:T(8,128)(2,1)S(1)}, bf16[64,768]{1,0:T(8,128)(2,1)S(1)}, u32[]{:S(2)}, u32[]{:S(2)}) collective-permute-start(bf16[64,768]{1,0:T(8,128)(2,1)S(1)} %get-tuple-element.39), channel_id=1, source_target_pairs={{0,8},{4,12},{8,0},{12,4},{16,24},{20,28},{24,16},{28,20},{1,9},{5... | collective-permute-start | bytes 294920 | tf_op jit(solution)/shard_map/ppermute | solution.py:20
  90.9 4.6 %collective-permute-start.34 = (bf16[64,768]{1,0:T(8,128)(2,1)S(1)}, bf16[64,768]{1,0:T(8,128)(2,1)S(1)}, u32[]{:S(2)}, u32[]{:S(2)}) collective-permute-start(bf16[64,768]{1,0:T(8,128)(2,1)S(1)} %get-tuple-element.27), channel_id=1, source_target_pairs={{0,8},{4,12},{8,0},{12,4},{16,24},{20,28},{24,16},{28,20},{1,9},{5... | collective-permute-start | bytes 294920 | tf_op jit(solution)/shard_map/ppermute | solution.py:20
  91.8 4.9 %collective-permute-start.19 = (bf16[64,768]{1,0:T(8,128)(2,1)S(1)}, bf16[64,768]{1,0:T(8,128)(2,1)S(1)}, u32[]{:S(2)}, u32[]{:S(2)}) collective-permute-start(bf16[64,768]{1,0:T(8,128)(2,1)S(1)} %get-tuple-element.41), channel_id=1, source_target_pairs={{0,4},{4,0},{8,12},{12,8},{16,20},{20,16},{24,28},{28,24},{1,5},{5... | collective-permute-start | bytes 294920 | tf_op jit(solution)/shard_map/ppermute | solution.py:20
  95.5 4.6 %collective-permute-start.20 = (bf16[64,768]{1,0:T(8,128)(2,1)S(1)}, bf16[64,768]{1,0:T(8,128)(2,1)S(1)}, u32[]{:S(2)}, u32[]{:S(2)}) collective-permute-start(bf16[64,768]{1,0:T(8,128)(2,1)S(1)} %get-tuple-element.41), channel_id=1, source_target_pairs={{0,8},{4,12},{8,0},{12,4},{16,24},{20,28},{24,16},{28,20},{1,9},{5... | collective-permute-start | bytes 294920 | tf_op jit(solution)/shard_map/ppermute | solution.py:20
  98.1 4.9 %collective-permute-start.36 = (bf16[64,768]{1,0:T(8,128)(2,1)S(1)}, bf16[64,768]{1,0:T(8,128)(2,1)S(1)}, u32[]{:S(2)}, u32[]{:S(2)}) collective-permute-start(bf16[64,768]{1,0:T(8,128)(2,1)S(1)} %get-tuple-element.29), channel_id=1, source_target_pairs={{0,8},{4,12},{8,0},{12,4},{16,24},{20,28},{24,16},{28,20},{1,9},{5... | collective-permute-start | bytes 294920 | tf_op jit(solution)/shard_map/ppermute | solution.py:20
  112.5 9.7 %collective-permute-start.39 = (bf16[128,768]{1,0:T(8,128)(2,1)S(1)}, bf16[128,768]{1,0:T(8,128)(2,1)S(1)}, u32[]{:S(2)}, u32[]{:S(2)}) collective-permute-start(bf16[128,768]{1,0:T(8,128)(2,1)S(1)} %pad_maximum_fusion.5), channel_id=1, source_target_pairs={{0,1},{1,2},{2,3},{3,0},{4,5},{5,6},{6,7},{7,4},{8,9},{9,10},{10,1... | collective-permute-start | bytes 589832 | tf_op jit(solution)/shard_map/ppermute | solution.py:29
  113.3 14.0 %collective-permute-start.40 = (bf16[128,768]{1,0:T(8,128)(2,1)S(1)}, bf16[128,768]{1,0:T(8,128)(2,1)S(1)}, u32[]{:S(2)}, u32[]{:S(2)}) collective-permute-start(bf16[128,768]{1,0:T(8,128)(2,1)S(1)} %pad_maximum_fusion.5), channel_id=1, source_target_pairs={{0,2},{1,3},{2,0},{3,1},{4,6},{5,7},{6,4},{7,5},{8,10},{9,11},{10,... | collective-permute-start | bytes 589832 | tf_op jit(solution)/shard_map/ppermute | solution.py:29
  113.6 13.7 %collective-permute-start.41 = (bf16[128,768]{1,0:T(8,128)(2,1)S(1)}, bf16[128,768]{1,0:T(8,128)(2,1)S(1)}, u32[]{:S(2)}, u32[]{:S(2)}) collective-permute-start(bf16[128,768]{1,0:T(8,128)(2,1)S(1)} %pad_maximum_fusion.5), channel_id=1, source_target_pairs={{0,3},{1,0},{2,1},{3,2},{4,7},{5,4},{6,5},{7,6},{8,11},{9,8},{10,9... | collective-permute-start | bytes 589832 | tf_op jit(solution)/shard_map/ppermute | solution.py:29
  116.6 12.5 %collective-permute-start.42 = (bf16[4,3,256,128]{3,2,1,0:T(8,128)(2,1)S(1)}, bf16[4,3,256,128]{3,2,1,0:T(8,128)(2,1)}, u32[]{:S(2)}, u32[]{:S(2)}) collective-permute-start(bf16[4,3,256,128]{3,2,1,0:T(8,128)(2,1)S(1)} %pad_maximum_fusion.3), channel_id=1, source_target_pairs={{0,4},{4,0},{8,12},{12,8},{16,20},{20,16},{24,28},{28,24},{1,5},{5... | collective-permute-start | bytes 2359304 | tf_op jit(solution)/shard_map/ppermute | solution.py:20
  (35 other events, 96.3 us)

commit v12 on v9

--- a/solution.py
+++ b/solution.py
@@ -125,13 +125,11 @@
         mine = jnp.where(first_of_pair, held[:, :half_rows], held[:, half_rows:])
         mine = gather_pieces(mine)
         theirs = swapped(mine, "atoms", 0)
-        gathered.append(
-            jnp.where(
-                first_of_pair,
-                jnp.concatenate([mine, theirs], axis=2),
-                jnp.concatenate([theirs, mine], axis=2),
-            )
-        )
+        mine_start = (atoms_here % 2) * half_rows
+        whole = jnp.zeros(mine.shape[:2] + (2 * half_rows,) + mine.shape[3:], mine.dtype)
+        whole = lax.dynamic_update_slice_in_dim(whole, mine, mine_start, axis=2)
+        whole = lax.dynamic_update_slice_in_dim(whole, theirs, half_rows - mine_start, axis=2)
+        gathered.append(whole)
         return current
 
     half_bands = subspace.shape[0] // 2

time: 169 us -> 169 us (level)
  other arithmetic: 14.3 us -> 10.8 us
  waiting for transfers between devices: 45.1 us -> 48.5 us
  local copies, waits for them, and re-layouts: 23.5 us -> 25.6 us
  starting transfers between devices: 48.5 us -> 46.4 us
    select_n x1 -> x0, other arithmetic: 3.8 us -> none  [start_rotation_gather(): jnp.where(first_of_pair, jnp.concatenate([mine, theirs], axis=2), jnp.con...]
    ppermute x49, waiting for transfers between devices: 32.6 us -> 35.7 us  [swapped(): return lax.ppermute(value, axis, pairs)]
    ppermute x49, starting transfers between devices: 37.7 us -> 34.7 us  [swapped(): return lax.ppermute(value, axis, pairs)]
  transfers between devices with their start and end apart: 55 -> 55, of which waited for: 22 -> 21; matrix products, arithmetic and copies ran while one was open for 35% -> 35% of each run, Pallas kernels for 0% -> 0%
where the time goes in v12:
time: 169 us; the launch traced here: 167 us
  waiting for transfers between devices  48.5 us (29%)
  starting transfers between devices  46.4 us (27%)
  matrix products  34.8 us (21%)
  local copies, waits for them, and re-layouts  25.6 us (15%)
  other arithmetic  10.8 us (6%)
    ppermute x49, waiting for transfers between devices, swapped(): return lax.ppermute(value, axis, pairs)  35.7 us
    ppermute x49, starting transfers between devices, swapped(): return lax.ppermute(value, axis, pairs)  34.7 us
    dot_general x32, matrix products, apply_operator(): jnp.dot(other_rows, other_pair[round_index], preferred_element_type=jnp.f...  14.5 us
    ppermute x3, waiting for transfers between devices, gather_bands(): pieces.append(lax.ppermute(value, 'bands', pairs))  12.8 us
    dot_general x4, matrix products, pattern_mask(): lax.dot_general(per_row.astype(jnp.bfloat16), col_onehot, (((1,), (1,)),...  8.59 us
    dot_general x16, matrix products, apply_operator(): result = jnp.dot(values, diag_sym, preferred_element_type=jnp.float32)  6.63 us
    ppermute x3, starting transfers between devices, gather_bands(): pieces.append(lax.ppermute(value, 'bands', pairs))  6.07 us
    ppermute x3, starting transfers between devices, gather_pieces(): pieces.append(lax.ppermute(value, 'bands', pairs))  5.64 us
  transfers between devices with their start and end apart: 55, of which 21 were waited for; matrix products, arithmetic and copies ran while one was open for 35% of the time, Pallas kernels for 0%

profile of v12, /device:TPU:0, one launch (start us, length us, event | category | flops | bytes accessed | tf_op | source)
XLA Modules:
  0.0 166.8 jit_solution(10364481066711205392)
XLA Ops:
  2.1 2.5 %collective-permute-start.5 = (bf16[64,768]{1,0:T(8,128)(2,1)}, bf16[64,768]{1,0:T(8,128)(2,1)}, u32[]{:S(2)}, u32[]{:S(2)}) collective-permute-start(bf16[64,768]{1,0:T(8,128)(2,1)} %get-tuple-element.16), channel_id=1, source_target_pairs={{0,8},{4,12},{8,0},{12,4},{16,24},{20,28},{24,16},{28,20},{1,9},{5... | collective-permute-start | bytes 294920 | tf_op jit(solution)/shard_map/ppermute | solution.py:20
  6.1 2.8 %slice_bitcast_fusion = (bf16[768,768]{1,0:T(8,128)(2,1)}, bf16[1,768,768]{2,1,0:T(8,128)(2,1)S(1)}) fusion(bf16[2,768,768]{2,1,0:T(8,128)(2,1)} %param.8), kind=kLoop, calls=%fused_computation.21 | loop fusion | bytes 4718592 | tf_op jit(solution)/shard_map/squeeze | solution.py:74
  12.5 1.9 %add_multiply_fusion = f32[768,768]{1,0:T(8,128)S(1)} fusion(bf16[768,768]{1,0:T(8,128)(2,1)} %param.7, s32[768]{0:T(1024)S(1)} %get-tuple-element.49), kind=kLoop, calls=%fused_computation.7 | loop fusion | flops 4128768 | bytes 3542016 | tf_op jit(solution)/shard_map/mul | solution.py:81
  16.4 2.4 %copy.23 = bf16[768,768]{0,1:T(8,128)(2,1)} copy(bf16[768,768]{1,0:T(8,128)(2,1)} %get-tuple-element.12) | data formatting | bytes 2359296 | tf_op jit(solution)/shard_map/squeeze | solution.py:74
  18.8 2.4 %copy.20 = pred[768,768]{0,1:T(8,128)(4,1)} copy(pred[768,768]{1,0:T(8,128)(4,1)} %convolution_compare_fusion.1) | data formatting | bytes 1179648 | tf_op jit(solution)/shard_map/gt | solution.py:67
  21.3 2.0 %copy.16 = f32[768,768]{0,1:T(8,128)} copy(f32[768,768]{1,0:T(8,128)S(1)} %add_multiply_fusion) | data formatting | bytes 4718592 | tf_op jit(solution)/shard_map/mul | solution.py:81
  23.3 2.8 %copy.22 = pred[768,768]{0,1:T(32,128)(4,1)} copy(pred[768,768]{1,0:T(32,128)(4,1)} %convolution_compare_fusion) | data formatting | bytes 1179648 | tf_op jit(solution)/shard_map/gt | solution.py:67
  27.8 2.4 %fusion.2 = bf16[768,768]{1,0:T(8,128)(2,1)S(1)} fusion(f32[768,768]{0,1:T(8,128)} %copy.16, s32[768]{0:T(1024)S(1)} %get-tuple-element.49, bf16[768,768]{1,0:T(8,128)(2,1)S(1)} %copy-done.2), kind=kLoop, calls=%fused_computation.6 | loop fusion | flops 5308416 | bytes 4721664 | tf_op jit(solution)/shard_map/convert_element_type | solution.py:82
  32.3 1.9 %collective-permute-start.3 = (s32[4,4]{1,0:T(4,128)S(1)}, s32[4,4]{1,0:T(4,128)}, u32[]{:S(2)}, u32[]{:S(2)}) collective-permute-start(s32[4,4]{1,0:T(4,128)S(1)} %copy-done.9), channel_id=1, source_target_pairs={{0,8},{4,12},{8,0},{12,4},{16,24},{20,28},{24,16},{28,20},{1,9},{5... | collective-permute-start | bytes 200 | tf_op jit(solution)/shard_map/ppermute | solution.py:20
  34.2 2.8 %fusion.3 = f32[768,768]{1,0:T(8,128)} fusion(s32[768]{0:T(1024)S(1)} %get-tuple-element.49, s32[768]{0:T(1024)S(1)} %convert_reduce_fusion.1, s32[4,4]{1,0:T(4,128)} %collective-permute-done), kind=kOutput, calls=%fused_computation.26 | convolution fusion | flops 4752400 | bytes 2365504 | tf_op jit(solution)/shard_map/dot_general | solution.py:63
  37.0 2.4 %copy.18 = bf16[768,768]{1,0:T(8,128)(2,1)} copy(bf16[768,768]{0,1:T(8,128)(2,1)} %collective-permute-done.1) | data formatting | bytes 2359296 | tf_op jit(solution)/shard_map/ppermute | solution.py:20
  39.4 2.8 %fusion.1 = bf16[768,768]{1,0:T(8,128)(2,1)S(1)} fusion(bf16[768,768]{1,0:T(8,128)(2,1)} %copy.18, f32[768,768]{1,0:T(8,128)} %fusion.3, pred[768,768]{0,1:T(8,128)(4,1)} %copy.20, bf16[1,768,768]{1,2,0:T(8,128)(2,1)S(1)} %copy.25), kind=kLoop, calls=%fused_computation.4 | loop fusion | flops 4128768 | bytes 6488064 | tf_op jit(solution)/shard_map/convert_element_type | solution.py:96
  42.4 2.7 %fusion = bf16[768,768]{1,0:T(8,128)(2,1)S(1)} fusion(bf16[768,768]{1,0:T(8,128)(2,1)} %collective-permute-done.4, pred[768,768]{0,1:T(32,128)(4,1)} %copy.22, bf16[768,768]{0,1:T(8,128)(2,1)} %copy.23, s32[768]{0:T(1024)S(1)} %get-tuple-element.48, s32[768]{0:T(1024)S(1)} %get-tuple-element.49, s32[4,4]{1,0:T(4,128)} %collective-permute-done.3), kind=kOutput, calls=%fused_computation.2 | convolution fusion | flops 8881168 | bytes 4134976 | tf_op jit(solution)/shard_map/dot_general | solution.py:63
  56.8 2.6 %collective-permute-start.9 = (bf16[3,256,128]{2,1,0:T(8,128)(2,1)S(1)}, bf16[3,256,128]{2,1,0:T(8,128)(2,1)S(1)}, u32[]{:S(2)}, u32[]{:S(2)}) collective-permute-start(bf16[3,256,128]{2,1,0:T(8,128)(2,1)S(1)} %slice_select_fusion), channel_id=1, source_target_pairs={{0,2},{1,3},{2,0},{3,1},{4,6},{5,7},{6,4},{7,5},{8,10},{9,11},{10,... | collective-permute-start | bytes 589832 | tf_op jit(solution)/shard_map/ppermute | solution.py:39
  64.4 2.4 %collective-permute-done.13 = bf16[64,768]{1,0:T(8,128)(2,1)S(1)} collective-permute-done((bf16[64,768]{1,0:T(8,128)(2,1)S(1)}, bf16[64,768]{1,0:T(8,128)(2,1)S(1)}, u32[]{:S(2)}, u32[]{:S(2)}) %collective-permute-start.13) | collective-permute-done | bytes 98336 | tf_op jit(solution)/shard_map/ppermute | solution.py:20
  69.4 2.0 %collective-permute-done.29 = bf16[64,768]{1,0:T(8,128)(2,1)S(1)} collective-permute-done((bf16[64,768]{1,0:T(8,128)(2,1)S(1)}, bf16[64,768]{1,0:T(8,128)(2,1)S(1)}, u32[]{:S(2)}, u32[]{:S(2)}) %collective-permute-start.29) | collective-permute-done | bytes 98336 | tf_op jit(solution)/shard_map/ppermute | solution.py:20
  83.3 1.9 %collective-permute-start.19 = (bf16[64,768]{1,0:T(8,128)(2,1)S(1)}, bf16[64,768]{1,0:T(8,128)(2,1)S(1)}, u32[]{:S(2)}, u32[]{:S(2)}) collective-permute-start(bf16[64,768]{1,0:T(8,128)(2,1)S(1)} %get-tuple-element.40), channel_id=1, source_target_pairs={{0,8},{4,12},{8,0},{12,4},{16,24},{20,28},{24,16},{28,20},{1,9},{5... | collective-permute-start | bytes 294920 | tf_op jit(solution)/shard_map/ppermute | solution.py:20
  89.2 2.1 %collective-permute-start.21 = (bf16[64,768]{1,0:T(8,128)(2,1)S(1)}, bf16[64,768]{1,0:T(8,128)(2,1)S(1)}, u32[]{:S(2)}, u32[]{:S(2)}) collective-permute-start(bf16[64,768]{1,0:T(8,128)(2,1)S(1)} %get-tuple-element.42), channel_id=1, source_target_pairs={{0,8},{4,12},{8,0},{12,4},{16,24},{20,28},{24,16},{28,20},{1,9},{5... | collective-permute-start | bytes 294920 | tf_op jit(solution)/shard_map/ppermute | solution.py:20
  95.4 2.0 %collective-permute-start.23 = (bf16[64,768]{1,0:T(8,128)(2,1)S(1)}, bf16[64,768]{1,0:T(8,128)(2,1)S(1)}, u32[]{:S(2)}, u32[]{:S(2)}) collective-permute-start(bf16[64,768]{1,0:T(8,128)(2,1)S(1)} %get-tuple-element.44), channel_id=1, source_target_pairs={{0,8},{4,12},{8,0},{12,4},{16,24},{20,28},{24,16},{28,20},{1,9},{5... | collective-permute-start | bytes 294920 | tf_op jit(solution)/shard_map/ppermute | solution.py:20
  101.6 2.2 %collective-permute-done.39 = bf16[64,768]{1,0:T(8,128)(2,1)S(1)} collective-permute-done((bf16[64,768]{1,0:T(8,128)(2,1)S(1)}, bf16[64,768]{1,0:T(8,128)(2,1)S(1)}, u32[]{:S(2)}, u32[]{:S(2)}) %collective-permute-start.39) | collective-permute-done | bytes 98336 | tf_op jit(solution)/shard_map/ppermute | solution.py:20
  104.1 3.5 %collective-permute-start.40 = (bf16[128,768]{1,0:T(8,128)(2,1)S(1)}, bf16[128,768]{1,0:T(8,128)(2,1)S(1)}, u32[]{:S(2)}, u32[]{:S(2)}) collective-permute-start(bf16[128,768]{1,0:T(8,128)(2,1)S(1)} %pad_maximum_fusion.5), channel_id=1, source_target_pairs={{0,1},{1,2},{2,3},{3,0},{4,5},{5,6},{6,7},{7,4},{8,9},{9,10},{10,1... | collective-permute-start | bytes 589832 | tf_op jit(solution)/shard_map/ppermute | solution.py:29
  107.6 2.6 %collective-permute-start.41 = (bf16[128,768]{1,0:T(8,128)(2,1)S(1)}, bf16[128,768]{1,0:T(8,128)(2,1)S(1)}, u32[]{:S(2)}, u32[]{:S(2)}) collective-permute-start(bf16[128,768]{1,0:T(8,128)(2,1)S(1)} %pad_maximum_fusion.5), channel_id=1, source_target_pairs={{0,2},{1,3},{2,0},{3,1},{4,6},{5,7},{6,4},{7,5},{8,10},{9,11},{10,... | collective-permute-start | bytes 589832 | tf_op jit(solution)/shard_map/ppermute | solution.py:29
  110.2 5.2 %collective-permute-done.40 = bf16[128,768]{1,0:T(8,128)(2,1)S(1)} collective-permute-done((bf16[128,768]{1,0:T(8,128)(2,1)S(1)}, bf16[128,768]{1,0:T(8,128)(2,1)S(1)}, u32[]{:S(2)}, u32[]{:S(2)}) %collective-permute-start.40) | collective-permute-done | bytes 196640 | tf_op jit(solution)/shard_map/ppermute | solution.py:29
  115.5 7.5 %collective-permute-done.41 = bf16[128,768]{1,0:T(8,128)(2,1)S(1)} collective-permute-done((bf16[128,768]{1,0:T(8,128)(2,1)S(1)}, bf16[128,768]{1,0:T(8,128)(2,1)S(1)}, u32[]{:S(2)}, u32[]{:S(2)}) %collective-permute-start.41) | collective-permute-done | bytes 196640 | tf_op jit(solution)/shard_map/ppermute | solution.py:29
  129.8 2.8 %collective-permute-done.44 = f32[512]{0:T(512)S(1)} collective-permute-done((f32[512]{0:T(512)S(1)}, f32[512]{0:T(512)S(1)}, u32[]{:S(2)}, u32[]{:S(2)}) %collective-permute-start.44) | collective-permute-done | bytes 2080 | tf_op jit(solution)/shard_map/ppermute | solution.py:20
  134.1 2.1 %collective-permute-done.45 = f32[512]{0:T(512)S(1)} collective-permute-done((f32[512]{0:T(512)S(1)}, f32[512]{0:T(512)S(1)}, u32[]{:S(2)}, u32[]{:S(2)}) %collective-permute-start.45) | collective-permute-done | bytes 2080 | tf_op jit(solution)/shard_map/ppermute | solution.py:20
  139.7 2.8 %collective-permute-done.47 = f32[512]{0:T(512)S(1)} collective-permute-done((f32[512]{0:T(512)S(1)}, f32[512]{0:T(512)S(1)}, u32[]{:S(2)}, u32[]{:S(2)}) %collective-permute-start.47) | collective-permute-done | bytes 2080 | tf_op jit(solution)/shard_map/ppermute | solution.py:20
  144.0 2.1 %collective-permute-done.48 = f32[512]{0:T(512)S(1)} collective-permute-done((f32[512]{0:T(512)S(1)}, f32[512]{0:T(512)S(1)}, u32[]{:S(2)}, u32[]{:S(2)}) %collective-permute-start.48) | collective-permute-done | bytes 2080 | tf_op jit(solution)/shard_map/ppermute | solution.py:20
  149.7 2.8 %collective-permute-done.50 = f32[512]{0:T(512)S(1)} collective-permute-done((f32[512]{0:T(512)S(1)}, f32[512]{0:T(512)S(1)}, u32[]{:S(2)}, u32[]{:S(2)}) %collective-permute-start.50) | collective-permute-done | bytes 2080 | tf_op jit(solution)/shard_map/ppermute | solution.py:20
  154.0 2.1 %collective-permute-done.51 = f32[512]{0:T(512)S(1)} collective-permute-done((f32[512]{0:T(512)S(1)}, f32[512]{0:T(512)S(1)}, u32[]{:S(2)}, u32[]{:S(2)}) %collective-permute-start.51) | collective-permute-done | bytes 2080 | tf_op jit(solution)/shard_map/ppermute | solution.py:20
  159.5 2.7 %collective-permute-done.53 = f32[128]{0:T(128)S(1)} collective-permute-done((f32[128]{0:T(128)S(1)}, f32[128]{0:T(128)S(1)}, u32[]{:S(2)}, u32[]{:S(2)}) %collective-permute-start.53) | collective-permute-done | bytes 544 | tf_op jit(solution)/shard_map/ppermute | solution.py:20
  163.8 2.0 %collective-permute-done.54 = f32[128]{0:T(128)S(1)} collective-permute-done((f32[128]{0:T(128)S(1)}, f32[128]{0:T(128)S(1)}, u32[]{:S(2)}, u32[]{:S(2)}) %collective-permute-start.54) | collective-permute-done | bytes 544 | tf_op jit(solution)/shard_map/ppermute | solution.py:20
  (216 shorter events, 80.9 us)
Async XLA Ops:
  1.6 43.5 %collective-permute-start.2 = (bf16[64,768]{1,0:T(8,128)(2,1)}, bf16[64,768]{1,0:T(8,128)(2,1)}, u32[]{:S(2)}, u32[]{:S(2)}) collective-permute-start(bf16[64,768]{1,0:T(8,128)(2,1)} %get-tuple-element.16), channel_id=1, source_target_pairs={{0,4},{4,0},{8,12},{12,8},{16,20},{20,16},{24,28},{28,24},{1,5},{5... | collective-permute-start | bytes 294920 | tf_op jit(solution)/shard_map/ppermute | solution.py:20
  2.1 44.4 %collective-permute-start.5 = (bf16[64,768]{1,0:T(8,128)(2,1)}, bf16[64,768]{1,0:T(8,128)(2,1)}, u32[]{:S(2)}, u32[]{:S(2)}) collective-permute-start(bf16[64,768]{1,0:T(8,128)(2,1)} %get-tuple-element.16), channel_id=1, source_target_pairs={{0,8},{4,12},{8,0},{12,4},{16,24},{20,28},{24,16},{28,20},{1,9},{5... | collective-permute-start | bytes 294920 | tf_op jit(solution)/shard_map/ppermute | solution.py:20
  5.9 26.4 %collective-permute-start = (s32[4,4]{1,0:T(4,128)}, s32[4,4]{1,0:T(4,128)}, u32[]{:S(2)}, u32[]{:S(2)}) collective-permute-start(s32[4,4]{1,0:T(4,128)} %get-tuple-element.19), channel_id=1, source_target_pairs={{0,4},{4,0},{8,12},{12,8},{16,20},{20,16},{24,28},{28,24},{1,5},{5... | collective-permute-start | bytes 200 | tf_op jit(solution)/shard_map/ppermute | solution.py:20
  9.6 27.4 %collective-permute-start.1 = (bf16[768,768]{0,1:T(8,128)(2,1)S(1)}, bf16[768,768]{0,1:T(8,128)(2,1)}, u32[]{:S(2)}, u32[]{:S(2)}) collective-permute-start(bf16[768,768]{0,1:T(8,128)(2,1)S(1)} %bitcast.208), channel_id=1, source_target_pairs={{0,4},{4,0},{8,12},{12,8},{16,20},{20,16},{24,28},{28,24},{1,5},{5... | collective-permute-start | bytes 3538952 | tf_op jit(solution)/shard_map/ppermute | solution.py:20
  9.9 32.5 %collective-permute-start.4 = (bf16[768,768]{1,0:T(8,128)(2,1)}, bf16[768,768]{1,0:T(8,128)(2,1)}, u32[]{:S(2)}, u32[]{:S(2)}) collective-permute-start(bf16[768,768]{1,0:T(8,128)(2,1)} %get-tuple-element.12), channel_id=1, source_target_pairs={{0,8},{4,12},{8,0},{12,4},{16,24},{20,28},{24,16},{28,20},{1,9},{5... | collective-permute-start | bytes 3538952 | tf_op jit(solution)/shard_map/ppermute | solution.py:20
  32.3 10.0 %collective-permute-start.3 = (s32[4,4]{1,0:T(4,128)S(1)}, s32[4,4]{1,0:T(4,128)}, u32[]{:S(2)}, u32[]{:S(2)}) collective-permute-start(s32[4,4]{1,0:T(4,128)S(1)} %copy-done.9), channel_id=1, source_target_pairs={{0,8},{4,12},{8,0},{12,4},{16,24},{20,28},{24,16},{28,20},{1,9},{5... | collective-permute-start | bytes 200 | tf_op jit(solution)/shard_map/ppermute | solution.py:20
  37.0 13.3 %collective-permute-start.24 = (bf16[64,768]{1,0:T(8,128)(2,1)}, bf16[64,768]{1,0:T(8,128)(2,1)}, u32[]{:S(2)}, u32[]{:S(2)}) collective-permute-start(bf16[64,768]{1,0:T(8,128)(2,1)} %get-tuple-element.17), channel_id=1, source_target_pairs={{0,4},{4,0},{8,12},{12,8},{16,20},{20,16},{24,28},{28,24},{1,5},{5... | collective-permute-start | bytes 294920 | tf_op jit(solution)/shard_map/ppermute | solution.py:20
  42.3 9.3 %collective-permute-start.25 = (bf16[64,768]{1,0:T(8,128)(2,1)}, bf16[64,768]{1,0:T(8,128)(2,1)}, u32[]{:S(2)}, u32[]{:S(2)}) collective-permute-start(bf16[64,768]{1,0:T(8,128)(2,1)} %get-tuple-element.17), channel_id=1, source_target_pairs={{0,8},{4,12},{8,0},{12,4},{16,24},{20,28},{24,16},{28,20},{1,9},{5... | collective-permute-start | bytes 294920 | tf_op jit(solution)/shard_map/ppermute | solution.py:20
  48.1 5.6 %collective-permute-start.6 = (bf16[64,768]{1,0:T(8,128)(2,1)S(1)}, bf16[64,768]{1,0:T(8,128)(2,1)S(1)}, u32[]{:S(2)}, u32[]{:S(2)}) collective-permute-start(bf16[64,768]{1,0:T(8,128)(2,1)S(1)} %get-tuple-element.34), channel_id=1, source_target_pairs={{0,4},{4,0},{8,12},{12,8},{16,20},{20,16},{24,28},{28,24},{1,5},{5... | collective-permute-start | bytes 294920 | tf_op jit(solution)/shard_map/ppermute | solution.py:20
  48.6 5.5 %collective-permute-start.7 = (bf16[64,768]{1,0:T(8,128)(2,1)S(1)}, bf16[64,768]{1,0:T(8,128)(2,1)S(1)}, u32[]{:S(2)}, u32[]{:S(2)}) collective-permute-start(bf16[64,768]{1,0:T(8,128)(2,1)S(1)} %get-tuple-element.34), channel_id=1, source_target_pairs={{0,8},{4,12},{8,0},{12,4},{16,24},{20,28},{24,16},{28,20},{1,9},{5... | collective-permute-start | bytes 294920 | tf_op jit(solution)/shard_map/ppermute | solution.py:20
  53.2 7.9 %collective-permute-start.26 = (bf16[64,768]{1,0:T(8,128)(2,1)S(1)}, bf16[64,768]{1,0:T(8,128)(2,1)S(1)}, u32[]{:S(2)}, u32[]{:S(2)}) collective-permute-start(bf16[64,768]{1,0:T(8,128)(2,1)S(1)} %get-tuple-element.20), channel_id=1, source_target_pairs={{0,4},{4,0},{8,12},{12,8},{16,20},{20,16},{24,28},{28,24},{1,5},{5... | collective-permute-start | bytes 294920 | tf_op jit(solution)/shard_map/ppermute | solution.py:20
  53.2 8.3 %collective-permute-start.27 = (bf16[64,768]{1,0:T(8,128)(2,1)S(1)}, bf16[64,768]{1,0:T(8,128)(2,1)S(1)}, u32[]{:S(2)}, u32[]{:S(2)}) collective-permute-start(bf16[64,768]{1,0:T(8,128)(2,1)S(1)} %get-tuple-element.20), channel_id=1, source_target_pairs={{0,8},{4,12},{8,0},{12,4},{16,24},{20,28},{24,16},{28,20},{1,9},{5... | collective-permute-start | bytes 294920 | tf_op jit(solution)/shard_map/ppermute | solution.py:20
  55.1 18.5 %collective-permute-start.8 = (bf16[3,256,128]{2,1,0:T(8,128)(2,1)S(1)}, bf16[3,256,128]{2,1,0:T(8,128)(2,1)S(1)}, u32[]{:S(2)}, u32[]{:S(2)}) collective-permute-start(bf16[3,256,128]{2,1,0:T(8,128)(2,1)S(1)} %slice_select_fusion), channel_id=1, source_target_pairs={{0,1},{1,2},{2,3},{3,0},{4,5},{5,6},{6,7},{7,4},{8,9},{9,10},{10,1... | collective-permute-start | bytes 589832 | tf_op jit(solution)/shard_map/ppermute | solution.py:39
  56.8 16.8 %collective-permute-start.9 = (bf16[3,256,128]{2,1,0:T(8,128)(2,1)S(1)}, bf16[3,256,128]{2,1,0:T(8,128)(2,1)S(1)}, u32[]{:S(2)}, u32[]{:S(2)}) collective-permute-start(bf16[3,256,128]{2,1,0:T(8,128)(2,1)S(1)} %slice_select_fusion), channel_id=1, source_target_pairs={{0,2},{1,3},{2,0},{3,1},{4,6},{5,7},{6,4},{7,5},{8,10},{9,11},{10,... | collective-permute-start | bytes 589832 | tf_op jit(solution)/shard_map/ppermute | solution.py:39
  59.4 14.9 %collective-permute-start.10 = (bf16[3,256,128]{2,1,0:T(8,128)(2,1)S(1)}, bf16[3,256,128]{2,1,0:T(8,128)(2,1)S(1)}, u32[]{:S(2)}, u32[]{:S(2)}) collective-permute-start(bf16[3,256,128]{2,1,0:T(8,128)(2,1)S(1)} %slice_select_fusion), channel_id=1, source_target_pairs={{0,3},{1,0},{2,1},{3,2},{4,7},{5,4},{6,5},{7,6},{8,11},{9,8},{10,9... | collective-permute-start | bytes 589832 | tf_op jit(solution)/shard_map/ppermute | solution.py:39
  61.6 5.2 %collective-permute-start.13 = (bf16[64,768]{1,0:T(8,128)(2,1)S(1)}, bf16[64,768]{1,0:T(8,128)(2,1)S(1)}, u32[]{:S(2)}, u32[]{:S(2)}) collective-permute-start(bf16[64,768]{1,0:T(8,128)(2,1)S(1)} %convert_element_type.164), channel_id=1, source_target_pairs={{0,8},{4,12},{8,0},{12,4},{16,24},{20,28},{24,16},{28,20},{1,9},{5... | collective-permute-start | bytes 294920 | tf_op jit(solution)/shard_map/ppermute | solution.py:20
  68.6 7.3 %collective-permute-start.14 = (bf16[64,768]{1,0:T(8,128)(2,1)S(1)}, bf16[64,768]{1,0:T(8,128)(2,1)S(1)}, u32[]{:S(2)}, u32[]{:S(2)}) collective-permute-start(bf16[64,768]{1,0:T(8,128)(2,1)S(1)} %get-tuple-element.36), channel_id=1, source_target_pairs={{0,4},{4,0},{8,12},{12,8},{16,20},{20,16},{24,28},{28,24},{1,5},{5... | collective-permute-start | bytes 294920 | tf_op jit(solution)/shard_map/ppermute | solution.py:20
  73.6 5.4 %collective-permute-start.30 = (bf16[64,768]{1,0:T(8,128)(2,1)S(1)}, bf16[64,768]{1,0:T(8,128)(2,1)S(1)}, u32[]{:S(2)}, u32[]{:S(2)}) collective-permute-start(bf16[64,768]{1,0:T(8,128)(2,1)S(1)} %get-tuple-element.24), channel_id=1, source_target_pairs={{0,4},{4,0},{8,12},{12,8},{16,20},{20,16},{24,28},{28,24},{1,5},{5... | collective-permute-start | bytes 294920 | tf_op jit(solution)/shard_map/ppermute | solution.py:20
  73.6 5.7 %collective-permute-start.31 = (bf16[64,768]{1,0:T(8,128)(2,1)S(1)}, bf16[64,768]{1,0:T(8,128)(2,1)S(1)}, u32[]{:S(2)}, u32[]{:S(2)}) collective-permute-start(bf16[64,768]{1,0:T(8,128)(2,1)S(1)} %get-tuple-element.24), channel_id=1, source_target_pairs={{0,8},{4,12},{8,0},{12,4},{16,24},{20,28},{24,16},{28,20},{1,9},{5... | collective-permute-start | bytes 294920 | tf_op jit(solution)/shard_map/ppermute | solution.py:20
  75.8 48.1 %collective-permute-start.11 = (bf16[4,3,256,128]{3,2,1,0:T(8,128)(2,1)}, bf16[4,3,256,128]{3,2,1,0:T(8,128)(2,1)}, u32[]{:S(2)}, u32[]{:S(2)}) collective-permute-start(bf16[4,3,256,128]{3,2,1,0:T(8,128)(2,1)} %get-tuple-element.14), channel_id=1, source_target_pairs={{0,4},{4,0},{8,12},{12,8},{16,20},{20,16},{24,28},{28,24},{1,5},{5... | collective-permute-start | bytes 2359304 | tf_op jit(solution)/shard_map/ppermute | solution.py:20
  80.0 5.1 %collective-permute-start.32 = (bf16[64,768]{1,0:T(8,128)(2,1)S(1)}, bf16[64,768]{1,0:T(8,128)(2,1)S(1)}, u32[]{:S(2)}, u32[]{:S(2)}) collective-permute-start(bf16[64,768]{1,0:T(8,128)(2,1)S(1)} %get-tuple-element.26), channel_id=1, source_target_pairs={{0,4},{4,0},{8,12},{12,8},{16,20},{20,16},{24,28},{28,24},{1,5},{5... | collective-permute-start | bytes 294920 | tf_op jit(solution)/shard_map/ppermute | solution.py:20
  80.1 5.3 %collective-permute-start.33 = (bf16[64,768]{1,0:T(8,128)(2,1)S(1)}, bf16[64,768]{1,0:T(8,128)(2,1)S(1)}, u32[]{:S(2)}, u32[]{:S(2)}) collective-permute-start(bf16[64,768]{1,0:T(8,128)(2,1)S(1)} %get-tuple-element.26), channel_id=1, source_target_pairs={{0,8},{4,12},{8,0},{12,4},{16,24},{20,28},{24,16},{28,20},{1,9},{5... | collective-permute-start | bytes 294920 | tf_op jit(solution)/shard_map/ppermute | solution.py:20
  83.3 5.2 %collective-permute-start.19 = (bf16[64,768]{1,0:T(8,128)(2,1)S(1)}, bf16[64,768]{1,0:T(8,128)(2,1)S(1)}, u32[]{:S(2)}, u32[]{:S(2)}) collective-permute-start(bf16[64,768]{1,0:T(8,128)(2,1)S(1)} %get-tuple-element.40), channel_id=1, source_target_pairs={{0,8},{4,12},{8,0},{12,4},{16,24},{20,28},{24,16},{28,20},{1,9},{5... | collective-permute-start | bytes 294920 | tf_op jit(solution)/shard_map/ppermute | solution.py:20
  86.1 5.2 %collective-permute-start.34 = (bf16[64,768]{1,0:T(8,128)(2,1)S(1)}, bf16[64,768]{1,0:T(8,128)(2,1)S(1)}, u32[]{:S(2)}, u32[]{:S(2)}) collective-permute-start(bf16[64,768]{1,0:T(8,128)(2,1)S(1)} %get-tuple-element.28), channel_id=1, source_target_pairs={{0,4},{4,0},{8,12},{12,8},{16,20},{20,16},{24,28},{28,24},{1,5},{5... | collective-permute-start | bytes 294920 | tf_op jit(solution)/shard_map/ppermute | solution.py:20
  86.4 5.3 %collective-permute-start.35 = (bf16[64,768]{1,0:T(8,128)(2,1)S(1)}, bf16[64,768]{1,0:T(8,128)(2,1)S(1)}, u32[]{:S(2)}, u32[]{:S(2)}) collective-permute-start(bf16[64,768]{1,0:T(8,128)(2,1)S(1)} %get-tuple-element.28), channel_id=1, source_target_pairs={{0,8},{4,12},{8,0},{12,4},{16,24},{20,28},{24,16},{28,20},{1,9},{5... | collective-permute-start | bytes 294920 | tf_op jit(solution)/shard_map/ppermute | solution.py:20
  89.2 5.5 %collective-permute-start.21 = (bf16[64,768]{1,0:T(8,128)(2,1)S(1)}, bf16[64,768]{1,0:T(8,128)(2,1)S(1)}, u32[]{:S(2)}, u32[]{:S(2)}) collective-permute-start(bf16[64,768]{1,0:T(8,128)(2,1)S(1)} %get-tuple-element.42), channel_id=1, source_target_pairs={{0,8},{4,12},{8,0},{12,4},{16,24},{20,28},{24,16},{28,20},{1,9},{5... | collective-permute-start | bytes 294920 | tf_op jit(solution)/shard_map/ppermute | solution.py:20
  92.3 5.1 %collective-permute-start.36 = (bf16[64,768]{1,0:T(8,128)(2,1)S(1)}, bf16[64,768]{1,0:T(8,128)(2,1)S(1)}, u32[]{:S(2)}, u32[]{:S(2)}) collective-permute-start(bf16[64,768]{1,0:T(8,128)(2,1)S(1)} %get-tuple-element.30), channel_id=1, source_target_pairs={{0,4},{4,0},{8,12},{12,8},{16,20},{20,16},{24,28},{28,24},{1,5},{5... | collective-permute-start | bytes 294920 | tf_op jit(solution)/shard_map/ppermute | solution.py:20
  92.6 5.3 %collective-permute-start.37 = (bf16[64,768]{1,0:T(8,128)(2,1)S(1)}, bf16[64,768]{1,0:T(8,128)(2,1)S(1)}, u32[]{:S(2)}, u32[]{:S(2)}) collective-permute-start(bf16[64,768]{1,0:T(8,128)(2,1)S(1)} %get-tuple-element.30), channel_id=1, source_target_pairs={{0,8},{4,12},{8,0},{12,4},{16,24},{20,28},{24,16},{28,20},{1,9},{5... | collective-permute-start | bytes 294920 | tf_op jit(solution)/shard_map/ppermute | solution.py:20
  95.4 5.4 %collective-permute-start.23 = (bf16[64,768]{1,0:T(8,128)(2,1)S(1)}, bf16[64,768]{1,0:T(8,128)(2,1)S(1)}, u32[]{:S(2)}, u32[]{:S(2)}) collective-permute-start(bf16[64,768]{1,0:T(8,128)(2,1)S(1)} %get-tuple-element.44), channel_id=1, source_target_pairs={{0,8},{4,12},{8,0},{12,4},{16,24},{20,28},{24,16},{28,20},{1,9},{5... | collective-permute-start | bytes 294920 | tf_op jit(solution)/shard_map/ppermute | solution.py:20
  104.1 11.4 %collective-permute-start.40 = (bf16[128,768]{1,0:T(8,128)(2,1)S(1)}, bf16[128,768]{1,0:T(8,128)(2,1)S(1)}, u32[]{:S(2)}, u32[]{:S(2)}) collective-permute-start(bf16[128,768]{1,0:T(8,128)(2,1)S(1)} %pad_maximum_fusion.5), channel_id=1, source_target_pairs={{0,1},{1,2},{2,3},{3,0},{4,5},{5,6},{6,7},{7,4},{8,9},{9,10},{10,1... | collective-permute-start | bytes 589832 | tf_op jit(solution)/shard_map/ppermute | solution.py:29
  107.6 15.4 %collective-permute-start.41 = (bf16[128,768]{1,0:T(8,128)(2,1)S(1)}, bf16[128,768]{1,0:T(8,128)(2,1)S(1)}, u32[]{:S(2)}, u32[]{:S(2)}) collective-permute-start(bf16[128,768]{1,0:T(8,128)(2,1)S(1)} %pad_maximum_fusion.5), channel_id=1, source_target_pairs={{0,2},{1,3},{2,0},{3,1},{4,6},{5,7},{6,4},{7,5},{8,10},{9,11},{10,... | collective-permute-start | bytes 589832 | tf_op jit(solution)/shard_map/ppermute | solution.py:29
  110.2 12.8 %collective-permute-start.42 = (bf16[128,768]{1,0:T(8,128)(2,1)S(1)}, bf16[128,768]{1,0:T(8,128)(2,1)S(1)}, u32[]{:S(2)}, u32[]{:S(2)}) collective-permute-start(bf16[128,768]{1,0:T(8,128)(2,1)S(1)} %pad_maximum_fusion.5), channel_id=1, source_target_pairs={{0,3},{1,0},{2,1},{3,2},{4,7},{5,4},{6,5},{7,6},{8,11},{9,8},{10,9... | collective-permute-start | bytes 589832 | tf_op jit(solution)/shard_map/ppermute | solution.py:29
  (34 other events, 104.1 us)

commit v13 on v12

--- a/solution.py
+++ b/solution.py
@@ -6,7 +6,7 @@
 ROUNDS = 2
 DEGREE = 8
 ROTS = 4
-GATHER_AT = 2
+GATHER_AT = 0
 
 
 filter_center = 0.1
@@ -106,6 +106,8 @@
         return result
 
     def chebyshev(start_rows, hook):
+        if GATHER_AT == 0:
+            start_rows = hook(start_rows)
         previous = start_rows.astype(jnp.float32)
         current = (apply_operator(start_rows) - filter_center * previous) / filter_half
         for degree_index in range(1, DEGREE):

time: 169 us -> 173 us (1.024)
  matrix products: 34.8 us -> 45.9 us
  waiting for transfers between devices: 48.5 us -> 45 us
  local copies, waits for them, and re-layouts: 25.6 us -> 22.2 us
  other arithmetic: 10.8 us -> 12.7 us
  starting transfers between devices: 46.4 us -> 44.5 us
    dot_general x12, matrix products: 3.6 us -> 14.5 us  [body(): lax.dot_general(piece[rotation_index], basis_all, (((0,), (0,)), ((), ())...]
    ppermute x49, waiting for transfers between devices: 35.7 us -> 32.2 us  [swapped(): return lax.ppermute(value, axis, pairs)]
    ppermute x3, starting transfers between devices: 6.07 us -> 3.87 us  [gather_bands(): pieces.append(lax.ppermute(value, 'bands', pairs))]
    gt x2, local copies, waits for them, and re-layouts: 5.21 us -> 3.07 us  [pattern_mask(): return mask > 0.5]
    ppermute x3, waiting for transfers between devices: 12.8 us -> 10.8 us  [gather_bands(): pieces.append(lax.ppermute(value, 'bands', pairs))]
    another operation x2, other arithmetic: 1.26 us -> 3.27 us  [gather_pieces(): return jnp.stack(pieces)]
    ppermute x3, waiting for transfers between devices: 0.01 us -> 2 us  [gather_pieces(): pieces.append(lax.ppermute(value, 'bands', pairs))]
    dot_general x4, matrix products: 8.59 us -> 6.86 us  [pattern_mask(): lax.dot_general(per_row.astype(jnp.bfloat16), col_onehot, (((1,), (1,)),...]
  transfers between devices with their start and end apart: 55 -> 55, of which waited for: 21 -> 28; matrix products, arithmetic and copies ran while one was open for 35% -> 34% of each run, Pallas kernels for 0% -> 0%
where the time goes in v13:
time: 173 us; the launch traced here: 171 us
  matrix products  45.9 us (27%)
  waiting for transfers between devices  45 us (26%)
  starting transfers between devices  44.5 us (26%)
  local copies, waits for them, and re-layouts  22.2 us (13%)
  other arithmetic  12.7 us (7%)
    ppermute x49, starting transfers between devices, swapped(): return lax.ppermute(value, axis, pairs)  33.7 us
    ppermute x49, waiting for transfers between devices, swapped(): return lax.ppermute(value, axis, pairs)  32.2 us
    dot_general x32, matrix products, apply_operator(): jnp.dot(other_rows, other_pair[round_index], preferred_element_type=jnp.f...  15.4 us
    dot_general x12, matrix products, body(): lax.dot_general(piece[rotation_index], basis_all, (((0,), (0,)), ((), ())...  14.5 us
    ppermute x3, waiting for transfers between devices, gather_bands(): pieces.append(lax.ppermute(value, 'bands', pairs))  10.8 us
    dot_general x16, matrix products, apply_operator(): result = jnp.dot(values, diag_sym, preferred_element_type=jnp.float32)  7.74 us
    ppermute x3, starting transfers between devices, gather_pieces(): pieces.append(lax.ppermute(value, 'bands', pairs))  6.96 us
    dot_general x4, matrix products, pattern_mask(): lax.dot_general(per_row.astype(jnp.bfloat16), col_onehot, (((1,), (1,)),...  6.86 us
  transfers between devices with their start and end apart: 55, of which 28 were waited for; matrix products, arithmetic and copies ran while one was open for 34% of the time, Pallas kernels for 0%

profile of v13, /device:TPU:0, one launch (start us, length us, event | category | flops | bytes accessed | tf_op | source)
XLA Modules:
  0.0 171.0 jit_solution(7610965853066405999)
XLA Ops:
  0.0 1.6 fusion.107
  3.4 3.0 %collective-permute-start = (bf16[3,256,128]{2,1,0:T(8,128)(2,1)}, bf16[3,256,128]{2,1,0:T(8,128)(2,1)}, u32[]{:S(2)}, u32[]{:S(2)}) collective-permute-start(bf16[3,256,128]{2,1,0:T(8,128)(2,1)} %slice_select_fusion), channel_id=1, source_target_pairs={{0,1},{1,2},{2,3},{3,0},{4,5},{5,6},{6,7},{7,4},{8,9},{9,10},{10,1... | collective-permute-start | bytes 589832 | tf_op jit(solution)/shard_map/ppermute | solution.py:39
  6.4 2.6 %collective-permute-start.1 = (bf16[3,256,128]{2,1,0:T(8,128)(2,1)}, bf16[3,256,128]{2,1,0:T(8,128)(2,1)}, u32[]{:S(2)}, u32[]{:S(2)}) collective-permute-start(bf16[3,256,128]{2,1,0:T(8,128)(2,1)} %slice_select_fusion), channel_id=1, source_target_pairs={{0,2},{1,3},{2,0},{3,1},{4,6},{5,7},{6,4},{7,5},{8,10},{9,11},{10,... | collective-permute-start | bytes 589832 | tf_op jit(solution)/shard_map/ppermute | solution.py:39
  9.6 2.8 %slice_bitcast_fusion = (bf16[768,768]{1,0:T(8,128)(2,1)}, bf16[1,768,768]{2,1,0:T(8,128)(2,1)S(1)}) fusion(bf16[2,768,768]{2,1,0:T(8,128)(2,1)} %param.8), kind=kLoop, calls=%fused_computation.21 | loop fusion | bytes 4718592 | tf_op jit(solution)/shard_map/squeeze | solution.py:74
  15.9 2.4 %copy.23 = bf16[768,768]{0,1:T(8,128)(2,1)} copy(bf16[768,768]{1,0:T(8,128)(2,1)} %get-tuple-element.12) | data formatting | bytes 2359296 | tf_op jit(solution)/shard_map/squeeze | solution.py:74
  20.7 1.6 copy.20
  22.3 2.0 %add_multiply_fusion = f32[768,768]{1,0:T(8,128)} fusion(bf16[768,768]{1,0:T(8,128)(2,1)S(1)} %copy-done, s32[768]{0:T(1024)S(1)} %get-tuple-element.51), kind=kLoop, calls=%fused_computation.7 | loop fusion | flops 4128768 | bytes 3542016 | tf_op jit(solution)/shard_map/mul | solution.py:81
  24.3 2.0 %copy.16 = f32[768,768]{0,1:T(8,128)S(1)} copy(f32[768,768]{1,0:T(8,128)} %add_multiply_fusion) | data formatting | bytes 4718592 | tf_op jit(solution)/shard_map/mul | solution.py:81
  26.4 2.0 %fusion.2 = bf16[768,768]{1,0:T(8,128)(2,1)S(1)} fusion(f32[768,768]{0,1:T(8,128)S(1)} %copy.16, s32[768]{0:T(1024)S(1)} %get-tuple-element.51, bf16[768,768]{1,0:T(8,128)(2,1)} %param.7), kind=kLoop, calls=%fused_computation.6 | loop fusion | flops 5308416 | bytes 4721664 | tf_op jit(solution)/shard_map/convert_element_type | solution.py:82
  31.6 1.9 %fusion.120 = f32[64,768]{1,0:T(8,128)} fusion(bf16[64,768]{1,0:T(8,128)(2,1)} %get-tuple-element.8, bf16[768,768]{1,0:T(8,128)(2,1)S(1)} %fusion.2), kind=kOutput, calls=%fused_computation.220 | convolution fusion | flops 75497472 | bytes 1474560 | tf_op jit(solution)/shard_map/dot_general | solution.py:100
  34.9 2.8 %fusion.3 = f32[768,768]{1,0:T(8,128)} fusion(s32[768]{0:T(1024)S(1)} %get-tuple-element.51, s32[768]{0:T(1024)S(1)} %convert_reduce_fusion.1, s32[4,4]{1,0:T(4,128)} %collective-permute-done.5), kind=kOutput, calls=%fused_computation.26 | convolution fusion | flops 4752400 | bytes 2365504 | tf_op jit(solution)/shard_map/dot_general | solution.py:63
  38.3 2.0 %collective-permute-done.2 = bf16[3,256,128]{2,1,0:T(8,128)(2,1)S(1)} collective-permute-done((bf16[3,256,128]{2,1,0:T(8,128)(2,1)}, bf16[3,256,128]{2,1,0:T(8,128)(2,1)S(1)}, u32[]{:S(2)}, u32[]{:S(2)}) %collective-permute-start.2) | collective-permute-done | bytes 196640 | tf_op jit(solution)/shard_map/ppermute | solution.py:39
  42.2 2.5 %pad_maximum_fusion.3 = (bf16[4,3,256,128]{3,2,1,0:T(8,128)(2,1)}, bf16[4,3,512,128]{3,2,1,0:T(8,128)(2,1)}) fusion(bf16[1,3,256,128]{3,2,1,0:T(8,128)(2,1)S(1)} %bitcast.207, bf16[1,3,256,128]{3,2,1,0:T(8,128)(2,1)} %bitcast.2, bf16[1,3,256,128]{3,2,1,0:T(8,128)(2,1)} %bitcast.1, bf16[1,3,256,128]{3,2,1,0:T(8,128)(2,1)S(1)} %copy-done.3, ...), kind=kLoop, calls=%fused_computation.106 | loop fusion | flops 3145728 | bytes 2359300 | tf_op jit(solution)/shard_map/stack | solution.py:40
  44.8 1.7 %copy.18 = bf16[768,768]{1,0:T(8,128)(2,1)S(1)} copy(bf16[768,768]{0,1:T(8,128)(2,1)} %collective-permute-done.6) | data formatting | bytes 2359296 | tf_op jit(solution)/shard_map/ppermute | solution.py:20
  46.5 2.8 %fusion.1 = bf16[768,768]{1,0:T(8,128)(2,1)S(1)} fusion(bf16[768,768]{1,0:T(8,128)(2,1)S(1)} %copy.18, f32[768,768]{1,0:T(8,128)} %fusion.3, pred[768,768]{0,1:T(8,128)(4,1)} %copy.20, bf16[1,768,768]{1,2,0:T(8,128)(2,1)} %copy.25), kind=kLoop, calls=%fused_computation.4 | loop fusion | flops 4128768 | bytes 6488064 | tf_op jit(solution)/shard_map/convert_element_type | solution.py:96
  51.1 2.7 %fusion = bf16[768,768]{1,0:T(8,128)(2,1)S(1)} fusion(bf16[768,768]{1,0:T(8,128)(2,1)} %collective-permute-done.9, pred[768,768]{0,1:T(32,128)(4,1)} %copy.22, bf16[768,768]{0,1:T(8,128)(2,1)} %copy.23, s32[768]{0:T(1024)S(1)} %get-tuple-element.50, s32[768]{0:T(1024)S(1)} %get-tuple-element.51, s32[4,4]{1,0:T(4,128)S(1)} %collective-permute-done.8), kind=kOutput, calls=%fused_computation.2 | convolution fusion | flops 8881168 | bytes 4134976 | tf_op jit(solution)/shard_map/dot_general | solution.py:63
  99.8 1.9 %collective-permute-done.39 = bf16[64,768]{1,0:T(8,128)(2,1)S(1)} collective-permute-done((bf16[64,768]{1,0:T(8,128)(2,1)S(1)}, bf16[64,768]{1,0:T(8,128)(2,1)S(1)}, u32[]{:S(2)}, u32[]{:S(2)}) %collective-permute-start.39) | collective-permute-done | bytes 98336 | tf_op jit(solution)/shard_map/ppermute | solution.py:20
  102.1 3.7 %collective-permute-start.41 = (bf16[128,768]{1,0:T(8,128)(2,1)S(1)}, bf16[128,768]{1,0:T(8,128)(2,1)S(1)}, u32[]{:S(2)}, u32[]{:S(2)}) collective-permute-start(bf16[128,768]{1,0:T(8,128)(2,1)S(1)} %pad_maximum_fusion.5), channel_id=1, source_target_pairs={{0,2},{1,3},{2,0},{3,1},{4,6},{5,7},{6,4},{7,5},{8,10},{9,11},{10,... | collective-permute-start | bytes 589832 | tf_op jit(solution)/shard_map/ppermute | solution.py:29
  106.0 2.2 %constant_dynamic-update-slice_fusion = bf16[4,3,512,128]{3,2,1,0:T(8,128)(2,1)} fusion(bf16[4,3,512,128]{3,2,1,0:T(8,128)(2,1)} %get-tuple-element.15, bf16[4,3,256,128]{3,2,1,0:T(8,128)(2,1)} %collective-permute-done.3, s32[]{:T(128)S(6)} %select_n.162), kind=kLoop, calls=%fused_computation.176 | loop fusion | bytes 1572868 | tf_op jit(solution)/shard_map/dynamic_update_slice | solution.py:133
  108.1 3.7 %collective-permute-done.40 = bf16[128,768]{1,0:T(8,128)(2,1)S(1)} collective-permute-done((bf16[128,768]{1,0:T(8,128)(2,1)S(1)}, bf16[128,768]{1,0:T(8,128)(2,1)S(1)}, u32[]{:S(2)}, u32[]{:S(2)}) %collective-permute-start.40) | collective-permute-done | bytes 196640 | tf_op jit(solution)/shard_map/ppermute | solution.py:29
  111.8 7.1 %collective-permute-done.41 = bf16[128,768]{1,0:T(8,128)(2,1)S(1)} collective-permute-done((bf16[128,768]{1,0:T(8,128)(2,1)S(1)}, bf16[128,768]{1,0:T(8,128)(2,1)S(1)}, u32[]{:S(2)}, u32[]{:S(2)}) %collective-permute-start.41) | collective-permute-done | bytes 196640 | tf_op jit(solution)/shard_map/ppermute | solution.py:29
  127.5 2.1 %collective-permute-done.44 = f32[512]{0:T(512)S(1)} collective-permute-done((f32[512]{0:T(512)S(1)}, f32[512]{0:T(512)S(1)}, u32[]{:S(2)}, u32[]{:S(2)}) %collective-permute-start.44) | collective-permute-done | bytes 2080 | tf_op jit(solution)/shard_map/ppermute | solution.py:20
  129.5 1.6 collective-permute-start.45
  131.1 2.0 %collective-permute-done.45 = f32[512]{0:T(512)S(1)} collective-permute-done((f32[512]{0:T(512)S(1)}, f32[512]{0:T(512)S(1)}, u32[]{:S(2)}, u32[]{:S(2)}) %collective-permute-start.45) | collective-permute-done | bytes 2080 | tf_op jit(solution)/shard_map/ppermute | solution.py:20
  141.1 2.1 %collective-permute-done.47 = f32[512]{0:T(512)S(1)} collective-permute-done((f32[512]{0:T(512)S(1)}, f32[512]{0:T(512)S(1)}, u32[]{:S(2)}, u32[]{:S(2)}) %collective-permute-start.47) | collective-permute-done | bytes 2080 | tf_op jit(solution)/shard_map/ppermute | solution.py:20
  143.1 1.6 collective-permute-start.48
  144.7 2.0 %collective-permute-done.48 = f32[512]{0:T(512)S(1)} collective-permute-done((f32[512]{0:T(512)S(1)}, f32[512]{0:T(512)S(1)}, u32[]{:S(2)}, u32[]{:S(2)}) %collective-permute-start.48) | collective-permute-done | bytes 2080 | tf_op jit(solution)/shard_map/ppermute | solution.py:20
  154.7 2.1 %collective-permute-done.50 = f32[512]{0:T(512)S(1)} collective-permute-done((f32[512]{0:T(512)S(1)}, f32[512]{0:T(512)S(1)}, u32[]{:S(2)}, u32[]{:S(2)}) %collective-permute-start.50) | collective-permute-done | bytes 2080 | tf_op jit(solution)/shard_map/ppermute | solution.py:20
  156.7 1.6 collective-permute-start.51
  158.3 2.0 %collective-permute-done.51 = f32[512]{0:T(512)S(1)} collective-permute-done((f32[512]{0:T(512)S(1)}, f32[512]{0:T(512)S(1)}, u32[]{:S(2)}, u32[]{:S(2)}) %collective-permute-start.51) | collective-permute-done | bytes 2080 | tf_op jit(solution)/shard_map/ppermute | solution.py:20
  164.5 2.0 %collective-permute-done.53 = f32[128]{0:T(128)S(1)} collective-permute-done((f32[128]{0:T(128)S(1)}, f32[128]{0:T(128)S(1)}, u32[]{:S(2)}, u32[]{:S(2)}) %collective-permute-start.53) | collective-permute-done | bytes 544 | tf_op jit(solution)/shard_map/ppermute | solution.py:20
  168.1 2.0 %collective-permute-done.54 = f32[128]{0:T(128)S(1)} collective-permute-done((f32[128]{0:T(128)S(1)}, f32[128]{0:T(128)S(1)}, u32[]{:S(2)}, u32[]{:S(2)}) %collective-permute-start.54) | collective-permute-done | bytes 544 | tf_op jit(solution)/shard_map/ppermute | solution.py:20
  (207 shorter events, 94.3 us)
Async XLA Ops:
  3.4 34.3 %collective-permute-start = (bf16[3,256,128]{2,1,0:T(8,128)(2,1)}, bf16[3,256,128]{2,1,0:T(8,128)(2,1)}, u32[]{:S(2)}, u32[]{:S(2)}) collective-permute-start(bf16[3,256,128]{2,1,0:T(8,128)(2,1)} %slice_select_fusion), channel_id=1, source_target_pairs={{0,1},{1,2},{2,3},{3,0},{4,5},{5,6},{6,7},{7,4},{8,9},{9,10},{10,1... | collective-permute-start | bytes 589832 | tf_op jit(solution)/shard_map/ppermute | solution.py:39
  6.4 31.2 %collective-permute-start.1 = (bf16[3,256,128]{2,1,0:T(8,128)(2,1)}, bf16[3,256,128]{2,1,0:T(8,128)(2,1)}, u32[]{:S(2)}, u32[]{:S(2)}) collective-permute-start(bf16[3,256,128]{2,1,0:T(8,128)(2,1)} %slice_select_fusion), channel_id=1, source_target_pairs={{0,2},{1,3},{2,0},{3,1},{4,6},{5,7},{6,4},{7,5},{8,10},{9,11},{10,... | collective-permute-start | bytes 589832 | tf_op jit(solution)/shard_map/ppermute | solution.py:39
  9.6 23.9 %collective-permute-start.5 = (s32[4,4]{1,0:T(4,128)}, s32[4,4]{1,0:T(4,128)}, u32[]{:S(2)}, u32[]{:S(2)}) collective-permute-start(s32[4,4]{1,0:T(4,128)} %get-tuple-element.19), channel_id=1, source_target_pairs={{0,4},{4,0},{8,12},{12,8},{16,20},{20,16},{24,28},{28,24},{1,5},{5... | collective-permute-start | bytes 200 | tf_op jit(solution)/shard_map/ppermute | solution.py:20
  13.9 30.8 %collective-permute-start.6 = (bf16[768,768]{0,1:T(8,128)(2,1)}, bf16[768,768]{0,1:T(8,128)(2,1)}, u32[]{:S(2)}, u32[]{:S(2)}) collective-permute-start(bf16[768,768]{0,1:T(8,128)(2,1)} %bitcast.11), channel_id=1, source_target_pairs={{0,4},{4,0},{8,12},{12,8},{16,20},{20,16},{24,28},{28,24},{1,5},{5... | collective-permute-start | bytes 3538952 | tf_op jit(solution)/shard_map/ppermute | solution.py:20
  14.4 36.5 %collective-permute-start.9 = (bf16[768,768]{1,0:T(8,128)(2,1)}, bf16[768,768]{1,0:T(8,128)(2,1)}, u32[]{:S(2)}, u32[]{:S(2)}) collective-permute-start(bf16[768,768]{1,0:T(8,128)(2,1)} %get-tuple-element.12), channel_id=1, source_target_pairs={{0,8},{4,12},{8,0},{12,4},{16,24},{20,28},{24,16},{28,20},{1,9},{5... | collective-permute-start | bytes 3538952 | tf_op jit(solution)/shard_map/ppermute | solution.py:20
  33.5 6.7 %collective-permute-start.2 = (bf16[3,256,128]{2,1,0:T(8,128)(2,1)}, bf16[3,256,128]{2,1,0:T(8,128)(2,1)S(1)}, u32[]{:S(2)}, u32[]{:S(2)}) collective-permute-start(bf16[3,256,128]{2,1,0:T(8,128)(2,1)} %slice_select_fusion), channel_id=1, source_target_pairs={{0,3},{1,0},{2,1},{3,2},{4,7},{5,4},{6,5},{7,6},{8,11},{9,8},{10,9... | collective-permute-start | bytes 589832 | tf_op jit(solution)/shard_map/ppermute | solution.py:39
  37.6 16.2 %collective-permute-start.4 = (bf16[64,768]{1,0:T(8,128)(2,1)}, bf16[64,768]{1,0:T(8,128)(2,1)}, u32[]{:S(2)}, u32[]{:S(2)}) collective-permute-start(bf16[64,768]{1,0:T(8,128)(2,1)} %get-tuple-element.8), channel_id=1, source_target_pairs={{0,4},{4,0},{8,12},{12,8},{16,20},{20,16},{24,28},{28,24},{1,5},{5... | collective-permute-start | bytes 294920 | tf_op jit(solution)/shard_map/ppermute | solution.py:20
  37.7 17.6 %collective-permute-start.7 = (bf16[64,768]{1,0:T(8,128)(2,1)}, bf16[64,768]{1,0:T(8,128)(2,1)}, u32[]{:S(2)}, u32[]{:S(2)}) collective-permute-start(bf16[64,768]{1,0:T(8,128)(2,1)} %get-tuple-element.8), channel_id=1, source_target_pairs={{0,8},{4,12},{8,0},{12,4},{16,24},{20,28},{24,16},{28,20},{1,9},{5... | collective-permute-start | bytes 294920 | tf_op jit(solution)/shard_map/ppermute | solution.py:20
  40.3 9.1 %collective-permute-start.8 = (s32[4,4]{1,0:T(4,128)}, s32[4,4]{1,0:T(4,128)S(1)}, u32[]{:S(2)}, u32[]{:S(2)}) collective-permute-start(s32[4,4]{1,0:T(4,128)} %get-tuple-element.18), channel_id=1, source_target_pairs={{0,8},{4,12},{8,0},{12,4},{16,24},{20,28},{24,16},{28,20},{1,9},{5... | collective-permute-start | bytes 200 | tf_op jit(solution)/shard_map/ppermute | solution.py:20
  44.8 13.0 %collective-permute-start.24 = (bf16[64,768]{1,0:T(8,128)(2,1)}, bf16[64,768]{1,0:T(8,128)(2,1)}, u32[]{:S(2)}, u32[]{:S(2)}) collective-permute-start(bf16[64,768]{1,0:T(8,128)(2,1)} %get-tuple-element.17), channel_id=1, source_target_pairs={{0,4},{4,0},{8,12},{12,8},{16,20},{20,16},{24,28},{28,24},{1,5},{5... | collective-permute-start | bytes 294920 | tf_op jit(solution)/shard_map/ppermute | solution.py:20
  49.4 9.6 %collective-permute-start.25 = (bf16[64,768]{1,0:T(8,128)(2,1)}, bf16[64,768]{1,0:T(8,128)(2,1)}, u32[]{:S(2)}, u32[]{:S(2)}) collective-permute-start(bf16[64,768]{1,0:T(8,128)(2,1)} %get-tuple-element.17), channel_id=1, source_target_pairs={{0,8},{4,12},{8,0},{12,4},{16,24},{20,28},{24,16},{28,20},{1,9},{5... | collective-permute-start | bytes 294920 | tf_op jit(solution)/shard_map/ppermute | solution.py:20
  50.9 55.0 %collective-permute-start.3 = (bf16[4,3,256,128]{3,2,1,0:T(8,128)(2,1)}, bf16[4,3,256,128]{3,2,1,0:T(8,128)(2,1)}, u32[]{:S(2)}, u32[]{:S(2)}) collective-permute-start(bf16[4,3,256,128]{3,2,1,0:T(8,128)(2,1)} %get-tuple-element.14), channel_id=1, source_target_pairs={{0,4},{4,0},{8,12},{12,8},{16,20},{20,16},{24,28},{28,24},{1,5},{5... | collective-permute-start | bytes 2359304 | tf_op jit(solution)/shard_map/ppermute | solution.py:20
  56.9 5.3 %collective-permute-start.10 = (bf16[64,768]{1,0:T(8,128)(2,1)S(1)}, bf16[64,768]{1,0:T(8,128)(2,1)S(1)}, u32[]{:S(2)}, u32[]{:S(2)}) collective-permute-start(bf16[64,768]{1,0:T(8,128)(2,1)S(1)} %get-tuple-element.34), channel_id=1, source_target_pairs={{0,4},{4,0},{8,12},{12,8},{16,20},{20,16},{24,28},{28,24},{1,5},{5... | collective-permute-start | bytes 294920 | tf_op jit(solution)/shard_map/ppermute | solution.py:20
  57.2 5.3 %collective-permute-start.11 = (bf16[64,768]{1,0:T(8,128)(2,1)S(1)}, bf16[64,768]{1,0:T(8,128)(2,1)S(1)}, u32[]{:S(2)}, u32[]{:S(2)}) collective-permute-start(bf16[64,768]{1,0:T(8,128)(2,1)S(1)} %get-tuple-element.34), channel_id=1, source_target_pairs={{0,8},{4,12},{8,0},{12,4},{16,24},{20,28},{24,16},{28,20},{1,9},{5... | collective-permute-start | bytes 294920 | tf_op jit(solution)/shard_map/ppermute | solution.py:20
  60.6 4.3 %collective-permute-start.26 = (bf16[64,768]{1,0:T(8,128)(2,1)S(1)}, bf16[64,768]{1,0:T(8,128)(2,1)S(1)}, u32[]{:S(2)}, u32[]{:S(2)}) collective-permute-start(bf16[64,768]{1,0:T(8,128)(2,1)S(1)} %get-tuple-element.20), channel_id=1, source_target_pairs={{0,4},{4,0},{8,12},{12,8},{16,20},{20,16},{24,28},{28,24},{1,5},{5... | collective-permute-start | bytes 294920 | tf_op jit(solution)/shard_map/ppermute | solution.py:20
  60.6 5.2 %collective-permute-start.27 = (bf16[64,768]{1,0:T(8,128)(2,1)S(1)}, bf16[64,768]{1,0:T(8,128)(2,1)S(1)}, u32[]{:S(2)}, u32[]{:S(2)}) collective-permute-start(bf16[64,768]{1,0:T(8,128)(2,1)S(1)} %get-tuple-element.20), channel_id=1, source_target_pairs={{0,8},{4,12},{8,0},{12,4},{16,24},{20,28},{24,16},{28,20},{1,9},{5... | collective-permute-start | bytes 294920 | tf_op jit(solution)/shard_map/ppermute | solution.py:20
  64.3 5.0 %collective-permute-start.13 = (bf16[64,768]{1,0:T(8,128)(2,1)S(1)}, bf16[64,768]{1,0:T(8,128)(2,1)S(1)}, u32[]{:S(2)}, u32[]{:S(2)}) collective-permute-start(bf16[64,768]{1,0:T(8,128)(2,1)S(1)} %get-tuple-element.36), channel_id=1, source_target_pairs={{0,8},{4,12},{8,0},{12,4},{16,24},{20,28},{24,16},{28,20},{1,9},{5... | collective-permute-start | bytes 294920 | tf_op jit(solution)/shard_map/ppermute | solution.py:20
  66.6 5.2 %collective-permute-start.29 = (bf16[64,768]{1,0:T(8,128)(2,1)S(1)}, bf16[64,768]{1,0:T(8,128)(2,1)S(1)}, u32[]{:S(2)}, u32[]{:S(2)}) collective-permute-start(bf16[64,768]{1,0:T(8,128)(2,1)S(1)} %get-tuple-element.22), channel_id=1, source_target_pairs={{0,8},{4,12},{8,0},{12,4},{16,24},{20,28},{24,16},{28,20},{1,9},{5... | collective-permute-start | bytes 294920 | tf_op jit(solution)/shard_map/ppermute | solution.py:20
  70.1 5.2 %collective-permute-start.15 = (bf16[64,768]{1,0:T(8,128)(2,1)S(1)}, bf16[64,768]{1,0:T(8,128)(2,1)S(1)}, u32[]{:S(2)}, u32[]{:S(2)}) collective-permute-start(bf16[64,768]{1,0:T(8,128)(2,1)S(1)} %get-tuple-element.38), channel_id=1, source_target_pairs={{0,8},{4,12},{8,0},{12,4},{16,24},{20,28},{24,16},{28,20},{1,9},{5... | collective-permute-start | bytes 294920 | tf_op jit(solution)/shard_map/ppermute | solution.py:20
  72.5 5.2 %collective-permute-start.31 = (bf16[64,768]{1,0:T(8,128)(2,1)S(1)}, bf16[64,768]{1,0:T(8,128)(2,1)S(1)}, u32[]{:S(2)}, u32[]{:S(2)}) collective-permute-start(bf16[64,768]{1,0:T(8,128)(2,1)S(1)} %get-tuple-element.24), channel_id=1, source_target_pairs={{0,8},{4,12},{8,0},{12,4},{16,24},{20,28},{24,16},{28,20},{1,9},{5... | collective-permute-start | bytes 294920 | tf_op jit(solution)/shard_map/ppermute | solution.py:20
  76.0 5.2 %collective-permute-start.17 = (bf16[64,768]{1,0:T(8,128)(2,1)S(1)}, bf16[64,768]{1,0:T(8,128)(2,1)S(1)}, u32[]{:S(2)}, u32[]{:S(2)}) collective-permute-start(bf16[64,768]{1,0:T(8,128)(2,1)S(1)} %get-tuple-element.40), channel_id=1, source_target_pairs={{0,8},{4,12},{8,0},{12,4},{16,24},{20,28},{24,16},{28,20},{1,9},{5... | collective-permute-start | bytes 294920 | tf_op jit(solution)/shard_map/ppermute | solution.py:20
  78.5 5.2 %collective-permute-start.33 = (bf16[64,768]{1,0:T(8,128)(2,1)S(1)}, bf16[64,768]{1,0:T(8,128)(2,1)S(1)}, u32[]{:S(2)}, u32[]{:S(2)}) collective-permute-start(bf16[64,768]{1,0:T(8,128)(2,1)S(1)} %get-tuple-element.26), channel_id=1, source_target_pairs={{0,8},{4,12},{8,0},{12,4},{16,24},{20,28},{24,16},{28,20},{1,9},{5... | collective-permute-start | bytes 294920 | tf_op jit(solution)/shard_map/ppermute | solution.py:20
  82.0 5.2 %collective-permute-start.19 = (bf16[64,768]{1,0:T(8,128)(2,1)S(1)}, bf16[64,768]{1,0:T(8,128)(2,1)S(1)}, u32[]{:S(2)}, u32[]{:S(2)}) collective-permute-start(bf16[64,768]{1,0:T(8,128)(2,1)S(1)} %get-tuple-element.42), channel_id=1, source_target_pairs={{0,8},{4,12},{8,0},{12,4},{16,24},{20,28},{24,16},{28,20},{1,9},{5... | collective-permute-start | bytes 294920 | tf_op jit(solution)/shard_map/ppermute | solution.py:20
  84.4 5.2 %collective-permute-start.35 = (bf16[64,768]{1,0:T(8,128)(2,1)S(1)}, bf16[64,768]{1,0:T(8,128)(2,1)S(1)}, u32[]{:S(2)}, u32[]{:S(2)}) collective-permute-start(bf16[64,768]{1,0:T(8,128)(2,1)S(1)} %get-tuple-element.28), channel_id=1, source_target_pairs={{0,8},{4,12},{8,0},{12,4},{16,24},{20,28},{24,16},{28,20},{1,9},{5... | collective-permute-start | bytes 294920 | tf_op jit(solution)/shard_map/ppermute | solution.py:20
  87.9 5.2 %collective-permute-start.21 = (bf16[64,768]{1,0:T(8,128)(2,1)S(1)}, bf16[64,768]{1,0:T(8,128)(2,1)S(1)}, u32[]{:S(2)}, u32[]{:S(2)}) collective-permute-start(bf16[64,768]{1,0:T(8,128)(2,1)S(1)} %get-tuple-element.44), channel_id=1, source_target_pairs={{0,8},{4,12},{8,0},{12,4},{16,24},{20,28},{24,16},{28,20},{1,9},{5... | collective-permute-start | bytes 294920 | tf_op jit(solution)/shard_map/ppermute | solution.py:20
  90.4 5.2 %collective-permute-start.37 = (bf16[64,768]{1,0:T(8,128)(2,1)S(1)}, bf16[64,768]{1,0:T(8,128)(2,1)S(1)}, u32[]{:S(2)}, u32[]{:S(2)}) collective-permute-start(bf16[64,768]{1,0:T(8,128)(2,1)S(1)} %get-tuple-element.30), channel_id=1, source_target_pairs={{0,8},{4,12},{8,0},{12,4},{16,24},{20,28},{24,16},{28,20},{1,9},{5... | collective-permute-start | bytes 294920 | tf_op jit(solution)/shard_map/ppermute | solution.py:20
  93.8 4.2 %collective-permute-start.22 = (bf16[64,768]{1,0:T(8,128)(2,1)S(1)}, bf16[64,768]{1,0:T(8,128)(2,1)S(1)}, u32[]{:S(2)}, u32[]{:S(2)}) collective-permute-start(bf16[64,768]{1,0:T(8,128)(2,1)S(1)} %get-tuple-element.46), channel_id=1, source_target_pairs={{0,4},{4,0},{8,12},{12,8},{16,20},{20,16},{24,28},{28,24},{1,5},{5... | collective-permute-start | bytes 294920 | tf_op jit(solution)/shard_map/ppermute | solution.py:20
  93.9 5.2 %collective-permute-start.23 = (bf16[64,768]{1,0:T(8,128)(2,1)S(1)}, bf16[64,768]{1,0:T(8,128)(2,1)S(1)}, u32[]{:S(2)}, u32[]{:S(2)}) collective-permute-start(bf16[64,768]{1,0:T(8,128)(2,1)S(1)} %get-tuple-element.46), channel_id=1, source_target_pairs={{0,8},{4,12},{8,0},{12,4},{16,24},{20,28},{24,16},{28,20},{1,9},{5... | collective-permute-start | bytes 294920 | tf_op jit(solution)/shard_map/ppermute | solution.py:20
  96.5 5.2 %collective-permute-start.39 = (bf16[64,768]{1,0:T(8,128)(2,1)S(1)}, bf16[64,768]{1,0:T(8,128)(2,1)S(1)}, u32[]{:S(2)}, u32[]{:S(2)}) collective-permute-start(bf16[64,768]{1,0:T(8,128)(2,1)S(1)} %get-tuple-element.32), channel_id=1, source_target_pairs={{0,8},{4,12},{8,0},{12,4},{16,24},{20,28},{24,16},{28,20},{1,9},{5... | collective-permute-start | bytes 294920 | tf_op jit(solution)/shard_map/ppermute | solution.py:20
  102.1 9.7 %collective-permute-start.40 = (bf16[128,768]{1,0:T(8,128)(2,1)S(1)}, bf16[128,768]{1,0:T(8,128)(2,1)S(1)}, u32[]{:S(2)}, u32[]{:S(2)}) collective-permute-start(bf16[128,768]{1,0:T(8,128)(2,1)S(1)} %pad_maximum_fusion.5), channel_id=1, source_target_pairs={{0,1},{1,2},{2,3},{3,0},{4,5},{5,6},{6,7},{7,4},{8,9},{9,10},{10,1... | collective-permute-start | bytes 589832 | tf_op jit(solution)/shard_map/ppermute | solution.py:29
  102.1 16.8 %collective-permute-start.41 = (bf16[128,768]{1,0:T(8,128)(2,1)S(1)}, bf16[128,768]{1,0:T(8,128)(2,1)S(1)}, u32[]{:S(2)}, u32[]{:S(2)}) collective-permute-start(bf16[128,768]{1,0:T(8,128)(2,1)S(1)} %pad_maximum_fusion.5), channel_id=1, source_target_pairs={{0,2},{1,3},{2,0},{3,1},{4,6},{5,7},{6,4},{7,5},{8,10},{9,11},{10,... | collective-permute-start | bytes 589832 | tf_op jit(solution)/shard_map/ppermute | solution.py:29
  105.8 13.1 %collective-permute-start.42 = (bf16[128,768]{1,0:T(8,128)(2,1)S(1)}, bf16[128,768]{1,0:T(8,128)(2,1)S(1)}, u32[]{:S(2)}, u32[]{:S(2)}) collective-permute-start(bf16[128,768]{1,0:T(8,128)(2,1)S(1)} %pad_maximum_fusion.5), channel_id=1, source_target_pairs={{0,3},{1,0},{2,1},{3,2},{4,7},{5,4},{6,5},{7,6},{8,11},{9,8},{10,9... | collective-permute-start | bytes 589832 | tf_op jit(solution)/shard_map/ppermute | solution.py:29
  (30 other events, 100.8 us)

commit v14 on v10

--- a/solution.py
+++ b/solution.py
@@ -121,8 +121,19 @@
     gathered = []
 
     def start_rotation_gather(current):
-        held, current = lax.optimization_barrier((rotations[: ROTS - 1], current))
-        gathered.append(gather_pieces(held))
+        held, current = lax.optimization_barrier((rotations, current))
+        half_rows = held.shape[1] // 2
+        first_of_pair = (atoms_here % 2) == 0
+        mine = jnp.where(
+            first_of_pair, held[: ROTS - 1, :half_rows], held[: ROTS - 1, half_rows:]
+        )
+        mine = gather_pieces(mine)
+        theirs = swapped(mine, "atoms", 0)
+        mine_start = (atoms_here % 2) * half_rows
+        whole = jnp.zeros(mine.shape[:2] + (2 * half_rows,) + mine.shape[3:], mine.dtype)
+        whole = lax.dynamic_update_slice_in_dim(whole, mine, mine_start, axis=2)
+        whole = lax.dynamic_update_slice_in_dim(whole, theirs, half_rows - mine_start, axis=2)
+        gathered.append(whole)
         return current
 
     half_bands = subspace.shape[0] // 2

time: 170 us -> 166 us (0.976)
  waiting for transfers between devices: 61.7 us -> 52.4 us
  local copies, waits for them, and re-layouts: 14.7 us -> 17.7 us
  starting transfers between devices: 43.7 us -> 46.1 us
    ppermute x48 -> x49, waiting for transfers between devices: 52.5 us -> 39.6 us  [swapped(): return lax.ppermute(value, axis, pairs)]
    ppermute x3, waiting for transfers between devices: 9.14 us -> 12.8 us  [gather_bands(): pieces.append(lax.ppermute(value, 'bands', pairs))]
    unnamed x29 -> x27, local copies, waits for them, and re-layouts: 1.74 us -> 3.98 us
    ppermute x3, starting transfers between devices: 3.88 us -> 5.97 us  [gather_bands(): pieces.append(lax.ppermute(value, 'bands', pairs))]
    ppermute x48 -> x49, starting transfers between devices: 34.1 us -> 34.4 us  [swapped(): return lax.ppermute(value, axis, pairs)]
  transfers between devices with their start and end apart: 54 -> 55, of which waited for: 29 -> 22; matrix products, arithmetic and copies ran while one was open for 31% -> 32% of each run, Pallas kernels for 0% -> 0%
where the time goes in v14:
time: 166 us; the launch traced here: 164 us
  waiting for transfers between devices  52.4 us (32%)
  starting transfers between devices  46.1 us (28%)
  matrix products  36.1 us (22%)
  local copies, waits for them, and re-layouts  17.7 us (11%)
  other arithmetic  10.6 us (6%)
    ppermute x49, waiting for transfers between devices, swapped(): return lax.ppermute(value, axis, pairs)  39.6 us
    ppermute x49, starting transfers between devices, swapped(): return lax.ppermute(value, axis, pairs)  34.4 us
    dot_general x32, matrix products, apply_operator(): jnp.dot(other_rows, other_pair[round_index], preferred_element_type=jnp.f...  14.5 us
    ppermute x3, waiting for transfers between devices, gather_bands(): pieces.append(lax.ppermute(value, 'bands', pairs))  12.8 us
    dot_general x4, matrix products, pattern_mask(): lax.dot_general(per_row.astype(jnp.bfloat16), col_onehot, (((1,), (1,)),...  9.92 us
    dot_general x16, matrix products, apply_operator(): result = jnp.dot(values, diag_sym, preferred_element_type=jnp.float32)  6.63 us
    ppermute x3, starting transfers between devices, gather_bands(): pieces.append(lax.ppermute(value, 'bands', pairs))  5.97 us
    ppermute x3, starting transfers between devices, gather_pieces(): pieces.append(lax.ppermute(value, 'bands', pairs))  5.74 us
  transfers between devices with their start and end apart: 55, of which 22 were waited for; matrix products, arithmetic and copies ran while one was open for 32% of the time, Pallas kernels for 0%

profile of v14, /device:TPU:0, one launch (start us, length us, event | category | flops | bytes accessed | tf_op | source)
XLA Modules:
  0.0 163.6 jit_solution(16879960404704510652)
XLA Ops:
  2.1 2.5 %collective-permute-start.5 = (bf16[64,768]{1,0:T(8,128)(2,1)}, bf16[64,768]{1,0:T(8,128)(2,1)}, u32[]{:S(2)}, u32[]{:S(2)}) collective-permute-start(bf16[64,768]{1,0:T(8,128)(2,1)} %get-tuple-element.17), channel_id=1, source_target_pairs={{0,8},{4,12},{8,0},{12,4},{16,24},{20,28},{24,16},{28,20},{1,9},{5... | collective-permute-start | bytes 294920 | tf_op jit(solution)/shard_map/ppermute | solution.py:20
  6.1 3.3 %slice_bitcast_fusion.1 = (bf16[768,768]{1,0:T(8,128)(2,1)}, bf16[768,768]{0,1:T(8,128)(2,1)}, bf16[1,768,768]{2,1,0:T(8,128)(2,1)S(1)}) fusion(bf16[2,768,768]{2,1,0:T(8,128)(2,1)} %param.8), kind=kLoop, calls=%fused_computation.109 | loop fusion | bytes 5898240 | tf_op jit(solution)/shard_map/squeeze | solution.py:74
  14.1 2.0 %copy.12 = f32[768,768]{1,0:T(8,128)S(1)} copy(f32[768,768]{0,1:T(8,128)} %convert_bitcast_fusion) | data formatting | bytes 4718592 | tf_op jit(solution)/shard_map/convert_element_type | solution.py:85
  16.3 2.3 %fusion.1 = bf16[768,768]{1,0:T(8,128)(2,1)S(1)} fusion(bf16[768,768]{1,0:T(8,128)(2,1)} %param.7, f32[768,768]{1,0:T(8,128)S(1)} %copy.12, s32[768]{0:T(1024)S(1)} %get-tuple-element.50), kind=kLoop, calls=%fused_computation.6 | loop fusion | flops 7667712 | bytes 4721664 | tf_op jit(solution)/shard_map/convert_element_type | solution.py:86
  21.1 3.0 %compare_select_fusion.2 = bf16[768,768]{1,0:T(8,128)(2,1)} fusion(bf16[1,768,768]{1,2,0:T(8,128)(2,1)} %copy.17, s32[768]{0:T(1024)S(1)} %get-tuple-element.50, s32[768]{0:T(1024)S(1)} %convert_reduce_fusion.1, s32[2,4,4]{2,1,0:T(4,128)S(1)} %copy-done.10), kind=kOutput, calls=%fused_computation.12 | convolution fusion | flops 5932048 | bytes 2369536 | tf_op jit(solution)/shard_map/dot_general | solution.py:63
  25.2 1.8 %compare_select_fusion = bf16[768,768]{1,0:T(8,128)(2,1)} fusion(bf16[768,768]{1,0:T(8,128)(2,1)S(1)} %copy.15, s32[768]{0:T(1024)S(1)} %get-tuple-element.49, s32[768]{0:T(1024)S(1)} %get-tuple-element.50, s32[2,4,4]{2,1,0:T(4,128)S(1)} %copy-done.10), kind=kOutput, calls=%fused_computation.10 | convolution fusion | flops 5932048 | bytes 2369536 | tf_op jit(solution)/shard_map/dot_general | solution.py:63
  27.0 2.0 %collective-permute-start.3 = (s32[4,4]{1,0:T(4,128)}, s32[4,4]{1,0:T(4,128)S(1)}, u32[]{:S(2)}, u32[]{:S(2)}) collective-permute-start(s32[4,4]{1,0:T(4,128)} %get-tuple-element.19), channel_id=1, source_target_pairs={{0,8},{4,12},{8,0},{12,4},{16,24},{20,28},{24,16},{28,20},{1,9},{5... | collective-permute-start | bytes 200 | tf_op jit(solution)/shard_map/ppermute | solution.py:20
  29.0 2.7 %fusion.3 = f32[768,768]{1,0:T(8,128)} fusion(s32[768]{0:T(1024)S(1)} %get-tuple-element.50, s32[768]{0:T(1024)S(1)} %convert_reduce_fusion.1, s32[4,4]{1,0:T(4,128)} %collective-permute-done), kind=kOutput, calls=%fused_computation.27 | convolution fusion | flops 4752400 | bytes 2365504 | tf_op jit(solution)/shard_map/dot_general | solution.py:63
  33.3 2.5 %add_convert_fusion.1 = bf16[768,768]{1,0:T(8,128)(2,1)S(1)} fusion(bf16[768,768]{1,0:T(8,128)(2,1)} %compare_select_fusion.2, bf16[768,768]{1,0:T(8,128)(2,1)S(1)} %copy.14, f32[768,768]{1,0:T(8,128)} %fusion.3), kind=kLoop, calls=%fused_computation.9 | loop fusion | flops 3538944 | bytes 5898240 | tf_op jit(solution)/shard_map/convert_element_type | solution.py:98
  35.8 3.8 %collective-permute-done.3 = s32[4,4]{1,0:T(4,128)S(1)} collective-permute-done((s32[4,4]{1,0:T(4,128)}, s32[4,4]{1,0:T(4,128)S(1)}, u32[]{:S(2)}, u32[]{:S(2)}) %collective-permute-start.3) | collective-permute-done | bytes 96 | tf_op jit(solution)/shard_map/ppermute | solution.py:20
  39.9 2.4 %add_convert_fusion = bf16[768,768]{1,0:T(8,128)(2,1)S(1)} fusion(bf16[768,768]{1,0:T(8,128)(2,1)} %compare_select_fusion, bf16[768,768]{1,0:T(8,128)(2,1)} %collective-permute-done.4, s32[768]{0:T(1024)S(1)} %get-tuple-element.49, s32[768]{0:T(1024)S(1)} %get-tuple-element.50, s32[4,4]{1,0:T(4,128)S(1)} %collective-permute-done.3), kind=kOutput, calls=%fused_computation.8 | convolution fusion | flops 8291344 | bytes 3545152 | tf_op jit(solution)/shard_map/dot_general | solution.py:63
  45.3 1.8 %collective-permute-start.7 = (bf16[64,768]{1,0:T(8,128)(2,1)S(1)}, bf16[64,768]{1,0:T(8,128)(2,1)S(1)}, u32[]{:S(2)}, u32[]{:S(2)}) collective-permute-start(bf16[64,768]{1,0:T(8,128)(2,1)S(1)} %get-tuple-element.35), channel_id=1, source_target_pairs={{0,8},{4,12},{8,0},{12,4},{16,24},{20,28},{24,16},{28,20},{1,9},{5... | collective-permute-start | bytes 294920 | tf_op jit(solution)/shard_map/ppermute | solution.py:20
  51.9 1.8 %collective-permute-start.8 = (bf16[3,256,128]{2,1,0:T(8,128)(2,1)S(1)}, bf16[3,256,128]{2,1,0:T(8,128)(2,1)S(1)}, u32[]{:S(2)}, u32[]{:S(2)}) collective-permute-start(bf16[3,256,128]{2,1,0:T(8,128)(2,1)S(1)} %slice_select_fusion), channel_id=1, source_target_pairs={{0,1},{1,2},{2,3},{3,0},{4,5},{5,6},{6,7},{7,4},{8,9},{9,10},{10,1... | collective-permute-start | bytes 589832 | tf_op jit(solution)/shard_map/ppermute | solution.py:39
  53.7 2.6 %collective-permute-start.9 = (bf16[3,256,128]{2,1,0:T(8,128)(2,1)S(1)}, bf16[3,256,128]{2,1,0:T(8,128)(2,1)S(1)}, u32[]{:S(2)}, u32[]{:S(2)}) collective-permute-start(bf16[3,256,128]{2,1,0:T(8,128)(2,1)S(1)} %slice_select_fusion), channel_id=1, source_target_pairs={{0,2},{1,3},{2,0},{3,1},{4,6},{5,7},{6,4},{7,5},{8,10},{9,11},{10,... | collective-permute-start | bytes 589832 | tf_op jit(solution)/shard_map/ppermute | solution.py:39
  61.3 2.4 %collective-permute-done.13 = bf16[64,768]{1,0:T(8,128)(2,1)S(1)} collective-permute-done((bf16[64,768]{1,0:T(8,128)(2,1)S(1)}, bf16[64,768]{1,0:T(8,128)(2,1)S(1)}, u32[]{:S(2)}, u32[]{:S(2)}) %collective-permute-start.13) | collective-permute-done | bytes 98336 | tf_op jit(solution)/shard_map/ppermute | solution.py:20
  66.3 2.0 %collective-permute-done.29 = bf16[64,768]{1,0:T(8,128)(2,1)S(1)} collective-permute-done((bf16[64,768]{1,0:T(8,128)(2,1)S(1)}, bf16[64,768]{1,0:T(8,128)(2,1)S(1)}, u32[]{:S(2)}, u32[]{:S(2)}) %collective-permute-start.29) | collective-permute-done | bytes 98336 | tf_op jit(solution)/shard_map/ppermute | solution.py:20
  80.2 1.8 %collective-permute-start.19 = (bf16[64,768]{1,0:T(8,128)(2,1)S(1)}, bf16[64,768]{1,0:T(8,128)(2,1)S(1)}, u32[]{:S(2)}, u32[]{:S(2)}) collective-permute-start(bf16[64,768]{1,0:T(8,128)(2,1)S(1)} %get-tuple-element.41), channel_id=1, source_target_pairs={{0,8},{4,12},{8,0},{12,4},{16,24},{20,28},{24,16},{28,20},{1,9},{5... | collective-permute-start | bytes 294920 | tf_op jit(solution)/shard_map/ppermute | solution.py:20
  86.2 2.1 %collective-permute-start.21 = (bf16[64,768]{1,0:T(8,128)(2,1)S(1)}, bf16[64,768]{1,0:T(8,128)(2,1)S(1)}, u32[]{:S(2)}, u32[]{:S(2)}) collective-permute-start(bf16[64,768]{1,0:T(8,128)(2,1)S(1)} %get-tuple-element.43), channel_id=1, source_target_pairs={{0,8},{4,12},{8,0},{12,4},{16,24},{20,28},{24,16},{28,20},{1,9},{5... | collective-permute-start | bytes 294920 | tf_op jit(solution)/shard_map/ppermute | solution.py:20
  92.4 2.0 %collective-permute-start.23 = (bf16[64,768]{1,0:T(8,128)(2,1)S(1)}, bf16[64,768]{1,0:T(8,128)(2,1)S(1)}, u32[]{:S(2)}, u32[]{:S(2)}) collective-permute-start(bf16[64,768]{1,0:T(8,128)(2,1)S(1)} %get-tuple-element.45), channel_id=1, source_target_pairs={{0,8},{4,12},{8,0},{12,4},{16,24},{20,28},{24,16},{28,20},{1,9},{5... | collective-permute-start | bytes 294920 | tf_op jit(solution)/shard_map/ppermute | solution.py:20
  98.5 2.2 %collective-permute-done.39 = bf16[64,768]{1,0:T(8,128)(2,1)S(1)} collective-permute-done((bf16[64,768]{1,0:T(8,128)(2,1)S(1)}, bf16[64,768]{1,0:T(8,128)(2,1)S(1)}, u32[]{:S(2)}, u32[]{:S(2)}) %collective-permute-start.39) | collective-permute-done | bytes 98336 | tf_op jit(solution)/shard_map/ppermute | solution.py:20
  101.1 3.4 %collective-permute-start.40 = (bf16[128,768]{1,0:T(8,128)(2,1)S(1)}, bf16[128,768]{1,0:T(8,128)(2,1)S(1)}, u32[]{:S(2)}, u32[]{:S(2)}) collective-permute-start(bf16[128,768]{1,0:T(8,128)(2,1)S(1)} %pad_maximum_fusion.5), channel_id=1, source_target_pairs={{0,1},{1,2},{2,3},{3,0},{4,5},{5,6},{6,7},{7,4},{8,9},{9,10},{10,1... | collective-permute-start | bytes 589832 | tf_op jit(solution)/shard_map/ppermute | solution.py:29
  104.4 2.6 %collective-permute-start.41 = (bf16[128,768]{1,0:T(8,128)(2,1)S(1)}, bf16[128,768]{1,0:T(8,128)(2,1)S(1)}, u32[]{:S(2)}, u32[]{:S(2)}) collective-permute-start(bf16[128,768]{1,0:T(8,128)(2,1)S(1)} %pad_maximum_fusion.5), channel_id=1, source_target_pairs={{0,2},{1,3},{2,0},{3,1},{4,6},{5,7},{6,4},{7,5},{8,10},{9,11},{10,... | collective-permute-start | bytes 589832 | tf_op jit(solution)/shard_map/ppermute | solution.py:29
  107.1 5.2 %collective-permute-done.40 = bf16[128,768]{1,0:T(8,128)(2,1)S(1)} collective-permute-done((bf16[128,768]{1,0:T(8,128)(2,1)S(1)}, bf16[128,768]{1,0:T(8,128)(2,1)S(1)}, u32[]{:S(2)}, u32[]{:S(2)}) %collective-permute-start.40) | collective-permute-done | bytes 196640 | tf_op jit(solution)/shard_map/ppermute | solution.py:29
  112.3 7.5 %collective-permute-done.41 = bf16[128,768]{1,0:T(8,128)(2,1)S(1)} collective-permute-done((bf16[128,768]{1,0:T(8,128)(2,1)S(1)}, bf16[128,768]{1,0:T(8,128)(2,1)S(1)}, u32[]{:S(2)}, u32[]{:S(2)}) %collective-permute-start.41) | collective-permute-done | bytes 196640 | tf_op jit(solution)/shard_map/ppermute | solution.py:29
  126.6 2.8 %collective-permute-done.44 = f32[512]{0:T(512)S(1)} collective-permute-done((f32[512]{0:T(512)S(1)}, f32[512]{0:T(512)S(1)}, u32[]{:S(2)}, u32[]{:S(2)}) %collective-permute-start.44) | collective-permute-done | bytes 2080 | tf_op jit(solution)/shard_map/ppermute | solution.py:20
  130.9 2.1 %collective-permute-done.45 = f32[512]{0:T(512)S(1)} collective-permute-done((f32[512]{0:T(512)S(1)}, f32[512]{0:T(512)S(1)}, u32[]{:S(2)}, u32[]{:S(2)}) %collective-permute-start.45) | collective-permute-done | bytes 2080 | tf_op jit(solution)/shard_map/ppermute | solution.py:20
  136.6 2.8 %collective-permute-done.47 = f32[512]{0:T(512)S(1)} collective-permute-done((f32[512]{0:T(512)S(1)}, f32[512]{0:T(512)S(1)}, u32[]{:S(2)}, u32[]{:S(2)}) %collective-permute-start.47) | collective-permute-done | bytes 2080 | tf_op jit(solution)/shard_map/ppermute | solution.py:20
  140.9 2.1 %collective-permute-done.48 = f32[512]{0:T(512)S(1)} collective-permute-done((f32[512]{0:T(512)S(1)}, f32[512]{0:T(512)S(1)}, u32[]{:S(2)}, u32[]{:S(2)}) %collective-permute-start.48) | collective-permute-done | bytes 2080 | tf_op jit(solution)/shard_map/ppermute | solution.py:20
  146.5 2.8 %collective-permute-done.50 = f32[512]{0:T(512)S(1)} collective-permute-done((f32[512]{0:T(512)S(1)}, f32[512]{0:T(512)S(1)}, u32[]{:S(2)}, u32[]{:S(2)}) %collective-permute-start.50) | collective-permute-done | bytes 2080 | tf_op jit(solution)/shard_map/ppermute | solution.py:20
  150.9 2.1 %collective-permute-done.51 = f32[512]{0:T(512)S(1)} collective-permute-done((f32[512]{0:T(512)S(1)}, f32[512]{0:T(512)S(1)}, u32[]{:S(2)}, u32[]{:S(2)}) %collective-permute-start.51) | collective-permute-done | bytes 2080 | tf_op jit(solution)/shard_map/ppermute | solution.py:20
  156.4 2.8 %collective-permute-done.53 = f32[128]{0:T(128)S(1)} collective-permute-done((f32[128]{0:T(128)S(1)}, f32[128]{0:T(128)S(1)}, u32[]{:S(2)}, u32[]{:S(2)}) %collective-permute-start.53) | collective-permute-done | bytes 544 | tf_op jit(solution)/shard_map/ppermute | solution.py:20
  160.6 2.0 %collective-permute-done.54 = f32[128]{0:T(128)S(1)} collective-permute-done((f32[128]{0:T(128)S(1)}, f32[128]{0:T(128)S(1)}, u32[]{:S(2)}, u32[]{:S(2)}) %collective-permute-start.54) | collective-permute-done | bytes 544 | tf_op jit(solution)/shard_map/ppermute | solution.py:20
  (217 shorter events, 77.5 us)
Async XLA Ops:
  1.6 40.7 %collective-permute-start.2 = (bf16[64,768]{1,0:T(8,128)(2,1)}, bf16[64,768]{1,0:T(8,128)(2,1)}, u32[]{:S(2)}, u32[]{:S(2)}) collective-permute-start(bf16[64,768]{1,0:T(8,128)(2,1)} %get-tuple-element.17), channel_id=1, source_target_pairs={{0,4},{4,0},{8,12},{12,8},{16,20},{20,16},{24,28},{28,24},{1,5},{5... | collective-permute-start | bytes 294920 | tf_op jit(solution)/shard_map/ppermute | solution.py:20
  2.1 41.6 %collective-permute-start.5 = (bf16[64,768]{1,0:T(8,128)(2,1)}, bf16[64,768]{1,0:T(8,128)(2,1)}, u32[]{:S(2)}, u32[]{:S(2)}) collective-permute-start(bf16[64,768]{1,0:T(8,128)(2,1)} %get-tuple-element.17), channel_id=1, source_target_pairs={{0,8},{4,12},{8,0},{12,4},{16,24},{20,28},{24,16},{28,20},{1,9},{5... | collective-permute-start | bytes 294920 | tf_op jit(solution)/shard_map/ppermute | solution.py:20
  5.9 21.1 %collective-permute-start = (s32[4,4]{1,0:T(4,128)}, s32[4,4]{1,0:T(4,128)}, u32[]{:S(2)}, u32[]{:S(2)}) collective-permute-start(s32[4,4]{1,0:T(4,128)} %get-tuple-element.20), channel_id=1, source_target_pairs={{0,4},{4,0},{8,12},{12,8},{16,20},{20,16},{24,28},{28,24},{1,5},{5... | collective-permute-start | bytes 200 | tf_op jit(solution)/shard_map/ppermute | solution.py:20
  10.9 20.8 %collective-permute-start.1 = (bf16[768,768]{0,1:T(8,128)(2,1)}, bf16[768,768]{0,1:T(8,128)(2,1)}, u32[]{:S(2)}, u32[]{:S(2)}) collective-permute-start(bf16[768,768]{0,1:T(8,128)(2,1)} %bitcast.4), channel_id=1, source_target_pairs={{0,4},{4,0},{8,12},{12,8},{16,20},{20,16},{24,28},{28,24},{1,5},{5... | collective-permute-start | bytes 3538952 | tf_op jit(solution)/shard_map/ppermute | solution.py:20
  11.2 28.7 %collective-permute-start.4 = (bf16[768,768]{1,0:T(8,128)(2,1)}, bf16[768,768]{1,0:T(8,128)(2,1)}, u32[]{:S(2)}, u32[]{:S(2)}) collective-permute-start(bf16[768,768]{1,0:T(8,128)(2,1)} %get-tuple-element.12), channel_id=1, source_target_pairs={{0,8},{4,12},{8,0},{12,4},{16,24},{20,28},{24,16},{28,20},{1,9},{5... | collective-permute-start | bytes 3538952 | tf_op jit(solution)/shard_map/ppermute | solution.py:20
  27.0 12.6 %collective-permute-start.3 = (s32[4,4]{1,0:T(4,128)}, s32[4,4]{1,0:T(4,128)S(1)}, u32[]{:S(2)}, u32[]{:S(2)}) collective-permute-start(s32[4,4]{1,0:T(4,128)} %get-tuple-element.19), channel_id=1, source_target_pairs={{0,8},{4,12},{8,0},{12,4},{16,24},{20,28},{24,16},{28,20},{1,9},{5... | collective-permute-start | bytes 200 | tf_op jit(solution)/shard_map/ppermute | solution.py:20
  31.7 15.4 %collective-permute-start.24 = (bf16[64,768]{1,0:T(8,128)(2,1)}, bf16[64,768]{1,0:T(8,128)(2,1)}, u32[]{:S(2)}, u32[]{:S(2)}) collective-permute-start(bf16[64,768]{1,0:T(8,128)(2,1)} %get-tuple-element.18), channel_id=1, source_target_pairs={{0,4},{4,0},{8,12},{12,8},{16,20},{20,16},{24,28},{28,24},{1,5},{5... | collective-permute-start | bytes 294920 | tf_op jit(solution)/shard_map/ppermute | solution.py:20
  39.6 8.7 %collective-permute-start.25 = (bf16[64,768]{1,0:T(8,128)(2,1)}, bf16[64,768]{1,0:T(8,128)(2,1)}, u32[]{:S(2)}, u32[]{:S(2)}) collective-permute-start(bf16[64,768]{1,0:T(8,128)(2,1)} %get-tuple-element.18), channel_id=1, source_target_pairs={{0,8},{4,12},{8,0},{12,4},{16,24},{20,28},{24,16},{28,20},{1,9},{5... | collective-permute-start | bytes 294920 | tf_op jit(solution)/shard_map/ppermute | solution.py:20
  45.3 5.3 %collective-permute-start.6 = (bf16[64,768]{1,0:T(8,128)(2,1)S(1)}, bf16[64,768]{1,0:T(8,128)(2,1)S(1)}, u32[]{:S(2)}, u32[]{:S(2)}) collective-permute-start(bf16[64,768]{1,0:T(8,128)(2,1)S(1)} %get-tuple-element.35), channel_id=1, source_target_pairs={{0,4},{4,0},{8,12},{12,8},{16,20},{20,16},{24,28},{28,24},{1,5},{5... | collective-permute-start | bytes 294920 | tf_op jit(solution)/shard_map/ppermute | solution.py:20
  45.3 5.5 %collective-permute-start.7 = (bf16[64,768]{1,0:T(8,128)(2,1)S(1)}, bf16[64,768]{1,0:T(8,128)(2,1)S(1)}, u32[]{:S(2)}, u32[]{:S(2)}) collective-permute-start(bf16[64,768]{1,0:T(8,128)(2,1)S(1)} %get-tuple-element.35), channel_id=1, source_target_pairs={{0,8},{4,12},{8,0},{12,4},{16,24},{20,28},{24,16},{28,20},{1,9},{5... | collective-permute-start | bytes 294920 | tf_op jit(solution)/shard_map/ppermute | solution.py:20
  49.9 8.1 %collective-permute-start.26 = (bf16[64,768]{1,0:T(8,128)(2,1)S(1)}, bf16[64,768]{1,0:T(8,128)(2,1)S(1)}, u32[]{:S(2)}, u32[]{:S(2)}) collective-permute-start(bf16[64,768]{1,0:T(8,128)(2,1)S(1)} %get-tuple-element.21), channel_id=1, source_target_pairs={{0,4},{4,0},{8,12},{12,8},{16,20},{20,16},{24,28},{28,24},{1,5},{5... | collective-permute-start | bytes 294920 | tf_op jit(solution)/shard_map/ppermute | solution.py:20
  50.1 8.3 %collective-permute-start.27 = (bf16[64,768]{1,0:T(8,128)(2,1)S(1)}, bf16[64,768]{1,0:T(8,128)(2,1)S(1)}, u32[]{:S(2)}, u32[]{:S(2)}) collective-permute-start(bf16[64,768]{1,0:T(8,128)(2,1)S(1)} %get-tuple-element.21), channel_id=1, source_target_pairs={{0,8},{4,12},{8,0},{12,4},{16,24},{20,28},{24,16},{28,20},{1,9},{5... | collective-permute-start | bytes 294920 | tf_op jit(solution)/shard_map/ppermute | solution.py:20
  51.9 18.5 %collective-permute-start.8 = (bf16[3,256,128]{2,1,0:T(8,128)(2,1)S(1)}, bf16[3,256,128]{2,1,0:T(8,128)(2,1)S(1)}, u32[]{:S(2)}, u32[]{:S(2)}) collective-permute-start(bf16[3,256,128]{2,1,0:T(8,128)(2,1)S(1)} %slice_select_fusion), channel_id=1, source_target_pairs={{0,1},{1,2},{2,3},{3,0},{4,5},{5,6},{6,7},{7,4},{8,9},{9,10},{10,1... | collective-permute-start | bytes 589832 | tf_op jit(solution)/shard_map/ppermute | solution.py:39
  53.7 16.8 %collective-permute-start.9 = (bf16[3,256,128]{2,1,0:T(8,128)(2,1)S(1)}, bf16[3,256,128]{2,1,0:T(8,128)(2,1)S(1)}, u32[]{:S(2)}, u32[]{:S(2)}) collective-permute-start(bf16[3,256,128]{2,1,0:T(8,128)(2,1)S(1)} %slice_select_fusion), channel_id=1, source_target_pairs={{0,2},{1,3},{2,0},{3,1},{4,6},{5,7},{6,4},{7,5},{8,10},{9,11},{10,... | collective-permute-start | bytes 589832 | tf_op jit(solution)/shard_map/ppermute | solution.py:39
  56.3 14.9 %collective-permute-start.10 = (bf16[3,256,128]{2,1,0:T(8,128)(2,1)S(1)}, bf16[3,256,128]{2,1,0:T(8,128)(2,1)S(1)}, u32[]{:S(2)}, u32[]{:S(2)}) collective-permute-start(bf16[3,256,128]{2,1,0:T(8,128)(2,1)S(1)} %slice_select_fusion), channel_id=1, source_target_pairs={{0,3},{1,0},{2,1},{3,2},{4,7},{5,4},{6,5},{7,6},{8,11},{9,8},{10,9... | collective-permute-start | bytes 589832 | tf_op jit(solution)/shard_map/ppermute | solution.py:39
  58.5 5.2 %collective-permute-start.13 = (bf16[64,768]{1,0:T(8,128)(2,1)S(1)}, bf16[64,768]{1,0:T(8,128)(2,1)S(1)}, u32[]{:S(2)}, u32[]{:S(2)}) collective-permute-start(bf16[64,768]{1,0:T(8,128)(2,1)S(1)} %convert_element_type.170), channel_id=1, source_target_pairs={{0,8},{4,12},{8,0},{12,4},{16,24},{20,28},{24,16},{28,20},{1,9},{5... | collective-permute-start | bytes 294920 | tf_op jit(solution)/shard_map/ppermute | solution.py:20
  65.5 7.3 %collective-permute-start.14 = (bf16[64,768]{1,0:T(8,128)(2,1)S(1)}, bf16[64,768]{1,0:T(8,128)(2,1)S(1)}, u32[]{:S(2)}, u32[]{:S(2)}) collective-permute-start(bf16[64,768]{1,0:T(8,128)(2,1)S(1)} %get-tuple-element.37), channel_id=1, source_target_pairs={{0,4},{4,0},{8,12},{12,8},{16,20},{20,16},{24,28},{28,24},{1,5},{5... | collective-permute-start | bytes 294920 | tf_op jit(solution)/shard_map/ppermute | solution.py:20
  70.5 5.4 %collective-permute-start.30 = (bf16[64,768]{1,0:T(8,128)(2,1)S(1)}, bf16[64,768]{1,0:T(8,128)(2,1)S(1)}, u32[]{:S(2)}, u32[]{:S(2)}) collective-permute-start(bf16[64,768]{1,0:T(8,128)(2,1)S(1)} %get-tuple-element.25), channel_id=1, source_target_pairs={{0,4},{4,0},{8,12},{12,8},{16,20},{20,16},{24,28},{28,24},{1,5},{5... | collective-permute-start | bytes 294920 | tf_op jit(solution)/shard_map/ppermute | solution.py:20
  70.6 5.7 %collective-permute-start.31 = (bf16[64,768]{1,0:T(8,128)(2,1)S(1)}, bf16[64,768]{1,0:T(8,128)(2,1)S(1)}, u32[]{:S(2)}, u32[]{:S(2)}) collective-permute-start(bf16[64,768]{1,0:T(8,128)(2,1)S(1)} %get-tuple-element.25), channel_id=1, source_target_pairs={{0,8},{4,12},{8,0},{12,4},{16,24},{20,28},{24,16},{28,20},{1,9},{5... | collective-permute-start | bytes 294920 | tf_op jit(solution)/shard_map/ppermute | solution.py:20
  72.7 48.0 %collective-permute-start.11 = (bf16[4,3,256,128]{3,2,1,0:T(8,128)(2,1)}, bf16[4,3,256,128]{3,2,1,0:T(8,128)(2,1)}, u32[]{:S(2)}, u32[]{:S(2)}) collective-permute-start(bf16[4,3,256,128]{3,2,1,0:T(8,128)(2,1)} %get-tuple-element.15), channel_id=1, source_target_pairs={{0,4},{4,0},{8,12},{12,8},{16,20},{20,16},{24,28},{28,24},{1,5},{5... | collective-permute-start | bytes 2359304 | tf_op jit(solution)/shard_map/ppermute | solution.py:20
  76.9 5.1 %collective-permute-start.32 = (bf16[64,768]{1,0:T(8,128)(2,1)S(1)}, bf16[64,768]{1,0:T(8,128)(2,1)S(1)}, u32[]{:S(2)}, u32[]{:S(2)}) collective-permute-start(bf16[64,768]{1,0:T(8,128)(2,1)S(1)} %get-tuple-element.27), channel_id=1, source_target_pairs={{0,4},{4,0},{8,12},{12,8},{16,20},{20,16},{24,28},{28,24},{1,5},{5... | collective-permute-start | bytes 294920 | tf_op jit(solution)/shard_map/ppermute | solution.py:20
  77.0 5.3 %collective-permute-start.33 = (bf16[64,768]{1,0:T(8,128)(2,1)S(1)}, bf16[64,768]{1,0:T(8,128)(2,1)S(1)}, u32[]{:S(2)}, u32[]{:S(2)}) collective-permute-start(bf16[64,768]{1,0:T(8,128)(2,1)S(1)} %get-tuple-element.27), channel_id=1, source_target_pairs={{0,8},{4,12},{8,0},{12,4},{16,24},{20,28},{24,16},{28,20},{1,9},{5... | collective-permute-start | bytes 294920 | tf_op jit(solution)/shard_map/ppermute | solution.py:20
  80.2 5.2 %collective-permute-start.19 = (bf16[64,768]{1,0:T(8,128)(2,1)S(1)}, bf16[64,768]{1,0:T(8,128)(2,1)S(1)}, u32[]{:S(2)}, u32[]{:S(2)}) collective-permute-start(bf16[64,768]{1,0:T(8,128)(2,1)S(1)} %get-tuple-element.41), channel_id=1, source_target_pairs={{0,8},{4,12},{8,0},{12,4},{16,24},{20,28},{24,16},{28,20},{1,9},{5... | collective-permute-start | bytes 294920 | tf_op jit(solution)/shard_map/ppermute | solution.py:20
  83.1 5.2 %collective-permute-start.34 = (bf16[64,768]{1,0:T(8,128)(2,1)S(1)}, bf16[64,768]{1,0:T(8,128)(2,1)S(1)}, u32[]{:S(2)}, u32[]{:S(2)}) collective-permute-start(bf16[64,768]{1,0:T(8,128)(2,1)S(1)} %get-tuple-element.29), channel_id=1, source_target_pairs={{0,4},{4,0},{8,12},{12,8},{16,20},{20,16},{24,28},{28,24},{1,5},{5... | collective-permute-start | bytes 294920 | tf_op jit(solution)/shard_map/ppermute | solution.py:20
  83.3 5.3 %collective-permute-start.35 = (bf16[64,768]{1,0:T(8,128)(2,1)S(1)}, bf16[64,768]{1,0:T(8,128)(2,1)S(1)}, u32[]{:S(2)}, u32[]{:S(2)}) collective-permute-start(bf16[64,768]{1,0:T(8,128)(2,1)S(1)} %get-tuple-element.29), channel_id=1, source_target_pairs={{0,8},{4,12},{8,0},{12,4},{16,24},{20,28},{24,16},{28,20},{1,9},{5... | collective-permute-start | bytes 294920 | tf_op jit(solution)/shard_map/ppermute | solution.py:20
  86.2 5.5 %collective-permute-start.21 = (bf16[64,768]{1,0:T(8,128)(2,1)S(1)}, bf16[64,768]{1,0:T(8,128)(2,1)S(1)}, u32[]{:S(2)}, u32[]{:S(2)}) collective-permute-start(bf16[64,768]{1,0:T(8,128)(2,1)S(1)} %get-tuple-element.43), channel_id=1, source_target_pairs={{0,8},{4,12},{8,0},{12,4},{16,24},{20,28},{24,16},{28,20},{1,9},{5... | collective-permute-start | bytes 294920 | tf_op jit(solution)/shard_map/ppermute | solution.py:20
  89.3 5.1 %collective-permute-start.36 = (bf16[64,768]{1,0:T(8,128)(2,1)S(1)}, bf16[64,768]{1,0:T(8,128)(2,1)S(1)}, u32[]{:S(2)}, u32[]{:S(2)}) collective-permute-start(bf16[64,768]{1,0:T(8,128)(2,1)S(1)} %get-tuple-element.31), channel_id=1, source_target_pairs={{0,4},{4,0},{8,12},{12,8},{16,20},{20,16},{24,28},{28,24},{1,5},{5... | collective-permute-start | bytes 294920 | tf_op jit(solution)/shard_map/ppermute | solution.py:20
  89.5 5.3 %collective-permute-start.37 = (bf16[64,768]{1,0:T(8,128)(2,1)S(1)}, bf16[64,768]{1,0:T(8,128)(2,1)S(1)}, u32[]{:S(2)}, u32[]{:S(2)}) collective-permute-start(bf16[64,768]{1,0:T(8,128)(2,1)S(1)} %get-tuple-element.31), channel_id=1, source_target_pairs={{0,8},{4,12},{8,0},{12,4},{16,24},{20,28},{24,16},{28,20},{1,9},{5... | collective-permute-start | bytes 294920 | tf_op jit(solution)/shard_map/ppermute | solution.py:20
  92.4 5.4 %collective-permute-start.23 = (bf16[64,768]{1,0:T(8,128)(2,1)S(1)}, bf16[64,768]{1,0:T(8,128)(2,1)S(1)}, u32[]{:S(2)}, u32[]{:S(2)}) collective-permute-start(bf16[64,768]{1,0:T(8,128)(2,1)S(1)} %get-tuple-element.45), channel_id=1, source_target_pairs={{0,8},{4,12},{8,0},{12,4},{16,24},{20,28},{24,16},{28,20},{1,9},{5... | collective-permute-start | bytes 294920 | tf_op jit(solution)/shard_map/ppermute | solution.py:20
  101.1 11.3 %collective-permute-start.40 = (bf16[128,768]{1,0:T(8,128)(2,1)S(1)}, bf16[128,768]{1,0:T(8,128)(2,1)S(1)}, u32[]{:S(2)}, u32[]{:S(2)}) collective-permute-start(bf16[128,768]{1,0:T(8,128)(2,1)S(1)} %pad_maximum_fusion.5), channel_id=1, source_target_pairs={{0,1},{1,2},{2,3},{3,0},{4,5},{5,6},{6,7},{7,4},{8,9},{9,10},{10,1... | collective-permute-start | bytes 589832 | tf_op jit(solution)/shard_map/ppermute | solution.py:29
  104.4 15.4 %collective-permute-start.41 = (bf16[128,768]{1,0:T(8,128)(2,1)S(1)}, bf16[128,768]{1,0:T(8,128)(2,1)S(1)}, u32[]{:S(2)}, u32[]{:S(2)}) collective-permute-start(bf16[128,768]{1,0:T(8,128)(2,1)S(1)} %pad_maximum_fusion.5), channel_id=1, source_target_pairs={{0,2},{1,3},{2,0},{3,1},{4,6},{5,7},{6,4},{7,5},{8,10},{9,11},{10,... | collective-permute-start | bytes 589832 | tf_op jit(solution)/shard_map/ppermute | solution.py:29
  107.0 12.8 %collective-permute-start.42 = (bf16[128,768]{1,0:T(8,128)(2,1)S(1)}, bf16[128,768]{1,0:T(8,128)(2,1)S(1)}, u32[]{:S(2)}, u32[]{:S(2)}) collective-permute-start(bf16[128,768]{1,0:T(8,128)(2,1)S(1)} %pad_maximum_fusion.5), channel_id=1, source_target_pairs={{0,3},{1,0},{2,1},{3,2},{4,7},{5,4},{6,5},{7,6},{8,11},{9,8},{10,9... | collective-permute-start | bytes 589832 | tf_op jit(solution)/shard_map/ppermute | solution.py:29
  (36 other events, 106.3 us)

commit v15 on v14

--- a/solution.py
+++ b/solution.py
@@ -98,18 +98,21 @@
             (other_block.astype(jnp.float32) + own_block_t.astype(jnp.float32)).astype(jnp.bfloat16)
         )
 
-    def apply_operator(values):
+    def apply_operator(values, received=None):
         result = jnp.dot(values, diag_sym, preferred_element_type=jnp.float32)
         for round_index in range(ROUNDS):
-            other_rows = swapped(values, "atoms", round_index)
+            if received is None:
+                other_rows = swapped(values, "atoms", round_index)
+            else:
+                other_rows = received[round_index]
             result = result + jnp.dot(
                 other_rows, other_pair[round_index], preferred_element_type=jnp.float32
             )
         return result
 
-    def chebyshev(start_rows, hook):
+    def chebyshev(start_rows, hook, received):
         previous = start_rows.astype(jnp.float32)
-        current = (apply_operator(start_rows) - filter_center * previous) / filter_half
+        current = (apply_operator(start_rows, received) - filter_center * previous) / filter_half
         for degree_index in range(1, DEGREE):
             if degree_index == GATHER_AT:
                 current = hook(current)
@@ -137,10 +140,17 @@
         return current
 
     half_bands = subspace.shape[0] // 2
+    first_rows = [swapped(subspace, "atoms", r) for r in range(ROUNDS)]
     current = jnp.concatenate(
         [
-            chebyshev(subspace[:half_bands], start_rotation_gather),
-            chebyshev(subspace[half_bands:], lambda rows: rows),
+            chebyshev(
+                subspace[:half_bands], start_rotation_gather,
+                [rows[:half_bands] for rows in first_rows],
+            ),
+            chebyshev(
+                subspace[half_bands:], lambda rows: rows,
+                [rows[half_bands:] for rows in first_rows],
+            ),
         ],
         axis=0,
     )

time: 166 us -> 169 us (1.018); the launches traced: 164 us -> 169 us
  waiting for transfers between devices: 52.4 us -> 66 us
  starting transfers between devices: 46.1 us -> 40.9 us
  local copies, waits for them, and re-layouts: 17.7 us -> 14.8 us
    ppermute x3, waiting for transfers between devices: 0.01 us -> 13 us  [gather_pieces(): pieces.append(lax.ppermute(value, 'bands', pairs))]
    ppermute x3, waiting for transfers between devices: 12.8 us -> 15.4 us  [gather_bands(): pieces.append(lax.ppermute(value, 'bands', pairs))]
    ppermute x3, starting transfers between devices: 5.97 us -> 3.83 us  [gather_bands(): pieces.append(lax.ppermute(value, 'bands', pairs))]
    ppermute x49 -> x47, starting transfers between devices: 34.4 us -> 32.4 us  [swapped(): return lax.ppermute(value, axis, pairs)]
    ppermute x49 -> x47, waiting for transfers between devices: 39.6 us -> 37.6 us  [swapped(): return lax.ppermute(value, axis, pairs)]
    unnamed x27 -> x25, local copies, waits for them, and re-layouts: 3.98 us -> 3.39 us
  transfers between devices with their start and end apart: 55 -> 53, of which waited for: 22 -> 23; matrix products, arithmetic and copies ran while one was open for 32% -> 29% of each run, Pallas kernels for 0% -> 0%
where the time goes in v15:
time: 169 us
  waiting for transfers between devices  66 us (39%)
  starting transfers between devices  40.9 us (24%)
  matrix products  36.1 us (21%)
  local copies, waits for them, and re-layouts  14.8 us (9%)
  other arithmetic  10.1 us (6%)
    ppermute x47, waiting for transfers between devices, swapped(): return lax.ppermute(value, axis, pairs)  37.6 us
    ppermute x47, starting transfers between devices, swapped(): return lax.ppermute(value, axis, pairs)  32.4 us
    ppermute x3, waiting for transfers between devices, gather_bands(): pieces.append(lax.ppermute(value, 'bands', pairs))  15.4 us
    dot_general x32, matrix products, apply_operator(): jnp.dot(other_rows, other_pair[round_index], preferred_element_type=jnp.f...  14.5 us
    ppermute x3, waiting for transfers between devices, gather_pieces(): pieces.append(lax.ppermute(value, 'bands', pairs))  13 us
    dot_general x4, matrix products, pattern_mask(): lax.dot_general(per_row.astype(jnp.bfloat16), col_onehot, (((1,), (1,)),...  9.96 us
    dot_general x16, matrix products, apply_operator(): result = jnp.dot(values, diag_sym, preferred_element_type=jnp.float32)  6.63 us
    ppermute x3, starting transfers between devices, gather_pieces(): pieces.append(lax.ppermute(value, 'bands', pairs))  4.7 us
  transfers between devices with their start and end apart: 53, of which 23 were waited for; matrix products, arithmetic and copies ran while one was open for 29% of the time, Pallas kernels for 0%

profile of v15, /device:TPU:0, one launch (start us, length us, event | category | flops | bytes accessed | tf_op | source)
XLA Modules:
  0.0 168.6 jit_solution(6496641578869004533)
XLA Ops:
  0.5 2.5 %collective-permute-start.5 = (bf16[128,768]{1,0:T(8,128)(2,1)}, bf16[128,768]{1,0:T(8,128)(2,1)}, u32[]{:S(2)}, u32[]{:S(2)}) collective-permute-start(bf16[128,768]{1,0:T(8,128)(2,1)} %param.6), channel_id=1, source_target_pairs={{0,8},{4,12},{8,0},{12,4},{16,24},{20,28},{24,16},{28,20},{1,9},{5... | collective-permute-start | bytes 589832 | tf_op jit(solution)/shard_map/ppermute | solution.py:20
  2.9 3.3 %slice_bitcast_fusion.1 = (bf16[768,768]{1,0:T(8,128)(2,1)}, bf16[768,768]{0,1:T(8,128)(2,1)}, bf16[1,768,768]{2,1,0:T(8,128)(2,1)S(1)}) fusion(bf16[2,768,768]{2,1,0:T(8,128)(2,1)} %param.8), kind=kLoop, calls=%fused_computation.109 | loop fusion | bytes 5898240 | tf_op jit(solution)/shard_map/squeeze | solution.py:74
  8.8 1.6 convert_bitcast_fusion
  10.4 2.0 %copy.12 = f32[768,768]{1,0:T(8,128)S(1)} copy(f32[768,768]{0,1:T(8,128)} %convert_bitcast_fusion) | data formatting | bytes 4718592 | tf_op jit(solution)/shard_map/convert_element_type | solution.py:85
  13.2 2.3 %fusion.1 = bf16[768,768]{1,0:T(8,128)(2,1)S(1)} fusion(bf16[768,768]{1,0:T(8,128)(2,1)} %param.7, f32[768,768]{1,0:T(8,128)S(1)} %copy.12, s32[768]{0:T(1024)S(1)} %get-tuple-element.48), kind=kLoop, calls=%fused_computation.6 | loop fusion | flops 7667712 | bytes 4721664 | tf_op jit(solution)/shard_map/convert_element_type | solution.py:86
  18.1 3.0 %compare_select_fusion.2 = bf16[768,768]{1,0:T(8,128)(2,1)} fusion(bf16[1,768,768]{1,2,0:T(8,128)(2,1)} %copy.17, s32[768]{0:T(1024)S(1)} %get-tuple-element.48, s32[768]{0:T(1024)S(1)} %convert_reduce_fusion.1, s32[2,4,4]{2,1,0:T(4,128)S(1)} %copy-done.10), kind=kOutput, calls=%fused_computation.12 | convolution fusion | flops 5932048 | bytes 2369536 | tf_op jit(solution)/shard_map/dot_general | solution.py:63
  22.1 1.8 %compare_select_fusion = bf16[768,768]{1,0:T(8,128)(2,1)} fusion(bf16[768,768]{1,0:T(8,128)(2,1)S(1)} %copy.15, s32[768]{0:T(1024)S(1)} %get-tuple-element.47, s32[768]{0:T(1024)S(1)} %get-tuple-element.48, s32[2,4,4]{2,1,0:T(4,128)S(1)} %copy-done.10), kind=kOutput, calls=%fused_computation.10 | convolution fusion | flops 5932048 | bytes 2369536 | tf_op jit(solution)/shard_map/dot_general | solution.py:63
  23.9 2.0 %collective-permute-start.3 = (s32[4,4]{1,0:T(4,128)}, s32[4,4]{1,0:T(4,128)S(1)}, u32[]{:S(2)}, u32[]{:S(2)}) collective-permute-start(s32[4,4]{1,0:T(4,128)} %get-tuple-element.17), channel_id=1, source_target_pairs={{0,8},{4,12},{8,0},{12,4},{16,24},{20,28},{24,16},{28,20},{1,9},{5... | collective-permute-start | bytes 200 | tf_op jit(solution)/shard_map/ppermute | solution.py:20
  25.9 2.8 %fusion.3 = f32[768,768]{1,0:T(8,128)} fusion(s32[768]{0:T(1024)S(1)} %get-tuple-element.48, s32[768]{0:T(1024)S(1)} %convert_reduce_fusion.1, s32[4,4]{1,0:T(4,128)} %collective-permute-done), kind=kOutput, calls=%fused_computation.27 | convolution fusion | flops 4752400 | bytes 2365504 | tf_op jit(solution)/shard_map/dot_general | solution.py:63
  30.3 2.5 %add_convert_fusion.1 = bf16[768,768]{1,0:T(8,128)(2,1)S(1)} fusion(bf16[768,768]{1,0:T(8,128)(2,1)} %compare_select_fusion.2, bf16[768,768]{1,0:T(8,128)(2,1)S(1)} %copy.14, f32[768,768]{1,0:T(8,128)} %fusion.3), kind=kLoop, calls=%fused_computation.9 | loop fusion | flops 3538944 | bytes 5898240 | tf_op jit(solution)/shard_map/convert_element_type | solution.py:98
  32.7 4.5 %collective-permute-done.3 = s32[4,4]{1,0:T(4,128)S(1)} collective-permute-done((s32[4,4]{1,0:T(4,128)}, s32[4,4]{1,0:T(4,128)S(1)}, u32[]{:S(2)}, u32[]{:S(2)}) %collective-permute-start.3) | collective-permute-done | bytes 96 | tf_op jit(solution)/shard_map/ppermute | solution.py:20
  37.3 2.4 %add_convert_fusion = bf16[768,768]{1,0:T(8,128)(2,1)S(1)} fusion(bf16[768,768]{1,0:T(8,128)(2,1)} %compare_select_fusion, bf16[768,768]{1,0:T(8,128)(2,1)} %collective-permute-done.4, s32[768]{0:T(1024)S(1)} %get-tuple-element.47, s32[768]{0:T(1024)S(1)} %get-tuple-element.48, s32[4,4]{1,0:T(4,128)S(1)} %collective-permute-done.3), kind=kOutput, calls=%fused_computation.8 | convolution fusion | flops 8291344 | bytes 3545152 | tf_op jit(solution)/shard_map/dot_general | solution.py:63
  46.1 1.7 %collective-permute-start.7 = (bf16[64,768]{1,0:T(8,128)(2,1)S(1)}, bf16[64,768]{1,0:T(8,128)(2,1)S(1)}, u32[]{:S(2)}, u32[]{:S(2)}) collective-permute-start(bf16[64,768]{1,0:T(8,128)(2,1)S(1)} %get-tuple-element.33), channel_id=1, source_target_pairs={{0,8},{4,12},{8,0},{12,4},{16,24},{20,28},{24,16},{28,20},{1,9},{5... | collective-permute-start | bytes 294920 | tf_op jit(solution)/shard_map/ppermute | solution.py:20
  52.0 2.1 %collective-permute-start.13 = (bf16[64,768]{1,0:T(8,128)(2,1)S(1)}, bf16[64,768]{1,0:T(8,128)(2,1)S(1)}, u32[]{:S(2)}, u32[]{:S(2)}) collective-permute-start(bf16[64,768]{1,0:T(8,128)(2,1)S(1)} %convert_element_type.170), channel_id=1, source_target_pairs={{0,8},{4,12},{8,0},{12,4},{16,24},{20,28},{24,16},{28,20},{1,9},{5... | collective-permute-start | bytes 294920 | tf_op jit(solution)/shard_map/ppermute | solution.py:20
  54.2 3.5 %collective-permute-start.10 = (bf16[3,256,128]{2,1,0:T(8,128)(2,1)S(1)}, bf16[3,256,128]{2,1,0:T(8,128)(2,1)S(1)}, u32[]{:S(2)}, u32[]{:S(2)}) collective-permute-start(bf16[3,256,128]{2,1,0:T(8,128)(2,1)S(1)} %slice_select_fusion), channel_id=1, source_target_pairs={{0,3},{1,0},{2,1},{3,2},{4,7},{5,4},{6,5},{7,6},{8,11},{9,8},{10,9... | collective-permute-start | bytes 589832 | tf_op jit(solution)/shard_map/ppermute | solution.py:39
  63.0 11.7 %collective-permute-done.9 = bf16[3,256,128]{2,1,0:T(8,128)(2,1)S(1)} collective-permute-done((bf16[3,256,128]{2,1,0:T(8,128)(2,1)S(1)}, bf16[3,256,128]{2,1,0:T(8,128)(2,1)S(1)}, u32[]{:S(2)}, u32[]{:S(2)}) %collective-permute-start.9) | collective-permute-done | bytes 196640 | tf_op jit(solution)/shard_map/ppermute | solution.py:39
  78.1 1.8 %collective-permute-start.31 = (bf16[64,768]{1,0:T(8,128)(2,1)S(1)}, bf16[64,768]{1,0:T(8,128)(2,1)S(1)}, u32[]{:S(2)}, u32[]{:S(2)}) collective-permute-start(bf16[64,768]{1,0:T(8,128)(2,1)S(1)} %get-tuple-element.25), channel_id=1, source_target_pairs={{0,8},{4,12},{8,0},{12,4},{16,24},{20,28},{24,16},{28,20},{1,9},{5... | collective-permute-start | bytes 294920 | tf_op jit(solution)/shard_map/ppermute | solution.py:20
  84.0 2.3 %collective-permute-start.33 = (bf16[64,768]{1,0:T(8,128)(2,1)S(1)}, bf16[64,768]{1,0:T(8,128)(2,1)S(1)}, u32[]{:S(2)}, u32[]{:S(2)}) collective-permute-start(bf16[64,768]{1,0:T(8,128)(2,1)S(1)} %get-tuple-element.27), channel_id=1, source_target_pairs={{0,8},{4,12},{8,0},{12,4},{16,24},{20,28},{24,16},{28,20},{1,9},{5... | collective-permute-start | bytes 294920 | tf_op jit(solution)/shard_map/ppermute | solution.py:20
  90.4 2.2 %collective-permute-start.35 = (bf16[64,768]{1,0:T(8,128)(2,1)S(1)}, bf16[64,768]{1,0:T(8,128)(2,1)S(1)}, u32[]{:S(2)}, u32[]{:S(2)}) collective-permute-start(bf16[64,768]{1,0:T(8,128)(2,1)S(1)} %get-tuple-element.29), channel_id=1, source_target_pairs={{0,8},{4,12},{8,0},{12,4},{16,24},{20,28},{24,16},{28,20},{1,9},{5... | collective-permute-start | bytes 294920 | tf_op jit(solution)/shard_map/ppermute | solution.py:20
  96.7 2.2 %collective-permute-start.37 = (bf16[64,768]{1,0:T(8,128)(2,1)S(1)}, bf16[64,768]{1,0:T(8,128)(2,1)S(1)}, u32[]{:S(2)}, u32[]{:S(2)}) collective-permute-start(bf16[64,768]{1,0:T(8,128)(2,1)S(1)} %get-tuple-element.31), channel_id=1, source_target_pairs={{0,8},{4,12},{8,0},{12,4},{16,24},{20,28},{24,16},{28,20},{1,9},{5... | collective-permute-start | bytes 294920 | tf_op jit(solution)/shard_map/ppermute | solution.py:20
  103.1 2.2 %collective-permute-done.23 = bf16[64,768]{1,0:T(8,128)(2,1)S(1)} collective-permute-done((bf16[64,768]{1,0:T(8,128)(2,1)S(1)}, bf16[64,768]{1,0:T(8,128)(2,1)S(1)}, u32[]{:S(2)}, u32[]{:S(2)}) %collective-permute-start.23) | collective-permute-done | bytes 98336 | tf_op jit(solution)/shard_map/ppermute | solution.py:20
  107.5 1.9 %collective-permute-start.38 = (bf16[128,768]{1,0:T(8,128)(2,1)S(1)}, bf16[128,768]{1,0:T(8,128)(2,1)S(1)}, u32[]{:S(2)}, u32[]{:S(2)}) collective-permute-start(bf16[128,768]{1,0:T(8,128)(2,1)S(1)} %pad_maximum_fusion.5), channel_id=1, source_target_pairs={{0,1},{1,2},{2,3},{3,0},{4,5},{5,6},{6,7},{7,4},{8,9},{9,10},{10,1... | collective-permute-start | bytes 589832 | tf_op jit(solution)/shard_map/ppermute | solution.py:29
  109.5 3.1 %collective-permute-done.40 = bf16[128,768]{1,0:T(8,128)(2,1)S(1)} collective-permute-done((bf16[128,768]{1,0:T(8,128)(2,1)S(1)}, bf16[128,768]{1,0:T(8,128)(2,1)S(1)}, u32[]{:S(2)}, u32[]{:S(2)}) %collective-permute-start.40) | collective-permute-done | bytes 196640 | tf_op jit(solution)/shard_map/ppermute | solution.py:29
  112.6 12.3 %collective-permute-done.39 = bf16[128,768]{1,0:T(8,128)(2,1)S(1)} collective-permute-done((bf16[128,768]{1,0:T(8,128)(2,1)S(1)}, bf16[128,768]{1,0:T(8,128)(2,1)S(1)}, u32[]{:S(2)}, u32[]{:S(2)}) %collective-permute-start.39) | collective-permute-done | bytes 196640 | tf_op jit(solution)/shard_map/ppermute | solution.py:29
  131.7 2.7 %collective-permute-done.42 = f32[512]{0:T(512)S(1)} collective-permute-done((f32[512]{0:T(512)S(1)}, f32[512]{0:T(512)S(1)}, u32[]{:S(2)}, u32[]{:S(2)}) %collective-permute-start.42) | collective-permute-done | bytes 2080 | tf_op jit(solution)/shard_map/ppermute | solution.py:20
  135.9 2.1 %collective-permute-done.43 = f32[512]{0:T(512)S(1)} collective-permute-done((f32[512]{0:T(512)S(1)}, f32[512]{0:T(512)S(1)}, u32[]{:S(2)}, u32[]{:S(2)}) %collective-permute-start.43) | collective-permute-done | bytes 2080 | tf_op jit(solution)/shard_map/ppermute | solution.py:20
  141.6 2.7 %collective-permute-done.45 = f32[512]{0:T(512)S(1)} collective-permute-done((f32[512]{0:T(512)S(1)}, f32[512]{0:T(512)S(1)}, u32[]{:S(2)}, u32[]{:S(2)}) %collective-permute-start.45) | collective-permute-done | bytes 2080 | tf_op jit(solution)/shard_map/ppermute | solution.py:20
  145.9 2.1 %collective-permute-done.46 = f32[512]{0:T(512)S(1)} collective-permute-done((f32[512]{0:T(512)S(1)}, f32[512]{0:T(512)S(1)}, u32[]{:S(2)}, u32[]{:S(2)}) %collective-permute-start.46) | collective-permute-done | bytes 2080 | tf_op jit(solution)/shard_map/ppermute | solution.py:20
  151.6 2.7 %collective-permute-done.48 = f32[512]{0:T(512)S(1)} collective-permute-done((f32[512]{0:T(512)S(1)}, f32[512]{0:T(512)S(1)}, u32[]{:S(2)}, u32[]{:S(2)}) %collective-permute-start.48) | collective-permute-done | bytes 2080 | tf_op jit(solution)/shard_map/ppermute | solution.py:20
  155.9 2.1 %collective-permute-done.49 = f32[512]{0:T(512)S(1)} collective-permute-done((f32[512]{0:T(512)S(1)}, f32[512]{0:T(512)S(1)}, u32[]{:S(2)}, u32[]{:S(2)}) %collective-permute-start.49) | collective-permute-done | bytes 2080 | tf_op jit(solution)/shard_map/ppermute | solution.py:20
  161.4 2.7 %collective-permute-done.51 = f32[128]{0:T(128)S(1)} collective-permute-done((f32[128]{0:T(128)S(1)}, f32[128]{0:T(128)S(1)}, u32[]{:S(2)}, u32[]{:S(2)}) %collective-permute-start.51) | collective-permute-done | bytes 544 | tf_op jit(solution)/shard_map/ppermute | solution.py:20
  165.6 2.0 %collective-permute-done.52 = f32[128]{0:T(128)S(1)} collective-permute-done((f32[128]{0:T(128)S(1)}, f32[128]{0:T(128)S(1)}, u32[]{:S(2)}, u32[]{:S(2)}) %collective-permute-start.52) | collective-permute-done | bytes 544 | tf_op jit(solution)/shard_map/ppermute | solution.py:20
  (210 shorter events, 71.1 us)
Async XLA Ops:
  0.0 39.7 %collective-permute-start.2 = (bf16[128,768]{1,0:T(8,128)(2,1)}, bf16[128,768]{1,0:T(8,128)(2,1)}, u32[]{:S(2)}, u32[]{:S(2)}) collective-permute-start(bf16[128,768]{1,0:T(8,128)(2,1)} %param.6), channel_id=1, source_target_pairs={{0,4},{4,0},{8,12},{12,8},{16,20},{20,16},{24,28},{28,24},{1,5},{5... | collective-permute-start | bytes 589832 | tf_op jit(solution)/shard_map/ppermute | solution.py:20
  0.5 40.6 %collective-permute-start.5 = (bf16[128,768]{1,0:T(8,128)(2,1)}, bf16[128,768]{1,0:T(8,128)(2,1)}, u32[]{:S(2)}, u32[]{:S(2)}) collective-permute-start(bf16[128,768]{1,0:T(8,128)(2,1)} %param.6), channel_id=1, source_target_pairs={{0,8},{4,12},{8,0},{12,4},{16,24},{20,28},{24,16},{28,20},{1,9},{5... | collective-permute-start | bytes 589832 | tf_op jit(solution)/shard_map/ppermute | solution.py:20
  7.7 21.0 %collective-permute-start.1 = (bf16[768,768]{0,1:T(8,128)(2,1)}, bf16[768,768]{0,1:T(8,128)(2,1)}, u32[]{:S(2)}, u32[]{:S(2)}) collective-permute-start(bf16[768,768]{0,1:T(8,128)(2,1)} %bitcast.4), channel_id=1, source_target_pairs={{0,4},{4,0},{8,12},{12,8},{16,20},{20,16},{24,28},{28,24},{1,5},{5... | collective-permute-start | bytes 3538952 | tf_op jit(solution)/shard_map/ppermute | solution.py:20
  8.5 15.4 %collective-permute-start = (s32[4,4]{1,0:T(4,128)}, s32[4,4]{1,0:T(4,128)}, u32[]{:S(2)}, u32[]{:S(2)}) collective-permute-start(s32[4,4]{1,0:T(4,128)} %get-tuple-element.18), channel_id=1, source_target_pairs={{0,4},{4,0},{8,12},{12,8},{16,20},{20,16},{24,28},{28,24},{1,5},{5... | collective-permute-start | bytes 200 | tf_op jit(solution)/shard_map/ppermute | solution.py:20
  8.8 28.4 %collective-permute-start.4 = (bf16[768,768]{1,0:T(8,128)(2,1)}, bf16[768,768]{1,0:T(8,128)(2,1)}, u32[]{:S(2)}, u32[]{:S(2)}) collective-permute-start(bf16[768,768]{1,0:T(8,128)(2,1)} %get-tuple-element.12), channel_id=1, source_target_pairs={{0,8},{4,12},{8,0},{12,4},{16,24},{20,28},{24,16},{28,20},{1,9},{5... | collective-permute-start | bytes 3538952 | tf_op jit(solution)/shard_map/ppermute | solution.py:20
  23.9 13.3 %collective-permute-start.3 = (s32[4,4]{1,0:T(4,128)}, s32[4,4]{1,0:T(4,128)S(1)}, u32[]{:S(2)}, u32[]{:S(2)}) collective-permute-start(s32[4,4]{1,0:T(4,128)} %get-tuple-element.17), channel_id=1, source_target_pairs={{0,8},{4,12},{8,0},{12,4},{16,24},{20,28},{24,16},{28,20},{1,9},{5... | collective-permute-start | bytes 200 | tf_op jit(solution)/shard_map/ppermute | solution.py:20
  42.7 5.4 %collective-permute-start.25 = (bf16[64,768]{1,0:T(8,128)(2,1)S(1)}, bf16[64,768]{1,0:T(8,128)(2,1)S(1)}, u32[]{:S(2)}, u32[]{:S(2)}) collective-permute-start(bf16[64,768]{1,0:T(8,128)(2,1)S(1)} %get-tuple-element.19), channel_id=1, source_target_pairs={{0,8},{4,12},{8,0},{12,4},{16,24},{20,28},{24,16},{28,20},{1,9},{5... | collective-permute-start | bytes 294920 | tf_op jit(solution)/shard_map/ppermute | solution.py:20
  46.1 5.2 %collective-permute-start.7 = (bf16[64,768]{1,0:T(8,128)(2,1)S(1)}, bf16[64,768]{1,0:T(8,128)(2,1)S(1)}, u32[]{:S(2)}, u32[]{:S(2)}) collective-permute-start(bf16[64,768]{1,0:T(8,128)(2,1)S(1)} %get-tuple-element.33), channel_id=1, source_target_pairs={{0,8},{4,12},{8,0},{12,4},{16,24},{20,28},{24,16},{28,20},{1,9},{5... | collective-permute-start | bytes 294920 | tf_op jit(solution)/shard_map/ppermute | solution.py:20
  48.8 8.9 %collective-permute-start.26 = (bf16[64,768]{1,0:T(8,128)(2,1)S(1)}, bf16[64,768]{1,0:T(8,128)(2,1)S(1)}, u32[]{:S(2)}, u32[]{:S(2)}) collective-permute-start(bf16[64,768]{1,0:T(8,128)(2,1)S(1)} %get-tuple-element.21), channel_id=1, source_target_pairs={{0,4},{4,0},{8,12},{12,8},{16,20},{20,16},{24,28},{28,24},{1,5},{5... | collective-permute-start | bytes 294920 | tf_op jit(solution)/shard_map/ppermute | solution.py:20
  48.9 9.1 %collective-permute-start.27 = (bf16[64,768]{1,0:T(8,128)(2,1)S(1)}, bf16[64,768]{1,0:T(8,128)(2,1)S(1)}, u32[]{:S(2)}, u32[]{:S(2)}) collective-permute-start(bf16[64,768]{1,0:T(8,128)(2,1)S(1)} %get-tuple-element.21), channel_id=1, source_target_pairs={{0,8},{4,12},{8,0},{12,4},{16,24},{20,28},{24,16},{28,20},{1,9},{5... | collective-permute-start | bytes 294920 | tf_op jit(solution)/shard_map/ppermute | solution.py:20
  52.0 7.6 %collective-permute-start.12 = (bf16[64,768]{1,0:T(8,128)(2,1)S(1)}, bf16[64,768]{1,0:T(8,128)(2,1)S(1)}, u32[]{:S(2)}, u32[]{:S(2)}) collective-permute-start(bf16[64,768]{1,0:T(8,128)(2,1)S(1)} %convert_element_type.170), channel_id=1, source_target_pairs={{0,4},{4,0},{8,12},{12,8},{16,20},{20,16},{24,28},{28,24},{1,5},{5... | collective-permute-start | bytes 294920 | tf_op jit(solution)/shard_map/ppermute | solution.py:20
  52.0 8.3 %collective-permute-start.13 = (bf16[64,768]{1,0:T(8,128)(2,1)S(1)}, bf16[64,768]{1,0:T(8,128)(2,1)S(1)}, u32[]{:S(2)}, u32[]{:S(2)}) collective-permute-start(bf16[64,768]{1,0:T(8,128)(2,1)S(1)} %convert_element_type.170), channel_id=1, source_target_pairs={{0,8},{4,12},{8,0},{12,4},{16,24},{20,28},{24,16},{28,20},{1,9},{5... | collective-permute-start | bytes 294920 | tf_op jit(solution)/shard_map/ppermute | solution.py:20
  54.2 8.8 %collective-permute-start.10 = (bf16[3,256,128]{2,1,0:T(8,128)(2,1)S(1)}, bf16[3,256,128]{2,1,0:T(8,128)(2,1)S(1)}, u32[]{:S(2)}, u32[]{:S(2)}) collective-permute-start(bf16[3,256,128]{2,1,0:T(8,128)(2,1)S(1)} %slice_select_fusion), channel_id=1, source_target_pairs={{0,3},{1,0},{2,1},{3,2},{4,7},{5,4},{6,5},{7,6},{8,11},{9,8},{10,9... | collective-permute-start | bytes 589832 | tf_op jit(solution)/shard_map/ppermute | solution.py:39
  57.7 17.0 %collective-permute-start.9 = (bf16[3,256,128]{2,1,0:T(8,128)(2,1)S(1)}, bf16[3,256,128]{2,1,0:T(8,128)(2,1)S(1)}, u32[]{:S(2)}, u32[]{:S(2)}) collective-permute-start(bf16[3,256,128]{2,1,0:T(8,128)(2,1)S(1)} %slice_select_fusion), channel_id=1, source_target_pairs={{0,2},{1,3},{2,0},{3,1},{4,6},{5,7},{6,4},{7,5},{8,10},{9,11},{10,... | collective-permute-start | bytes 589832 | tf_op jit(solution)/shard_map/ppermute | solution.py:39
  58.0 16.9 %collective-permute-start.8 = (bf16[3,256,128]{2,1,0:T(8,128)(2,1)S(1)}, bf16[3,256,128]{2,1,0:T(8,128)(2,1)S(1)}, u32[]{:S(2)}, u32[]{:S(2)}) collective-permute-start(bf16[3,256,128]{2,1,0:T(8,128)(2,1)S(1)} %slice_select_fusion), channel_id=1, source_target_pairs={{0,1},{1,2},{2,3},{3,0},{4,5},{5,6},{6,7},{7,4},{8,9},{9,10},{10,1... | collective-permute-start | bytes 589832 | tf_op jit(solution)/shard_map/ppermute | solution.py:39
  59.6 16.9 %collective-permute-start.28 = (bf16[64,768]{1,0:T(8,128)(2,1)S(1)}, bf16[64,768]{1,0:T(8,128)(2,1)S(1)}, u32[]{:S(2)}, u32[]{:S(2)}) collective-permute-start(bf16[64,768]{1,0:T(8,128)(2,1)S(1)} %get-tuple-element.23), channel_id=1, source_target_pairs={{0,4},{4,0},{8,12},{12,8},{16,20},{20,16},{24,28},{28,24},{1,5},{5... | collective-permute-start | bytes 294920 | tf_op jit(solution)/shard_map/ppermute | solution.py:20
  60.4 16.4 %collective-permute-start.29 = (bf16[64,768]{1,0:T(8,128)(2,1)S(1)}, bf16[64,768]{1,0:T(8,128)(2,1)S(1)}, u32[]{:S(2)}, u32[]{:S(2)}) collective-permute-start(bf16[64,768]{1,0:T(8,128)(2,1)S(1)} %get-tuple-element.23), channel_id=1, source_target_pairs={{0,8},{4,12},{8,0},{12,4},{16,24},{20,28},{24,16},{28,20},{1,9},{5... | collective-permute-start | bytes 294920 | tf_op jit(solution)/shard_map/ppermute | solution.py:20
  63.0 16.8 %collective-permute-start.14 = (bf16[64,768]{1,0:T(8,128)(2,1)S(1)}, bf16[64,768]{1,0:T(8,128)(2,1)S(1)}, u32[]{:S(2)}, u32[]{:S(2)}) collective-permute-start(bf16[64,768]{1,0:T(8,128)(2,1)S(1)} %get-tuple-element.35), channel_id=1, source_target_pairs={{0,4},{4,0},{8,12},{12,8},{16,20},{20,16},{24,28},{28,24},{1,5},{5... | collective-permute-start | bytes 294920 | tf_op jit(solution)/shard_map/ppermute | solution.py:20
  74.7 5.5 %collective-permute-start.15 = (bf16[64,768]{1,0:T(8,128)(2,1)S(1)}, bf16[64,768]{1,0:T(8,128)(2,1)S(1)}, u32[]{:S(2)}, u32[]{:S(2)}) collective-permute-start(bf16[64,768]{1,0:T(8,128)(2,1)S(1)} %get-tuple-element.35), channel_id=1, source_target_pairs={{0,8},{4,12},{8,0},{12,4},{16,24},{20,28},{24,16},{28,20},{1,9},{5... | collective-permute-start | bytes 294920 | tf_op jit(solution)/shard_map/ppermute | solution.py:20
  76.5 49.2 %collective-permute-start.11 = (bf16[4,3,256,128]{3,2,1,0:T(8,128)(2,1)}, bf16[4,3,256,128]{3,2,1,0:T(8,128)(2,1)}, u32[]{:S(2)}, u32[]{:S(2)}) collective-permute-start(bf16[4,3,256,128]{3,2,1,0:T(8,128)(2,1)} %get-tuple-element.15), channel_id=1, source_target_pairs={{0,4},{4,0},{8,12},{12,8},{16,20},{20,16},{24,28},{28,24},{1,5},{5... | collective-permute-start | bytes 2359304 | tf_op jit(solution)/shard_map/ppermute | solution.py:20
  80.9 5.4 %collective-permute-start.16 = (bf16[64,768]{1,0:T(8,128)(2,1)S(1)}, bf16[64,768]{1,0:T(8,128)(2,1)S(1)}, u32[]{:S(2)}, u32[]{:S(2)}) collective-permute-start(bf16[64,768]{1,0:T(8,128)(2,1)S(1)} %get-tuple-element.37), channel_id=1, source_target_pairs={{0,4},{4,0},{8,12},{12,8},{16,20},{20,16},{24,28},{28,24},{1,5},{5... | collective-permute-start | bytes 294920 | tf_op jit(solution)/shard_map/ppermute | solution.py:20
  81.1 5.5 %collective-permute-start.17 = (bf16[64,768]{1,0:T(8,128)(2,1)S(1)}, bf16[64,768]{1,0:T(8,128)(2,1)S(1)}, u32[]{:S(2)}, u32[]{:S(2)}) collective-permute-start(bf16[64,768]{1,0:T(8,128)(2,1)S(1)} %get-tuple-element.37), channel_id=1, source_target_pairs={{0,8},{4,12},{8,0},{12,4},{16,24},{20,28},{24,16},{28,20},{1,9},{5... | collective-permute-start | bytes 294920 | tf_op jit(solution)/shard_map/ppermute | solution.py:20
  84.0 5.7 %collective-permute-start.33 = (bf16[64,768]{1,0:T(8,128)(2,1)S(1)}, bf16[64,768]{1,0:T(8,128)(2,1)S(1)}, u32[]{:S(2)}, u32[]{:S(2)}) collective-permute-start(bf16[64,768]{1,0:T(8,128)(2,1)S(1)} %get-tuple-element.27), channel_id=1, source_target_pairs={{0,8},{4,12},{8,0},{12,4},{16,24},{20,28},{24,16},{28,20},{1,9},{5... | collective-permute-start | bytes 294920 | tf_op jit(solution)/shard_map/ppermute | solution.py:20
  87.3 5.3 %collective-permute-start.18 = (bf16[64,768]{1,0:T(8,128)(2,1)S(1)}, bf16[64,768]{1,0:T(8,128)(2,1)S(1)}, u32[]{:S(2)}, u32[]{:S(2)}) collective-permute-start(bf16[64,768]{1,0:T(8,128)(2,1)S(1)} %get-tuple-element.39), channel_id=1, source_target_pairs={{0,4},{4,0},{8,12},{12,8},{16,20},{20,16},{24,28},{28,24},{1,5},{5... | collective-permute-start | bytes 294920 | tf_op jit(solution)/shard_map/ppermute | solution.py:20
  87.5 5.5 %collective-permute-start.19 = (bf16[64,768]{1,0:T(8,128)(2,1)S(1)}, bf16[64,768]{1,0:T(8,128)(2,1)S(1)}, u32[]{:S(2)}, u32[]{:S(2)}) collective-permute-start(bf16[64,768]{1,0:T(8,128)(2,1)S(1)} %get-tuple-element.39), channel_id=1, source_target_pairs={{0,8},{4,12},{8,0},{12,4},{16,24},{20,28},{24,16},{28,20},{1,9},{5... | collective-permute-start | bytes 294920 | tf_op jit(solution)/shard_map/ppermute | solution.py:20
  90.4 5.6 %collective-permute-start.35 = (bf16[64,768]{1,0:T(8,128)(2,1)S(1)}, bf16[64,768]{1,0:T(8,128)(2,1)S(1)}, u32[]{:S(2)}, u32[]{:S(2)}) collective-permute-start(bf16[64,768]{1,0:T(8,128)(2,1)S(1)} %get-tuple-element.29), channel_id=1, source_target_pairs={{0,8},{4,12},{8,0},{12,4},{16,24},{20,28},{24,16},{28,20},{1,9},{5... | collective-permute-start | bytes 294920 | tf_op jit(solution)/shard_map/ppermute | solution.py:20
  93.6 5.3 %collective-permute-start.20 = (bf16[64,768]{1,0:T(8,128)(2,1)S(1)}, bf16[64,768]{1,0:T(8,128)(2,1)S(1)}, u32[]{:S(2)}, u32[]{:S(2)}) collective-permute-start(bf16[64,768]{1,0:T(8,128)(2,1)S(1)} %get-tuple-element.41), channel_id=1, source_target_pairs={{0,4},{4,0},{8,12},{12,8},{16,20},{20,16},{24,28},{28,24},{1,5},{5... | collective-permute-start | bytes 294920 | tf_op jit(solution)/shard_map/ppermute | solution.py:20
  93.9 5.4 %collective-permute-start.21 = (bf16[64,768]{1,0:T(8,128)(2,1)S(1)}, bf16[64,768]{1,0:T(8,128)(2,1)S(1)}, u32[]{:S(2)}, u32[]{:S(2)}) collective-permute-start(bf16[64,768]{1,0:T(8,128)(2,1)S(1)} %get-tuple-element.41), channel_id=1, source_target_pairs={{0,8},{4,12},{8,0},{12,4},{16,24},{20,28},{24,16},{28,20},{1,9},{5... | collective-permute-start | bytes 294920 | tf_op jit(solution)/shard_map/ppermute | solution.py:20
  96.7 5.6 %collective-permute-start.37 = (bf16[64,768]{1,0:T(8,128)(2,1)S(1)}, bf16[64,768]{1,0:T(8,128)(2,1)S(1)}, u32[]{:S(2)}, u32[]{:S(2)}) collective-permute-start(bf16[64,768]{1,0:T(8,128)(2,1)S(1)} %get-tuple-element.31), channel_id=1, source_target_pairs={{0,8},{4,12},{8,0},{12,4},{16,24},{20,28},{24,16},{28,20},{1,9},{5... | collective-permute-start | bytes 294920 | tf_op jit(solution)/shard_map/ppermute | solution.py:20
  105.6 6.9 %collective-permute-start.40 = (bf16[128,768]{1,0:T(8,128)(2,1)S(1)}, bf16[128,768]{1,0:T(8,128)(2,1)S(1)}, u32[]{:S(2)}, u32[]{:S(2)}) collective-permute-start(bf16[128,768]{1,0:T(8,128)(2,1)S(1)} %pad_maximum_fusion.5), channel_id=1, source_target_pairs={{0,3},{1,0},{2,1},{3,2},{4,7},{5,4},{6,5},{7,6},{8,11},{9,8},{10,9... | collective-permute-start | bytes 589832 | tf_op jit(solution)/shard_map/ppermute | solution.py:29
  106.0 18.9 %collective-permute-start.39 = (bf16[128,768]{1,0:T(8,128)(2,1)S(1)}, bf16[128,768]{1,0:T(8,128)(2,1)S(1)}, u32[]{:S(2)}, u32[]{:S(2)}) collective-permute-start(bf16[128,768]{1,0:T(8,128)(2,1)S(1)} %pad_maximum_fusion.5), channel_id=1, source_target_pairs={{0,2},{1,3},{2,0},{3,1},{4,6},{5,7},{6,4},{7,5},{8,10},{9,11},{10,... | collective-permute-start | bytes 589832 | tf_op jit(solution)/shard_map/ppermute | solution.py:29
  107.5 17.4 %collective-permute-start.38 = (bf16[128,768]{1,0:T(8,128)(2,1)S(1)}, bf16[128,768]{1,0:T(8,128)(2,1)S(1)}, u32[]{:S(2)}, u32[]{:S(2)}) collective-permute-start(bf16[128,768]{1,0:T(8,128)(2,1)S(1)} %pad_maximum_fusion.5), channel_id=1, source_target_pairs={{0,1},{1,2},{2,3},{3,0},{4,5},{5,6},{6,7},{7,4},{8,9},{9,10},{10,1... | collective-permute-start | bytes 589832 | tf_op jit(solution)/shard_map/ppermute | solution.py:29
  (33 other events, 94.9 us)

commit v16 on v14

--- a/solution.py
+++ b/solution.py
@@ -113,6 +113,9 @@
         for degree_index in range(1, DEGREE):
             if degree_index == GATHER_AT:
                 current = hook(current)
+            if degree_index == DEGREE - 1 and gathered:
+                settled, current = lax.optimization_barrier((gathered[0], current))
+                gathered[0] = settled
             applied = apply_operator(current.astype(jnp.bfloat16))
             following = 2.0 * (applied - filter_center * current) / filter_half - previous
             previous, current = (current, following)

time: 166 us -> 166 us (level)
  waiting for transfers between devices: 52.4 us -> 57.8 us
  starting transfers between devices: 46.1 us -> 43.4 us
  local copies, waits for them, and re-layouts: 17.7 us -> 15.6 us
    ppermute x3, waiting for transfers between devices: 0.01 us -> 3.54 us  [gather_pieces(): pieces.append(lax.ppermute(value, 'bands', pairs))]
    ppermute x49, starting transfers between devices: 34.4 us -> 31.2 us  [swapped(): return lax.ppermute(value, axis, pairs)]
    ppermute x49, waiting for transfers between devices: 39.6 us -> 41.6 us  [swapped(): return lax.ppermute(value, axis, pairs)]
  transfers between devices with their start and end apart: 55 -> 55, of which waited for: 22 -> 25; matrix products, arithmetic and copies ran while one was open for 32% -> 30% of each run, Pallas kernels for 0% -> 0%
where the time goes in v16:
time: 166 us; the launch traced here: 163 us
  waiting for transfers between devices  57.8 us (35%)
  starting transfers between devices  43.4 us (26%)
  matrix products  36.1 us (22%)
  local copies, waits for them, and re-layouts  15.6 us (9%)
  other arithmetic  9.9 us (6%)
    ppermute x49, waiting for transfers between devices, swapped(): return lax.ppermute(value, axis, pairs)  41.6 us
    ppermute x49, starting transfers between devices, swapped(): return lax.ppermute(value, axis, pairs)  31.2 us
    dot_general x32, matrix products, apply_operator(): jnp.dot(other_rows, other_pair[round_index], preferred_element_type=jnp.f...  14.5 us
    ppermute x3, waiting for transfers between devices, gather_bands(): pieces.append(lax.ppermute(value, 'bands', pairs))  12.6 us
    dot_general x4, matrix products, pattern_mask(): lax.dot_general(per_row.astype(jnp.bfloat16), col_onehot, (((1,), (1,)),...  9.97 us
    dot_general x16, matrix products, apply_operator(): result = jnp.dot(values, diag_sym, preferred_element_type=jnp.float32)  6.62 us
    ppermute x3, starting transfers between devices, gather_bands(): pieces.append(lax.ppermute(value, 'bands', pairs))  6.36 us
    ppermute x3, starting transfers between devices, gather_pieces(): pieces.append(lax.ppermute(value, 'bands', pairs))  5.8 us
  transfers between devices with their start and end apart: 55, of which 25 were waited for; matrix products, arithmetic and copies ran while one was open for 30% of the time, Pallas kernels for 0%

profile of v16, /device:TPU:0, one launch (start us, length us, event | category | flops | bytes accessed | tf_op | source)
XLA Modules:
  0.0 163.5 jit_solution(11398678838246822374)
XLA Ops:
  0.0 1.6 fusion.110
  2.1 2.5 %collective-permute-start.5 = (bf16[64,768]{1,0:T(8,128)(2,1)}, bf16[64,768]{1,0:T(8,128)(2,1)}, u32[]{:S(2)}, u32[]{:S(2)}) collective-permute-start(bf16[64,768]{1,0:T(8,128)(2,1)} %get-tuple-element.25), channel_id=1, source_target_pairs={{0,8},{4,12},{8,0},{12,4},{16,24},{20,28},{24,16},{28,20},{1,9},{5... | collective-permute-start | bytes 294920 | tf_op jit(solution)/shard_map/ppermute | solution.py:20
  6.1 3.3 %slice_bitcast_fusion.1 = (bf16[768,768]{1,0:T(8,128)(2,1)}, bf16[768,768]{0,1:T(8,128)(2,1)}, bf16[1,768,768]{2,1,0:T(8,128)(2,1)S(1)}) fusion(bf16[2,768,768]{2,1,0:T(8,128)(2,1)} %param.8), kind=kLoop, calls=%fused_computation.109 | loop fusion | bytes 5898240 | tf_op jit(solution)/shard_map/squeeze | solution.py:74
  12.5 1.6 convert_bitcast_fusion
  14.1 2.0 %copy.12 = f32[768,768]{1,0:T(8,128)S(1)} copy(f32[768,768]{0,1:T(8,128)} %convert_bitcast_fusion) | data formatting | bytes 4718592 | tf_op jit(solution)/shard_map/convert_element_type | solution.py:85
  16.3 2.3 %fusion.1 = bf16[768,768]{1,0:T(8,128)(2,1)S(1)} fusion(bf16[768,768]{1,0:T(8,128)(2,1)} %param.7, f32[768,768]{1,0:T(8,128)S(1)} %copy.12, s32[768]{0:T(1024)S(1)} %get-tuple-element.54), kind=kLoop, calls=%fused_computation.6 | loop fusion | flops 7667712 | bytes 4721664 | tf_op jit(solution)/shard_map/convert_element_type | solution.py:86
  21.1 3.0 %compare_select_fusion.2 = bf16[768,768]{1,0:T(8,128)(2,1)} fusion(bf16[1,768,768]{1,2,0:T(8,128)(2,1)} %copy.17, s32[768]{0:T(1024)S(1)} %get-tuple-element.54, s32[768]{0:T(1024)S(1)} %convert_reduce_fusion.1, s32[2,4,4]{2,1,0:T(4,128)S(1)} %copy-done.10), kind=kOutput, calls=%fused_computation.12 | convolution fusion | flops 5932048 | bytes 2369536 | tf_op jit(solution)/shard_map/dot_general | solution.py:63
  25.2 1.8 %compare_select_fusion = bf16[768,768]{1,0:T(8,128)(2,1)} fusion(bf16[768,768]{1,0:T(8,128)(2,1)S(1)} %copy.15, s32[768]{0:T(1024)S(1)} %get-tuple-element.53, s32[768]{0:T(1024)S(1)} %get-tuple-element.54, s32[2,4,4]{2,1,0:T(4,128)S(1)} %copy-done.10), kind=kOutput, calls=%fused_computation.10 | convolution fusion | flops 5932048 | bytes 2369536 | tf_op jit(solution)/shard_map/dot_general | solution.py:63
  27.0 2.0 %collective-permute-start.3 = (s32[4,4]{1,0:T(4,128)}, s32[4,4]{1,0:T(4,128)S(1)}, u32[]{:S(2)}, u32[]{:S(2)}) collective-permute-start(s32[4,4]{1,0:T(4,128)} %get-tuple-element.27), channel_id=1, source_target_pairs={{0,8},{4,12},{8,0},{12,4},{16,24},{20,28},{24,16},{28,20},{1,9},{5... | collective-permute-start | bytes 200 | tf_op jit(solution)/shard_map/ppermute | solution.py:20
  29.0 2.8 %fusion.3 = f32[768,768]{1,0:T(8,128)} fusion(s32[768]{0:T(1024)S(1)} %get-tuple-element.54, s32[768]{0:T(1024)S(1)} %convert_reduce_fusion.1, s32[4,4]{1,0:T(4,128)} %collective-permute-done), kind=kOutput, calls=%fused_computation.27 | convolution fusion | flops 4752400 | bytes 2365504 | tf_op jit(solution)/shard_map/dot_general | solution.py:63
  33.4 2.5 %add_convert_fusion.1 = bf16[768,768]{1,0:T(8,128)(2,1)S(1)} fusion(bf16[768,768]{1,0:T(8,128)(2,1)} %compare_select_fusion.2, bf16[768,768]{1,0:T(8,128)(2,1)S(1)} %copy.14, f32[768,768]{1,0:T(8,128)} %fusion.3), kind=kLoop, calls=%fused_computation.9 | loop fusion | flops 3538944 | bytes 5898240 | tf_op jit(solution)/shard_map/convert_element_type | solution.py:98
  35.8 3.8 %collective-permute-done.3 = s32[4,4]{1,0:T(4,128)S(1)} collective-permute-done((s32[4,4]{1,0:T(4,128)}, s32[4,4]{1,0:T(4,128)S(1)}, u32[]{:S(2)}, u32[]{:S(2)}) %collective-permute-start.3) | collective-permute-done | bytes 96 | tf_op jit(solution)/shard_map/ppermute | solution.py:20
  39.9 2.4 %add_convert_fusion = bf16[768,768]{1,0:T(8,128)(2,1)S(1)} fusion(bf16[768,768]{1,0:T(8,128)(2,1)} %compare_select_fusion, bf16[768,768]{1,0:T(8,128)(2,1)} %collective-permute-done.4, s32[768]{0:T(1024)S(1)} %get-tuple-element.53, s32[768]{0:T(1024)S(1)} %get-tuple-element.54, s32[4,4]{1,0:T(4,128)S(1)} %collective-permute-done.3), kind=kOutput, calls=%fused_computation.8 | convolution fusion | flops 8291344 | bytes 3545152 | tf_op jit(solution)/shard_map/dot_general | solution.py:63
  45.3 1.8 %collective-permute-start.7 = (bf16[64,768]{1,0:T(8,128)(2,1)S(1)}, bf16[64,768]{1,0:T(8,128)(2,1)S(1)}, u32[]{:S(2)}, u32[]{:S(2)}) collective-permute-start(bf16[64,768]{1,0:T(8,128)(2,1)S(1)} %get-tuple-element.39), channel_id=1, source_target_pairs={{0,8},{4,12},{8,0},{12,4},{16,24},{20,28},{24,16},{28,20},{1,9},{5... | collective-permute-start | bytes 294920 | tf_op jit(solution)/shard_map/ppermute | solution.py:20
  53.3 1.6 collective-permute-start.8
  55.0 2.6 %collective-permute-start.9 = (bf16[3,256,128]{2,1,0:T(8,128)(2,1)S(1)}, bf16[3,256,128]{2,1,0:T(8,128)(2,1)S(1)}, u32[]{:S(2)}, u32[]{:S(2)}) collective-permute-start(bf16[3,256,128]{2,1,0:T(8,128)(2,1)S(1)} %slice_select_fusion), channel_id=1, source_target_pairs={{0,2},{1,3},{2,0},{3,1},{4,6},{5,7},{6,4},{7,5},{8,10},{9,11},{10,... | collective-permute-start | bytes 589832 | tf_op jit(solution)/shard_map/ppermute | solution.py:39
  62.6 3.3 %collective-permute-done.27 = bf16[64,768]{1,0:T(8,128)(2,1)S(1)} collective-permute-done((bf16[64,768]{1,0:T(8,128)(2,1)S(1)}, bf16[64,768]{1,0:T(8,128)(2,1)S(1)}, u32[]{:S(2)}, u32[]{:S(2)}) %collective-permute-start.27) | collective-permute-done | bytes 98336 | tf_op jit(solution)/shard_map/ppermute | solution.py:20
  67.2 3.5 %collective-permute-done.9 = bf16[3,256,128]{2,1,0:T(8,128)(2,1)S(1)} collective-permute-done((bf16[3,256,128]{2,1,0:T(8,128)(2,1)S(1)}, bf16[3,256,128]{2,1,0:T(8,128)(2,1)S(1)}, u32[]{:S(2)}, u32[]{:S(2)}) %collective-permute-start.9) | collective-permute-done | bytes 196640 | tf_op jit(solution)/shard_map/ppermute | solution.py:39
  91.0 2.3 %collective-permute-done.35 = bf16[64,768]{1,0:T(8,128)(2,1)S(1)} collective-permute-done((bf16[64,768]{1,0:T(8,128)(2,1)S(1)}, bf16[64,768]{1,0:T(8,128)(2,1)S(1)}, u32[]{:S(2)}, u32[]{:S(2)}) %collective-permute-start.35) | collective-permute-done | bytes 98336 | tf_op jit(solution)/shard_map/ppermute | solution.py:20
  97.2 2.6 %collective-permute-done.37 = bf16[64,768]{1,0:T(8,128)(2,1)S(1)} collective-permute-done((bf16[64,768]{1,0:T(8,128)(2,1)S(1)}, bf16[64,768]{1,0:T(8,128)(2,1)S(1)}, u32[]{:S(2)}, u32[]{:S(2)}) %collective-permute-start.37) | collective-permute-done | bytes 98336 | tf_op jit(solution)/shard_map/ppermute | solution.py:20
  101.9 3.3 %collective-permute-start.40 = (bf16[128,768]{1,0:T(8,128)(2,1)S(1)}, bf16[128,768]{1,0:T(8,128)(2,1)S(1)}, u32[]{:S(2)}, u32[]{:S(2)}) collective-permute-start(bf16[128,768]{1,0:T(8,128)(2,1)S(1)} %pad_maximum_fusion.5), channel_id=1, source_target_pairs={{0,1},{1,2},{2,3},{3,0},{4,5},{5,6},{6,7},{7,4},{8,9},{9,10},{10,1... | collective-permute-start | bytes 589832 | tf_op jit(solution)/shard_map/ppermute | solution.py:29
  105.2 3.0 %collective-permute-start.41 = (bf16[128,768]{1,0:T(8,128)(2,1)S(1)}, bf16[128,768]{1,0:T(8,128)(2,1)S(1)}, u32[]{:S(2)}, u32[]{:S(2)}) collective-permute-start(bf16[128,768]{1,0:T(8,128)(2,1)S(1)} %pad_maximum_fusion.5), channel_id=1, source_target_pairs={{0,2},{1,3},{2,0},{3,1},{4,6},{5,7},{6,4},{7,5},{8,10},{9,11},{10,... | collective-permute-start | bytes 589832 | tf_op jit(solution)/shard_map/ppermute | solution.py:29
  108.3 5.3 %collective-permute-done.40 = bf16[128,768]{1,0:T(8,128)(2,1)S(1)} collective-permute-done((bf16[128,768]{1,0:T(8,128)(2,1)S(1)}, bf16[128,768]{1,0:T(8,128)(2,1)S(1)}, u32[]{:S(2)}, u32[]{:S(2)}) %collective-permute-start.40) | collective-permute-done | bytes 196640 | tf_op jit(solution)/shard_map/ppermute | solution.py:29
  113.6 7.4 %collective-permute-done.41 = bf16[128,768]{1,0:T(8,128)(2,1)S(1)} collective-permute-done((bf16[128,768]{1,0:T(8,128)(2,1)S(1)}, bf16[128,768]{1,0:T(8,128)(2,1)S(1)}, u32[]{:S(2)}, u32[]{:S(2)}) %collective-permute-start.41) | collective-permute-done | bytes 196640 | tf_op jit(solution)/shard_map/ppermute | solution.py:29
  126.4 2.9 %collective-permute-done.44 = f32[512]{0:T(512)S(1)} collective-permute-done((f32[512]{0:T(512)S(1)}, f32[512]{0:T(512)S(1)}, u32[]{:S(2)}, u32[]{:S(2)}) %collective-permute-start.44) | collective-permute-done | bytes 2080 | tf_op jit(solution)/shard_map/ppermute | solution.py:20
  130.8 2.1 %collective-permute-done.45 = f32[512]{0:T(512)S(1)} collective-permute-done((f32[512]{0:T(512)S(1)}, f32[512]{0:T(512)S(1)}, u32[]{:S(2)}, u32[]{:S(2)}) %collective-permute-start.45) | collective-permute-done | bytes 2080 | tf_op jit(solution)/shard_map/ppermute | solution.py:20
  136.4 2.9 %collective-permute-done.47 = f32[512]{0:T(512)S(1)} collective-permute-done((f32[512]{0:T(512)S(1)}, f32[512]{0:T(512)S(1)}, u32[]{:S(2)}, u32[]{:S(2)}) %collective-permute-start.47) | collective-permute-done | bytes 2080 | tf_op jit(solution)/shard_map/ppermute | solution.py:20
  140.7 2.1 %collective-permute-done.48 = f32[512]{0:T(512)S(1)} collective-permute-done((f32[512]{0:T(512)S(1)}, f32[512]{0:T(512)S(1)}, u32[]{:S(2)}, u32[]{:S(2)}) %collective-permute-start.48) | collective-permute-done | bytes 2080 | tf_op jit(solution)/shard_map/ppermute | solution.py:20
  146.3 2.9 %collective-permute-done.50 = f32[512]{0:T(512)S(1)} collective-permute-done((f32[512]{0:T(512)S(1)}, f32[512]{0:T(512)S(1)}, u32[]{:S(2)}, u32[]{:S(2)}) %collective-permute-start.50) | collective-permute-done | bytes 2080 | tf_op jit(solution)/shard_map/ppermute | solution.py:20
  150.7 2.1 %collective-permute-done.51 = f32[512]{0:T(512)S(1)} collective-permute-done((f32[512]{0:T(512)S(1)}, f32[512]{0:T(512)S(1)}, u32[]{:S(2)}, u32[]{:S(2)}) %collective-permute-start.51) | collective-permute-done | bytes 2080 | tf_op jit(solution)/shard_map/ppermute | solution.py:20
  156.2 2.8 %collective-permute-done.53 = f32[128]{0:T(128)S(1)} collective-permute-done((f32[128]{0:T(128)S(1)}, f32[128]{0:T(128)S(1)}, u32[]{:S(2)}, u32[]{:S(2)}) %collective-permute-start.53) | collective-permute-done | bytes 544 | tf_op jit(solution)/shard_map/ppermute | solution.py:20
  160.5 2.0 %collective-permute-done.54 = f32[128]{0:T(128)S(1)} collective-permute-done((f32[128]{0:T(128)S(1)}, f32[128]{0:T(128)S(1)}, u32[]{:S(2)}, u32[]{:S(2)}) %collective-permute-start.54) | collective-permute-done | bytes 544 | tf_op jit(solution)/shard_map/ppermute | solution.py:20
  (219 shorter events, 74.6 us)
Async XLA Ops:
  1.6 40.6 %collective-permute-start.2 = (bf16[64,768]{1,0:T(8,128)(2,1)}, bf16[64,768]{1,0:T(8,128)(2,1)}, u32[]{:S(2)}, u32[]{:S(2)}) collective-permute-start(bf16[64,768]{1,0:T(8,128)(2,1)} %get-tuple-element.25), channel_id=1, source_target_pairs={{0,4},{4,0},{8,12},{12,8},{16,20},{20,16},{24,28},{28,24},{1,5},{5... | collective-permute-start | bytes 294920 | tf_op jit(solution)/shard_map/ppermute | solution.py:20
  2.1 41.5 %collective-permute-start.5 = (bf16[64,768]{1,0:T(8,128)(2,1)}, bf16[64,768]{1,0:T(8,128)(2,1)}, u32[]{:S(2)}, u32[]{:S(2)}) collective-permute-start(bf16[64,768]{1,0:T(8,128)(2,1)} %get-tuple-element.25), channel_id=1, source_target_pairs={{0,8},{4,12},{8,0},{12,4},{16,24},{20,28},{24,16},{28,20},{1,9},{5... | collective-permute-start | bytes 294920 | tf_op jit(solution)/shard_map/ppermute | solution.py:20
  5.8 21.1 %collective-permute-start = (s32[4,4]{1,0:T(4,128)}, s32[4,4]{1,0:T(4,128)}, u32[]{:S(2)}, u32[]{:S(2)}) collective-permute-start(s32[4,4]{1,0:T(4,128)} %get-tuple-element.28), channel_id=1, source_target_pairs={{0,4},{4,0},{8,12},{12,8},{16,20},{20,16},{24,28},{28,24},{1,5},{5... | collective-permute-start | bytes 200 | tf_op jit(solution)/shard_map/ppermute | solution.py:20
  10.8 20.9 %collective-permute-start.1 = (bf16[768,768]{0,1:T(8,128)(2,1)}, bf16[768,768]{0,1:T(8,128)(2,1)}, u32[]{:S(2)}, u32[]{:S(2)}) collective-permute-start(bf16[768,768]{0,1:T(8,128)(2,1)} %bitcast.4), channel_id=1, source_target_pairs={{0,4},{4,0},{8,12},{12,8},{16,20},{20,16},{24,28},{28,24},{1,5},{5... | collective-permute-start | bytes 3538952 | tf_op jit(solution)/shard_map/ppermute | solution.py:20
  11.1 28.7 %collective-permute-start.4 = (bf16[768,768]{1,0:T(8,128)(2,1)}, bf16[768,768]{1,0:T(8,128)(2,1)}, u32[]{:S(2)}, u32[]{:S(2)}) collective-permute-start(bf16[768,768]{1,0:T(8,128)(2,1)} %get-tuple-element.20), channel_id=1, source_target_pairs={{0,8},{4,12},{8,0},{12,4},{16,24},{20,28},{24,16},{28,20},{1,9},{5... | collective-permute-start | bytes 3538952 | tf_op jit(solution)/shard_map/ppermute | solution.py:20
  27.0 12.6 %collective-permute-start.3 = (s32[4,4]{1,0:T(4,128)}, s32[4,4]{1,0:T(4,128)S(1)}, u32[]{:S(2)}, u32[]{:S(2)}) collective-permute-start(s32[4,4]{1,0:T(4,128)} %get-tuple-element.27), channel_id=1, source_target_pairs={{0,8},{4,12},{8,0},{12,4},{16,24},{20,28},{24,16},{28,20},{1,9},{5... | collective-permute-start | bytes 200 | tf_op jit(solution)/shard_map/ppermute | solution.py:20
  31.8 15.3 %collective-permute-start.22 = (bf16[64,768]{1,0:T(8,128)(2,1)}, bf16[64,768]{1,0:T(8,128)(2,1)}, u32[]{:S(2)}, u32[]{:S(2)}) collective-permute-start(bf16[64,768]{1,0:T(8,128)(2,1)} %get-tuple-element.26), channel_id=1, source_target_pairs={{0,4},{4,0},{8,12},{12,8},{16,20},{20,16},{24,28},{28,24},{1,5},{5... | collective-permute-start | bytes 294920 | tf_op jit(solution)/shard_map/ppermute | solution.py:20
  39.6 8.7 %collective-permute-start.23 = (bf16[64,768]{1,0:T(8,128)(2,1)}, bf16[64,768]{1,0:T(8,128)(2,1)}, u32[]{:S(2)}, u32[]{:S(2)}) collective-permute-start(bf16[64,768]{1,0:T(8,128)(2,1)} %get-tuple-element.26), channel_id=1, source_target_pairs={{0,8},{4,12},{8,0},{12,4},{16,24},{20,28},{24,16},{28,20},{1,9},{5... | collective-permute-start | bytes 294920 | tf_op jit(solution)/shard_map/ppermute | solution.py:20
  45.2 5.3 %collective-permute-start.6 = (bf16[64,768]{1,0:T(8,128)(2,1)S(1)}, bf16[64,768]{1,0:T(8,128)(2,1)S(1)}, u32[]{:S(2)}, u32[]{:S(2)}) collective-permute-start(bf16[64,768]{1,0:T(8,128)(2,1)S(1)} %get-tuple-element.39), channel_id=1, source_target_pairs={{0,4},{4,0},{8,12},{12,8},{16,20},{20,16},{24,28},{28,24},{1,5},{5... | collective-permute-start | bytes 294920 | tf_op jit(solution)/shard_map/ppermute | solution.py:20
  45.3 5.5 %collective-permute-start.7 = (bf16[64,768]{1,0:T(8,128)(2,1)S(1)}, bf16[64,768]{1,0:T(8,128)(2,1)S(1)}, u32[]{:S(2)}, u32[]{:S(2)}) collective-permute-start(bf16[64,768]{1,0:T(8,128)(2,1)S(1)} %get-tuple-element.39), channel_id=1, source_target_pairs={{0,8},{4,12},{8,0},{12,4},{16,24},{20,28},{24,16},{28,20},{1,9},{5... | collective-permute-start | bytes 294920 | tf_op jit(solution)/shard_map/ppermute | solution.py:20
  49.9 5.1 %collective-permute-start.24 = (bf16[64,768]{1,0:T(8,128)(2,1)S(1)}, bf16[64,768]{1,0:T(8,128)(2,1)S(1)}, u32[]{:S(2)}, u32[]{:S(2)}) collective-permute-start(bf16[64,768]{1,0:T(8,128)(2,1)S(1)} %get-tuple-element.29), channel_id=1, source_target_pairs={{0,4},{4,0},{8,12},{12,8},{16,20},{20,16},{24,28},{28,24},{1,5},{5... | collective-permute-start | bytes 294920 | tf_op jit(solution)/shard_map/ppermute | solution.py:20
  50.1 7.8 %collective-permute-start.25 = (bf16[64,768]{1,0:T(8,128)(2,1)S(1)}, bf16[64,768]{1,0:T(8,128)(2,1)S(1)}, u32[]{:S(2)}, u32[]{:S(2)}) collective-permute-start(bf16[64,768]{1,0:T(8,128)(2,1)S(1)} %get-tuple-element.29), channel_id=1, source_target_pairs={{0,8},{4,12},{8,0},{12,4},{16,24},{20,28},{24,16},{28,20},{1,9},{5... | collective-permute-start | bytes 294920 | tf_op jit(solution)/shard_map/ppermute | solution.py:20
  51.5 8.7 %collective-permute-start.12 = (bf16[64,768]{1,0:T(8,128)(2,1)S(1)}, bf16[64,768]{1,0:T(8,128)(2,1)S(1)}, u32[]{:S(2)}, u32[]{:S(2)}) collective-permute-start(bf16[64,768]{1,0:T(8,128)(2,1)S(1)} %convert_element_type.170), channel_id=1, source_target_pairs={{0,4},{4,0},{8,12},{12,8},{16,20},{20,16},{24,28},{28,24},{1,5},{5... | collective-permute-start | bytes 294920 | tf_op jit(solution)/shard_map/ppermute | solution.py:20
  51.7 8.9 %collective-permute-start.13 = (bf16[64,768]{1,0:T(8,128)(2,1)S(1)}, bf16[64,768]{1,0:T(8,128)(2,1)S(1)}, u32[]{:S(2)}, u32[]{:S(2)}) collective-permute-start(bf16[64,768]{1,0:T(8,128)(2,1)S(1)} %convert_element_type.170), channel_id=1, source_target_pairs={{0,8},{4,12},{8,0},{12,4},{16,24},{20,28},{24,16},{28,20},{1,9},{5... | collective-permute-start | bytes 294920 | tf_op jit(solution)/shard_map/ppermute | solution.py:20
  53.3 13.8 %collective-permute-start.8 = (bf16[3,256,128]{2,1,0:T(8,128)(2,1)S(1)}, bf16[3,256,128]{2,1,0:T(8,128)(2,1)S(1)}, u32[]{:S(2)}, u32[]{:S(2)}) collective-permute-start(bf16[3,256,128]{2,1,0:T(8,128)(2,1)S(1)} %slice_select_fusion), channel_id=1, source_target_pairs={{0,1},{1,2},{2,3},{3,0},{4,5},{5,6},{6,7},{7,4},{8,9},{9,10},{10,1... | collective-permute-start | bytes 589832 | tf_op jit(solution)/shard_map/ppermute | solution.py:39
  55.0 15.8 %collective-permute-start.9 = (bf16[3,256,128]{2,1,0:T(8,128)(2,1)S(1)}, bf16[3,256,128]{2,1,0:T(8,128)(2,1)S(1)}, u32[]{:S(2)}, u32[]{:S(2)}) collective-permute-start(bf16[3,256,128]{2,1,0:T(8,128)(2,1)S(1)} %slice_select_fusion), channel_id=1, source_target_pairs={{0,2},{1,3},{2,0},{3,1},{4,6},{5,7},{6,4},{7,5},{8,10},{9,11},{10,... | collective-permute-start | bytes 589832 | tf_op jit(solution)/shard_map/ppermute | solution.py:39
  57.9 13.4 %collective-permute-start.10 = (bf16[3,256,128]{2,1,0:T(8,128)(2,1)S(1)}, bf16[3,256,128]{2,1,0:T(8,128)(2,1)S(1)}, u32[]{:S(2)}, u32[]{:S(2)}) collective-permute-start(bf16[3,256,128]{2,1,0:T(8,128)(2,1)S(1)} %slice_select_fusion), channel_id=1, source_target_pairs={{0,3},{1,0},{2,1},{3,2},{4,7},{5,4},{6,5},{7,6},{8,11},{9,8},{10,9... | collective-permute-start | bytes 589832 | tf_op jit(solution)/shard_map/ppermute | solution.py:39
  60.6 5.3 %collective-permute-start.27 = (bf16[64,768]{1,0:T(8,128)(2,1)S(1)}, bf16[64,768]{1,0:T(8,128)(2,1)S(1)}, u32[]{:S(2)}, u32[]{:S(2)}) collective-permute-start(bf16[64,768]{1,0:T(8,128)(2,1)S(1)} %get-tuple-element.31), channel_id=1, source_target_pairs={{0,8},{4,12},{8,0},{12,4},{16,24},{20,28},{24,16},{28,20},{1,9},{5... | collective-permute-start | bytes 294920 | tf_op jit(solution)/shard_map/ppermute | solution.py:20
  61.6 10.5 %collective-permute-start.14 = (bf16[64,768]{1,0:T(8,128)(2,1)S(1)}, bf16[64,768]{1,0:T(8,128)(2,1)S(1)}, u32[]{:S(2)}, u32[]{:S(2)}) collective-permute-start(bf16[64,768]{1,0:T(8,128)(2,1)S(1)} %get-tuple-element.41), channel_id=1, source_target_pairs={{0,4},{4,0},{8,12},{12,8},{16,20},{20,16},{24,28},{28,24},{1,5},{5... | collective-permute-start | bytes 294920 | tf_op jit(solution)/shard_map/ppermute | solution.py:20
  65.9 6.5 %collective-permute-start.15 = (bf16[64,768]{1,0:T(8,128)(2,1)S(1)}, bf16[64,768]{1,0:T(8,128)(2,1)S(1)}, u32[]{:S(2)}, u32[]{:S(2)}) collective-permute-start(bf16[64,768]{1,0:T(8,128)(2,1)S(1)} %get-tuple-element.41), channel_id=1, source_target_pairs={{0,8},{4,12},{8,0},{12,4},{16,24},{20,28},{24,16},{28,20},{1,9},{5... | collective-permute-start | bytes 294920 | tf_op jit(solution)/shard_map/ppermute | solution.py:20
  67.1 8.0 %collective-permute-start.28 = (bf16[64,768]{1,0:T(8,128)(2,1)S(1)}, bf16[64,768]{1,0:T(8,128)(2,1)S(1)}, u32[]{:S(2)}, u32[]{:S(2)}) collective-permute-start(bf16[64,768]{1,0:T(8,128)(2,1)S(1)} %get-tuple-element.33), channel_id=1, source_target_pairs={{0,4},{4,0},{8,12},{12,8},{16,20},{20,16},{24,28},{28,24},{1,5},{5... | collective-permute-start | bytes 294920 | tf_op jit(solution)/shard_map/ppermute | solution.py:20
  72.0 21.7 %collective-permute-start.11 = (bf16[4,3,256,128]{3,2,1,0:T(8,128)(2,1)S(1)}, bf16[4,3,256,128]{3,2,1,0:T(8,128)(2,1)S(1)}, u32[]{:S(2)}, u32[]{:S(2)}) collective-permute-start(bf16[4,3,256,128]{3,2,1,0:T(8,128)(2,1)S(1)} %get-tuple-element.23), channel_id=1, source_target_pairs={{0,4},{4,0},{8,12},{12,8},{16,20},{20,16},{24,28},{28,24},{1,5},{5... | collective-permute-start | bytes 2359304 | tf_op jit(solution)/shard_map/ppermute | solution.py:20
  76.2 5.2 %collective-permute-start.31 = (bf16[64,768]{1,0:T(8,128)(2,1)S(1)}, bf16[64,768]{1,0:T(8,128)(2,1)S(1)}, u32[]{:S(2)}, u32[]{:S(2)}) collective-permute-start(bf16[64,768]{1,0:T(8,128)(2,1)S(1)} %get-tuple-element.35), channel_id=1, source_target_pairs={{0,8},{4,12},{8,0},{12,4},{16,24},{20,28},{24,16},{28,20},{1,9},{5... | collective-permute-start | bytes 294920 | tf_op jit(solution)/shard_map/ppermute | solution.py:20
  79.2 5.2 %collective-permute-start.19 = (bf16[64,768]{1,0:T(8,128)(2,1)S(1)}, bf16[64,768]{1,0:T(8,128)(2,1)S(1)}, u32[]{:S(2)}, u32[]{:S(2)}) collective-permute-start(bf16[64,768]{1,0:T(8,128)(2,1)S(1)} %get-tuple-element.45), channel_id=1, source_target_pairs={{0,8},{4,12},{8,0},{12,4},{16,24},{20,28},{24,16},{28,20},{1,9},{5... | collective-permute-start | bytes 294920 | tf_op jit(solution)/shard_map/ppermute | solution.py:20
  82.2 5.2 %collective-permute-start.33 = (bf16[64,768]{1,0:T(8,128)(2,1)S(1)}, bf16[64,768]{1,0:T(8,128)(2,1)S(1)}, u32[]{:S(2)}, u32[]{:S(2)}) collective-permute-start(bf16[64,768]{1,0:T(8,128)(2,1)S(1)} %get-tuple-element.37), channel_id=1, source_target_pairs={{0,8},{4,12},{8,0},{12,4},{16,24},{20,28},{24,16},{28,20},{1,9},{5... | collective-permute-start | bytes 294920 | tf_op jit(solution)/shard_map/ppermute | solution.py:20
  85.1 5.2 %collective-permute-start.21 = (bf16[64,768]{1,0:T(8,128)(2,1)S(1)}, bf16[64,768]{1,0:T(8,128)(2,1)S(1)}, u32[]{:S(2)}, u32[]{:S(2)}) collective-permute-start(bf16[64,768]{1,0:T(8,128)(2,1)S(1)} %get-tuple-element.47), channel_id=1, source_target_pairs={{0,8},{4,12},{8,0},{12,4},{16,24},{20,28},{24,16},{28,20},{1,9},{5... | collective-permute-start | bytes 294920 | tf_op jit(solution)/shard_map/ppermute | solution.py:20
  88.1 5.2 %collective-permute-start.35 = (bf16[64,768]{1,0:T(8,128)(2,1)S(1)}, bf16[64,768]{1,0:T(8,128)(2,1)S(1)}, u32[]{:S(2)}, u32[]{:S(2)}) collective-permute-start(bf16[64,768]{1,0:T(8,128)(2,1)S(1)} %get-tuple-element.49), channel_id=1, source_target_pairs={{0,8},{4,12},{8,0},{12,4},{16,24},{20,28},{24,16},{28,20},{1,9},{5... | collective-permute-start | bytes 294920 | tf_op jit(solution)/shard_map/ppermute | solution.py:20
  94.2 5.7 %collective-permute-start.37 = (bf16[64,768]{1,0:T(8,128)(2,1)S(1)}, bf16[64,768]{1,0:T(8,128)(2,1)S(1)}, u32[]{:S(2)}, u32[]{:S(2)}) collective-permute-start(bf16[64,768]{1,0:T(8,128)(2,1)S(1)} %convert_element_type.182), channel_id=1, source_target_pairs={{0,8},{4,12},{8,0},{12,4},{16,24},{20,28},{24,16},{28,20},{1,9},{5... | collective-permute-start | bytes 294920 | tf_op jit(solution)/shard_map/ppermute | solution.py:20
  95.5 6.0 %collective-permute-start.39 = (bf16[64,768]{1,0:T(8,128)(2,1)S(1)}, bf16[64,768]{1,0:T(8,128)(2,1)S(1)}, u32[]{:S(2)}, u32[]{:S(2)}) collective-permute-start(bf16[64,768]{1,0:T(8,128)(2,1)S(1)} %convert_element_type.183), channel_id=1, source_target_pairs={{0,8},{4,12},{8,0},{12,4},{16,24},{20,28},{24,16},{28,20},{1,9},{5... | collective-permute-start | bytes 294920 | tf_op jit(solution)/shard_map/ppermute | solution.py:20
  101.9 11.7 %collective-permute-start.40 = (bf16[128,768]{1,0:T(8,128)(2,1)S(1)}, bf16[128,768]{1,0:T(8,128)(2,1)S(1)}, u32[]{:S(2)}, u32[]{:S(2)}) collective-permute-start(bf16[128,768]{1,0:T(8,128)(2,1)S(1)} %pad_maximum_fusion.5), channel_id=1, source_target_pairs={{0,1},{1,2},{2,3},{3,0},{4,5},{5,6},{6,7},{7,4},{8,9},{9,10},{10,1... | collective-permute-start | bytes 589832 | tf_op jit(solution)/shard_map/ppermute | solution.py:29
  105.2 15.7 %collective-permute-start.41 = (bf16[128,768]{1,0:T(8,128)(2,1)S(1)}, bf16[128,768]{1,0:T(8,128)(2,1)S(1)}, u32[]{:S(2)}, u32[]{:S(2)}) collective-permute-start(bf16[128,768]{1,0:T(8,128)(2,1)S(1)} %pad_maximum_fusion.5), channel_id=1, source_target_pairs={{0,2},{1,3},{2,0},{3,1},{4,6},{5,7},{6,4},{7,5},{8,10},{9,11},{10,... | collective-permute-start | bytes 589832 | tf_op jit(solution)/shard_map/ppermute | solution.py:29
  108.3 12.7 %collective-permute-start.42 = (bf16[128,768]{1,0:T(8,128)(2,1)S(1)}, bf16[128,768]{1,0:T(8,128)(2,1)S(1)}, u32[]{:S(2)}, u32[]{:S(2)}) collective-permute-start(bf16[128,768]{1,0:T(8,128)(2,1)S(1)} %pad_maximum_fusion.5), channel_id=1, source_target_pairs={{0,3},{1,0},{2,1},{3,2},{4,7},{5,4},{6,5},{7,6},{8,11},{9,8},{10,9... | collective-permute-start | bytes 589832 | tf_op jit(solution)/shard_map/ppermute | solution.py:29
  (36 other events, 106.1 us)

commit v17 on v16

--- a/solution.py
+++ b/solution.py
@@ -140,19 +140,16 @@
         return current
 
     half_bands = subspace.shape[0] // 2
-    current = jnp.concatenate(
-        [
-            chebyshev(subspace[:half_bands], start_rotation_gather),
-            chebyshev(subspace[half_bands:], lambda rows: rows),
-        ],
-        axis=0,
-    )
+    first_half = chebyshev(subspace[:half_bands], start_rotation_gather)
+    first_gathered = gather_bands(first_half.astype(jnp.bfloat16))
+    second_half = chebyshev(subspace[half_bands:], lambda rows: rows)
+    second_gathered = gather_bands(second_half.astype(jnp.bfloat16))
     rot_pieces = gathered[0]
     total_orbitals = orb_dev * lax.axis_size("atoms")
     band_count = lax.axis_size("bands")
     band_here = lax.axis_index("bands")
     all_bands = rotations.shape[1]
-    basis_all = gather_bands(current.astype(jnp.bfloat16)).reshape(all_bands, orb_dev)
+    basis_all = jnp.stack([first_gathered, second_gathered], axis=1).reshape(all_bands, orb_dev)
     for rotation_index in range(ROTS - 1):
         groups = []
         for group in range(band_count):

time: 166 us -> 165 us (level); the launches traced: 163 us -> 164 us
  waiting for transfers between devices: 57.8 us -> 55 us
  starting transfers between devices: 43.4 us -> 45.3 us
    ppermute x49, waiting for transfers between devices: 41.6 us -> 37.2 us  [swapped(): return lax.ppermute(value, axis, pairs)]
    ppermute x3, waiting for transfers between devices: 3.54 us -> 7.7 us  [gather_pieces(): pieces.append(lax.ppermute(value, 'bands', pairs))]
    ppermute x3 -> x6, waiting for transfers between devices: 12.6 us -> 10.1 us  [gather_bands(): pieces.append(lax.ppermute(value, 'bands', pairs))]
    ppermute x49, starting transfers between devices: 31.2 us -> 33.3 us  [swapped(): return lax.ppermute(value, axis, pairs)]
    ppermute x3 -> x6, starting transfers between devices: 6.36 us -> 7.08 us  [gather_bands(): pieces.append(lax.ppermute(value, 'bands', pairs))]
  transfers between devices with their start and end apart: 55 -> 58, of which waited for: 25 -> 24; matrix products, arithmetic and copies ran while one was open for 30% -> 32% of each run, Pallas kernels for 0% -> 0%
where the time goes in v17:
time: 165 us; the launch traced here: 164 us
  waiting for transfers between devices  55 us (33%)
  starting transfers between devices  45.3 us (27%)
  matrix products  36.7 us (22%)
  local copies, waits for them, and re-layouts  15.4 us (9%)
  other arithmetic  11.2 us (7%)
    ppermute x49, waiting for transfers between devices, swapped(): return lax.ppermute(value, axis, pairs)  37.2 us
    ppermute x49, starting transfers between devices, swapped(): return lax.ppermute(value, axis, pairs)  33.3 us
    dot_general x32, matrix products, apply_operator(): jnp.dot(other_rows, other_pair[round_index], preferred_element_type=jnp.f...  14.5 us
    dot_general x4, matrix products, pattern_mask(): lax.dot_general(per_row.astype(jnp.bfloat16), col_onehot, (((1,), (1,)),...  10.6 us
    ppermute x6, waiting for transfers between devices, gather_bands(): pieces.append(lax.ppermute(value, 'bands', pairs))  10.1 us
    ppermute x3, waiting for transfers between devices, gather_pieces(): pieces.append(lax.ppermute(value, 'bands', pairs))  7.7 us
    ppermute x6, starting transfers between devices, gather_bands(): pieces.append(lax.ppermute(value, 'bands', pairs))  7.08 us
    dot_general x16, matrix products, apply_operator(): result = jnp.dot(values, diag_sym, preferred_element_type=jnp.float32)  6.61 us
  transfers between devices with their start and end apart: 58, of which 24 were waited for; matrix products, arithmetic and copies ran while one was open for 32% of the time, Pallas kernels for 0%

profile of v17, /device:TPU:0, one launch (start us, length us, event | category | flops | bytes accessed | tf_op | source)
XLA Modules:
  0.0 164.3 jit_solution(8294727665192278981)
XLA Ops:
  0.0 1.6 fusion.108
  2.1 2.5 %collective-permute-start.5 = (bf16[64,768]{1,0:T(8,128)(2,1)}, bf16[64,768]{1,0:T(8,128)(2,1)}, u32[]{:S(2)}, u32[]{:S(2)}) collective-permute-start(bf16[64,768]{1,0:T(8,128)(2,1)} %get-tuple-element.26), channel_id=1, source_target_pairs={{0,8},{4,12},{8,0},{12,4},{16,24},{20,28},{24,16},{28,20},{1,9},{5... | collective-permute-start | bytes 294920 | tf_op jit(solution)/shard_map/ppermute | solution.py:20
  4.6 3.3 %slice_bitcast_fusion.1 = (bf16[768,768]{1,0:T(8,128)(2,1)}, bf16[768,768]{0,1:T(8,128)(2,1)}, bf16[1,768,768]{2,1,0:T(8,128)(2,1)S(1)}) fusion(bf16[2,768,768]{2,1,0:T(8,128)(2,1)} %param.10), kind=kLoop, calls=%fused_computation.110 | loop fusion | bytes 5898240 | tf_op jit(solution)/shard_map/squeeze | solution.py:74
  12.6 2.0 %copy.18 = f32[768,768]{1,0:T(8,128)S(1)} copy(f32[768,768]{0,1:T(8,128)} %convert_bitcast_fusion) | data formatting | bytes 4718592 | tf_op jit(solution)/shard_map/convert_element_type | solution.py:85
  15.9 2.3 %fusion.1 = bf16[768,768]{1,0:T(8,128)(2,1)S(1)} fusion(bf16[768,768]{1,0:T(8,128)(2,1)} %param.9, f32[768,768]{1,0:T(8,128)S(1)} %copy.18, s32[768]{0:T(1024)S(1)} %get-tuple-element.57), kind=kLoop, calls=%fused_computation.7 | loop fusion | flops 7667712 | bytes 4721664 | tf_op jit(solution)/shard_map/convert_element_type | solution.py:86
  21.4 3.1 %compare_select_fusion.2 = bf16[768,768]{1,0:T(8,128)(2,1)} fusion(bf16[1,768,768]{1,2,0:T(8,128)(2,1)} %copy.24, s32[768]{0:T(1024)S(1)} %get-tuple-element.57, s32[768]{0:T(1024)S(1)} %convert_reduce_fusion.1, s32[2,4,4]{2,1,0:T(4,128)S(1)} %copy-done.10), kind=kOutput, calls=%fused_computation.13 | convolution fusion | flops 5932048 | bytes 2369536 | tf_op jit(solution)/shard_map/dot_general | solution.py:63
  25.5 1.9 %compare_select_fusion = bf16[768,768]{1,0:T(8,128)(2,1)} fusion(bf16[768,768]{1,0:T(8,128)(2,1)S(1)} %copy.21, s32[768]{0:T(1024)S(1)} %copy-done.11, s32[768]{0:T(1024)S(1)} %get-tuple-element.57, s32[2,4,4]{2,1,0:T(4,128)S(1)} %copy-done.10), kind=kOutput, calls=%fused_computation.11 | convolution fusion | flops 5932048 | bytes 2369536 | tf_op jit(solution)/shard_map/dot_general | solution.py:63
  27.5 2.0 %collective-permute-start.3 = (s32[4,4]{1,0:T(4,128)}, s32[4,4]{1,0:T(4,128)S(1)}, u32[]{:S(2)}, u32[]{:S(2)}) collective-permute-start(s32[4,4]{1,0:T(4,128)} %get-tuple-element.28), channel_id=1, source_target_pairs={{0,8},{4,12},{8,0},{12,4},{16,24},{20,28},{24,16},{28,20},{1,9},{5... | collective-permute-start | bytes 200 | tf_op jit(solution)/shard_map/ppermute | solution.py:20
  29.5 2.9 %fusion.51 = f32[768,768]{1,0:T(8,128)} fusion(s32[768]{0:T(1024)S(1)} %get-tuple-element.57, s32[768]{0:T(1024)S(1)} %convert_reduce_fusion.1, s32[4,4]{1,0:T(4,128)} %collective-permute-done), kind=kOutput, calls=%fused_computation.108 | convolution fusion | flops 4752400 | bytes 2365504 | tf_op jit(solution)/shard_map/dot_general | solution.py:63
  33.9 2.5 %add_convert_fusion.1 = bf16[768,768]{1,0:T(8,128)(2,1)S(1)} fusion(bf16[768,768]{1,0:T(8,128)(2,1)} %compare_select_fusion.2, bf16[768,768]{1,0:T(8,128)(2,1)S(1)} %copy.20, f32[768,768]{1,0:T(8,128)} %fusion.51), kind=kLoop, calls=%fused_computation.10 | loop fusion | flops 3538944 | bytes 5898240 | tf_op jit(solution)/shard_map/convert_element_type | solution.py:98
  36.4 2.5 %collective-permute-done.3 = s32[4,4]{1,0:T(4,128)S(1)} collective-permute-done((s32[4,4]{1,0:T(4,128)}, s32[4,4]{1,0:T(4,128)S(1)}, u32[]{:S(2)}, u32[]{:S(2)}) %collective-permute-start.3) | collective-permute-done | bytes 96 | tf_op jit(solution)/shard_map/ppermute | solution.py:20
  39.2 2.6 %add_convert_fusion = bf16[768,768]{1,0:T(8,128)(2,1)S(1)} fusion(bf16[768,768]{1,0:T(8,128)(2,1)} %compare_select_fusion, bf16[768,768]{1,0:T(8,128)(2,1)} %collective-permute-done.4, s32[768]{0:T(1024)S(1)} %copy-done.12, s32[768]{0:T(1024)S(1)} %get-tuple-element.57, s32[4,4]{1,0:T(4,128)S(1)} %collective-permute-done.3), kind=kOutput, calls=%fused_computation.9 | convolution fusion | flops 8291344 | bytes 3545152 | tf_op jit(solution)/shard_map/dot_general | solution.py:63
  44.8 1.8 %collective-permute-start.7 = (bf16[64,768]{1,0:T(8,128)(2,1)S(1)}, bf16[64,768]{1,0:T(8,128)(2,1)S(1)}, u32[]{:S(2)}, u32[]{:S(2)}) collective-permute-start(bf16[64,768]{1,0:T(8,128)(2,1)S(1)} %get-tuple-element.32), channel_id=1, source_target_pairs={{0,8},{4,12},{8,0},{12,4},{16,24},{20,28},{24,16},{28,20},{1,9},{5... | collective-permute-start | bytes 294920 | tf_op jit(solution)/shard_map/ppermute | solution.py:20
  52.9 3.7 %collective-permute-start.10 = (bf16[3,256,128]{2,1,0:T(8,128)(2,1)S(1)}, bf16[3,256,128]{2,1,0:T(8,128)(2,1)S(1)}, u32[]{:S(2)}, u32[]{:S(2)}) collective-permute-start(bf16[3,256,128]{2,1,0:T(8,128)(2,1)S(1)} %slice_select_fusion), channel_id=1, source_target_pairs={{0,3},{1,0},{2,1},{3,2},{4,7},{5,4},{6,5},{7,6},{8,11},{9,8},{10,9... | collective-permute-start | bytes 589832 | tf_op jit(solution)/shard_map/ppermute | solution.py:39
  61.2 3.3 %collective-permute-done.27 = bf16[64,768]{1,0:T(8,128)(2,1)S(1)} collective-permute-done((bf16[64,768]{1,0:T(8,128)(2,1)S(1)}, bf16[64,768]{1,0:T(8,128)(2,1)S(1)}, u32[]{:S(2)}, u32[]{:S(2)}) %collective-permute-start.27) | collective-permute-done | bytes 98336 | tf_op jit(solution)/shard_map/ppermute | solution.py:20
  65.9 7.7 %collective-permute-done.9 = bf16[3,256,128]{2,1,0:T(8,128)(2,1)S(1)} collective-permute-done((bf16[3,256,128]{2,1,0:T(8,128)(2,1)S(1)}, bf16[3,256,128]{2,1,0:T(8,128)(2,1)S(1)}, u32[]{:S(2)}, u32[]{:S(2)}) %collective-permute-start.9) | collective-permute-done | bytes 196640 | tf_op jit(solution)/shard_map/ppermute | solution.py:39
  82.0 1.6 collective-permute-start.19
  93.9 2.3 %collective-permute-done.35 = bf16[64,768]{1,0:T(8,128)(2,1)S(1)} collective-permute-done((bf16[64,768]{1,0:T(8,128)(2,1)S(1)}, bf16[64,768]{1,0:T(8,128)(2,1)S(1)}, u32[]{:S(2)}, u32[]{:S(2)}) %collective-permute-start.35) | collective-permute-done | bytes 98336 | tf_op jit(solution)/shard_map/ppermute | solution.py:20
  100.1 2.6 %collective-permute-done.37 = bf16[64,768]{1,0:T(8,128)(2,1)S(1)} collective-permute-done((bf16[64,768]{1,0:T(8,128)(2,1)S(1)}, bf16[64,768]{1,0:T(8,128)(2,1)S(1)}, u32[]{:S(2)}, u32[]{:S(2)}) %collective-permute-start.37) | collective-permute-done | bytes 98336 | tf_op jit(solution)/shard_map/ppermute | solution.py:20
  104.3 1.9 %collective-permute-start.38 = (bf16[64,768]{1,0:T(8,128)(2,1)S(1)}, bf16[64,768]{1,0:T(8,128)(2,1)S(1)}, u32[]{:S(2)}, u32[]{:S(2)}) collective-permute-start(bf16[64,768]{1,0:T(8,128)(2,1)S(1)} %fusion.49), channel_id=1, source_target_pairs={{0,1},{1,2},{2,3},{3,0},{4,5},{5,6},{6,7},{7,4},{8,9},{9,10},{10,1... | collective-permute-start | bytes 294920 | tf_op jit(solution)/shard_map/ppermute | solution.py:29
  107.0 1.9 %collective-permute-start.45 = (bf16[64,768]{1,0:T(8,128)(2,1)S(1)}, bf16[64,768]{1,0:T(8,128)(2,1)S(1)}, u32[]{:S(2)}, u32[]{:S(2)}) collective-permute-start(bf16[64,768]{1,0:T(8,128)(2,1)S(1)} %fusion.50), channel_id=1, source_target_pairs={{0,3},{1,0},{2,1},{3,2},{4,7},{5,4},{6,5},{7,6},{8,11},{9,8},{10,9... | collective-permute-start | bytes 294920 | tf_op jit(solution)/shard_map/ppermute | solution.py:29
  109.2 1.7 %collective-permute-start.43 = (bf16[64,768]{1,0:T(8,128)(2,1)S(1)}, bf16[64,768]{1,0:T(8,128)(2,1)S(1)}, u32[]{:S(2)}, u32[]{:S(2)}) collective-permute-start(bf16[64,768]{1,0:T(8,128)(2,1)S(1)} %fusion.50), channel_id=1, source_target_pairs={{0,1},{1,2},{2,3},{3,0},{4,5},{5,6},{6,7},{7,4},{8,9},{9,10},{10,1... | collective-permute-start | bytes 294920 | tf_op jit(solution)/shard_map/ppermute | solution.py:29
  110.9 4.2 %collective-permute-done.39 = bf16[64,768]{1,0:T(8,128)(2,1)S(1)} collective-permute-done((bf16[64,768]{1,0:T(8,128)(2,1)S(1)}, bf16[64,768]{1,0:T(8,128)(2,1)S(1)}, u32[]{:S(2)}, u32[]{:S(2)}) %collective-permute-start.39) | collective-permute-done | bytes 98336 | tf_op jit(solution)/shard_map/ppermute | solution.py:29
  115.7 5.9 %collective-permute-done.44 = bf16[64,768]{1,0:T(8,128)(2,1)S(1)} collective-permute-done((bf16[64,768]{1,0:T(8,128)(2,1)S(1)}, bf16[64,768]{1,0:T(8,128)(2,1)S(1)}, u32[]{:S(2)}, u32[]{:S(2)}) %collective-permute-start.44) | collective-permute-done | bytes 98336 | tf_op jit(solution)/shard_map/ppermute | solution.py:29
  127.7 2.3 %collective-permute-done.47 = f32[512]{0:T(512)S(1)} collective-permute-done((f32[512]{0:T(512)S(1)}, f32[512]{0:T(512)S(1)}, u32[]{:S(2)}, u32[]{:S(2)}) %collective-permute-start.47) | collective-permute-done | bytes 2080 | tf_op jit(solution)/shard_map/ppermute | solution.py:20
  131.6 2.1 %collective-permute-done.48 = f32[512]{0:T(512)S(1)} collective-permute-done((f32[512]{0:T(512)S(1)}, f32[512]{0:T(512)S(1)}, u32[]{:S(2)}, u32[]{:S(2)}) %collective-permute-start.48) | collective-permute-done | bytes 2080 | tf_op jit(solution)/shard_map/ppermute | solution.py:20
  137.7 2.3 %collective-permute-done.50 = f32[512]{0:T(512)S(1)} collective-permute-done((f32[512]{0:T(512)S(1)}, f32[512]{0:T(512)S(1)}, u32[]{:S(2)}, u32[]{:S(2)}) %collective-permute-start.50) | collective-permute-done | bytes 2080 | tf_op jit(solution)/shard_map/ppermute | solution.py:20
  141.6 2.1 %collective-permute-done.51 = f32[512]{0:T(512)S(1)} collective-permute-done((f32[512]{0:T(512)S(1)}, f32[512]{0:T(512)S(1)}, u32[]{:S(2)}, u32[]{:S(2)}) %collective-permute-start.51) | collective-permute-done | bytes 2080 | tf_op jit(solution)/shard_map/ppermute | solution.py:20
  147.7 2.3 %collective-permute-done.53 = f32[512]{0:T(512)S(1)} collective-permute-done((f32[512]{0:T(512)S(1)}, f32[512]{0:T(512)S(1)}, u32[]{:S(2)}, u32[]{:S(2)}) %collective-permute-start.53) | collective-permute-done | bytes 2080 | tf_op jit(solution)/shard_map/ppermute | solution.py:20
  151.6 2.1 %collective-permute-done.54 = f32[512]{0:T(512)S(1)} collective-permute-done((f32[512]{0:T(512)S(1)}, f32[512]{0:T(512)S(1)}, u32[]{:S(2)}, u32[]{:S(2)}) %collective-permute-start.54) | collective-permute-done | bytes 2080 | tf_op jit(solution)/shard_map/ppermute | solution.py:20
  157.5 2.3 %collective-permute-done.56 = f32[128]{0:T(128)S(1)} collective-permute-done((f32[128]{0:T(128)S(1)}, f32[128]{0:T(128)S(1)}, u32[]{:S(2)}, u32[]{:S(2)}) %collective-permute-start.56) | collective-permute-done | bytes 544 | tf_op jit(solution)/shard_map/ppermute | solution.py:20
  161.3 2.0 %collective-permute-done.57 = f32[128]{0:T(128)S(1)} collective-permute-done((f32[128]{0:T(128)S(1)}, f32[128]{0:T(128)S(1)}, u32[]{:S(2)}, u32[]{:S(2)}) %collective-permute-start.57) | collective-permute-done | bytes 544 | tf_op jit(solution)/shard_map/ppermute | solution.py:20
  (230 shorter events, 78.0 us)
Async XLA Ops:
  1.6 40.2 %collective-permute-start.2 = (bf16[64,768]{1,0:T(8,128)(2,1)}, bf16[64,768]{1,0:T(8,128)(2,1)}, u32[]{:S(2)}, u32[]{:S(2)}) collective-permute-start(bf16[64,768]{1,0:T(8,128)(2,1)} %get-tuple-element.26), channel_id=1, source_target_pairs={{0,4},{4,0},{8,12},{12,8},{16,20},{20,16},{24,28},{28,24},{1,5},{5... | collective-permute-start | bytes 294920 | tf_op jit(solution)/shard_map/ppermute | solution.py:20
  2.1 41.1 %collective-permute-start.5 = (bf16[64,768]{1,0:T(8,128)(2,1)}, bf16[64,768]{1,0:T(8,128)(2,1)}, u32[]{:S(2)}, u32[]{:S(2)}) collective-permute-start(bf16[64,768]{1,0:T(8,128)(2,1)} %get-tuple-element.26), channel_id=1, source_target_pairs={{0,8},{4,12},{8,0},{12,4},{16,24},{20,28},{24,16},{28,20},{1,9},{5... | collective-permute-start | bytes 294920 | tf_op jit(solution)/shard_map/ppermute | solution.py:20
  9.4 23.0 %collective-permute-start.1 = (bf16[768,768]{0,1:T(8,128)(2,1)}, bf16[768,768]{0,1:T(8,128)(2,1)}, u32[]{:S(2)}, u32[]{:S(2)}) collective-permute-start(bf16[768,768]{0,1:T(8,128)(2,1)} %bitcast.4), channel_id=1, source_target_pairs={{0,4},{4,0},{8,12},{12,8},{16,20},{20,16},{24,28},{28,24},{1,5},{5... | collective-permute-start | bytes 3538952 | tf_op jit(solution)/shard_map/ppermute | solution.py:20
  10.2 17.3 %collective-permute-start = (s32[4,4]{1,0:T(4,128)}, s32[4,4]{1,0:T(4,128)}, u32[]{:S(2)}, u32[]{:S(2)}) collective-permute-start(s32[4,4]{1,0:T(4,128)} %get-tuple-element.29), channel_id=1, source_target_pairs={{0,4},{4,0},{8,12},{12,8},{16,20},{20,16},{24,28},{28,24},{1,5},{5... | collective-permute-start | bytes 200 | tf_op jit(solution)/shard_map/ppermute | solution.py:20
  10.5 28.7 %collective-permute-start.4 = (bf16[768,768]{1,0:T(8,128)(2,1)}, bf16[768,768]{1,0:T(8,128)(2,1)}, u32[]{:S(2)}, u32[]{:S(2)}) collective-permute-start(bf16[768,768]{1,0:T(8,128)(2,1)} %get-tuple-element.21), channel_id=1, source_target_pairs={{0,8},{4,12},{8,0},{12,4},{16,24},{20,28},{24,16},{28,20},{1,9},{5... | collective-permute-start | bytes 3538952 | tf_op jit(solution)/shard_map/ppermute | solution.py:20
  27.5 11.4 %collective-permute-start.3 = (s32[4,4]{1,0:T(4,128)}, s32[4,4]{1,0:T(4,128)S(1)}, u32[]{:S(2)}, u32[]{:S(2)}) collective-permute-start(s32[4,4]{1,0:T(4,128)} %get-tuple-element.28), channel_id=1, source_target_pairs={{0,8},{4,12},{8,0},{12,4},{16,24},{20,28},{24,16},{28,20},{1,9},{5... | collective-permute-start | bytes 200 | tf_op jit(solution)/shard_map/ppermute | solution.py:20
  32.4 14.3 %collective-permute-start.22 = (bf16[64,768]{1,0:T(8,128)(2,1)}, bf16[64,768]{1,0:T(8,128)(2,1)}, u32[]{:S(2)}, u32[]{:S(2)}) collective-permute-start(bf16[64,768]{1,0:T(8,128)(2,1)} %get-tuple-element.27), channel_id=1, source_target_pairs={{0,4},{4,0},{8,12},{12,8},{16,20},{20,16},{24,28},{28,24},{1,5},{5... | collective-permute-start | bytes 294920 | tf_op jit(solution)/shard_map/ppermute | solution.py:20
  38.9 9.0 %collective-permute-start.23 = (bf16[64,768]{1,0:T(8,128)(2,1)}, bf16[64,768]{1,0:T(8,128)(2,1)}, u32[]{:S(2)}, u32[]{:S(2)}) collective-permute-start(bf16[64,768]{1,0:T(8,128)(2,1)} %get-tuple-element.27), channel_id=1, source_target_pairs={{0,8},{4,12},{8,0},{12,4},{16,24},{20,28},{24,16},{28,20},{1,9},{5... | collective-permute-start | bytes 294920 | tf_op jit(solution)/shard_map/ppermute | solution.py:20
  44.8 5.3 %collective-permute-start.6 = (bf16[64,768]{1,0:T(8,128)(2,1)S(1)}, bf16[64,768]{1,0:T(8,128)(2,1)S(1)}, u32[]{:S(2)}, u32[]{:S(2)}) collective-permute-start(bf16[64,768]{1,0:T(8,128)(2,1)S(1)} %get-tuple-element.32), channel_id=1, source_target_pairs={{0,4},{4,0},{8,12},{12,8},{16,20},{20,16},{24,28},{28,24},{1,5},{5... | collective-permute-start | bytes 294920 | tf_op jit(solution)/shard_map/ppermute | solution.py:20
  44.8 5.5 %collective-permute-start.7 = (bf16[64,768]{1,0:T(8,128)(2,1)S(1)}, bf16[64,768]{1,0:T(8,128)(2,1)S(1)}, u32[]{:S(2)}, u32[]{:S(2)}) collective-permute-start(bf16[64,768]{1,0:T(8,128)(2,1)S(1)} %get-tuple-element.32), channel_id=1, source_target_pairs={{0,8},{4,12},{8,0},{12,4},{16,24},{20,28},{24,16},{28,20},{1,9},{5... | collective-permute-start | bytes 294920 | tf_op jit(solution)/shard_map/ppermute | solution.py:20
  49.4 7.1 %collective-permute-start.24 = (bf16[64,768]{1,0:T(8,128)(2,1)S(1)}, bf16[64,768]{1,0:T(8,128)(2,1)S(1)}, u32[]{:S(2)}, u32[]{:S(2)}) collective-permute-start(bf16[64,768]{1,0:T(8,128)(2,1)S(1)} %get-tuple-element.42), channel_id=1, source_target_pairs={{0,4},{4,0},{8,12},{12,8},{16,20},{20,16},{24,28},{28,24},{1,5},{5... | collective-permute-start | bytes 294920 | tf_op jit(solution)/shard_map/ppermute | solution.py:20
  49.7 7.2 %collective-permute-start.25 = (bf16[64,768]{1,0:T(8,128)(2,1)S(1)}, bf16[64,768]{1,0:T(8,128)(2,1)S(1)}, u32[]{:S(2)}, u32[]{:S(2)}) collective-permute-start(bf16[64,768]{1,0:T(8,128)(2,1)S(1)} %get-tuple-element.42), channel_id=1, source_target_pairs={{0,8},{4,12},{8,0},{12,4},{16,24},{20,28},{24,16},{28,20},{1,9},{5... | collective-permute-start | bytes 294920 | tf_op jit(solution)/shard_map/ppermute | solution.py:20
  51.1 7.8 %collective-permute-start.12 = (bf16[64,768]{1,0:T(8,128)(2,1)S(1)}, bf16[64,768]{1,0:T(8,128)(2,1)S(1)}, u32[]{:S(2)}, u32[]{:S(2)}) collective-permute-start(bf16[64,768]{1,0:T(8,128)(2,1)S(1)} %convert_element_type.168), channel_id=1, source_target_pairs={{0,4},{4,0},{8,12},{12,8},{16,20},{20,16},{24,28},{28,24},{1,5},{5... | collective-permute-start | bytes 294920 | tf_op jit(solution)/shard_map/ppermute | solution.py:20
  51.3 8.0 %collective-permute-start.13 = (bf16[64,768]{1,0:T(8,128)(2,1)S(1)}, bf16[64,768]{1,0:T(8,128)(2,1)S(1)}, u32[]{:S(2)}, u32[]{:S(2)}) collective-permute-start(bf16[64,768]{1,0:T(8,128)(2,1)S(1)} %convert_element_type.168), channel_id=1, source_target_pairs={{0,8},{4,12},{8,0},{12,4},{16,24},{20,28},{24,16},{28,20},{1,9},{5... | collective-permute-start | bytes 294920 | tf_op jit(solution)/shard_map/ppermute | solution.py:20
  52.9 12.9 %collective-permute-start.10 = (bf16[3,256,128]{2,1,0:T(8,128)(2,1)S(1)}, bf16[3,256,128]{2,1,0:T(8,128)(2,1)S(1)}, u32[]{:S(2)}, u32[]{:S(2)}) collective-permute-start(bf16[3,256,128]{2,1,0:T(8,128)(2,1)S(1)} %slice_select_fusion), channel_id=1, source_target_pairs={{0,3},{1,0},{2,1},{3,2},{4,7},{5,4},{6,5},{7,6},{8,11},{9,8},{10,9... | collective-permute-start | bytes 589832 | tf_op jit(solution)/shard_map/ppermute | solution.py:39
  56.6 17.0 %collective-permute-start.9 = (bf16[3,256,128]{2,1,0:T(8,128)(2,1)S(1)}, bf16[3,256,128]{2,1,0:T(8,128)(2,1)S(1)}, u32[]{:S(2)}, u32[]{:S(2)}) collective-permute-start(bf16[3,256,128]{2,1,0:T(8,128)(2,1)S(1)} %slice_select_fusion), channel_id=1, source_target_pairs={{0,2},{1,3},{2,0},{3,1},{4,6},{5,7},{6,4},{7,5},{8,10},{9,11},{10,... | collective-permute-start | bytes 589832 | tf_op jit(solution)/shard_map/ppermute | solution.py:39
  56.9 17.2 %collective-permute-start.8 = (bf16[3,256,128]{2,1,0:T(8,128)(2,1)S(1)}, bf16[3,256,128]{2,1,0:T(8,128)(2,1)S(1)}, u32[]{:S(2)}, u32[]{:S(2)}) collective-permute-start(bf16[3,256,128]{2,1,0:T(8,128)(2,1)S(1)} %slice_select_fusion), channel_id=1, source_target_pairs={{0,1},{1,2},{2,3},{3,0},{4,5},{5,6},{6,7},{7,4},{8,9},{9,10},{10,1... | collective-permute-start | bytes 589832 | tf_op jit(solution)/shard_map/ppermute | solution.py:39
  59.3 5.3 %collective-permute-start.27 = (bf16[64,768]{1,0:T(8,128)(2,1)S(1)}, bf16[64,768]{1,0:T(8,128)(2,1)S(1)}, u32[]{:S(2)}, u32[]{:S(2)}) collective-permute-start(bf16[64,768]{1,0:T(8,128)(2,1)S(1)} %get-tuple-element.44), channel_id=1, source_target_pairs={{0,8},{4,12},{8,0},{12,4},{16,24},{20,28},{24,16},{28,20},{1,9},{5... | collective-permute-start | bytes 294920 | tf_op jit(solution)/shard_map/ppermute | solution.py:20
  60.3 14.6 %collective-permute-start.14 = (bf16[64,768]{1,0:T(8,128)(2,1)S(1)}, bf16[64,768]{1,0:T(8,128)(2,1)S(1)}, u32[]{:S(2)}, u32[]{:S(2)}) collective-permute-start(bf16[64,768]{1,0:T(8,128)(2,1)S(1)} %get-tuple-element.34), channel_id=1, source_target_pairs={{0,4},{4,0},{8,12},{12,8},{16,20},{20,16},{24,28},{28,24},{1,5},{5... | collective-permute-start | bytes 294920 | tf_op jit(solution)/shard_map/ppermute | solution.py:20
  64.6 10.7 %collective-permute-start.15 = (bf16[64,768]{1,0:T(8,128)(2,1)S(1)}, bf16[64,768]{1,0:T(8,128)(2,1)S(1)}, u32[]{:S(2)}, u32[]{:S(2)}) collective-permute-start(bf16[64,768]{1,0:T(8,128)(2,1)S(1)} %get-tuple-element.34), channel_id=1, source_target_pairs={{0,8},{4,12},{8,0},{12,4},{16,24},{20,28},{24,16},{28,20},{1,9},{5... | collective-permute-start | bytes 294920 | tf_op jit(solution)/shard_map/ppermute | solution.py:20
  65.8 12.2 %collective-permute-start.28 = (bf16[64,768]{1,0:T(8,128)(2,1)S(1)}, bf16[64,768]{1,0:T(8,128)(2,1)S(1)}, u32[]{:S(2)}, u32[]{:S(2)}) collective-permute-start(bf16[64,768]{1,0:T(8,128)(2,1)S(1)} %get-tuple-element.46), channel_id=1, source_target_pairs={{0,4},{4,0},{8,12},{12,8},{16,20},{20,16},{24,28},{28,24},{1,5},{5... | collective-permute-start | bytes 294920 | tf_op jit(solution)/shard_map/ppermute | solution.py:20
  74.8 21.7 %collective-permute-start.11 = (bf16[4,3,256,128]{3,2,1,0:T(8,128)(2,1)S(1)}, bf16[4,3,256,128]{3,2,1,0:T(8,128)(2,1)S(1)}, u32[]{:S(2)}, u32[]{:S(2)}) collective-permute-start(bf16[4,3,256,128]{3,2,1,0:T(8,128)(2,1)S(1)} %get-tuple-element.24), channel_id=1, source_target_pairs={{0,4},{4,0},{8,12},{12,8},{16,20},{20,16},{24,28},{28,24},{1,5},{5... | collective-permute-start | bytes 2359304 | tf_op jit(solution)/shard_map/ppermute | solution.py:20
  79.1 5.2 %collective-permute-start.31 = (bf16[64,768]{1,0:T(8,128)(2,1)S(1)}, bf16[64,768]{1,0:T(8,128)(2,1)S(1)}, u32[]{:S(2)}, u32[]{:S(2)}) collective-permute-start(bf16[64,768]{1,0:T(8,128)(2,1)S(1)} %get-tuple-element.48), channel_id=1, source_target_pairs={{0,8},{4,12},{8,0},{12,4},{16,24},{20,28},{24,16},{28,20},{1,9},{5... | collective-permute-start | bytes 294920 | tf_op jit(solution)/shard_map/ppermute | solution.py:20
  97.1 5.7 %collective-permute-start.37 = (bf16[64,768]{1,0:T(8,128)(2,1)S(1)}, bf16[64,768]{1,0:T(8,128)(2,1)S(1)}, u32[]{:S(2)}, u32[]{:S(2)}) collective-permute-start(bf16[64,768]{1,0:T(8,128)(2,1)S(1)} %convert_element_type.180), channel_id=1, source_target_pairs={{0,8},{4,12},{8,0},{12,4},{16,24},{20,28},{24,16},{28,20},{1,9},{5... | collective-permute-start | bytes 294920 | tf_op jit(solution)/shard_map/ppermute | solution.py:20
  98.1 8.2 %collective-permute-start.41 = (bf16[64,768]{1,0:T(8,128)(2,1)S(1)}, bf16[64,768]{1,0:T(8,128)(2,1)S(1)}, u32[]{:S(2)}, u32[]{:S(2)}) collective-permute-start(bf16[64,768]{1,0:T(8,128)(2,1)S(1)} %convert_element_type.182), channel_id=1, source_target_pairs={{0,4},{4,0},{8,12},{12,8},{16,20},{20,16},{24,28},{28,24},{1,5},{5... | collective-permute-start | bytes 294920 | tf_op jit(solution)/shard_map/ppermute | solution.py:20
  98.3 8.3 %collective-permute-start.42 = (bf16[64,768]{1,0:T(8,128)(2,1)S(1)}, bf16[64,768]{1,0:T(8,128)(2,1)S(1)}, u32[]{:S(2)}, u32[]{:S(2)}) collective-permute-start(bf16[64,768]{1,0:T(8,128)(2,1)S(1)} %convert_element_type.182), channel_id=1, source_target_pairs={{0,8},{4,12},{8,0},{12,4},{16,24},{20,28},{24,16},{28,20},{1,9},{5... | collective-permute-start | bytes 294920 | tf_op jit(solution)/shard_map/ppermute | solution.py:20
  103.1 6.1 %collective-permute-start.40 = (bf16[64,768]{1,0:T(8,128)(2,1)S(1)}, bf16[64,768]{1,0:T(8,128)(2,1)S(1)}, u32[]{:S(2)}, u32[]{:S(2)}) collective-permute-start(bf16[64,768]{1,0:T(8,128)(2,1)S(1)} %fusion.49), channel_id=1, source_target_pairs={{0,3},{1,0},{2,1},{3,2},{4,7},{5,4},{6,5},{7,6},{8,11},{9,8},{10,9... | collective-permute-start | bytes 294920 | tf_op jit(solution)/shard_map/ppermute | solution.py:29
  103.5 11.6 %collective-permute-start.39 = (bf16[64,768]{1,0:T(8,128)(2,1)S(1)}, bf16[64,768]{1,0:T(8,128)(2,1)S(1)}, u32[]{:S(2)}, u32[]{:S(2)}) collective-permute-start(bf16[64,768]{1,0:T(8,128)(2,1)S(1)} %fusion.49), channel_id=1, source_target_pairs={{0,2},{1,3},{2,0},{3,1},{4,6},{5,7},{6,4},{7,5},{8,10},{9,11},{10,... | collective-permute-start | bytes 294920 | tf_op jit(solution)/shard_map/ppermute | solution.py:29
  104.3 10.7 %collective-permute-start.38 = (bf16[64,768]{1,0:T(8,128)(2,1)S(1)}, bf16[64,768]{1,0:T(8,128)(2,1)S(1)}, u32[]{:S(2)}, u32[]{:S(2)}) collective-permute-start(bf16[64,768]{1,0:T(8,128)(2,1)S(1)} %fusion.49), channel_id=1, source_target_pairs={{0,1},{1,2},{2,3},{3,0},{4,5},{5,6},{6,7},{7,4},{8,9},{9,10},{10,1... | collective-permute-start | bytes 294920 | tf_op jit(solution)/shard_map/ppermute | solution.py:29
  107.0 8.8 %collective-permute-start.45 = (bf16[64,768]{1,0:T(8,128)(2,1)S(1)}, bf16[64,768]{1,0:T(8,128)(2,1)S(1)}, u32[]{:S(2)}, u32[]{:S(2)}) collective-permute-start(bf16[64,768]{1,0:T(8,128)(2,1)S(1)} %fusion.50), channel_id=1, source_target_pairs={{0,3},{1,0},{2,1},{3,2},{4,7},{5,4},{6,5},{7,6},{8,11},{9,8},{10,9... | collective-permute-start | bytes 294920 | tf_op jit(solution)/shard_map/ppermute | solution.py:29
  108.9 12.7 %collective-permute-start.44 = (bf16[64,768]{1,0:T(8,128)(2,1)S(1)}, bf16[64,768]{1,0:T(8,128)(2,1)S(1)}, u32[]{:S(2)}, u32[]{:S(2)}) collective-permute-start(bf16[64,768]{1,0:T(8,128)(2,1)S(1)} %fusion.50), channel_id=1, source_target_pairs={{0,2},{1,3},{2,0},{3,1},{4,6},{5,7},{6,4},{7,5},{8,10},{9,11},{10,... | collective-permute-start | bytes 294920 | tf_op jit(solution)/shard_map/ppermute | solution.py:29
  109.2 12.4 %collective-permute-start.43 = (bf16[64,768]{1,0:T(8,128)(2,1)S(1)}, bf16[64,768]{1,0:T(8,128)(2,1)S(1)}, u32[]{:S(2)}, u32[]{:S(2)}) collective-permute-start(bf16[64,768]{1,0:T(8,128)(2,1)S(1)} %fusion.50), channel_id=1, source_target_pairs={{0,1},{1,2},{2,3},{3,0},{4,5},{5,6},{6,7},{7,4},{8,9},{9,10},{10,1... | collective-permute-start | bytes 294920 | tf_op jit(solution)/shard_map/ppermute | solution.py:29
  (40 other events, 126.5 us)

commit v18 on v17

--- a/solution.py
+++ b/solution.py
@@ -114,8 +114,24 @@
             if degree_index == GATHER_AT:
                 current = hook(current)
             if degree_index == DEGREE - 1 and gathered:
-                settled, current = lax.optimization_barrier((gathered[0], current))
+                whole = gathered[0]
+                count = whole.shape[0]
+                block = whole.shape[2] // count
+                here = lax.axis_index("bands")
+                first_step = jnp.concatenate(
+                    [
+                        lax.dynamic_slice_in_dim(
+                            whole[:, 0], ((here - shift) % count) * block, block, axis=1
+                        )
+                        for shift in range(count)
+                    ],
+                    axis=1,
+                )
+                settled, first_step, current = lax.optimization_barrier(
+                    (whole, first_step, current)
+                )
                 gathered[0] = settled
+                gathered.append(first_step)
             applied = apply_operator(current.astype(jnp.bfloat16))
             following = 2.0 * (applied - filter_center * current) / filter_half - previous
             previous, current = (current, following)
@@ -141,24 +157,29 @@
 
     half_bands = subspace.shape[0] // 2
     first_half = chebyshev(subspace[:half_bands], start_rotation_gather)
-    first_gathered = gather_bands(first_half.astype(jnp.bfloat16))
+    first_gathered = gather_pieces(first_half.astype(jnp.bfloat16))
     second_half = chebyshev(subspace[half_bands:], lambda rows: rows)
-    second_gathered = gather_bands(second_half.astype(jnp.bfloat16))
+    second_gathered = gather_pieces(second_half.astype(jnp.bfloat16))
     rot_pieces = gathered[0]
     total_orbitals = orb_dev * lax.axis_size("atoms")
     band_count = lax.axis_size("bands")
     band_here = lax.axis_index("bands")
     all_bands = rotations.shape[1]
     basis_all = jnp.stack([first_gathered, second_gathered], axis=1).reshape(all_bands, orb_dev)
+    first_step = gathered[1]
     for rotation_index in range(ROTS - 1):
         groups = []
         for group in range(band_count):
-            piece = lax.dynamic_index_in_dim(
-                rot_pieces, (band_here - group) % band_count, 0, keepdims=False
-            )
+            shift = (band_here - group) % band_count
+            if rotation_index == 0:
+                piece = lax.dynamic_index_in_dim(first_step, shift, 0, keepdims=False)
+            else:
+                piece = lax.dynamic_index_in_dim(
+                    rot_pieces, shift, 0, keepdims=False
+                )[rotation_index]
             groups.append(
                 lax.dot_general(
-                    piece[rotation_index],
+                    piece,
                     basis_all,
                     (((0,), (0,)), ((), ())),
                     preferred_element_type=jnp.float32,

time: 165 us -> 165 us (level)
  waiting for transfers between devices: 55 us -> 51.6 us
  starting transfers between devices: 45.3 us -> 48.4 us
    ppermute x3 -> x9, starting transfers between devices: 4.9 us -> 17.7 us  [gather_pieces(): pieces.append(lax.ppermute(value, 'bands', pairs))]
    ppermute x6 -> x0, waiting for transfers between devices: 10.1 us -> none  [gather_bands(): pieces.append(lax.ppermute(value, 'bands', pairs))]
    ppermute x6 -> x0, starting transfers between devices: 7.08 us -> none  [gather_bands(): pieces.append(lax.ppermute(value, 'bands', pairs))]
    ppermute x3 -> x9, waiting for transfers between devices: 7.7 us -> 11.6 us  [gather_pieces(): pieces.append(lax.ppermute(value, 'bands', pairs))]
    ppermute x49, waiting for transfers between devices: 37.2 us -> 40 us  [swapped(): return lax.ppermute(value, axis, pairs)]
    ppermute x49, starting transfers between devices: 33.3 us -> 30.8 us  [swapped(): return lax.ppermute(value, axis, pairs)]
    unnamed x29 -> x25, local copies, waits for them, and re-layouts: 2.83 us -> 3.99 us
  transfers between devices with their start and end apart: 58 -> 58, of which waited for: 24 -> 27; matrix products, arithmetic and copies ran while one was open for 32% -> 31% of each run, Pallas kernels for 0% -> 0%
where the time goes in v18:
time: 165 us; the launch traced here: 164 us
  waiting for transfers between devices  51.6 us (31%)
  starting transfers between devices  48.4 us (29%)
  matrix products  36.8 us (22%)
  local copies, waits for them, and re-layouts  16.1 us (10%)
  other arithmetic  10.5 us (6%)
    ppermute x49, waiting for transfers between devices, swapped(): return lax.ppermute(value, axis, pairs)  40 us
    ppermute x49, starting transfers between devices, swapped(): return lax.ppermute(value, axis, pairs)  30.8 us
    ppermute x9, starting transfers between devices, gather_pieces(): pieces.append(lax.ppermute(value, 'bands', pairs))  17.7 us
    dot_general x32, matrix products, apply_operator(): jnp.dot(other_rows, other_pair[round_index], preferred_element_type=jnp.f...  14.5 us
    ppermute x9, waiting for transfers between devices, gather_pieces(): pieces.append(lax.ppermute(value, 'bands', pairs))  11.6 us
    dot_general x4, matrix products, pattern_mask(): lax.dot_general(per_row.astype(jnp.bfloat16), col_onehot, (((1,), (1,)),...  10.6 us
    dot_general x16, matrix products, apply_operator(): result = jnp.dot(values, diag_sym, preferred_element_type=jnp.float32)  6.63 us
    unnamed x25, local copies, waits for them, and re-layouts  3.99 us
  transfers between devices with their start and end apart: 58, of which 27 were waited for; matrix products, arithmetic and copies ran while one was open for 31% of the time, Pallas kernels for 0%

profile of v18, /device:TPU:0, one launch (start us, length us, event | category | flops | bytes accessed | tf_op | source)
XLA Modules:
  0.0 164.2 jit_solution(8129973256806455849)
XLA Ops:
  0.0 1.6 fusion.115
  2.1 2.5 %collective-permute-start.5 = (bf16[64,768]{1,0:T(8,128)(2,1)}, bf16[64,768]{1,0:T(8,128)(2,1)}, u32[]{:S(2)}, u32[]{:S(2)}) collective-permute-start(bf16[64,768]{1,0:T(8,128)(2,1)} %get-tuple-element.31), channel_id=1, source_target_pairs={{0,8},{4,12},{8,0},{12,4},{16,24},{20,28},{24,16},{28,20},{1,9},{5... | collective-permute-start | bytes 294920 | tf_op jit(solution)/shard_map/ppermute | solution.py:20
  6.0 3.4 %slice_bitcast_fusion.1 = (bf16[768,768]{1,0:T(8,128)(2,1)}, bf16[768,768]{0,1:T(8,128)(2,1)}, bf16[1,768,768]{2,1,0:T(8,128)(2,1)S(1)}) fusion(bf16[2,768,768]{2,1,0:T(8,128)(2,1)} %param.8), kind=kLoop, calls=%fused_computation.108 | loop fusion | bytes 5898240 | tf_op jit(solution)/shard_map/squeeze | solution.py:74
  14.6 2.0 %copy.18 = f32[768,768]{1,0:T(8,128)S(1)} copy(f32[768,768]{0,1:T(8,128)} %convert_bitcast_fusion) | data formatting | bytes 4718592 | tf_op jit(solution)/shard_map/convert_element_type | solution.py:85
  16.7 2.3 %fusion.1 = bf16[768,768]{1,0:T(8,128)(2,1)S(1)} fusion(bf16[768,768]{1,0:T(8,128)(2,1)} %param.7, f32[768,768]{1,0:T(8,128)S(1)} %copy.18, s32[768]{0:T(1024)S(1)} %get-tuple-element.60), kind=kLoop, calls=%fused_computation.5 | loop fusion | flops 7667712 | bytes 4721664 | tf_op jit(solution)/shard_map/convert_element_type | solution.py:86
  21.8 3.2 %compare_select_fusion.2 = bf16[768,768]{1,0:T(8,128)(2,1)} fusion(bf16[1,768,768]{1,2,0:T(8,128)(2,1)} %copy.24, s32[768]{0:T(1024)S(1)} %get-tuple-element.60, s32[768]{0:T(1024)S(1)} %convert_reduce_fusion.1, s32[2,4,4]{2,1,0:T(4,128)S(1)} %copy-done.10), kind=kOutput, calls=%fused_computation.11 | convolution fusion | flops 5932048 | bytes 2369536 | tf_op jit(solution)/shard_map/dot_general | solution.py:63
  26.0 1.9 %compare_select_fusion = bf16[768,768]{1,0:T(8,128)(2,1)} fusion(bf16[768,768]{1,0:T(8,128)(2,1)S(1)} %copy.21, s32[768]{0:T(1024)S(1)} %get-tuple-element.59, s32[768]{0:T(1024)S(1)} %get-tuple-element.60, s32[2,4,4]{2,1,0:T(4,128)S(1)} %copy-done.10), kind=kOutput, calls=%fused_computation.9 | convolution fusion | flops 5932048 | bytes 2369536 | tf_op jit(solution)/shard_map/dot_general | solution.py:63
  27.9 2.0 %collective-permute-start.3 = (s32[4,4]{1,0:T(4,128)S(1)}, s32[4,4]{1,0:T(4,128)S(1)}, u32[]{:S(2)}, u32[]{:S(2)}) collective-permute-start(s32[4,4]{1,0:T(4,128)S(1)} %get-tuple-element.33), channel_id=1, source_target_pairs={{0,8},{4,12},{8,0},{12,4},{16,24},{20,28},{24,16},{28,20},{1,9},{5... | collective-permute-start | bytes 200 | tf_op jit(solution)/shard_map/ppermute | solution.py:20
  30.0 2.9 %fusion.51 = f32[768,768]{1,0:T(8,128)} fusion(s32[768]{0:T(1024)S(1)} %get-tuple-element.60, s32[768]{0:T(1024)S(1)} %convert_reduce_fusion.1, s32[4,4]{1,0:T(4,128)} %collective-permute-done), kind=kOutput, calls=%fused_computation.106 | convolution fusion | flops 4752400 | bytes 2365504 | tf_op jit(solution)/shard_map/dot_general | solution.py:63
  34.5 2.5 %add_convert_fusion.1 = bf16[768,768]{1,0:T(8,128)(2,1)S(1)} fusion(bf16[768,768]{1,0:T(8,128)(2,1)} %compare_select_fusion.2, bf16[768,768]{1,0:T(8,128)(2,1)S(1)} %copy.20, f32[768,768]{1,0:T(8,128)} %fusion.51), kind=kLoop, calls=%fused_computation.8 | loop fusion | flops 3538944 | bytes 5898240 | tf_op jit(solution)/shard_map/convert_element_type | solution.py:98
  36.9 2.6 %collective-permute-done.3 = s32[4,4]{1,0:T(4,128)S(1)} collective-permute-done((s32[4,4]{1,0:T(4,128)S(1)}, s32[4,4]{1,0:T(4,128)S(1)}, u32[]{:S(2)}, u32[]{:S(2)}) %collective-permute-start.3) | collective-permute-done | bytes 96 | tf_op jit(solution)/shard_map/ppermute | solution.py:20
  39.9 2.6 %add_convert_fusion = bf16[768,768]{1,0:T(8,128)(2,1)S(1)} fusion(bf16[768,768]{1,0:T(8,128)(2,1)} %compare_select_fusion, bf16[768,768]{1,0:T(8,128)(2,1)} %collective-permute-done.4, s32[768]{0:T(1024)S(1)} %get-tuple-element.59, s32[768]{0:T(1024)S(1)} %get-tuple-element.60, s32[4,4]{1,0:T(4,128)S(1)} %collective-permute-done.3), kind=kOutput, calls=%fused_computation.7 | convolution fusion | flops 8291344 | bytes 3545152 | tf_op jit(solution)/shard_map/dot_general | solution.py:63
  45.5 1.8 %collective-permute-start.7 = (bf16[64,768]{1,0:T(8,128)(2,1)S(1)}, bf16[64,768]{1,0:T(8,128)(2,1)S(1)}, u32[]{:S(2)}, u32[]{:S(2)}) collective-permute-start(bf16[64,768]{1,0:T(8,128)(2,1)S(1)} %get-tuple-element.45), channel_id=1, source_target_pairs={{0,8},{4,12},{8,0},{12,4},{16,24},{20,28},{24,16},{28,20},{1,9},{5... | collective-permute-start | bytes 294920 | tf_op jit(solution)/shard_map/ppermute | solution.py:20
  55.2 2.6 %collective-permute-start.9 = (bf16[3,256,128]{2,1,0:T(8,128)(2,1)S(1)}, bf16[3,256,128]{2,1,0:T(8,128)(2,1)S(1)}, u32[]{:S(2)}, u32[]{:S(2)}) collective-permute-start(bf16[3,256,128]{2,1,0:T(8,128)(2,1)S(1)} %slice_select_fusion), channel_id=1, source_target_pairs={{0,2},{1,3},{2,0},{3,1},{4,6},{5,7},{6,4},{7,5},{8,10},{9,11},{10,... | collective-permute-start | bytes 589832 | tf_op jit(solution)/shard_map/ppermute | solution.py:39
  62.8 3.3 %collective-permute-done.27 = bf16[64,768]{1,0:T(8,128)(2,1)S(1)} collective-permute-done((bf16[64,768]{1,0:T(8,128)(2,1)S(1)}, bf16[64,768]{1,0:T(8,128)(2,1)S(1)}, u32[]{:S(2)}, u32[]{:S(2)}) %collective-permute-start.27) | collective-permute-done | bytes 98336 | tf_op jit(solution)/shard_map/ppermute | solution.py:20
  67.5 3.5 %collective-permute-done.9 = bf16[3,256,128]{2,1,0:T(8,128)(2,1)S(1)} collective-permute-done((bf16[3,256,128]{2,1,0:T(8,128)(2,1)S(1)}, bf16[3,256,128]{2,1,0:T(8,128)(2,1)S(1)}, u32[]{:S(2)}, u32[]{:S(2)}) %collective-permute-start.9) | collective-permute-done | bytes 196640 | tf_op jit(solution)/shard_map/ppermute | solution.py:39
  91.3 2.3 %collective-permute-done.35 = bf16[64,768]{1,0:T(8,128)(2,1)S(1)} collective-permute-done((bf16[64,768]{1,0:T(8,128)(2,1)S(1)}, bf16[64,768]{1,0:T(8,128)(2,1)S(1)}, u32[]{:S(2)}, u32[]{:S(2)}) %collective-permute-start.35) | collective-permute-done | bytes 98336 | tf_op jit(solution)/shard_map/ppermute | solution.py:20
  98.6 2.7 %collective-permute-done.37 = bf16[64,768]{1,0:T(8,128)(2,1)S(1)} collective-permute-done((bf16[64,768]{1,0:T(8,128)(2,1)S(1)}, bf16[64,768]{1,0:T(8,128)(2,1)S(1)}, u32[]{:S(2)}, u32[]{:S(2)}) %collective-permute-start.37) | collective-permute-done | bytes 98336 | tf_op jit(solution)/shard_map/ppermute | solution.py:20
  101.6 3.1 %collective-permute-start.38 = (bf16[64,768]{1,0:T(8,128)(2,1)S(1)}, bf16[64,768]{1,0:T(8,128)(2,1)S(1)}, u32[]{:S(2)}, u32[]{:S(2)}) collective-permute-start(bf16[64,768]{1,0:T(8,128)(2,1)S(1)} %fusion.49), channel_id=1, source_target_pairs={{0,1},{1,2},{2,3},{3,0},{4,5},{5,6},{6,7},{7,4},{8,9},{9,10},{10,1... | collective-permute-start | bytes 294920 | tf_op jit(solution)/shard_map/ppermute | solution.py:39
  104.7 3.3 %collective-permute-start.39 = (bf16[64,768]{1,0:T(8,128)(2,1)S(1)}, bf16[64,768]{1,0:T(8,128)(2,1)S(1)}, u32[]{:S(2)}, u32[]{:S(2)}) collective-permute-start(bf16[64,768]{1,0:T(8,128)(2,1)S(1)} %fusion.49), channel_id=1, source_target_pairs={{0,2},{1,3},{2,0},{3,1},{4,6},{5,7},{6,4},{7,5},{8,10},{9,11},{10,... | collective-permute-start | bytes 294920 | tf_op jit(solution)/shard_map/ppermute | solution.py:39
  108.7 2.1 %collective-permute-start.43 = (bf16[64,768]{1,0:T(8,128)(2,1)S(1)}, bf16[64,768]{1,0:T(8,128)(2,1)S(1)}, u32[]{:S(2)}, u32[]{:S(2)}) collective-permute-start(bf16[64,768]{1,0:T(8,128)(2,1)S(1)} %fusion.50), channel_id=1, source_target_pairs={{0,1},{1,2},{2,3},{3,0},{4,5},{5,6},{6,7},{7,4},{8,9},{9,10},{10,1... | collective-permute-start | bytes 294920 | tf_op jit(solution)/shard_map/ppermute | solution.py:39
  111.3 3.4 %collective-permute-start.45 = (bf16[64,768]{1,0:T(8,128)(2,1)S(1)}, bf16[64,768]{1,0:T(8,128)(2,1)S(1)}, u32[]{:S(2)}, u32[]{:S(2)}) collective-permute-start(bf16[64,768]{1,0:T(8,128)(2,1)S(1)} %fusion.50), channel_id=1, source_target_pairs={{0,3},{1,0},{2,1},{3,2},{4,7},{5,4},{6,5},{7,6},{8,11},{9,8},{10,9... | collective-permute-start | bytes 294920 | tf_op jit(solution)/shard_map/ppermute | solution.py:39
  114.7 1.9 %collective-permute-done.39 = bf16[64,768]{1,0:T(8,128)(2,1)S(1)} collective-permute-done((bf16[64,768]{1,0:T(8,128)(2,1)S(1)}, bf16[64,768]{1,0:T(8,128)(2,1)S(1)}, u32[]{:S(2)}, u32[]{:S(2)}) %collective-permute-start.39) | collective-permute-done | bytes 98336 | tf_op jit(solution)/shard_map/ppermute | solution.py:39
  117.5 4.8 %collective-permute-done.44 = bf16[64,768]{1,0:T(8,128)(2,1)S(1)} collective-permute-done((bf16[64,768]{1,0:T(8,128)(2,1)S(1)}, bf16[64,768]{1,0:T(8,128)(2,1)S(1)}, u32[]{:S(2)}, u32[]{:S(2)}) %collective-permute-start.44) | collective-permute-done | bytes 98336 | tf_op jit(solution)/shard_map/ppermute | solution.py:39
  125.8 3.0 %collective-permute-done.47 = f32[512]{0:T(512)S(1)} collective-permute-done((f32[512]{0:T(512)S(1)}, f32[512]{0:T(512)S(1)}, u32[]{:S(2)}, u32[]{:S(2)}) %collective-permute-start.47) | collective-permute-done | bytes 2080 | tf_op jit(solution)/shard_map/ppermute | solution.py:20
  130.3 2.1 %collective-permute-done.48 = f32[512]{0:T(512)S(1)} collective-permute-done((f32[512]{0:T(512)S(1)}, f32[512]{0:T(512)S(1)}, u32[]{:S(2)}, u32[]{:S(2)}) %collective-permute-start.48) | collective-permute-done | bytes 2080 | tf_op jit(solution)/shard_map/ppermute | solution.py:20
  137.0 3.0 %collective-permute-done.50 = f32[512]{0:T(512)S(1)} collective-permute-done((f32[512]{0:T(512)S(1)}, f32[512]{0:T(512)S(1)}, u32[]{:S(2)}, u32[]{:S(2)}) %collective-permute-start.50) | collective-permute-done | bytes 2080 | tf_op jit(solution)/shard_map/ppermute | solution.py:20
  141.5 2.1 %collective-permute-done.51 = f32[512]{0:T(512)S(1)} collective-permute-done((f32[512]{0:T(512)S(1)}, f32[512]{0:T(512)S(1)}, u32[]{:S(2)}, u32[]{:S(2)}) %collective-permute-start.51) | collective-permute-done | bytes 2080 | tf_op jit(solution)/shard_map/ppermute | solution.py:20
  147.0 3.0 %collective-permute-done.53 = f32[512]{0:T(512)S(1)} collective-permute-done((f32[512]{0:T(512)S(1)}, f32[512]{0:T(512)S(1)}, u32[]{:S(2)}, u32[]{:S(2)}) %collective-permute-start.53) | collective-permute-done | bytes 2080 | tf_op jit(solution)/shard_map/ppermute | solution.py:20
  151.5 2.1 %collective-permute-done.54 = f32[512]{0:T(512)S(1)} collective-permute-done((f32[512]{0:T(512)S(1)}, f32[512]{0:T(512)S(1)}, u32[]{:S(2)}, u32[]{:S(2)}) %collective-permute-start.54) | collective-permute-done | bytes 2080 | tf_op jit(solution)/shard_map/ppermute | solution.py:20
  156.8 2.9 %collective-permute-done.56 = f32[128]{0:T(128)S(1)} collective-permute-done((f32[128]{0:T(128)S(1)}, f32[128]{0:T(128)S(1)}, u32[]{:S(2)}, u32[]{:S(2)}) %collective-permute-start.56) | collective-permute-done | bytes 544 | tf_op jit(solution)/shard_map/ppermute | solution.py:20
  161.2 2.0 %collective-permute-done.57 = f32[128]{0:T(128)S(1)} collective-permute-done((f32[128]{0:T(128)S(1)}, f32[128]{0:T(128)S(1)}, u32[]{:S(2)}, u32[]{:S(2)}) %collective-permute-start.57) | collective-permute-done | bytes 544 | tf_op jit(solution)/shard_map/ppermute | solution.py:20
  (223 shorter events, 78.9 us)
Async XLA Ops:
  1.6 40.8 %collective-permute-start.2 = (bf16[64,768]{1,0:T(8,128)(2,1)}, bf16[64,768]{1,0:T(8,128)(2,1)}, u32[]{:S(2)}, u32[]{:S(2)}) collective-permute-start(bf16[64,768]{1,0:T(8,128)(2,1)} %get-tuple-element.31), channel_id=1, source_target_pairs={{0,4},{4,0},{8,12},{12,8},{16,20},{20,16},{24,28},{28,24},{1,5},{5... | collective-permute-start | bytes 294920 | tf_op jit(solution)/shard_map/ppermute | solution.py:20
  2.1 41.8 %collective-permute-start.5 = (bf16[64,768]{1,0:T(8,128)(2,1)}, bf16[64,768]{1,0:T(8,128)(2,1)}, u32[]{:S(2)}, u32[]{:S(2)}) collective-permute-start(bf16[64,768]{1,0:T(8,128)(2,1)} %get-tuple-element.31), channel_id=1, source_target_pairs={{0,8},{4,12},{8,0},{12,4},{16,24},{20,28},{24,16},{28,20},{1,9},{5... | collective-permute-start | bytes 294920 | tf_op jit(solution)/shard_map/ppermute | solution.py:20
  5.8 22.1 %collective-permute-start = (s32[4,4]{1,0:T(4,128)}, s32[4,4]{1,0:T(4,128)}, u32[]{:S(2)}, u32[]{:S(2)}) collective-permute-start(s32[4,4]{1,0:T(4,128)} %get-tuple-element.34), channel_id=1, source_target_pairs={{0,4},{4,0},{8,12},{12,8},{16,20},{20,16},{24,28},{28,24},{1,5},{5... | collective-permute-start | bytes 200 | tf_op jit(solution)/shard_map/ppermute | solution.py:20
  10.9 22.1 %collective-permute-start.1 = (bf16[768,768]{0,1:T(8,128)(2,1)}, bf16[768,768]{0,1:T(8,128)(2,1)}, u32[]{:S(2)}, u32[]{:S(2)}) collective-permute-start(bf16[768,768]{0,1:T(8,128)(2,1)} %bitcast.4), channel_id=1, source_target_pairs={{0,4},{4,0},{8,12},{12,8},{16,20},{20,16},{24,28},{28,24},{1,5},{5... | collective-permute-start | bytes 3538952 | tf_op jit(solution)/shard_map/ppermute | solution.py:20
  11.1 28.7 %collective-permute-start.4 = (bf16[768,768]{1,0:T(8,128)(2,1)}, bf16[768,768]{1,0:T(8,128)(2,1)}, u32[]{:S(2)}, u32[]{:S(2)}) collective-permute-start(bf16[768,768]{1,0:T(8,128)(2,1)} %get-tuple-element.22), channel_id=1, source_target_pairs={{0,8},{4,12},{8,0},{12,4},{16,24},{20,28},{24,16},{28,20},{1,9},{5... | collective-permute-start | bytes 3538952 | tf_op jit(solution)/shard_map/ppermute | solution.py:20
  27.9 11.6 %collective-permute-start.3 = (s32[4,4]{1,0:T(4,128)S(1)}, s32[4,4]{1,0:T(4,128)S(1)}, u32[]{:S(2)}, u32[]{:S(2)}) collective-permute-start(s32[4,4]{1,0:T(4,128)S(1)} %get-tuple-element.33), channel_id=1, source_target_pairs={{0,8},{4,12},{8,0},{12,4},{16,24},{20,28},{24,16},{28,20},{1,9},{5... | collective-permute-start | bytes 200 | tf_op jit(solution)/shard_map/ppermute | solution.py:20
  32.9 14.4 %collective-permute-start.22 = (bf16[64,768]{1,0:T(8,128)(2,1)}, bf16[64,768]{1,0:T(8,128)(2,1)}, u32[]{:S(2)}, u32[]{:S(2)}) collective-permute-start(bf16[64,768]{1,0:T(8,128)(2,1)} %get-tuple-element.32), channel_id=1, source_target_pairs={{0,4},{4,0},{8,12},{12,8},{16,20},{20,16},{24,28},{28,24},{1,5},{5... | collective-permute-start | bytes 294920 | tf_op jit(solution)/shard_map/ppermute | solution.py:20
  39.6 9.0 %collective-permute-start.23 = (bf16[64,768]{1,0:T(8,128)(2,1)}, bf16[64,768]{1,0:T(8,128)(2,1)}, u32[]{:S(2)}, u32[]{:S(2)}) collective-permute-start(bf16[64,768]{1,0:T(8,128)(2,1)} %get-tuple-element.32), channel_id=1, source_target_pairs={{0,8},{4,12},{8,0},{12,4},{16,24},{20,28},{24,16},{28,20},{1,9},{5... | collective-permute-start | bytes 294920 | tf_op jit(solution)/shard_map/ppermute | solution.py:20
  45.4 5.3 %collective-permute-start.6 = (bf16[64,768]{1,0:T(8,128)(2,1)S(1)}, bf16[64,768]{1,0:T(8,128)(2,1)S(1)}, u32[]{:S(2)}, u32[]{:S(2)}) collective-permute-start(bf16[64,768]{1,0:T(8,128)(2,1)S(1)} %get-tuple-element.45), channel_id=1, source_target_pairs={{0,4},{4,0},{8,12},{12,8},{16,20},{20,16},{24,28},{28,24},{1,5},{5... | collective-permute-start | bytes 294920 | tf_op jit(solution)/shard_map/ppermute | solution.py:20
  45.5 5.5 %collective-permute-start.7 = (bf16[64,768]{1,0:T(8,128)(2,1)S(1)}, bf16[64,768]{1,0:T(8,128)(2,1)S(1)}, u32[]{:S(2)}, u32[]{:S(2)}) collective-permute-start(bf16[64,768]{1,0:T(8,128)(2,1)S(1)} %get-tuple-element.45), channel_id=1, source_target_pairs={{0,8},{4,12},{8,0},{12,4},{16,24},{20,28},{24,16},{28,20},{1,9},{5... | collective-permute-start | bytes 294920 | tf_op jit(solution)/shard_map/ppermute | solution.py:20
  50.3 7.8 %collective-permute-start.25 = (bf16[64,768]{1,0:T(8,128)(2,1)S(1)}, bf16[64,768]{1,0:T(8,128)(2,1)S(1)}, u32[]{:S(2)}, u32[]{:S(2)}) collective-permute-start(bf16[64,768]{1,0:T(8,128)(2,1)S(1)} %get-tuple-element.35), channel_id=1, source_target_pairs={{0,8},{4,12},{8,0},{12,4},{16,24},{20,28},{24,16},{28,20},{1,9},{5... | collective-permute-start | bytes 294920 | tf_op jit(solution)/shard_map/ppermute | solution.py:20
  51.8 8.7 %collective-permute-start.12 = (bf16[64,768]{1,0:T(8,128)(2,1)S(1)}, bf16[64,768]{1,0:T(8,128)(2,1)S(1)}, u32[]{:S(2)}, u32[]{:S(2)}) collective-permute-start(bf16[64,768]{1,0:T(8,128)(2,1)S(1)} %convert_element_type.168), channel_id=1, source_target_pairs={{0,4},{4,0},{8,12},{12,8},{16,20},{20,16},{24,28},{28,24},{1,5},{5... | collective-permute-start | bytes 294920 | tf_op jit(solution)/shard_map/ppermute | solution.py:20
  52.0 8.9 %collective-permute-start.13 = (bf16[64,768]{1,0:T(8,128)(2,1)S(1)}, bf16[64,768]{1,0:T(8,128)(2,1)S(1)}, u32[]{:S(2)}, u32[]{:S(2)}) collective-permute-start(bf16[64,768]{1,0:T(8,128)(2,1)S(1)} %convert_element_type.168), channel_id=1, source_target_pairs={{0,8},{4,12},{8,0},{12,4},{16,24},{20,28},{24,16},{28,20},{1,9},{5... | collective-permute-start | bytes 294920 | tf_op jit(solution)/shard_map/ppermute | solution.py:20
  53.6 13.8 %collective-permute-start.8 = (bf16[3,256,128]{2,1,0:T(8,128)(2,1)S(1)}, bf16[3,256,128]{2,1,0:T(8,128)(2,1)S(1)}, u32[]{:S(2)}, u32[]{:S(2)}) collective-permute-start(bf16[3,256,128]{2,1,0:T(8,128)(2,1)S(1)} %slice_select_fusion), channel_id=1, source_target_pairs={{0,1},{1,2},{2,3},{3,0},{4,5},{5,6},{6,7},{7,4},{8,9},{9,10},{10,1... | collective-permute-start | bytes 589832 | tf_op jit(solution)/shard_map/ppermute | solution.py:39
  55.2 15.8 %collective-permute-start.9 = (bf16[3,256,128]{2,1,0:T(8,128)(2,1)S(1)}, bf16[3,256,128]{2,1,0:T(8,128)(2,1)S(1)}, u32[]{:S(2)}, u32[]{:S(2)}) collective-permute-start(bf16[3,256,128]{2,1,0:T(8,128)(2,1)S(1)} %slice_select_fusion), channel_id=1, source_target_pairs={{0,2},{1,3},{2,0},{3,1},{4,6},{5,7},{6,4},{7,5},{8,10},{9,11},{10,... | collective-permute-start | bytes 589832 | tf_op jit(solution)/shard_map/ppermute | solution.py:39
  58.1 13.4 %collective-permute-start.10 = (bf16[3,256,128]{2,1,0:T(8,128)(2,1)S(1)}, bf16[3,256,128]{2,1,0:T(8,128)(2,1)S(1)}, u32[]{:S(2)}, u32[]{:S(2)}) collective-permute-start(bf16[3,256,128]{2,1,0:T(8,128)(2,1)S(1)} %slice_select_fusion), channel_id=1, source_target_pairs={{0,3},{1,0},{2,1},{3,2},{4,7},{5,4},{6,5},{7,6},{8,11},{9,8},{10,9... | collective-permute-start | bytes 589832 | tf_op jit(solution)/shard_map/ppermute | solution.py:39
  60.9 5.3 %collective-permute-start.27 = (bf16[64,768]{1,0:T(8,128)(2,1)S(1)}, bf16[64,768]{1,0:T(8,128)(2,1)S(1)}, u32[]{:S(2)}, u32[]{:S(2)}) collective-permute-start(bf16[64,768]{1,0:T(8,128)(2,1)S(1)} %get-tuple-element.37), channel_id=1, source_target_pairs={{0,8},{4,12},{8,0},{12,4},{16,24},{20,28},{24,16},{28,20},{1,9},{5... | collective-permute-start | bytes 294920 | tf_op jit(solution)/shard_map/ppermute | solution.py:20
  61.9 10.5 %collective-permute-start.14 = (bf16[64,768]{1,0:T(8,128)(2,1)S(1)}, bf16[64,768]{1,0:T(8,128)(2,1)S(1)}, u32[]{:S(2)}, u32[]{:S(2)}) collective-permute-start(bf16[64,768]{1,0:T(8,128)(2,1)S(1)} %get-tuple-element.47), channel_id=1, source_target_pairs={{0,4},{4,0},{8,12},{12,8},{16,20},{20,16},{24,28},{28,24},{1,5},{5... | collective-permute-start | bytes 294920 | tf_op jit(solution)/shard_map/ppermute | solution.py:20
  66.1 6.5 %collective-permute-start.15 = (bf16[64,768]{1,0:T(8,128)(2,1)S(1)}, bf16[64,768]{1,0:T(8,128)(2,1)S(1)}, u32[]{:S(2)}, u32[]{:S(2)}) collective-permute-start(bf16[64,768]{1,0:T(8,128)(2,1)S(1)} %get-tuple-element.47), channel_id=1, source_target_pairs={{0,8},{4,12},{8,0},{12,4},{16,24},{20,28},{24,16},{28,20},{1,9},{5... | collective-permute-start | bytes 294920 | tf_op jit(solution)/shard_map/ppermute | solution.py:20
  67.4 8.0 %collective-permute-start.28 = (bf16[64,768]{1,0:T(8,128)(2,1)S(1)}, bf16[64,768]{1,0:T(8,128)(2,1)S(1)}, u32[]{:S(2)}, u32[]{:S(2)}) collective-permute-start(bf16[64,768]{1,0:T(8,128)(2,1)S(1)} %get-tuple-element.39), channel_id=1, source_target_pairs={{0,4},{4,0},{8,12},{12,8},{16,20},{20,16},{24,28},{28,24},{1,5},{5... | collective-permute-start | bytes 294920 | tf_op jit(solution)/shard_map/ppermute | solution.py:20
  72.2 21.7 %collective-permute-start.11 = (bf16[4,3,256,128]{3,2,1,0:T(8,128)(2,1)S(1)}, bf16[4,3,256,128]{3,2,1,0:T(8,128)(2,1)S(1)}, u32[]{:S(2)}, u32[]{:S(2)}) collective-permute-start(bf16[4,3,256,128]{3,2,1,0:T(8,128)(2,1)S(1)} %get-tuple-element.25), channel_id=1, source_target_pairs={{0,4},{4,0},{8,12},{12,8},{16,20},{20,16},{24,28},{28,24},{1,5},{5... | collective-permute-start | bytes 2359304 | tf_op jit(solution)/shard_map/ppermute | solution.py:20
  76.5 5.2 %collective-permute-start.31 = (bf16[64,768]{1,0:T(8,128)(2,1)S(1)}, bf16[64,768]{1,0:T(8,128)(2,1)S(1)}, u32[]{:S(2)}, u32[]{:S(2)}) collective-permute-start(bf16[64,768]{1,0:T(8,128)(2,1)S(1)} %get-tuple-element.41), channel_id=1, source_target_pairs={{0,8},{4,12},{8,0},{12,4},{16,24},{20,28},{24,16},{28,20},{1,9},{5... | collective-permute-start | bytes 294920 | tf_op jit(solution)/shard_map/ppermute | solution.py:20
  79.4 5.2 %collective-permute-start.19 = (bf16[64,768]{1,0:T(8,128)(2,1)S(1)}, bf16[64,768]{1,0:T(8,128)(2,1)S(1)}, u32[]{:S(2)}, u32[]{:S(2)}) collective-permute-start(bf16[64,768]{1,0:T(8,128)(2,1)S(1)} %get-tuple-element.51), channel_id=1, source_target_pairs={{0,8},{4,12},{8,0},{12,4},{16,24},{20,28},{24,16},{28,20},{1,9},{5... | collective-permute-start | bytes 294920 | tf_op jit(solution)/shard_map/ppermute | solution.py:20
  95.6 5.7 %collective-permute-start.37 = (bf16[64,768]{1,0:T(8,128)(2,1)S(1)}, bf16[64,768]{1,0:T(8,128)(2,1)S(1)}, u32[]{:S(2)}, u32[]{:S(2)}) collective-permute-start(bf16[64,768]{1,0:T(8,128)(2,1)S(1)} %convert_element_type.180), channel_id=1, source_target_pairs={{0,8},{4,12},{8,0},{12,4},{16,24},{20,28},{24,16},{28,20},{1,9},{5... | collective-permute-start | bytes 294920 | tf_op jit(solution)/shard_map/ppermute | solution.py:20
  96.7 11.3 %collective-permute-start.41 = (bf16[64,768]{1,0:T(8,128)(2,1)S(1)}, bf16[64,768]{1,0:T(8,128)(2,1)S(1)}, u32[]{:S(2)}, u32[]{:S(2)}) collective-permute-start(bf16[64,768]{1,0:T(8,128)(2,1)S(1)} %convert_element_type.182), channel_id=1, source_target_pairs={{0,4},{4,0},{8,12},{12,8},{16,20},{20,16},{24,28},{28,24},{1,5},{5... | collective-permute-start | bytes 294920 | tf_op jit(solution)/shard_map/ppermute | solution.py:20
  96.9 11.5 %collective-permute-start.42 = (bf16[64,768]{1,0:T(8,128)(2,1)S(1)}, bf16[64,768]{1,0:T(8,128)(2,1)S(1)}, u32[]{:S(2)}, u32[]{:S(2)}) collective-permute-start(bf16[64,768]{1,0:T(8,128)(2,1)S(1)} %convert_element_type.182), channel_id=1, source_target_pairs={{0,8},{4,12},{8,0},{12,4},{16,24},{20,28},{24,16},{28,20},{1,9},{5... | collective-permute-start | bytes 294920 | tf_op jit(solution)/shard_map/ppermute | solution.py:20
  101.6 9.7 %collective-permute-start.38 = (bf16[64,768]{1,0:T(8,128)(2,1)S(1)}, bf16[64,768]{1,0:T(8,128)(2,1)S(1)}, u32[]{:S(2)}, u32[]{:S(2)}) collective-permute-start(bf16[64,768]{1,0:T(8,128)(2,1)S(1)} %fusion.49), channel_id=1, source_target_pairs={{0,1},{1,2},{2,3},{3,0},{4,5},{5,6},{6,7},{7,4},{8,9},{9,10},{10,1... | collective-permute-start | bytes 294920 | tf_op jit(solution)/shard_map/ppermute | solution.py:39
  104.7 11.9 %collective-permute-start.39 = (bf16[64,768]{1,0:T(8,128)(2,1)S(1)}, bf16[64,768]{1,0:T(8,128)(2,1)S(1)}, u32[]{:S(2)}, u32[]{:S(2)}) collective-permute-start(bf16[64,768]{1,0:T(8,128)(2,1)S(1)} %fusion.49), channel_id=1, source_target_pairs={{0,2},{1,3},{2,0},{3,1},{4,6},{5,7},{6,4},{7,5},{8,10},{9,11},{10,... | collective-permute-start | bytes 294920 | tf_op jit(solution)/shard_map/ppermute | solution.py:39
  108.0 8.9 %collective-permute-start.40 = (bf16[64,768]{1,0:T(8,128)(2,1)S(1)}, bf16[64,768]{1,0:T(8,128)(2,1)S(1)}, u32[]{:S(2)}, u32[]{:S(2)}) collective-permute-start(bf16[64,768]{1,0:T(8,128)(2,1)S(1)} %fusion.49), channel_id=1, source_target_pairs={{0,3},{1,0},{2,1},{3,2},{4,7},{5,4},{6,5},{7,6},{8,11},{9,8},{10,9... | collective-permute-start | bytes 294920 | tf_op jit(solution)/shard_map/ppermute | solution.py:39
  108.7 8.8 %collective-permute-start.43 = (bf16[64,768]{1,0:T(8,128)(2,1)S(1)}, bf16[64,768]{1,0:T(8,128)(2,1)S(1)}, u32[]{:S(2)}, u32[]{:S(2)}) collective-permute-start(bf16[64,768]{1,0:T(8,128)(2,1)S(1)} %fusion.50), channel_id=1, source_target_pairs={{0,1},{1,2},{2,3},{3,0},{4,5},{5,6},{6,7},{7,4},{8,9},{9,10},{10,1... | collective-permute-start | bytes 294920 | tf_op jit(solution)/shard_map/ppermute | solution.py:39
  110.8 11.6 %collective-permute-start.44 = (bf16[64,768]{1,0:T(8,128)(2,1)S(1)}, bf16[64,768]{1,0:T(8,128)(2,1)S(1)}, u32[]{:S(2)}, u32[]{:S(2)}) collective-permute-start(bf16[64,768]{1,0:T(8,128)(2,1)S(1)} %fusion.50), channel_id=1, source_target_pairs={{0,2},{1,3},{2,0},{3,1},{4,6},{5,7},{6,4},{7,5},{8,10},{9,11},{10,... | collective-permute-start | bytes 294920 | tf_op jit(solution)/shard_map/ppermute | solution.py:39
  111.3 11.1 %collective-permute-start.45 = (bf16[64,768]{1,0:T(8,128)(2,1)S(1)}, bf16[64,768]{1,0:T(8,128)(2,1)S(1)}, u32[]{:S(2)}, u32[]{:S(2)}) collective-permute-start(bf16[64,768]{1,0:T(8,128)(2,1)S(1)} %fusion.50), channel_id=1, source_target_pairs={{0,3},{1,0},{2,1},{3,2},{4,7},{5,4},{6,5},{7,6},{8,11},{9,8},{10,9... | collective-permute-start | bytes 294920 | tf_op jit(solution)/shard_map/ppermute | solution.py:39
  (38 other events, 114.7 us)

commit v19 on v17

--- a/solution.py
+++ b/solution.py
@@ -6,7 +6,7 @@
 ROUNDS = 2
 DEGREE = 8
 ROTS = 4
-GATHER_AT = 2
+GATHER_AT = 1
 
 
 filter_center = 0.1

time: 165 us -> 166 us (level)
  transfers between devices with their start and end apart: 58 -> 58, of which waited for: 24 -> 26; matrix products, arithmetic and copies ran while one was open for 32% -> 31% of each run, Pallas kernels for 0% -> 0%
where the time goes in v19:
time: 166 us; the launch traced here: 165 us
  waiting for transfers between devices  56.2 us (34%)
  starting transfers between devices  45.1 us (27%)
  matrix products  36.7 us (22%)
  local copies, waits for them, and re-layouts  15.4 us (9%)
  other arithmetic  11.2 us (7%)
    ppermute x49, waiting for transfers between devices, swapped(): return lax.ppermute(value, axis, pairs)  38.7 us
    ppermute x49, starting transfers between devices, swapped(): return lax.ppermute(value, axis, pairs)  33.4 us
    dot_general x32, matrix products, apply_operator(): jnp.dot(other_rows, other_pair[round_index], preferred_element_type=jnp.f...  14.5 us
    dot_general x4, matrix products, pattern_mask(): lax.dot_general(per_row.astype(jnp.bfloat16), col_onehot, (((1,), (1,)),...  10.6 us
    ppermute x6, waiting for transfers between devices, gather_bands(): pieces.append(lax.ppermute(value, 'bands', pairs))  10.1 us
    ppermute x3, waiting for transfers between devices, gather_pieces(): pieces.append(lax.ppermute(value, 'bands', pairs))  7.41 us
    ppermute x6, starting transfers between devices, gather_bands(): pieces.append(lax.ppermute(value, 'bands', pairs))  7.08 us
    dot_general x16, matrix products, apply_operator(): result = jnp.dot(values, diag_sym, preferred_element_type=jnp.float32)  6.61 us
  transfers between devices with their start and end apart: 58, of which 26 were waited for; matrix products, arithmetic and copies ran while one was open for 31% of the time, Pallas kernels for 0%

profile of v19, /device:TPU:0, one launch (start us, length us, event | category | flops | bytes accessed | tf_op | source)
XLA Modules:
  0.0 165.3 jit_solution(18119606697156955958)
XLA Ops:
  0.0 1.6 fusion.109
  2.1 2.5 %collective-permute-start.5 = (bf16[64,768]{1,0:T(8,128)(2,1)}, bf16[64,768]{1,0:T(8,128)(2,1)}, u32[]{:S(2)}, u32[]{:S(2)}) collective-permute-start(bf16[64,768]{1,0:T(8,128)(2,1)} %get-tuple-element.26), channel_id=1, source_target_pairs={{0,8},{4,12},{8,0},{12,4},{16,24},{20,28},{24,16},{28,20},{1,9},{5... | collective-permute-start | bytes 294920 | tf_op jit(solution)/shard_map/ppermute | solution.py:20
  4.6 3.3 %slice_bitcast_fusion.1 = (bf16[768,768]{1,0:T(8,128)(2,1)}, bf16[768,768]{0,1:T(8,128)(2,1)}, bf16[1,768,768]{2,1,0:T(8,128)(2,1)S(1)}) fusion(bf16[2,768,768]{2,1,0:T(8,128)(2,1)} %param.10), kind=kLoop, calls=%fused_computation.111 | loop fusion | bytes 5898240 | tf_op jit(solution)/shard_map/squeeze | solution.py:74
  12.6 2.0 %copy.18 = f32[768,768]{1,0:T(8,128)S(1)} copy(f32[768,768]{0,1:T(8,128)} %convert_bitcast_fusion) | data formatting | bytes 4718592 | tf_op jit(solution)/shard_map/convert_element_type | solution.py:85
  15.9 2.3 %fusion.1 = bf16[768,768]{1,0:T(8,128)(2,1)S(1)} fusion(bf16[768,768]{1,0:T(8,128)(2,1)} %param.9, f32[768,768]{1,0:T(8,128)S(1)} %copy.18, s32[768]{0:T(1024)S(1)} %get-tuple-element.57), kind=kLoop, calls=%fused_computation.7 | loop fusion | flops 7667712 | bytes 4721664 | tf_op jit(solution)/shard_map/convert_element_type | solution.py:86
  21.4 3.1 %compare_select_fusion.2 = bf16[768,768]{1,0:T(8,128)(2,1)} fusion(bf16[1,768,768]{1,2,0:T(8,128)(2,1)} %copy.24, s32[768]{0:T(1024)S(1)} %get-tuple-element.57, s32[768]{0:T(1024)S(1)} %convert_reduce_fusion.1, s32[2,4,4]{2,1,0:T(4,128)S(1)} %copy-done.10), kind=kOutput, calls=%fused_computation.13 | convolution fusion | flops 5932048 | bytes 2369536 | tf_op jit(solution)/shard_map/dot_general | solution.py:63
  25.5 1.9 %compare_select_fusion = bf16[768,768]{1,0:T(8,128)(2,1)} fusion(bf16[768,768]{1,0:T(8,128)(2,1)S(1)} %copy.21, s32[768]{0:T(1024)S(1)} %copy-done.11, s32[768]{0:T(1024)S(1)} %get-tuple-element.57, s32[2,4,4]{2,1,0:T(4,128)S(1)} %copy-done.10), kind=kOutput, calls=%fused_computation.11 | convolution fusion | flops 5932048 | bytes 2369536 | tf_op jit(solution)/shard_map/dot_general | solution.py:63
  27.5 2.0 %collective-permute-start.3 = (s32[4,4]{1,0:T(4,128)}, s32[4,4]{1,0:T(4,128)S(1)}, u32[]{:S(2)}, u32[]{:S(2)}) collective-permute-start(s32[4,4]{1,0:T(4,128)} %get-tuple-element.28), channel_id=1, source_target_pairs={{0,8},{4,12},{8,0},{12,4},{16,24},{20,28},{24,16},{28,20},{1,9},{5... | collective-permute-start | bytes 200 | tf_op jit(solution)/shard_map/ppermute | solution.py:20
  29.5 2.9 %fusion.52 = f32[768,768]{1,0:T(8,128)} fusion(s32[768]{0:T(1024)S(1)} %get-tuple-element.57, s32[768]{0:T(1024)S(1)} %convert_reduce_fusion.1, s32[4,4]{1,0:T(4,128)} %collective-permute-done), kind=kOutput, calls=%fused_computation.109 | convolution fusion | flops 4752400 | bytes 2365504 | tf_op jit(solution)/shard_map/dot_general | solution.py:63
  33.9 2.5 %add_convert_fusion.1 = bf16[768,768]{1,0:T(8,128)(2,1)S(1)} fusion(bf16[768,768]{1,0:T(8,128)(2,1)} %compare_select_fusion.2, bf16[768,768]{1,0:T(8,128)(2,1)S(1)} %copy.20, f32[768,768]{1,0:T(8,128)} %fusion.52), kind=kLoop, calls=%fused_computation.10 | loop fusion | flops 3538944 | bytes 5898240 | tf_op jit(solution)/shard_map/convert_element_type | solution.py:98
  36.4 2.5 %collective-permute-done.3 = s32[4,4]{1,0:T(4,128)S(1)} collective-permute-done((s32[4,4]{1,0:T(4,128)}, s32[4,4]{1,0:T(4,128)S(1)}, u32[]{:S(2)}, u32[]{:S(2)}) %collective-permute-start.3) | collective-permute-done | bytes 96 | tf_op jit(solution)/shard_map/ppermute | solution.py:20
  39.2 2.6 %add_convert_fusion = bf16[768,768]{1,0:T(8,128)(2,1)S(1)} fusion(bf16[768,768]{1,0:T(8,128)(2,1)} %compare_select_fusion, bf16[768,768]{1,0:T(8,128)(2,1)} %collective-permute-done.4, s32[768]{0:T(1024)S(1)} %copy-done.12, s32[768]{0:T(1024)S(1)} %get-tuple-element.57, s32[4,4]{1,0:T(4,128)S(1)} %collective-permute-done.3), kind=kOutput, calls=%fused_computation.9 | convolution fusion | flops 8291344 | bytes 3545152 | tf_op jit(solution)/shard_map/dot_general | solution.py:63
  44.9 1.8 %collective-permute-start.11 = (bf16[64,768]{1,0:T(8,128)(2,1)S(1)}, bf16[64,768]{1,0:T(8,128)(2,1)S(1)}, u32[]{:S(2)}, u32[]{:S(2)}) collective-permute-start(bf16[64,768]{1,0:T(8,128)(2,1)S(1)} %convert_element_type.167), channel_id=1, source_target_pairs={{0,8},{4,12},{8,0},{12,4},{16,24},{20,28},{24,16},{28,20},{1,9},{5... | collective-permute-start | bytes 294920 | tf_op jit(solution)/shard_map/ppermute | solution.py:20
  48.0 3.7 %collective-permute-start.8 = (bf16[3,256,128]{2,1,0:T(8,128)(2,1)S(1)}, bf16[3,256,128]{2,1,0:T(8,128)(2,1)S(1)}, u32[]{:S(2)}, u32[]{:S(2)}) collective-permute-start(bf16[3,256,128]{2,1,0:T(8,128)(2,1)S(1)} %slice_select_fusion), channel_id=1, source_target_pairs={{0,3},{1,0},{2,1},{3,2},{4,7},{5,4},{6,5},{7,6},{8,11},{9,8},{10,9... | collective-permute-start | bytes 589832 | tf_op jit(solution)/shard_map/ppermute | solution.py:39
  56.6 3.4 %collective-permute-done.25 = bf16[64,768]{1,0:T(8,128)(2,1)S(1)} collective-permute-done((bf16[64,768]{1,0:T(8,128)(2,1)S(1)}, bf16[64,768]{1,0:T(8,128)(2,1)S(1)}, u32[]{:S(2)}, u32[]{:S(2)}) %collective-permute-start.25) | collective-permute-done | bytes 98336 | tf_op jit(solution)/shard_map/ppermute | solution.py:20
  61.2 7.4 %collective-permute-done.7 = bf16[3,256,128]{2,1,0:T(8,128)(2,1)S(1)} collective-permute-done((bf16[3,256,128]{2,1,0:T(8,128)(2,1)S(1)}, bf16[3,256,128]{2,1,0:T(8,128)(2,1)S(1)}, u32[]{:S(2)}, u32[]{:S(2)}) %collective-permute-start.7) | collective-permute-done | bytes 196640 | tf_op jit(solution)/shard_map/ppermute | solution.py:39
  77.1 1.6 collective-permute-start.17
  94.9 2.3 %collective-permute-done.35 = bf16[64,768]{1,0:T(8,128)(2,1)S(1)} collective-permute-done((bf16[64,768]{1,0:T(8,128)(2,1)S(1)}, bf16[64,768]{1,0:T(8,128)(2,1)S(1)}, u32[]{:S(2)}, u32[]{:S(2)}) %collective-permute-start.35) | collective-permute-done | bytes 98336 | tf_op jit(solution)/shard_map/ppermute | solution.py:20
  101.1 2.6 %collective-permute-done.37 = bf16[64,768]{1,0:T(8,128)(2,1)S(1)} collective-permute-done((bf16[64,768]{1,0:T(8,128)(2,1)S(1)}, bf16[64,768]{1,0:T(8,128)(2,1)S(1)}, u32[]{:S(2)}, u32[]{:S(2)}) %collective-permute-start.37) | collective-permute-done | bytes 98336 | tf_op jit(solution)/shard_map/ppermute | solution.py:20
  105.3 1.9 %collective-permute-start.38 = (bf16[64,768]{1,0:T(8,128)(2,1)S(1)}, bf16[64,768]{1,0:T(8,128)(2,1)S(1)}, u32[]{:S(2)}, u32[]{:S(2)}) collective-permute-start(bf16[64,768]{1,0:T(8,128)(2,1)S(1)} %fusion.50), channel_id=1, source_target_pairs={{0,1},{1,2},{2,3},{3,0},{4,5},{5,6},{6,7},{7,4},{8,9},{9,10},{10,1... | collective-permute-start | bytes 294920 | tf_op jit(solution)/shard_map/ppermute | solution.py:29
  107.9 1.9 %collective-permute-start.45 = (bf16[64,768]{1,0:T(8,128)(2,1)S(1)}, bf16[64,768]{1,0:T(8,128)(2,1)S(1)}, u32[]{:S(2)}, u32[]{:S(2)}) collective-permute-start(bf16[64,768]{1,0:T(8,128)(2,1)S(1)} %fusion.51), channel_id=1, source_target_pairs={{0,3},{1,0},{2,1},{3,2},{4,7},{5,4},{6,5},{7,6},{8,11},{9,8},{10,9... | collective-permute-start | bytes 294920 | tf_op jit(solution)/shard_map/ppermute | solution.py:29
  110.2 1.7 %collective-permute-start.43 = (bf16[64,768]{1,0:T(8,128)(2,1)S(1)}, bf16[64,768]{1,0:T(8,128)(2,1)S(1)}, u32[]{:S(2)}, u32[]{:S(2)}) collective-permute-start(bf16[64,768]{1,0:T(8,128)(2,1)S(1)} %fusion.51), channel_id=1, source_target_pairs={{0,1},{1,2},{2,3},{3,0},{4,5},{5,6},{6,7},{7,4},{8,9},{9,10},{10,1... | collective-permute-start | bytes 294920 | tf_op jit(solution)/shard_map/ppermute | solution.py:29
  111.9 4.1 %collective-permute-done.39 = bf16[64,768]{1,0:T(8,128)(2,1)S(1)} collective-permute-done((bf16[64,768]{1,0:T(8,128)(2,1)S(1)}, bf16[64,768]{1,0:T(8,128)(2,1)S(1)}, u32[]{:S(2)}, u32[]{:S(2)}) %collective-permute-start.39) | collective-permute-done | bytes 98336 | tf_op jit(solution)/shard_map/ppermute | solution.py:29
  116.6 5.9 %collective-permute-done.44 = bf16[64,768]{1,0:T(8,128)(2,1)S(1)} collective-permute-done((bf16[64,768]{1,0:T(8,128)(2,1)S(1)}, bf16[64,768]{1,0:T(8,128)(2,1)S(1)}, u32[]{:S(2)}, u32[]{:S(2)}) %collective-permute-start.44) | collective-permute-done | bytes 98336 | tf_op jit(solution)/shard_map/ppermute | solution.py:29
  128.7 2.3 %collective-permute-done.47 = f32[512]{0:T(512)S(1)} collective-permute-done((f32[512]{0:T(512)S(1)}, f32[512]{0:T(512)S(1)}, u32[]{:S(2)}, u32[]{:S(2)}) %collective-permute-start.47) | collective-permute-done | bytes 2080 | tf_op jit(solution)/shard_map/ppermute | solution.py:20
  132.6 2.1 %collective-permute-done.48 = f32[512]{0:T(512)S(1)} collective-permute-done((f32[512]{0:T(512)S(1)}, f32[512]{0:T(512)S(1)}, u32[]{:S(2)}, u32[]{:S(2)}) %collective-permute-start.48) | collective-permute-done | bytes 2080 | tf_op jit(solution)/shard_map/ppermute | solution.py:20
  138.7 2.3 %collective-permute-done.50 = f32[512]{0:T(512)S(1)} collective-permute-done((f32[512]{0:T(512)S(1)}, f32[512]{0:T(512)S(1)}, u32[]{:S(2)}, u32[]{:S(2)}) %collective-permute-start.50) | collective-permute-done | bytes 2080 | tf_op jit(solution)/shard_map/ppermute | solution.py:20
  142.6 2.1 %collective-permute-done.51 = f32[512]{0:T(512)S(1)} collective-permute-done((f32[512]{0:T(512)S(1)}, f32[512]{0:T(512)S(1)}, u32[]{:S(2)}, u32[]{:S(2)}) %collective-permute-start.51) | collective-permute-done | bytes 2080 | tf_op jit(solution)/shard_map/ppermute | solution.py:20
  148.7 2.3 %collective-permute-done.53 = f32[512]{0:T(512)S(1)} collective-permute-done((f32[512]{0:T(512)S(1)}, f32[512]{0:T(512)S(1)}, u32[]{:S(2)}, u32[]{:S(2)}) %collective-permute-start.53) | collective-permute-done | bytes 2080 | tf_op jit(solution)/shard_map/ppermute | solution.py:20
  152.5 2.1 %collective-permute-done.54 = f32[512]{0:T(512)S(1)} collective-permute-done((f32[512]{0:T(512)S(1)}, f32[512]{0:T(512)S(1)}, u32[]{:S(2)}, u32[]{:S(2)}) %collective-permute-start.54) | collective-permute-done | bytes 2080 | tf_op jit(solution)/shard_map/ppermute | solution.py:20
  158.5 2.3 %collective-permute-done.56 = f32[128]{0:T(128)S(1)} collective-permute-done((f32[128]{0:T(128)S(1)}, f32[128]{0:T(128)S(1)}, u32[]{:S(2)}, u32[]{:S(2)}) %collective-permute-start.56) | collective-permute-done | bytes 544 | tf_op jit(solution)/shard_map/ppermute | solution.py:20
  162.3 2.0 %collective-permute-done.57 = f32[128]{0:T(128)S(1)} collective-permute-done((f32[128]{0:T(128)S(1)}, f32[128]{0:T(128)S(1)}, u32[]{:S(2)}, u32[]{:S(2)}) %collective-permute-start.57) | collective-permute-done | bytes 544 | tf_op jit(solution)/shard_map/ppermute | solution.py:20
  (230 shorter events, 79.4 us)
Async XLA Ops:
  1.6 40.2 %collective-permute-start.2 = (bf16[64,768]{1,0:T(8,128)(2,1)}, bf16[64,768]{1,0:T(8,128)(2,1)}, u32[]{:S(2)}, u32[]{:S(2)}) collective-permute-start(bf16[64,768]{1,0:T(8,128)(2,1)} %get-tuple-element.26), channel_id=1, source_target_pairs={{0,4},{4,0},{8,12},{12,8},{16,20},{20,16},{24,28},{28,24},{1,5},{5... | collective-permute-start | bytes 294920 | tf_op jit(solution)/shard_map/ppermute | solution.py:20
  2.1 41.1 %collective-permute-start.5 = (bf16[64,768]{1,0:T(8,128)(2,1)}, bf16[64,768]{1,0:T(8,128)(2,1)}, u32[]{:S(2)}, u32[]{:S(2)}) collective-permute-start(bf16[64,768]{1,0:T(8,128)(2,1)} %get-tuple-element.26), channel_id=1, source_target_pairs={{0,8},{4,12},{8,0},{12,4},{16,24},{20,28},{24,16},{28,20},{1,9},{5... | collective-permute-start | bytes 294920 | tf_op jit(solution)/shard_map/ppermute | solution.py:20
  9.4 23.0 %collective-permute-start.1 = (bf16[768,768]{0,1:T(8,128)(2,1)}, bf16[768,768]{0,1:T(8,128)(2,1)}, u32[]{:S(2)}, u32[]{:S(2)}) collective-permute-start(bf16[768,768]{0,1:T(8,128)(2,1)} %bitcast.4), channel_id=1, source_target_pairs={{0,4},{4,0},{8,12},{12,8},{16,20},{20,16},{24,28},{28,24},{1,5},{5... | collective-permute-start | bytes 3538952 | tf_op jit(solution)/shard_map/ppermute | solution.py:20
  10.2 17.3 %collective-permute-start = (s32[4,4]{1,0:T(4,128)}, s32[4,4]{1,0:T(4,128)}, u32[]{:S(2)}, u32[]{:S(2)}) collective-permute-start(s32[4,4]{1,0:T(4,128)} %get-tuple-element.29), channel_id=1, source_target_pairs={{0,4},{4,0},{8,12},{12,8},{16,20},{20,16},{24,28},{28,24},{1,5},{5... | collective-permute-start | bytes 200 | tf_op jit(solution)/shard_map/ppermute | solution.py:20
  10.5 28.7 %collective-permute-start.4 = (bf16[768,768]{1,0:T(8,128)(2,1)}, bf16[768,768]{1,0:T(8,128)(2,1)}, u32[]{:S(2)}, u32[]{:S(2)}) collective-permute-start(bf16[768,768]{1,0:T(8,128)(2,1)} %get-tuple-element.21), channel_id=1, source_target_pairs={{0,8},{4,12},{8,0},{12,4},{16,24},{20,28},{24,16},{28,20},{1,9},{5... | collective-permute-start | bytes 3538952 | tf_op jit(solution)/shard_map/ppermute | solution.py:20
  27.5 11.4 %collective-permute-start.3 = (s32[4,4]{1,0:T(4,128)}, s32[4,4]{1,0:T(4,128)S(1)}, u32[]{:S(2)}, u32[]{:S(2)}) collective-permute-start(s32[4,4]{1,0:T(4,128)} %get-tuple-element.28), channel_id=1, source_target_pairs={{0,8},{4,12},{8,0},{12,4},{16,24},{20,28},{24,16},{28,20},{1,9},{5... | collective-permute-start | bytes 200 | tf_op jit(solution)/shard_map/ppermute | solution.py:20
  32.4 14.3 %collective-permute-start.22 = (bf16[64,768]{1,0:T(8,128)(2,1)}, bf16[64,768]{1,0:T(8,128)(2,1)}, u32[]{:S(2)}, u32[]{:S(2)}) collective-permute-start(bf16[64,768]{1,0:T(8,128)(2,1)} %get-tuple-element.27), channel_id=1, source_target_pairs={{0,4},{4,0},{8,12},{12,8},{16,20},{20,16},{24,28},{28,24},{1,5},{5... | collective-permute-start | bytes 294920 | tf_op jit(solution)/shard_map/ppermute | solution.py:20
  38.9 12.7 %collective-permute-start.23 = (bf16[64,768]{1,0:T(8,128)(2,1)}, bf16[64,768]{1,0:T(8,128)(2,1)}, u32[]{:S(2)}, u32[]{:S(2)}) collective-permute-start(bf16[64,768]{1,0:T(8,128)(2,1)} %get-tuple-element.27), channel_id=1, source_target_pairs={{0,8},{4,12},{8,0},{12,4},{16,24},{20,28},{24,16},{28,20},{1,9},{5... | collective-permute-start | bytes 294920 | tf_op jit(solution)/shard_map/ppermute | solution.py:20
  44.8 9.4 %collective-permute-start.10 = (bf16[64,768]{1,0:T(8,128)(2,1)S(1)}, bf16[64,768]{1,0:T(8,128)(2,1)S(1)}, u32[]{:S(2)}, u32[]{:S(2)}) collective-permute-start(bf16[64,768]{1,0:T(8,128)(2,1)S(1)} %convert_element_type.167), channel_id=1, source_target_pairs={{0,4},{4,0},{8,12},{12,8},{16,20},{20,16},{24,28},{28,24},{1,5},{5... | collective-permute-start | bytes 294920 | tf_op jit(solution)/shard_map/ppermute | solution.py:20
  44.9 9.8 %collective-permute-start.11 = (bf16[64,768]{1,0:T(8,128)(2,1)S(1)}, bf16[64,768]{1,0:T(8,128)(2,1)S(1)}, u32[]{:S(2)}, u32[]{:S(2)}) collective-permute-start(bf16[64,768]{1,0:T(8,128)(2,1)S(1)} %convert_element_type.167), channel_id=1, source_target_pairs={{0,8},{4,12},{8,0},{12,4},{16,24},{20,28},{24,16},{28,20},{1,9},{5... | collective-permute-start | bytes 294920 | tf_op jit(solution)/shard_map/ppermute | solution.py:20
  48.0 13.2 %collective-permute-start.8 = (bf16[3,256,128]{2,1,0:T(8,128)(2,1)S(1)}, bf16[3,256,128]{2,1,0:T(8,128)(2,1)S(1)}, u32[]{:S(2)}, u32[]{:S(2)}) collective-permute-start(bf16[3,256,128]{2,1,0:T(8,128)(2,1)S(1)} %slice_select_fusion), channel_id=1, source_target_pairs={{0,3},{1,0},{2,1},{3,2},{4,7},{5,4},{6,5},{7,6},{8,11},{9,8},{10,9... | collective-permute-start | bytes 589832 | tf_op jit(solution)/shard_map/ppermute | solution.py:39
  51.6 17.0 %collective-permute-start.7 = (bf16[3,256,128]{2,1,0:T(8,128)(2,1)S(1)}, bf16[3,256,128]{2,1,0:T(8,128)(2,1)S(1)}, u32[]{:S(2)}, u32[]{:S(2)}) collective-permute-start(bf16[3,256,128]{2,1,0:T(8,128)(2,1)S(1)} %slice_select_fusion), channel_id=1, source_target_pairs={{0,2},{1,3},{2,0},{3,1},{4,6},{5,7},{6,4},{7,5},{8,10},{9,11},{10,... | collective-permute-start | bytes 589832 | tf_op jit(solution)/shard_map/ppermute | solution.py:39
  51.6 17.6 %collective-permute-start.6 = (bf16[3,256,128]{2,1,0:T(8,128)(2,1)S(1)}, bf16[3,256,128]{2,1,0:T(8,128)(2,1)S(1)}, u32[]{:S(2)}, u32[]{:S(2)}) collective-permute-start(bf16[3,256,128]{2,1,0:T(8,128)(2,1)S(1)} %slice_select_fusion), channel_id=1, source_target_pairs={{0,1},{1,2},{2,3},{3,0},{4,5},{5,6},{6,7},{7,4},{8,9},{9,10},{10,1... | collective-permute-start | bytes 589832 | tf_op jit(solution)/shard_map/ppermute | solution.py:39
  54.7 5.3 %collective-permute-start.25 = (bf16[64,768]{1,0:T(8,128)(2,1)S(1)}, bf16[64,768]{1,0:T(8,128)(2,1)S(1)}, u32[]{:S(2)}, u32[]{:S(2)}) collective-permute-start(bf16[64,768]{1,0:T(8,128)(2,1)S(1)} %get-tuple-element.42), channel_id=1, source_target_pairs={{0,8},{4,12},{8,0},{12,4},{16,24},{20,28},{24,16},{28,20},{1,9},{5... | collective-permute-start | bytes 294920 | tf_op jit(solution)/shard_map/ppermute | solution.py:20
  55.6 14.4 %collective-permute-start.12 = (bf16[64,768]{1,0:T(8,128)(2,1)S(1)}, bf16[64,768]{1,0:T(8,128)(2,1)S(1)}, u32[]{:S(2)}, u32[]{:S(2)}) collective-permute-start(bf16[64,768]{1,0:T(8,128)(2,1)S(1)} %get-tuple-element.32), channel_id=1, source_target_pairs={{0,4},{4,0},{8,12},{12,8},{16,20},{20,16},{24,28},{28,24},{1,5},{5... | collective-permute-start | bytes 294920 | tf_op jit(solution)/shard_map/ppermute | solution.py:20
  59.9 10.4 %collective-permute-start.13 = (bf16[64,768]{1,0:T(8,128)(2,1)S(1)}, bf16[64,768]{1,0:T(8,128)(2,1)S(1)}, u32[]{:S(2)}, u32[]{:S(2)}) collective-permute-start(bf16[64,768]{1,0:T(8,128)(2,1)S(1)} %get-tuple-element.32), channel_id=1, source_target_pairs={{0,8},{4,12},{8,0},{12,4},{16,24},{20,28},{24,16},{28,20},{1,9},{5... | collective-permute-start | bytes 294920 | tf_op jit(solution)/shard_map/ppermute | solution.py:20
  61.2 11.9 %collective-permute-start.26 = (bf16[64,768]{1,0:T(8,128)(2,1)S(1)}, bf16[64,768]{1,0:T(8,128)(2,1)S(1)}, u32[]{:S(2)}, u32[]{:S(2)}) collective-permute-start(bf16[64,768]{1,0:T(8,128)(2,1)S(1)} %get-tuple-element.44), channel_id=1, source_target_pairs={{0,4},{4,0},{8,12},{12,8},{16,20},{20,16},{24,28},{28,24},{1,5},{5... | collective-permute-start | bytes 294920 | tf_op jit(solution)/shard_map/ppermute | solution.py:20
  69.9 27.6 %collective-permute-start.9 = (bf16[4,3,256,128]{3,2,1,0:T(8,128)(2,1)S(1)}, bf16[4,3,256,128]{3,2,1,0:T(8,128)(2,1)S(1)}, u32[]{:S(2)}, u32[]{:S(2)}) collective-permute-start(bf16[4,3,256,128]{3,2,1,0:T(8,128)(2,1)S(1)} %get-tuple-element.24), channel_id=1, source_target_pairs={{0,4},{4,0},{8,12},{12,8},{16,20},{20,16},{24,28},{28,24},{1,5},{5... | collective-permute-start | bytes 2359304 | tf_op jit(solution)/shard_map/ppermute | solution.py:20
  74.1 5.2 %collective-permute-start.29 = (bf16[64,768]{1,0:T(8,128)(2,1)S(1)}, bf16[64,768]{1,0:T(8,128)(2,1)S(1)}, u32[]{:S(2)}, u32[]{:S(2)}) collective-permute-start(bf16[64,768]{1,0:T(8,128)(2,1)S(1)} %get-tuple-element.46), channel_id=1, source_target_pairs={{0,8},{4,12},{8,0},{12,4},{16,24},{20,28},{24,16},{28,20},{1,9},{5... | collective-permute-start | bytes 294920 | tf_op jit(solution)/shard_map/ppermute | solution.py:20
  77.1 5.2 %collective-permute-start.17 = (bf16[64,768]{1,0:T(8,128)(2,1)S(1)}, bf16[64,768]{1,0:T(8,128)(2,1)S(1)}, u32[]{:S(2)}, u32[]{:S(2)}) collective-permute-start(bf16[64,768]{1,0:T(8,128)(2,1)S(1)} %get-tuple-element.36), channel_id=1, source_target_pairs={{0,8},{4,12},{8,0},{12,4},{16,24},{20,28},{24,16},{28,20},{1,9},{5... | collective-permute-start | bytes 294920 | tf_op jit(solution)/shard_map/ppermute | solution.py:20
  80.1 5.2 %collective-permute-start.31 = (bf16[64,768]{1,0:T(8,128)(2,1)S(1)}, bf16[64,768]{1,0:T(8,128)(2,1)S(1)}, u32[]{:S(2)}, u32[]{:S(2)}) collective-permute-start(bf16[64,768]{1,0:T(8,128)(2,1)S(1)} %get-tuple-element.48), channel_id=1, source_target_pairs={{0,8},{4,12},{8,0},{12,4},{16,24},{20,28},{24,16},{28,20},{1,9},{5... | collective-permute-start | bytes 294920 | tf_op jit(solution)/shard_map/ppermute | solution.py:20
  86.0 5.2 %collective-permute-start.33 = (bf16[64,768]{1,0:T(8,128)(2,1)S(1)}, bf16[64,768]{1,0:T(8,128)(2,1)S(1)}, u32[]{:S(2)}, u32[]{:S(2)}) collective-permute-start(bf16[64,768]{1,0:T(8,128)(2,1)S(1)} %get-tuple-element.50), channel_id=1, source_target_pairs={{0,8},{4,12},{8,0},{12,4},{16,24},{20,28},{24,16},{28,20},{1,9},{5... | collective-permute-start | bytes 294920 | tf_op jit(solution)/shard_map/ppermute | solution.py:20
  89.0 5.2 %collective-permute-start.21 = (bf16[64,768]{1,0:T(8,128)(2,1)S(1)}, bf16[64,768]{1,0:T(8,128)(2,1)S(1)}, u32[]{:S(2)}, u32[]{:S(2)}) collective-permute-start(bf16[64,768]{1,0:T(8,128)(2,1)S(1)} %get-tuple-element.40), channel_id=1, source_target_pairs={{0,8},{4,12},{8,0},{12,4},{16,24},{20,28},{24,16},{28,20},{1,9},{5... | collective-permute-start | bytes 294920 | tf_op jit(solution)/shard_map/ppermute | solution.py:20
  98.1 5.7 %collective-permute-start.37 = (bf16[64,768]{1,0:T(8,128)(2,1)S(1)}, bf16[64,768]{1,0:T(8,128)(2,1)S(1)}, u32[]{:S(2)}, u32[]{:S(2)}) collective-permute-start(bf16[64,768]{1,0:T(8,128)(2,1)S(1)} %convert_element_type.180), channel_id=1, source_target_pairs={{0,8},{4,12},{8,0},{12,4},{16,24},{20,28},{24,16},{28,20},{1,9},{5... | collective-permute-start | bytes 294920 | tf_op jit(solution)/shard_map/ppermute | solution.py:20
  99.1 8.1 %collective-permute-start.41 = (bf16[64,768]{1,0:T(8,128)(2,1)S(1)}, bf16[64,768]{1,0:T(8,128)(2,1)S(1)}, u32[]{:S(2)}, u32[]{:S(2)}) collective-permute-start(bf16[64,768]{1,0:T(8,128)(2,1)S(1)} %convert_element_type.182), channel_id=1, source_target_pairs={{0,4},{4,0},{8,12},{12,8},{16,20},{20,16},{24,28},{28,24},{1,5},{5... | collective-permute-start | bytes 294920 | tf_op jit(solution)/shard_map/ppermute | solution.py:20
  99.3 8.3 %collective-permute-start.42 = (bf16[64,768]{1,0:T(8,128)(2,1)S(1)}, bf16[64,768]{1,0:T(8,128)(2,1)S(1)}, u32[]{:S(2)}, u32[]{:S(2)}) collective-permute-start(bf16[64,768]{1,0:T(8,128)(2,1)S(1)} %convert_element_type.182), channel_id=1, source_target_pairs={{0,8},{4,12},{8,0},{12,4},{16,24},{20,28},{24,16},{28,20},{1,9},{5... | collective-permute-start | bytes 294920 | tf_op jit(solution)/shard_map/ppermute | solution.py:20
  104.1 6.1 %collective-permute-start.40 = (bf16[64,768]{1,0:T(8,128)(2,1)S(1)}, bf16[64,768]{1,0:T(8,128)(2,1)S(1)}, u32[]{:S(2)}, u32[]{:S(2)}) collective-permute-start(bf16[64,768]{1,0:T(8,128)(2,1)S(1)} %fusion.50), channel_id=1, source_target_pairs={{0,3},{1,0},{2,1},{3,2},{4,7},{5,4},{6,5},{7,6},{8,11},{9,8},{10,9... | collective-permute-start | bytes 294920 | tf_op jit(solution)/shard_map/ppermute | solution.py:29
  104.5 11.5 %collective-permute-start.39 = (bf16[64,768]{1,0:T(8,128)(2,1)S(1)}, bf16[64,768]{1,0:T(8,128)(2,1)S(1)}, u32[]{:S(2)}, u32[]{:S(2)}) collective-permute-start(bf16[64,768]{1,0:T(8,128)(2,1)S(1)} %fusion.50), channel_id=1, source_target_pairs={{0,2},{1,3},{2,0},{3,1},{4,6},{5,7},{6,4},{7,5},{8,10},{9,11},{10,... | collective-permute-start | bytes 294920 | tf_op jit(solution)/shard_map/ppermute | solution.py:29
  105.3 10.7 %collective-permute-start.38 = (bf16[64,768]{1,0:T(8,128)(2,1)S(1)}, bf16[64,768]{1,0:T(8,128)(2,1)S(1)}, u32[]{:S(2)}, u32[]{:S(2)}) collective-permute-start(bf16[64,768]{1,0:T(8,128)(2,1)S(1)} %fusion.50), channel_id=1, source_target_pairs={{0,1},{1,2},{2,3},{3,0},{4,5},{5,6},{6,7},{7,4},{8,9},{9,10},{10,1... | collective-permute-start | bytes 294920 | tf_op jit(solution)/shard_map/ppermute | solution.py:29
  107.9 8.7 %collective-permute-start.45 = (bf16[64,768]{1,0:T(8,128)(2,1)S(1)}, bf16[64,768]{1,0:T(8,128)(2,1)S(1)}, u32[]{:S(2)}, u32[]{:S(2)}) collective-permute-start(bf16[64,768]{1,0:T(8,128)(2,1)S(1)} %fusion.51), channel_id=1, source_target_pairs={{0,3},{1,0},{2,1},{3,2},{4,7},{5,4},{6,5},{7,6},{8,11},{9,8},{10,9... | collective-permute-start | bytes 294920 | tf_op jit(solution)/shard_map/ppermute | solution.py:29
  109.9 12.7 %collective-permute-start.44 = (bf16[64,768]{1,0:T(8,128)(2,1)S(1)}, bf16[64,768]{1,0:T(8,128)(2,1)S(1)}, u32[]{:S(2)}, u32[]{:S(2)}) collective-permute-start(bf16[64,768]{1,0:T(8,128)(2,1)S(1)} %fusion.51), channel_id=1, source_target_pairs={{0,2},{1,3},{2,0},{3,1},{4,6},{5,7},{6,4},{7,5},{8,10},{9,11},{10,... | collective-permute-start | bytes 294920 | tf_op jit(solution)/shard_map/ppermute | solution.py:29
  110.2 12.4 %collective-permute-start.43 = (bf16[64,768]{1,0:T(8,128)(2,1)S(1)}, bf16[64,768]{1,0:T(8,128)(2,1)S(1)}, u32[]{:S(2)}, u32[]{:S(2)}) collective-permute-start(bf16[64,768]{1,0:T(8,128)(2,1)S(1)} %fusion.51), channel_id=1, source_target_pairs={{0,1},{1,2},{2,3},{3,0},{4,5},{5,6},{6,7},{7,4},{8,9},{9,10},{10,1... | collective-permute-start | bytes 294920 | tf_op jit(solution)/shard_map/ppermute | solution.py:29
  (40 other events, 125.5 us)

commit v20 on v19

--- a/solution.py
+++ b/solution.py
@@ -6,7 +6,7 @@
 ROUNDS = 2
 DEGREE = 8
 ROTS = 4
-GATHER_AT = 1
+GATHER_AT = 3
 
 
 filter_center = 0.1

time: 166 us -> 165 us (level)
  transfers between devices with their start and end apart: 58 -> 58, of which waited for: 26 -> 24; matrix products, arithmetic and copies ran while one was open for 31% -> 32% of each run, Pallas kernels for 0% -> 0%
where the time goes in v20:
time: 165 us
  waiting for transfers between devices  56.3 us (34%)
  starting transfers between devices  44.3 us (27%)
  matrix products  36.7 us (22%)
  local copies, waits for them, and re-layouts  15.4 us (9%)
  other arithmetic  11.2 us (7%)
    ppermute x49, waiting for transfers between devices, swapped(): return lax.ppermute(value, axis, pairs)  38.5 us
    ppermute x49, starting transfers between devices, swapped(): return lax.ppermute(value, axis, pairs)  32.6 us
    dot_general x32, matrix products, apply_operator(): jnp.dot(other_rows, other_pair[round_index], preferred_element_type=jnp.f...  14.5 us
    dot_general x4, matrix products, pattern_mask(): lax.dot_general(per_row.astype(jnp.bfloat16), col_onehot, (((1,), (1,)),...  10.6 us
    ppermute x6, waiting for transfers between devices, gather_bands(): pieces.append(lax.ppermute(value, 'bands', pairs))  10.2 us
    ppermute x3, waiting for transfers between devices, gather_pieces(): pieces.append(lax.ppermute(value, 'bands', pairs))  7.58 us
    ppermute x6, starting transfers between devices, gather_bands(): pieces.append(lax.ppermute(value, 'bands', pairs))  7.08 us
    dot_general x16, matrix products, apply_operator(): result = jnp.dot(values, diag_sym, preferred_element_type=jnp.float32)  6.61 us
  transfers between devices with their start and end apart: 58, of which 24 were waited for; matrix products, arithmetic and copies ran while one was open for 32% of the time, Pallas kernels for 0%

profile of v20, /device:TPU:0, one launch (start us, length us, event | category | flops | bytes accessed | tf_op | source)
XLA Modules:
  0.0 164.6 jit_solution(13501652458369144673)
XLA Ops:
  2.1 2.5 %collective-permute-start.5 = (bf16[64,768]{1,0:T(8,128)(2,1)}, bf16[64,768]{1,0:T(8,128)(2,1)}, u32[]{:S(2)}, u32[]{:S(2)}) collective-permute-start(bf16[64,768]{1,0:T(8,128)(2,1)} %get-tuple-element.26), channel_id=1, source_target_pairs={{0,8},{4,12},{8,0},{12,4},{16,24},{20,28},{24,16},{28,20},{1,9},{5... | collective-permute-start | bytes 294920 | tf_op jit(solution)/shard_map/ppermute | solution.py:20
  4.6 3.3 %slice_bitcast_fusion.1 = (bf16[768,768]{1,0:T(8,128)(2,1)}, bf16[768,768]{0,1:T(8,128)(2,1)}, bf16[1,768,768]{2,1,0:T(8,128)(2,1)S(1)}) fusion(bf16[2,768,768]{2,1,0:T(8,128)(2,1)} %param.10), kind=kLoop, calls=%fused_computation.110 | loop fusion | bytes 5898240 | tf_op jit(solution)/shard_map/squeeze | solution.py:74
  12.6 2.0 %copy.18 = f32[768,768]{1,0:T(8,128)S(1)} copy(f32[768,768]{0,1:T(8,128)} %convert_bitcast_fusion) | data formatting | bytes 4718592 | tf_op jit(solution)/shard_map/convert_element_type | solution.py:85
  15.9 2.3 %fusion.1 = bf16[768,768]{1,0:T(8,128)(2,1)S(1)} fusion(bf16[768,768]{1,0:T(8,128)(2,1)} %param.9, f32[768,768]{1,0:T(8,128)S(1)} %copy.18, s32[768]{0:T(1024)S(1)} %get-tuple-element.57), kind=kLoop, calls=%fused_computation.7 | loop fusion | flops 7667712 | bytes 4721664 | tf_op jit(solution)/shard_map/convert_element_type | solution.py:86
  21.4 3.1 %compare_select_fusion.2 = bf16[768,768]{1,0:T(8,128)(2,1)} fusion(bf16[1,768,768]{1,2,0:T(8,128)(2,1)} %copy.24, s32[768]{0:T(1024)S(1)} %get-tuple-element.57, s32[768]{0:T(1024)S(1)} %convert_reduce_fusion.1, s32[2,4,4]{2,1,0:T(4,128)S(1)} %copy-done.10), kind=kOutput, calls=%fused_computation.13 | convolution fusion | flops 5932048 | bytes 2369536 | tf_op jit(solution)/shard_map/dot_general | solution.py:63
  25.5 1.9 %compare_select_fusion = bf16[768,768]{1,0:T(8,128)(2,1)} fusion(bf16[768,768]{1,0:T(8,128)(2,1)S(1)} %copy.21, s32[768]{0:T(1024)S(1)} %copy-done.11, s32[768]{0:T(1024)S(1)} %get-tuple-element.57, s32[2,4,4]{2,1,0:T(4,128)S(1)} %copy-done.10), kind=kOutput, calls=%fused_computation.11 | convolution fusion | flops 5932048 | bytes 2369536 | tf_op jit(solution)/shard_map/dot_general | solution.py:63
  27.5 2.0 %collective-permute-start.3 = (s32[4,4]{1,0:T(4,128)}, s32[4,4]{1,0:T(4,128)S(1)}, u32[]{:S(2)}, u32[]{:S(2)}) collective-permute-start(s32[4,4]{1,0:T(4,128)} %get-tuple-element.28), channel_id=1, source_target_pairs={{0,8},{4,12},{8,0},{12,4},{16,24},{20,28},{24,16},{28,20},{1,9},{5... | collective-permute-start | bytes 200 | tf_op jit(solution)/shard_map/ppermute | solution.py:20
  29.5 2.9 %fusion.51 = f32[768,768]{1,0:T(8,128)} fusion(s32[768]{0:T(1024)S(1)} %get-tuple-element.57, s32[768]{0:T(1024)S(1)} %convert_reduce_fusion.1, s32[4,4]{1,0:T(4,128)} %collective-permute-done), kind=kOutput, calls=%fused_computation.108 | convolution fusion | flops 4752400 | bytes 2365504 | tf_op jit(solution)/shard_map/dot_general | solution.py:63
  33.9 2.5 %add_convert_fusion.1 = bf16[768,768]{1,0:T(8,128)(2,1)S(1)} fusion(bf16[768,768]{1,0:T(8,128)(2,1)} %compare_select_fusion.2, bf16[768,768]{1,0:T(8,128)(2,1)S(1)} %copy.20, f32[768,768]{1,0:T(8,128)} %fusion.51), kind=kLoop, calls=%fused_computation.10 | loop fusion | flops 3538944 | bytes 5898240 | tf_op jit(solution)/shard_map/convert_element_type | solution.py:98
  36.4 2.5 %collective-permute-done.3 = s32[4,4]{1,0:T(4,128)S(1)} collective-permute-done((s32[4,4]{1,0:T(4,128)}, s32[4,4]{1,0:T(4,128)S(1)}, u32[]{:S(2)}, u32[]{:S(2)}) %collective-permute-start.3) | collective-permute-done | bytes 96 | tf_op jit(solution)/shard_map/ppermute | solution.py:20
  39.2 2.6 %add_convert_fusion = bf16[768,768]{1,0:T(8,128)(2,1)S(1)} fusion(bf16[768,768]{1,0:T(8,128)(2,1)} %compare_select_fusion, bf16[768,768]{1,0:T(8,128)(2,1)} %collective-permute-done.4, s32[768]{0:T(1024)S(1)} %copy-done.12, s32[768]{0:T(1024)S(1)} %get-tuple-element.57, s32[4,4]{1,0:T(4,128)S(1)} %collective-permute-done.3), kind=kOutput, calls=%fused_computation.9 | convolution fusion | flops 8291344 | bytes 3545152 | tf_op jit(solution)/shard_map/dot_general | solution.py:63
  44.8 1.8 %collective-permute-start.7 = (bf16[64,768]{1,0:T(8,128)(2,1)S(1)}, bf16[64,768]{1,0:T(8,128)(2,1)S(1)}, u32[]{:S(2)}, u32[]{:S(2)}) collective-permute-start(bf16[64,768]{1,0:T(8,128)(2,1)S(1)} %get-tuple-element.32), channel_id=1, source_target_pairs={{0,8},{4,12},{8,0},{12,4},{16,24},{20,28},{24,16},{28,20},{1,9},{5... | collective-permute-start | bytes 294920 | tf_op jit(solution)/shard_map/ppermute | solution.py:20
  53.2 2.0 %collective-permute-done.25 = bf16[64,768]{1,0:T(8,128)(2,1)S(1)} collective-permute-done((bf16[64,768]{1,0:T(8,128)(2,1)S(1)}, bf16[64,768]{1,0:T(8,128)(2,1)S(1)}, u32[]{:S(2)}, u32[]{:S(2)}) %collective-permute-start.25) | collective-permute-done | bytes 98336 | tf_op jit(solution)/shard_map/ppermute | solution.py:20
  57.6 1.7 %collective-permute-start.15 = (bf16[64,768]{1,0:T(8,128)(2,1)S(1)}, bf16[64,768]{1,0:T(8,128)(2,1)S(1)}, u32[]{:S(2)}, u32[]{:S(2)}) collective-permute-start(bf16[64,768]{1,0:T(8,128)(2,1)S(1)} %convert_element_type.169), channel_id=1, source_target_pairs={{0,8},{4,12},{8,0},{12,4},{16,24},{20,28},{24,16},{28,20},{1,9},{5... | collective-permute-start | bytes 294920 | tf_op jit(solution)/shard_map/ppermute | solution.py:20
  59.3 3.5 %collective-permute-start.12 = (bf16[3,256,128]{2,1,0:T(8,128)(2,1)S(1)}, bf16[3,256,128]{2,1,0:T(8,128)(2,1)S(1)}, u32[]{:S(2)}, u32[]{:S(2)}) collective-permute-start(bf16[3,256,128]{2,1,0:T(8,128)(2,1)S(1)} %slice_select_fusion), channel_id=1, source_target_pairs={{0,3},{1,0},{2,1},{3,2},{4,7},{5,4},{6,5},{7,6},{8,11},{9,8},{10,9... | collective-permute-start | bytes 589832 | tf_op jit(solution)/shard_map/ppermute | solution.py:39
  67.5 3.3 %collective-permute-done.29 = bf16[64,768]{1,0:T(8,128)(2,1)S(1)} collective-permute-done((bf16[64,768]{1,0:T(8,128)(2,1)S(1)}, bf16[64,768]{1,0:T(8,128)(2,1)S(1)}, u32[]{:S(2)}, u32[]{:S(2)}) %collective-permute-start.29) | collective-permute-done | bytes 98336 | tf_op jit(solution)/shard_map/ppermute | solution.py:20
  72.1 7.6 %collective-permute-done.11 = bf16[3,256,128]{2,1,0:T(8,128)(2,1)S(1)} collective-permute-done((bf16[3,256,128]{2,1,0:T(8,128)(2,1)S(1)}, bf16[3,256,128]{2,1,0:T(8,128)(2,1)S(1)}, u32[]{:S(2)}, u32[]{:S(2)}) %collective-permute-start.11) | collective-permute-done | bytes 196640 | tf_op jit(solution)/shard_map/ppermute | solution.py:39
  94.2 2.2 %collective-permute-done.35 = bf16[64,768]{1,0:T(8,128)(2,1)S(1)} collective-permute-done((bf16[64,768]{1,0:T(8,128)(2,1)S(1)}, bf16[64,768]{1,0:T(8,128)(2,1)S(1)}, u32[]{:S(2)}, u32[]{:S(2)}) %collective-permute-start.35) | collective-permute-done | bytes 98336 | tf_op jit(solution)/shard_map/ppermute | solution.py:20
  100.3 2.6 %collective-permute-done.37 = bf16[64,768]{1,0:T(8,128)(2,1)S(1)} collective-permute-done((bf16[64,768]{1,0:T(8,128)(2,1)S(1)}, bf16[64,768]{1,0:T(8,128)(2,1)S(1)}, u32[]{:S(2)}, u32[]{:S(2)}) %collective-permute-start.37) | collective-permute-done | bytes 98336 | tf_op jit(solution)/shard_map/ppermute | solution.py:20
  104.6 1.9 %collective-permute-start.38 = (bf16[64,768]{1,0:T(8,128)(2,1)S(1)}, bf16[64,768]{1,0:T(8,128)(2,1)S(1)}, u32[]{:S(2)}, u32[]{:S(2)}) collective-permute-start(bf16[64,768]{1,0:T(8,128)(2,1)S(1)} %fusion.49), channel_id=1, source_target_pairs={{0,1},{1,2},{2,3},{3,0},{4,5},{5,6},{6,7},{7,4},{8,9},{9,10},{10,1... | collective-permute-start | bytes 294920 | tf_op jit(solution)/shard_map/ppermute | solution.py:29
  107.3 1.9 %collective-permute-start.45 = (bf16[64,768]{1,0:T(8,128)(2,1)S(1)}, bf16[64,768]{1,0:T(8,128)(2,1)S(1)}, u32[]{:S(2)}, u32[]{:S(2)}) collective-permute-start(bf16[64,768]{1,0:T(8,128)(2,1)S(1)} %fusion.50), channel_id=1, source_target_pairs={{0,3},{1,0},{2,1},{3,2},{4,7},{5,4},{6,5},{7,6},{8,11},{9,8},{10,9... | collective-permute-start | bytes 294920 | tf_op jit(solution)/shard_map/ppermute | solution.py:29
  109.3 1.7 %collective-permute-start.43 = (bf16[64,768]{1,0:T(8,128)(2,1)S(1)}, bf16[64,768]{1,0:T(8,128)(2,1)S(1)}, u32[]{:S(2)}, u32[]{:S(2)}) collective-permute-start(bf16[64,768]{1,0:T(8,128)(2,1)S(1)} %fusion.50), channel_id=1, source_target_pairs={{0,1},{1,2},{2,3},{3,0},{4,5},{5,6},{6,7},{7,4},{8,9},{9,10},{10,1... | collective-permute-start | bytes 294920 | tf_op jit(solution)/shard_map/ppermute | solution.py:29
  111.0 4.7 %collective-permute-done.39 = bf16[64,768]{1,0:T(8,128)(2,1)S(1)} collective-permute-done((bf16[64,768]{1,0:T(8,128)(2,1)S(1)}, bf16[64,768]{1,0:T(8,128)(2,1)S(1)}, u32[]{:S(2)}, u32[]{:S(2)}) %collective-permute-start.39) | collective-permute-done | bytes 98336 | tf_op jit(solution)/shard_map/ppermute | solution.py:29
  116.4 5.4 %collective-permute-done.44 = bf16[64,768]{1,0:T(8,128)(2,1)S(1)} collective-permute-done((bf16[64,768]{1,0:T(8,128)(2,1)S(1)}, bf16[64,768]{1,0:T(8,128)(2,1)S(1)}, u32[]{:S(2)}, u32[]{:S(2)}) %collective-permute-start.44) | collective-permute-done | bytes 98336 | tf_op jit(solution)/shard_map/ppermute | solution.py:29
  127.9 2.4 %collective-permute-done.47 = f32[512]{0:T(512)S(1)} collective-permute-done((f32[512]{0:T(512)S(1)}, f32[512]{0:T(512)S(1)}, u32[]{:S(2)}, u32[]{:S(2)}) %collective-permute-start.47) | collective-permute-done | bytes 2080 | tf_op jit(solution)/shard_map/ppermute | solution.py:20
  131.9 2.1 %collective-permute-done.48 = f32[512]{0:T(512)S(1)} collective-permute-done((f32[512]{0:T(512)S(1)}, f32[512]{0:T(512)S(1)}, u32[]{:S(2)}, u32[]{:S(2)}) %collective-permute-start.48) | collective-permute-done | bytes 2080 | tf_op jit(solution)/shard_map/ppermute | solution.py:20
  137.9 2.4 %collective-permute-done.50 = f32[512]{0:T(512)S(1)} collective-permute-done((f32[512]{0:T(512)S(1)}, f32[512]{0:T(512)S(1)}, u32[]{:S(2)}, u32[]{:S(2)}) %collective-permute-start.50) | collective-permute-done | bytes 2080 | tf_op jit(solution)/shard_map/ppermute | solution.py:20
  141.9 2.1 %collective-permute-done.51 = f32[512]{0:T(512)S(1)} collective-permute-done((f32[512]{0:T(512)S(1)}, f32[512]{0:T(512)S(1)}, u32[]{:S(2)}, u32[]{:S(2)}) %collective-permute-start.51) | collective-permute-done | bytes 2080 | tf_op jit(solution)/shard_map/ppermute | solution.py:20
  147.9 2.4 %collective-permute-done.53 = f32[512]{0:T(512)S(1)} collective-permute-done((f32[512]{0:T(512)S(1)}, f32[512]{0:T(512)S(1)}, u32[]{:S(2)}, u32[]{:S(2)}) %collective-permute-start.53) | collective-permute-done | bytes 2080 | tf_op jit(solution)/shard_map/ppermute | solution.py:20
  151.8 2.1 %collective-permute-done.54 = f32[512]{0:T(512)S(1)} collective-permute-done((f32[512]{0:T(512)S(1)}, f32[512]{0:T(512)S(1)}, u32[]{:S(2)}, u32[]{:S(2)}) %collective-permute-start.54) | collective-permute-done | bytes 2080 | tf_op jit(solution)/shard_map/ppermute | solution.py:20
  157.7 2.4 %collective-permute-done.56 = f32[128]{0:T(128)S(1)} collective-permute-done((f32[128]{0:T(128)S(1)}, f32[128]{0:T(128)S(1)}, u32[]{:S(2)}, u32[]{:S(2)}) %collective-permute-start.56) | collective-permute-done | bytes 544 | tf_op jit(solution)/shard_map/ppermute | solution.py:20
  161.6 2.0 %collective-permute-done.57 = f32[128]{0:T(128)S(1)} collective-permute-done((f32[128]{0:T(128)S(1)}, f32[128]{0:T(128)S(1)}, u32[]{:S(2)}, u32[]{:S(2)}) %collective-permute-start.57) | collective-permute-done | bytes 544 | tf_op jit(solution)/shard_map/ppermute | solution.py:20
  (230 shorter events, 77.7 us)
Async XLA Ops:
  1.6 40.2 %collective-permute-start.2 = (bf16[64,768]{1,0:T(8,128)(2,1)}, bf16[64,768]{1,0:T(8,128)(2,1)}, u32[]{:S(2)}, u32[]{:S(2)}) collective-permute-start(bf16[64,768]{1,0:T(8,128)(2,1)} %get-tuple-element.26), channel_id=1, source_target_pairs={{0,4},{4,0},{8,12},{12,8},{16,20},{20,16},{24,28},{28,24},{1,5},{5... | collective-permute-start | bytes 294920 | tf_op jit(solution)/shard_map/ppermute | solution.py:20
  2.1 41.1 %collective-permute-start.5 = (bf16[64,768]{1,0:T(8,128)(2,1)}, bf16[64,768]{1,0:T(8,128)(2,1)}, u32[]{:S(2)}, u32[]{:S(2)}) collective-permute-start(bf16[64,768]{1,0:T(8,128)(2,1)} %get-tuple-element.26), channel_id=1, source_target_pairs={{0,8},{4,12},{8,0},{12,4},{16,24},{20,28},{24,16},{28,20},{1,9},{5... | collective-permute-start | bytes 294920 | tf_op jit(solution)/shard_map/ppermute | solution.py:20
  9.4 23.0 %collective-permute-start.1 = (bf16[768,768]{0,1:T(8,128)(2,1)}, bf16[768,768]{0,1:T(8,128)(2,1)}, u32[]{:S(2)}, u32[]{:S(2)}) collective-permute-start(bf16[768,768]{0,1:T(8,128)(2,1)} %bitcast.4), channel_id=1, source_target_pairs={{0,4},{4,0},{8,12},{12,8},{16,20},{20,16},{24,28},{28,24},{1,5},{5... | collective-permute-start | bytes 3538952 | tf_op jit(solution)/shard_map/ppermute | solution.py:20
  10.2 17.3 %collective-permute-start = (s32[4,4]{1,0:T(4,128)}, s32[4,4]{1,0:T(4,128)}, u32[]{:S(2)}, u32[]{:S(2)}) collective-permute-start(s32[4,4]{1,0:T(4,128)} %get-tuple-element.29), channel_id=1, source_target_pairs={{0,4},{4,0},{8,12},{12,8},{16,20},{20,16},{24,28},{28,24},{1,5},{5... | collective-permute-start | bytes 200 | tf_op jit(solution)/shard_map/ppermute | solution.py:20
  10.5 28.7 %collective-permute-start.4 = (bf16[768,768]{1,0:T(8,128)(2,1)}, bf16[768,768]{1,0:T(8,128)(2,1)}, u32[]{:S(2)}, u32[]{:S(2)}) collective-permute-start(bf16[768,768]{1,0:T(8,128)(2,1)} %get-tuple-element.21), channel_id=1, source_target_pairs={{0,8},{4,12},{8,0},{12,4},{16,24},{20,28},{24,16},{28,20},{1,9},{5... | collective-permute-start | bytes 3538952 | tf_op jit(solution)/shard_map/ppermute | solution.py:20
  27.5 11.4 %collective-permute-start.3 = (s32[4,4]{1,0:T(4,128)}, s32[4,4]{1,0:T(4,128)S(1)}, u32[]{:S(2)}, u32[]{:S(2)}) collective-permute-start(s32[4,4]{1,0:T(4,128)} %get-tuple-element.28), channel_id=1, source_target_pairs={{0,8},{4,12},{8,0},{12,4},{16,24},{20,28},{24,16},{28,20},{1,9},{5... | collective-permute-start | bytes 200 | tf_op jit(solution)/shard_map/ppermute | solution.py:20
  32.4 14.3 %collective-permute-start.22 = (bf16[64,768]{1,0:T(8,128)(2,1)}, bf16[64,768]{1,0:T(8,128)(2,1)}, u32[]{:S(2)}, u32[]{:S(2)}) collective-permute-start(bf16[64,768]{1,0:T(8,128)(2,1)} %get-tuple-element.27), channel_id=1, source_target_pairs={{0,4},{4,0},{8,12},{12,8},{16,20},{20,16},{24,28},{28,24},{1,5},{5... | collective-permute-start | bytes 294920 | tf_op jit(solution)/shard_map/ppermute | solution.py:20
  38.9 9.0 %collective-permute-start.23 = (bf16[64,768]{1,0:T(8,128)(2,1)}, bf16[64,768]{1,0:T(8,128)(2,1)}, u32[]{:S(2)}, u32[]{:S(2)}) collective-permute-start(bf16[64,768]{1,0:T(8,128)(2,1)} %get-tuple-element.27), channel_id=1, source_target_pairs={{0,8},{4,12},{8,0},{12,4},{16,24},{20,28},{24,16},{28,20},{1,9},{5... | collective-permute-start | bytes 294920 | tf_op jit(solution)/shard_map/ppermute | solution.py:20
  44.8 5.3 %collective-permute-start.6 = (bf16[64,768]{1,0:T(8,128)(2,1)S(1)}, bf16[64,768]{1,0:T(8,128)(2,1)S(1)}, u32[]{:S(2)}, u32[]{:S(2)}) collective-permute-start(bf16[64,768]{1,0:T(8,128)(2,1)S(1)} %get-tuple-element.32), channel_id=1, source_target_pairs={{0,4},{4,0},{8,12},{12,8},{16,20},{20,16},{24,28},{28,24},{1,5},{5... | collective-permute-start | bytes 294920 | tf_op jit(solution)/shard_map/ppermute | solution.py:20
  44.8 5.5 %collective-permute-start.7 = (bf16[64,768]{1,0:T(8,128)(2,1)S(1)}, bf16[64,768]{1,0:T(8,128)(2,1)S(1)}, u32[]{:S(2)}, u32[]{:S(2)}) collective-permute-start(bf16[64,768]{1,0:T(8,128)(2,1)S(1)} %get-tuple-element.32), channel_id=1, source_target_pairs={{0,8},{4,12},{8,0},{12,4},{16,24},{20,28},{24,16},{28,20},{1,9},{5... | collective-permute-start | bytes 294920 | tf_op jit(solution)/shard_map/ppermute | solution.py:20
  49.7 5.5 %collective-permute-start.25 = (bf16[64,768]{1,0:T(8,128)(2,1)S(1)}, bf16[64,768]{1,0:T(8,128)(2,1)S(1)}, u32[]{:S(2)}, u32[]{:S(2)}) collective-permute-start(bf16[64,768]{1,0:T(8,128)(2,1)S(1)} %get-tuple-element.42), channel_id=1, source_target_pairs={{0,8},{4,12},{8,0},{12,4},{16,24},{20,28},{24,16},{28,20},{1,9},{5... | collective-permute-start | bytes 294920 | tf_op jit(solution)/shard_map/ppermute | solution.py:20
  51.3 5.5 %collective-permute-start.9 = (bf16[64,768]{1,0:T(8,128)(2,1)S(1)}, bf16[64,768]{1,0:T(8,128)(2,1)S(1)}, u32[]{:S(2)}, u32[]{:S(2)}) collective-permute-start(bf16[64,768]{1,0:T(8,128)(2,1)S(1)} %get-tuple-element.34), channel_id=1, source_target_pairs={{0,8},{4,12},{8,0},{12,4},{16,24},{20,28},{24,16},{28,20},{1,9},{5... | collective-permute-start | bytes 294920 | tf_op jit(solution)/shard_map/ppermute | solution.py:20
  55.9 6.9 %collective-permute-start.26 = (bf16[64,768]{1,0:T(8,128)(2,1)S(1)}, bf16[64,768]{1,0:T(8,128)(2,1)S(1)}, u32[]{:S(2)}, u32[]{:S(2)}) collective-permute-start(bf16[64,768]{1,0:T(8,128)(2,1)S(1)} %get-tuple-element.44), channel_id=1, source_target_pairs={{0,4},{4,0},{8,12},{12,8},{16,20},{20,16},{24,28},{28,24},{1,5},{5... | collective-permute-start | bytes 294920 | tf_op jit(solution)/shard_map/ppermute | solution.py:20
  55.9 7.2 %collective-permute-start.27 = (bf16[64,768]{1,0:T(8,128)(2,1)S(1)}, bf16[64,768]{1,0:T(8,128)(2,1)S(1)}, u32[]{:S(2)}, u32[]{:S(2)}) collective-permute-start(bf16[64,768]{1,0:T(8,128)(2,1)S(1)} %get-tuple-element.44), channel_id=1, source_target_pairs={{0,8},{4,12},{8,0},{12,4},{16,24},{20,28},{24,16},{28,20},{1,9},{5... | collective-permute-start | bytes 294920 | tf_op jit(solution)/shard_map/ppermute | solution.py:20
  57.5 7.6 %collective-permute-start.14 = (bf16[64,768]{1,0:T(8,128)(2,1)S(1)}, bf16[64,768]{1,0:T(8,128)(2,1)S(1)}, u32[]{:S(2)}, u32[]{:S(2)}) collective-permute-start(bf16[64,768]{1,0:T(8,128)(2,1)S(1)} %convert_element_type.169), channel_id=1, source_target_pairs={{0,4},{4,0},{8,12},{12,8},{16,20},{20,16},{24,28},{28,24},{1,5},{5... | collective-permute-start | bytes 294920 | tf_op jit(solution)/shard_map/ppermute | solution.py:20
  57.6 7.9 %collective-permute-start.15 = (bf16[64,768]{1,0:T(8,128)(2,1)S(1)}, bf16[64,768]{1,0:T(8,128)(2,1)S(1)}, u32[]{:S(2)}, u32[]{:S(2)}) collective-permute-start(bf16[64,768]{1,0:T(8,128)(2,1)S(1)} %convert_element_type.169), channel_id=1, source_target_pairs={{0,8},{4,12},{8,0},{12,4},{16,24},{20,28},{24,16},{28,20},{1,9},{5... | collective-permute-start | bytes 294920 | tf_op jit(solution)/shard_map/ppermute | solution.py:20
  59.3 12.7 %collective-permute-start.12 = (bf16[3,256,128]{2,1,0:T(8,128)(2,1)S(1)}, bf16[3,256,128]{2,1,0:T(8,128)(2,1)S(1)}, u32[]{:S(2)}, u32[]{:S(2)}) collective-permute-start(bf16[3,256,128]{2,1,0:T(8,128)(2,1)S(1)} %slice_select_fusion), channel_id=1, source_target_pairs={{0,3},{1,0},{2,1},{3,2},{4,7},{5,4},{6,5},{7,6},{8,11},{9,8},{10,9... | collective-permute-start | bytes 589832 | tf_op jit(solution)/shard_map/ppermute | solution.py:39
  62.8 16.9 %collective-permute-start.11 = (bf16[3,256,128]{2,1,0:T(8,128)(2,1)S(1)}, bf16[3,256,128]{2,1,0:T(8,128)(2,1)S(1)}, u32[]{:S(2)}, u32[]{:S(2)}) collective-permute-start(bf16[3,256,128]{2,1,0:T(8,128)(2,1)S(1)} %slice_select_fusion), channel_id=1, source_target_pairs={{0,2},{1,3},{2,0},{3,1},{4,6},{5,7},{6,4},{7,5},{8,10},{9,11},{10,... | collective-permute-start | bytes 589832 | tf_op jit(solution)/shard_map/ppermute | solution.py:39
  63.1 17.2 %collective-permute-start.10 = (bf16[3,256,128]{2,1,0:T(8,128)(2,1)S(1)}, bf16[3,256,128]{2,1,0:T(8,128)(2,1)S(1)}, u32[]{:S(2)}, u32[]{:S(2)}) collective-permute-start(bf16[3,256,128]{2,1,0:T(8,128)(2,1)S(1)} %slice_select_fusion), channel_id=1, source_target_pairs={{0,1},{1,2},{2,3},{3,0},{4,5},{5,6},{6,7},{7,4},{8,9},{9,10},{10,1... | collective-permute-start | bytes 589832 | tf_op jit(solution)/shard_map/ppermute | solution.py:39
  66.5 14.7 %collective-permute-start.16 = (bf16[64,768]{1,0:T(8,128)(2,1)S(1)}, bf16[64,768]{1,0:T(8,128)(2,1)S(1)}, u32[]{:S(2)}, u32[]{:S(2)}) collective-permute-start(bf16[64,768]{1,0:T(8,128)(2,1)S(1)} %get-tuple-element.36), channel_id=1, source_target_pairs={{0,4},{4,0},{8,12},{12,8},{16,20},{20,16},{24,28},{28,24},{1,5},{5... | collective-permute-start | bytes 294920 | tf_op jit(solution)/shard_map/ppermute | solution.py:20
  70.8 10.8 %collective-permute-start.17 = (bf16[64,768]{1,0:T(8,128)(2,1)S(1)}, bf16[64,768]{1,0:T(8,128)(2,1)S(1)}, u32[]{:S(2)}, u32[]{:S(2)}) collective-permute-start(bf16[64,768]{1,0:T(8,128)(2,1)S(1)} %get-tuple-element.36), channel_id=1, source_target_pairs={{0,8},{4,12},{8,0},{12,4},{16,24},{20,28},{24,16},{28,20},{1,9},{5... | collective-permute-start | bytes 294920 | tf_op jit(solution)/shard_map/ppermute | solution.py:20
  72.0 12.1 %collective-permute-start.30 = (bf16[64,768]{1,0:T(8,128)(2,1)S(1)}, bf16[64,768]{1,0:T(8,128)(2,1)S(1)}, u32[]{:S(2)}, u32[]{:S(2)}) collective-permute-start(bf16[64,768]{1,0:T(8,128)(2,1)S(1)} %get-tuple-element.48), channel_id=1, source_target_pairs={{0,4},{4,0},{8,12},{12,8},{16,20},{20,16},{24,28},{28,24},{1,5},{5... | collective-permute-start | bytes 294920 | tf_op jit(solution)/shard_map/ppermute | solution.py:20
  81.1 15.6 %collective-permute-start.13 = (bf16[4,3,256,128]{3,2,1,0:T(8,128)(2,1)S(1)}, bf16[4,3,256,128]{3,2,1,0:T(8,128)(2,1)S(1)}, u32[]{:S(2)}, u32[]{:S(2)}) collective-permute-start(bf16[4,3,256,128]{3,2,1,0:T(8,128)(2,1)S(1)} %get-tuple-element.24), channel_id=1, source_target_pairs={{0,4},{4,0},{8,12},{12,8},{16,20},{20,16},{24,28},{28,24},{1,5},{5... | collective-permute-start | bytes 2359304 | tf_op jit(solution)/shard_map/ppermute | solution.py:20
  97.2 5.7 %collective-permute-start.37 = (bf16[64,768]{1,0:T(8,128)(2,1)S(1)}, bf16[64,768]{1,0:T(8,128)(2,1)S(1)}, u32[]{:S(2)}, u32[]{:S(2)}) collective-permute-start(bf16[64,768]{1,0:T(8,128)(2,1)S(1)} %convert_element_type.180), channel_id=1, source_target_pairs={{0,8},{4,12},{8,0},{12,4},{16,24},{20,28},{24,16},{28,20},{1,9},{5... | collective-permute-start | bytes 294920 | tf_op jit(solution)/shard_map/ppermute | solution.py:20
  98.3 8.2 %collective-permute-start.41 = (bf16[64,768]{1,0:T(8,128)(2,1)S(1)}, bf16[64,768]{1,0:T(8,128)(2,1)S(1)}, u32[]{:S(2)}, u32[]{:S(2)}) collective-permute-start(bf16[64,768]{1,0:T(8,128)(2,1)S(1)} %convert_element_type.182), channel_id=1, source_target_pairs={{0,4},{4,0},{8,12},{12,8},{16,20},{20,16},{24,28},{28,24},{1,5},{5... | collective-permute-start | bytes 294920 | tf_op jit(solution)/shard_map/ppermute | solution.py:20
  98.6 8.3 %collective-permute-start.42 = (bf16[64,768]{1,0:T(8,128)(2,1)S(1)}, bf16[64,768]{1,0:T(8,128)(2,1)S(1)}, u32[]{:S(2)}, u32[]{:S(2)}) collective-permute-start(bf16[64,768]{1,0:T(8,128)(2,1)S(1)} %convert_element_type.182), channel_id=1, source_target_pairs={{0,8},{4,12},{8,0},{12,4},{16,24},{20,28},{24,16},{28,20},{1,9},{5... | collective-permute-start | bytes 294920 | tf_op jit(solution)/shard_map/ppermute | solution.py:20
  103.2 6.1 %collective-permute-start.40 = (bf16[64,768]{1,0:T(8,128)(2,1)S(1)}, bf16[64,768]{1,0:T(8,128)(2,1)S(1)}, u32[]{:S(2)}, u32[]{:S(2)}) collective-permute-start(bf16[64,768]{1,0:T(8,128)(2,1)S(1)} %fusion.49), channel_id=1, source_target_pairs={{0,3},{1,0},{2,1},{3,2},{4,7},{5,4},{6,5},{7,6},{8,11},{9,8},{10,9... | collective-permute-start | bytes 294920 | tf_op jit(solution)/shard_map/ppermute | solution.py:29
  103.6 12.1 %collective-permute-start.39 = (bf16[64,768]{1,0:T(8,128)(2,1)S(1)}, bf16[64,768]{1,0:T(8,128)(2,1)S(1)}, u32[]{:S(2)}, u32[]{:S(2)}) collective-permute-start(bf16[64,768]{1,0:T(8,128)(2,1)S(1)} %fusion.49), channel_id=1, source_target_pairs={{0,2},{1,3},{2,0},{3,1},{4,6},{5,7},{6,4},{7,5},{8,10},{9,11},{10,... | collective-permute-start | bytes 294920 | tf_op jit(solution)/shard_map/ppermute | solution.py:29
  104.6 11.2 %collective-permute-start.38 = (bf16[64,768]{1,0:T(8,128)(2,1)S(1)}, bf16[64,768]{1,0:T(8,128)(2,1)S(1)}, u32[]{:S(2)}, u32[]{:S(2)}) collective-permute-start(bf16[64,768]{1,0:T(8,128)(2,1)S(1)} %fusion.49), channel_id=1, source_target_pairs={{0,1},{1,2},{2,3},{3,0},{4,5},{5,6},{6,7},{7,4},{8,9},{9,10},{10,1... | collective-permute-start | bytes 294920 | tf_op jit(solution)/shard_map/ppermute | solution.py:29
  107.3 9.2 %collective-permute-start.45 = (bf16[64,768]{1,0:T(8,128)(2,1)S(1)}, bf16[64,768]{1,0:T(8,128)(2,1)S(1)}, u32[]{:S(2)}, u32[]{:S(2)}) collective-permute-start(bf16[64,768]{1,0:T(8,128)(2,1)S(1)} %fusion.50), channel_id=1, source_target_pairs={{0,3},{1,0},{2,1},{3,2},{4,7},{5,4},{6,5},{7,6},{8,11},{9,8},{10,9... | collective-permute-start | bytes 294920 | tf_op jit(solution)/shard_map/ppermute | solution.py:29
  109.2 12.7 %collective-permute-start.44 = (bf16[64,768]{1,0:T(8,128)(2,1)S(1)}, bf16[64,768]{1,0:T(8,128)(2,1)S(1)}, u32[]{:S(2)}, u32[]{:S(2)}) collective-permute-start(bf16[64,768]{1,0:T(8,128)(2,1)S(1)} %fusion.50), channel_id=1, source_target_pairs={{0,2},{1,3},{2,0},{3,1},{4,6},{5,7},{6,4},{7,5},{8,10},{9,11},{10,... | collective-permute-start | bytes 294920 | tf_op jit(solution)/shard_map/ppermute | solution.py:29
  109.3 12.5 %collective-permute-start.43 = (bf16[64,768]{1,0:T(8,128)(2,1)S(1)}, bf16[64,768]{1,0:T(8,128)(2,1)S(1)}, u32[]{:S(2)}, u32[]{:S(2)}) collective-permute-start(bf16[64,768]{1,0:T(8,128)(2,1)S(1)} %fusion.50), channel_id=1, source_target_pairs={{0,1},{1,2},{2,3},{3,0},{4,5},{5,6},{6,7},{7,4},{8,9},{9,10},{10,1... | collective-permute-start | bytes 294920 | tf_op jit(solution)/shard_map/ppermute | solution.py:29
  (40 other events, 126.3 us)

commit v21 on v17

--- a/solution.py
+++ b/solution.py
@@ -128,7 +128,7 @@
         half_rows = held.shape[1] // 2
         first_of_pair = (atoms_here % 2) == 0
         mine = jnp.where(
-            first_of_pair, held[: ROTS - 1, :half_rows], held[: ROTS - 1, half_rows:]
+            first_of_pair, held[:, :half_rows], held[:, half_rows:]
         )
         mine = gather_pieces(mine)
         theirs = swapped(mine, "atoms", 0)
@@ -169,7 +169,7 @@
         col_norm = jnp.sqrt(squares / total_orbitals + norm_eps)
         basis_all = (mixed_rows / col_norm[:, None]).astype(jnp.bfloat16)
     mixed_rows = lax.dot_general(
-        rotations[ROTS - 1],
+        rot_pieces[0, ROTS - 1],
         basis_all,
         (((0,), (0,)), ((), ())),
         preferred_element_type=jnp.float32,

time: 165 us -> 167 us (1.012)
  waiting for transfers between devices: 55 us -> 50.8 us
  starting transfers between devices: 45.3 us -> 48.7 us
  other arithmetic: 11.2 us -> 13.9 us
    ppermute x3, waiting for transfers between devices: 7.7 us -> 1.73 us  [gather_pieces(): pieces.append(lax.ppermute(value, 'bands', pairs))]
    ppermute x6, starting transfers between devices: 7.08 us -> 10 us  [gather_bands(): pieces.append(lax.ppermute(value, 'bands', pairs))]
    ppermute x49, waiting for transfers between devices: 37.2 us -> 40.2 us  [swapped(): return lax.ppermute(value, axis, pairs)]
    unnamed x29 -> x33, local copies, waits for them, and re-layouts: 2.83 us -> 5.08 us
    convert_element_type x2, other arithmetic: 0.34 us -> 2.32 us  [body(): basis_all = (mixed_rows / col_norm[:, None]).astype(jnp.bfloat16)]
  transfers between devices with their start and end apart: 58 -> 58, of which waited for: 24 -> 24; matrix products, arithmetic and copies ran while one was open for 32% -> 31% of each run, Pallas kernels for 0% -> 0%
where the time goes in v21:
time: 167 us
  waiting for transfers between devices  50.8 us (30%)
  starting transfers between devices  48.7 us (29%)
  matrix products  35.7 us (21%)
  local copies, waits for them, and re-layouts  16.8 us (10%)
  other arithmetic  13.9 us (8%)
    ppermute x49, waiting for transfers between devices, swapped(): return lax.ppermute(value, axis, pairs)  40.2 us
    ppermute x49, starting transfers between devices, swapped(): return lax.ppermute(value, axis, pairs)  33.6 us
    dot_general x32, matrix products, apply_operator(): jnp.dot(other_rows, other_pair[round_index], preferred_element_type=jnp.f...  14.5 us
    dot_general x4, matrix products, pattern_mask(): lax.dot_general(per_row.astype(jnp.bfloat16), col_onehot, (((1,), (1,)),...  10.5 us
    ppermute x6, starting transfers between devices, gather_bands(): pieces.append(lax.ppermute(value, 'bands', pairs))  10 us
    ppermute x6, waiting for transfers between devices, gather_bands(): pieces.append(lax.ppermute(value, 'bands', pairs))  8.88 us
    dot_general x16, matrix products, apply_operator(): result = jnp.dot(values, diag_sym, preferred_element_type=jnp.float32)  6.61 us
    unnamed x33, local copies, waits for them, and re-layouts  5.08 us
  transfers between devices with their start and end apart: 58, of which 24 were waited for; matrix products, arithmetic and copies ran while one was open for 31% of the time, Pallas kernels for 0%

profile of v21, /device:TPU:0, one launch (start us, length us, event | category | flops | bytes accessed | tf_op | source)
XLA Modules:
  0.0 166.7 jit_solution(13267916679194244320)
XLA Ops:
  0.0 1.6 fusion.108
  2.1 2.5 %collective-permute-start.5 = (bf16[64,768]{1,0:T(8,128)(2,1)}, bf16[64,768]{1,0:T(8,128)(2,1)}, u32[]{:S(2)}, u32[]{:S(2)}) collective-permute-start(bf16[64,768]{1,0:T(8,128)(2,1)} %get-tuple-element.26), channel_id=1, source_target_pairs={{0,8},{4,12},{8,0},{12,4},{16,24},{20,28},{24,16},{28,20},{1,9},{5... | collective-permute-start | bytes 294920 | tf_op jit(solution)/shard_map/ppermute | solution.py:20
  4.6 3.3 %slice_bitcast_fusion.1 = (bf16[768,768]{1,0:T(8,128)(2,1)}, bf16[768,768]{0,1:T(8,128)(2,1)}, bf16[1,768,768]{2,1,0:T(8,128)(2,1)S(1)}) fusion(bf16[2,768,768]{2,1,0:T(8,128)(2,1)} %param.10), kind=kLoop, calls=%fused_computation.111 | loop fusion | bytes 5898240 | tf_op jit(solution)/shard_map/squeeze | solution.py:74
  12.5 2.0 %copy.16 = f32[768,768]{1,0:T(8,128)S(1)} copy(f32[768,768]{0,1:T(8,128)} %convert_bitcast_fusion) | data formatting | bytes 4718592 | tf_op jit(solution)/shard_map/convert_element_type | solution.py:85
  15.9 2.3 %fusion.1 = bf16[768,768]{1,0:T(8,128)(2,1)S(1)} fusion(bf16[768,768]{1,0:T(8,128)(2,1)} %param.9, f32[768,768]{1,0:T(8,128)S(1)} %copy.16, s32[768]{0:T(1024)S(1)} %get-tuple-element.57), kind=kLoop, calls=%fused_computation.7 | loop fusion | flops 7667712 | bytes 4721664 | tf_op jit(solution)/shard_map/convert_element_type | solution.py:86
  21.3 3.1 %compare_select_fusion.2 = bf16[768,768]{1,0:T(8,128)(2,1)} fusion(bf16[1,768,768]{1,2,0:T(8,128)(2,1)} %copy.21, s32[768]{0:T(1024)S(1)} %get-tuple-element.57, s32[768]{0:T(1024)S(1)} %convert_reduce_fusion.1, s32[2,4,4]{2,1,0:T(4,128)S(1)} %copy-done.12), kind=kOutput, calls=%fused_computation.13 | convolution fusion | flops 5932048 | bytes 2369536 | tf_op jit(solution)/shard_map/dot_general | solution.py:63
  25.4 1.9 %compare_select_fusion = bf16[768,768]{1,0:T(8,128)(2,1)} fusion(bf16[768,768]{1,0:T(8,128)(2,1)S(1)} %copy.19, s32[768]{0:T(1024)S(1)} %copy-done.13, s32[768]{0:T(1024)S(1)} %get-tuple-element.57, s32[2,4,4]{2,1,0:T(4,128)S(1)} %copy-done.12), kind=kOutput, calls=%fused_computation.11 | convolution fusion | flops 5932048 | bytes 2369536 | tf_op jit(solution)/shard_map/dot_general | solution.py:63
  27.4 2.0 %collective-permute-start.3 = (s32[4,4]{1,0:T(4,128)}, s32[4,4]{1,0:T(4,128)S(1)}, u32[]{:S(2)}, u32[]{:S(2)}) collective-permute-start(s32[4,4]{1,0:T(4,128)} %get-tuple-element.28), channel_id=1, source_target_pairs={{0,8},{4,12},{8,0},{12,4},{16,24},{20,28},{24,16},{28,20},{1,9},{5... | collective-permute-start | bytes 200 | tf_op jit(solution)/shard_map/ppermute | solution.py:20
  29.4 2.9 %fusion.51 = f32[768,768]{1,0:T(8,128)} fusion(s32[768]{0:T(1024)S(1)} %get-tuple-element.57, s32[768]{0:T(1024)S(1)} %convert_reduce_fusion.1, s32[4,4]{1,0:T(4,128)} %collective-permute-done), kind=kOutput, calls=%fused_computation.108 | convolution fusion | flops 4752400 | bytes 2365504 | tf_op jit(solution)/shard_map/dot_general | solution.py:63
  33.9 2.5 %add_convert_fusion.1 = bf16[768,768]{1,0:T(8,128)(2,1)S(1)} fusion(bf16[768,768]{1,0:T(8,128)(2,1)} %compare_select_fusion.2, bf16[768,768]{1,0:T(8,128)(2,1)S(1)} %copy.18, f32[768,768]{1,0:T(8,128)} %fusion.51), kind=kLoop, calls=%fused_computation.10 | loop fusion | flops 3538944 | bytes 5898240 | tf_op jit(solution)/shard_map/convert_element_type | solution.py:98
  36.3 2.5 %collective-permute-done.3 = s32[4,4]{1,0:T(4,128)S(1)} collective-permute-done((s32[4,4]{1,0:T(4,128)}, s32[4,4]{1,0:T(4,128)S(1)}, u32[]{:S(2)}, u32[]{:S(2)}) %collective-permute-start.3) | collective-permute-done | bytes 96 | tf_op jit(solution)/shard_map/ppermute | solution.py:20
  39.1 2.6 %add_convert_fusion = bf16[768,768]{1,0:T(8,128)(2,1)S(1)} fusion(bf16[768,768]{1,0:T(8,128)(2,1)} %compare_select_fusion, bf16[768,768]{1,0:T(8,128)(2,1)} %collective-permute-done.4, s32[768]{0:T(1024)S(1)} %copy-done.14, s32[768]{0:T(1024)S(1)} %get-tuple-element.57, s32[4,4]{1,0:T(4,128)S(1)} %collective-permute-done.3), kind=kOutput, calls=%fused_computation.9 | convolution fusion | flops 8291344 | bytes 3545152 | tf_op jit(solution)/shard_map/dot_general | solution.py:63
  44.8 1.8 %collective-permute-start.7 = (bf16[64,768]{1,0:T(8,128)(2,1)S(1)}, bf16[64,768]{1,0:T(8,128)(2,1)S(1)}, u32[]{:S(2)}, u32[]{:S(2)}) collective-permute-start(bf16[64,768]{1,0:T(8,128)(2,1)S(1)} %get-tuple-element.32), channel_id=1, source_target_pairs={{0,8},{4,12},{8,0},{12,4},{16,24},{20,28},{24,16},{28,20},{1,9},{5... | collective-permute-start | bytes 294920 | tf_op jit(solution)/shard_map/ppermute | solution.py:20
  51.4 3.8 %collective-permute-start.10 = (bf16[4,256,128]{2,1,0:T(8,128)(2,1)S(1)}, bf16[4,256,128]{2,1,0:T(8,128)(2,1)S(1)}, u32[]{:S(2)}, u32[]{:S(2)}) collective-permute-start(bf16[4,256,128]{2,1,0:T(8,128)(2,1)S(1)} %slice_select_fusion), channel_id=1, source_target_pairs={{0,3},{1,0},{2,1},{3,2},{4,7},{5,4},{6,5},{7,6},{8,11},{9,8},{10,9... | collective-permute-start | bytes 786440 | tf_op jit(solution)/shard_map/ppermute | solution.py:39
  62.5 2.7 %collective-permute-done.27 = bf16[64,768]{1,0:T(8,128)(2,1)S(1)} collective-permute-done((bf16[64,768]{1,0:T(8,128)(2,1)S(1)}, bf16[64,768]{1,0:T(8,128)(2,1)S(1)}, u32[]{:S(2)}, u32[]{:S(2)}) %collective-permute-start.27) | collective-permute-done | bytes 98336 | tf_op jit(solution)/shard_map/ppermute | solution.py:20
  67.1 2.7 %collective-permute-done.15 = bf16[64,768]{1,0:T(8,128)(2,1)S(1)} collective-permute-done((bf16[64,768]{1,0:T(8,128)(2,1)S(1)}, bf16[64,768]{1,0:T(8,128)(2,1)S(1)}, u32[]{:S(2)}, u32[]{:S(2)}) %collective-permute-start.15) | collective-permute-done | bytes 98336 | tf_op jit(solution)/shard_map/ppermute | solution.py:20
  71.8 2.7 %collective-permute-done.29 = bf16[64,768]{1,0:T(8,128)(2,1)S(1)} collective-permute-done((bf16[64,768]{1,0:T(8,128)(2,1)S(1)}, bf16[64,768]{1,0:T(8,128)(2,1)S(1)}, u32[]{:S(2)}, u32[]{:S(2)}) %collective-permute-start.29) | collective-permute-done | bytes 98336 | tf_op jit(solution)/shard_map/ppermute | solution.py:20
  76.0 1.7 %collective-permute-done.9 = bf16[4,256,128]{2,1,0:T(8,128)(2,1)S(1)} collective-permute-done((bf16[4,256,128]{2,1,0:T(8,128)(2,1)S(1)}, bf16[4,256,128]{2,1,0:T(8,128)(2,1)S(1)}, u32[]{:S(2)}, u32[]{:S(2)}) %collective-permute-start.9) | collective-permute-done | bytes 262176 | tf_op jit(solution)/shard_map/ppermute | solution.py:39
  98.5 2.3 %collective-permute-done.37 = bf16[64,768]{1,0:T(8,128)(2,1)S(1)} collective-permute-done((bf16[64,768]{1,0:T(8,128)(2,1)S(1)}, bf16[64,768]{1,0:T(8,128)(2,1)S(1)}, u32[]{:S(2)}, u32[]{:S(2)}) %collective-permute-start.37) | collective-permute-done | bytes 98336 | tf_op jit(solution)/shard_map/ppermute | solution.py:20
  101.2 2.1 %collective-permute-start.40 = (bf16[64,768]{1,0:T(8,128)(2,1)S(1)}, bf16[64,768]{1,0:T(8,128)(2,1)S(1)}, u32[]{:S(2)}, u32[]{:S(2)}) collective-permute-start(bf16[64,768]{1,0:T(8,128)(2,1)S(1)} %fusion.49), channel_id=1, source_target_pairs={{0,3},{1,0},{2,1},{3,2},{4,7},{5,4},{6,5},{7,6},{8,11},{9,8},{10,9... | collective-permute-start | bytes 294920 | tf_op jit(solution)/shard_map/ppermute | solution.py:29
  106.5 2.5 %collective-permute-start.45 = (bf16[64,768]{1,0:T(8,128)(2,1)S(1)}, bf16[64,768]{1,0:T(8,128)(2,1)S(1)}, u32[]{:S(2)}, u32[]{:S(2)}) collective-permute-start(bf16[64,768]{1,0:T(8,128)(2,1)S(1)} %fusion.50), channel_id=1, source_target_pairs={{0,3},{1,0},{2,1},{3,2},{4,7},{5,4},{6,5},{7,6},{8,11},{9,8},{10,9... | collective-permute-start | bytes 294920 | tf_op jit(solution)/shard_map/ppermute | solution.py:29
  108.9 3.0 %collective-permute-start.43 = (bf16[64,768]{1,0:T(8,128)(2,1)S(1)}, bf16[64,768]{1,0:T(8,128)(2,1)S(1)}, u32[]{:S(2)}, u32[]{:S(2)}) collective-permute-start(bf16[64,768]{1,0:T(8,128)(2,1)S(1)} %fusion.50), channel_id=1, source_target_pairs={{0,1},{1,2},{2,3},{3,0},{4,5},{5,6},{6,7},{7,4},{8,9},{9,10},{10,1... | collective-permute-start | bytes 294920 | tf_op jit(solution)/shard_map/ppermute | solution.py:29
  111.9 6.6 %collective-permute-done.39 = bf16[64,768]{1,0:T(8,128)(2,1)S(1)} collective-permute-done((bf16[64,768]{1,0:T(8,128)(2,1)S(1)}, bf16[64,768]{1,0:T(8,128)(2,1)S(1)}, u32[]{:S(2)}, u32[]{:S(2)}) %collective-permute-start.39) | collective-permute-done | bytes 98336 | tf_op jit(solution)/shard_map/ppermute | solution.py:29
  119.2 2.3 %collective-permute-done.44 = bf16[64,768]{1,0:T(8,128)(2,1)S(1)} collective-permute-done((bf16[64,768]{1,0:T(8,128)(2,1)S(1)}, bf16[64,768]{1,0:T(8,128)(2,1)S(1)}, u32[]{:S(2)}, u32[]{:S(2)}) %collective-permute-start.44) | collective-permute-done | bytes 98336 | tf_op jit(solution)/shard_map/ppermute | solution.py:29
  128.3 2.5 %collective-permute-done.47 = f32[512]{0:T(512)S(1)} collective-permute-done((f32[512]{0:T(512)S(1)}, f32[512]{0:T(512)S(1)}, u32[]{:S(2)}, u32[]{:S(2)}) %collective-permute-start.47) | collective-permute-done | bytes 2080 | tf_op jit(solution)/shard_map/ppermute | solution.py:20
  132.3 2.1 %collective-permute-done.48 = f32[512]{0:T(512)S(1)} collective-permute-done((f32[512]{0:T(512)S(1)}, f32[512]{0:T(512)S(1)}, u32[]{:S(2)}, u32[]{:S(2)}) %collective-permute-start.48) | collective-permute-done | bytes 2080 | tf_op jit(solution)/shard_map/ppermute | solution.py:20
  140.0 2.5 %collective-permute-done.50 = f32[512]{0:T(512)S(1)} collective-permute-done((f32[512]{0:T(512)S(1)}, f32[512]{0:T(512)S(1)}, u32[]{:S(2)}, u32[]{:S(2)}) %collective-permute-start.50) | collective-permute-done | bytes 2080 | tf_op jit(solution)/shard_map/ppermute | solution.py:20
  144.1 2.1 %collective-permute-done.51 = f32[512]{0:T(512)S(1)} collective-permute-done((f32[512]{0:T(512)S(1)}, f32[512]{0:T(512)S(1)}, u32[]{:S(2)}, u32[]{:S(2)}) %collective-permute-start.51) | collective-permute-done | bytes 2080 | tf_op jit(solution)/shard_map/ppermute | solution.py:20
  151.0 2.5 %collective-permute-done.53 = f32[512]{0:T(512)S(1)} collective-permute-done((f32[512]{0:T(512)S(1)}, f32[512]{0:T(512)S(1)}, u32[]{:S(2)}, u32[]{:S(2)}) %collective-permute-start.53) | collective-permute-done | bytes 2080 | tf_op jit(solution)/shard_map/ppermute | solution.py:20
  155.0 2.1 %collective-permute-done.54 = f32[512]{0:T(512)S(1)} collective-permute-done((f32[512]{0:T(512)S(1)}, f32[512]{0:T(512)S(1)}, u32[]{:S(2)}, u32[]{:S(2)}) %collective-permute-start.54) | collective-permute-done | bytes 2080 | tf_op jit(solution)/shard_map/ppermute | solution.py:20
  159.8 2.5 %collective-permute-done.56 = f32[128]{0:T(128)S(1)} collective-permute-done((f32[128]{0:T(128)S(1)}, f32[128]{0:T(128)S(1)}, u32[]{:S(2)}, u32[]{:S(2)}) %collective-permute-start.56) | collective-permute-done | bytes 544 | tf_op jit(solution)/shard_map/ppermute | solution.py:20
  163.8 2.0 %collective-permute-done.57 = f32[128]{0:T(128)S(1)} collective-permute-done((f32[128]{0:T(128)S(1)}, f32[128]{0:T(128)S(1)}, u32[]{:S(2)}, u32[]{:S(2)}) %collective-permute-start.57) | collective-permute-done | bytes 544 | tf_op jit(solution)/shard_map/ppermute | solution.py:20
  (233 shorter events, 84.1 us)
Async XLA Ops:
  1.6 40.1 %collective-permute-start.2 = (bf16[64,768]{1,0:T(8,128)(2,1)}, bf16[64,768]{1,0:T(8,128)(2,1)}, u32[]{:S(2)}, u32[]{:S(2)}) collective-permute-start(bf16[64,768]{1,0:T(8,128)(2,1)} %get-tuple-element.26), channel_id=1, source_target_pairs={{0,4},{4,0},{8,12},{12,8},{16,20},{20,16},{24,28},{28,24},{1,5},{5... | collective-permute-start | bytes 294920 | tf_op jit(solution)/shard_map/ppermute | solution.py:20
  2.1 41.0 %collective-permute-start.5 = (bf16[64,768]{1,0:T(8,128)(2,1)}, bf16[64,768]{1,0:T(8,128)(2,1)}, u32[]{:S(2)}, u32[]{:S(2)}) collective-permute-start(bf16[64,768]{1,0:T(8,128)(2,1)} %get-tuple-element.26), channel_id=1, source_target_pairs={{0,8},{4,12},{8,0},{12,4},{16,24},{20,28},{24,16},{28,20},{1,9},{5... | collective-permute-start | bytes 294920 | tf_op jit(solution)/shard_map/ppermute | solution.py:20
  9.4 22.9 %collective-permute-start.1 = (bf16[768,768]{0,1:T(8,128)(2,1)}, bf16[768,768]{0,1:T(8,128)(2,1)}, u32[]{:S(2)}, u32[]{:S(2)}) collective-permute-start(bf16[768,768]{0,1:T(8,128)(2,1)} %bitcast.4), channel_id=1, source_target_pairs={{0,4},{4,0},{8,12},{12,8},{16,20},{20,16},{24,28},{28,24},{1,5},{5... | collective-permute-start | bytes 3538952 | tf_op jit(solution)/shard_map/ppermute | solution.py:20
  10.1 17.2 %collective-permute-start = (s32[4,4]{1,0:T(4,128)}, s32[4,4]{1,0:T(4,128)}, u32[]{:S(2)}, u32[]{:S(2)}) collective-permute-start(s32[4,4]{1,0:T(4,128)} %get-tuple-element.29), channel_id=1, source_target_pairs={{0,4},{4,0},{8,12},{12,8},{16,20},{20,16},{24,28},{28,24},{1,5},{5... | collective-permute-start | bytes 200 | tf_op jit(solution)/shard_map/ppermute | solution.py:20
  10.4 28.7 %collective-permute-start.4 = (bf16[768,768]{1,0:T(8,128)(2,1)}, bf16[768,768]{1,0:T(8,128)(2,1)}, u32[]{:S(2)}, u32[]{:S(2)}) collective-permute-start(bf16[768,768]{1,0:T(8,128)(2,1)} %get-tuple-element.21), channel_id=1, source_target_pairs={{0,8},{4,12},{8,0},{12,4},{16,24},{20,28},{24,16},{28,20},{1,9},{5... | collective-permute-start | bytes 3538952 | tf_op jit(solution)/shard_map/ppermute | solution.py:20
  27.4 11.5 %collective-permute-start.3 = (s32[4,4]{1,0:T(4,128)}, s32[4,4]{1,0:T(4,128)S(1)}, u32[]{:S(2)}, u32[]{:S(2)}) collective-permute-start(s32[4,4]{1,0:T(4,128)} %get-tuple-element.28), channel_id=1, source_target_pairs={{0,8},{4,12},{8,0},{12,4},{16,24},{20,28},{24,16},{28,20},{1,9},{5... | collective-permute-start | bytes 200 | tf_op jit(solution)/shard_map/ppermute | solution.py:20
  32.3 14.3 %collective-permute-start.22 = (bf16[64,768]{1,0:T(8,128)(2,1)}, bf16[64,768]{1,0:T(8,128)(2,1)}, u32[]{:S(2)}, u32[]{:S(2)}) collective-permute-start(bf16[64,768]{1,0:T(8,128)(2,1)} %get-tuple-element.27), channel_id=1, source_target_pairs={{0,4},{4,0},{8,12},{12,8},{16,20},{20,16},{24,28},{28,24},{1,5},{5... | collective-permute-start | bytes 294920 | tf_op jit(solution)/shard_map/ppermute | solution.py:20
  38.8 9.0 %collective-permute-start.23 = (bf16[64,768]{1,0:T(8,128)(2,1)}, bf16[64,768]{1,0:T(8,128)(2,1)}, u32[]{:S(2)}, u32[]{:S(2)}) collective-permute-start(bf16[64,768]{1,0:T(8,128)(2,1)} %get-tuple-element.27), channel_id=1, source_target_pairs={{0,8},{4,12},{8,0},{12,4},{16,24},{20,28},{24,16},{28,20},{1,9},{5... | collective-permute-start | bytes 294920 | tf_op jit(solution)/shard_map/ppermute | solution.py:20
  44.7 5.3 %collective-permute-start.6 = (bf16[64,768]{1,0:T(8,128)(2,1)S(1)}, bf16[64,768]{1,0:T(8,128)(2,1)S(1)}, u32[]{:S(2)}, u32[]{:S(2)}) collective-permute-start(bf16[64,768]{1,0:T(8,128)(2,1)S(1)} %get-tuple-element.32), channel_id=1, source_target_pairs={{0,4},{4,0},{8,12},{12,8},{16,20},{20,16},{24,28},{28,24},{1,5},{5... | collective-permute-start | bytes 294920 | tf_op jit(solution)/shard_map/ppermute | solution.py:20
  44.8 5.5 %collective-permute-start.7 = (bf16[64,768]{1,0:T(8,128)(2,1)S(1)}, bf16[64,768]{1,0:T(8,128)(2,1)S(1)}, u32[]{:S(2)}, u32[]{:S(2)}) collective-permute-start(bf16[64,768]{1,0:T(8,128)(2,1)S(1)} %get-tuple-element.32), channel_id=1, source_target_pairs={{0,8},{4,12},{8,0},{12,4},{16,24},{20,28},{24,16},{28,20},{1,9},{5... | collective-permute-start | bytes 294920 | tf_op jit(solution)/shard_map/ppermute | solution.py:20
  49.4 7.4 %collective-permute-start.24 = (bf16[64,768]{1,0:T(8,128)(2,1)S(1)}, bf16[64,768]{1,0:T(8,128)(2,1)S(1)}, u32[]{:S(2)}, u32[]{:S(2)}) collective-permute-start(bf16[64,768]{1,0:T(8,128)(2,1)S(1)} %get-tuple-element.42), channel_id=1, source_target_pairs={{0,4},{4,0},{8,12},{12,8},{16,20},{20,16},{24,28},{28,24},{1,5},{5... | collective-permute-start | bytes 294920 | tf_op jit(solution)/shard_map/ppermute | solution.py:20
  49.6 7.9 %collective-permute-start.25 = (bf16[64,768]{1,0:T(8,128)(2,1)S(1)}, bf16[64,768]{1,0:T(8,128)(2,1)S(1)}, u32[]{:S(2)}, u32[]{:S(2)}) collective-permute-start(bf16[64,768]{1,0:T(8,128)(2,1)S(1)} %get-tuple-element.42), channel_id=1, source_target_pairs={{0,8},{4,12},{8,0},{12,4},{16,24},{20,28},{24,16},{28,20},{1,9},{5... | collective-permute-start | bytes 294920 | tf_op jit(solution)/shard_map/ppermute | solution.py:20
  51.4 24.6 %collective-permute-start.10 = (bf16[4,256,128]{2,1,0:T(8,128)(2,1)S(1)}, bf16[4,256,128]{2,1,0:T(8,128)(2,1)S(1)}, u32[]{:S(2)}, u32[]{:S(2)}) collective-permute-start(bf16[4,256,128]{2,1,0:T(8,128)(2,1)S(1)} %slice_select_fusion), channel_id=1, source_target_pairs={{0,3},{1,0},{2,1},{3,2},{4,7},{5,4},{6,5},{7,6},{8,11},{9,8},{10,9... | collective-permute-start | bytes 786440 | tf_op jit(solution)/shard_map/ppermute | solution.py:39
  55.2 22.5 %collective-permute-start.9 = (bf16[4,256,128]{2,1,0:T(8,128)(2,1)S(1)}, bf16[4,256,128]{2,1,0:T(8,128)(2,1)S(1)}, u32[]{:S(2)}, u32[]{:S(2)}) collective-permute-start(bf16[4,256,128]{2,1,0:T(8,128)(2,1)S(1)} %slice_select_fusion), channel_id=1, source_target_pairs={{0,2},{1,3},{2,0},{3,1},{4,6},{5,7},{6,4},{7,5},{8,10},{9,11},{10,... | collective-permute-start | bytes 786440 | tf_op jit(solution)/shard_map/ppermute | solution.py:39
  57.5 21.7 %collective-permute-start.8 = (bf16[4,256,128]{2,1,0:T(8,128)(2,1)S(1)}, bf16[4,256,128]{2,1,0:T(8,128)(2,1)S(1)}, u32[]{:S(2)}, u32[]{:S(2)}) collective-permute-start(bf16[4,256,128]{2,1,0:T(8,128)(2,1)S(1)} %slice_select_fusion), channel_id=1, source_target_pairs={{0,1},{1,2},{2,3},{3,0},{4,5},{5,6},{6,7},{7,4},{8,9},{9,10},{10,1... | collective-permute-start | bytes 786440 | tf_op jit(solution)/shard_map/ppermute | solution.py:39
  59.9 5.3 %collective-permute-start.27 = (bf16[64,768]{1,0:T(8,128)(2,1)S(1)}, bf16[64,768]{1,0:T(8,128)(2,1)S(1)}, u32[]{:S(2)}, u32[]{:S(2)}) collective-permute-start(bf16[64,768]{1,0:T(8,128)(2,1)S(1)} %get-tuple-element.44), channel_id=1, source_target_pairs={{0,8},{4,12},{8,0},{12,4},{16,24},{20,28},{24,16},{28,20},{1,9},{5... | collective-permute-start | bytes 294920 | tf_op jit(solution)/shard_map/ppermute | solution.py:20
  71.0 9.1 %collective-permute-start.16 = (bf16[64,768]{1,0:T(8,128)(2,1)S(1)}, bf16[64,768]{1,0:T(8,128)(2,1)S(1)}, u32[]{:S(2)}, u32[]{:S(2)}) collective-permute-start(bf16[64,768]{1,0:T(8,128)(2,1)S(1)} %get-tuple-element.36), channel_id=1, source_target_pairs={{0,4},{4,0},{8,12},{12,8},{16,20},{20,16},{24,28},{28,24},{1,5},{5... | collective-permute-start | bytes 294920 | tf_op jit(solution)/shard_map/ppermute | solution.py:20
  74.4 6.0 %collective-permute-start.17 = (bf16[64,768]{1,0:T(8,128)(2,1)S(1)}, bf16[64,768]{1,0:T(8,128)(2,1)S(1)}, u32[]{:S(2)}, u32[]{:S(2)}) collective-permute-start(bf16[64,768]{1,0:T(8,128)(2,1)S(1)} %get-tuple-element.36), channel_id=1, source_target_pairs={{0,8},{4,12},{8,0},{12,4},{16,24},{20,28},{24,16},{28,20},{1,9},{5... | collective-permute-start | bytes 294920 | tf_op jit(solution)/shard_map/ppermute | solution.py:20
  76.0 6.3 %collective-permute-start.30 = (bf16[64,768]{1,0:T(8,128)(2,1)S(1)}, bf16[64,768]{1,0:T(8,128)(2,1)S(1)}, u32[]{:S(2)}, u32[]{:S(2)}) collective-permute-start(bf16[64,768]{1,0:T(8,128)(2,1)S(1)} %get-tuple-element.48), channel_id=1, source_target_pairs={{0,4},{4,0},{8,12},{12,8},{16,20},{20,16},{24,28},{28,24},{1,5},{5... | collective-permute-start | bytes 294920 | tf_op jit(solution)/shard_map/ppermute | solution.py:20
  80.1 14.8 %collective-permute-start.11 = (bf16[4,4,256,128]{3,2,1,0:T(8,128)(2,1)S(1)}, bf16[4,4,256,128]{3,2,1,0:T(8,128)(2,1)S(1)}, u32[]{:S(2)}, u32[]{:S(2)}) collective-permute-start(bf16[4,4,256,128]{3,2,1,0:T(8,128)(2,1)S(1)} %get-tuple-element.24), channel_id=1, source_target_pairs={{0,4},{4,0},{8,12},{12,8},{16,20},{20,16},{24,28},{28,24},{1,5},{5... | collective-permute-start | bytes 3145736 | tf_op jit(solution)/shard_map/ppermute | solution.py:20
  83.3 5.3 %collective-permute-start.33 = (bf16[64,768]{1,0:T(8,128)(2,1)S(1)}, bf16[64,768]{1,0:T(8,128)(2,1)S(1)}, u32[]{:S(2)}, u32[]{:S(2)}) collective-permute-start(bf16[64,768]{1,0:T(8,128)(2,1)S(1)} %get-tuple-element.50), channel_id=1, source_target_pairs={{0,8},{4,12},{8,0},{12,4},{16,24},{20,28},{24,16},{28,20},{1,9},{5... | collective-permute-start | bytes 294920 | tf_op jit(solution)/shard_map/ppermute | solution.py:20
  87.2 5.2 %collective-permute-start.21 = (bf16[64,768]{1,0:T(8,128)(2,1)S(1)}, bf16[64,768]{1,0:T(8,128)(2,1)S(1)}, u32[]{:S(2)}, u32[]{:S(2)}) collective-permute-start(bf16[64,768]{1,0:T(8,128)(2,1)S(1)} %get-tuple-element.40), channel_id=1, source_target_pairs={{0,8},{4,12},{8,0},{12,4},{16,24},{20,28},{24,16},{28,20},{1,9},{5... | collective-permute-start | bytes 294920 | tf_op jit(solution)/shard_map/ppermute | solution.py:20
  89.3 5.2 %collective-permute-start.35 = (bf16[64,768]{1,0:T(8,128)(2,1)S(1)}, bf16[64,768]{1,0:T(8,128)(2,1)S(1)}, u32[]{:S(2)}, u32[]{:S(2)}) collective-permute-start(bf16[64,768]{1,0:T(8,128)(2,1)S(1)} %get-tuple-element.52), channel_id=1, source_target_pairs={{0,8},{4,12},{8,0},{12,4},{16,24},{20,28},{24,16},{28,20},{1,9},{5... | collective-permute-start | bytes 294920 | tf_op jit(solution)/shard_map/ppermute | solution.py:20
  95.5 5.4 %collective-permute-start.37 = (bf16[64,768]{1,0:T(8,128)(2,1)S(1)}, bf16[64,768]{1,0:T(8,128)(2,1)S(1)}, u32[]{:S(2)}, u32[]{:S(2)}) collective-permute-start(bf16[64,768]{1,0:T(8,128)(2,1)S(1)} %convert_element_type.180), channel_id=1, source_target_pairs={{0,8},{4,12},{8,0},{12,4},{16,24},{20,28},{24,16},{28,20},{1,9},{5... | collective-permute-start | bytes 294920 | tf_op jit(solution)/shard_map/ppermute | solution.py:20
  97.3 8.4 %collective-permute-start.41 = (bf16[64,768]{1,0:T(8,128)(2,1)S(1)}, bf16[64,768]{1,0:T(8,128)(2,1)S(1)}, u32[]{:S(2)}, u32[]{:S(2)}) collective-permute-start(bf16[64,768]{1,0:T(8,128)(2,1)S(1)} %convert_element_type.182), channel_id=1, source_target_pairs={{0,4},{4,0},{8,12},{12,8},{16,20},{20,16},{24,28},{28,24},{1,5},{5... | collective-permute-start | bytes 294920 | tf_op jit(solution)/shard_map/ppermute | solution.py:20
  97.6 8.5 %collective-permute-start.42 = (bf16[64,768]{1,0:T(8,128)(2,1)S(1)}, bf16[64,768]{1,0:T(8,128)(2,1)S(1)}, u32[]{:S(2)}, u32[]{:S(2)}) collective-permute-start(bf16[64,768]{1,0:T(8,128)(2,1)S(1)} %convert_element_type.182), channel_id=1, source_target_pairs={{0,8},{4,12},{8,0},{12,4},{16,24},{20,28},{24,16},{28,20},{1,9},{5... | collective-permute-start | bytes 294920 | tf_op jit(solution)/shard_map/ppermute | solution.py:20
  101.2 7.8 %collective-permute-start.40 = (bf16[64,768]{1,0:T(8,128)(2,1)S(1)}, bf16[64,768]{1,0:T(8,128)(2,1)S(1)}, u32[]{:S(2)}, u32[]{:S(2)}) collective-permute-start(bf16[64,768]{1,0:T(8,128)(2,1)S(1)} %fusion.49), channel_id=1, source_target_pairs={{0,3},{1,0},{2,1},{3,2},{4,7},{5,4},{6,5},{7,6},{8,11},{9,8},{10,9... | collective-permute-start | bytes 294920 | tf_op jit(solution)/shard_map/ppermute | solution.py:29
  103.2 15.3 %collective-permute-start.39 = (bf16[64,768]{1,0:T(8,128)(2,1)S(1)}, bf16[64,768]{1,0:T(8,128)(2,1)S(1)}, u32[]{:S(2)}, u32[]{:S(2)}) collective-permute-start(bf16[64,768]{1,0:T(8,128)(2,1)S(1)} %fusion.49), channel_id=1, source_target_pairs={{0,2},{1,3},{2,0},{3,1},{4,6},{5,7},{6,4},{7,5},{8,10},{9,11},{10,... | collective-permute-start | bytes 294920 | tf_op jit(solution)/shard_map/ppermute | solution.py:29
  104.4 14.2 %collective-permute-start.38 = (bf16[64,768]{1,0:T(8,128)(2,1)S(1)}, bf16[64,768]{1,0:T(8,128)(2,1)S(1)}, u32[]{:S(2)}, u32[]{:S(2)}) collective-permute-start(bf16[64,768]{1,0:T(8,128)(2,1)S(1)} %fusion.49), channel_id=1, source_target_pairs={{0,1},{1,2},{2,3},{3,0},{4,5},{5,6},{6,7},{7,4},{8,9},{9,10},{10,1... | collective-permute-start | bytes 294920 | tf_op jit(solution)/shard_map/ppermute | solution.py:29
  106.5 12.7 %collective-permute-start.45 = (bf16[64,768]{1,0:T(8,128)(2,1)S(1)}, bf16[64,768]{1,0:T(8,128)(2,1)S(1)}, u32[]{:S(2)}, u32[]{:S(2)}) collective-permute-start(bf16[64,768]{1,0:T(8,128)(2,1)S(1)} %fusion.50), channel_id=1, source_target_pairs={{0,3},{1,0},{2,1},{3,2},{4,7},{5,4},{6,5},{7,6},{8,11},{9,8},{10,9... | collective-permute-start | bytes 294920 | tf_op jit(solution)/shard_map/ppermute | solution.py:29
  108.9 12.5 %collective-permute-start.44 = (bf16[64,768]{1,0:T(8,128)(2,1)S(1)}, bf16[64,768]{1,0:T(8,128)(2,1)S(1)}, u32[]{:S(2)}, u32[]{:S(2)}) collective-permute-start(bf16[64,768]{1,0:T(8,128)(2,1)S(1)} %fusion.50), channel_id=1, source_target_pairs={{0,2},{1,3},{2,0},{3,1},{4,6},{5,7},{6,4},{7,5},{8,10},{9,11},{10,... | collective-permute-start | bytes 294920 | tf_op jit(solution)/shard_map/ppermute | solution.py:29
  108.9 12.5 %collective-permute-start.43 = (bf16[64,768]{1,0:T(8,128)(2,1)S(1)}, bf16[64,768]{1,0:T(8,128)(2,1)S(1)}, u32[]{:S(2)}, u32[]{:S(2)}) collective-permute-start(bf16[64,768]{1,0:T(8,128)(2,1)S(1)} %fusion.50), channel_id=1, source_target_pairs={{0,1},{1,2},{2,3},{3,0},{4,5},{5,6},{6,7},{7,4},{8,9},{9,10},{10,1... | collective-permute-start | bytes 294920 | tf_op jit(solution)/shard_map/ppermute | solution.py:29
  (42 other events, 121.3 us)

commit v22 on v17

--- a/solution.py
+++ b/solution.py
@@ -114,8 +114,11 @@
             if degree_index == GATHER_AT:
                 current = hook(current)
             if degree_index == DEGREE - 1 and gathered:
-                settled, current = lax.optimization_barrier((gathered[0], current))
+                settled, last_cols, current = lax.optimization_barrier(
+                    (gathered[0], rotations[ROTS - 1], current)
+                )
                 gathered[0] = settled
+                gathered.append(last_cols)
             applied = apply_operator(current.astype(jnp.bfloat16))
             following = 2.0 * (applied - filter_center * current) / filter_half - previous
             previous, current = (current, following)
@@ -169,7 +172,7 @@
         col_norm = jnp.sqrt(squares / total_orbitals + norm_eps)
         basis_all = (mixed_rows / col_norm[:, None]).astype(jnp.bfloat16)
     mixed_rows = lax.dot_general(
-        rotations[ROTS - 1],
+        gathered[1],
         basis_all,
         (((0,), (0,)), ((), ())),
         preferred_element_type=jnp.float32,

time: 165 us -> 167 us (1.012)
  waiting for transfers between devices: 55 us -> 50.7 us
  local copies, waits for them, and re-layouts: 15.4 us -> 18.1 us
  starting transfers between devices: 45.3 us -> 47.2 us
  other arithmetic: 11.2 us -> 12.9 us
    ppermute x3, waiting for transfers between devices: 7.7 us -> 3.02 us  [gather_pieces(): pieces.append(lax.ppermute(value, 'bands', pairs))]
    unnamed x29 -> x33, local copies, waits for them, and re-layouts: 2.83 us -> 4.98 us
    convert_element_type x2, other arithmetic: 0.34 us -> 2.32 us  [body(): basis_all = (mixed_rows / col_norm[:, None]).astype(jnp.bfloat16)]
    ppermute x6, starting transfers between devices: 7.08 us -> 8.85 us  [gather_bands(): pieces.append(lax.ppermute(value, 'bands', pairs))]
  transfers between devices with their start and end apart: 58 -> 58, of which waited for: 24 -> 25; matrix products, arithmetic and copies ran while one was open for 32% -> 32% of each run, Pallas kernels for 0% -> 0%
where the time goes in v22:
time: 167 us; the launch traced here: 166 us
  waiting for transfers between devices  50.7 us (30%)
  starting transfers between devices  47.2 us (28%)
  matrix products  36.3 us (22%)
  local copies, waits for them, and re-layouts  18.1 us (11%)
  other arithmetic  12.9 us (8%)
    ppermute x49, waiting for transfers between devices, swapped(): return lax.ppermute(value, axis, pairs)  38.4 us
    ppermute x49, starting transfers between devices, swapped(): return lax.ppermute(value, axis, pairs)  33.5 us
    dot_general x32, matrix products, apply_operator(): jnp.dot(other_rows, other_pair[round_index], preferred_element_type=jnp.f...  14.5 us
    dot_general x4, matrix products, pattern_mask(): lax.dot_general(per_row.astype(jnp.bfloat16), col_onehot, (((1,), (1,)),...  11.2 us
    ppermute x6, waiting for transfers between devices, gather_bands(): pieces.append(lax.ppermute(value, 'bands', pairs))  9.25 us
    ppermute x6, starting transfers between devices, gather_bands(): pieces.append(lax.ppermute(value, 'bands', pairs))  8.85 us
    dot_general x16, matrix products, apply_operator(): result = jnp.dot(values, diag_sym, preferred_element_type=jnp.float32)  6.6 us
    unnamed x33, local copies, waits for them, and re-layouts  4.98 us
  transfers between devices with their start and end apart: 58, of which 25 were waited for; matrix products, arithmetic and copies ran while one was open for 32% of the time, Pallas kernels for 0%

profile of v22, /device:TPU:0, one launch (start us, length us, event | category | flops | bytes accessed | tf_op | source)
XLA Modules:
  0.0 166.0 jit_solution(11963520913899463320)
XLA Ops:
  0.0 1.6 fusion.106
  2.1 2.5 %collective-permute-start.5 = (bf16[64,768]{1,0:T(8,128)(2,1)}, bf16[64,768]{1,0:T(8,128)(2,1)}, u32[]{:S(2)}, u32[]{:S(2)}) collective-permute-start(bf16[64,768]{1,0:T(8,128)(2,1)} %get-tuple-element.29), channel_id=1, source_target_pairs={{0,8},{4,12},{8,0},{12,4},{16,24},{20,28},{24,16},{28,20},{1,9},{5... | collective-permute-start | bytes 294920 | tf_op jit(solution)/shard_map/ppermute | solution.py:20
  4.6 3.3 %slice_bitcast_fusion.1 = (bf16[768,768]{1,0:T(8,128)(2,1)}, bf16[768,768]{0,1:T(8,128)(2,1)}, bf16[1,768,768]{2,1,0:T(8,128)(2,1)S(1)}) fusion(bf16[2,768,768]{2,1,0:T(8,128)(2,1)} %param.10), kind=kLoop, calls=%fused_computation.110 | loop fusion | bytes 5898240 | tf_op jit(solution)/shard_map/squeeze | solution.py:74
  10.4 1.6 convert_bitcast_fusion
  12.0 2.0 %copy.16 = f32[768,768]{1,0:T(8,128)S(1)} copy(f32[768,768]{0,1:T(8,128)} %convert_bitcast_fusion) | data formatting | bytes 4718592 | tf_op jit(solution)/shard_map/convert_element_type | solution.py:85
  15.3 2.3 %fusion.1 = bf16[768,768]{1,0:T(8,128)(2,1)S(1)} fusion(bf16[768,768]{1,0:T(8,128)(2,1)} %param.9, f32[768,768]{1,0:T(8,128)S(1)} %copy.16, s32[768]{0:T(1024)S(1)} %get-tuple-element.59), kind=kLoop, calls=%fused_computation.7 | loop fusion | flops 7667712 | bytes 4721664 | tf_op jit(solution)/shard_map/convert_element_type | solution.py:86
  19.0 3.1 %compare_select_fusion.2 = bf16[768,768]{1,0:T(8,128)(2,1)} fusion(bf16[1,768,768]{1,2,0:T(8,128)(2,1)} %copy.21, s32[768]{0:T(1024)S(1)} %get-tuple-element.59, s32[768]{0:T(1024)S(1)} %convert_reduce_fusion.1, s32[2,4,4]{2,1,0:T(4,128)S(1)} %copy-done.13), kind=kOutput, calls=%fused_computation.13 | convolution fusion | flops 5932048 | bytes 2369536 | tf_op jit(solution)/shard_map/dot_general | solution.py:63
  25.9 2.6 %compare_select_fusion = bf16[768,768]{1,0:T(8,128)(2,1)} fusion(bf16[768,768]{1,0:T(8,128)(2,1)S(1)} %copy.19, s32[768]{0:T(1024)} %get-tuple-element.58, s32[768]{0:T(1024)S(1)} %get-tuple-element.59, s32[2,4,4]{2,1,0:T(4,128)S(1)} %copy-done.13), kind=kOutput, calls=%fused_computation.11 | convolution fusion | flops 5932048 | bytes 2368512 | tf_op jit(solution)/shard_map/dot_general | solution.py:63
  28.5 2.0 %collective-permute-start.3 = (s32[4,4]{1,0:T(4,128)}, s32[4,4]{1,0:T(4,128)S(1)}, u32[]{:S(2)}, u32[]{:S(2)}) collective-permute-start(s32[4,4]{1,0:T(4,128)} %get-tuple-element.30), channel_id=1, source_target_pairs={{0,8},{4,12},{8,0},{12,4},{16,24},{20,28},{24,16},{28,20},{1,9},{5... | collective-permute-start | bytes 200 | tf_op jit(solution)/shard_map/ppermute | solution.py:20
  30.6 2.9 %fusion.51 = f32[768,768]{1,0:T(8,128)} fusion(s32[768]{0:T(1024)S(1)} %get-tuple-element.59, s32[768]{0:T(1024)S(1)} %convert_reduce_fusion.1, s32[4,4]{1,0:T(4,128)} %collective-permute-done), kind=kOutput, calls=%fused_computation.108 | convolution fusion | flops 4752400 | bytes 2365504 | tf_op jit(solution)/shard_map/dot_general | solution.py:63
  35.1 2.5 %add_convert_fusion.1 = bf16[768,768]{1,0:T(8,128)(2,1)S(1)} fusion(bf16[768,768]{1,0:T(8,128)(2,1)} %compare_select_fusion.2, bf16[768,768]{1,0:T(8,128)(2,1)S(1)} %copy.18, f32[768,768]{1,0:T(8,128)} %fusion.51), kind=kLoop, calls=%fused_computation.10 | loop fusion | flops 3538944 | bytes 5898240 | tf_op jit(solution)/shard_map/convert_element_type | solution.py:98
  39.1 2.6 %add_convert_fusion = bf16[768,768]{1,0:T(8,128)(2,1)S(1)} fusion(bf16[768,768]{1,0:T(8,128)(2,1)} %compare_select_fusion, bf16[768,768]{1,0:T(8,128)(2,1)} %collective-permute-done.4, s32[768]{0:T(1024)S(1)} %copy-done.14, s32[768]{0:T(1024)S(1)} %get-tuple-element.59, s32[4,4]{1,0:T(4,128)S(1)} %collective-permute-done.3), kind=kOutput, calls=%fused_computation.9 | convolution fusion | flops 8291344 | bytes 3545152 | tf_op jit(solution)/shard_map/dot_general | solution.py:63
  44.8 1.8 %collective-permute-start.7 = (bf16[64,768]{1,0:T(8,128)(2,1)S(1)}, bf16[64,768]{1,0:T(8,128)(2,1)S(1)}, u32[]{:S(2)}, u32[]{:S(2)}) collective-permute-start(bf16[64,768]{1,0:T(8,128)(2,1)S(1)} %get-tuple-element.34), channel_id=1, source_target_pairs={{0,8},{4,12},{8,0},{12,4},{16,24},{20,28},{24,16},{28,20},{1,9},{5... | collective-permute-start | bytes 294920 | tf_op jit(solution)/shard_map/ppermute | solution.py:20
  51.4 3.8 %collective-permute-start.10 = (bf16[3,256,128]{2,1,0:T(8,128)(2,1)S(1)}, bf16[3,256,128]{2,1,0:T(8,128)(2,1)S(1)}, u32[]{:S(2)}, u32[]{:S(2)}) collective-permute-start(bf16[3,256,128]{2,1,0:T(8,128)(2,1)S(1)} %slice_select_fusion), channel_id=1, source_target_pairs={{0,3},{1,0},{2,1},{3,2},{4,7},{5,4},{6,5},{7,6},{8,11},{9,8},{10,9... | collective-permute-start | bytes 589832 | tf_op jit(solution)/shard_map/ppermute | solution.py:39
  59.8 2.4 %collective-permute-done.13 = bf16[64,768]{1,0:T(8,128)(2,1)S(1)} collective-permute-done((bf16[64,768]{1,0:T(8,128)(2,1)S(1)}, bf16[64,768]{1,0:T(8,128)(2,1)S(1)}, u32[]{:S(2)}, u32[]{:S(2)}) %collective-permute-start.13) | collective-permute-done | bytes 98336 | tf_op jit(solution)/shard_map/ppermute | solution.py:20
  64.8 2.0 %collective-permute-done.27 = bf16[64,768]{1,0:T(8,128)(2,1)S(1)} collective-permute-done((bf16[64,768]{1,0:T(8,128)(2,1)S(1)}, bf16[64,768]{1,0:T(8,128)(2,1)S(1)}, u32[]{:S(2)}, u32[]{:S(2)}) %collective-permute-start.27) | collective-permute-done | bytes 98336 | tf_op jit(solution)/shard_map/ppermute | solution.py:20
  69.1 3.0 %collective-permute-done.9 = bf16[3,256,128]{2,1,0:T(8,128)(2,1)S(1)} collective-permute-done((bf16[3,256,128]{2,1,0:T(8,128)(2,1)S(1)}, bf16[3,256,128]{2,1,0:T(8,128)(2,1)S(1)}, u32[]{:S(2)}, u32[]{:S(2)}) %collective-permute-start.9) | collective-permute-done | bytes 196640 | tf_op jit(solution)/shard_map/ppermute | solution.py:39
  98.7 2.4 %collective-permute-done.37 = bf16[64,768]{1,0:T(8,128)(2,1)S(1)} collective-permute-done((bf16[64,768]{1,0:T(8,128)(2,1)S(1)}, bf16[64,768]{1,0:T(8,128)(2,1)S(1)}, u32[]{:S(2)}, u32[]{:S(2)}) %collective-permute-start.37) | collective-permute-done | bytes 98336 | tf_op jit(solution)/shard_map/ppermute | solution.py:20
  101.7 2.3 %collective-permute-start.39 = (bf16[64,768]{1,0:T(8,128)(2,1)S(1)}, bf16[64,768]{1,0:T(8,128)(2,1)S(1)}, u32[]{:S(2)}, u32[]{:S(2)}) collective-permute-start(bf16[64,768]{1,0:T(8,128)(2,1)S(1)} %fusion.49), channel_id=1, source_target_pairs={{0,2},{1,3},{2,0},{3,1},{4,6},{5,7},{6,4},{7,5},{8,10},{9,11},{10,... | collective-permute-start | bytes 294920 | tf_op jit(solution)/shard_map/ppermute | solution.py:29
  104.0 1.9 %collective-permute-start.38 = (bf16[64,768]{1,0:T(8,128)(2,1)S(1)}, bf16[64,768]{1,0:T(8,128)(2,1)S(1)}, u32[]{:S(2)}, u32[]{:S(2)}) collective-permute-start(bf16[64,768]{1,0:T(8,128)(2,1)S(1)} %fusion.49), channel_id=1, source_target_pairs={{0,1},{1,2},{2,3},{3,0},{4,5},{5,6},{6,7},{7,4},{8,9},{9,10},{10,1... | collective-permute-start | bytes 294920 | tf_op jit(solution)/shard_map/ppermute | solution.py:29
  106.7 1.9 %collective-permute-start.45 = (bf16[64,768]{1,0:T(8,128)(2,1)S(1)}, bf16[64,768]{1,0:T(8,128)(2,1)S(1)}, u32[]{:S(2)}, u32[]{:S(2)}) collective-permute-start(bf16[64,768]{1,0:T(8,128)(2,1)S(1)} %fusion.50), channel_id=1, source_target_pairs={{0,3},{1,0},{2,1},{3,2},{4,7},{5,4},{6,5},{7,6},{8,11},{9,8},{10,9... | collective-permute-start | bytes 294920 | tf_op jit(solution)/shard_map/ppermute | solution.py:29
  108.6 2.4 %collective-permute-start.43 = (bf16[64,768]{1,0:T(8,128)(2,1)S(1)}, bf16[64,768]{1,0:T(8,128)(2,1)S(1)}, u32[]{:S(2)}, u32[]{:S(2)}) collective-permute-start(bf16[64,768]{1,0:T(8,128)(2,1)S(1)} %fusion.50), channel_id=1, source_target_pairs={{0,1},{1,2},{2,3},{3,0},{4,5},{5,6},{6,7},{7,4},{8,9},{9,10},{10,1... | collective-permute-start | bytes 294920 | tf_op jit(solution)/shard_map/ppermute | solution.py:29
  111.0 7.2 %collective-permute-done.39 = bf16[64,768]{1,0:T(8,128)(2,1)S(1)} collective-permute-done((bf16[64,768]{1,0:T(8,128)(2,1)S(1)}, bf16[64,768]{1,0:T(8,128)(2,1)S(1)}, u32[]{:S(2)}, u32[]{:S(2)}) %collective-permute-start.39) | collective-permute-done | bytes 98336 | tf_op jit(solution)/shard_map/ppermute | solution.py:29
  118.8 2.0 %collective-permute-done.44 = bf16[64,768]{1,0:T(8,128)(2,1)S(1)} collective-permute-done((bf16[64,768]{1,0:T(8,128)(2,1)S(1)}, bf16[64,768]{1,0:T(8,128)(2,1)S(1)}, u32[]{:S(2)}, u32[]{:S(2)}) %collective-permute-start.44) | collective-permute-done | bytes 98336 | tf_op jit(solution)/shard_map/ppermute | solution.py:29
  127.3 2.8 %collective-permute-done.47 = f32[512]{0:T(512)S(1)} collective-permute-done((f32[512]{0:T(512)S(1)}, f32[512]{0:T(512)S(1)}, u32[]{:S(2)}, u32[]{:S(2)}) %collective-permute-start.47) | collective-permute-done | bytes 2080 | tf_op jit(solution)/shard_map/ppermute | solution.py:20
  131.6 2.1 %collective-permute-done.48 = f32[512]{0:T(512)S(1)} collective-permute-done((f32[512]{0:T(512)S(1)}, f32[512]{0:T(512)S(1)}, u32[]{:S(2)}, u32[]{:S(2)}) %collective-permute-start.48) | collective-permute-done | bytes 2080 | tf_op jit(solution)/shard_map/ppermute | solution.py:20
  139.0 2.8 %collective-permute-done.50 = f32[512]{0:T(512)S(1)} collective-permute-done((f32[512]{0:T(512)S(1)}, f32[512]{0:T(512)S(1)}, u32[]{:S(2)}, u32[]{:S(2)}) %collective-permute-start.50) | collective-permute-done | bytes 2080 | tf_op jit(solution)/shard_map/ppermute | solution.py:20
  143.3 2.1 %collective-permute-done.51 = f32[512]{0:T(512)S(1)} collective-permute-done((f32[512]{0:T(512)S(1)}, f32[512]{0:T(512)S(1)}, u32[]{:S(2)}, u32[]{:S(2)}) %collective-permute-start.51) | collective-permute-done | bytes 2080 | tf_op jit(solution)/shard_map/ppermute | solution.py:20
  150.0 2.8 %collective-permute-done.53 = f32[512]{0:T(512)S(1)} collective-permute-done((f32[512]{0:T(512)S(1)}, f32[512]{0:T(512)S(1)}, u32[]{:S(2)}, u32[]{:S(2)}) %collective-permute-start.53) | collective-permute-done | bytes 2080 | tf_op jit(solution)/shard_map/ppermute | solution.py:20
  154.3 2.1 %collective-permute-done.54 = f32[512]{0:T(512)S(1)} collective-permute-done((f32[512]{0:T(512)S(1)}, f32[512]{0:T(512)S(1)}, u32[]{:S(2)}, u32[]{:S(2)}) %collective-permute-start.54) | collective-permute-done | bytes 2080 | tf_op jit(solution)/shard_map/ppermute | solution.py:20
  158.8 2.8 %collective-permute-done.56 = f32[128]{0:T(128)S(1)} collective-permute-done((f32[128]{0:T(128)S(1)}, f32[128]{0:T(128)S(1)}, u32[]{:S(2)}, u32[]{:S(2)}) %collective-permute-start.56) | collective-permute-done | bytes 544 | tf_op jit(solution)/shard_map/ppermute | solution.py:20
  163.1 2.0 %collective-permute-done.57 = f32[128]{0:T(128)S(1)} collective-permute-done((f32[128]{0:T(128)S(1)}, f32[128]{0:T(128)S(1)}, u32[]{:S(2)}, u32[]{:S(2)}) %collective-permute-start.57) | collective-permute-done | bytes 544 | tf_op jit(solution)/shard_map/ppermute | solution.py:20
  (234 shorter events, 83.4 us)
Async XLA Ops:
  1.6 40.1 %collective-permute-start.2 = (bf16[64,768]{1,0:T(8,128)(2,1)}, bf16[64,768]{1,0:T(8,128)(2,1)}, u32[]{:S(2)}, u32[]{:S(2)}) collective-permute-start(bf16[64,768]{1,0:T(8,128)(2,1)} %get-tuple-element.29), channel_id=1, source_target_pairs={{0,4},{4,0},{8,12},{12,8},{16,20},{20,16},{24,28},{28,24},{1,5},{5... | collective-permute-start | bytes 294920 | tf_op jit(solution)/shard_map/ppermute | solution.py:20
  2.1 41.0 %collective-permute-start.5 = (bf16[64,768]{1,0:T(8,128)(2,1)}, bf16[64,768]{1,0:T(8,128)(2,1)}, u32[]{:S(2)}, u32[]{:S(2)}) collective-permute-start(bf16[64,768]{1,0:T(8,128)(2,1)} %get-tuple-element.29), channel_id=1, source_target_pairs={{0,8},{4,12},{8,0},{12,4},{16,24},{20,28},{24,16},{28,20},{1,9},{5... | collective-permute-start | bytes 294920 | tf_op jit(solution)/shard_map/ppermute | solution.py:20
  9.3 24.1 %collective-permute-start.1 = (bf16[768,768]{0,1:T(8,128)(2,1)}, bf16[768,768]{0,1:T(8,128)(2,1)}, u32[]{:S(2)}, u32[]{:S(2)}) collective-permute-start(bf16[768,768]{0,1:T(8,128)(2,1)} %bitcast.4), channel_id=1, source_target_pairs={{0,4},{4,0},{8,12},{12,8},{16,20},{20,16},{24,28},{28,24},{1,5},{5... | collective-permute-start | bytes 3538952 | tf_op jit(solution)/shard_map/ppermute | solution.py:20
  10.1 18.4 %collective-permute-start = (s32[4,4]{1,0:T(4,128)}, s32[4,4]{1,0:T(4,128)}, u32[]{:S(2)}, u32[]{:S(2)}) collective-permute-start(s32[4,4]{1,0:T(4,128)} %get-tuple-element.31), channel_id=1, source_target_pairs={{0,4},{4,0},{8,12},{12,8},{16,20},{20,16},{24,28},{28,24},{1,5},{5... | collective-permute-start | bytes 200 | tf_op jit(solution)/shard_map/ppermute | solution.py:20
  10.4 28.7 %collective-permute-start.4 = (bf16[768,768]{1,0:T(8,128)(2,1)}, bf16[768,768]{1,0:T(8,128)(2,1)}, u32[]{:S(2)}, u32[]{:S(2)}) collective-permute-start(bf16[768,768]{1,0:T(8,128)(2,1)} %get-tuple-element.23), channel_id=1, source_target_pairs={{0,8},{4,12},{8,0},{12,4},{16,24},{20,28},{24,16},{28,20},{1,9},{5... | collective-permute-start | bytes 3538952 | tf_op jit(solution)/shard_map/ppermute | solution.py:20
  28.5 10.3 %collective-permute-start.3 = (s32[4,4]{1,0:T(4,128)}, s32[4,4]{1,0:T(4,128)S(1)}, u32[]{:S(2)}, u32[]{:S(2)}) collective-permute-start(s32[4,4]{1,0:T(4,128)} %get-tuple-element.30), channel_id=1, source_target_pairs={{0,8},{4,12},{8,0},{12,4},{16,24},{20,28},{24,16},{28,20},{1,9},{5... | collective-permute-start | bytes 200 | tf_op jit(solution)/shard_map/ppermute | solution.py:20
  33.5 13.1 %collective-permute-start.22 = (bf16[64,768]{1,0:T(8,128)(2,1)}, bf16[64,768]{1,0:T(8,128)(2,1)}, u32[]{:S(2)}, u32[]{:S(2)}) collective-permute-start(bf16[64,768]{1,0:T(8,128)(2,1)} %get-tuple-element.28), channel_id=1, source_target_pairs={{0,4},{4,0},{8,12},{12,8},{16,20},{20,16},{24,28},{28,24},{1,5},{5... | collective-permute-start | bytes 294920 | tf_op jit(solution)/shard_map/ppermute | solution.py:20
  38.8 9.0 %collective-permute-start.23 = (bf16[64,768]{1,0:T(8,128)(2,1)}, bf16[64,768]{1,0:T(8,128)(2,1)}, u32[]{:S(2)}, u32[]{:S(2)}) collective-permute-start(bf16[64,768]{1,0:T(8,128)(2,1)} %get-tuple-element.28), channel_id=1, source_target_pairs={{0,8},{4,12},{8,0},{12,4},{16,24},{20,28},{24,16},{28,20},{1,9},{5... | collective-permute-start | bytes 294920 | tf_op jit(solution)/shard_map/ppermute | solution.py:20
  44.7 5.3 %collective-permute-start.6 = (bf16[64,768]{1,0:T(8,128)(2,1)S(1)}, bf16[64,768]{1,0:T(8,128)(2,1)S(1)}, u32[]{:S(2)}, u32[]{:S(2)}) collective-permute-start(bf16[64,768]{1,0:T(8,128)(2,1)S(1)} %get-tuple-element.34), channel_id=1, source_target_pairs={{0,4},{4,0},{8,12},{12,8},{16,20},{20,16},{24,28},{28,24},{1,5},{5... | collective-permute-start | bytes 294920 | tf_op jit(solution)/shard_map/ppermute | solution.py:20
  44.8 5.6 %collective-permute-start.7 = (bf16[64,768]{1,0:T(8,128)(2,1)S(1)}, bf16[64,768]{1,0:T(8,128)(2,1)S(1)}, u32[]{:S(2)}, u32[]{:S(2)}) collective-permute-start(bf16[64,768]{1,0:T(8,128)(2,1)S(1)} %get-tuple-element.34), channel_id=1, source_target_pairs={{0,8},{4,12},{8,0},{12,4},{16,24},{20,28},{24,16},{28,20},{1,9},{5... | collective-permute-start | bytes 294920 | tf_op jit(solution)/shard_map/ppermute | solution.py:20
  49.4 7.2 %collective-permute-start.24 = (bf16[64,768]{1,0:T(8,128)(2,1)S(1)}, bf16[64,768]{1,0:T(8,128)(2,1)S(1)}, u32[]{:S(2)}, u32[]{:S(2)}) collective-permute-start(bf16[64,768]{1,0:T(8,128)(2,1)S(1)} %get-tuple-element.44), channel_id=1, source_target_pairs={{0,4},{4,0},{8,12},{12,8},{16,20},{20,16},{24,28},{28,24},{1,5},{5... | collective-permute-start | bytes 294920 | tf_op jit(solution)/shard_map/ppermute | solution.py:20
  49.6 7.4 %collective-permute-start.25 = (bf16[64,768]{1,0:T(8,128)(2,1)S(1)}, bf16[64,768]{1,0:T(8,128)(2,1)S(1)}, u32[]{:S(2)}, u32[]{:S(2)}) collective-permute-start(bf16[64,768]{1,0:T(8,128)(2,1)S(1)} %get-tuple-element.44), channel_id=1, source_target_pairs={{0,8},{4,12},{8,0},{12,4},{16,24},{20,28},{24,16},{28,20},{1,9},{5... | collective-permute-start | bytes 294920 | tf_op jit(solution)/shard_map/ppermute | solution.py:20
  51.4 17.6 %collective-permute-start.10 = (bf16[3,256,128]{2,1,0:T(8,128)(2,1)S(1)}, bf16[3,256,128]{2,1,0:T(8,128)(2,1)S(1)}, u32[]{:S(2)}, u32[]{:S(2)}) collective-permute-start(bf16[3,256,128]{2,1,0:T(8,128)(2,1)S(1)} %slice_select_fusion), channel_id=1, source_target_pairs={{0,3},{1,0},{2,1},{3,2},{4,7},{5,4},{6,5},{7,6},{8,11},{9,8},{10,9... | collective-permute-start | bytes 589832 | tf_op jit(solution)/shard_map/ppermute | solution.py:39
  55.2 16.9 %collective-permute-start.9 = (bf16[3,256,128]{2,1,0:T(8,128)(2,1)S(1)}, bf16[3,256,128]{2,1,0:T(8,128)(2,1)S(1)}, u32[]{:S(2)}, u32[]{:S(2)}) collective-permute-start(bf16[3,256,128]{2,1,0:T(8,128)(2,1)S(1)} %slice_select_fusion), channel_id=1, source_target_pairs={{0,2},{1,3},{2,0},{3,1},{4,6},{5,7},{6,4},{7,5},{8,10},{9,11},{10,... | collective-permute-start | bytes 589832 | tf_op jit(solution)/shard_map/ppermute | solution.py:39
  55.2 18.4 %collective-permute-start.8 = (bf16[3,256,128]{2,1,0:T(8,128)(2,1)S(1)}, bf16[3,256,128]{2,1,0:T(8,128)(2,1)S(1)}, u32[]{:S(2)}, u32[]{:S(2)}) collective-permute-start(bf16[3,256,128]{2,1,0:T(8,128)(2,1)S(1)} %slice_select_fusion), channel_id=1, source_target_pairs={{0,1},{1,2},{2,3},{3,0},{4,5},{5,6},{6,7},{7,4},{8,9},{9,10},{10,1... | collective-permute-start | bytes 589832 | tf_op jit(solution)/shard_map/ppermute | solution.py:39
  64.1 10.3 %collective-permute-start.14 = (bf16[64,768]{1,0:T(8,128)(2,1)S(1)}, bf16[64,768]{1,0:T(8,128)(2,1)S(1)}, u32[]{:S(2)}, u32[]{:S(2)}) collective-permute-start(bf16[64,768]{1,0:T(8,128)(2,1)S(1)} %get-tuple-element.36), channel_id=1, source_target_pairs={{0,4},{4,0},{8,12},{12,8},{16,20},{20,16},{24,28},{28,24},{1,5},{5... | collective-permute-start | bytes 294920 | tf_op jit(solution)/shard_map/ppermute | solution.py:20
  66.9 7.9 %collective-permute-start.15 = (bf16[64,768]{1,0:T(8,128)(2,1)S(1)}, bf16[64,768]{1,0:T(8,128)(2,1)S(1)}, u32[]{:S(2)}, u32[]{:S(2)}) collective-permute-start(bf16[64,768]{1,0:T(8,128)(2,1)S(1)} %get-tuple-element.36), channel_id=1, source_target_pairs={{0,8},{4,12},{8,0},{12,4},{16,24},{20,28},{24,16},{28,20},{1,9},{5... | collective-permute-start | bytes 294920 | tf_op jit(solution)/shard_map/ppermute | solution.py:20
  69.0 7.5 %collective-permute-start.28 = (bf16[64,768]{1,0:T(8,128)(2,1)S(1)}, bf16[64,768]{1,0:T(8,128)(2,1)S(1)}, u32[]{:S(2)}, u32[]{:S(2)}) collective-permute-start(bf16[64,768]{1,0:T(8,128)(2,1)S(1)} %get-tuple-element.48), channel_id=1, source_target_pairs={{0,4},{4,0},{8,12},{12,8},{16,20},{20,16},{24,28},{28,24},{1,5},{5... | collective-permute-start | bytes 294920 | tf_op jit(solution)/shard_map/ppermute | solution.py:20
  74.3 20.8 %collective-permute-start.11 = (bf16[4,3,256,128]{3,2,1,0:T(8,128)(2,1)S(1)}, bf16[4,3,256,128]{3,2,1,0:T(8,128)(2,1)S(1)}, u32[]{:S(2)}, u32[]{:S(2)}) collective-permute-start(bf16[4,3,256,128]{3,2,1,0:T(8,128)(2,1)S(1)} %get-tuple-element.26), channel_id=1, source_target_pairs={{0,4},{4,0},{8,12},{12,8},{16,20},{20,16},{24,28},{28,24},{1,5},{5... | collective-permute-start | bytes 2359304 | tf_op jit(solution)/shard_map/ppermute | solution.py:20
  77.6 5.3 %collective-permute-start.31 = (bf16[64,768]{1,0:T(8,128)(2,1)S(1)}, bf16[64,768]{1,0:T(8,128)(2,1)S(1)}, u32[]{:S(2)}, u32[]{:S(2)}) collective-permute-start(bf16[64,768]{1,0:T(8,128)(2,1)S(1)} %get-tuple-element.50), channel_id=1, source_target_pairs={{0,8},{4,12},{8,0},{12,4},{16,24},{20,28},{24,16},{28,20},{1,9},{5... | collective-permute-start | bytes 294920 | tf_op jit(solution)/shard_map/ppermute | solution.py:20
  83.6 5.2 %collective-permute-start.33 = (bf16[64,768]{1,0:T(8,128)(2,1)S(1)}, bf16[64,768]{1,0:T(8,128)(2,1)S(1)}, u32[]{:S(2)}, u32[]{:S(2)}) collective-permute-start(bf16[64,768]{1,0:T(8,128)(2,1)S(1)} %get-tuple-element.52), channel_id=1, source_target_pairs={{0,8},{4,12},{8,0},{12,4},{16,24},{20,28},{24,16},{28,20},{1,9},{5... | collective-permute-start | bytes 294920 | tf_op jit(solution)/shard_map/ppermute | solution.py:20
  87.5 5.2 %collective-permute-start.21 = (bf16[64,768]{1,0:T(8,128)(2,1)S(1)}, bf16[64,768]{1,0:T(8,128)(2,1)S(1)}, u32[]{:S(2)}, u32[]{:S(2)}) collective-permute-start(bf16[64,768]{1,0:T(8,128)(2,1)S(1)} %get-tuple-element.42), channel_id=1, source_target_pairs={{0,8},{4,12},{8,0},{12,4},{16,24},{20,28},{24,16},{28,20},{1,9},{5... | collective-permute-start | bytes 294920 | tf_op jit(solution)/shard_map/ppermute | solution.py:20
  89.6 5.2 %collective-permute-start.35 = (bf16[64,768]{1,0:T(8,128)(2,1)S(1)}, bf16[64,768]{1,0:T(8,128)(2,1)S(1)}, u32[]{:S(2)}, u32[]{:S(2)}) collective-permute-start(bf16[64,768]{1,0:T(8,128)(2,1)S(1)} %get-tuple-element.54), channel_id=1, source_target_pairs={{0,8},{4,12},{8,0},{12,4},{16,24},{20,28},{24,16},{28,20},{1,9},{5... | collective-permute-start | bytes 294920 | tf_op jit(solution)/shard_map/ppermute | solution.py:20
  95.7 5.4 %collective-permute-start.37 = (bf16[64,768]{1,0:T(8,128)(2,1)S(1)}, bf16[64,768]{1,0:T(8,128)(2,1)S(1)}, u32[]{:S(2)}, u32[]{:S(2)}) collective-permute-start(bf16[64,768]{1,0:T(8,128)(2,1)S(1)} %convert_element_type.180), channel_id=1, source_target_pairs={{0,8},{4,12},{8,0},{12,4},{16,24},{20,28},{24,16},{28,20},{1,9},{5... | collective-permute-start | bytes 294920 | tf_op jit(solution)/shard_map/ppermute | solution.py:20
  97.5 8.4 %collective-permute-start.41 = (bf16[64,768]{1,0:T(8,128)(2,1)S(1)}, bf16[64,768]{1,0:T(8,128)(2,1)S(1)}, u32[]{:S(2)}, u32[]{:S(2)}) collective-permute-start(bf16[64,768]{1,0:T(8,128)(2,1)S(1)} %convert_element_type.182), channel_id=1, source_target_pairs={{0,4},{4,0},{8,12},{12,8},{16,20},{20,16},{24,28},{28,24},{1,5},{5... | collective-permute-start | bytes 294920 | tf_op jit(solution)/shard_map/ppermute | solution.py:20
  97.8 8.5 %collective-permute-start.42 = (bf16[64,768]{1,0:T(8,128)(2,1)S(1)}, bf16[64,768]{1,0:T(8,128)(2,1)S(1)}, u32[]{:S(2)}, u32[]{:S(2)}) collective-permute-start(bf16[64,768]{1,0:T(8,128)(2,1)S(1)} %convert_element_type.182), channel_id=1, source_target_pairs={{0,8},{4,12},{8,0},{12,4},{16,24},{20,28},{24,16},{28,20},{1,9},{5... | collective-permute-start | bytes 294920 | tf_op jit(solution)/shard_map/ppermute | solution.py:20
  101.4 7.2 %collective-permute-start.40 = (bf16[64,768]{1,0:T(8,128)(2,1)S(1)}, bf16[64,768]{1,0:T(8,128)(2,1)S(1)}, u32[]{:S(2)}, u32[]{:S(2)}) collective-permute-start(bf16[64,768]{1,0:T(8,128)(2,1)S(1)} %fusion.49), channel_id=1, source_target_pairs={{0,3},{1,0},{2,1},{3,2},{4,7},{5,4},{6,5},{7,6},{8,11},{9,8},{10,9... | collective-permute-start | bytes 294920 | tf_op jit(solution)/shard_map/ppermute | solution.py:29
  101.7 16.4 %collective-permute-start.39 = (bf16[64,768]{1,0:T(8,128)(2,1)S(1)}, bf16[64,768]{1,0:T(8,128)(2,1)S(1)}, u32[]{:S(2)}, u32[]{:S(2)}) collective-permute-start(bf16[64,768]{1,0:T(8,128)(2,1)S(1)} %fusion.49), channel_id=1, source_target_pairs={{0,2},{1,3},{2,0},{3,1},{4,6},{5,7},{6,4},{7,5},{8,10},{9,11},{10,... | collective-permute-start | bytes 294920 | tf_op jit(solution)/shard_map/ppermute | solution.py:29
  104.0 14.2 %collective-permute-start.38 = (bf16[64,768]{1,0:T(8,128)(2,1)S(1)}, bf16[64,768]{1,0:T(8,128)(2,1)S(1)}, u32[]{:S(2)}, u32[]{:S(2)}) collective-permute-start(bf16[64,768]{1,0:T(8,128)(2,1)S(1)} %fusion.49), channel_id=1, source_target_pairs={{0,1},{1,2},{2,3},{3,0},{4,5},{5,6},{6,7},{7,4},{8,9},{9,10},{10,1... | collective-permute-start | bytes 294920 | tf_op jit(solution)/shard_map/ppermute | solution.py:29
  106.7 12.2 %collective-permute-start.45 = (bf16[64,768]{1,0:T(8,128)(2,1)S(1)}, bf16[64,768]{1,0:T(8,128)(2,1)S(1)}, u32[]{:S(2)}, u32[]{:S(2)}) collective-permute-start(bf16[64,768]{1,0:T(8,128)(2,1)S(1)} %fusion.50), channel_id=1, source_target_pairs={{0,3},{1,0},{2,1},{3,2},{4,7},{5,4},{6,5},{7,6},{8,11},{9,8},{10,9... | collective-permute-start | bytes 294920 | tf_op jit(solution)/shard_map/ppermute | solution.py:29
  108.6 12.3 %collective-permute-start.44 = (bf16[64,768]{1,0:T(8,128)(2,1)S(1)}, bf16[64,768]{1,0:T(8,128)(2,1)S(1)}, u32[]{:S(2)}, u32[]{:S(2)}) collective-permute-start(bf16[64,768]{1,0:T(8,128)(2,1)S(1)} %fusion.50), channel_id=1, source_target_pairs={{0,2},{1,3},{2,0},{3,1},{4,6},{5,7},{6,4},{7,5},{8,10},{9,11},{10,... | collective-permute-start | bytes 294920 | tf_op jit(solution)/shard_map/ppermute | solution.py:29
  108.6 12.3 %collective-permute-start.43 = (bf16[64,768]{1,0:T(8,128)(2,1)S(1)}, bf16[64,768]{1,0:T(8,128)(2,1)S(1)}, u32[]{:S(2)}, u32[]{:S(2)}) collective-permute-start(bf16[64,768]{1,0:T(8,128)(2,1)S(1)} %fusion.50), channel_id=1, source_target_pairs={{0,1},{1,2},{2,3},{3,0},{4,5},{5,6},{6,7},{7,4},{8,9},{9,10},{10,1... | collective-permute-start | bytes 294920 | tf_op jit(solution)/shard_map/ppermute | solution.py:29
  (42 other events, 130.9 us)
